TPU v7x, 32 devices: a whole 2x2x4 slice. The times are simulated.
32 devices in a mesh: rep: 2 (over y), tp: 8 (over z, x), sub: 2 (over core).
Axes of the slice: x: 2, y: 2, z: 4, core: 2. Of those that a mesh axis runs over, the one named last changes fastest.
Arguments:
- queries: bfloat16 [2, 16, 16384], P(None, ('rep', 'sub'), 'tp'), parts along dimension 1, may hold values from -53 to 53
- prefix_kv: bfloat16 [2, 16384, 1024], P(None, ('rep', 'tp')), parts along dimension 1, may hold values from -6 to 6
- tail_kv: bfloat16 [2, 16, 1024, 1024], P(None, ('rep', 'sub'), 'tp'), parts along dimension 1, may hold values from -6 to 6
- tail_lengths: int32 [16], P(('rep', 'sub')), parts along dimension 0, may hold values from 1 to 1024, as said below
- fresh_kv: bfloat16 [2, 2, 16, 1024], P(None, None, ('rep', 'sub')), parts along dimension 2, may hold values from -6 to 6
- out_weight: bfloat16 [16384, 16384], P('tp', 'sub'), may hold values from -0.5 to 0.5
- scale_in: int32 [128], replicated, may hold values from 9 to 14
- scale_out: int32 [128], replicated, may hold values from 5 to 10
- residual: bfloat16 [2, 16, 16384], P(None, 'rep', 'sub'), parts along dimension 1, may hold values from -1.5 to 1.5
Outputs:
- hidden: bfloat16 [2, 16, 16384], P(None, 'rep', 'sub'), parts along dimension 1
There are 2 independent parts, one for each index of `rep`. A program takes and returns all parts, laid end to end along the dimension named above; an argument that names none is the same for every part. Nothing has to cross between parts.
Inputs may be any that keep to these rules, and one draw needn't show every extreme that they name: `tail_lengths`: some sample's tail reaches 1024 tokens.
All inputs are finite; a program needn't handle non-finite values.
Results may differ from a plain program's by a relative error of at most 0.0065.
Values may be sent and summed in bfloat16 or wider, within the bound.
No kernel may reach another device: no remote copies, remote signals or barrier semaphores. Data moves between devices by JAX's collectives and lax.ppermute only.
A program may use at most 192 MiB of HBM per device.

v0:
```python
import math

import jax
import jax.numpy as jnp
from jax import lax
from jax.sharding import PartitionSpec as P

DH = 128


NEG_FILL = -1e30


def per_device(
    queries, prefix_kv, tail_kv, tail_lengths, fresh_kv, out_weight, scale_in, scale_out, residual
):
    steps_n, rows_dev, width_dev = queries.shape
    heads_dev = width_dev // DH
    tp_count = lax.axis_size("tp")
    tp_rank = lax.axis_index("tp")
    sub_rank = lax.axis_index("sub")
    kv_heads = prefix_kv.shape[2] // DH
    copies = tp_count // kv_heads
    kv_group = tp_rank // copies
    prefix_dev = prefix_kv.shape[1]
    tail_dev = tail_kv.shape[2]
    score_scale = 1.0 / math.sqrt(DH)
    own_query = queries.reshape(steps_n, rows_dev, heads_dev, DH)
    own_fresh = lax.dynamic_slice_in_dim(fresh_kv, kv_group * DH, DH, 3)
    fresh_live = jnp.arange(steps_n)[None, :] <= jnp.arange(steps_n)[:, None]
    own_fresh_scores = (
        jnp.einsum("sbhd,ubd->sbhu", own_query, own_fresh[0], preferred_element_type=jnp.float32)
        * score_scale
    )
    own_fresh_scores = jnp.where(fresh_live[:, None, None, :], own_fresh_scores, NEG_FILL)
    spread_prompt = jnp.repeat(
        prefix_kv.reshape(2, prefix_dev, kv_heads, DH), copies, axis=2
    ).reshape(2, prefix_dev, tp_count * DH)
    spread_tail = jnp.repeat(
        tail_kv.reshape(2 * rows_dev, tail_dev, kv_heads, DH), copies, axis=2
    ).reshape(2 * rows_dev, tail_dev, tp_count * DH)
    moved_prompt, moved_tail = (
        lax.all_to_all(spread_prompt, "tp", split_axis=2, concat_axis=1, tiled=True),
        lax.all_to_all(spread_tail, "tp", split_axis=2, concat_axis=1, tiled=True),
    )
    tail_full = moved_tail.reshape(2, rows_dev, tail_dev * tp_count, DH)
    prompt_scores = (
        jnp.einsum("sbhd,pd->sbhp", own_query, moved_prompt[0], preferred_element_type=jnp.float32)
        * score_scale
    )
    tail_scores = (
        jnp.einsum("sbhd,btd->sbht", own_query, tail_full[0], preferred_element_type=jnp.float32)
        * score_scale
    )
    tail_live = jnp.arange(tail_dev * tp_count)[None, :] < tail_lengths[:, None]
    tail_scores = jnp.where(tail_live[None, :, None, :], tail_scores, NEG_FILL)
    peak = jnp.maximum(
        jnp.maximum(prompt_scores.max(-1), tail_scores.max(-1)), own_fresh_scores.max(-1)
    )
    prompt_weights = jnp.exp(prompt_scores - peak[..., None])
    tail_weights = jnp.exp(tail_scores - peak[..., None])
    fresh_weights = jnp.exp(own_fresh_scores - peak[..., None])
    mass = prompt_weights.sum(-1) + tail_weights.sum(-1) + fresh_weights.sum(-1)
    numer = jnp.einsum(
        "sbhp,pd->sbhd",
        prompt_weights.astype(jnp.bfloat16),
        moved_prompt[1],
        preferred_element_type=jnp.float32,
    )
    numer = numer + jnp.einsum(
        "sbht,btd->sbhd",
        tail_weights.astype(jnp.bfloat16),
        tail_full[1],
        preferred_element_type=jnp.float32,
    )
    numer = numer + jnp.einsum(
        "sbhu,ubd->sbhd",
        fresh_weights.astype(jnp.bfloat16),
        own_fresh[1],
        preferred_element_type=jnp.float32,
    )
    attended = (numer / mass[..., None]).astype(jnp.bfloat16).reshape(steps_n, rows_dev, width_dev)
    gathered = lax.all_gather(attended, "sub", axis=1, tiled=True)
    samples = gathered.shape[1]
    local_width = out_weight.shape[1]
    head_rows_in = gathered.reshape(steps_n * samples, heads_dev, DH)
    head_weights = out_weight.reshape(heads_dev, DH, local_width)
    scale_a = jnp.repeat(jnp.exp2(-scale_in.astype(jnp.float32)), 128)
    scale_b = jnp.repeat(jnp.exp2(-scale_out.astype(jnp.float32)), 128)
    local_a = lax.dynamic_slice_in_dim(scale_a, sub_rank * local_width, local_width, 0)
    local_b = lax.dynamic_slice_in_dim(scale_b, sub_rank * local_width, local_width, 0)
    per_head_term = jnp.einsum(
        "rhd,hdf->rhf", head_rows_in, head_weights, preferred_element_type=jnp.float32
    )
    clipped = jnp.clip(per_head_term / local_a[None, None, :], -127.0, 127.0).sum(1)
    summed = lax.psum_scatter(clipped, "tp", scatter_dimension=1, tiled=True)
    piece_cols = local_width // tp_count
    piece_start = sub_rank * local_width + tp_rank * piece_cols
    piece_a = lax.dynamic_slice_in_dim(scale_a, piece_start, piece_cols, 0)
    piece_b = lax.dynamic_slice_in_dim(scale_b, piece_start, piece_cols, 0)
    levels = jnp.clip(summed * piece_a / piece_b, -127.0, 127.0).astype(jnp.bfloat16)
    all_levels = lax.all_gather(levels, "tp", axis=1, tiled=True)
    restored = all_levels.astype(jnp.float32) * local_b
    hidden = residual.reshape(steps_n * samples, local_width).astype(jnp.float32) + restored
    return hidden.astype(jnp.bfloat16).reshape(steps_n, samples, local_width)


def solution(mesh):
    return jax.shard_map(
        per_device,
        mesh=mesh,
        in_specs=(
            P(None, ("rep", "sub"), "tp"),
            P(None, ("rep", "tp"), None),
            P(None, ("rep", "sub"), "tp", None),
            P(("rep", "sub")),
            P(None, None, ("rep", "sub"), None),
            P("tp", "sub"),
            P(),
            P(),
            P(None, "rep", "sub"),
        ),
        out_specs=P(None, "rep", "sub"),
        check_vma=False,
    )
```

profile of v0, /device:TPU:0, one launch (start us, length us, event | category | flops | bytes accessed | tf_op | source)
XLA Modules:
  0.0 296.8 jit_solution(12583703444207786706)
XLA Ops:
  6.5 4.3 %copy.48 = bf16[2,4,128,1024]{2,1,0,3:T(4,128)(2,1)} copy(bf16[2,4,128,1024]{3,2,1,0:T(8,128)(2,1)} %param.11) | data formatting | bytes 4194304 | tf_op args[2]
  10.8 7.3 %all-to-all-start.1 = ((bf16[8,128,1024]{1,0,2:T(8,128)(2,1)}), bf16[8,128,1024]{1,0,2:T(8,128)(2,1)S(1)}, u32[]{:S(2)}, u32[]{:S(2)}) async-start(bf16[8,128,1024]{1,0,2:T(8,128)(2,1)} %bitcast.78), calls=%async_computation.1 | async-start | bytes 4194304 | tf_op jit(solution)/shard_map/all_to_all | solution.py:44
  18.1 11.3 %copy.46 = bf16[2,1024,1024]{1,0,2:T(2,128)(2,1)} copy(bf16[2,1024,1024]{2,1,0:T(8,128)(2,1)} %param.10) | data formatting | bytes 8388608 | tf_op args[1]
  29.4 0.0 copy-start.3
  29.4 0.0 copy-start.5
  29.4 0.0 copy-start.4
  29.4 36.9 %all-to-all-done.1 = bf16[8,128,1024]{1,0,2:T(8,128)(2,1)S(1)} async-done(((bf16[8,128,1024]{1,0,2:T(8,128)(2,1)}), bf16[8,128,1024]{1,0,2:T(8,128)(2,1)S(1)}, u32[]{:S(2)}, u32[]{:S(2)}) %all-to-all-start.1) | async-done | bytes 2097184 | tf_op jit(solution)/shard_map/all_to_all | solution.py:44
  66.3 4.5 %all-to-all-start = ((bf16[2,1024,1024]{1,0,2:T(2,128)(2,1)}), bf16[2,1024,1024]{1,0,2:T(2,128)(2,1)}, u32[]{:S(2)}, u32[]{:S(2)}) async-start(bf16[2,1024,1024]{1,0,2:T(2,128)(2,1)} %copy.46), calls=%async_computation | async-start | bytes 8388608 | tf_op jit(solution)/shard_map/all_to_all | solution.py:43
  70.9 0.0 reduce-scatter.2.cloned.1.call-start
  70.9 0.0 copy-done.3
  71.0 0.0 copy-done.5
  71.0 0.1 broadcast_bitcast_fusion.1
  71.1 0.0 copy-start.1
  71.1 0.7 constant_dynamic-slice_fusion.1
  71.8 0.0 copy-done.4
  71.8 0.1 iota_compare_fusion
  71.9 0.2 fusion.28
  72.1 0.3 copy.49
  72.4 0.1 fusion.27
  72.5 0.0 copy-done.1
  72.5 0.7 copy.57
  73.2 0.7 copy.50
  73.9 0.5 fusion.30
  74.4 89.0 %all-to-all-done = bf16[2,1024,1024]{1,0,2:T(2,128)(2,1)} async-done(((bf16[2,1024,1024]{1,0,2:T(2,128)(2,1)}), bf16[2,1024,1024]{1,0,2:T(2,128)(2,1)}, u32[]{:S(2)}, u32[]{:S(2)}) %all-to-all-start) | async-done | bytes 4194336 | tf_op jit(solution)/shard_map/all_to_all | solution.py:43
  163.4 11.2 %copy.47 = bf16[2,1024,8,128]{3,1,2,0:T(8,128)(2,1)} copy(bf16[2,1024,8,128]{1,0,3,2:T(2,128)(2,1)} %bitcast.1) | data formatting | bytes 8388608 | tf_op jit(solution)/shard_map/all_to_all | solution.py:43
  174.6 2.5 fusion.26
  177.2 0.8 fusion.29
  178.0 0.8 fusion.1
  178.8 0.0 dynamic-slice-start
  178.8 0.9 fusion.3
  179.7 0.2 fusion.16
  179.9 0.3 fusion.11
  180.2 0.2 fusion.12
  180.5 1.9 all_gather.6
  182.4 0.0 dynamic-slice-done
  182.4 0.0 copy-start.6
  182.4 0.0 copy-start.2
  182.4 0.0 copy-start
  182.4 13.7 %fusion.6 = f32[16,8192]{1,0:T(8,128)} fusion(f32[8192]{0:T(1024)S(1)} %dynamic-slice-done, bf16[16,128,8192]{2,1,0:T(8,128)(2,1)} %bitcast.86, bf16[16,16,128]{2,1,0:T(8,128)(2,1)S(1)} %bitcast.85), kind=kOutput, calls=%fused_computation.8 | convolution fusion | flops 543031296 | bytes 34177024 | tf_op jit(solution)/shard_map/rhd,hdf->rhf/dot_general | solution.py:92
  196.2 0.0 reduce-scatter.2.cloned.1.call-update
  196.2 0.0 copy-done.6
  196.2 0.1 broadcast_bitcast_fusion
  196.3 0.0 copy-done.2
  196.4 61.0 %reduce-scatter.2.cloned.1.call-done = f32[16,1024]{1,0:T(8,128)} async-done(((f32[16,8192]{1,0:T(8,128)}), f32[16,1024]{1,0:T(8,128)}) %reduce-scatter.2.cloned.1.call-update) | async-done | bytes 65552 | tf_op jit(solution)/shard_map/reduce_scatter | solution.py:96
  257.4 0.9 clamp_convert_fusion
  258.2 30.9 %all_gather.7 = bf16[16,8192]{1,0:T(8,128)(2,1)S(1)} all-gather(bf16[16,1024]{1,0:T(8,128)(2,1)S(1)} %clamp_convert_fusion), channel_id=1, replica_groups=mesh['rep'=2,'tp'=8,'sub'=2] {'tp'}, dimensions={1}, use_global_device_ids=true | all-gather | bytes 294912 | tf_op jit(solution)/shard_map/all_gather | solution.py:102
  289.2 0.0 copy-done
  289.2 0.8 fusion.18
  (15 shorter events, 0.2 us)
Async XLA Ops:
  10.8 55.5 %all-to-all-start.1 = ((bf16[8,128,1024]{1,0,2:T(8,128)(2,1)}), bf16[8,128,1024]{1,0,2:T(8,128)(2,1)S(1)}, u32[]{:S(2)}, u32[]{:S(2)}) async-start(bf16[8,128,1024]{1,0,2:T(8,128)(2,1)} %bitcast.78), calls=%async_computation.1 | async-start | bytes 4194304 | tf_op jit(solution)/shard_map/all_to_all | solution.py:44
  29.4 41.5 %copy-start.3 = (bf16[2,4,2048]{2,1,0:T(4,128)(2,1)S(1)}, bf16[2,4,2048]{2,1,0:T(4,128)(2,1)}, u32[]{:S(2)}) copy-start(bf16[2,4,2048]{2,1,0:T(4,128)(2,1)} %param.9) | copy-start | bytes 98308
  29.4 41.6 %copy-start.5 = (s32[128]{0:T(128)S(1)}, s32[128]{0:T(128)}, u32[]{:S(2)}) copy-start(s32[128]{0:T(128)} %param.15) | copy-start | bytes 1540
  29.4 42.4 %copy-start.4 = (s32[4]{0:T(128)S(1)}, s32[4]{0:T(128)}, u32[]{:S(2)}) copy-start(s32[4]{0:T(128)} %param.12) | copy-start | bytes 52
  66.3 97.1 %all-to-all-start = ((bf16[2,1024,1024]{1,0,2:T(2,128)(2,1)}), bf16[2,1024,1024]{1,0,2:T(2,128)(2,1)}, u32[]{:S(2)}, u32[]{:S(2)}) async-start(bf16[2,1024,1024]{1,0,2:T(2,128)(2,1)} %copy.46), calls=%async_computation | async-start | bytes 8388608 | tf_op jit(solution)/shard_map/all_to_all | solution.py:43
  70.9 186.5 %reduce-scatter.2.cloned.1.call-start = ((), (), s32[]{:S(2)}) async-start(), calls=%async_computation.3 | async-start | bytes 589824 | tf_op jit(solution)/shard_map/reduce_scatter | solution.py:96
  71.1 1.5 copy-start.1
  178.8 3.6 %dynamic-slice-start = ((f32[16384]{0:T(1024)}, s32[]{:T(128)}), f32[8192]{0:T(1024)S(1)}, s32[]{:S(2)}) async-start(f32[16384]{0:T(1024)} %copy-done.1, s32[]{:T(128)} %select_n.29), calls=%async_computation.4 | async-start | bytes 66048 | tf_op jit(solution)/shard_map/dynamic_slice | solution.py:90
  182.4 13.8 %copy-start.6 = (s32[128]{0:T(128)S(1)}, s32[128]{0:T(128)}, u32[]{:S(2)}) copy-start(s32[128]{0:T(128)} %param.16) | copy-start | bytes 1540
  182.4 13.9 %copy-start.2 = (f32[16384]{0:T(1024)S(1)}, f32[16384]{0:T(1024)}, u32[]{:S(2)}) copy-start(f32[16384]{0:T(1024)} %copy-done.1) | copy-start | bytes 196612
  182.4 106.7 %copy-start = (bf16[2,8,8192]{2,1,0:T(8,128)(2,1)S(1)}, bf16[2,8,8192]{2,1,0:T(8,128)(2,1)}, u32[]{:S(2)}) copy-start(bf16[2,8,8192]{2,1,0:T(8,128)(2,1)} %param.17) | copy-start | bytes 786436
Sparse Core Ops, SparseCore 0:
  196.3 61.0 reduce-scatter.1
where the time goes:
time: 298 us; the launch traced here: 297 us
  waiting for transfers between devices  187 us (63%)
  blocking collectives  32.8 us (11%)
  local copies, waits for them, and re-layouts  32.1 us (11%)
  matrix products  16.6 us (6%)
  between operations  13.7 us (5%)
  starting transfers between devices  11.8 us (4%)
    all_to_all x1, waiting for transfers between devices, per_device(): lax.all_to_all(spread_prompt, 'tp', split_axis=2, concat_axis=1, tiled=True)  89 us
    reduce_scatter x1, waiting for transfers between devices, per_device(): summed = lax.psum_scatter(clipped, 'tp', scatter_dimension=1, tiled=True)  61 us
    all_to_all x1, waiting for transfers between devices, per_device(): lax.all_to_all(spread_tail, 'tp', split_axis=2, concat_axis=1, tiled=True)  36.9 us
    all_gather x1, blocking collectives, per_device(): all_levels = lax.all_gather(levels, 'tp', axis=1, tiled=True)  30.9 us
    unnamed x17, local copies, waits for them, and re-layouts  15.7 us
    dot_general x1, matrix products, per_device(): jnp.einsum('rhd,hdf->rhf', head_rows_in, head_weights, preferred_element_...  13.7 us
    all_to_all x1, local copies, waits for them, and re-layouts, per_device(): lax.all_to_all(spread_prompt, 'tp', split_axis=2, concat_axis=1, tiled=True)  11.2 us
    all_to_all x1, starting transfers between devices, per_device(): lax.all_to_all(spread_tail, 'tp', split_axis=2, concat_axis=1, tiled=True)  7.25 us
  transfers between devices with their start and end apart: 3, of which 3 were waited for; matrix products, arithmetic and copies ran while one was open for 5% of the time, Pallas kernels for 0%

commit v1 on v0

v1 whole, which is shorter than its diff:
```python
import math

import jax
import jax.numpy as jnp
from jax import lax
from jax.sharding import PartitionSpec as P

DH = 128


NEG_FILL = -1e30


def _is_pow2(n):
    return n >= 1 and (n & (n - 1)) == 0


def _gather_blocks(x, axis_name, count):
    if count == 1:
        return x[None]
    if not _is_pow2(count):
        return lax.all_gather(x, axis_name, axis=0, tiled=False)
    me = lax.axis_index(axis_name)
    cur = x[None]
    k = 1
    while k < count:
        other = lax.ppermute(cur, axis_name, [(i, i ^ k) for i in range(count)])
        low = (me // k) % 2 == 0
        cur = jnp.where(low, jnp.concatenate([cur, other]), jnp.concatenate([other, cur]))
        k *= 2
    return cur


def _exchange(blocks, axis_name, count, direct_max=8):
    if count == 1:
        return blocks
    if count > direct_max:
        return jax.tree.map(
            lambda b: lax.all_to_all(b, axis_name, split_axis=0, concat_axis=0, tiled=True), blocks
        )
    me = lax.axis_index(axis_name)
    got = [jax.tree.map(lambda b: lax.dynamic_index_in_dim(b, me, 0, keepdims=False), blocks)]
    for k in range(1, count):
        dst = (me + k) % count
        send = jax.tree.map(lambda b: lax.dynamic_index_in_dim(b, dst, 0, keepdims=False), blocks)
        got.append(lax.ppermute(send, axis_name, [(i, (i + k) % count) for i in range(count)]))
    return jax.tree.map(lambda *xs: jnp.stack(xs), *got)


def per_device(
    queries, prefix_kv, tail_kv, tail_lengths, fresh_kv, out_weight, scale_in, scale_out, residual
):
    steps_n, rows_dev, width_dev = queries.shape
    heads_dev = width_dev // DH
    tp_count = lax.axis_size("tp")
    tp_rank = lax.axis_index("tp")
    sub_rank = lax.axis_index("sub")
    kv_heads = prefix_kv.shape[2] // DH
    heads_all = heads_dev * tp_count
    group = heads_all // kv_heads
    prefix_dev = prefix_kv.shape[1]
    tail_dev = tail_kv.shape[2]
    score_scale = 1.0 / math.sqrt(DH)

    q_blocks = _gather_blocks(queries, "tp", tp_count)
    q_all = jnp.moveaxis(q_blocks, 0, 2).reshape(steps_n, rows_dev, kv_heads, group, DH)

    p_keys = prefix_kv[0].reshape(prefix_dev, kv_heads, DH)
    p_vals = prefix_kv[1].reshape(prefix_dev, kv_heads, DH)
    t_keys = tail_kv[0].reshape(rows_dev, tail_dev, kv_heads, DH)
    t_vals = tail_kv[1].reshape(rows_dev, tail_dev, kv_heads, DH)
    p_scores = (
        jnp.einsum("sbkgd,pkd->sbkgp", q_all, p_keys, preferred_element_type=jnp.float32)
        * score_scale
    )
    t_scores = (
        jnp.einsum("sbkgd,btkd->sbkgt", q_all, t_keys, preferred_element_type=jnp.float32)
        * score_scale
    )
    t_pos = tp_rank * tail_dev + jnp.arange(tail_dev)
    t_live = t_pos[None, :] < tail_lengths[:, None]
    t_scores = jnp.where(t_live[None, :, None, None, :], t_scores, NEG_FILL)
    loc_peak = jnp.maximum(p_scores.max(-1), t_scores.max(-1))
    p_w = jnp.exp(p_scores - loc_peak[..., None])
    t_w = jnp.exp(t_scores - loc_peak[..., None])
    loc_mass = p_w.sum(-1) + t_w.sum(-1)
    loc_numer = jnp.einsum(
        "sbkgp,pkd->sbkgd", p_w.astype(jnp.bfloat16), p_vals, preferred_element_type=jnp.float32
    )
    loc_numer = loc_numer + jnp.einsum(
        "sbkgt,btkd->sbkgd", t_w.astype(jnp.bfloat16), t_vals, preferred_element_type=jnp.float32
    )

    def by_owner(x):
        x = x.reshape((steps_n, rows_dev, tp_count, heads_dev) + x.shape[4:])
        return jnp.moveaxis(x, 2, 0)

    stats = jnp.stack([by_owner(loc_peak), by_owner(loc_mass)], axis=1)
    got_numer, got_stats = _exchange(
        (by_owner(loc_numer), stats.reshape(tp_count, 2, -1)), "tp", tp_count
    )
    got_stats = got_stats.reshape(tp_count, 2, steps_n, rows_dev, heads_dev)
    got_peak = got_stats[:, 0]
    got_mass = got_stats[:, 1]

    own_query = queries.reshape(steps_n, rows_dev, heads_dev, DH)
    f_kv = fresh_kv.reshape(2, steps_n, rows_dev, kv_heads, DH)
    if group % heads_dev == 0:
        one_kv = lax.dynamic_index_in_dim(f_kv, tp_rank * heads_dev // group, 3, keepdims=True)
        f_kv = jnp.broadcast_to(one_kv, (2, steps_n, rows_dev, heads_dev, DH))
    else:
        kv_of_head = (tp_rank * heads_dev + jnp.arange(heads_dev)) // group
        f_kv = jnp.take(f_kv, kv_of_head, axis=3)
    f_scores = (
        jnp.einsum("sbhd,ubhd->sbhu", own_query, f_kv[0], preferred_element_type=jnp.float32)
        * score_scale
    )
    fresh_live = jnp.arange(steps_n)[None, :] <= jnp.arange(steps_n)[:, None]
    f_scores = jnp.where(fresh_live[:, None, None, :], f_scores, NEG_FILL)

    peak = jnp.maximum(got_peak.max(0), f_scores.max(-1))
    rescale = jnp.exp(got_peak - peak[None])
    f_w = jnp.exp(f_scores - peak[..., None])
    mass = (got_mass * rescale).sum(0) + f_w.sum(-1)
    numer = (got_numer * rescale[..., None]).sum(0)
    numer = numer + jnp.einsum(
        "sbhu,ubhd->sbhd", f_w.astype(jnp.bfloat16), f_kv[1], preferred_element_type=jnp.float32
    )
    attended = (numer / mass[..., None]).astype(jnp.bfloat16).reshape(steps_n, rows_dev, width_dev)

    gathered = lax.all_gather(attended, "sub", axis=1, tiled=True)
    samples = gathered.shape[1]
    local_width = out_weight.shape[1]
    head_rows_in = gathered.reshape(steps_n * samples, heads_dev, DH)
    head_weights = out_weight.reshape(heads_dev, DH, local_width)
    scale_a = jnp.repeat(jnp.exp2(-scale_in.astype(jnp.float32)), 128)
    scale_b = jnp.repeat(jnp.exp2(-scale_out.astype(jnp.float32)), 128)
    local_a = lax.dynamic_slice_in_dim(scale_a, sub_rank * local_width, local_width, 0)
    local_b = lax.dynamic_slice_in_dim(scale_b, sub_rank * local_width, local_width, 0)
    per_head_term = jnp.einsum(
        "rhd,hdf->rhf", head_rows_in, head_weights, preferred_element_type=jnp.float32
    )
    clipped = jnp.clip(per_head_term / local_a[None, None, :], -127.0, 127.0).sum(1)

    piece_cols = local_width // tp_count
    pieces = jnp.moveaxis(clipped.reshape(steps_n * samples, tp_count, piece_cols), 1, 0)
    got_pieces = _exchange(pieces, "tp", tp_count)
    summed = got_pieces.sum(0)
    piece_start = sub_rank * local_width + tp_rank * piece_cols
    piece_a = lax.dynamic_slice_in_dim(scale_a, piece_start, piece_cols, 0)
    piece_b = lax.dynamic_slice_in_dim(scale_b, piece_start, piece_cols, 0)
    levels = jnp.clip(summed * piece_a / piece_b, -127.0, 127.0).astype(jnp.bfloat16)
    level_blocks = _gather_blocks(levels, "tp", tp_count)
    all_levels = jnp.moveaxis(level_blocks, 0, 1).reshape(steps_n * samples, local_width)
    restored = all_levels.astype(jnp.float32) * local_b
    hidden = residual.reshape(steps_n * samples, local_width).astype(jnp.float32) + restored
    return hidden.astype(jnp.bfloat16).reshape(steps_n, samples, local_width)


def solution(mesh):
    return jax.shard_map(
        per_device,
        mesh=mesh,
        in_specs=(
            P(None, ("rep", "sub"), "tp"),
            P(None, ("rep", "tp"), None),
            P(None, ("rep", "sub"), "tp", None),
            P(("rep", "sub")),
            P(None, None, ("rep", "sub"), None),
            P("tp", "sub"),
            P(),
            P(),
            P(None, "rep", "sub"),
        ),
        out_specs=P(None, "rep", "sub"),
        check_vma=False,
    )
```

time: 298 us -> 116 us (0.39)
  waiting for transfers between devices: 187 us -> 20.5 us
  starting transfers between devices: 11.8 us -> 45.9 us
  blocking collectives: 32.8 us -> 2.03 us
  between operations: 13.7 us -> 0.58 us
  local copies, waits for them, and re-layouts: 32.1 us -> 23.2 us
    all_to_all x2 -> x0, waiting for transfers between devices: 126 us -> none  [the longest x1 89 us: per_device(): lax.all_to_all(spread_prompt, 'tp', split_axis=2, concat_axis=1, tiled=True)]
    reduce_scatter x1 -> x0, waiting for transfers between devices: 61 us -> none  [per_device(): summed = lax.psum_scatter(clipped, 'tp', scatter_dimension=1, tiled=True)]
    ppermute x0 -> x27, starting transfers between devices: none -> 45.9 us  [the longest x21 34.5 us: _exchange(): lax.ppermute(send, axis_name, [(i, (i + k) % count) for i in range(count)])]
    all_gather x1 -> x0, blocking collectives: 30.9 us -> none  [per_device(): all_levels = lax.all_gather(levels, 'tp', axis=1, tiled=True)]
    ppermute x0 -> x27, waiting for transfers between devices: none -> 20.5 us  [the longest x6 14.3 us: _gather_blocks(): other = lax.ppermute(cur, axis_name, [(i, i ^ k) for i in range(count)])]
    all_to_all x2 -> x0, starting transfers between devices: 11.8 us -> none  [the longest x1 7.25 us: per_device(): lax.all_to_all(spread_tail, 'tp', split_axis=2, concat_axis=1, tiled=True)]
    all_to_all x2 -> x0, local copies, waits for them, and re-layouts: 11.5 us -> none  [the longest x1 11.2 us: per_device(): lax.all_to_all(spread_prompt, 'tp', split_axis=2, concat_axis=1, tiled=True)]
    unnamed x17 -> x52, local copies, waits for them, and re-layouts: 15.7 us -> 11.9 us
  transfers between devices with their start and end apart: 3 -> 27, of which waited for: 3 -> 10; matrix products, arithmetic and copies ran while one was open for 5% -> 17% of each run, Pallas kernels for 0% -> 0%
where the time goes in v1:
time: 116 us; the launch traced here: 115 us
  starting transfers between devices  45.9 us (40%)
  local copies, waits for them, and re-layouts  23.2 us (20%)
  waiting for transfers between devices  20.5 us (18%)
  matrix products  19 us (16%)
  other arithmetic  4.12 us (4%)
  blocking collectives  2.03 us (2%)
    ppermute x21, starting transfers between devices, _exchange(): lax.ppermute(send, axis_name, [(i, (i + k) % count) for i in range(count)])  34.5 us
    ppermute x6, waiting for transfers between devices, _gather_blocks(): other = lax.ppermute(cur, axis_name, [(i, i ^ k) for i in range(count)])  14.3 us
    dot_general x1, matrix products, per_device(): jnp.einsum('rhd,hdf->rhf', head_rows_in, head_weights, preferred_element_...  12.9 us
    unnamed x52, local copies, waits for them, and re-layouts  11.9 us
    ppermute x6, starting transfers between devices, _gather_blocks(): other = lax.ppermute(cur, axis_name, [(i, i ^ k) for i in range(count)])  11.4 us
    ppermute x21, waiting for transfers between devices, _exchange(): lax.ppermute(send, axis_name, [(i, (i + k) % count) for i in range(count)])  6.26 us
    slice x1, local copies, waits for them, and re-layouts, per_device(): p_keys = prefix_kv[0].reshape(prefix_dev, kv_heads, DH)  4.77 us
    dot_general x1, matrix products, per_device(): jnp.einsum('sbkgp,pkd->sbkgd', p_w.astype(jnp.bfloat16), p_vals, preferre...  3.15 us
  transfers between devices with their start and end apart: 27, of which 10 were waited for; matrix products, arithmetic and copies ran while one was open for 17% of the time, Pallas kernels for 0%

profile of v1, /device:TPU:0, one launch (start us, length us, event | category | flops | bytes accessed | tf_op | source)
XLA Modules:
  0.0 115.3 jit_solution(6752972308053549501)
XLA Ops:
  0.0 2.9 %collective-permute-start = (bf16[1,2,4,2048]{3,2,1,0:T(4,128)(2,1)}, bf16[1,2,4,2048]{3,2,1,0:T(4,128)(2,1)S(1)}, u32[]{:S(2)}, u32[]{:S(2)}) collective-permute-start(bf16[1,2,4,2048]{3,2,1,0:T(4,128)(2,1)} %bitcast.187), channel_id=1, source_target_pairs={{0,2},{2,0},{4,6},{6,4},{8,10},{10,8},{12,14},{14,12},{1,3},{3,1},... | collective-permute-start | bytes 98312 | tf_op jit(solution)/shard_map/ppermute | solution.py:27
  2.9 0.8 reshape.209
  3.8 4.8 %fusion.48 = (bf16[1,1024,1024]{2,1,0:T(8,128)(2,1)}, bf16[1,1024,1024]{2,1,0:T(8,128)(2,1)}) fusion(bf16[2,1024,1024]{2,1,0:T(8,128)(2,1)} %param.10), kind=kLoop, calls=%fused_computation.129 | loop fusion | bytes 8388608 | tf_op jit(solution)/shard_map/slice | solution.py:68
  8.6 1.2 %fusion.49 = (bf16[1,4,128,1024]{3,2,1,0:T(8,128)(2,1)}, bf16[1,4,128,1024]{3,2,1,0:T(8,128)(2,1)S(1)}) fusion(bf16[2,4,128,1024]{3,2,1,0:T(8,128)(2,1)S(1)} %copy-done.3), kind=kLoop, calls=%fused_computation.130 | loop fusion | bytes 4194304 | tf_op jit(solution)/shard_map/slice | solution.py:71
  10.0 0.8 fusion.37
  10.9 1.6 %collective-permute-start.1 = (bf16[2,2,4,2048]{3,2,1,0:T(4,128)(2,1)S(1)}, bf16[2,2,4,2048]{3,2,1,0:T(4,128)(2,1)S(1)}, u32[]{:S(2)}, u32[]{:S(2)}) collective-permute-start(bf16[2,2,4,2048]{3,2,1,0:T(4,128)(2,1)S(1)} %maximum_select_fusion.4), channel_id=1, source_target_pairs={{0,4},{2,6},{4,0},{6,2},{8,12},{10,14},{12,8},{14,10},{1,5},{3,7},... | collective-permute-start | bytes 196616 | tf_op jit(solution)/shard_map/ppermute | solution.py:27
  12.6 2.6 %collective-permute-done.1 = bf16[2,2,4,2048]{3,2,1,0:T(4,128)(2,1)S(1)} collective-permute-done((bf16[2,2,4,2048]{3,2,1,0:T(4,128)(2,1)S(1)}, bf16[2,2,4,2048]{3,2,1,0:T(4,128)(2,1)S(1)}, u32[]{:S(2)}, u32[]{:S(2)}) %collective-permute-start.1) | collective-permute-done | bytes 65568 | tf_op jit(solution)/shard_map/ppermute | solution.py:27
  15.4 2.7 %collective-permute-start.2 = (bf16[4,2,4,2048]{3,2,1,0:T(4,128)(2,1)S(1)}, bf16[4,2,4,2048]{3,2,1,0:T(4,128)(2,1)S(1)}, u32[]{:S(2)}, u32[]{:S(2)}) collective-permute-start(bf16[4,2,4,2048]{3,2,1,0:T(4,128)(2,1)S(1)} %maximum_select_fusion.2), channel_id=1, source_target_pairs={{0,8},{2,10},{4,12},{6,14},{8,0},{10,2},{12,4},{14,6},{1,9},{3,11}... | collective-permute-start | bytes 393224 | tf_op jit(solution)/shard_map/ppermute | solution.py:27
  18.0 2.9 %copy.185 = bf16[1,1024,1024]{1,2,0:T(8,128)(2,1)S(1)} copy(bf16[1,1024,1024]{2,1,0:T(8,128)(2,1)} %get-tuple-element.7) | data formatting | bytes 4194304
  20.9 1.3 %copy.186 = bf16[1,4,128,1024]{2,3,1,0:T(8,128)(2,1)} copy(bf16[1,4,128,1024]{3,2,1,0:T(8,128)(2,1)S(1)} %get-tuple-element.10) | data formatting | bytes 2097152
  22.3 1.0 copy.151
  23.2 3.9 %copy.187 = bf16[1,1024,1024]{1,2,0:T(8,128)(2,1)} copy(bf16[1,1024,1024]{2,1,0:T(8,128)(2,1)} %get-tuple-element.8) | data formatting | bytes 4194304
  27.2 1.6 %copy.188 = bf16[1,4,128,1024]{2,3,1,0:T(8,128)(2,1)S(1)} copy(bf16[1,4,128,1024]{3,2,1,0:T(8,128)(2,1)} %get-tuple-element.9) | data formatting | bytes 2097152
  28.9 1.0 fusion.18
  29.9 1.1 reshape.207
  31.0 0.8 bitcast_reduce_fusion
  32.8 1.2 %copy-done = f32[8,2,4,16,1024]{4,3,2,1,0:T(8,128)} copy-done((f32[8,2,4,16,1024]{4,3,2,1,0:T(8,128)}, f32[8,2,4,16,1024]{4,3,2,1,0:T(8,128)S(1)}, u32[]{:S(2)}) %copy-start) | copy-done | bytes 4194328
  34.0 0.9 fusion.2
  35.6 3.2 %fusion.9 = f32[2,4,8,16,128]{4,3,1,0,2:T(8,128)S(1)} fusion(bf16[1024,8,128,1,1]{0,2,4,3,1:T(8,128)(2,1)S(1)} %bitcast.180, f32[8,2,4,16,1024]{4,3,2,1,0:T(8,128)} %copy-done, f32[2,4,8,16]{3,1,0,2:T(4,128)S(1)} %copy_maximum_fusion), kind=kOutput, calls=%fused_computation.11 | convolution fusion | flops 271581184 | bytes 6819840 | tf_op jit(solution)/shard_map/sbkgp,pkd->sbkgd/dot_general | solution.py:87
  38.8 0.6 fusion.14
  40.1 1.6 %collective-permute-start.11 = (f32[2,128]{1,0:T(2,128)S(1)}, f32[2,128]{1,0:T(2,128)S(1)}, u32[]{:S(2)}, u32[]{:S(2)}) collective-permute-start(f32[2,128]{1,0:T(2,128)S(1)} %bitcast.202), channel_id=1, source_target_pairs={{0,4},{2,6},{4,8},{6,10},{8,12},{10,14},{12,0},{14,2},{1,5},{3,7},... | collective-permute-start | bytes 3080 | tf_op jit(solution)/shard_map/ppermute | solution.py:46
  41.7 1.3 %collective-permute-start.12 = (f32[2,128]{1,0:T(2,128)S(1)}, f32[2,128]{1,0:T(2,128)S(1)}, u32[]{:S(2)}, u32[]{:S(2)}) collective-permute-start(f32[2,128]{1,0:T(2,128)S(1)} %bitcast.201), channel_id=1, source_target_pairs={{0,6},{2,8},{4,10},{6,12},{8,14},{10,0},{12,2},{14,4},{1,7},{3,9},... | collective-permute-start | bytes 3080 | tf_op jit(solution)/shard_map/ppermute | solution.py:46
  43.0 3.5 %collective-permute-start.13 = (f32[2,128]{1,0:T(2,128)S(1)}, f32[2,128]{1,0:T(2,128)S(1)}, u32[]{:S(2)}, u32[]{:S(2)}) collective-permute-start(f32[2,128]{1,0:T(2,128)S(1)} %bitcast.200), channel_id=1, source_target_pairs={{0,8},{2,10},{4,12},{6,14},{8,0},{10,2},{12,4},{14,6},{1,9},{3,11}... | collective-permute-start | bytes 3080 | tf_op jit(solution)/shard_map/ppermute | solution.py:46
  46.5 2.4 %collective-permute-start.15 = (f32[2,128]{1,0:T(2,128)S(1)}, f32[2,128]{1,0:T(2,128)S(1)}, u32[]{:S(2)}, u32[]{:S(2)}) collective-permute-start(f32[2,128]{1,0:T(2,128)S(1)} %bitcast.198), channel_id=1, source_target_pairs={{0,12},{2,14},{4,0},{6,2},{8,4},{10,6},{12,8},{14,10},{1,13},{3,15... | collective-permute-start | bytes 3080 | tf_op jit(solution)/shard_map/ppermute | solution.py:46
  48.9 1.5 %collective-permute-start.16 = (f32[2,128]{1,0:T(2,128)S(1)}, f32[2,128]{1,0:T(2,128)S(1)}, u32[]{:S(2)}, u32[]{:S(2)}) collective-permute-start(f32[2,128]{1,0:T(2,128)S(1)} %bitcast.197), channel_id=1, source_target_pairs={{0,14},{2,0},{4,2},{6,4},{8,6},{10,8},{12,10},{14,12},{1,15},{3,1}... | collective-permute-start | bytes 3080 | tf_op jit(solution)/shard_map/ppermute | solution.py:46
  51.9 3.1 %collective-permute-start.5 = (f32[2,4,16,128]{3,2,1,0:T(8,128)S(1)}, f32[2,4,16,128]{3,2,1,0:T(8,128)S(1)}, u32[]{:S(2)}, u32[]{:S(2)}) collective-permute-start(f32[2,4,16,128]{3,2,1,0:T(8,128)S(1)} %get-tuple-element.25), channel_id=1, source_target_pairs={{0,6},{2,8},{4,10},{6,12},{8,14},{10,0},{12,2},{14,4},{1,7},{3,9},... | collective-permute-start | bytes 196616 | tf_op jit(solution)/shard_map/ppermute | solution.py:46
  55.0 1.9 %collective-permute-start.6 = (f32[2,4,16,128]{3,2,1,0:T(8,128)S(1)}, f32[2,4,16,128]{3,2,1,0:T(8,128)S(1)}, u32[]{:S(2)}, u32[]{:S(2)}) collective-permute-start(f32[2,4,16,128]{3,2,1,0:T(8,128)S(1)} %get-tuple-element.24), channel_id=1, source_target_pairs={{0,8},{2,10},{4,12},{6,14},{8,0},{10,2},{12,4},{14,6},{1,9},{3,11}... | collective-permute-start | bytes 196616 | tf_op jit(solution)/shard_map/ppermute | solution.py:46
  57.0 0.6 collective-permute-start.7
  58.2 2.3 %collective-permute-start.8 = (f32[2,4,16,128]{3,2,1,0:T(8,128)S(1)}, f32[2,4,16,128]{3,2,1,0:T(8,128)S(1)}, u32[]{:S(2)}, u32[]{:S(2)}) collective-permute-start(f32[2,4,16,128]{3,2,1,0:T(8,128)S(1)} %get-tuple-element.22), channel_id=1, source_target_pairs={{0,12},{2,14},{4,0},{6,2},{8,4},{10,6},{12,8},{14,10},{1,13},{3,15... | collective-permute-start | bytes 196616 | tf_op jit(solution)/shard_map/ppermute | solution.py:46
  60.5 3.0 %collective-permute-start.9 = (f32[2,4,16,128]{3,2,1,0:T(8,128)S(1)}, f32[2,4,16,128]{3,2,1,0:T(8,128)S(1)}, u32[]{:S(2)}, u32[]{:S(2)}) collective-permute-start(f32[2,4,16,128]{3,2,1,0:T(8,128)S(1)} %get-tuple-element.21), channel_id=1, source_target_pairs={{0,14},{2,0},{4,2},{6,4},{8,6},{10,8},{12,10},{14,12},{1,15},{3,1}... | collective-permute-start | bytes 196616 | tf_op jit(solution)/shard_map/ppermute | solution.py:46
  63.9 1.5 %collective-permute-done.9 = f32[2,4,16,128]{3,2,1,0:T(8,128)S(1)} collective-permute-done((f32[2,4,16,128]{3,2,1,0:T(8,128)S(1)}, f32[2,4,16,128]{3,2,1,0:T(8,128)S(1)}, u32[]{:S(2)}, u32[]{:S(2)}) %collective-permute-start.9) | collective-permute-done | bytes 65568 | tf_op jit(solution)/shard_map/ppermute | solution.py:46
  65.8 2.0 %all_gather.3 = bf16[2,8,2048]{2,0,1:T(2,128)(2,1)S(1)} all-gather(bf16[2,4,2048]{2,0,1:T(2,128)(2,1)S(1)} %copy.159), channel_id=1, replica_groups=mesh['rep'=2,'tp'=8,'sub'=2] {'sub'}, dimensions={1}, use_global_device_ids=true | all-gather | bytes 98304 | tf_op jit(solution)/shard_map/all_gather | solution.py:131
  67.9 12.9 %fusion.8 = f32[16,8192]{1,0:T(8,128)S(1)} fusion(f32[8192]{0:T(1024)S(1)} %dynamic-slice-done, bf16[16,128,8192]{2,1,0:T(8,128)(2,1)} %bitcast.204, bf16[16,16,128]{2,1,0:T(8,128)(2,1)S(1)} %bitcast.196), kind=kOutput, calls=%fused_computation.10 | convolution fusion | flops 543031296 | bytes 34177024 | tf_op jit(solution)/shard_map/rhd,hdf->rhf/dot_general | solution.py:140
  81.7 1.6 %collective-permute-start.17 = (f32[16,1024]{1,0:T(8,128)S(1)}, f32[16,1024]{1,0:T(8,128)S(1)}, u32[]{:S(2)}, u32[]{:S(2)}) collective-permute-start(f32[16,1024]{1,0:T(8,128)S(1)} %bitcast.195), channel_id=1, source_target_pairs={{0,2},{2,4},{4,6},{6,8},{8,10},{10,12},{12,14},{14,0},{1,3},{3,5},... | collective-permute-start | bytes 196616 | tf_op jit(solution)/shard_map/ppermute | solution.py:46
  83.3 1.9 %collective-permute-start.18 = (f32[16,1024]{1,0:T(8,128)S(1)}, f32[16,1024]{1,0:T(8,128)S(1)}, u32[]{:S(2)}, u32[]{:S(2)}) collective-permute-start(f32[16,1024]{1,0:T(8,128)S(1)} %bitcast.194), channel_id=1, source_target_pairs={{0,4},{2,6},{4,8},{6,10},{8,12},{10,14},{12,0},{14,2},{1,5},{3,7},... | collective-permute-start | bytes 196616 | tf_op jit(solution)/shard_map/ppermute | solution.py:46
  85.6 2.6 %collective-permute-start.20 = (f32[16,1024]{1,0:T(8,128)S(1)}, f32[16,1024]{1,0:T(8,128)S(1)}, u32[]{:S(2)}, u32[]{:S(2)}) collective-permute-start(f32[16,1024]{1,0:T(8,128)S(1)} %bitcast.190), channel_id=1, source_target_pairs={{0,8},{2,10},{4,12},{6,14},{8,0},{10,2},{12,4},{14,6},{1,9},{3,11}... | collective-permute-start | bytes 196616 | tf_op jit(solution)/shard_map/ppermute | solution.py:46
  88.2 3.9 %collective-permute-start.21 = (f32[16,1024]{1,0:T(8,128)S(1)}, f32[16,1024]{1,0:T(8,128)S(1)}, u32[]{:S(2)}, u32[]{:S(2)}) collective-permute-start(f32[16,1024]{1,0:T(8,128)S(1)} %bitcast.191), channel_id=1, source_target_pairs={{0,10},{2,12},{4,14},{6,0},{8,2},{10,4},{12,6},{14,8},{1,11},{3,13... | collective-permute-start | bytes 196616 | tf_op jit(solution)/shard_map/ppermute | solution.py:46
  92.2 1.5 %collective-permute-start.23 = (f32[16,1024]{1,0:T(8,128)S(1)}, f32[16,1024]{1,0:T(8,128)S(1)}, u32[]{:S(2)}, u32[]{:S(2)}) collective-permute-start(f32[16,1024]{1,0:T(8,128)S(1)} %bitcast.192), channel_id=1, source_target_pairs={{0,14},{2,0},{4,2},{6,4},{8,6},{10,8},{12,10},{14,12},{1,15},{3,1}... | collective-permute-start | bytes 196616 | tf_op jit(solution)/shard_map/ppermute | solution.py:46
  93.8 1.2 %collective-permute-done.19 = f32[16,1024]{1,0:T(8,128)S(1)} collective-permute-done((f32[16,1024]{1,0:T(8,128)S(1)}, f32[16,1024]{1,0:T(8,128)S(1)}, u32[]{:S(2)}, u32[]{:S(2)}) %collective-permute-start.19) | collective-permute-done | bytes 65568 | tf_op jit(solution)/shard_map/ppermute | solution.py:46
  95.4 1.2 %collective-permute-done.21 = f32[16,1024]{1,0:T(8,128)S(1)} collective-permute-done((f32[16,1024]{1,0:T(8,128)S(1)}, f32[16,1024]{1,0:T(8,128)S(1)}, u32[]{:S(2)}, u32[]{:S(2)}) %collective-permute-start.21) | collective-permute-done | bytes 65568 | tf_op jit(solution)/shard_map/ppermute | solution.py:46
  96.6 1.6 %collective-permute-done.22 = f32[16,1024]{1,0:T(8,128)S(1)} collective-permute-done((f32[16,1024]{1,0:T(8,128)S(1)}, f32[16,1024]{1,0:T(8,128)S(1)}, u32[]{:S(2)}, u32[]{:S(2)}) %collective-permute-start.22) | collective-permute-done | bytes 65568 | tf_op jit(solution)/shard_map/ppermute | solution.py:46
  98.2 2.3 %collective-permute-start.24 = (bf16[1,16,1024]{2,1,0:T(8,128)(2,1)S(1)}, bf16[1,16,1024]{2,1,0:T(8,128)(2,1)S(1)}, u32[]{:S(2)}, u32[]{:S(2)}) collective-permute-start(bf16[1,16,1024]{2,1,0:T(8,128)(2,1)S(1)} %fusion.36), channel_id=1, source_target_pairs={{0,2},{2,0},{4,6},{6,4},{8,10},{10,8},{12,14},{14,12},{1,3},{3,1},... | collective-permute-start | bytes 98312 | tf_op jit(solution)/shard_map/ppermute | solution.py:27
  100.5 1.9 %collective-permute-done.24 = bf16[1,16,1024]{2,1,0:T(8,128)(2,1)S(1)} collective-permute-done((bf16[1,16,1024]{2,1,0:T(8,128)(2,1)S(1)}, bf16[1,16,1024]{2,1,0:T(8,128)(2,1)S(1)}, u32[]{:S(2)}, u32[]{:S(2)}) %collective-permute-start.24) | collective-permute-done | bytes 32800 | tf_op jit(solution)/shard_map/ppermute | solution.py:27
  102.4 1.2 %collective-permute-start.25 = (bf16[2,16,1024]{2,1,0:T(8,128)(2,1)S(1)}, bf16[2,16,1024]{2,1,0:T(8,128)(2,1)S(1)}, u32[]{:S(2)}, u32[]{:S(2)}) collective-permute-start(bf16[2,16,1024]{2,1,0:T(8,128)(2,1)S(1)} %maximum_select_fusion.5), channel_id=1, source_target_pairs={{0,4},{2,6},{4,0},{6,2},{8,12},{10,14},{12,8},{14,10},{1,5},{3,7},... | collective-permute-start | bytes 196616 | tf_op jit(solution)/shard_map/ppermute | solution.py:27
  103.6 3.2 %collective-permute-done.25 = bf16[2,16,1024]{2,1,0:T(8,128)(2,1)S(1)} collective-permute-done((bf16[2,16,1024]{2,1,0:T(8,128)(2,1)S(1)}, bf16[2,16,1024]{2,1,0:T(8,128)(2,1)S(1)}, u32[]{:S(2)}, u32[]{:S(2)}) %collective-permute-start.25) | collective-permute-done | bytes 65568 | tf_op jit(solution)/shard_map/ppermute | solution.py:27
  106.7 0.7 collective-permute-start.26
  107.5 6.6 %collective-permute-done.26 = bf16[4,16,1024]{2,1,0:T(8,128)(2,1)S(1)} collective-permute-done((bf16[4,16,1024]{2,1,0:T(8,128)(2,1)S(1)}, bf16[4,16,1024]{2,1,0:T(8,128)(2,1)S(1)}, u32[]{:S(2)}, u32[]{:S(2)}) %collective-permute-start.26) | collective-permute-done | bytes 131104 | tf_op jit(solution)/shard_map/ppermute | solution.py:27
  114.6 0.8 add_convert_fusion
  (131 shorter events, 8.4 us)
Async XLA Ops:
  0.0 10.8 %collective-permute-start = (bf16[1,2,4,2048]{3,2,1,0:T(4,128)(2,1)}, bf16[1,2,4,2048]{3,2,1,0:T(4,128)(2,1)S(1)}, u32[]{:S(2)}, u32[]{:S(2)}) collective-permute-start(bf16[1,2,4,2048]{3,2,1,0:T(4,128)(2,1)} %bitcast.187), channel_id=1, source_target_pairs={{0,2},{2,0},{4,6},{6,4},{8,10},{10,8},{12,14},{14,12},{1,3},{3,1},... | collective-permute-start | bytes 98312 | tf_op jit(solution)/shard_map/ppermute | solution.py:27
  3.8 4.8 %copy-start.3 = (bf16[2,4,128,1024]{3,2,1,0:T(8,128)(2,1)S(1)}, bf16[2,4,128,1024]{3,2,1,0:T(8,128)(2,1)}, u32[]{:S(2)}) copy-start(bf16[2,4,128,1024]{3,2,1,0:T(8,128)(2,1)} %param.11) | copy-start | bytes 6291460
  8.5 1.3 %copy-start.8 = (bf16[2,2,4,1024]{3,2,1,0:T(4,128)(2,1)S(1)}, bf16[2,2,4,1024]{3,2,1,0:T(4,128)(2,1)}, u32[]{:S(2)}) copy-start(bf16[2,2,4,1024]{3,2,1,0:T(4,128)(2,1)} %param.13) | copy-start | bytes 98308
  8.5 1.3 %copy-start.9 = (s32[128]{0:T(128)S(1)}, s32[128]{0:T(128)}, u32[]{:S(2)}) copy-start(s32[128]{0:T(128)} %param.15) | copy-start | bytes 1540
  8.5 2.3 %copy-start.7 = (bf16[2,4,2048]{2,1,0:T(4,128)(2,1)S(1)}, bf16[2,4,2048]{2,1,0:T(4,128)(2,1)}, u32[]{:S(2)}) copy-start(bf16[2,4,2048]{2,1,0:T(4,128)(2,1)} %param.9) | copy-start | bytes 98308
  8.6 4.0 %copy-start.10 = (s32[4]{0:T(128)S(1)}, s32[4]{0:T(128)}, u32[]{:S(2)}) copy-start(s32[4]{0:T(128)} %param.12) | copy-start | bytes 52
  10.0 18.9 %copy-start.5 = (f32[16384]{0:T(1024)}, f32[16384]{0:T(1024)S(1)}, u32[]{:S(2)}) copy-start(f32[16384]{0:T(1024)S(1)} %broadcast_bitcast_fusion.1) | copy-start | bytes 196612
  10.9 4.3 %collective-permute-start.1 = (bf16[2,2,4,2048]{3,2,1,0:T(4,128)(2,1)S(1)}, bf16[2,2,4,2048]{3,2,1,0:T(4,128)(2,1)S(1)}, u32[]{:S(2)}, u32[]{:S(2)}) collective-permute-start(bf16[2,2,4,2048]{3,2,1,0:T(4,128)(2,1)S(1)} %maximum_select_fusion.4), channel_id=1, source_target_pairs={{0,4},{2,6},{4,0},{6,2},{8,12},{10,14},{12,8},{14,10},{1,5},{3,7},... | collective-permute-start | bytes 196616 | tf_op jit(solution)/shard_map/ppermute | solution.py:27
  15.4 13.5 %collective-permute-start.2 = (bf16[4,2,4,2048]{3,2,1,0:T(4,128)(2,1)S(1)}, bf16[4,2,4,2048]{3,2,1,0:T(4,128)(2,1)S(1)}, u32[]{:S(2)}, u32[]{:S(2)}) collective-permute-start(bf16[4,2,4,2048]{3,2,1,0:T(4,128)(2,1)S(1)} %maximum_select_fusion.2), channel_id=1, source_target_pairs={{0,8},{2,10},{4,12},{6,14},{8,0},{10,2},{12,4},{14,6},{1,9},{3,11}... | collective-permute-start | bytes 393224 | tf_op jit(solution)/shard_map/ppermute | solution.py:27
  31.0 1.2 %copy-start.2 = (bf16[1,4,128,1024]{2,3,1,0:T(8,128)(2,1)S(1)}, bf16[1,4,128,1024]{2,3,1,0:T(8,128)(2,1)}, u32[]{:S(2)}) copy-start(bf16[1,4,128,1024]{2,3,1,0:T(8,128)(2,1)} %copy.186) | copy-start | bytes 3145732
  31.8 2.1 %copy-start = (f32[8,2,4,16,1024]{4,3,2,1,0:T(8,128)}, f32[8,2,4,16,1024]{4,3,2,1,0:T(8,128)S(1)}, u32[]{:S(2)}) copy-start(f32[8,2,4,16,1024]{4,3,2,1,0:T(8,128)S(1)} %get-tuple-element.41) | copy-start | bytes 12582916
  31.8 3.7 %copy-start.1 = (bf16[1,1024,1024]{1,2,0:T(8,128)(2,1)S(1)}, bf16[1,1024,1024]{1,2,0:T(8,128)(2,1)}, u32[]{:S(2)}) copy-start(bf16[1,1024,1024]{1,2,0:T(8,128)(2,1)} %copy.187) | copy-start | bytes 6291460
  38.7 29.1 %dynamic-slice-start = ((f32[16384]{0:T(1024)}, s32[]{:T(128)}), f32[8192]{0:T(1024)S(1)}, s32[]{:S(2)}) async-start(f32[16384]{0:T(1024)} %copy-done.5, s32[]{:T(128)} %select_n.225), calls=%async_computation | async-start | bytes 66048 | tf_op jit(solution)/shard_map/dynamic_slice | solution.py:138
  39.6 6.9 %collective-permute-start.10 = (f32[2,128]{1,0:T(2,128)S(1)}, f32[2,128]{1,0:T(2,128)S(1)}, u32[]{:S(2)}, u32[]{:S(2)}) collective-permute-start(f32[2,128]{1,0:T(2,128)S(1)} %bitcast.203), channel_id=1, source_target_pairs={{0,2},{2,4},{4,6},{6,8},{8,10},{10,12},{12,14},{14,0},{1,3},{3,5},... | collective-permute-start | bytes 3080 | tf_op jit(solution)/shard_map/ppermute | solution.py:46
  40.1 8.8 %collective-permute-start.11 = (f32[2,128]{1,0:T(2,128)S(1)}, f32[2,128]{1,0:T(2,128)S(1)}, u32[]{:S(2)}, u32[]{:S(2)}) collective-permute-start(f32[2,128]{1,0:T(2,128)S(1)} %bitcast.202), channel_id=1, source_target_pairs={{0,4},{2,6},{4,8},{6,10},{8,12},{10,14},{12,0},{14,2},{1,5},{3,7},... | collective-permute-start | bytes 3080 | tf_op jit(solution)/shard_map/ppermute | solution.py:46
  41.7 8.8 %collective-permute-start.12 = (f32[2,128]{1,0:T(2,128)S(1)}, f32[2,128]{1,0:T(2,128)S(1)}, u32[]{:S(2)}, u32[]{:S(2)}) collective-permute-start(f32[2,128]{1,0:T(2,128)S(1)} %bitcast.201), channel_id=1, source_target_pairs={{0,6},{2,8},{4,10},{6,12},{8,14},{10,0},{12,2},{14,4},{1,7},{3,9},... | collective-permute-start | bytes 3080 | tf_op jit(solution)/shard_map/ppermute | solution.py:46
  43.0 8.3 %collective-permute-start.13 = (f32[2,128]{1,0:T(2,128)S(1)}, f32[2,128]{1,0:T(2,128)S(1)}, u32[]{:S(2)}, u32[]{:S(2)}) collective-permute-start(f32[2,128]{1,0:T(2,128)S(1)} %bitcast.200), channel_id=1, source_target_pairs={{0,8},{2,10},{4,12},{6,14},{8,0},{10,2},{12,4},{14,6},{1,9},{3,11}... | collective-permute-start | bytes 3080 | tf_op jit(solution)/shard_map/ppermute | solution.py:46
  46.5 5.4 %collective-permute-start.14 = (f32[2,128]{1,0:T(2,128)S(1)}, f32[2,128]{1,0:T(2,128)S(1)}, u32[]{:S(2)}, u32[]{:S(2)}) collective-permute-start(f32[2,128]{1,0:T(2,128)S(1)} %bitcast.199), channel_id=1, source_target_pairs={{0,10},{2,12},{4,14},{6,0},{8,2},{10,4},{12,6},{14,8},{1,11},{3,13... | collective-permute-start | bytes 3080 | tf_op jit(solution)/shard_map/ppermute | solution.py:46
  46.5 8.6 %collective-permute-start.15 = (f32[2,128]{1,0:T(2,128)S(1)}, f32[2,128]{1,0:T(2,128)S(1)}, u32[]{:S(2)}, u32[]{:S(2)}) collective-permute-start(f32[2,128]{1,0:T(2,128)S(1)} %bitcast.198), channel_id=1, source_target_pairs={{0,12},{2,14},{4,0},{6,2},{8,4},{10,6},{12,8},{14,10},{1,13},{3,15... | collective-permute-start | bytes 3080 | tf_op jit(solution)/shard_map/ppermute | solution.py:46
  48.9 8.0 %collective-permute-start.16 = (f32[2,128]{1,0:T(2,128)S(1)}, f32[2,128]{1,0:T(2,128)S(1)}, u32[]{:S(2)}, u32[]{:S(2)}) collective-permute-start(f32[2,128]{1,0:T(2,128)S(1)} %bitcast.197), channel_id=1, source_target_pairs={{0,14},{2,0},{4,2},{6,4},{8,6},{10,8},{12,10},{14,12},{1,15},{3,1}... | collective-permute-start | bytes 3080 | tf_op jit(solution)/shard_map/ppermute | solution.py:46
  50.5 7.7 %collective-permute-start.3 = (f32[2,4,16,128]{3,2,1,0:T(8,128)S(1)}, f32[2,4,16,128]{3,2,1,0:T(8,128)S(1)}, u32[]{:S(2)}, u32[]{:S(2)}) collective-permute-start(f32[2,4,16,128]{3,2,1,0:T(8,128)S(1)} %get-tuple-element.27), channel_id=1, source_target_pairs={{0,2},{2,4},{4,6},{6,8},{8,10},{10,12},{12,14},{14,0},{1,3},{3,5},... | collective-permute-start | bytes 196616 | tf_op jit(solution)/shard_map/ppermute | solution.py:46
  51.3 9.3 %collective-permute-start.4 = (f32[2,4,16,128]{3,2,1,0:T(8,128)S(1)}, f32[2,4,16,128]{3,2,1,0:T(8,128)S(1)}, u32[]{:S(2)}, u32[]{:S(2)}) collective-permute-start(f32[2,4,16,128]{3,2,1,0:T(8,128)S(1)} %get-tuple-element.26), channel_id=1, source_target_pairs={{0,4},{2,6},{4,8},{6,10},{8,12},{10,14},{12,0},{14,2},{1,5},{3,7},... | collective-permute-start | bytes 196616 | tf_op jit(solution)/shard_map/ppermute | solution.py:46
  51.9 11.7 %collective-permute-start.5 = (f32[2,4,16,128]{3,2,1,0:T(8,128)S(1)}, f32[2,4,16,128]{3,2,1,0:T(8,128)S(1)}, u32[]{:S(2)}, u32[]{:S(2)}) collective-permute-start(f32[2,4,16,128]{3,2,1,0:T(8,128)S(1)} %get-tuple-element.25), channel_id=1, source_target_pairs={{0,6},{2,8},{4,10},{6,12},{8,14},{10,0},{12,2},{14,4},{1,7},{3,9},... | collective-permute-start | bytes 196616 | tf_op jit(solution)/shard_map/ppermute | solution.py:46
  55.0 8.5 %collective-permute-start.6 = (f32[2,4,16,128]{3,2,1,0:T(8,128)S(1)}, f32[2,4,16,128]{3,2,1,0:T(8,128)S(1)}, u32[]{:S(2)}, u32[]{:S(2)}) collective-permute-start(f32[2,4,16,128]{3,2,1,0:T(8,128)S(1)} %get-tuple-element.24), channel_id=1, source_target_pairs={{0,8},{2,10},{4,12},{6,14},{8,0},{10,2},{12,4},{14,6},{1,9},{3,11}... | collective-permute-start | bytes 196616 | tf_op jit(solution)/shard_map/ppermute | solution.py:46
  57.0 6.6 %collective-permute-start.7 = (f32[2,4,16,128]{3,2,1,0:T(8,128)S(1)}, f32[2,4,16,128]{3,2,1,0:T(8,128)S(1)}, u32[]{:S(2)}, u32[]{:S(2)}) collective-permute-start(f32[2,4,16,128]{3,2,1,0:T(8,128)S(1)} %get-tuple-element.23), channel_id=1, source_target_pairs={{0,10},{2,12},{4,14},{6,0},{8,2},{10,4},{12,6},{14,8},{1,11},{3,13... | collective-permute-start | bytes 196616 | tf_op jit(solution)/shard_map/ppermute | solution.py:46
  58.2 5.7 %collective-permute-start.8 = (f32[2,4,16,128]{3,2,1,0:T(8,128)S(1)}, f32[2,4,16,128]{3,2,1,0:T(8,128)S(1)}, u32[]{:S(2)}, u32[]{:S(2)}) collective-permute-start(f32[2,4,16,128]{3,2,1,0:T(8,128)S(1)} %get-tuple-element.22), channel_id=1, source_target_pairs={{0,12},{2,14},{4,0},{6,2},{8,4},{10,6},{12,8},{14,10},{1,13},{3,15... | collective-permute-start | bytes 196616 | tf_op jit(solution)/shard_map/ppermute | solution.py:46
  60.5 4.9 %collective-permute-start.9 = (f32[2,4,16,128]{3,2,1,0:T(8,128)S(1)}, f32[2,4,16,128]{3,2,1,0:T(8,128)S(1)}, u32[]{:S(2)}, u32[]{:S(2)}) collective-permute-start(f32[2,4,16,128]{3,2,1,0:T(8,128)S(1)} %get-tuple-element.21), channel_id=1, source_target_pairs={{0,14},{2,0},{4,2},{6,4},{8,6},{10,8},{12,10},{14,12},{1,15},{3,1}... | collective-permute-start | bytes 196616 | tf_op jit(solution)/shard_map/ppermute | solution.py:46
  67.9 17.3 %copy-start.11 = (s32[128]{0:T(128)S(1)}, s32[128]{0:T(128)}, u32[]{:S(2)}) copy-start(s32[128]{0:T(128)} %param.16) | copy-start | bytes 1540
  67.9 25.8 %copy-start.6 = (f32[16384]{0:T(1024)S(1)}, f32[16384]{0:T(1024)}, u32[]{:S(2)}) copy-start(f32[16384]{0:T(1024)} %copy-done.5) | copy-start | bytes 196612
  80.8 33.8 %copy-start.4 = (bf16[2,8,8192]{2,1,0:T(8,128)(2,1)S(1)}, bf16[2,8,8192]{2,1,0:T(8,128)(2,1)}, u32[]{:S(2)}) copy-start(bf16[2,8,8192]{2,1,0:T(8,128)(2,1)} %param.17) | copy-start | bytes 786436
  81.7 10.4 %collective-permute-start.17 = (f32[16,1024]{1,0:T(8,128)S(1)}, f32[16,1024]{1,0:T(8,128)S(1)}, u32[]{:S(2)}, u32[]{:S(2)}) collective-permute-start(f32[16,1024]{1,0:T(8,128)S(1)} %bitcast.195), channel_id=1, source_target_pairs={{0,2},{2,4},{4,6},{6,8},{8,10},{10,12},{12,14},{14,0},{1,3},{3,5},... | collective-permute-start | bytes 196616 | tf_op jit(solution)/shard_map/ppermute | solution.py:46
  83.3 8.8 %collective-permute-start.18 = (f32[16,1024]{1,0:T(8,128)S(1)}, f32[16,1024]{1,0:T(8,128)S(1)}, u32[]{:S(2)}, u32[]{:S(2)}) collective-permute-start(f32[16,1024]{1,0:T(8,128)S(1)} %bitcast.194), channel_id=1, source_target_pairs={{0,4},{2,6},{4,8},{6,10},{8,12},{10,14},{12,0},{14,2},{1,5},{3,7},... | collective-permute-start | bytes 196616 | tf_op jit(solution)/shard_map/ppermute | solution.py:46
  85.2 9.7 %collective-permute-start.19 = (f32[16,1024]{1,0:T(8,128)S(1)}, f32[16,1024]{1,0:T(8,128)S(1)}, u32[]{:S(2)}, u32[]{:S(2)}) collective-permute-start(f32[16,1024]{1,0:T(8,128)S(1)} %bitcast.189), channel_id=1, source_target_pairs={{0,6},{2,8},{4,10},{6,12},{8,14},{10,0},{12,2},{14,4},{1,7},{3,9},... | collective-permute-start | bytes 196616 | tf_op jit(solution)/shard_map/ppermute | solution.py:46
  85.6 9.9 %collective-permute-start.20 = (f32[16,1024]{1,0:T(8,128)S(1)}, f32[16,1024]{1,0:T(8,128)S(1)}, u32[]{:S(2)}, u32[]{:S(2)}) collective-permute-start(f32[16,1024]{1,0:T(8,128)S(1)} %bitcast.190), channel_id=1, source_target_pairs={{0,8},{2,10},{4,12},{6,14},{8,0},{10,2},{12,4},{14,6},{1,9},{3,11}... | collective-permute-start | bytes 196616 | tf_op jit(solution)/shard_map/ppermute | solution.py:46
  88.2 8.4 %collective-permute-start.21 = (f32[16,1024]{1,0:T(8,128)S(1)}, f32[16,1024]{1,0:T(8,128)S(1)}, u32[]{:S(2)}, u32[]{:S(2)}) collective-permute-start(f32[16,1024]{1,0:T(8,128)S(1)} %bitcast.191), channel_id=1, source_target_pairs={{0,10},{2,12},{4,14},{6,0},{8,2},{10,4},{12,6},{14,8},{1,11},{3,13... | collective-permute-start | bytes 196616 | tf_op jit(solution)/shard_map/ppermute | solution.py:46
  92.1 6.1 %collective-permute-start.22 = (f32[16,1024]{1,0:T(8,128)S(1)}, f32[16,1024]{1,0:T(8,128)S(1)}, u32[]{:S(2)}, u32[]{:S(2)}) collective-permute-start(f32[16,1024]{1,0:T(8,128)S(1)} %bitcast.193), channel_id=1, source_target_pairs={{0,12},{2,14},{4,0},{6,2},{8,4},{10,6},{12,8},{14,10},{1,13},{3,15... | collective-permute-start | bytes 196616 | tf_op jit(solution)/shard_map/ppermute | solution.py:46
  92.2 6.0 %collective-permute-start.23 = (f32[16,1024]{1,0:T(8,128)S(1)}, f32[16,1024]{1,0:T(8,128)S(1)}, u32[]{:S(2)}, u32[]{:S(2)}) collective-permute-start(f32[16,1024]{1,0:T(8,128)S(1)} %bitcast.192), channel_id=1, source_target_pairs={{0,14},{2,0},{4,2},{6,4},{8,6},{10,8},{12,10},{14,12},{1,15},{3,1}... | collective-permute-start | bytes 196616 | tf_op jit(solution)/shard_map/ppermute | solution.py:46
  98.2 4.2 %collective-permute-start.24 = (bf16[1,16,1024]{2,1,0:T(8,128)(2,1)S(1)}, bf16[1,16,1024]{2,1,0:T(8,128)(2,1)S(1)}, u32[]{:S(2)}, u32[]{:S(2)}) collective-permute-start(bf16[1,16,1024]{2,1,0:T(8,128)(2,1)S(1)} %fusion.36), channel_id=1, source_target_pairs={{0,2},{2,0},{4,6},{6,4},{8,10},{10,8},{12,14},{14,12},{1,3},{3,1},... | collective-permute-start | bytes 98312 | tf_op jit(solution)/shard_map/ppermute | solution.py:27
  102.4 4.3 %collective-permute-start.25 = (bf16[2,16,1024]{2,1,0:T(8,128)(2,1)S(1)}, bf16[2,16,1024]{2,1,0:T(8,128)(2,1)S(1)}, u32[]{:S(2)}, u32[]{:S(2)}) collective-permute-start(bf16[2,16,1024]{2,1,0:T(8,128)(2,1)S(1)} %maximum_select_fusion.5), channel_id=1, source_target_pairs={{0,4},{2,6},{4,0},{6,2},{8,12},{10,14},{12,8},{14,10},{1,5},{3,7},... | collective-permute-start | bytes 196616 | tf_op jit(solution)/shard_map/ppermute | solution.py:27
  106.7 7.3 %collective-permute-start.26 = (bf16[4,16,1024]{2,1,0:T(8,128)(2,1)S(1)}, bf16[4,16,1024]{2,1,0:T(8,128)(2,1)S(1)}, u32[]{:S(2)}, u32[]{:S(2)}) collective-permute-start(bf16[4,16,1024]{2,1,0:T(8,128)(2,1)S(1)} %maximum_select_fusion.3), channel_id=1, source_target_pairs={{0,8},{2,10},{4,12},{6,14},{8,0},{10,2},{12,4},{14,6},{1,9},{3,11}... | collective-permute-start | bytes 393224 | tf_op jit(solution)/shard_map/ppermute | solution.py:27

commit v2 on v1

--- a/solution.py
+++ b/solution.py
@@ -62,33 +62,108 @@
     tail_dev = tail_kv.shape[2]
     score_scale = 1.0 / math.sqrt(DH)
 
-    q_blocks = _gather_blocks(queries, "tp", tp_count)
-    q_all = jnp.moveaxis(q_blocks, 0, 2).reshape(steps_n, rows_dev, kv_heads, group, DH)
-
-    p_keys = prefix_kv[0].reshape(prefix_dev, kv_heads, DH)
-    p_vals = prefix_kv[1].reshape(prefix_dev, kv_heads, DH)
-    t_keys = tail_kv[0].reshape(rows_dev, tail_dev, kv_heads, DH)
-    t_vals = tail_kv[1].reshape(rows_dev, tail_dev, kv_heads, DH)
+    if tp_count <= 8 and heads_dev % group == 0:
+        got_numer, got_peak, got_mass = _partials_by_shift(
+            queries, prefix_kv, tail_kv, tail_lengths, tp_count, tp_rank, group
+        )
+    else:
+        got_numer, got_peak, got_mass = _partials_vectorized(
+            queries, prefix_kv, tail_kv, tail_lengths, tp_count, tp_rank, group
+        )
+    return _finish(
+        queries, fresh_kv, out_weight, scale_in, scale_out, residual,
+        got_numer, got_peak, got_mass, tp_count, tp_rank, sub_rank, group,
+    )
+
+
+def _local_partial(q, keys, vals, t_keys, t_vals, t_live):
+    score_scale = 1.0 / math.sqrt(DH)
     p_scores = (
-        jnp.einsum("sbkgd,pkd->sbkgp", q_all, p_keys, preferred_element_type=jnp.float32)
+        jnp.einsum("sbkgd,pkd->sbkgp", q, keys, preferred_element_type=jnp.float32) * score_scale
+    )
+    t_scores = (
+        jnp.einsum("sbkgd,btkd->sbkgt", q, t_keys, preferred_element_type=jnp.float32)
         * score_scale
     )
-    t_scores = (
-        jnp.einsum("sbkgd,btkd->sbkgt", q_all, t_keys, preferred_element_type=jnp.float32)
-        * score_scale
-    )
-    t_pos = tp_rank * tail_dev + jnp.arange(tail_dev)
-    t_live = t_pos[None, :] < tail_lengths[:, None]
     t_scores = jnp.where(t_live[None, :, None, None, :], t_scores, NEG_FILL)
     loc_peak = jnp.maximum(p_scores.max(-1), t_scores.max(-1))
     p_w = jnp.exp(p_scores - loc_peak[..., None])
     t_w = jnp.exp(t_scores - loc_peak[..., None])
     loc_mass = p_w.sum(-1) + t_w.sum(-1)
     loc_numer = jnp.einsum(
-        "sbkgp,pkd->sbkgd", p_w.astype(jnp.bfloat16), p_vals, preferred_element_type=jnp.float32
+        "sbkgp,pkd->sbkgd", p_w.astype(jnp.bfloat16), vals, preferred_element_type=jnp.float32
     )
     loc_numer = loc_numer + jnp.einsum(
         "sbkgt,btkd->sbkgd", t_w.astype(jnp.bfloat16), t_vals, preferred_element_type=jnp.float32
+    )
+    return loc_numer, loc_peak, loc_mass
+
+
+def _partials_by_shift(queries, prefix_kv, tail_kv, tail_lengths, tp_count, tp_rank, group):
+    steps_n, rows_dev, width_dev = queries.shape
+    heads_dev = width_dev // DH
+    kv_blk = heads_dev // group
+    prefix_dev = prefix_kv.shape[1]
+    tail_dev = tail_kv.shape[2]
+    t_pos = tp_rank * tail_dev + jnp.arange(tail_dev)
+    t_live = t_pos[None, :] < tail_lengths[:, None]
+    n_rows = steps_n * rows_dev * heads_dev
+    n_stat = -(-2 * n_rows // DH)
+    got = []
+    for shift in range(tp_count):
+        src = (tp_rank + shift) % tp_count
+        if shift == 0:
+            q = queries
+        else:
+            q = lax.ppermute(
+                queries, "tp", [(i, (i - shift) % tp_count) for i in range(tp_count)]
+            )
+        col = src * (kv_blk * DH)
+        keys = lax.dynamic_slice_in_dim(prefix_kv[0], col, kv_blk * DH, 1)
+        vals = lax.dynamic_slice_in_dim(prefix_kv[1], col, kv_blk * DH, 1)
+        t_keys = lax.dynamic_slice_in_dim(tail_kv[0], col, kv_blk * DH, 2)
+        t_vals = lax.dynamic_slice_in_dim(tail_kv[1], col, kv_blk * DH, 2)
+        numer, peak, mass = _local_partial(
+            q.reshape(steps_n, rows_dev, kv_blk, group, DH),
+            keys.reshape(prefix_dev, kv_blk, DH),
+            vals.reshape(prefix_dev, kv_blk, DH),
+            t_keys.reshape(rows_dev, tail_dev, kv_blk, DH),
+            t_vals.reshape(rows_dev, tail_dev, kv_blk, DH),
+            t_live,
+        )
+        stats = jnp.stack([peak.reshape(-1), mass.reshape(-1)]).reshape(-1)
+        stats = jnp.pad(stats, (0, n_stat * DH - 2 * n_rows)).reshape(n_stat, DH)
+        packed = jnp.concatenate([numer.reshape(n_rows, DH), stats], axis=0)
+        if shift != 0:
+            packed = lax.ppermute(
+                packed, "tp", [(i, (i + shift) % tp_count) for i in range(tp_count)]
+            )
+        got.append(packed)
+    got = jnp.stack(got)
+    got_numer = got[:, :n_rows].reshape(tp_count, steps_n, rows_dev, heads_dev, DH)
+    got_stats = got[:, n_rows:].reshape(tp_count, -1)[:, : 2 * n_rows]
+    got_stats = got_stats.reshape(tp_count, 2, steps_n, rows_dev, heads_dev)
+    return got_numer, got_stats[:, 0], got_stats[:, 1]
+
+
+def _partials_vectorized(queries, prefix_kv, tail_kv, tail_lengths, tp_count, tp_rank, group):
+    steps_n, rows_dev, width_dev = queries.shape
+    heads_dev = width_dev // DH
+    kv_heads = prefix_kv.shape[2] // DH
+    prefix_dev = prefix_kv.shape[1]
+    tail_dev = tail_kv.shape[2]
+    q_blocks = _gather_blocks(queries, "tp", tp_count)
+    q_all = jnp.moveaxis(q_blocks, 0, 2).reshape(steps_n, rows_dev, kv_heads, group, DH)
+
+    t_pos = tp_rank * tail_dev + jnp.arange(tail_dev)
+    t_live = t_pos[None, :] < tail_lengths[:, None]
+    loc_numer, loc_peak, loc_mass = _local_partial(
+        q_all,
+        prefix_kv[0].reshape(prefix_dev, kv_heads, DH),
+        prefix_kv[1].reshape(prefix_dev, kv_heads, DH),
+        tail_kv[0].reshape(rows_dev, tail_dev, kv_heads, DH),
+        tail_kv[1].reshape(rows_dev, tail_dev, kv_heads, DH),
+        t_live,
     )
 
     def by_owner(x):
@@ -100,9 +175,17 @@
         (by_owner(loc_numer), stats.reshape(tp_count, 2, -1)), "tp", tp_count
     )
     got_stats = got_stats.reshape(tp_count, 2, steps_n, rows_dev, heads_dev)
-    got_peak = got_stats[:, 0]
-    got_mass = got_stats[:, 1]
-
+    return got_numer, got_stats[:, 0], got_stats[:, 1]
+
+
+def _finish(
+    queries, fresh_kv, out_weight, scale_in, scale_out, residual,
+    got_numer, got_peak, got_mass, tp_count, tp_rank, sub_rank, group,
+):
+    steps_n, rows_dev, width_dev = queries.shape
+    heads_dev = width_dev // DH
+    kv_heads = fresh_kv.shape[3] // DH
+    score_scale = 1.0 / math.sqrt(DH)
     own_query = queries.reshape(steps_n, rows_dev, heads_dev, DH)
     f_kv = fresh_kv.reshape(2, steps_n, rows_dev, kv_heads, DH)
     if group % heads_dev == 0:

time: 116 us -> 147 us (1.27)
  matrix products: 19 us -> 44 us
  waiting for transfers between devices: 20.5 us -> 31.7 us
  starting transfers between devices: 45.9 us -> 35.6 us
  other arithmetic: 4.12 us -> 13 us
  local copies, waits for them, and re-layouts: 23.2 us -> 18.7 us
    ppermute x21 -> x7, starting transfers between devices: 34.5 us -> 7.84 us  [_exchange(): lax.ppermute(send, axis_name, [(i, (i + k) % count) for i in range(count)])]
    dot_general x7 -> x35, matrix products: 19 us -> 44 us  [the longest x8 14.1 us: _local_partial(): jnp.einsum('sbkgp,pkd->sbkgd', p_w.astype(jnp.bfloat16), vals, preferred_...]
    ppermute x0 -> x14, starting transfers between devices: none -> 20.5 us  [the longest x7 14.6 us: _partials_by_shift(): lax.ppermute(queries, 'tp', [(i, (i - shift) % tp_count) for i in range(t...]
    ppermute x0 -> x14, waiting for transfers between devices: none -> 18.8 us  [the longest x7 18.8 us: _partials_by_shift(): lax.ppermute(packed, 'tp', [(i, (i + shift) % tp_count) for i in range(tp...]
    unnamed x52 -> x67, local copies, waits for them, and re-layouts: 11.9 us -> 0.59 us
    ppermute x6 -> x3, waiting for transfers between devices: 14.3 us -> 7.59 us  [_gather_blocks(): other = lax.ppermute(cur, axis_name, [(i, i ^ k) for i in range(count)])]
    max x1 -> x17, local copies, waits for them, and re-layouts: 0.02 us -> 6.43 us  [the longest x16 6.35 us: _local_partial(): loc_peak = jnp.maximum(p_scores.max(-1), t_scores.max(-1))]
    ppermute x6 -> x3, starting transfers between devices: 11.4 us -> 7.22 us  [_gather_blocks(): other = lax.ppermute(cur, axis_name, [(i, i ^ k) for i in range(count)])]
  transfers between devices with their start and end apart: 27 -> 24, of which waited for: 10 -> 9; matrix products, arithmetic and copies ran while one was open for 17% -> 34% of each run, Pallas kernels for 0% -> 0%
where the time goes in v2:
time: 147 us; the launch traced here: 146 us
  matrix products  44 us (30%)
  starting transfers between devices  35.6 us (24%)
  waiting for transfers between devices  31.7 us (22%)
  local copies, waits for them, and re-layouts  18.7 us (13%)
  other arithmetic  13 us (9%)
  blocking collectives  2.03 us (1%)
    ppermute x7, waiting for transfers between devices, _partials_by_shift(): lax.ppermute(packed, 'tp', [(i, (i + shift) % tp_count) for i in range(tp...  18.8 us
    ppermute x7, starting transfers between devices, _partials_by_shift(): lax.ppermute(queries, 'tp', [(i, (i - shift) % tp_count) for i in range(t...  14.6 us
    dot_general x8, matrix products, _local_partial(): jnp.einsum('sbkgp,pkd->sbkgd', p_w.astype(jnp.bfloat16), vals, preferred_...  14.1 us
    dot_general x1, matrix products, _finish(): jnp.einsum('rhd,hdf->rhf', head_rows_in, head_weights, preferred_element_...  12.9 us
    dot_general x8, matrix products, _local_partial(): jnp.einsum('sbkgd,btkd->sbkgt', q, t_keys, preferred_element_type=jnp.flo...  10.5 us
    ppermute x7, starting transfers between devices, _exchange(): lax.ppermute(send, axis_name, [(i, (i + k) % count) for i in range(count)])  7.84 us
    ppermute x3, waiting for transfers between devices, _gather_blocks(): other = lax.ppermute(cur, axis_name, [(i, i ^ k) for i in range(count)])  7.59 us
    ppermute x3, starting transfers between devices, _gather_blocks(): other = lax.ppermute(cur, axis_name, [(i, i ^ k) for i in range(count)])  7.22 us
  transfers between devices with their start and end apart: 24, of which 9 were waited for; matrix products, arithmetic and copies ran while one was open for 34% of the time, Pallas kernels for 0%

profile of v2, /device:TPU:0, one launch (start us, length us, event | category | flops | bytes accessed | tf_op | source)
XLA Modules:
  0.0 146.1 jit_solution(5079163801472414439)
XLA Ops:
  0.0 4.0 %collective-permute-start.8 = (bf16[2,4,2048]{2,1,0:T(4,128)(2,1)}, bf16[2,4,2048]{2,1,0:T(4,128)(2,1)S(1)}, u32[]{:S(2)}, u32[]{:S(2)}) collective-permute-start(bf16[2,4,2048]{2,1,0:T(4,128)(2,1)} %param.9), channel_id=1, source_target_pairs={{0,6},{2,8},{4,10},{6,12},{8,14},{10,0},{12,2},{14,4},{1,7},{3,9},... | collective-permute-start | bytes 98312 | tf_op jit(solution)/shard_map/ppermute | solution.py:118
  4.0 2.6 %collective-permute-start.6 = (bf16[2,4,2048]{2,1,0:T(4,128)(2,1)}, bf16[2,4,2048]{2,1,0:T(4,128)(2,1)}, u32[]{:S(2)}, u32[]{:S(2)}) collective-permute-start(bf16[2,4,2048]{2,1,0:T(4,128)(2,1)} %param.9), channel_id=1, source_target_pairs={{0,8},{2,10},{4,12},{6,14},{8,0},{10,2},{12,4},{14,6},{1,9},{3,11}... | collective-permute-start | bytes 98312 | tf_op jit(solution)/shard_map/ppermute | solution.py:118
  6.5 1.3 collective-permute-start.4
  7.9 1.3 collective-permute-start.2
  10.7 2.9 %fusion.244 = (bf16[1,4,128,1024]{3,2,1,0:T(8,128)(2,1)S(1)}, bf16[1,4,128,1024]{3,2,1,0:T(8,128)(2,1)}) fusion(bf16[2,4,128,1024]{3,2,1,0:T(8,128)(2,1)} %param.11), kind=kLoop, calls=%fused_computation.358 | loop fusion | bytes 4194304 | tf_op jit(solution)/shard_map/slice | solution.py:125
  13.6 1.8 %fusion.243 = (bf16[1,1024,1024]{2,1,0:T(8,128)(2,1)}, bf16[1,1024,1024]{2,1,0:T(8,128)(2,1)S(1)}) fusion(bf16[2,1024,1024]{2,1,0:T(8,128)(2,1)S(1)} %copy-done), kind=kLoop, calls=%fused_computation.357 | loop fusion | bytes 8388608 | tf_op jit(solution)/shard_map/slice | solution.py:123
  15.5 1.0 fusion.245
  16.5 1.2 fusion.246
  18.3 1.3 fusion.43
  19.6 1.4 convolution_bitcast_fusion.15
  23.4 1.6 %collective-permute-start.10 = (bf16[2,4,2048]{2,1,0:T(4,128)(2,1)}, bf16[2,4,2048]{2,1,0:T(4,128)(2,1)S(1)}, u32[]{:S(2)}, u32[]{:S(2)}) collective-permute-start(bf16[2,4,2048]{2,1,0:T(4,128)(2,1)} %param.9), channel_id=1, source_target_pairs={{0,4},{2,6},{4,8},{6,10},{8,12},{10,14},{12,0},{14,2},{1,5},{3,7},... | collective-permute-start | bytes 98312 | tf_op jit(solution)/shard_map/ppermute | solution.py:118
  25.0 1.7 %fusion.260 = (f32[2,4,16]{2,0,1:T(2,128)S(1)}, f32[2,4,1,16,128]{4,3,0,1,2:T(8,128)}) fusion(bf16[2,4,16,128]{3,2,1,0:T(8,128)(2,1)S(1)} %reshape.1149, bf16[1,4,128,1024]{3,2,1,0:T(8,128)(2,1)} %get-tuple-element.8, s32[]{:T(128)S(6)} %select_n.271, pred[4,128]{1,0:T(4,128)(4,1)S(1)} %broadcast_compare_fusion), kind=kOutput, calls=%fused_computation.374 | convolution fusion | flops 4243328 | bytes 230404 | tf_op jit(solution)/shard_map/sbkgd,btkd->sbkgt/dot_general | solution.py:85
  27.0 1.9 %convolution_bitcast_fusion.8 = f32[2,4,1,16,128]{4,3,1,0,2:T(8,128)} fusion(f32[2,4,1,16,1024]{4,3,1,0,2:T(8,128)S(1)} %get-tuple-element.68, f32[2,4,16]{2,1,0:T(4,128)S(1)} %copy_maximum_fusion, bf16[1,1024,1024]{2,1,0:T(8,128)(2,1)} %get-tuple-element.5, s32[]{:T(128)S(6)} %select_n.271), kind=kOutput, calls=%fused_computation.51 | convolution fusion | flops 33816576 | bytes 852484 | tf_op jit(solution)/shard_map/sbkgp,pkd->sbkgd/dot_general | solution.py:93
  29.7 3.2 %collective-permute-start = (bf16[2,4,2048]{2,1,0:T(4,128)(2,1)}, bf16[2,4,2048]{2,1,0:T(4,128)(2,1)}, u32[]{:S(2)}, u32[]{:S(2)}) collective-permute-start(bf16[2,4,2048]{2,1,0:T(4,128)(2,1)} %param.9), channel_id=1, source_target_pairs={{0,14},{2,0},{4,2},{6,4},{8,6},{10,8},{12,10},{14,12},{1,15},{3,1}... | collective-permute-start | bytes 98312 | tf_op jit(solution)/shard_map/ppermute | solution.py:118
  33.0 1.2 fusion.258
  34.5 1.9 %convolution_bitcast_fusion.9 = f32[2,4,1,16,128]{4,3,1,0,2:T(8,128)} fusion(f32[2,4,1,16,1024]{4,3,1,0,2:T(8,128)S(1)} %get-tuple-element.64, f32[2,4,16]{2,1,0:T(4,128)S(1)} %copy_maximum_fusion.1, bf16[1,1024,1024]{2,1,0:T(8,128)(2,1)} %get-tuple-element.5, s32[]{:T(128)S(6)} %select_n.267), kind=kOutput, calls=%fused_computation.52 | convolution fusion | flops 33816576 | bytes 852484 | tf_op jit(solution)/shard_map/sbkgp,pkd->sbkgd/dot_general | solution.py:93
  37.2 1.2 fusion.256
  38.8 1.9 %convolution_bitcast_fusion.10 = f32[2,4,1,16,128]{4,3,1,0,2:T(8,128)} fusion(f32[2,4,1,16,1024]{4,3,1,0,2:T(8,128)S(1)} %get-tuple-element.60, f32[2,4,16]{2,1,0:T(4,128)S(1)} %copy_maximum_fusion.2, bf16[1,1024,1024]{2,1,0:T(8,128)(2,1)} %get-tuple-element.5, s32[]{:T(128)S(6)} %select_n.263), kind=kOutput, calls=%fused_computation.53 | convolution fusion | flops 33816576 | bytes 852484 | tf_op jit(solution)/shard_map/sbkgp,pkd->sbkgd/dot_general | solution.py:93
  41.6 1.2 fusion.254
  43.2 1.9 %convolution_bitcast_fusion.11 = f32[2,4,1,16,128]{4,3,1,0,2:T(8,128)} fusion(f32[2,4,1,16,1024]{4,3,1,0,2:T(8,128)S(1)} %get-tuple-element.56, f32[2,4,16]{2,1,0:T(4,128)S(1)} %copy_maximum_fusion.3, bf16[1,1024,1024]{2,1,0:T(8,128)(2,1)} %get-tuple-element.5, s32[]{:T(128)S(6)} %select_n.259), kind=kOutput, calls=%fused_computation.54 | convolution fusion | flops 33816576 | bytes 852484 | tf_op jit(solution)/shard_map/sbkgp,pkd->sbkgd/dot_general | solution.py:93
  46.1 1.2 fusion.252
  47.6 1.9 %convolution_bitcast_fusion.12 = f32[2,4,1,16,128]{4,3,1,0,2:T(8,128)} fusion(f32[2,4,1,16,1024]{4,3,1,0,2:T(8,128)S(1)} %get-tuple-element.52, f32[2,4,16]{2,1,0:T(4,128)S(1)} %copy_maximum_fusion.4, bf16[1,1024,1024]{2,1,0:T(8,128)(2,1)} %get-tuple-element.5, s32[]{:T(128)S(6)} %select_n.255), kind=kOutput, calls=%fused_computation.55 | convolution fusion | flops 33816576 | bytes 852484 | tf_op jit(solution)/shard_map/sbkgp,pkd->sbkgd/dot_general | solution.py:93
  50.5 1.2 fusion.250
  52.0 1.9 %convolution_bitcast_fusion.13 = f32[2,4,1,16,128]{4,3,1,0,2:T(8,128)} fusion(f32[2,4,1,16,1024]{4,3,1,0,2:T(8,128)S(1)} %get-tuple-element.48, f32[2,4,16]{2,1,0:T(4,128)S(1)} %copy_maximum_fusion.5, bf16[1,1024,1024]{2,1,0:T(8,128)(2,1)} %get-tuple-element.5, s32[]{:T(128)S(6)} %select_n.251), kind=kOutput, calls=%fused_computation.56 | convolution fusion | flops 33816576 | bytes 852484 | tf_op jit(solution)/shard_map/sbkgp,pkd->sbkgd/dot_general | solution.py:93
  61.1 1.7 %fusion.248 = (f32[2,4,16]{2,0,1:T(2,128)S(1)}, f32[2,4,1,16,128]{4,3,0,1,2:T(8,128)}) fusion(bf16[2,4,16,128]{3,2,1,0:T(8,128)(2,1)S(1)} %reshape.1101, bf16[1,4,128,1024]{3,2,1,0:T(8,128)(2,1)} %get-tuple-element.8, s32[]{:T(128)S(6)} %select_n.247, pred[4,128]{1,0:T(4,128)(4,1)S(1)} %broadcast_compare_fusion), kind=kOutput, calls=%fused_computation.362 | convolution fusion | flops 4243328 | bytes 230404 | tf_op jit(solution)/shard_map/sbkgd,btkd->sbkgt/dot_general | solution.py:85
  62.8 1.0 fusion.247
  64.0 1.3 fusion.45
  65.3 1.5 convolution_bitcast_fusion.14
  66.8 1.1 fusion.175
  68.7 1.0 fusion.10
  74.0 1.4 collective-permute-start.9
  75.8 3.1 %collective-permute-start.7 = (f32[130,128]{1,0:T(8,128)S(1)}, f32[130,128]{1,0:T(8,128)S(1)}, u32[]{:S(2)}, u32[]{:S(2)}) collective-permute-start(f32[130,128]{1,0:T(8,128)S(1)} %pad_maximum_fusion.3), channel_id=1, source_target_pairs={{0,8},{2,10},{4,12},{6,14},{8,0},{10,2},{12,4},{14,6},{1,9},{3,11}... | collective-permute-start | bytes 199688 | tf_op jit(solution)/shard_map/ppermute | solution.py:138
  80.4 6.6 %collective-permute-done.1 = f32[130,128]{1,0:T(8,128)S(1)} collective-permute-done((f32[130,128]{1,0:T(8,128)S(1)}, f32[130,128]{1,0:T(8,128)S(1)}, u32[]{:S(2)}, u32[]{:S(2)}) %collective-permute-start.1) | collective-permute-done | bytes 66592 | tf_op jit(solution)/shard_map/ppermute | solution.py:138
  87.0 6.1 %collective-permute-done.3 = f32[130,128]{1,0:T(8,128)S(1)} collective-permute-done((f32[130,128]{1,0:T(8,128)S(1)}, f32[130,128]{1,0:T(8,128)S(1)}, u32[]{:S(2)}, u32[]{:S(2)}) %collective-permute-start.3) | collective-permute-done | bytes 66592 | tf_op jit(solution)/shard_map/ppermute | solution.py:138
  93.1 6.1 %collective-permute-done.5 = f32[130,128]{1,0:T(8,128)S(1)} collective-permute-done((f32[130,128]{1,0:T(8,128)S(1)}, f32[130,128]{1,0:T(8,128)S(1)}, u32[]{:S(2)}, u32[]{:S(2)}) %collective-permute-start.5) | collective-permute-done | bytes 66592 | tf_op jit(solution)/shard_map/ppermute | solution.py:138
  100.5 2.0 %all_gather.3 = bf16[2,8,2048]{2,0,1:T(2,128)(2,1)S(1)} all-gather(bf16[2,4,2048]{2,0,1:T(2,128)(2,1)S(1)} %copy.272), channel_id=1, replica_groups=mesh['rep'=2,'tp'=8,'sub'=2] {'sub'}, dimensions={1}, use_global_device_ids=true | all-gather | bytes 98304 | tf_op jit(solution)/shard_map/all_gather | solution.py:214
  102.6 12.9 %fusion.1 = f32[16,8192]{1,0:T(8,128)S(1)} fusion(f32[8192]{0:T(1024)S(1)} %dynamic-slice-done, bf16[16,128,8192]{2,1,0:T(8,128)(2,1)} %bitcast.592, bf16[16,16,128]{2,1,0:T(8,128)(2,1)S(1)} %bitcast.591), kind=kOutput, calls=%fused_computation.2 | convolution fusion | flops 543031296 | bytes 34177024 | tf_op jit(solution)/shard_map/rhd,hdf->rhf/dot_general | solution.py:223
  116.7 1.6 %collective-permute-start.16 = (f32[16,1024]{1,0:T(8,128)S(1)}, f32[16,1024]{1,0:T(8,128)S(1)}, u32[]{:S(2)}, u32[]{:S(2)}) collective-permute-start(f32[16,1024]{1,0:T(8,128)S(1)} %bitcast.588), channel_id=1, source_target_pairs={{0,6},{2,8},{4,10},{6,12},{8,14},{10,0},{12,2},{14,4},{1,7},{3,9},... | collective-permute-start | bytes 196616 | tf_op jit(solution)/shard_map/ppermute | solution.py:46
  118.4 3.6 %collective-permute-start.17 = (f32[16,1024]{1,0:T(8,128)S(1)}, f32[16,1024]{1,0:T(8,128)S(1)}, u32[]{:S(2)}, u32[]{:S(2)}) collective-permute-start(f32[16,1024]{1,0:T(8,128)S(1)} %bitcast.587), channel_id=1, source_target_pairs={{0,8},{2,10},{4,12},{6,14},{8,0},{10,2},{12,4},{14,6},{1,9},{3,11}... | collective-permute-start | bytes 196616 | tf_op jit(solution)/shard_map/ppermute | solution.py:46
  122.1 2.1 %collective-permute-done.14 = f32[16,1024]{1,0:T(8,128)S(1)} collective-permute-done((f32[16,1024]{1,0:T(8,128)S(1)}, f32[16,1024]{1,0:T(8,128)S(1)}, u32[]{:S(2)}, u32[]{:S(2)}) %collective-permute-start.14) | collective-permute-done | bytes 65568 | tf_op jit(solution)/shard_map/ppermute | solution.py:46
  124.9 1.7 %collective-permute-start.20 = (f32[16,1024]{1,0:T(8,128)S(1)}, f32[16,1024]{1,0:T(8,128)S(1)}, u32[]{:S(2)}, u32[]{:S(2)}) collective-permute-start(f32[16,1024]{1,0:T(8,128)S(1)} %bitcast.584), channel_id=1, source_target_pairs={{0,14},{2,0},{4,2},{6,4},{8,6},{10,8},{12,10},{14,12},{1,15},{3,1}... | collective-permute-start | bytes 196616 | tf_op jit(solution)/shard_map/ppermute | solution.py:46
  126.7 2.5 %collective-permute-done.16 = f32[16,1024]{1,0:T(8,128)S(1)} collective-permute-done((f32[16,1024]{1,0:T(8,128)S(1)}, f32[16,1024]{1,0:T(8,128)S(1)}, u32[]{:S(2)}, u32[]{:S(2)}) %collective-permute-start.16) | collective-permute-done | bytes 65568 | tf_op jit(solution)/shard_map/ppermute | solution.py:46
  130.0 2.2 %collective-permute-start.21 = (bf16[1,16,1024]{2,1,0:T(8,128)(2,1)S(1)}, bf16[1,16,1024]{2,1,0:T(8,128)(2,1)S(1)}, u32[]{:S(2)}, u32[]{:S(2)}) collective-permute-start(bf16[1,16,1024]{2,1,0:T(8,128)(2,1)S(1)} %fusion.202), channel_id=1, source_target_pairs={{0,2},{2,0},{4,6},{6,4},{8,10},{10,8},{12,14},{14,12},{1,3},{3,1},... | collective-permute-start | bytes 98312 | tf_op jit(solution)/shard_map/ppermute | solution.py:27
  132.2 1.9 %collective-permute-done.21 = bf16[1,16,1024]{2,1,0:T(8,128)(2,1)S(1)} collective-permute-done((bf16[1,16,1024]{2,1,0:T(8,128)(2,1)S(1)}, bf16[1,16,1024]{2,1,0:T(8,128)(2,1)S(1)}, u32[]{:S(2)}, u32[]{:S(2)}) %collective-permute-start.21) | collective-permute-done | bytes 32800 | tf_op jit(solution)/shard_map/ppermute | solution.py:27
  134.1 2.5 %collective-permute-start.22 = (bf16[2,16,1024]{2,1,0:T(8,128)(2,1)S(1)}, bf16[2,16,1024]{2,1,0:T(8,128)(2,1)S(1)}, u32[]{:S(2)}, u32[]{:S(2)}) collective-permute-start(bf16[2,16,1024]{2,1,0:T(8,128)(2,1)S(1)} %maximum_select_fusion.2), channel_id=1, source_target_pairs={{0,4},{2,6},{4,0},{6,2},{8,12},{10,14},{12,8},{14,10},{1,5},{3,7},... | collective-permute-start | bytes 196616 | tf_op jit(solution)/shard_map/ppermute | solution.py:27
  136.6 2.2 %collective-permute-done.22 = bf16[2,16,1024]{2,1,0:T(8,128)(2,1)S(1)} collective-permute-done((bf16[2,16,1024]{2,1,0:T(8,128)(2,1)S(1)}, bf16[2,16,1024]{2,1,0:T(8,128)(2,1)S(1)}, u32[]{:S(2)}, u32[]{:S(2)}) %collective-permute-start.22) | collective-permute-done | bytes 65568 | tf_op jit(solution)/shard_map/ppermute | solution.py:27
  138.9 2.5 %collective-permute-start.23 = (bf16[4,16,1024]{2,1,0:T(8,128)(2,1)S(1)}, bf16[4,16,1024]{2,1,0:T(8,128)(2,1)S(1)}, u32[]{:S(2)}, u32[]{:S(2)}) collective-permute-start(bf16[4,16,1024]{2,1,0:T(8,128)(2,1)S(1)} %maximum_select_fusion.1), channel_id=1, source_target_pairs={{0,8},{2,10},{4,12},{6,14},{8,0},{10,2},{12,4},{14,6},{1,9},{3,11}... | collective-permute-start | bytes 393224 | tf_op jit(solution)/shard_map/ppermute | solution.py:27
  141.4 3.4 %collective-permute-done.23 = bf16[4,16,1024]{2,1,0:T(8,128)(2,1)S(1)} collective-permute-done((bf16[4,16,1024]{2,1,0:T(8,128)(2,1)S(1)}, bf16[4,16,1024]{2,1,0:T(8,128)(2,1)S(1)}, u32[]{:S(2)}, u32[]{:S(2)}) %collective-permute-start.23) | collective-permute-done | bytes 131104 | tf_op jit(solution)/shard_map/ppermute | solution.py:27
  (222 shorter events, 30.6 us)
Async XLA Ops:
  0.0 37.2 %collective-permute-start.8 = (bf16[2,4,2048]{2,1,0:T(4,128)(2,1)}, bf16[2,4,2048]{2,1,0:T(4,128)(2,1)S(1)}, u32[]{:S(2)}, u32[]{:S(2)}) collective-permute-start(bf16[2,4,2048]{2,1,0:T(4,128)(2,1)} %param.9), channel_id=1, source_target_pairs={{0,6},{2,8},{4,10},{6,12},{8,14},{10,0},{12,2},{14,4},{1,7},{3,9},... | collective-permute-start | bytes 98312 | tf_op jit(solution)/shard_map/ppermute | solution.py:118
  4.0 36.9 %collective-permute-start.6 = (bf16[2,4,2048]{2,1,0:T(4,128)(2,1)}, bf16[2,4,2048]{2,1,0:T(4,128)(2,1)}, u32[]{:S(2)}, u32[]{:S(2)}) collective-permute-start(bf16[2,4,2048]{2,1,0:T(4,128)(2,1)} %param.9), channel_id=1, source_target_pairs={{0,8},{2,10},{4,12},{6,14},{8,0},{10,2},{12,4},{14,6},{1,9},{3,11}... | collective-permute-start | bytes 98312 | tf_op jit(solution)/shard_map/ppermute | solution.py:118
  6.5 38.7 %collective-permute-start.4 = (bf16[2,4,2048]{2,1,0:T(4,128)(2,1)}, bf16[2,4,2048]{2,1,0:T(4,128)(2,1)}, u32[]{:S(2)}, u32[]{:S(2)}) collective-permute-start(bf16[2,4,2048]{2,1,0:T(4,128)(2,1)} %param.9), channel_id=1, source_target_pairs={{0,10},{2,12},{4,14},{6,0},{8,2},{10,4},{12,6},{14,8},{1,11},{3,13... | collective-permute-start | bytes 98312 | tf_op jit(solution)/shard_map/ppermute | solution.py:118
  7.9 41.8 %collective-permute-start.2 = (bf16[2,4,2048]{2,1,0:T(4,128)(2,1)}, bf16[2,4,2048]{2,1,0:T(4,128)(2,1)}, u32[]{:S(2)}, u32[]{:S(2)}) collective-permute-start(bf16[2,4,2048]{2,1,0:T(4,128)(2,1)} %param.9), channel_id=1, source_target_pairs={{0,12},{2,14},{4,0},{6,2},{8,4},{10,6},{12,8},{14,10},{1,13},{3,15... | collective-permute-start | bytes 98312 | tf_op jit(solution)/shard_map/ppermute | solution.py:118
  9.2 14.2 %collective-permute-start.12 = (bf16[2,4,2048]{2,1,0:T(4,128)(2,1)}, bf16[2,4,2048]{2,1,0:T(4,128)(2,1)S(1)}, u32[]{:S(2)}, u32[]{:S(2)}) collective-permute-start(bf16[2,4,2048]{2,1,0:T(4,128)(2,1)} %param.9), channel_id=1, source_target_pairs={{0,2},{2,4},{4,6},{6,8},{8,10},{10,12},{12,14},{14,0},{1,3},{3,5},... | collective-permute-start | bytes 98312 | tf_op jit(solution)/shard_map/ppermute | solution.py:118
  9.8 12.3 %copy-start.21 = (pred[2,2]{1,0:T(4,128)(4,1)}, pred[2,2]{1,0:T(4,128)(4,1)S(1)}, u32[]{:S(2)}) copy-start(pred[2,2]{1,0:T(4,128)(4,1)S(1)} %iota_compare_fusion) | copy-start | bytes 16
  13.6 4.2 %copy-start.24 = (s32[128]{0:T(128)S(1)}, s32[128]{0:T(128)}, u32[]{:S(2)}) copy-start(s32[128]{0:T(128)} %param.15) | copy-start | bytes 1540
  13.6 4.2 %copy-start.11 = (bf16[2,2,4,1024]{3,2,1,0:T(4,128)(2,1)S(1)}, bf16[2,2,4,1024]{3,2,1,0:T(4,128)(2,1)}, u32[]{:S(2)}) copy-start(bf16[2,2,4,1024]{3,2,1,0:T(4,128)(2,1)} %param.13) | copy-start | bytes 98308
  18.3 10.6 %copy-start.4 = (f32[16384]{0:T(1024)}, f32[16384]{0:T(1024)S(1)}, u32[]{:S(2)}) copy-start(f32[16384]{0:T(1024)S(1)} %broadcast_bitcast_fusion.1) | copy-start | bytes 196612
  23.4 6.3 %collective-permute-start.10 = (bf16[2,4,2048]{2,1,0:T(4,128)(2,1)}, bf16[2,4,2048]{2,1,0:T(4,128)(2,1)S(1)}, u32[]{:S(2)}, u32[]{:S(2)}) collective-permute-start(bf16[2,4,2048]{2,1,0:T(4,128)(2,1)} %param.9), channel_id=1, source_target_pairs={{0,4},{2,6},{4,8},{6,10},{8,12},{10,14},{12,0},{14,2},{1,5},{3,7},... | collective-permute-start | bytes 98312 | tf_op jit(solution)/shard_map/ppermute | solution.py:118
  29.7 30.6 %collective-permute-start = (bf16[2,4,2048]{2,1,0:T(4,128)(2,1)}, bf16[2,4,2048]{2,1,0:T(4,128)(2,1)}, u32[]{:S(2)}, u32[]{:S(2)}) collective-permute-start(bf16[2,4,2048]{2,1,0:T(4,128)(2,1)} %param.9), channel_id=1, source_target_pairs={{0,14},{2,0},{4,2},{6,4},{8,6},{10,8},{12,10},{14,12},{1,15},{3,1}... | collective-permute-start | bytes 98312 | tf_op jit(solution)/shard_map/ppermute | solution.py:118
  62.8 12.6 %copy-start.13 = (f32[2,4,16]{2,0,1:T(2,128)S(1)}, f32[2,4,16]{2,0,1:T(2,128)}, u32[]{:S(2)}) copy-start(f32[2,4,16]{2,0,1:T(2,128)} %copy.242) | copy-start | bytes 1540
  63.8 7.0 %copy-start.15 = (f32[2,4,16]{2,0,1:T(2,128)S(1)}, f32[2,4,16]{2,0,1:T(2,128)}, u32[]{:S(2)}) copy-start(f32[2,4,16]{2,0,1:T(2,128)} %copy.252) | copy-start | bytes 1540
  63.8 8.0 %copy-start.10 = (f32[2,4,1,16,128]{4,3,1,0,2:T(8,128)S(1)}, f32[2,4,1,16,128]{4,3,1,0,2:T(8,128)}, u32[]{:S(2)}) copy-start(f32[2,4,1,16,128]{4,3,1,0,2:T(8,128)} %convolution_bitcast_fusion.9) | copy-start | bytes 196612
  63.8 8.2 %copy-start.19 = (f32[1,128]{1,0:T(1,128)S(1)}, f32[1,128]{1,0:T(1,128)}, u32[]{:S(2)}) copy-start(f32[1,128]{1,0:T(1,128)} %max.194) | copy-start | bytes 1540
  63.8 9.1 %copy-start.14 = (f32[2,4,16]{2,0,1:T(2,128)S(1)}, f32[2,4,16]{2,0,1:T(2,128)}, u32[]{:S(2)}) copy-start(f32[2,4,16]{2,0,1:T(2,128)} %copy.247) | copy-start | bytes 1540
  63.8 9.4 %copy-start.9 = (f32[2,4,1,16,128]{4,3,1,0,2:T(8,128)S(1)}, f32[2,4,1,16,128]{4,3,1,0,2:T(8,128)}, u32[]{:S(2)}) copy-start(f32[2,4,1,16,128]{4,3,1,0,2:T(8,128)} %convolution_bitcast_fusion.10) | copy-start | bytes 196612
  63.9 11.8 %copy-start.8 = (f32[2,4,1,16,128]{4,3,1,0,2:T(8,128)S(1)}, f32[2,4,1,16,128]{4,3,1,0,2:T(8,128)}, u32[]{:S(2)}) copy-start(f32[2,4,1,16,128]{4,3,1,0,2:T(8,128)} %convolution_bitcast_fusion.11) | copy-start | bytes 196612
  63.9 11.9 %copy-start.18 = (f32[1,128]{1,0:T(1,128)S(1)}, f32[1,128]{1,0:T(1,128)}, u32[]{:S(2)}) copy-start(f32[1,128]{1,0:T(1,128)} %max.190) | copy-start | bytes 1540
  63.9 15.6 %copy-start.2 = (f32[2,4,1,16,128]{4,3,0,1,2:T(8,128)S(1)}, f32[2,4,1,16,128]{4,3,0,1,2:T(8,128)}, u32[]{:S(2)}) copy-start(f32[2,4,1,16,128]{4,3,0,1,2:T(8,128)} %get-tuple-element.46) | copy-start | bytes 196612
  65.3 14.7 %copy-start.6 = (f32[2,4,1,16,128]{4,3,1,0,2:T(8,128)S(1)}, f32[2,4,1,16,128]{4,3,1,0,2:T(8,128)}, u32[]{:S(2)}) copy-start(f32[2,4,1,16,128]{4,3,1,0,2:T(8,128)} %convolution_bitcast_fusion.12) | copy-start | bytes 196612
  65.3 14.9 %copy-start.7 = (f32[2,4,1,16,128]{4,3,1,0,2:T(8,128)S(1)}, f32[2,4,1,16,128]{4,3,1,0,2:T(8,128)}, u32[]{:S(2)}) copy-start(f32[2,4,1,16,128]{4,3,1,0,2:T(8,128)} %convolution_bitcast_fusion.13) | copy-start | bytes 196612
  65.3 15.0 %copy-start.17 = (f32[1,128]{1,0:T(1,128)S(1)}, f32[1,128]{1,0:T(1,128)}, u32[]{:S(2)}) copy-start(f32[1,128]{1,0:T(1,128)} %max.188) | copy-start | bytes 1540
  66.8 13.6 %copy-start.16 = (f32[1,128]{1,0:T(1,128)S(1)}, f32[1,128]{1,0:T(1,128)}, u32[]{:S(2)}) copy-start(f32[1,128]{1,0:T(1,128)} %max.186) | copy-start | bytes 1540
  66.8 20.2 %copy-start.1 = (f32[8,130,128]{2,1,0:T(8,128)S(1)}, f32[8,130,128]{2,1,0:T(8,128)}, u32[]{:S(2)}) copy-start(f32[8,130,128]{2,1,0:T(8,128)} %fusion.147) | copy-start | bytes 1597444
  70.4 28.9 %collective-permute-start.13 = (f32[130,128]{1,0:T(8,128)S(1)}, f32[130,128]{1,0:T(8,128)S(1)}, u32[]{:S(2)}, u32[]{:S(2)}) collective-permute-start(f32[130,128]{1,0:T(8,128)S(1)} %pad_maximum_fusion.6), channel_id=1, source_target_pairs={{0,14},{2,0},{4,2},{6,4},{8,6},{10,8},{12,10},{14,12},{1,15},{3,1}... | collective-permute-start | bytes 199688 | tf_op jit(solution)/shard_map/ppermute | solution.py:138
  72.0 27.5 %copy-start.12 = (f32[2,4,16]{2,1,0:T(4,128)S(1)}, f32[2,4,16]{2,1,0:T(4,128)}, u32[]{:S(2)}) copy-start(f32[2,4,16]{2,1,0:T(4,128)} %fusion.242) | copy-start | bytes 1540
  72.0 27.5 %copy-start.22 = (pred[2,2]{1,0:T(4,128)(4,1)S(1)}, pred[2,2]{1,0:T(4,128)(4,1)}, u32[]{:S(2)}) copy-start(pred[2,2]{1,0:T(4,128)(4,1)} %copy-done.21) | copy-start | bytes 16
  72.0 27.3 %collective-permute-start.11 = (f32[130,128]{1,0:T(8,128)S(1)}, f32[130,128]{1,0:T(8,128)S(1)}, u32[]{:S(2)}, u32[]{:S(2)}) collective-permute-start(f32[130,128]{1,0:T(8,128)S(1)} %pad_maximum_fusion.5), channel_id=1, source_target_pairs={{0,12},{2,14},{4,0},{6,2},{8,4},{10,6},{12,8},{14,10},{1,13},{3,15... | collective-permute-start | bytes 199688 | tf_op jit(solution)/shard_map/ppermute | solution.py:138
  74.0 25.3 %collective-permute-start.9 = (f32[130,128]{1,0:T(8,128)S(1)}, f32[130,128]{1,0:T(8,128)S(1)}, u32[]{:S(2)}, u32[]{:S(2)}) collective-permute-start(f32[130,128]{1,0:T(8,128)S(1)} %pad_maximum_fusion.4), channel_id=1, source_target_pairs={{0,10},{2,12},{4,14},{6,0},{8,2},{10,4},{12,6},{14,8},{1,11},{3,13... | collective-permute-start | bytes 199688 | tf_op jit(solution)/shard_map/ppermute | solution.py:138
  75.3 24.8 %copy-start.20 = (bf16[2,4,128]{2,0,1:T(2,128)(2,1)S(1)}, bf16[2,4,128]{2,0,1:T(2,128)(2,1)}, u32[]{:S(2)}) copy-start(bf16[2,4,128]{2,0,1:T(2,128)(2,1)} %copy.267) | copy-start | bytes 6148
  75.8 23.4 %collective-permute-start.7 = (f32[130,128]{1,0:T(8,128)S(1)}, f32[130,128]{1,0:T(8,128)S(1)}, u32[]{:S(2)}, u32[]{:S(2)}) collective-permute-start(f32[130,128]{1,0:T(8,128)S(1)} %pad_maximum_fusion.3), channel_id=1, source_target_pairs={{0,8},{2,10},{4,12},{6,14},{8,0},{10,2},{12,4},{14,6},{1,9},{3,11}... | collective-permute-start | bytes 199688 | tf_op jit(solution)/shard_map/ppermute | solution.py:138
  79.4 23.3 %dynamic-slice-start = ((f32[16384]{0:T(1024)}, s32[]{:T(128)}), f32[8192]{0:T(1024)S(1)}, s32[]{:S(2)}) async-start(f32[16384]{0:T(1024)} %copy-done.4, s32[]{:T(128)} %select_n.277), calls=%async_computation | async-start | bytes 66048 | tf_op jit(solution)/shard_map/dynamic_slice | solution.py:221
  79.9 7.1 %collective-permute-start.1 = (f32[130,128]{1,0:T(8,128)S(1)}, f32[130,128]{1,0:T(8,128)S(1)}, u32[]{:S(2)}, u32[]{:S(2)}) collective-permute-start(f32[130,128]{1,0:T(8,128)S(1)} %pad_maximum_fusion), channel_id=1, source_target_pairs={{0,2},{2,4},{4,6},{6,8},{8,10},{10,12},{12,14},{14,0},{1,3},{3,5},... | collective-permute-start | bytes 199688 | tf_op jit(solution)/shard_map/ppermute | solution.py:138
  87.0 6.1 %collective-permute-start.3 = (f32[130,128]{1,0:T(8,128)S(1)}, f32[130,128]{1,0:T(8,128)S(1)}, u32[]{:S(2)}, u32[]{:S(2)}) collective-permute-start(f32[130,128]{1,0:T(8,128)S(1)} %pad_maximum_fusion.1), channel_id=1, source_target_pairs={{0,4},{2,6},{4,8},{6,10},{8,12},{10,14},{12,0},{14,2},{1,5},{3,7},... | collective-permute-start | bytes 199688 | tf_op jit(solution)/shard_map/ppermute | solution.py:138
  93.1 6.1 %collective-permute-start.5 = (f32[130,128]{1,0:T(8,128)S(1)}, f32[130,128]{1,0:T(8,128)S(1)}, u32[]{:S(2)}, u32[]{:S(2)}) collective-permute-start(f32[130,128]{1,0:T(8,128)S(1)} %pad_maximum_fusion.2), channel_id=1, source_target_pairs={{0,6},{2,8},{4,10},{6,12},{8,14},{10,0},{12,2},{14,4},{1,7},{3,9},... | collective-permute-start | bytes 199688 | tf_op jit(solution)/shard_map/ppermute | solution.py:138
  115.5 11.1 %copy-start.5 = (f32[16384]{0:T(1024)S(1)}, f32[16384]{0:T(1024)}, u32[]{:S(2)}) copy-start(f32[16384]{0:T(1024)} %copy-done.4) | copy-start | bytes 196612
  116.5 7.8 %collective-permute-start.14 = (f32[16,1024]{1,0:T(8,128)S(1)}, f32[16,1024]{1,0:T(8,128)S(1)}, u32[]{:S(2)}, u32[]{:S(2)}) collective-permute-start(f32[16,1024]{1,0:T(8,128)S(1)} %bitcast.590), channel_id=1, source_target_pairs={{0,2},{2,4},{4,6},{6,8},{8,10},{10,12},{12,14},{14,0},{1,3},{3,5},... | collective-permute-start | bytes 196616 | tf_op jit(solution)/shard_map/ppermute | solution.py:46
  116.5 8.4 %collective-permute-start.15 = (f32[16,1024]{1,0:T(8,128)S(1)}, f32[16,1024]{1,0:T(8,128)S(1)}, u32[]{:S(2)}, u32[]{:S(2)}) collective-permute-start(f32[16,1024]{1,0:T(8,128)S(1)} %bitcast.589), channel_id=1, source_target_pairs={{0,4},{2,6},{4,8},{6,10},{8,12},{10,14},{12,0},{14,2},{1,5},{3,7},... | collective-permute-start | bytes 196616 | tf_op jit(solution)/shard_map/ppermute | solution.py:46
  116.7 28.6 %copy-start.3 = (bf16[2,8,8192]{2,1,0:T(8,128)(2,1)S(1)}, bf16[2,8,8192]{2,1,0:T(8,128)(2,1)}, u32[]{:S(2)}) copy-start(bf16[2,8,8192]{2,1,0:T(8,128)(2,1)} %param.17) | copy-start | bytes 786436
  116.7 12.4 %collective-permute-start.16 = (f32[16,1024]{1,0:T(8,128)S(1)}, f32[16,1024]{1,0:T(8,128)S(1)}, u32[]{:S(2)}, u32[]{:S(2)}) collective-permute-start(f32[16,1024]{1,0:T(8,128)S(1)} %bitcast.588), channel_id=1, source_target_pairs={{0,6},{2,8},{4,10},{6,12},{8,14},{10,0},{12,2},{14,4},{1,7},{3,9},... | collective-permute-start | bytes 196616 | tf_op jit(solution)/shard_map/ppermute | solution.py:46
  118.4 10.8 %collective-permute-start.17 = (f32[16,1024]{1,0:T(8,128)S(1)}, f32[16,1024]{1,0:T(8,128)S(1)}, u32[]{:S(2)}, u32[]{:S(2)}) collective-permute-start(f32[16,1024]{1,0:T(8,128)S(1)} %bitcast.587), channel_id=1, source_target_pairs={{0,8},{2,10},{4,12},{6,14},{8,0},{10,2},{12,4},{14,6},{1,9},{3,11}... | collective-permute-start | bytes 196616 | tf_op jit(solution)/shard_map/ppermute | solution.py:46
  122.0 7.2 %collective-permute-start.18 = (f32[16,1024]{1,0:T(8,128)S(1)}, f32[16,1024]{1,0:T(8,128)S(1)}, u32[]{:S(2)}, u32[]{:S(2)}) collective-permute-start(f32[16,1024]{1,0:T(8,128)S(1)} %bitcast.586), channel_id=1, source_target_pairs={{0,10},{2,12},{4,14},{6,0},{8,2},{10,4},{12,6},{14,8},{1,11},{3,13... | collective-permute-start | bytes 196616 | tf_op jit(solution)/shard_map/ppermute | solution.py:46
  124.3 5.7 %collective-permute-start.19 = (f32[16,1024]{1,0:T(8,128)S(1)}, f32[16,1024]{1,0:T(8,128)S(1)}, u32[]{:S(2)}, u32[]{:S(2)}) collective-permute-start(f32[16,1024]{1,0:T(8,128)S(1)} %bitcast.585), channel_id=1, source_target_pairs={{0,12},{2,14},{4,0},{6,2},{8,4},{10,6},{12,8},{14,10},{1,13},{3,15... | collective-permute-start | bytes 196616 | tf_op jit(solution)/shard_map/ppermute | solution.py:46
  124.9 5.0 %collective-permute-start.20 = (f32[16,1024]{1,0:T(8,128)S(1)}, f32[16,1024]{1,0:T(8,128)S(1)}, u32[]{:S(2)}, u32[]{:S(2)}) collective-permute-start(f32[16,1024]{1,0:T(8,128)S(1)} %bitcast.584), channel_id=1, source_target_pairs={{0,14},{2,0},{4,2},{6,4},{8,6},{10,8},{12,10},{14,12},{1,15},{3,1}... | collective-permute-start | bytes 196616 | tf_op jit(solution)/shard_map/ppermute | solution.py:46
  130.0 4.1 %collective-permute-start.21 = (bf16[1,16,1024]{2,1,0:T(8,128)(2,1)S(1)}, bf16[1,16,1024]{2,1,0:T(8,128)(2,1)S(1)}, u32[]{:S(2)}, u32[]{:S(2)}) collective-permute-start(bf16[1,16,1024]{2,1,0:T(8,128)(2,1)S(1)} %fusion.202), channel_id=1, source_target_pairs={{0,2},{2,0},{4,6},{6,4},{8,10},{10,8},{12,14},{14,12},{1,3},{3,1},... | collective-permute-start | bytes 98312 | tf_op jit(solution)/shard_map/ppermute | solution.py:27
  134.1 4.8 %collective-permute-start.22 = (bf16[2,16,1024]{2,1,0:T(8,128)(2,1)S(1)}, bf16[2,16,1024]{2,1,0:T(8,128)(2,1)S(1)}, u32[]{:S(2)}, u32[]{:S(2)}) collective-permute-start(bf16[2,16,1024]{2,1,0:T(8,128)(2,1)S(1)} %maximum_select_fusion.2), channel_id=1, source_target_pairs={{0,4},{2,6},{4,0},{6,2},{8,12},{10,14},{12,8},{14,10},{1,5},{3,7},... | collective-permute-start | bytes 196616 | tf_op jit(solution)/shard_map/ppermute | solution.py:27
  138.9 5.9 %collective-permute-start.23 = (bf16[4,16,1024]{2,1,0:T(8,128)(2,1)S(1)}, bf16[4,16,1024]{2,1,0:T(8,128)(2,1)S(1)}, u32[]{:S(2)}, u32[]{:S(2)}) collective-permute-start(bf16[4,16,1024]{2,1,0:T(8,128)(2,1)S(1)} %maximum_select_fusion.1), channel_id=1, source_target_pairs={{0,8},{2,10},{4,12},{6,14},{8,0},{10,2},{12,4},{14,6},{1,9},{3,11}... | collective-permute-start | bytes 393224 | tf_op jit(solution)/shard_map/ppermute | solution.py:27
  (3 other events, 5.8 us)

commit v3 on v1

--- a/solution.py
+++ b/solution.py
@@ -3,6 +3,8 @@
 import jax
 import jax.numpy as jnp
 from jax import lax
+from jax.experimental import pallas as pl
+from jax.experimental.pallas import tpu as pltpu
 from jax.sharding import PartitionSpec as P
 
 DH = 128
@@ -47,6 +49,73 @@
     return jax.tree.map(lambda *xs: jnp.stack(xs), *got)
 
 
+def _attend_kernel(q_ref, k_ref, v_ref, tk_ref, tv_ref, valid_ref, numer_ref, peak_ref, mass_ref):
+    rows_n = q_ref.shape[1]
+    samples = tk_ref.shape[1]
+    per_sample = rows_n // samples
+    score_scale = 1.0 / math.sqrt(DH)
+    dims_nt = (((1,), (1,)), ((), ()))
+    q = q_ref[0]
+    p_scores = lax.dot_general(q, k_ref[0], dims_nt, preferred_element_type=jnp.float32)
+    p_scores = p_scores * score_scale
+    t_parts = []
+    for r in range(samples):
+        qr = q[r * per_sample:(r + 1) * per_sample]
+        sr = lax.dot_general(qr, tk_ref[0, r], dims_nt, preferred_element_type=jnp.float32)
+        sr = sr * score_scale
+        t_parts.append(jnp.where(valid_ref[r:r + 1, :] > 0.0, sr, NEG_FILL))
+    t_scores = jnp.concatenate(t_parts, axis=0)
+    peak = jnp.maximum(
+        jnp.max(p_scores, axis=1, keepdims=True), jnp.max(t_scores, axis=1, keepdims=True)
+    )
+    p_w = jnp.exp(p_scores - peak)
+    t_w = jnp.exp(t_scores - peak)
+    mass = jnp.sum(p_w, axis=1, keepdims=True) + jnp.sum(t_w, axis=1, keepdims=True)
+    numer = jnp.dot(p_w.astype(jnp.bfloat16), v_ref[0], preferred_element_type=jnp.float32)
+    t_w16 = t_w.astype(jnp.bfloat16)
+    t_numer = [
+        jnp.dot(
+            t_w16[r * per_sample:(r + 1) * per_sample], tv_ref[0, r],
+            preferred_element_type=jnp.float32,
+        )
+        for r in range(samples)
+    ]
+    numer_ref[0] = numer + jnp.concatenate(t_numer, axis=0)
+    peak_ref[0] = jnp.broadcast_to(peak, peak_ref.shape[1:])
+    mass_ref[0] = jnp.broadcast_to(mass, mass_ref.shape[1:])
+
+
+def _attend_local(q_rows, prefix_kv, tail_kv, valid):
+    kv_heads, rows_n, _ = q_rows.shape
+    prefix_dev = prefix_kv.shape[1]
+    samples, tail_dev = tail_kv.shape[1], tail_kv.shape[2]
+    flops = 4 * kv_heads * rows_n * DH * (prefix_dev + tail_dev)
+    bytes_in = 2 * (prefix_kv.size + tail_kv.size + q_rows.size)
+    return pl.pallas_call(
+        _attend_kernel,
+        grid=(kv_heads,),
+        in_specs=[
+            pl.BlockSpec((1, rows_n, DH), lambda k: (k, 0, 0)),
+            pl.BlockSpec((1, prefix_dev, DH), lambda k: (0, 0, k)),
+            pl.BlockSpec((1, prefix_dev, DH), lambda k: (1, 0, k)),
+            pl.BlockSpec((1, samples, tail_dev, DH), lambda k: (0, 0, 0, k)),
+            pl.BlockSpec((1, samples, tail_dev, DH), lambda k: (1, 0, 0, k)),
+            pl.BlockSpec((samples, tail_dev), lambda k: (0, 0)),
+        ],
+        out_specs=[
+            pl.BlockSpec((1, rows_n, DH), lambda k: (k, 0, 0)),
+            pl.BlockSpec((1, rows_n, DH), lambda k: (k, 0, 0)),
+            pl.BlockSpec((1, rows_n, DH), lambda k: (k, 0, 0)),
+        ],
+        out_shape=[jax.ShapeDtypeStruct((kv_heads, rows_n, DH), jnp.float32)] * 3,
+        cost_estimate=pl.CostEstimate(
+            flops=flops,
+            transcendentals=kv_heads * rows_n * (prefix_dev + tail_dev),
+            bytes_accessed=bytes_in + 3 * 4 * kv_heads * rows_n * DH,
+        ),
+    )(q_rows, prefix_kv, prefix_kv, tail_kv, tail_kv, valid)
+
+
 def per_device(
     queries, prefix_kv, tail_kv, tail_lengths, fresh_kv, out_weight, scale_in, scale_out, residual
 ):
@@ -64,41 +133,27 @@
 
     q_blocks = _gather_blocks(queries, "tp", tp_count)
     q_all = jnp.moveaxis(q_blocks, 0, 2).reshape(steps_n, rows_dev, kv_heads, group, DH)
-
-    p_keys = prefix_kv[0].reshape(prefix_dev, kv_heads, DH)
-    p_vals = prefix_kv[1].reshape(prefix_dev, kv_heads, DH)
-    t_keys = tail_kv[0].reshape(rows_dev, tail_dev, kv_heads, DH)
-    t_vals = tail_kv[1].reshape(rows_dev, tail_dev, kv_heads, DH)
-    p_scores = (
-        jnp.einsum("sbkgd,pkd->sbkgp", q_all, p_keys, preferred_element_type=jnp.float32)
-        * score_scale
-    )
-    t_scores = (
-        jnp.einsum("sbkgd,btkd->sbkgt", q_all, t_keys, preferred_element_type=jnp.float32)
-        * score_scale
-    )
+    q_rows = jnp.transpose(q_all, (2, 1, 0, 3, 4)).reshape(kv_heads, -1, DH)
     t_pos = tp_rank * tail_dev + jnp.arange(tail_dev)
-    t_live = t_pos[None, :] < tail_lengths[:, None]
-    t_scores = jnp.where(t_live[None, :, None, None, :], t_scores, NEG_FILL)
-    loc_peak = jnp.maximum(p_scores.max(-1), t_scores.max(-1))
-    p_w = jnp.exp(p_scores - loc_peak[..., None])
-    t_w = jnp.exp(t_scores - loc_peak[..., None])
-    loc_mass = p_w.sum(-1) + t_w.sum(-1)
-    loc_numer = jnp.einsum(
-        "sbkgp,pkd->sbkgd", p_w.astype(jnp.bfloat16), p_vals, preferred_element_type=jnp.float32
-    )
-    loc_numer = loc_numer + jnp.einsum(
-        "sbkgt,btkd->sbkgd", t_w.astype(jnp.bfloat16), t_vals, preferred_element_type=jnp.float32
-    )
+    valid = (t_pos[None, :] < tail_lengths[:, None]).astype(jnp.float32)
+    k_numer, k_peak, k_mass = _attend_local(q_rows, prefix_kv, tail_kv, valid)
 
     def by_owner(x):
+        x = jnp.transpose(x, (2, 1, 0, 3) + tuple(range(4, x.ndim)))
         x = x.reshape((steps_n, rows_dev, tp_count, heads_dev) + x.shape[4:])
         return jnp.moveaxis(x, 2, 0)
 
-    stats = jnp.stack([by_owner(loc_peak), by_owner(loc_mass)], axis=1)
-    got_numer, got_stats = _exchange(
-        (by_owner(loc_numer), stats.reshape(tp_count, 2, -1)), "tp", tp_count
-    )
+    grid4 = (kv_heads, rows_dev, steps_n, group)
+    o_numer = by_owner(k_numer.reshape(grid4 + (DH,))).reshape(tp_count, -1, DH)
+    o_peak = by_owner(k_peak[..., 0].reshape(grid4)).reshape(tp_count, -1)
+    o_mass = by_owner(k_mass[..., 0].reshape(grid4)).reshape(tp_count, -1)
+    n_rows = steps_n * rows_dev * heads_dev
+    n_stat = -(-2 * n_rows // DH)
+    stats = jnp.concatenate([o_peak, o_mass], axis=1)
+    stats = jnp.pad(stats, ((0, 0), (0, n_stat * DH - 2 * n_rows))).reshape(tp_count, n_stat, DH)
+    got = _exchange(jnp.concatenate([o_numer, stats], axis=1), "tp", tp_count)
+    got_numer = got[:, :n_rows].reshape(tp_count, steps_n, rows_dev, heads_dev, DH)
+    got_stats = got[:, n_rows:].reshape(tp_count, -1)[:, : 2 * n_rows]
     got_stats = got_stats.reshape(tp_count, 2, steps_n, rows_dev, heads_dev)
     got_peak = got_stats[:, 0]
     got_mass = got_stats[:, 1]

time: 116 us -> 100 us (0.86)
  local copies, waits for them, and re-layouts: 23.2 us -> 7.81 us
  starting transfers between devices: 45.9 us -> 31.4 us
  waiting for transfers between devices: 20.5 us -> 31.1 us
  Pallas kernels: 0 us -> 8.58 us
  matrix products: 19 us -> 13.3 us
    ppermute x21 -> x14, starting transfers between devices: 34.5 us -> 22.4 us  [_exchange(): lax.ppermute(send, axis_name, [(i, (i + k) % count) for i in range(count)])]
    unnamed x52 -> x20, local copies, waits for them, and re-layouts: 11.9 us -> 0.47 us
    pallas_call x0 -> x1, Pallas kernels: none -> 8.58 us  [_attend_local(): pl.pallas_call(_attend_kernel, grid=(kv_heads,), in_specs=[pl.BlockSpec((...]
    ppermute x21 -> x14, waiting for transfers between devices: 6.26 us -> 11.6 us  [_exchange(): lax.ppermute(send, axis_name, [(i, (i + k) % count) for i in range(count)])]
    ppermute x6, waiting for transfers between devices: 14.3 us -> 19.5 us  [_gather_blocks(): other = lax.ppermute(cur, axis_name, [(i, i ^ k) for i in range(count)])]
    dot_general x4 -> x0, matrix products: 5.08 us -> none  [the longest x1 3.15 us: per_device(): jnp.einsum('sbkgp,pkd->sbkgd', p_w.astype(jnp.bfloat16), p_vals, preferre...]
    slice x2, local copies, waits for them, and re-layouts: 6 us -> 1.54 us  [the longest x1 1.54 us: per_device(): o_mass = by_owner(k_mass[..., 0].reshape(grid4)).reshape(tp_count, -1)]
    ppermute x6, starting transfers between devices: 11.4 us -> 8.94 us  [_gather_blocks(): other = lax.ppermute(cur, axis_name, [(i, i ^ k) for i in range(count)])]
  transfers between devices with their start and end apart: 27 -> 20, of which waited for: 10 -> 11; matrix products, arithmetic and copies ran while one was open for 17% -> 4% of each run, Pallas kernels for 0% -> 0%
where the time goes in v3:
time: 100 us; the launch traced here: 99.4 us
  starting transfers between devices  31.4 us (31%)
  waiting for transfers between devices  31.1 us (31%)
  matrix products  13.3 us (13%)
  Pallas kernels  8.58 us (9%)
  local copies, waits for them, and re-layouts  7.81 us (8%)
  other arithmetic  4.8 us (5%)
  blocking collectives  1.85 us (2%)
    ppermute x14, starting transfers between devices, _exchange(): lax.ppermute(send, axis_name, [(i, (i + k) % count) for i in range(count)])  22.4 us
    ppermute x6, waiting for transfers between devices, _gather_blocks(): other = lax.ppermute(cur, axis_name, [(i, i ^ k) for i in range(count)])  19.5 us
    dot_general x1, matrix products, per_device(): jnp.einsum('rhd,hdf->rhf', head_rows_in, head_weights, preferred_element_...  12.9 us
    ppermute x14, waiting for transfers between devices, _exchange(): lax.ppermute(send, axis_name, [(i, (i + k) % count) for i in range(count)])  11.6 us
    ppermute x6, starting transfers between devices, _gather_blocks(): other = lax.ppermute(cur, axis_name, [(i, i ^ k) for i in range(count)])  8.94 us
    pallas_call x1, Pallas kernels, _attend_local(): pl.pallas_call(_attend_kernel, grid=(kv_heads,), in_specs=[pl.BlockSpec((...  8.58 us
  transfers between devices with their start and end apart: 20, of which 11 were waited for; matrix products, arithmetic and copies ran while one was open for 4% of the time, Pallas kernels for 0%

profile of v3, /device:TPU:0, one launch (start us, length us, event | category | flops | bytes accessed | tf_op | source)
XLA Modules:
  0.0 99.4 jit_solution(11437174051233758067)
XLA Ops:
  0.0 2.9 %collective-permute-start = (bf16[1,2,4,2048]{3,2,1,0:T(4,128)(2,1)}, bf16[1,2,4,2048]{3,2,1,0:T(4,128)(2,1)S(1)}, u32[]{:S(2)}, u32[]{:S(2)}) collective-permute-start(bf16[1,2,4,2048]{3,2,1,0:T(4,128)(2,1)} %bitcast.156), channel_id=1, source_target_pairs={{0,2},{2,0},{4,6},{6,4},{8,10},{10,8},{12,14},{14,12},{1,3},{3,1},... | collective-permute-start | bytes 98312 | tf_op jit(solution)/shard_map/ppermute | solution.py:29
  2.9 0.8 reshape.170
  3.8 0.7 multiply_exponential_fusion.1
  4.5 0.8 reshape.169
  5.4 0.2 fusion.19
  5.6 0.9 maximum_select_fusion.4
  6.5 1.6 %collective-permute-start.1 = (bf16[2,2,4,2048]{3,2,1,0:T(4,128)(2,1)S(1)}, bf16[2,2,4,2048]{3,2,1,0:T(4,128)(2,1)S(1)}, u32[]{:S(2)}, u32[]{:S(2)}) collective-permute-start(bf16[2,2,4,2048]{3,2,1,0:T(4,128)(2,1)S(1)} %maximum_select_fusion.4), channel_id=1, source_target_pairs={{0,4},{2,6},{4,0},{6,2},{8,12},{10,14},{12,8},{14,10},{1,5},{3,7},... | collective-permute-start | bytes 196616 | tf_op jit(solution)/shard_map/ppermute | solution.py:29
  8.2 2.7 %collective-permute-done.1 = bf16[2,2,4,2048]{3,2,1,0:T(4,128)(2,1)S(1)} collective-permute-done((bf16[2,2,4,2048]{3,2,1,0:T(4,128)(2,1)S(1)}, bf16[2,2,4,2048]{3,2,1,0:T(4,128)(2,1)S(1)}, u32[]{:S(2)}, u32[]{:S(2)}) %collective-permute-start.1) | collective-permute-done | bytes 65568 | tf_op jit(solution)/shard_map/ppermute | solution.py:29
  10.8 0.1 maximum_select_fusion.2
  11.0 2.7 %collective-permute-start.2 = (bf16[4,2,4,2048]{3,2,1,0:T(4,128)(2,1)S(1)}, bf16[4,2,4,2048]{3,2,1,0:T(4,128)(2,1)S(1)}, u32[]{:S(2)}, u32[]{:S(2)}) collective-permute-start(bf16[4,2,4,2048]{3,2,1,0:T(4,128)(2,1)S(1)} %maximum_select_fusion.2), channel_id=1, source_target_pairs={{0,8},{2,10},{4,12},{6,14},{8,0},{10,2},{12,4},{14,6},{1,9},{3,11}... | collective-permute-start | bytes 393224 | tf_op jit(solution)/shard_map/ppermute | solution.py:29
  13.7 1.3 %compare_convert_fusion.valid_ref = f32[4,128]{1,0:T(4,128)} fusion(s32[128]{0:T(128)S(1)} %iota_add_fusion, s32[4]{0:T(128)} %param.12), kind=kLoop, calls=%fused_computation.86 | loop fusion | flops 1024 | bytes 2576 | tf_op jit(solution)/shard_map/convert_element_type | solution.py:138
  15.2 3.4 %collective-permute-done.2 = bf16[4,2,4,2048]{3,2,1,0:T(4,128)(2,1)S(1)} collective-permute-done((bf16[4,2,4,2048]{3,2,1,0:T(4,128)(2,1)S(1)}, bf16[4,2,4,2048]{3,2,1,0:T(4,128)(2,1)S(1)}, u32[]{:S(2)}, u32[]{:S(2)}) %collective-permute-start.2) | collective-permute-done | bytes 131104 | tf_op jit(solution)/shard_map/ppermute | solution.py:29
  18.6 0.3 fusion.3
  18.9 0.2 reshape.165
  19.1 0.7 copy.95
  19.8 8.6 %shard_map.91 = (f32[8,128,128]{2,1,0:T(8,128)}, f32[8,128,128]{2,1,0:T(8,128)}, f32[8,128,128]{2,1,0:T(8,128)}) custom-call(bf16[8,128,128]{2,1,0:T(8,128)(2,1)} %bitcast.149, bf16[2,1024,1024]{2,1,0:T(8,128)(2,1)} %v_ref.1, bf16[2,1024,1024]{2,1,0:T(8,128)(2,1)} %v_ref.1, bf16[2,4,128,1024]{3,2,1,0:T(8,128)(2,1)} %tv_ref.1, ...), custom_call_target="tpu_custom_call" | custom-call | flops 603979776 | bytes 8126464 | tf_op jit(solution)/shard_map/pallas_call | solution.py:94
  28.4 1.5 %slice_reduce_fusion = (f32[8,128]{1,0:T(8,128)S(1)}, f32[8,128]{1,0:T(8,128)S(1)}) fusion(f32[8,128,128]{2,1,0:T(8,128)} %get-tuple-element.10, f32[8,128,128]{2,1,0:T(8,128)} %get-tuple-element.9), kind=kLoop, calls=%fused_computation.8 | loop fusion | bytes 16384 | tf_op jit(solution)/shard_map/slice | solution.py:149
  30.3 1.1 %copy.96 = f32[8,4,2,16,128]{4,3,1,2,0:T(8,128)S(1)} copy(f32[8,4,2,16,128]{4,3,2,1,0:T(8,128)} %bitcast.150) | data formatting | bytes 1048576 | tf_op jit(solution)/shard_map/reshape | solution.py:147
  31.5 1.3 %collective-permute-start.3 = (f32[130,128]{1,0:T(8,128)S(1)}, f32[130,128]{1,0:T(8,128)S(1)}, u32[]{:S(2)}, u32[]{:S(2)}) collective-permute-start(f32[130,128]{1,0:T(8,128)S(1)} %get-tuple-element.17), channel_id=1, source_target_pairs={{0,2},{2,4},{4,6},{6,8},{8,10},{10,12},{12,14},{14,0},{1,3},{3,5},... | collective-permute-start | bytes 199688 | tf_op jit(solution)/shard_map/ppermute | solution.py:48
  32.9 0.7 collective-permute-start.4
  33.5 3.6 %collective-permute-start.5 = (f32[130,128]{1,0:T(8,128)S(1)}, f32[130,128]{1,0:T(8,128)S(1)}, u32[]{:S(2)}, u32[]{:S(2)}) collective-permute-start(f32[130,128]{1,0:T(8,128)S(1)} %get-tuple-element.15), channel_id=1, source_target_pairs={{0,6},{2,8},{4,10},{6,12},{8,14},{10,0},{12,2},{14,4},{1,7},{3,9},... | collective-permute-start | bytes 199688 | tf_op jit(solution)/shard_map/ppermute | solution.py:48
  37.2 0.4 collective-permute-start.6
  37.6 3.1 %collective-permute-start.7 = (f32[130,128]{1,0:T(8,128)S(1)}, f32[130,128]{1,0:T(8,128)S(1)}, u32[]{:S(2)}, u32[]{:S(2)}) collective-permute-start(f32[130,128]{1,0:T(8,128)S(1)} %get-tuple-element.13), channel_id=1, source_target_pairs={{0,10},{2,12},{4,14},{6,0},{8,2},{10,4},{12,6},{14,8},{1,11},{3,13... | collective-permute-start | bytes 199688 | tf_op jit(solution)/shard_map/ppermute | solution.py:48
  40.7 0.3 collective-permute-start.8
  41.0 1.5 %collective-permute-start.9 = (f32[130,128]{1,0:T(8,128)S(1)}, f32[130,128]{1,0:T(8,128)S(1)}, u32[]{:S(2)}, u32[]{:S(2)}) collective-permute-start(f32[130,128]{1,0:T(8,128)S(1)} %get-tuple-element.11), channel_id=1, source_target_pairs={{0,14},{2,0},{4,2},{6,4},{8,6},{10,8},{12,10},{14,12},{1,15},{3,1}... | collective-permute-start | bytes 199688 | tf_op jit(solution)/shard_map/ppermute | solution.py:48
  42.7 2.0 %collective-permute-done.6 = f32[130,128]{1,0:T(8,128)S(1)} collective-permute-done((f32[130,128]{1,0:T(8,128)S(1)}, f32[130,128]{1,0:T(8,128)S(1)}, u32[]{:S(2)}, u32[]{:S(2)}) %collective-permute-start.6) | collective-permute-done | bytes 66592 | tf_op jit(solution)/shard_map/ppermute | solution.py:48
  44.7 1.8 %collective-permute-done.8 = f32[130,128]{1,0:T(8,128)S(1)} collective-permute-done((f32[130,128]{1,0:T(8,128)S(1)}, f32[130,128]{1,0:T(8,128)S(1)}, u32[]{:S(2)}, u32[]{:S(2)}) %collective-permute-start.8) | collective-permute-done | bytes 66592 | tf_op jit(solution)/shard_map/ppermute | solution.py:48
  46.9 0.2 fusion.2
  47.3 0.2 fusion.21
  47.7 1.9 %all_gather.3 = bf16[2,8,2048]{2,0,1:T(2,128)(2,1)S(1)} all-gather(bf16[2,4,2048]{2,0,1:T(2,128)(2,1)S(1)} %copy.114), channel_id=1, replica_groups=mesh['rep'=2,'tp'=8,'sub'=2] {'sub'}, dimensions={1}, use_global_device_ids=true | all-gather | bytes 98304 | tf_op jit(solution)/shard_map/all_gather | solution.py:186
  49.6 12.9 %fusion.1 = f32[16,8192]{1,0:T(8,128)S(1)} fusion(f32[8192]{0:T(1024)S(1)} %dynamic_slice.61, bf16[16,128,8192]{2,1,0:T(8,128)(2,1)} %bitcast.168, bf16[16,16,128]{2,1,0:T(8,128)(2,1)S(1)} %bitcast.165), kind=kOutput, calls=%fused_computation.2 | convolution fusion | flops 543031296 | bytes 34177024 | tf_op jit(solution)/shard_map/rhd,hdf->rhf/dot_general | solution.py:195
  62.5 0.3 copy.134
  62.8 0.5 constant_dynamic-slice_fusion.8
  63.4 4.3 %collective-permute-start.16 = (f32[16,1024]{1,0:T(8,128)S(1)}, f32[16,1024]{1,0:T(8,128)S(1)}, u32[]{:S(2)}, u32[]{:S(2)}) collective-permute-start(f32[16,1024]{1,0:T(8,128)S(1)} %bitcast.164), channel_id=1, source_target_pairs={{0,14},{2,0},{4,2},{6,4},{8,6},{10,8},{12,10},{14,12},{1,15},{3,1}... | collective-permute-start | bytes 196616 | tf_op jit(solution)/shard_map/ppermute | solution.py:48
  67.8 2.0 %collective-permute-start.15 = (f32[16,1024]{1,0:T(8,128)S(1)}, f32[16,1024]{1,0:T(8,128)S(1)}, u32[]{:S(2)}, u32[]{:S(2)}) collective-permute-start(f32[16,1024]{1,0:T(8,128)S(1)} %bitcast.163), channel_id=1, source_target_pairs={{0,12},{2,14},{4,0},{6,2},{8,4},{10,6},{12,8},{14,10},{1,13},{3,15... | collective-permute-start | bytes 196616 | tf_op jit(solution)/shard_map/ppermute | solution.py:48
  69.9 1.2 %collective-permute-start.13 = (f32[16,1024]{1,0:T(8,128)S(1)}, f32[16,1024]{1,0:T(8,128)S(1)}, u32[]{:S(2)}, u32[]{:S(2)}) collective-permute-start(f32[16,1024]{1,0:T(8,128)S(1)} %bitcast.159), channel_id=1, source_target_pairs={{0,8},{2,10},{4,12},{6,14},{8,0},{10,2},{12,4},{14,6},{1,9},{3,11}... | collective-permute-start | bytes 196616 | tf_op jit(solution)/shard_map/ppermute | solution.py:48
  71.1 1.9 %collective-permute-start.12 = (f32[16,1024]{1,0:T(8,128)S(1)}, f32[16,1024]{1,0:T(8,128)S(1)}, u32[]{:S(2)}, u32[]{:S(2)}) collective-permute-start(f32[16,1024]{1,0:T(8,128)S(1)} %bitcast.160), channel_id=1, source_target_pairs={{0,6},{2,8},{4,10},{6,12},{8,14},{10,0},{12,2},{14,4},{1,7},{3,9},... | collective-permute-start | bytes 196616 | tf_op jit(solution)/shard_map/ppermute | solution.py:48
  73.0 1.9 %collective-permute-start.11 = (f32[16,1024]{1,0:T(8,128)S(1)}, f32[16,1024]{1,0:T(8,128)S(1)}, u32[]{:S(2)}, u32[]{:S(2)}) collective-permute-start(f32[16,1024]{1,0:T(8,128)S(1)} %bitcast.162), channel_id=1, source_target_pairs={{0,4},{2,6},{4,8},{6,10},{8,12},{10,14},{12,0},{14,2},{1,5},{3,7},... | collective-permute-start | bytes 196616 | tf_op jit(solution)/shard_map/ppermute | solution.py:48
  74.9 0.2 collective-permute-start.10
  75.2 0.4 collective-permute-done.14
  75.5 5.0 %collective-permute-done.13 = f32[16,1024]{1,0:T(8,128)S(1)} collective-permute-done((f32[16,1024]{1,0:T(8,128)S(1)}, f32[16,1024]{1,0:T(8,128)S(1)}, u32[]{:S(2)}, u32[]{:S(2)}) %collective-permute-start.13) | collective-permute-done | bytes 65568 | tf_op jit(solution)/shard_map/ppermute | solution.py:48
  80.6 2.4 %collective-permute-done.12 = f32[16,1024]{1,0:T(8,128)S(1)} collective-permute-done((f32[16,1024]{1,0:T(8,128)S(1)}, f32[16,1024]{1,0:T(8,128)S(1)}, u32[]{:S(2)}, u32[]{:S(2)}) %collective-permute-start.12) | collective-permute-done | bytes 65568 | tf_op jit(solution)/shard_map/ppermute | solution.py:48
  83.1 3.9 %collective-permute-done.17 = bf16[1,16,1024]{2,1,0:T(8,128)(2,1)S(1)} collective-permute-done((bf16[1,16,1024]{2,1,0:T(8,128)(2,1)S(1)}, bf16[1,16,1024]{2,1,0:T(8,128)(2,1)S(1)}, u32[]{:S(2)}, u32[]{:S(2)}) %collective-permute-start.17) | collective-permute-done | bytes 32800 | tf_op jit(solution)/shard_map/ppermute | solution.py:29
  87.1 4.3 %collective-permute-done.18 = bf16[2,16,1024]{2,1,0:T(8,128)(2,1)S(1)} collective-permute-done((bf16[2,16,1024]{2,1,0:T(8,128)(2,1)S(1)}, bf16[2,16,1024]{2,1,0:T(8,128)(2,1)S(1)}, u32[]{:S(2)}, u32[]{:S(2)}) %collective-permute-start.18) | collective-permute-done | bytes 65568 | tf_op jit(solution)/shard_map/ppermute | solution.py:29
  91.4 1.6 %collective-permute-start.19 = (bf16[4,16,1024]{2,1,0:T(8,128)(2,1)S(1)}, bf16[4,16,1024]{2,1,0:T(8,128)(2,1)S(1)}, u32[]{:S(2)}, u32[]{:S(2)}) collective-permute-start(bf16[4,16,1024]{2,1,0:T(8,128)(2,1)S(1)} %maximum_select_fusion.3), channel_id=1, source_target_pairs={{0,8},{2,10},{4,12},{6,14},{8,0},{10,2},{12,4},{14,6},{1,9},{3,11}... | collective-permute-start | bytes 393224 | tf_op jit(solution)/shard_map/ppermute | solution.py:29
  92.9 5.2 %collective-permute-done.19 = bf16[4,16,1024]{2,1,0:T(8,128)(2,1)S(1)} collective-permute-done((bf16[4,16,1024]{2,1,0:T(8,128)(2,1)S(1)}, bf16[4,16,1024]{2,1,0:T(8,128)(2,1)S(1)}, u32[]{:S(2)}, u32[]{:S(2)}) %collective-permute-start.19) | collective-permute-done | bytes 131104 | tf_op jit(solution)/shard_map/ppermute | solution.py:29
  98.2 0.3 copy.117
  98.6 0.8 add_convert_fusion
  (76 shorter events, 2.4 us)
Async XLA Ops:
  0.0 5.6 %collective-permute-start = (bf16[1,2,4,2048]{3,2,1,0:T(4,128)(2,1)}, bf16[1,2,4,2048]{3,2,1,0:T(4,128)(2,1)S(1)}, u32[]{:S(2)}, u32[]{:S(2)}) collective-permute-start(bf16[1,2,4,2048]{3,2,1,0:T(4,128)(2,1)} %bitcast.156), channel_id=1, source_target_pairs={{0,2},{2,0},{4,6},{6,4},{8,10},{10,8},{12,14},{14,12},{1,3},{3,1},... | collective-permute-start | bytes 98312 | tf_op jit(solution)/shard_map/ppermute | solution.py:29
  6.5 4.3 %collective-permute-start.1 = (bf16[2,2,4,2048]{3,2,1,0:T(4,128)(2,1)S(1)}, bf16[2,2,4,2048]{3,2,1,0:T(4,128)(2,1)S(1)}, u32[]{:S(2)}, u32[]{:S(2)}) collective-permute-start(bf16[2,2,4,2048]{3,2,1,0:T(4,128)(2,1)S(1)} %maximum_select_fusion.4), channel_id=1, source_target_pairs={{0,4},{2,6},{4,0},{6,2},{8,12},{10,14},{12,8},{14,10},{1,5},{3,7},... | collective-permute-start | bytes 196616 | tf_op jit(solution)/shard_map/ppermute | solution.py:29
  11.0 7.6 %collective-permute-start.2 = (bf16[4,2,4,2048]{3,2,1,0:T(4,128)(2,1)S(1)}, bf16[4,2,4,2048]{3,2,1,0:T(4,128)(2,1)S(1)}, u32[]{:S(2)}, u32[]{:S(2)}) collective-permute-start(bf16[4,2,4,2048]{3,2,1,0:T(4,128)(2,1)S(1)} %maximum_select_fusion.2), channel_id=1, source_target_pairs={{0,8},{2,10},{4,12},{6,14},{8,0},{10,2},{12,4},{14,6},{1,9},{3,11}... | collective-permute-start | bytes 393224 | tf_op jit(solution)/shard_map/ppermute | solution.py:29
  31.5 9.2 %collective-permute-start.3 = (f32[130,128]{1,0:T(8,128)S(1)}, f32[130,128]{1,0:T(8,128)S(1)}, u32[]{:S(2)}, u32[]{:S(2)}) collective-permute-start(f32[130,128]{1,0:T(8,128)S(1)} %get-tuple-element.17), channel_id=1, source_target_pairs={{0,2},{2,4},{4,6},{6,8},{8,10},{10,12},{12,14},{14,0},{1,3},{3,5},... | collective-permute-start | bytes 199688 | tf_op jit(solution)/shard_map/ppermute | solution.py:48
  32.9 8.2 %collective-permute-start.4 = (f32[130,128]{1,0:T(8,128)S(1)}, f32[130,128]{1,0:T(8,128)S(1)}, u32[]{:S(2)}, u32[]{:S(2)}) collective-permute-start(f32[130,128]{1,0:T(8,128)S(1)} %get-tuple-element.16), channel_id=1, source_target_pairs={{0,4},{2,6},{4,8},{6,10},{8,12},{10,14},{12,0},{14,2},{1,5},{3,7},... | collective-permute-start | bytes 199688 | tf_op jit(solution)/shard_map/ppermute | solution.py:48
  33.5 9.1 %collective-permute-start.5 = (f32[130,128]{1,0:T(8,128)S(1)}, f32[130,128]{1,0:T(8,128)S(1)}, u32[]{:S(2)}, u32[]{:S(2)}) collective-permute-start(f32[130,128]{1,0:T(8,128)S(1)} %get-tuple-element.15), channel_id=1, source_target_pairs={{0,6},{2,8},{4,10},{6,12},{8,14},{10,0},{12,2},{14,4},{1,7},{3,9},... | collective-permute-start | bytes 199688 | tf_op jit(solution)/shard_map/ppermute | solution.py:48
  37.2 7.5 %collective-permute-start.6 = (f32[130,128]{1,0:T(8,128)S(1)}, f32[130,128]{1,0:T(8,128)S(1)}, u32[]{:S(2)}, u32[]{:S(2)}) collective-permute-start(f32[130,128]{1,0:T(8,128)S(1)} %get-tuple-element.14), channel_id=1, source_target_pairs={{0,8},{2,10},{4,12},{6,14},{8,0},{10,2},{12,4},{14,6},{1,9},{3,11}... | collective-permute-start | bytes 199688 | tf_op jit(solution)/shard_map/ppermute | solution.py:48
  37.6 7.0 %collective-permute-start.7 = (f32[130,128]{1,0:T(8,128)S(1)}, f32[130,128]{1,0:T(8,128)S(1)}, u32[]{:S(2)}, u32[]{:S(2)}) collective-permute-start(f32[130,128]{1,0:T(8,128)S(1)} %get-tuple-element.13), channel_id=1, source_target_pairs={{0,10},{2,12},{4,14},{6,0},{8,2},{10,4},{12,6},{14,8},{1,11},{3,13... | collective-permute-start | bytes 199688 | tf_op jit(solution)/shard_map/ppermute | solution.py:48
  40.7 5.7 %collective-permute-start.8 = (f32[130,128]{1,0:T(8,128)S(1)}, f32[130,128]{1,0:T(8,128)S(1)}, u32[]{:S(2)}, u32[]{:S(2)}) collective-permute-start(f32[130,128]{1,0:T(8,128)S(1)} %get-tuple-element.12), channel_id=1, source_target_pairs={{0,12},{2,14},{4,0},{6,2},{8,4},{10,6},{12,8},{14,10},{1,13},{3,15... | collective-permute-start | bytes 199688 | tf_op jit(solution)/shard_map/ppermute | solution.py:48
  41.0 5.4 %collective-permute-start.9 = (f32[130,128]{1,0:T(8,128)S(1)}, f32[130,128]{1,0:T(8,128)S(1)}, u32[]{:S(2)}, u32[]{:S(2)}) collective-permute-start(f32[130,128]{1,0:T(8,128)S(1)} %get-tuple-element.11), channel_id=1, source_target_pairs={{0,14},{2,0},{4,2},{6,4},{8,6},{10,8},{12,10},{14,12},{1,15},{3,1}... | collective-permute-start | bytes 199688 | tf_op jit(solution)/shard_map/ppermute | solution.py:48
  49.6 20.2 %copy-start.1 = (s32[128]{0:T(128)S(1)}, s32[128]{0:T(128)}, u32[]{:S(2)}) copy-start(s32[128]{0:T(128)} %param.16) | copy-start | bytes 1540
  49.6 49.0 %copy-start = (bf16[2,8,8192]{2,1,0:T(8,128)(2,1)S(1)}, bf16[2,8,8192]{2,1,0:T(8,128)(2,1)}, u32[]{:S(2)}) copy-start(bf16[2,8,8192]{2,1,0:T(8,128)(2,1)} %param.17) | copy-start | bytes 786436
  63.4 9.6 %collective-permute-start.16 = (f32[16,1024]{1,0:T(8,128)S(1)}, f32[16,1024]{1,0:T(8,128)S(1)}, u32[]{:S(2)}, u32[]{:S(2)}) collective-permute-start(f32[16,1024]{1,0:T(8,128)S(1)} %bitcast.164), channel_id=1, source_target_pairs={{0,14},{2,0},{4,2},{6,4},{8,6},{10,8},{12,10},{14,12},{1,15},{3,1}... | collective-permute-start | bytes 196616 | tf_op jit(solution)/shard_map/ppermute | solution.py:48
  67.8 7.1 %collective-permute-start.15 = (f32[16,1024]{1,0:T(8,128)S(1)}, f32[16,1024]{1,0:T(8,128)S(1)}, u32[]{:S(2)}, u32[]{:S(2)}) collective-permute-start(f32[16,1024]{1,0:T(8,128)S(1)} %bitcast.163), channel_id=1, source_target_pairs={{0,12},{2,14},{4,0},{6,2},{8,4},{10,6},{12,8},{14,10},{1,13},{3,15... | collective-permute-start | bytes 196616 | tf_op jit(solution)/shard_map/ppermute | solution.py:48
  69.8 5.7 %collective-permute-start.14 = (f32[16,1024]{1,0:T(8,128)S(1)}, f32[16,1024]{1,0:T(8,128)S(1)}, u32[]{:S(2)}, u32[]{:S(2)}) collective-permute-start(f32[16,1024]{1,0:T(8,128)S(1)} %bitcast.158), channel_id=1, source_target_pairs={{0,10},{2,12},{4,14},{6,0},{8,2},{10,4},{12,6},{14,8},{1,11},{3,13... | collective-permute-start | bytes 196616 | tf_op jit(solution)/shard_map/ppermute | solution.py:48
  69.9 10.7 %collective-permute-start.13 = (f32[16,1024]{1,0:T(8,128)S(1)}, f32[16,1024]{1,0:T(8,128)S(1)}, u32[]{:S(2)}, u32[]{:S(2)}) collective-permute-start(f32[16,1024]{1,0:T(8,128)S(1)} %bitcast.159), channel_id=1, source_target_pairs={{0,8},{2,10},{4,12},{6,14},{8,0},{10,2},{12,4},{14,6},{1,9},{3,11}... | collective-permute-start | bytes 196616 | tf_op jit(solution)/shard_map/ppermute | solution.py:48
  71.1 11.9 %collective-permute-start.12 = (f32[16,1024]{1,0:T(8,128)S(1)}, f32[16,1024]{1,0:T(8,128)S(1)}, u32[]{:S(2)}, u32[]{:S(2)}) collective-permute-start(f32[16,1024]{1,0:T(8,128)S(1)} %bitcast.160), channel_id=1, source_target_pairs={{0,6},{2,8},{4,10},{6,12},{8,14},{10,0},{12,2},{14,4},{1,7},{3,9},... | collective-permute-start | bytes 196616 | tf_op jit(solution)/shard_map/ppermute | solution.py:48
  73.0 10.0 %collective-permute-start.11 = (f32[16,1024]{1,0:T(8,128)S(1)}, f32[16,1024]{1,0:T(8,128)S(1)}, u32[]{:S(2)}, u32[]{:S(2)}) collective-permute-start(f32[16,1024]{1,0:T(8,128)S(1)} %bitcast.162), channel_id=1, source_target_pairs={{0,4},{2,6},{4,8},{6,10},{8,12},{10,14},{12,0},{14,2},{1,5},{3,7},... | collective-permute-start | bytes 196616 | tf_op jit(solution)/shard_map/ppermute | solution.py:48
  74.9 8.1 %collective-permute-start.10 = (f32[16,1024]{1,0:T(8,128)S(1)}, f32[16,1024]{1,0:T(8,128)S(1)}, u32[]{:S(2)}, u32[]{:S(2)}) collective-permute-start(f32[16,1024]{1,0:T(8,128)S(1)} %bitcast.161), channel_id=1, source_target_pairs={{0,2},{2,4},{4,6},{6,8},{8,10},{10,12},{12,14},{14,0},{1,3},{3,5},... | collective-permute-start | bytes 196616 | tf_op jit(solution)/shard_map/ppermute | solution.py:48
  83.0 4.0 %collective-permute-start.17 = (bf16[1,16,1024]{2,1,0:T(8,128)(2,1)S(1)}, bf16[1,16,1024]{2,1,0:T(8,128)(2,1)S(1)}, u32[]{:S(2)}, u32[]{:S(2)}) collective-permute-start(bf16[1,16,1024]{2,1,0:T(8,128)(2,1)S(1)} %fusion.18), channel_id=1, source_target_pairs={{0,2},{2,0},{4,6},{6,4},{8,10},{10,8},{12,14},{14,12},{1,3},{3,1},... | collective-permute-start | bytes 98312 | tf_op jit(solution)/shard_map/ppermute | solution.py:29
  87.0 4.3 %collective-permute-start.18 = (bf16[2,16,1024]{2,1,0:T(8,128)(2,1)S(1)}, bf16[2,16,1024]{2,1,0:T(8,128)(2,1)S(1)}, u32[]{:S(2)}, u32[]{:S(2)}) collective-permute-start(bf16[2,16,1024]{2,1,0:T(8,128)(2,1)S(1)} %maximum_select_fusion.5), channel_id=1, source_target_pairs={{0,4},{2,6},{4,0},{6,2},{8,12},{10,14},{12,8},{14,10},{1,5},{3,7},... | collective-permute-start | bytes 196616 | tf_op jit(solution)/shard_map/ppermute | solution.py:29
  91.4 6.8 %collective-permute-start.19 = (bf16[4,16,1024]{2,1,0:T(8,128)(2,1)S(1)}, bf16[4,16,1024]{2,1,0:T(8,128)(2,1)S(1)}, u32[]{:S(2)}, u32[]{:S(2)}) collective-permute-start(bf16[4,16,1024]{2,1,0:T(8,128)(2,1)S(1)} %maximum_select_fusion.3), channel_id=1, source_target_pairs={{0,8},{2,10},{4,12},{6,14},{8,0},{10,2},{12,4},{14,6},{1,9},{3,11}... | collective-permute-start | bytes 393224 | tf_op jit(solution)/shard_map/ppermute | solution.py:29

commit v4 on v3

--- a/solution.py
+++ b/solution.py
@@ -116,6 +116,49 @@
     )(q_rows, prefix_kv, prefix_kv, tail_kv, tail_kv, valid)
 
 
+def _project_kernel(blk_ref, rows_ref, w_ref, a_ref, out_ref):
+    @pl.when(pl.program_id(0) == 0)
+    def _():
+        out_ref[...] = jnp.zeros_like(out_ref)
+
+    inv_rows = rows_ref.shape[1] // DH
+    acc = out_ref[...]
+    a = a_ref[...]
+    for h in range(inv_rows):
+        term = jnp.dot(
+            rows_ref[:, h * DH:(h + 1) * DH], w_ref[h * DH:(h + 1) * DH, :],
+            preferred_element_type=jnp.float32,
+        )
+        acc = acc + jnp.clip(term / a, -127.0, 127.0)
+    out_ref[...] = acc
+
+
+def _project_block(blk, rows, out_weight, local_a, piece_cols, heads_per_step=4):
+    n_rows, width = rows.shape
+    chunk = heads_per_step * DH
+    steps = width // chunk
+    grid_spec = pltpu.PrefetchScalarGridSpec(
+        num_scalar_prefetch=1,
+        grid=(steps,),
+        in_specs=[
+            pl.BlockSpec((n_rows, chunk), lambda c, b: (0, c)),
+            pl.BlockSpec((chunk, piece_cols), lambda c, b: (c, b[0])),
+            pl.BlockSpec((1, piece_cols), lambda c, b: (0, b[0])),
+        ],
+        out_specs=pl.BlockSpec((n_rows, piece_cols), lambda c, b: (0, 0)),
+    )
+    return pl.pallas_call(
+        _project_kernel,
+        grid_spec=grid_spec,
+        out_shape=jax.ShapeDtypeStruct((n_rows, piece_cols), jnp.float32),
+        cost_estimate=pl.CostEstimate(
+            flops=2 * n_rows * width * piece_cols,
+            transcendentals=0,
+            bytes_accessed=2 * width * piece_cols + 2 * rows.size + 8 * n_rows * piece_cols,
+        ),
+    )(jnp.reshape(blk, (1,)).astype(jnp.int32), rows, out_weight, local_a)
+
+
 def per_device(
     queries, prefix_kv, tail_kv, tail_lengths, fresh_kv, out_weight, scale_in, scale_out, residual
 ):
@@ -192,15 +235,30 @@
     scale_b = jnp.repeat(jnp.exp2(-scale_out.astype(jnp.float32)), 128)
     local_a = lax.dynamic_slice_in_dim(scale_a, sub_rank * local_width, local_width, 0)
     local_b = lax.dynamic_slice_in_dim(scale_b, sub_rank * local_width, local_width, 0)
-    per_head_term = jnp.einsum(
-        "rhd,hdf->rhf", head_rows_in, head_weights, preferred_element_type=jnp.float32
-    )
-    clipped = jnp.clip(per_head_term / local_a[None, None, :], -127.0, 127.0).sum(1)
-
     piece_cols = local_width // tp_count
-    pieces = jnp.moveaxis(clipped.reshape(steps_n * samples, tp_count, piece_cols), 1, 0)
-    got_pieces = _exchange(pieces, "tp", tp_count)
-    summed = got_pieces.sum(0)
+    if tp_count <= 8 and piece_cols % 128 == 0:
+        rows_flat = gathered.reshape(steps_n * samples, width_dev)
+        parts = []
+        for shift in range(tp_count):
+            blk = (tp_rank + shift) % tp_count
+            part = _project_block(
+                blk, rows_flat, out_weight, local_a.reshape(1, -1), piece_cols,
+                heads_per_step=4 if heads_dev % 4 == 0 else 1,
+            )
+            if shift != 0:
+                part = lax.ppermute(
+                    part, "tp", [(i, (i + shift) % tp_count) for i in range(tp_count)]
+                )
+            parts.append(part)
+        summed = sum(parts)
+    else:
+        per_head_term = jnp.einsum(
+            "rhd,hdf->rhf", head_rows_in, head_weights, preferred_element_type=jnp.float32
+        )
+        clipped = jnp.clip(per_head_term / local_a[None, None, :], -127.0, 127.0).sum(1)
+        pieces = jnp.moveaxis(clipped.reshape(steps_n * samples, tp_count, piece_cols), 1, 0)
+        got_pieces = _exchange(pieces, "tp", tp_count)
+        summed = got_pieces.sum(0)
     piece_start = sub_rank * local_width + tp_rank * piece_cols
     piece_a = lax.dynamic_slice_in_dim(scale_a, piece_start, piece_cols, 0)
     piece_b = lax.dynamic_slice_in_dim(scale_b, piece_start, piece_cols, 0)

time: 100 us -> 116 us (1.16)
  Pallas kernels: 8.58 us -> 41 us
  matrix products: 13.3 us -> 0.39 us
  waiting for transfers between devices: 31.1 us -> 27.1 us
  starting transfers between devices: 31.4 us -> 30.1 us
    pallas_call x0 -> x8, Pallas kernels: none -> 32.5 us  [_project_block(): pl.pallas_call(_project_kernel, grid_spec=grid_spec, out_shape=jax.ShapeD...]
    dot_general x1 -> x0, matrix products: 12.9 us -> none  [per_device(): jnp.einsum('rhd,hdf->rhf', head_rows_in, head_weights, preferred_element_...]
    ppermute x14 -> x7, starting transfers between devices: 22.4 us -> 10.9 us  [_exchange(): lax.ppermute(send, axis_name, [(i, (i + k) % count) for i in range(count)])]
    ppermute x0 -> x7, starting transfers between devices: none -> 11.3 us  [per_device(): lax.ppermute(part, 'tp', [(i, (i + shift) % tp_count) for i in range(tp_c...]
    ppermute x14 -> x7, waiting for transfers between devices: 11.6 us -> 3.86 us  [_exchange(): lax.ppermute(send, axis_name, [(i, (i + k) % count) for i in range(count)])]
    ppermute x0 -> x7, waiting for transfers between devices: none -> 2.7 us  [per_device(): lax.ppermute(part, 'tp', [(i, (i + shift) % tp_count) for i in range(tp_c...]
  transfers between devices with their start and end apart: 20 -> 20, of which waited for: 11 -> 9; matrix products, arithmetic and copies ran while one was open for 4% -> 4% of each run, Pallas kernels for 0% -> 25%
where the time goes in v4:
time: 116 us; the launch traced here: 115 us
  Pallas kernels  41 us (35%)
  starting transfers between devices  30.1 us (26%)
  waiting for transfers between devices  27.1 us (23%)
  local copies, waits for them, and re-layouts  8.09 us (7%)
  other arithmetic  5.64 us (5%)
  blocking collectives  1.85 us (2%)
    pallas_call x8, Pallas kernels, _project_block(): pl.pallas_call(_project_kernel, grid_spec=grid_spec, out_shape=jax.ShapeD...  32.5 us
    ppermute x6, waiting for transfers between devices, _gather_blocks(): other = lax.ppermute(cur, axis_name, [(i, i ^ k) for i in range(count)])  20.5 us
    ppermute x7, starting transfers between devices, per_device(): lax.ppermute(part, 'tp', [(i, (i + shift) % tp_count) for i in range(tp_c...  11.3 us
    ppermute x7, starting transfers between devices, _exchange(): lax.ppermute(send, axis_name, [(i, (i + k) % count) for i in range(count)])  10.9 us
    pallas_call x1, Pallas kernels, _attend_local(): pl.pallas_call(_attend_kernel, grid=(kv_heads,), in_specs=[pl.BlockSpec((...  8.58 us
    ppermute x6, starting transfers between devices, _gather_blocks(): other = lax.ppermute(cur, axis_name, [(i, i ^ k) for i in range(count)])  7.97 us
    ppermute x7, waiting for transfers between devices, _exchange(): lax.ppermute(send, axis_name, [(i, (i + k) % count) for i in range(count)])  3.86 us
    ppermute x7, waiting for transfers between devices, per_device(): lax.ppermute(part, 'tp', [(i, (i + shift) % tp_count) for i in range(tp_c...  2.7 us
  transfers between devices with their start and end apart: 20, of which 9 were waited for; matrix products, arithmetic and copies ran while one was open for 4% of the time, Pallas kernels for 25%

profile of v4, /device:TPU:0, one launch (start us, length us, event | category | flops | bytes accessed | tf_op | source)
XLA Modules:
  0.0 114.7 jit_solution(774835018174867495)
XLA Ops:
  0.0 2.9 %collective-permute-start = (bf16[1,2,4,2048]{3,2,1,0:T(4,128)(2,1)}, bf16[1,2,4,2048]{3,2,1,0:T(4,128)(2,1)S(1)}, u32[]{:S(2)}, u32[]{:S(2)}) collective-permute-start(bf16[1,2,4,2048]{3,2,1,0:T(4,128)(2,1)} %bitcast.129), channel_id=1, source_target_pairs={{0,2},{2,0},{4,6},{6,4},{8,10},{10,8},{12,14},{14,12},{1,3},{3,1},... | collective-permute-start | bytes 98312 | tf_op jit(solution)/shard_map/ppermute | solution.py:29
  2.9 0.8 reshape.142
  3.8 0.7 multiply_exponential_fusion.1
  4.5 0.8 reshape.141
  5.6 0.9 maximum_select_fusion.4
  6.5 1.6 %collective-permute-start.1 = (bf16[2,2,4,2048]{3,2,1,0:T(4,128)(2,1)S(1)}, bf16[2,2,4,2048]{3,2,1,0:T(4,128)(2,1)S(1)}, u32[]{:S(2)}, u32[]{:S(2)}) collective-permute-start(bf16[2,2,4,2048]{3,2,1,0:T(4,128)(2,1)S(1)} %maximum_select_fusion.4), channel_id=1, source_target_pairs={{0,4},{2,6},{4,0},{6,2},{8,12},{10,14},{12,8},{14,10},{1,5},{3,7},... | collective-permute-start | bytes 196616 | tf_op jit(solution)/shard_map/ppermute | solution.py:29
  8.2 2.7 %collective-permute-done.1 = bf16[2,2,4,2048]{3,2,1,0:T(4,128)(2,1)S(1)} collective-permute-done((bf16[2,2,4,2048]{3,2,1,0:T(4,128)(2,1)S(1)}, bf16[2,2,4,2048]{3,2,1,0:T(4,128)(2,1)S(1)}, u32[]{:S(2)}, u32[]{:S(2)}) %collective-permute-start.1) | collective-permute-done | bytes 65568 | tf_op jit(solution)/shard_map/ppermute | solution.py:29
  11.0 2.7 %collective-permute-start.2 = (bf16[4,2,4,2048]{3,2,1,0:T(4,128)(2,1)S(1)}, bf16[4,2,4,2048]{3,2,1,0:T(4,128)(2,1)S(1)}, u32[]{:S(2)}, u32[]{:S(2)}) collective-permute-start(bf16[4,2,4,2048]{3,2,1,0:T(4,128)(2,1)S(1)} %maximum_select_fusion.2), channel_id=1, source_target_pairs={{0,8},{2,10},{4,12},{6,14},{8,0},{10,2},{12,4},{14,6},{1,9},{3,11}... | collective-permute-start | bytes 393224 | tf_op jit(solution)/shard_map/ppermute | solution.py:29
  13.7 1.3 %compare_convert_fusion.valid_ref = f32[4,128]{1,0:T(4,128)} fusion(s32[128]{0:T(128)S(1)} %iota_add_fusion, s32[4]{0:T(128)} %param.12), kind=kLoop, calls=%fused_computation.58 | loop fusion | flops 1024 | bytes 2576 | tf_op jit(solution)/shard_map/convert_element_type | solution.py:181
  15.1 0.6 dynamic_slice.50
  15.7 2.8 %collective-permute-done.2 = bf16[4,2,4,2048]{3,2,1,0:T(4,128)(2,1)S(1)} collective-permute-done((bf16[4,2,4,2048]{3,2,1,0:T(4,128)(2,1)S(1)}, bf16[4,2,4,2048]{3,2,1,0:T(4,128)(2,1)S(1)}, u32[]{:S(2)}, u32[]{:S(2)}) %collective-permute-start.2) | collective-permute-done | bytes 131104 | tf_op jit(solution)/shard_map/ppermute | solution.py:29
  18.6 0.3 fusion.1
  19.1 0.7 copy.76
  19.8 8.6 %shard_map.91 = (f32[8,128,128]{2,1,0:T(8,128)}, f32[8,128,128]{2,1,0:T(8,128)}, f32[8,128,128]{2,1,0:T(8,128)}) custom-call(bf16[8,128,128]{2,1,0:T(8,128)(2,1)} %bitcast.124, bf16[2,1024,1024]{2,1,0:T(8,128)(2,1)} %v_ref.1, bf16[2,1024,1024]{2,1,0:T(8,128)(2,1)} %v_ref.1, bf16[2,4,128,1024]{3,2,1,0:T(8,128)(2,1)} %tv_ref.1, ...), custom_call_target="tpu_custom_call" | custom-call | flops 603979776 | bytes 8126464 | tf_op jit(solution)/shard_map/pallas_call | solution.py:94
  28.4 1.5 %slice_reduce_fusion = (f32[8,128]{1,0:T(8,128)S(1)}, f32[8,128]{1,0:T(8,128)S(1)}) fusion(f32[8,128,128]{2,1,0:T(8,128)} %get-tuple-element.10, f32[8,128,128]{2,1,0:T(8,128)} %get-tuple-element.9), kind=kLoop, calls=%fused_computation.5 | loop fusion | bytes 16384 | tf_op jit(solution)/shard_map/slice | solution.py:192
  30.3 1.1 copy.77
  31.5 1.3 %collective-permute-start.3 = (f32[130,128]{1,0:T(8,128)S(1)}, f32[130,128]{1,0:T(8,128)S(1)}, u32[]{:S(2)}, u32[]{:S(2)}) collective-permute-start(f32[130,128]{1,0:T(8,128)S(1)} %get-tuple-element.17), channel_id=1, source_target_pairs={{0,2},{2,4},{4,6},{6,8},{8,10},{10,12},{12,14},{14,0},{1,3},{3,5},... | collective-permute-start | bytes 199688 | tf_op jit(solution)/shard_map/ppermute | solution.py:48
  32.9 0.7 collective-permute-start.4
  33.5 3.6 %collective-permute-start.5 = (f32[130,128]{1,0:T(8,128)S(1)}, f32[130,128]{1,0:T(8,128)S(1)}, u32[]{:S(2)}, u32[]{:S(2)}) collective-permute-start(f32[130,128]{1,0:T(8,128)S(1)} %get-tuple-element.15), channel_id=1, source_target_pairs={{0,6},{2,8},{4,10},{6,12},{8,14},{10,0},{12,2},{14,4},{1,7},{3,9},... | collective-permute-start | bytes 199688 | tf_op jit(solution)/shard_map/ppermute | solution.py:48
  37.2 0.4 collective-permute-start.6
  37.6 3.1 %collective-permute-start.7 = (f32[130,128]{1,0:T(8,128)S(1)}, f32[130,128]{1,0:T(8,128)S(1)}, u32[]{:S(2)}, u32[]{:S(2)}) collective-permute-start(f32[130,128]{1,0:T(8,128)S(1)} %get-tuple-element.13), channel_id=1, source_target_pairs={{0,10},{2,12},{4,14},{6,0},{8,2},{10,4},{12,6},{14,8},{1,11},{3,13... | collective-permute-start | bytes 199688 | tf_op jit(solution)/shard_map/ppermute | solution.py:48
  41.0 1.5 %collective-permute-start.9 = (f32[130,128]{1,0:T(8,128)S(1)}, f32[130,128]{1,0:T(8,128)S(1)}, u32[]{:S(2)}, u32[]{:S(2)}) collective-permute-start(f32[130,128]{1,0:T(8,128)S(1)} %get-tuple-element.11), channel_id=1, source_target_pairs={{0,14},{2,0},{4,2},{6,4},{8,6},{10,8},{12,10},{14,12},{1,15},{3,1}... | collective-permute-start | bytes 199688 | tf_op jit(solution)/shard_map/ppermute | solution.py:48
  42.7 1.9 %collective-permute-done.6 = f32[130,128]{1,0:T(8,128)S(1)} collective-permute-done((f32[130,128]{1,0:T(8,128)S(1)}, f32[130,128]{1,0:T(8,128)S(1)}, u32[]{:S(2)}, u32[]{:S(2)}) %collective-permute-start.6) | collective-permute-done | bytes 66592 | tf_op jit(solution)/shard_map/ppermute | solution.py:48
  44.7 1.8 %collective-permute-done.8 = f32[130,128]{1,0:T(8,128)S(1)} collective-permute-done((f32[130,128]{1,0:T(8,128)S(1)}, f32[130,128]{1,0:T(8,128)S(1)}, u32[]{:S(2)}, u32[]{:S(2)}) %collective-permute-start.8) | collective-permute-done | bytes 66592 | tf_op jit(solution)/shard_map/ppermute | solution.py:48
  47.7 1.9 %all_gather.3 = bf16[2,8,2048]{2,0,1:T(2,128)(2,1)S(1)} all-gather(bf16[2,4,2048]{2,0,1:T(2,128)(2,1)S(1)} %copy.95), channel_id=1, replica_groups=mesh['rep'=2,'tp'=8,'sub'=2] {'sub'}, dimensions={1}, use_global_device_ids=true | all-gather | bytes 98304 | tf_op jit(solution)/shard_map/all_gather | solution.py:229
  49.5 0.7 copy.111
  50.2 4.0 %shard_map.99 = f32[16,1024]{1,0:T(8,128)} custom-call(s32[1]{0:T(128)} %bitcast.42.blk_ref, bf16[16,2048]{1,0:T(8,128)(2,1)} %bitcast.107, bf16[2048,8192]{1,0:T(8,128)(2,1)} %w_ref.15, f32[1,8192]{1,0:T(1,128)} %bitcast.115), custom_call_target="tpu_custom_call" | custom-call | flops 67108864 | bytes 4390912 | tf_op jit(solution)/shard_map/pallas_call | solution.py:150
  54.2 4.3 %collective-permute-start.16 = (f32[16,1024]{1,0:T(8,128)}, f32[16,1024]{1,0:T(8,128)S(1)}, u32[]{:S(2)}, u32[]{:S(2)}) collective-permute-start(f32[16,1024]{1,0:T(8,128)} %shard_map.99), channel_id=1, source_target_pairs={{0,14},{2,0},{4,2},{6,4},{8,6},{10,8},{12,10},{14,12},{1,15},{3,1}... | collective-permute-start | bytes 196616 | tf_op jit(solution)/shard_map/ppermute | solution.py:249
  58.5 4.0 %shard_map.98 = f32[16,1024]{1,0:T(8,128)} custom-call(s32[1]{0:T(128)} %bitcast.41.blk_ref, bf16[16,2048]{1,0:T(8,128)(2,1)} %bitcast.108, bf16[2048,8192]{1,0:T(8,128)(2,1)} %w_ref.15, f32[1,8192]{1,0:T(1,128)} %bitcast.116), custom_call_target="tpu_custom_call" | custom-call | flops 67108864 | bytes 4390912 | tf_op jit(solution)/shard_map/pallas_call | solution.py:150
  62.6 2.0 %collective-permute-start.15 = (f32[16,1024]{1,0:T(8,128)}, f32[16,1024]{1,0:T(8,128)S(1)}, u32[]{:S(2)}, u32[]{:S(2)}) collective-permute-start(f32[16,1024]{1,0:T(8,128)} %shard_map.98), channel_id=1, source_target_pairs={{0,12},{2,14},{4,0},{6,2},{8,4},{10,6},{12,8},{14,10},{1,13},{3,15... | collective-permute-start | bytes 196616 | tf_op jit(solution)/shard_map/ppermute | solution.py:249
  64.5 4.0 %shard_map.97 = f32[16,1024]{1,0:T(8,128)} custom-call(s32[1]{0:T(128)} %bitcast.40.blk_ref, bf16[16,2048]{1,0:T(8,128)(2,1)} %bitcast.109, bf16[2048,8192]{1,0:T(8,128)(2,1)} %w_ref.15, f32[1,8192]{1,0:T(1,128)} %bitcast.117), custom_call_target="tpu_custom_call" | custom-call | flops 67108864 | bytes 4390912 | tf_op jit(solution)/shard_map/pallas_call | solution.py:150
  68.6 4.0 %shard_map.96 = f32[16,1024]{1,0:T(8,128)} custom-call(s32[1]{0:T(128)} %bitcast.39.blk_ref, bf16[16,2048]{1,0:T(8,128)(2,1)} %bitcast.110, bf16[2048,8192]{1,0:T(8,128)(2,1)} %w_ref.15, f32[1,8192]{1,0:T(1,128)} %bitcast.118), custom_call_target="tpu_custom_call" | custom-call | flops 67108864 | bytes 4390912 | tf_op jit(solution)/shard_map/pallas_call | solution.py:150
  72.6 1.1 collective-permute-start.13
  73.7 4.0 %shard_map.95 = f32[16,1024]{1,0:T(8,128)} custom-call(s32[1]{0:T(128)} %bitcast.38.blk_ref, bf16[16,2048]{1,0:T(8,128)(2,1)} %bitcast.111, bf16[2048,8192]{1,0:T(8,128)(2,1)} %w_ref.15, f32[1,8192]{1,0:T(1,128)} %bitcast.119), custom_call_target="tpu_custom_call" | custom-call | flops 67108864 | bytes 4390912 | tf_op jit(solution)/shard_map/pallas_call | solution.py:150
  77.8 1.8 %collective-permute-start.12 = (f32[16,1024]{1,0:T(8,128)}, f32[16,1024]{1,0:T(8,128)S(1)}, u32[]{:S(2)}, u32[]{:S(2)}) collective-permute-start(f32[16,1024]{1,0:T(8,128)} %shard_map.95), channel_id=1, source_target_pairs={{0,6},{2,8},{4,10},{6,12},{8,14},{10,0},{12,2},{14,4},{1,7},{3,9},... | collective-permute-start | bytes 196616 | tf_op jit(solution)/shard_map/ppermute | solution.py:249
  79.6 4.0 %shard_map.94 = f32[16,1024]{1,0:T(8,128)} custom-call(s32[1]{0:T(128)} %bitcast.37.blk_ref, bf16[16,2048]{1,0:T(8,128)(2,1)} %bitcast.112, bf16[2048,8192]{1,0:T(8,128)(2,1)} %w_ref.15, f32[1,8192]{1,0:T(1,128)} %bitcast.120), custom_call_target="tpu_custom_call" | custom-call | flops 67108864 | bytes 4390912 | tf_op jit(solution)/shard_map/pallas_call | solution.py:150
  83.6 4.1 %shard_map.93 = f32[16,1024]{1,0:T(8,128)} custom-call(s32[1]{0:T(128)} %bitcast.36.blk_ref, bf16[16,2048]{1,0:T(8,128)(2,1)} %bitcast.113, bf16[2048,8192]{1,0:T(8,128)(2,1)} %w_ref.15, f32[1,8192]{1,0:T(1,128)} %bitcast.121), custom_call_target="tpu_custom_call" | custom-call | flops 67108864 | bytes 4390912 | tf_op jit(solution)/shard_map/pallas_call | solution.py:150
  87.7 1.9 %collective-permute-start.11 = (f32[16,1024]{1,0:T(8,128)S(1)}, f32[16,1024]{1,0:T(8,128)S(1)}, u32[]{:S(2)}, u32[]{:S(2)}) collective-permute-start(f32[16,1024]{1,0:T(8,128)S(1)} %copy-done.2), channel_id=1, source_target_pairs={{0,4},{2,6},{4,8},{6,10},{8,12},{10,14},{12,0},{14,2},{1,5},{3,7},... | collective-permute-start | bytes 196616 | tf_op jit(solution)/shard_map/ppermute | solution.py:249
  90.0 4.1 %shard_map.92 = f32[16,1024]{1,0:T(8,128)} custom-call(s32[1]{0:T(128)} %bitcast.blk_ref, bf16[16,2048]{1,0:T(8,128)(2,1)} %bitcast.114, bf16[2048,8192]{1,0:T(8,128)(2,1)} %w_ref.15, f32[1,8192]{1,0:T(1,128)} %bitcast.122), custom_call_target="tpu_custom_call" | custom-call | flops 67108864 | bytes 4390912 | tf_op jit(solution)/shard_map/pallas_call | solution.py:150
  94.1 2.7 %collective-permute-done.10 = f32[16,1024]{1,0:T(8,128)S(1)} collective-permute-done((f32[16,1024]{1,0:T(8,128)}, f32[16,1024]{1,0:T(8,128)S(1)}, u32[]{:S(2)}, u32[]{:S(2)}) %collective-permute-start.10) | collective-permute-done | bytes 65568 | tf_op jit(solution)/shard_map/ppermute | solution.py:249
  96.8 0.9 fusion.7
  97.7 0.3 collective-permute-start.17
  98.0 3.7 %collective-permute-done.17 = bf16[1,16,1024]{2,1,0:T(8,128)(2,1)S(1)} collective-permute-done((bf16[1,16,1024]{2,1,0:T(8,128)(2,1)S(1)}, bf16[1,16,1024]{2,1,0:T(8,128)(2,1)S(1)}, u32[]{:S(2)}, u32[]{:S(2)}) %collective-permute-start.17) | collective-permute-done | bytes 32800 | tf_op jit(solution)/shard_map/ppermute | solution.py:29
  101.7 4.9 %collective-permute-done.18 = bf16[2,16,1024]{2,1,0:T(8,128)(2,1)S(1)} collective-permute-done((bf16[2,16,1024]{2,1,0:T(8,128)(2,1)S(1)}, bf16[2,16,1024]{2,1,0:T(8,128)(2,1)S(1)}, u32[]{:S(2)}, u32[]{:S(2)}) %collective-permute-start.18) | collective-permute-done | bytes 65568 | tf_op jit(solution)/shard_map/ppermute | solution.py:29
  106.6 0.3 collective-permute-start.19
  107.0 6.5 %collective-permute-done.19 = bf16[4,16,1024]{2,1,0:T(8,128)(2,1)S(1)} collective-permute-done((bf16[4,16,1024]{2,1,0:T(8,128)(2,1)S(1)}, bf16[4,16,1024]{2,1,0:T(8,128)(2,1)S(1)}, u32[]{:S(2)}, u32[]{:S(2)}) %collective-permute-start.19) | collective-permute-done | bytes 131104 | tf_op jit(solution)/shard_map/ppermute | solution.py:29
  113.5 0.3 copy.97
  113.9 0.8 add_convert_fusion
  (78 shorter events, 3.5 us)
Async XLA Ops:
  0.0 5.6 %collective-permute-start = (bf16[1,2,4,2048]{3,2,1,0:T(4,128)(2,1)}, bf16[1,2,4,2048]{3,2,1,0:T(4,128)(2,1)S(1)}, u32[]{:S(2)}, u32[]{:S(2)}) collective-permute-start(bf16[1,2,4,2048]{3,2,1,0:T(4,128)(2,1)} %bitcast.129), channel_id=1, source_target_pairs={{0,2},{2,0},{4,6},{6,4},{8,10},{10,8},{12,14},{14,12},{1,3},{3,1},... | collective-permute-start | bytes 98312 | tf_op jit(solution)/shard_map/ppermute | solution.py:29
  4.5 85.4 %copy-start.1 = (f32[16384]{0:T(1024)}, f32[16384]{0:T(1024)S(1)}, u32[]{:S(2)}) copy-start(f32[16384]{0:T(1024)S(1)} %broadcast_bitcast_fusion.1) | copy-start | bytes 196612
  6.5 4.3 %collective-permute-start.1 = (bf16[2,2,4,2048]{3,2,1,0:T(4,128)(2,1)S(1)}, bf16[2,2,4,2048]{3,2,1,0:T(4,128)(2,1)S(1)}, u32[]{:S(2)}, u32[]{:S(2)}) collective-permute-start(bf16[2,2,4,2048]{3,2,1,0:T(4,128)(2,1)S(1)} %maximum_select_fusion.4), channel_id=1, source_target_pairs={{0,4},{2,6},{4,0},{6,2},{8,12},{10,14},{12,8},{14,10},{1,5},{3,7},... | collective-permute-start | bytes 196616 | tf_op jit(solution)/shard_map/ppermute | solution.py:29
  11.0 7.6 %collective-permute-start.2 = (bf16[4,2,4,2048]{3,2,1,0:T(4,128)(2,1)S(1)}, bf16[4,2,4,2048]{3,2,1,0:T(4,128)(2,1)S(1)}, u32[]{:S(2)}, u32[]{:S(2)}) collective-permute-start(bf16[4,2,4,2048]{3,2,1,0:T(4,128)(2,1)S(1)} %maximum_select_fusion.2), channel_id=1, source_target_pairs={{0,8},{2,10},{4,12},{6,14},{8,0},{10,2},{12,4},{14,6},{1,9},{3,11}... | collective-permute-start | bytes 393224 | tf_op jit(solution)/shard_map/ppermute | solution.py:29
  31.5 9.2 %collective-permute-start.3 = (f32[130,128]{1,0:T(8,128)S(1)}, f32[130,128]{1,0:T(8,128)S(1)}, u32[]{:S(2)}, u32[]{:S(2)}) collective-permute-start(f32[130,128]{1,0:T(8,128)S(1)} %get-tuple-element.17), channel_id=1, source_target_pairs={{0,2},{2,4},{4,6},{6,8},{8,10},{10,12},{12,14},{14,0},{1,3},{3,5},... | collective-permute-start | bytes 199688 | tf_op jit(solution)/shard_map/ppermute | solution.py:48
  32.9 8.2 %collective-permute-start.4 = (f32[130,128]{1,0:T(8,128)S(1)}, f32[130,128]{1,0:T(8,128)S(1)}, u32[]{:S(2)}, u32[]{:S(2)}) collective-permute-start(f32[130,128]{1,0:T(8,128)S(1)} %get-tuple-element.16), channel_id=1, source_target_pairs={{0,4},{2,6},{4,8},{6,10},{8,12},{10,14},{12,0},{14,2},{1,5},{3,7},... | collective-permute-start | bytes 199688 | tf_op jit(solution)/shard_map/ppermute | solution.py:48
  33.5 9.1 %collective-permute-start.5 = (f32[130,128]{1,0:T(8,128)S(1)}, f32[130,128]{1,0:T(8,128)S(1)}, u32[]{:S(2)}, u32[]{:S(2)}) collective-permute-start(f32[130,128]{1,0:T(8,128)S(1)} %get-tuple-element.15), channel_id=1, source_target_pairs={{0,6},{2,8},{4,10},{6,12},{8,14},{10,0},{12,2},{14,4},{1,7},{3,9},... | collective-permute-start | bytes 199688 | tf_op jit(solution)/shard_map/ppermute | solution.py:48
  37.2 7.5 %collective-permute-start.6 = (f32[130,128]{1,0:T(8,128)S(1)}, f32[130,128]{1,0:T(8,128)S(1)}, u32[]{:S(2)}, u32[]{:S(2)}) collective-permute-start(f32[130,128]{1,0:T(8,128)S(1)} %get-tuple-element.14), channel_id=1, source_target_pairs={{0,8},{2,10},{4,12},{6,14},{8,0},{10,2},{12,4},{14,6},{1,9},{3,11}... | collective-permute-start | bytes 199688 | tf_op jit(solution)/shard_map/ppermute | solution.py:48
  37.6 7.0 %collective-permute-start.7 = (f32[130,128]{1,0:T(8,128)S(1)}, f32[130,128]{1,0:T(8,128)S(1)}, u32[]{:S(2)}, u32[]{:S(2)}) collective-permute-start(f32[130,128]{1,0:T(8,128)S(1)} %get-tuple-element.13), channel_id=1, source_target_pairs={{0,10},{2,12},{4,14},{6,0},{8,2},{10,4},{12,6},{14,8},{1,11},{3,13... | collective-permute-start | bytes 199688 | tf_op jit(solution)/shard_map/ppermute | solution.py:48
  40.7 5.7 %collective-permute-start.8 = (f32[130,128]{1,0:T(8,128)S(1)}, f32[130,128]{1,0:T(8,128)S(1)}, u32[]{:S(2)}, u32[]{:S(2)}) collective-permute-start(f32[130,128]{1,0:T(8,128)S(1)} %get-tuple-element.12), channel_id=1, source_target_pairs={{0,12},{2,14},{4,0},{6,2},{8,4},{10,6},{12,8},{14,10},{1,13},{3,15... | collective-permute-start | bytes 199688 | tf_op jit(solution)/shard_map/ppermute | solution.py:48
  41.0 5.4 %collective-permute-start.9 = (f32[130,128]{1,0:T(8,128)S(1)}, f32[130,128]{1,0:T(8,128)S(1)}, u32[]{:S(2)}, u32[]{:S(2)}) collective-permute-start(f32[130,128]{1,0:T(8,128)S(1)} %get-tuple-element.11), channel_id=1, source_target_pairs={{0,14},{2,0},{4,2},{6,4},{8,6},{10,8},{12,10},{14,12},{1,15},{3,1}... | collective-permute-start | bytes 199688 | tf_op jit(solution)/shard_map/ppermute | solution.py:48
  54.2 33.5 %collective-permute-start.16 = (f32[16,1024]{1,0:T(8,128)}, f32[16,1024]{1,0:T(8,128)S(1)}, u32[]{:S(2)}, u32[]{:S(2)}) collective-permute-start(f32[16,1024]{1,0:T(8,128)} %shard_map.99), channel_id=1, source_target_pairs={{0,14},{2,0},{4,2},{6,4},{8,6},{10,8},{12,10},{14,12},{1,15},{3,1}... | collective-permute-start | bytes 196616 | tf_op jit(solution)/shard_map/ppermute | solution.py:249
  58.5 6.0 %copy-start.3 = (s32[128]{0:T(128)S(1)}, s32[128]{0:T(128)}, u32[]{:S(2)}) copy-start(s32[128]{0:T(128)} %param.16) | copy-start | bytes 1540
  62.6 27.0 %collective-permute-start.15 = (f32[16,1024]{1,0:T(8,128)}, f32[16,1024]{1,0:T(8,128)S(1)}, u32[]{:S(2)}, u32[]{:S(2)}) collective-permute-start(f32[16,1024]{1,0:T(8,128)} %shard_map.98), channel_id=1, source_target_pairs={{0,12},{2,14},{4,0},{6,2},{8,4},{10,6},{12,8},{14,10},{1,13},{3,15... | collective-permute-start | bytes 196616 | tf_op jit(solution)/shard_map/ppermute | solution.py:249
  68.6 25.5 %collective-permute-start.14 = (f32[16,1024]{1,0:T(8,128)}, f32[16,1024]{1,0:T(8,128)S(1)}, u32[]{:S(2)}, u32[]{:S(2)}) collective-permute-start(f32[16,1024]{1,0:T(8,128)} %shard_map.97), channel_id=1, source_target_pairs={{0,10},{2,12},{4,14},{6,0},{8,2},{10,4},{12,6},{14,8},{1,11},{3,13... | collective-permute-start | bytes 196616 | tf_op jit(solution)/shard_map/ppermute | solution.py:249
  72.6 21.4 %collective-permute-start.13 = (f32[16,1024]{1,0:T(8,128)}, f32[16,1024]{1,0:T(8,128)S(1)}, u32[]{:S(2)}, u32[]{:S(2)}) collective-permute-start(f32[16,1024]{1,0:T(8,128)} %shard_map.96), channel_id=1, source_target_pairs={{0,8},{2,10},{4,12},{6,14},{8,0},{10,2},{12,4},{14,6},{1,9},{3,11}... | collective-permute-start | bytes 196616 | tf_op jit(solution)/shard_map/ppermute | solution.py:249
  77.8 16.3 %collective-permute-start.12 = (f32[16,1024]{1,0:T(8,128)}, f32[16,1024]{1,0:T(8,128)S(1)}, u32[]{:S(2)}, u32[]{:S(2)}) collective-permute-start(f32[16,1024]{1,0:T(8,128)} %shard_map.95), channel_id=1, source_target_pairs={{0,6},{2,8},{4,10},{6,12},{8,14},{10,0},{12,2},{14,4},{1,7},{3,9},... | collective-permute-start | bytes 196616 | tf_op jit(solution)/shard_map/ppermute | solution.py:249
  83.6 4.1 %copy-start.2 = (f32[16,1024]{1,0:T(8,128)S(1)}, f32[16,1024]{1,0:T(8,128)}, u32[]{:S(2)}) copy-start(f32[16,1024]{1,0:T(8,128)} %shard_map.94) | copy-start | bytes 196612
  87.7 6.3 %collective-permute-start.11 = (f32[16,1024]{1,0:T(8,128)S(1)}, f32[16,1024]{1,0:T(8,128)S(1)}, u32[]{:S(2)}, u32[]{:S(2)}) collective-permute-start(f32[16,1024]{1,0:T(8,128)S(1)} %copy-done.2), channel_id=1, source_target_pairs={{0,4},{2,6},{4,8},{6,10},{8,12},{10,14},{12,0},{14,2},{1,5},{3,7},... | collective-permute-start | bytes 196616 | tf_op jit(solution)/shard_map/ppermute | solution.py:249
  89.6 7.2 %collective-permute-start.10 = (f32[16,1024]{1,0:T(8,128)}, f32[16,1024]{1,0:T(8,128)S(1)}, u32[]{:S(2)}, u32[]{:S(2)}) collective-permute-start(f32[16,1024]{1,0:T(8,128)} %shard_map.93), channel_id=1, source_target_pairs={{0,2},{2,4},{4,6},{6,8},{8,10},{10,12},{12,14},{14,0},{1,3},{3,5},... | collective-permute-start | bytes 196616 | tf_op jit(solution)/shard_map/ppermute | solution.py:249
  89.9 6.8 %dynamic-slice-start = ((f32[16384]{0:T(1024)}, s32[]{:T(128)}), f32[1024]{0:T(1024)S(1)}, s32[]{:S(2)}) async-start(f32[16384]{0:T(1024)} %copy-done.1, s32[]{:T(128)} %select_n.204), calls=%async_computation | async-start | bytes 8704 | tf_op jit(solution)/shard_map/dynamic_slice | solution.py:263
  89.9 24.0 %copy-start = (bf16[2,8,8192]{2,1,0:T(8,128)(2,1)S(1)}, bf16[2,8,8192]{2,1,0:T(8,128)(2,1)}, u32[]{:S(2)}) copy-start(bf16[2,8,8192]{2,1,0:T(8,128)(2,1)} %param.17) | copy-start | bytes 786436
  97.7 4.0 %collective-permute-start.17 = (bf16[1,16,1024]{2,1,0:T(8,128)(2,1)S(1)}, bf16[1,16,1024]{2,1,0:T(8,128)(2,1)S(1)}, u32[]{:S(2)}, u32[]{:S(2)}) collective-permute-start(bf16[1,16,1024]{2,1,0:T(8,128)(2,1)S(1)} %fusion.7), channel_id=1, source_target_pairs={{0,2},{2,0},{4,6},{6,4},{8,10},{10,8},{12,14},{14,12},{1,3},{3,1},... | collective-permute-start | bytes 98312 | tf_op jit(solution)/shard_map/ppermute | solution.py:29
  101.6 4.9 %collective-permute-start.18 = (bf16[2,16,1024]{2,1,0:T(8,128)(2,1)S(1)}, bf16[2,16,1024]{2,1,0:T(8,128)(2,1)S(1)}, u32[]{:S(2)}, u32[]{:S(2)}) collective-permute-start(bf16[2,16,1024]{2,1,0:T(8,128)(2,1)S(1)} %maximum_select_fusion.5), channel_id=1, source_target_pairs={{0,4},{2,6},{4,0},{6,2},{8,12},{10,14},{12,8},{14,10},{1,5},{3,7},... | collective-permute-start | bytes 196616 | tf_op jit(solution)/shard_map/ppermute | solution.py:29
  106.6 6.8 %collective-permute-start.19 = (bf16[4,16,1024]{2,1,0:T(8,128)(2,1)S(1)}, bf16[4,16,1024]{2,1,0:T(8,128)(2,1)S(1)}, u32[]{:S(2)}, u32[]{:S(2)}) collective-permute-start(bf16[4,16,1024]{2,1,0:T(8,128)(2,1)S(1)} %maximum_select_fusion.3), channel_id=1, source_target_pairs={{0,8},{2,10},{4,12},{6,14},{8,0},{10,2},{12,4},{14,6},{1,9},{3,11}... | collective-permute-start | bytes 393224 | tf_op jit(solution)/shard_map/ppermute | solution.py:29

commit v5 on v3

--- a/solution.py
+++ b/solution.py
@@ -23,6 +23,18 @@
     if not _is_pow2(count):
         return lax.all_gather(x, axis_name, axis=0, tiled=False)
     me = lax.axis_index(axis_name)
+    if count <= 8:
+        other = lax.ppermute(x, axis_name, [(i, i ^ 1) for i in range(count)])
+        low = me % 2 == 0
+        pair = jnp.where(low, jnp.stack([x, other]), jnp.stack([other, x]))
+        pairs = [pair]
+        for d in range(1, count // 2):
+            pairs.append(
+                lax.ppermute(pair, axis_name, [(i, (i + 2 * d) % count) for i in range(count)])
+            )
+        order = (me // 2 - jnp.arange(count // 2)) % (count // 2)
+        placed = jnp.zeros((count // 2,) + pair.shape, pair.dtype).at[order].set(jnp.stack(pairs))
+        return placed.reshape((count,) + x.shape)
     cur = x[None]
     k = 1
     while k < count:

time: 100 us -> 93.2 us (0.932)
  waiting for transfers between devices: 31.1 us -> 15.2 us
  starting transfers between devices: 31.4 us -> 38.2 us
  local copies, waits for them, and re-layouts: 7.81 us -> 9.32 us
    ppermute x6 -> x8, waiting for transfers between devices: 19.5 us -> 8.2 us  [the longest x6 6.31 us: _gather_blocks(): lax.ppermute(pair, axis_name, [(i, (i + 2 * d) % count) for i in range(co...]
    ppermute x6 -> x8, starting transfers between devices: 8.94 us -> 15 us  [the longest x6 9.8 us: _gather_blocks(): lax.ppermute(pair, axis_name, [(i, (i + 2 * d) % count) for i in range(co...]
    ppermute x14, waiting for transfers between devices: 11.6 us -> 6.96 us  [_exchange(): lax.ppermute(send, axis_name, [(i, (i + k) % count) for i in range(count)])]
    scatter x0 -> x2, local copies, waits for them, and re-layouts: none -> 1.38 us  [_gather_blocks(): jnp.zeros((count // 2,) + pair.shape, pair.dtype).at[order]]
  transfers between devices with their start and end apart: 20 -> 22, of which waited for: 11 -> 14; matrix products, arithmetic and copies ran while one was open for 4% -> 6% of each run, Pallas kernels for 0% -> 0%
where the time goes in v5:
time: 93.2 us; the launch traced here: 92.6 us
  starting transfers between devices  38.2 us (41%)
  waiting for transfers between devices  15.2 us (16%)
  matrix products  13.3 us (14%)
  local copies, waits for them, and re-layouts  9.32 us (10%)
  Pallas kernels  8.58 us (9%)
  other arithmetic  5.57 us (6%)
  blocking collectives  1.85 us (2%)
    ppermute x14, starting transfers between devices, _exchange(): lax.ppermute(send, axis_name, [(i, (i + k) % count) for i in range(count)])  23.3 us
    dot_general x1, matrix products, per_device(): jnp.einsum('rhd,hdf->rhf', head_rows_in, head_weights, preferred_element_...  12.9 us
    ppermute x6, starting transfers between devices, _gather_blocks(): lax.ppermute(pair, axis_name, [(i, (i + 2 * d) % count) for i in range(co...  9.8 us
    pallas_call x1, Pallas kernels, _attend_local(): pl.pallas_call(_attend_kernel, grid=(kv_heads,), in_specs=[pl.BlockSpec((...  8.58 us
    ppermute x14, waiting for transfers between devices, _exchange(): lax.ppermute(send, axis_name, [(i, (i + k) % count) for i in range(count)])  6.96 us
    ppermute x6, waiting for transfers between devices, _gather_blocks(): lax.ppermute(pair, axis_name, [(i, (i + 2 * d) % count) for i in range(co...  6.31 us
    ppermute x2, starting transfers between devices, _gather_blocks(): other = lax.ppermute(x, axis_name, [(i, i ^ 1) for i in range(count)])  5.16 us
    ppermute x2, waiting for transfers between devices, _gather_blocks(): other = lax.ppermute(x, axis_name, [(i, i ^ 1) for i in range(count)])  1.89 us
  transfers between devices with their start and end apart: 22, of which 14 were waited for; matrix products, arithmetic and copies ran while one was open for 6% of the time, Pallas kernels for 0%

profile of v5, /device:TPU:0, one launch (start us, length us, event | category | flops | bytes accessed | tf_op | source)
XLA Modules:
  0.0 92.6 jit_solution(2911276849467594923)
XLA Ops:
  0.0 2.9 %collective-permute-start = (bf16[2,4,2048]{2,1,0:T(4,128)(2,1)}, bf16[2,4,2048]{2,1,0:T(4,128)(2,1)S(1)}, u32[]{:S(2)}, u32[]{:S(2)}) collective-permute-start(bf16[2,4,2048]{2,1,0:T(4,128)(2,1)} %param.9), channel_id=1, source_target_pairs={{0,2},{2,0},{4,6},{6,4},{8,10},{10,8},{12,14},{14,12},{1,3},{3,1},... | collective-permute-start | bytes 98312 | tf_op jit(solution)/shard_map/ppermute | solution.py:27
  2.9 0.8 reshape.344
  3.8 0.8 reshape.343
  4.6 0.7 multiply_exponential_fusion.1
  5.4 1.3 %compare_convert_fusion.valid_ref = f32[4,128]{1,0:T(4,128)} fusion(s32[128]{0:T(128)S(1)} %iota_add_fusion, s32[4]{0:T(128)} %param.12), kind=kLoop, calls=%fused_computation.89 | loop fusion | flops 1024 | bytes 2576 | tf_op jit(solution)/shard_map/convert_element_type | solution.py:150
  7.2 0.9 maximum_select_fusion.1
  8.1 1.6 %collective-permute-start.1 = (bf16[2,2,4,2048]{3,2,1,0:T(4,128)(2,1)S(1)}, bf16[2,2,4,2048]{3,2,1,0:T(4,128)(2,1)S(1)}, u32[]{:S(2)}, u32[]{:S(2)}) collective-permute-start(bf16[2,2,4,2048]{3,2,1,0:T(4,128)(2,1)S(1)} %maximum_select_fusion.1), channel_id=1, source_target_pairs={{0,4},{2,6},{4,8},{6,10},{8,12},{10,14},{12,0},{14,2},{1,5},{3,7},... | collective-permute-start | bytes 196616 | tf_op jit(solution)/shard_map/ppermute | solution.py:33
  9.8 2.6 %collective-permute-start.2 = (bf16[2,2,4,2048]{3,2,1,0:T(4,128)(2,1)S(1)}, bf16[2,2,4,2048]{3,2,1,0:T(4,128)(2,1)S(1)}, u32[]{:S(2)}, u32[]{:S(2)}) collective-permute-start(bf16[2,2,4,2048]{3,2,1,0:T(4,128)(2,1)S(1)} %maximum_select_fusion.1), channel_id=1, source_target_pairs={{0,8},{2,10},{4,12},{6,14},{8,0},{10,2},{12,4},{14,6},{1,9},{3,11}... | collective-permute-start | bytes 196616 | tf_op jit(solution)/shard_map/ppermute | solution.py:33
  12.3 1.3 %collective-permute-start.3 = (bf16[2,2,4,2048]{3,2,1,0:T(4,128)(2,1)S(1)}, bf16[2,2,4,2048]{3,2,1,0:T(4,128)(2,1)S(1)}, u32[]{:S(2)}, u32[]{:S(2)}) collective-permute-start(bf16[2,2,4,2048]{3,2,1,0:T(4,128)(2,1)S(1)} %maximum_select_fusion.1), channel_id=1, source_target_pairs={{0,12},{2,14},{4,0},{6,2},{8,4},{10,6},{12,8},{14,10},{1,13},{3,15... | collective-permute-start | bytes 196616 | tf_op jit(solution)/shard_map/ppermute | solution.py:33
  13.7 0.9 maximum_select_fusion
  14.6 0.4 collective-permute-done.1
  15.0 2.1 %collective-permute-done.2 = bf16[2,2,4,2048]{3,2,1,0:T(4,128)(2,1)S(1)} collective-permute-done((bf16[2,2,4,2048]{3,2,1,0:T(4,128)(2,1)S(1)}, bf16[2,2,4,2048]{3,2,1,0:T(4,128)(2,1)S(1)}, u32[]{:S(2)}, u32[]{:S(2)}) %collective-permute-start.2) | collective-permute-done | bytes 65568 | tf_op jit(solution)/shard_map/ppermute | solution.py:33
  17.4 0.7 scatter_fusion
  18.4 0.7 copy.102
  19.1 8.6 %shard_map.91 = (f32[8,128,128]{2,1,0:T(8,128)}, f32[8,128,128]{2,1,0:T(8,128)}, f32[8,128,128]{2,1,0:T(8,128)}) custom-call(bf16[8,128,128]{2,1,0:T(8,128)(2,1)} %bitcast.165, bf16[2,1024,1024]{2,1,0:T(8,128)(2,1)} %v_ref.1, bf16[2,1024,1024]{2,1,0:T(8,128)(2,1)} %v_ref.1, bf16[2,4,128,1024]{3,2,1,0:T(8,128)(2,1)} %tv_ref.1, ...), custom_call_target="tpu_custom_call" | custom-call | flops 603979776 | bytes 8126464 | tf_op jit(solution)/shard_map/pallas_call | solution.py:106
  27.7 1.1 %copy.80 = f32[8,4,2,16,128]{4,3,1,2,0:T(8,128)S(1)} copy(f32[8,4,2,16,128]{4,3,2,1,0:T(8,128)} %bitcast.166) | data formatting | bytes 1048576 | tf_op jit(solution)/shard_map/reshape | solution.py:159
  28.8 1.5 %slice_reduce_fusion = (f32[8,128]{1,0:T(8,128)S(1)}, f32[8,128]{1,0:T(8,128)S(1)}) fusion(f32[8,128,128]{2,1,0:T(8,128)} %get-tuple-element.10, f32[8,128,128]{2,1,0:T(8,128)} %get-tuple-element.9), kind=kLoop, calls=%fused_computation.10 | loop fusion | bytes 16384 | tf_op jit(solution)/shard_map/slice | solution.py:161
  31.3 1.4 %collective-permute-start.5 = (f32[130,128]{1,0:T(8,128)S(1)}, f32[130,128]{1,0:T(8,128)S(1)}, u32[]{:S(2)}, u32[]{:S(2)}) collective-permute-start(f32[130,128]{1,0:T(8,128)S(1)} %get-tuple-element.16), channel_id=1, source_target_pairs={{0,4},{2,6},{4,8},{6,10},{8,12},{10,14},{12,0},{14,2},{1,5},{3,7},... | collective-permute-start | bytes 199688 | tf_op jit(solution)/shard_map/ppermute | solution.py:60
  32.8 2.9 %collective-permute-start.6 = (f32[130,128]{1,0:T(8,128)S(1)}, f32[130,128]{1,0:T(8,128)S(1)}, u32[]{:S(2)}, u32[]{:S(2)}) collective-permute-start(f32[130,128]{1,0:T(8,128)S(1)} %get-tuple-element.15), channel_id=1, source_target_pairs={{0,6},{2,8},{4,10},{6,12},{8,14},{10,0},{12,2},{14,4},{1,7},{3,9},... | collective-permute-start | bytes 199688 | tf_op jit(solution)/shard_map/ppermute | solution.py:60
  35.7 1.8 %collective-permute-start.7 = (f32[130,128]{1,0:T(8,128)S(1)}, f32[130,128]{1,0:T(8,128)S(1)}, u32[]{:S(2)}, u32[]{:S(2)}) collective-permute-start(f32[130,128]{1,0:T(8,128)S(1)} %get-tuple-element.14), channel_id=1, source_target_pairs={{0,8},{2,10},{4,12},{6,14},{8,0},{10,2},{12,4},{14,6},{1,9},{3,11}... | collective-permute-start | bytes 199688 | tf_op jit(solution)/shard_map/ppermute | solution.py:60
  37.5 1.1 %collective-permute-start.8 = (f32[130,128]{1,0:T(8,128)S(1)}, f32[130,128]{1,0:T(8,128)S(1)}, u32[]{:S(2)}, u32[]{:S(2)}) collective-permute-start(f32[130,128]{1,0:T(8,128)S(1)} %get-tuple-element.13), channel_id=1, source_target_pairs={{0,10},{2,12},{4,14},{6,0},{8,2},{10,4},{12,6},{14,8},{1,11},{3,13... | collective-permute-start | bytes 199688 | tf_op jit(solution)/shard_map/ppermute | solution.py:60
  38.7 1.2 %collective-permute-start.9 = (f32[130,128]{1,0:T(8,128)S(1)}, f32[130,128]{1,0:T(8,128)S(1)}, u32[]{:S(2)}, u32[]{:S(2)}) collective-permute-start(f32[130,128]{1,0:T(8,128)S(1)} %get-tuple-element.12), channel_id=1, source_target_pairs={{0,12},{2,14},{4,0},{6,2},{8,4},{10,6},{12,8},{14,10},{1,13},{3,15... | collective-permute-start | bytes 199688 | tf_op jit(solution)/shard_map/ppermute | solution.py:60
  39.9 1.6 %collective-permute-start.10 = (f32[130,128]{1,0:T(8,128)S(1)}, f32[130,128]{1,0:T(8,128)S(1)}, u32[]{:S(2)}, u32[]{:S(2)}) collective-permute-start(f32[130,128]{1,0:T(8,128)S(1)} %get-tuple-element.11), channel_id=1, source_target_pairs={{0,14},{2,0},{4,2},{6,4},{8,6},{10,8},{12,10},{14,12},{1,15},{3,1}... | collective-permute-start | bytes 199688 | tf_op jit(solution)/shard_map/ppermute | solution.py:60
  41.5 1.6 %collective-permute-done.6 = f32[130,128]{1,0:T(8,128)S(1)} collective-permute-done((f32[130,128]{1,0:T(8,128)S(1)}, f32[130,128]{1,0:T(8,128)S(1)}, u32[]{:S(2)}, u32[]{:S(2)}) %collective-permute-start.6) | collective-permute-done | bytes 66592 | tf_op jit(solution)/shard_map/ppermute | solution.py:60
  43.2 1.4 %collective-permute-done.8 = f32[130,128]{1,0:T(8,128)S(1)} collective-permute-done((f32[130,128]{1,0:T(8,128)S(1)}, f32[130,128]{1,0:T(8,128)S(1)}, u32[]{:S(2)}, u32[]{:S(2)}) %collective-permute-start.8) | collective-permute-done | bytes 66592 | tf_op jit(solution)/shard_map/ppermute | solution.py:60
  46.0 1.9 %all_gather.3 = bf16[2,8,2048]{2,0,1:T(2,128)(2,1)S(1)} all-gather(bf16[2,4,2048]{2,0,1:T(2,128)(2,1)S(1)} %copy.98), channel_id=1, replica_groups=mesh['rep'=2,'tp'=8,'sub'=2] {'sub'}, dimensions={1}, use_global_device_ids=true | all-gather | bytes 98304 | tf_op jit(solution)/shard_map/all_gather | solution.py:198
  47.9 12.9 %fusion.1 = f32[16,8192]{1,0:T(8,128)S(1)} fusion(f32[8192]{0:T(1024)S(1)} %dynamic_slice.61, bf16[16,128,8192]{2,1,0:T(8,128)(2,1)} %bitcast.196, bf16[16,16,128]{2,1,0:T(8,128)(2,1)S(1)} %bitcast.187), kind=kOutput, calls=%fused_computation.4 | convolution fusion | flops 543031296 | bytes 34177024 | tf_op jit(solution)/shard_map/rhd,hdf->rhf/dot_general | solution.py:207
  61.1 0.5 constant_dynamic-slice_fusion.8
  61.7 2.2 %collective-permute-start.11 = (f32[16,1024]{1,0:T(8,128)S(1)}, f32[16,1024]{1,0:T(8,128)S(1)}, u32[]{:S(2)}, u32[]{:S(2)}) collective-permute-start(f32[16,1024]{1,0:T(8,128)S(1)} %bitcast.186), channel_id=1, source_target_pairs={{0,2},{2,4},{4,6},{6,8},{8,10},{10,12},{12,14},{14,0},{1,3},{3,5},... | collective-permute-start | bytes 196616 | tf_op jit(solution)/shard_map/ppermute | solution.py:60
  64.0 2.7 %collective-permute-start.12 = (f32[16,1024]{1,0:T(8,128)S(1)}, f32[16,1024]{1,0:T(8,128)S(1)}, u32[]{:S(2)}, u32[]{:S(2)}) collective-permute-start(f32[16,1024]{1,0:T(8,128)S(1)} %bitcast.185), channel_id=1, source_target_pairs={{0,4},{2,6},{4,8},{6,10},{8,12},{10,14},{12,0},{14,2},{1,5},{3,7},... | collective-permute-start | bytes 196616 | tf_op jit(solution)/shard_map/ppermute | solution.py:60
  66.7 0.8 collective-permute-start.13
  67.5 1.8 %collective-permute-start.14 = (f32[16,1024]{1,0:T(8,128)S(1)}, f32[16,1024]{1,0:T(8,128)S(1)}, u32[]{:S(2)}, u32[]{:S(2)}) collective-permute-start(f32[16,1024]{1,0:T(8,128)S(1)} %bitcast.181), channel_id=1, source_target_pairs={{0,8},{2,10},{4,12},{6,14},{8,0},{10,2},{12,4},{14,6},{1,9},{3,11}... | collective-permute-start | bytes 196616 | tf_op jit(solution)/shard_map/ppermute | solution.py:60
  69.3 2.9 %collective-permute-start.15 = (f32[16,1024]{1,0:T(8,128)S(1)}, f32[16,1024]{1,0:T(8,128)S(1)}, u32[]{:S(2)}, u32[]{:S(2)}) collective-permute-start(f32[16,1024]{1,0:T(8,128)S(1)} %bitcast.182), channel_id=1, source_target_pairs={{0,10},{2,12},{4,14},{6,0},{8,2},{10,4},{12,6},{14,8},{1,11},{3,13... | collective-permute-start | bytes 196616 | tf_op jit(solution)/shard_map/ppermute | solution.py:60
  72.2 1.3 %collective-permute-start.16 = (f32[16,1024]{1,0:T(8,128)S(1)}, f32[16,1024]{1,0:T(8,128)S(1)}, u32[]{:S(2)}, u32[]{:S(2)}) collective-permute-start(f32[16,1024]{1,0:T(8,128)S(1)} %bitcast.184), channel_id=1, source_target_pairs={{0,12},{2,14},{4,0},{6,2},{8,4},{10,6},{12,8},{14,10},{1,13},{3,15... | collective-permute-start | bytes 196616 | tf_op jit(solution)/shard_map/ppermute | solution.py:60
  73.5 1.2 %collective-permute-start.17 = (f32[16,1024]{1,0:T(8,128)S(1)}, f32[16,1024]{1,0:T(8,128)S(1)}, u32[]{:S(2)}, u32[]{:S(2)}) collective-permute-start(f32[16,1024]{1,0:T(8,128)S(1)} %bitcast.183), channel_id=1, source_target_pairs={{0,14},{2,0},{4,2},{6,4},{8,6},{10,8},{12,10},{14,12},{1,15},{3,1}... | collective-permute-start | bytes 196616 | tf_op jit(solution)/shard_map/ppermute | solution.py:60
  74.8 0.5 collective-permute-done.13
  75.2 0.9 collective-permute-done.14
  76.1 1.0 %collective-permute-done.15 = f32[16,1024]{1,0:T(8,128)S(1)} collective-permute-done((f32[16,1024]{1,0:T(8,128)S(1)}, f32[16,1024]{1,0:T(8,128)S(1)}, u32[]{:S(2)}, u32[]{:S(2)}) %collective-permute-start.15) | collective-permute-done | bytes 65568 | tf_op jit(solution)/shard_map/ppermute | solution.py:60
  77.1 1.2 %collective-permute-done.16 = f32[16,1024]{1,0:T(8,128)S(1)} collective-permute-done((f32[16,1024]{1,0:T(8,128)S(1)}, f32[16,1024]{1,0:T(8,128)S(1)}, u32[]{:S(2)}, u32[]{:S(2)}) %collective-permute-start.16) | collective-permute-done | bytes 65568 | tf_op jit(solution)/shard_map/ppermute | solution.py:60
  78.4 2.2 %collective-permute-start.18 = (bf16[16,1024]{1,0:T(8,128)(2,1)S(1)}, bf16[16,1024]{1,0:T(8,128)(2,1)S(1)}, u32[]{:S(2)}, u32[]{:S(2)}) collective-permute-start(bf16[16,1024]{1,0:T(8,128)(2,1)S(1)} %clamp_convert_fusion), channel_id=1, source_target_pairs={{0,2},{2,0},{4,6},{6,4},{8,10},{10,8},{12,14},{14,12},{1,3},{3,1},... | collective-permute-start | bytes 98312 | tf_op jit(solution)/shard_map/ppermute | solution.py:27
  80.6 1.9 %collective-permute-done.18 = bf16[16,1024]{1,0:T(8,128)(2,1)S(1)} collective-permute-done((bf16[16,1024]{1,0:T(8,128)(2,1)S(1)}, bf16[16,1024]{1,0:T(8,128)(2,1)S(1)}, u32[]{:S(2)}, u32[]{:S(2)}) %collective-permute-start.18) | collective-permute-done | bytes 32800 | tf_op jit(solution)/shard_map/ppermute | solution.py:27
  82.5 1.8 %collective-permute-start.19 = (bf16[2,16,1024]{2,1,0:T(8,128)(2,1)S(1)}, bf16[2,16,1024]{2,1,0:T(8,128)(2,1)S(1)}, u32[]{:S(2)}, u32[]{:S(2)}) collective-permute-start(bf16[2,16,1024]{2,1,0:T(8,128)(2,1)S(1)} %maximum_select_fusion.3), channel_id=1, source_target_pairs={{0,4},{2,6},{4,8},{6,10},{8,12},{10,14},{12,0},{14,2},{1,5},{3,7},... | collective-permute-start | bytes 196616 | tf_op jit(solution)/shard_map/ppermute | solution.py:33
  84.3 1.3 %collective-permute-start.20 = (bf16[2,16,1024]{2,1,0:T(8,128)(2,1)S(1)}, bf16[2,16,1024]{2,1,0:T(8,128)(2,1)S(1)}, u32[]{:S(2)}, u32[]{:S(2)}) collective-permute-start(bf16[2,16,1024]{2,1,0:T(8,128)(2,1)S(1)} %maximum_select_fusion.3), channel_id=1, source_target_pairs={{0,8},{2,10},{4,12},{6,14},{8,0},{10,2},{12,4},{14,6},{1,9},{3,11}... | collective-permute-start | bytes 196616 | tf_op jit(solution)/shard_map/ppermute | solution.py:33
  85.6 1.1 %collective-permute-start.21 = (bf16[2,16,1024]{2,1,0:T(8,128)(2,1)S(1)}, bf16[2,16,1024]{2,1,0:T(8,128)(2,1)S(1)}, u32[]{:S(2)}, u32[]{:S(2)}) collective-permute-start(bf16[2,16,1024]{2,1,0:T(8,128)(2,1)S(1)} %maximum_select_fusion.3), channel_id=1, source_target_pairs={{0,12},{2,14},{4,0},{6,2},{8,4},{10,6},{12,8},{14,10},{1,13},{3,15... | collective-permute-start | bytes 196616 | tf_op jit(solution)/shard_map/ppermute | solution.py:33
  86.8 2.5 %collective-permute-done.19 = bf16[2,16,1024]{2,1,0:T(8,128)(2,1)S(1)} collective-permute-done((bf16[2,16,1024]{2,1,0:T(8,128)(2,1)S(1)}, bf16[2,16,1024]{2,1,0:T(8,128)(2,1)S(1)}, u32[]{:S(2)}, u32[]{:S(2)}) %collective-permute-start.19) | collective-permute-done | bytes 65568 | tf_op jit(solution)/shard_map/ppermute | solution.py:33
  89.2 1.3 %collective-permute-done.20 = bf16[2,16,1024]{2,1,0:T(8,128)(2,1)S(1)} collective-permute-done((bf16[2,16,1024]{2,1,0:T(8,128)(2,1)S(1)}, bf16[2,16,1024]{2,1,0:T(8,128)(2,1)S(1)}, u32[]{:S(2)}, u32[]{:S(2)}) %collective-permute-start.20) | collective-permute-done | bytes 65568 | tf_op jit(solution)/shard_map/ppermute | solution.py:33
  90.6 0.7 scatter_fusion.1
  91.8 0.8 add_convert_fusion
  (86 shorter events, 4.6 us)
Async XLA Ops:
  0.0 7.2 %collective-permute-start = (bf16[2,4,2048]{2,1,0:T(4,128)(2,1)}, bf16[2,4,2048]{2,1,0:T(4,128)(2,1)S(1)}, u32[]{:S(2)}, u32[]{:S(2)}) collective-permute-start(bf16[2,4,2048]{2,1,0:T(4,128)(2,1)} %param.9), channel_id=1, source_target_pairs={{0,2},{2,0},{4,6},{6,4},{8,10},{10,8},{12,14},{14,12},{1,3},{3,1},... | collective-permute-start | bytes 98312 | tf_op jit(solution)/shard_map/ppermute | solution.py:27
  8.1 6.9 %collective-permute-start.1 = (bf16[2,2,4,2048]{3,2,1,0:T(4,128)(2,1)S(1)}, bf16[2,2,4,2048]{3,2,1,0:T(4,128)(2,1)S(1)}, u32[]{:S(2)}, u32[]{:S(2)}) collective-permute-start(bf16[2,2,4,2048]{3,2,1,0:T(4,128)(2,1)S(1)} %maximum_select_fusion.1), channel_id=1, source_target_pairs={{0,4},{2,6},{4,8},{6,10},{8,12},{10,14},{12,0},{14,2},{1,5},{3,7},... | collective-permute-start | bytes 196616 | tf_op jit(solution)/shard_map/ppermute | solution.py:33
  9.8 7.3 %collective-permute-start.2 = (bf16[2,2,4,2048]{3,2,1,0:T(4,128)(2,1)S(1)}, bf16[2,2,4,2048]{3,2,1,0:T(4,128)(2,1)S(1)}, u32[]{:S(2)}, u32[]{:S(2)}) collective-permute-start(bf16[2,2,4,2048]{3,2,1,0:T(4,128)(2,1)S(1)} %maximum_select_fusion.1), channel_id=1, source_target_pairs={{0,8},{2,10},{4,12},{6,14},{8,0},{10,2},{12,4},{14,6},{1,9},{3,11}... | collective-permute-start | bytes 196616 | tf_op jit(solution)/shard_map/ppermute | solution.py:33
  12.3 4.8 %collective-permute-start.3 = (bf16[2,2,4,2048]{3,2,1,0:T(4,128)(2,1)S(1)}, bf16[2,2,4,2048]{3,2,1,0:T(4,128)(2,1)S(1)}, u32[]{:S(2)}, u32[]{:S(2)}) collective-permute-start(bf16[2,2,4,2048]{3,2,1,0:T(4,128)(2,1)S(1)} %maximum_select_fusion.1), channel_id=1, source_target_pairs={{0,12},{2,14},{4,0},{6,2},{8,4},{10,6},{12,8},{14,10},{1,13},{3,15... | collective-permute-start | bytes 196616 | tf_op jit(solution)/shard_map/ppermute | solution.py:33
  30.8 7.9 %collective-permute-start.4 = (f32[130,128]{1,0:T(8,128)S(1)}, f32[130,128]{1,0:T(8,128)S(1)}, u32[]{:S(2)}, u32[]{:S(2)}) collective-permute-start(f32[130,128]{1,0:T(8,128)S(1)} %get-tuple-element.17), channel_id=1, source_target_pairs={{0,2},{2,4},{4,6},{6,8},{8,10},{10,12},{12,14},{14,0},{1,3},{3,5},... | collective-permute-start | bytes 199688 | tf_op jit(solution)/shard_map/ppermute | solution.py:60
  31.3 8.6 %collective-permute-start.5 = (f32[130,128]{1,0:T(8,128)S(1)}, f32[130,128]{1,0:T(8,128)S(1)}, u32[]{:S(2)}, u32[]{:S(2)}) collective-permute-start(f32[130,128]{1,0:T(8,128)S(1)} %get-tuple-element.16), channel_id=1, source_target_pairs={{0,4},{2,6},{4,8},{6,10},{8,12},{10,14},{12,0},{14,2},{1,5},{3,7},... | collective-permute-start | bytes 199688 | tf_op jit(solution)/shard_map/ppermute | solution.py:60
  32.8 10.4 %collective-permute-start.6 = (f32[130,128]{1,0:T(8,128)S(1)}, f32[130,128]{1,0:T(8,128)S(1)}, u32[]{:S(2)}, u32[]{:S(2)}) collective-permute-start(f32[130,128]{1,0:T(8,128)S(1)} %get-tuple-element.15), channel_id=1, source_target_pairs={{0,6},{2,8},{4,10},{6,12},{8,14},{10,0},{12,2},{14,4},{1,7},{3,9},... | collective-permute-start | bytes 199688 | tf_op jit(solution)/shard_map/ppermute | solution.py:60
  35.7 7.5 %collective-permute-start.7 = (f32[130,128]{1,0:T(8,128)S(1)}, f32[130,128]{1,0:T(8,128)S(1)}, u32[]{:S(2)}, u32[]{:S(2)}) collective-permute-start(f32[130,128]{1,0:T(8,128)S(1)} %get-tuple-element.14), channel_id=1, source_target_pairs={{0,8},{2,10},{4,12},{6,14},{8,0},{10,2},{12,4},{14,6},{1,9},{3,11}... | collective-permute-start | bytes 199688 | tf_op jit(solution)/shard_map/ppermute | solution.py:60
  37.5 7.1 %collective-permute-start.8 = (f32[130,128]{1,0:T(8,128)S(1)}, f32[130,128]{1,0:T(8,128)S(1)}, u32[]{:S(2)}, u32[]{:S(2)}) collective-permute-start(f32[130,128]{1,0:T(8,128)S(1)} %get-tuple-element.13), channel_id=1, source_target_pairs={{0,10},{2,12},{4,14},{6,0},{8,2},{10,4},{12,6},{14,8},{1,11},{3,13... | collective-permute-start | bytes 199688 | tf_op jit(solution)/shard_map/ppermute | solution.py:60
  38.7 6.0 %collective-permute-start.9 = (f32[130,128]{1,0:T(8,128)S(1)}, f32[130,128]{1,0:T(8,128)S(1)}, u32[]{:S(2)}, u32[]{:S(2)}) collective-permute-start(f32[130,128]{1,0:T(8,128)S(1)} %get-tuple-element.12), channel_id=1, source_target_pairs={{0,12},{2,14},{4,0},{6,2},{8,4},{10,6},{12,8},{14,10},{1,13},{3,15... | collective-permute-start | bytes 199688 | tf_op jit(solution)/shard_map/ppermute | solution.py:60
  39.9 4.9 %collective-permute-start.10 = (f32[130,128]{1,0:T(8,128)S(1)}, f32[130,128]{1,0:T(8,128)S(1)}, u32[]{:S(2)}, u32[]{:S(2)}) collective-permute-start(f32[130,128]{1,0:T(8,128)S(1)} %get-tuple-element.11), channel_id=1, source_target_pairs={{0,14},{2,0},{4,2},{6,4},{8,6},{10,8},{12,10},{14,12},{1,15},{3,1}... | collective-permute-start | bytes 199688 | tf_op jit(solution)/shard_map/ppermute | solution.py:60
  47.9 18.8 %copy-start.1 = (s32[128]{0:T(128)S(1)}, s32[128]{0:T(128)}, u32[]{:S(2)}) copy-start(s32[128]{0:T(128)} %param.16) | copy-start | bytes 1540
  60.8 31.0 %copy-start = (bf16[2,8,8192]{2,1,0:T(8,128)(2,1)S(1)}, bf16[2,8,8192]{2,1,0:T(8,128)(2,1)}, u32[]{:S(2)}) copy-start(bf16[2,8,8192]{2,1,0:T(8,128)(2,1)} %param.17) | copy-start | bytes 786436
  61.7 10.5 %collective-permute-start.11 = (f32[16,1024]{1,0:T(8,128)S(1)}, f32[16,1024]{1,0:T(8,128)S(1)}, u32[]{:S(2)}, u32[]{:S(2)}) collective-permute-start(f32[16,1024]{1,0:T(8,128)S(1)} %bitcast.186), channel_id=1, source_target_pairs={{0,2},{2,4},{4,6},{6,8},{8,10},{10,12},{12,14},{14,0},{1,3},{3,5},... | collective-permute-start | bytes 196616 | tf_op jit(solution)/shard_map/ppermute | solution.py:60
  64.0 9.5 %collective-permute-start.12 = (f32[16,1024]{1,0:T(8,128)S(1)}, f32[16,1024]{1,0:T(8,128)S(1)}, u32[]{:S(2)}, u32[]{:S(2)}) collective-permute-start(f32[16,1024]{1,0:T(8,128)S(1)} %bitcast.185), channel_id=1, source_target_pairs={{0,4},{2,6},{4,8},{6,10},{8,12},{10,14},{12,0},{14,2},{1,5},{3,7},... | collective-permute-start | bytes 196616 | tf_op jit(solution)/shard_map/ppermute | solution.py:60
  66.7 8.6 %collective-permute-start.13 = (f32[16,1024]{1,0:T(8,128)S(1)}, f32[16,1024]{1,0:T(8,128)S(1)}, u32[]{:S(2)}, u32[]{:S(2)}) collective-permute-start(f32[16,1024]{1,0:T(8,128)S(1)} %bitcast.180), channel_id=1, source_target_pairs={{0,6},{2,8},{4,10},{6,12},{8,14},{10,0},{12,2},{14,4},{1,7},{3,9},... | collective-permute-start | bytes 196616 | tf_op jit(solution)/shard_map/ppermute | solution.py:60
  67.5 8.6 %collective-permute-start.14 = (f32[16,1024]{1,0:T(8,128)S(1)}, f32[16,1024]{1,0:T(8,128)S(1)}, u32[]{:S(2)}, u32[]{:S(2)}) collective-permute-start(f32[16,1024]{1,0:T(8,128)S(1)} %bitcast.181), channel_id=1, source_target_pairs={{0,8},{2,10},{4,12},{6,14},{8,0},{10,2},{12,4},{14,6},{1,9},{3,11}... | collective-permute-start | bytes 196616 | tf_op jit(solution)/shard_map/ppermute | solution.py:60
  69.3 7.8 %collective-permute-start.15 = (f32[16,1024]{1,0:T(8,128)S(1)}, f32[16,1024]{1,0:T(8,128)S(1)}, u32[]{:S(2)}, u32[]{:S(2)}) collective-permute-start(f32[16,1024]{1,0:T(8,128)S(1)} %bitcast.182), channel_id=1, source_target_pairs={{0,10},{2,12},{4,14},{6,0},{8,2},{10,4},{12,6},{14,8},{1,11},{3,13... | collective-permute-start | bytes 196616 | tf_op jit(solution)/shard_map/ppermute | solution.py:60
  72.2 6.1 %collective-permute-start.16 = (f32[16,1024]{1,0:T(8,128)S(1)}, f32[16,1024]{1,0:T(8,128)S(1)}, u32[]{:S(2)}, u32[]{:S(2)}) collective-permute-start(f32[16,1024]{1,0:T(8,128)S(1)} %bitcast.184), channel_id=1, source_target_pairs={{0,12},{2,14},{4,0},{6,2},{8,4},{10,6},{12,8},{14,10},{1,13},{3,15... | collective-permute-start | bytes 196616 | tf_op jit(solution)/shard_map/ppermute | solution.py:60
  73.5 4.9 %collective-permute-start.17 = (f32[16,1024]{1,0:T(8,128)S(1)}, f32[16,1024]{1,0:T(8,128)S(1)}, u32[]{:S(2)}, u32[]{:S(2)}) collective-permute-start(f32[16,1024]{1,0:T(8,128)S(1)} %bitcast.183), channel_id=1, source_target_pairs={{0,14},{2,0},{4,2},{6,4},{8,6},{10,8},{12,10},{14,12},{1,15},{3,1}... | collective-permute-start | bytes 196616 | tf_op jit(solution)/shard_map/ppermute | solution.py:60
  78.4 4.1 %collective-permute-start.18 = (bf16[16,1024]{1,0:T(8,128)(2,1)S(1)}, bf16[16,1024]{1,0:T(8,128)(2,1)S(1)}, u32[]{:S(2)}, u32[]{:S(2)}) collective-permute-start(bf16[16,1024]{1,0:T(8,128)(2,1)S(1)} %clamp_convert_fusion), channel_id=1, source_target_pairs={{0,2},{2,0},{4,6},{6,4},{8,10},{10,8},{12,14},{14,12},{1,3},{3,1},... | collective-permute-start | bytes 98312 | tf_op jit(solution)/shard_map/ppermute | solution.py:27
  82.5 6.7 %collective-permute-start.19 = (bf16[2,16,1024]{2,1,0:T(8,128)(2,1)S(1)}, bf16[2,16,1024]{2,1,0:T(8,128)(2,1)S(1)}, u32[]{:S(2)}, u32[]{:S(2)}) collective-permute-start(bf16[2,16,1024]{2,1,0:T(8,128)(2,1)S(1)} %maximum_select_fusion.3), channel_id=1, source_target_pairs={{0,4},{2,6},{4,8},{6,10},{8,12},{10,14},{12,0},{14,2},{1,5},{3,7},... | collective-permute-start | bytes 196616 | tf_op jit(solution)/shard_map/ppermute | solution.py:33
  84.3 6.3 %collective-permute-start.20 = (bf16[2,16,1024]{2,1,0:T(8,128)(2,1)S(1)}, bf16[2,16,1024]{2,1,0:T(8,128)(2,1)S(1)}, u32[]{:S(2)}, u32[]{:S(2)}) collective-permute-start(bf16[2,16,1024]{2,1,0:T(8,128)(2,1)S(1)} %maximum_select_fusion.3), channel_id=1, source_target_pairs={{0,8},{2,10},{4,12},{6,14},{8,0},{10,2},{12,4},{14,6},{1,9},{3,11}... | collective-permute-start | bytes 196616 | tf_op jit(solution)/shard_map/ppermute | solution.py:33
  85.6 5.0 %collective-permute-start.21 = (bf16[2,16,1024]{2,1,0:T(8,128)(2,1)S(1)}, bf16[2,16,1024]{2,1,0:T(8,128)(2,1)S(1)}, u32[]{:S(2)}, u32[]{:S(2)}) collective-permute-start(bf16[2,16,1024]{2,1,0:T(8,128)(2,1)S(1)} %maximum_select_fusion.3), channel_id=1, source_target_pairs={{0,12},{2,14},{4,0},{6,2},{8,4},{10,6},{12,8},{14,10},{1,13},{3,15... | collective-permute-start | bytes 196616 | tf_op jit(solution)/shard_map/ppermute | solution.py:33

commit v6 on v5

--- a/solution.py
+++ b/solution.py
@@ -45,6 +45,26 @@
     return cur
 
 
+def _two_stage(blocks, axis_name, count, reduce):
+    me = lax.axis_index(axis_name)
+    half = count // 2
+    by_parity = blocks.reshape((half, 2) + blocks.shape[1:])
+    mine = lax.dynamic_index_in_dim(by_parity, me % 2, 1, keepdims=False)
+    theirs = lax.dynamic_index_in_dim(by_parity, 1 - me % 2, 1, keepdims=False)
+    got = lax.ppermute(theirs, axis_name, [(i, i ^ 1) for i in range(count)])
+    if reduce:
+        held = mine + got
+    else:
+        held = jnp.stack([mine, got], axis=1)
+    out = [lax.dynamic_index_in_dim(held, me // 2, 0, keepdims=False)]
+    for d in range(1, half):
+        send = lax.dynamic_index_in_dim(held, ((me + 2 * d) % count) // 2, 0, keepdims=False)
+        out.append(lax.ppermute(send, axis_name, [(i, (i + 2 * d) % count) for i in range(count)]))
+    if reduce:
+        return sum(out)
+    return jnp.stack(out).reshape(blocks.shape)
+
+
 def _exchange(blocks, axis_name, count, direct_max=8):
     if count == 1:
         return blocks
@@ -163,7 +183,11 @@
     n_stat = -(-2 * n_rows // DH)
     stats = jnp.concatenate([o_peak, o_mass], axis=1)
     stats = jnp.pad(stats, ((0, 0), (0, n_stat * DH - 2 * n_rows))).reshape(tp_count, n_stat, DH)
-    got = _exchange(jnp.concatenate([o_numer, stats], axis=1), "tp", tp_count)
+    packed = jnp.concatenate([o_numer, stats], axis=1)
+    if 2 <= tp_count <= 8 and tp_count % 2 == 0:
+        got = _two_stage(packed, "tp", tp_count, reduce=False)
+    else:
+        got = _exchange(packed, "tp", tp_count)
     got_numer = got[:, :n_rows].reshape(tp_count, steps_n, rows_dev, heads_dev, DH)
     got_stats = got[:, n_rows:].reshape(tp_count, -1)[:, : 2 * n_rows]
     got_stats = got_stats.reshape(tp_count, 2, steps_n, rows_dev, heads_dev)
@@ -211,8 +235,10 @@
 
     piece_cols = local_width // tp_count
     pieces = jnp.moveaxis(clipped.reshape(steps_n * samples, tp_count, piece_cols), 1, 0)
-    got_pieces = _exchange(pieces, "tp", tp_count)
-    summed = got_pieces.sum(0)
+    if 2 <= tp_count <= 8 and tp_count % 2 == 0:
+        summed = _two_stage(pieces, "tp", tp_count, reduce=True)
+    else:
+        summed = _exchange(pieces, "tp", tp_count).sum(0)
     piece_start = sub_rank * local_width + tp_rank * piece_cols
     piece_a = lax.dynamic_slice_in_dim(scale_a, piece_start, piece_cols, 0)
     piece_b = lax.dynamic_slice_in_dim(scale_b, piece_start, piece_cols, 0)

time: 93.2 us -> 98 us (1.052)
  waiting for transfers between devices: 15.2 us -> 35.8 us
  starting transfers between devices: 38.2 us -> 23.6 us
  local copies, waits for them, and re-layouts: 9.32 us -> 8.19 us
    ppermute x14 -> x8, waiting for transfers between devices: 6.96 us -> 26.8 us  [the longest x2 13.5 us: _two_stage(): got = lax.ppermute(theirs, axis_name, [(i, i ^ 1) for i in range(count)])]
    ppermute x14 -> x8, starting transfers between devices: 23.3 us -> 10.8 us  [the longest x6 9.24 us: _two_stage(): lax.ppermute(send, axis_name, [(i, (i + 2 * d) % count) for i in range(co...]
    ppermute x2, starting transfers between devices: 5.16 us -> 3.29 us  [_gather_blocks(): other = lax.ppermute(x, axis_name, [(i, i ^ 1) for i in range(count)])]
    ppermute x2, waiting for transfers between devices: 1.89 us -> 3.63 us  [_gather_blocks(): other = lax.ppermute(x, axis_name, [(i, i ^ 1) for i in range(count)])]
  transfers between devices with their start and end apart: 22 -> 16, of which waited for: 14 -> 11; matrix products, arithmetic and copies ran while one was open for 6% -> 4% of each run, Pallas kernels for 0% -> 0%
where the time goes in v6:
time: 98 us; the launch traced here: 97.4 us
  waiting for transfers between devices  35.8 us (37%)
  starting transfers between devices  23.6 us (24%)
  matrix products  13.3 us (14%)
  Pallas kernels  8.59 us (9%)
  local copies, waits for them, and re-layouts  8.19 us (8%)
  other arithmetic  5.69 us (6%)
  blocking collectives  1.85 us (2%)
    ppermute x2, waiting for transfers between devices, _two_stage(): got = lax.ppermute(theirs, axis_name, [(i, i ^ 1) for i in range(count)])  13.5 us
    ppermute x6, waiting for transfers between devices, _two_stage(): lax.ppermute(send, axis_name, [(i, (i + 2 * d) % count) for i in range(co...  13.3 us
    dot_general x1, matrix products, per_device(): jnp.einsum('rhd,hdf->rhf', head_rows_in, head_weights, preferred_element_...  12.9 us
    ppermute x6, starting transfers between devices, _gather_blocks(): lax.ppermute(pair, axis_name, [(i, (i + 2 * d) % count) for i in range(co...  9.44 us
    ppermute x6, starting transfers between devices, _two_stage(): lax.ppermute(send, axis_name, [(i, (i + 2 * d) % count) for i in range(co...  9.24 us
    pallas_call x1, Pallas kernels, _attend_local(): pl.pallas_call(_attend_kernel, grid=(kv_heads,), in_specs=[pl.BlockSpec((...  8.59 us
    ppermute x6, waiting for transfers between devices, _gather_blocks(): lax.ppermute(pair, axis_name, [(i, (i + 2 * d) % count) for i in range(co...  5.43 us
    ppermute x2, waiting for transfers between devices, _gather_blocks(): other = lax.ppermute(x, axis_name, [(i, i ^ 1) for i in range(count)])  3.63 us
  transfers between devices with their start and end apart: 16, of which 11 were waited for; matrix products, arithmetic and copies ran while one was open for 4% of the time, Pallas kernels for 0%

profile of v6, /device:TPU:0, one launch (start us, length us, event | category | flops | bytes accessed | tf_op | source)
XLA Modules:
  0.0 97.4 jit_solution(5532754516288580069)
XLA Ops:
  0.0 2.9 %collective-permute-start = (bf16[2,4,2048]{2,1,0:T(4,128)(2,1)}, bf16[2,4,2048]{2,1,0:T(4,128)(2,1)S(1)}, u32[]{:S(2)}, u32[]{:S(2)}) collective-permute-start(bf16[2,4,2048]{2,1,0:T(4,128)(2,1)} %param.9), channel_id=1, source_target_pairs={{0,2},{2,0},{4,6},{6,4},{8,10},{10,8},{12,14},{14,12},{1,3},{3,1},... | collective-permute-start | bytes 98312 | tf_op jit(solution)/shard_map/ppermute | solution.py:27
  2.9 0.8 reshape.299
  3.7 0.7 multiply_exponential_fusion.1
  4.5 1.3 %compare_convert_fusion.valid_ref = f32[4,128]{1,0:T(4,128)} fusion(s32[128]{0:T(128)S(1)} %iota_add_fusion, s32[4]{0:T(128)} %param.12), kind=kLoop, calls=%fused_computation.78 | loop fusion | flops 1024 | bytes 2576 | tf_op jit(solution)/shard_map/convert_element_type | solution.py:170
  5.8 0.9 maximum_select_fusion.1
  6.8 1.6 %collective-permute-start.1 = (bf16[2,2,4,2048]{3,2,1,0:T(4,128)(2,1)S(1)}, bf16[2,2,4,2048]{3,2,1,0:T(4,128)(2,1)S(1)}, u32[]{:S(2)}, u32[]{:S(2)}) collective-permute-start(bf16[2,2,4,2048]{3,2,1,0:T(4,128)(2,1)S(1)} %maximum_select_fusion.1), channel_id=1, source_target_pairs={{0,4},{2,6},{4,8},{6,10},{8,12},{10,14},{12,0},{14,2},{1,5},{3,7},... | collective-permute-start | bytes 196616 | tf_op jit(solution)/shard_map/ppermute | solution.py:33
  8.4 2.6 %collective-permute-start.2 = (bf16[2,2,4,2048]{3,2,1,0:T(4,128)(2,1)S(1)}, bf16[2,2,4,2048]{3,2,1,0:T(4,128)(2,1)S(1)}, u32[]{:S(2)}, u32[]{:S(2)}) collective-permute-start(bf16[2,2,4,2048]{3,2,1,0:T(4,128)(2,1)S(1)} %maximum_select_fusion.1), channel_id=1, source_target_pairs={{0,8},{2,10},{4,12},{6,14},{8,0},{10,2},{12,4},{14,6},{1,9},{3,11}... | collective-permute-start | bytes 196616 | tf_op jit(solution)/shard_map/ppermute | solution.py:33
  11.0 1.3 %collective-permute-start.3 = (bf16[2,2,4,2048]{3,2,1,0:T(4,128)(2,1)S(1)}, bf16[2,2,4,2048]{3,2,1,0:T(4,128)(2,1)S(1)}, u32[]{:S(2)}, u32[]{:S(2)}) collective-permute-start(bf16[2,2,4,2048]{3,2,1,0:T(4,128)(2,1)S(1)} %maximum_select_fusion.1), channel_id=1, source_target_pairs={{0,12},{2,14},{4,0},{6,2},{8,4},{10,6},{12,8},{14,10},{1,13},{3,15... | collective-permute-start | bytes 196616 | tf_op jit(solution)/shard_map/ppermute | solution.py:33
  12.3 0.9 maximum_select_fusion
  13.2 0.4 collective-permute-done.1
  13.7 2.1 %collective-permute-done.2 = bf16[2,2,4,2048]{3,2,1,0:T(4,128)(2,1)S(1)} collective-permute-done((bf16[2,2,4,2048]{3,2,1,0:T(4,128)(2,1)S(1)}, bf16[2,2,4,2048]{3,2,1,0:T(4,128)(2,1)S(1)}, u32[]{:S(2)}, u32[]{:S(2)}) %collective-permute-start.2) | collective-permute-done | bytes 65568 | tf_op jit(solution)/shard_map/ppermute | solution.py:33
  15.7 0.2 pad_maximum_fusion.2
  16.1 0.7 scatter_fusion
  16.8 0.2 reshape.326
  17.0 0.7 copy.120
  17.7 8.6 %shard_map.91 = (f32[8,128,128]{2,1,0:T(8,128)}, f32[8,128,128]{2,1,0:T(8,128)}, f32[8,128,128]{2,1,0:T(8,128)}) custom-call(bf16[8,128,128]{2,1,0:T(8,128)(2,1)} %bitcast.135, bf16[2,1024,1024]{2,1,0:T(8,128)(2,1)} %v_ref.1, bf16[2,1024,1024]{2,1,0:T(8,128)(2,1)} %v_ref.1, bf16[2,4,128,1024]{3,2,1,0:T(8,128)(2,1)} %tv_ref.1, ...), custom_call_target="tpu_custom_call" | custom-call | flops 603979776 | bytes 8126464 | tf_op jit(solution)/shard_map/pallas_call | solution.py:126
  26.3 1.1 %copy.98 = f32[8,4,2,16,128]{4,3,1,2,0:T(8,128)S(1)} copy(f32[8,4,2,16,128]{4,3,2,1,0:T(8,128)} %bitcast.136) | data formatting | bytes 1048576 | tf_op jit(solution)/shard_map/reshape | solution.py:179
  27.4 1.5 %slice_reduce_fusion = (f32[8,128]{1,0:T(8,128)S(1)}, f32[8,128]{1,0:T(8,128)S(1)}) fusion(f32[8,128,128]{2,1,0:T(8,128)} %get-tuple-element.10, f32[8,128,128]{2,1,0:T(8,128)} %get-tuple-element.9), kind=kLoop, calls=%fused_computation.19 | loop fusion | bytes 16384 | tf_op jit(solution)/shard_map/slice | solution.py:181
  29.5 1.1 %collective-permute-start.4 = (f32[4,130,128]{2,1,0:T(8,128)S(1)}, f32[4,130,128]{2,1,0:T(8,128)S(1)}, u32[]{:S(2)}, u32[]{:S(2)}) collective-permute-start(f32[4,130,128]{2,1,0:T(8,128)S(1)} %get-tuple-element.15), channel_id=1, source_target_pairs={{0,2},{2,0},{4,6},{6,4},{8,10},{10,8},{12,14},{14,12},{1,3},{3,1},... | collective-permute-start | bytes 798728 | tf_op jit(solution)/shard_map/ppermute | solution.py:54
  30.7 0.2 fusion.22
  30.9 5.5 %collective-permute-done.4 = f32[4,130,128]{2,1,0:T(8,128)S(1)} collective-permute-done((f32[4,130,128]{2,1,0:T(8,128)S(1)}, f32[4,130,128]{2,1,0:T(8,128)S(1)}, u32[]{:S(2)}, u32[]{:S(2)}) %collective-permute-start.4) | collective-permute-done | bytes 266272 | tf_op jit(solution)/shard_map/ppermute | solution.py:54
  36.5 2.1 %collective-permute-start.5 = (f32[2,130,128]{2,1,0:T(8,128)S(1)}, f32[2,130,128]{2,1,0:T(8,128)S(1)}, u32[]{:S(2)}, u32[]{:S(2)}) collective-permute-start(f32[2,130,128]{2,1,0:T(8,128)S(1)} %get-tuple-element.12), channel_id=1, source_target_pairs={{0,4},{2,6},{4,8},{6,10},{8,12},{10,14},{12,0},{14,2},{1,5},{3,7},... | collective-permute-start | bytes 399368 | tf_op jit(solution)/shard_map/ppermute | solution.py:62
  38.6 0.9 collective-permute-start.6
  39.5 1.5 %collective-permute-start.7 = (f32[2,130,128]{2,1,0:T(8,128)S(1)}, f32[2,130,128]{2,1,0:T(8,128)S(1)}, u32[]{:S(2)}, u32[]{:S(2)}) collective-permute-start(f32[2,130,128]{2,1,0:T(8,128)S(1)} %get-tuple-element.14), channel_id=1, source_target_pairs={{0,12},{2,14},{4,0},{6,2},{8,4},{10,6},{12,8},{14,10},{1,13},{3,15... | collective-permute-start | bytes 399368 | tf_op jit(solution)/shard_map/ppermute | solution.py:62
  41.2 3.3 %collective-permute-done.5 = f32[2,130,128]{2,1,0:T(8,128)S(1)} collective-permute-done((f32[2,130,128]{2,1,0:T(8,128)S(1)}, f32[2,130,128]{2,1,0:T(8,128)S(1)}, u32[]{:S(2)}, u32[]{:S(2)}) %collective-permute-start.5) | collective-permute-done | bytes 133152 | tf_op jit(solution)/shard_map/ppermute | solution.py:62
  44.5 4.0 %collective-permute-done.6 = f32[2,130,128]{2,1,0:T(8,128)S(1)} collective-permute-done((f32[2,130,128]{2,1,0:T(8,128)S(1)}, f32[2,130,128]{2,1,0:T(8,128)S(1)}, u32[]{:S(2)}, u32[]{:S(2)}) %collective-permute-start.6) | collective-permute-done | bytes 133152 | tf_op jit(solution)/shard_map/ppermute | solution.py:62
  48.9 0.1 copy.111
  49.2 0.2 fusion.2
  49.4 0.2 fusion.24
  49.8 1.9 %all_gather.3 = bf16[2,8,2048]{2,0,1:T(2,128)(2,1)S(1)} all-gather(bf16[2,4,2048]{2,0,1:T(2,128)(2,1)S(1)} %copy.115), channel_id=1, replica_groups=mesh['rep'=2,'tp'=8,'sub'=2] {'sub'}, dimensions={1}, use_global_device_ids=true | all-gather | bytes 98304 | tf_op jit(solution)/shard_map/all_gather | solution.py:222
  51.7 12.9 %fusion.1 = f32[16,8192]{1,0:T(8,128)S(1)} fusion(f32[8192]{0:T(1024)S(1)} %dynamic_slice.63, bf16[16,128,8192]{2,1,0:T(8,128)(2,1)} %bitcast.163, bf16[16,16,128]{2,1,0:T(8,128)(2,1)S(1)} %bitcast.154), kind=kOutput, calls=%fused_computation.4 | convolution fusion | flops 543031296 | bytes 34177024 | tf_op jit(solution)/shard_map/rhd,hdf->rhf/dot_general | solution.py:231
  64.6 0.3 copy.127
  64.9 0.3 copy.118
  65.3 0.5 collective-permute-start.8
  65.7 8.0 %collective-permute-done.8 = f32[4,16,1024]{2,1,0:T(8,128)S(1)} collective-permute-done((f32[4,16,1024]{2,1,0:T(8,128)S(1)}, f32[4,16,1024]{2,1,0:T(8,128)S(1)}, u32[]{:S(2)}, u32[]{:S(2)}) %collective-permute-start.8) | collective-permute-done | bytes 262176 | tf_op jit(solution)/shard_map/ppermute | solution.py:54
  73.8 1.3 %collective-permute-start.10 = (f32[16,1024]{1,0:T(8,128)S(1)}, f32[16,1024]{1,0:T(8,128)S(1)}, u32[]{:S(2)}, u32[]{:S(2)}) collective-permute-start(f32[16,1024]{1,0:T(8,128)S(1)} %get-tuple-element.19), channel_id=1, source_target_pairs={{0,8},{2,10},{4,12},{6,14},{8,0},{10,2},{12,4},{14,6},{1,9},{3,11}... | collective-permute-start | bytes 196616 | tf_op jit(solution)/shard_map/ppermute | solution.py:62
  75.1 3.4 %collective-permute-start.11 = (f32[16,1024]{1,0:T(8,128)S(1)}, f32[16,1024]{1,0:T(8,128)S(1)}, u32[]{:S(2)}, u32[]{:S(2)}) collective-permute-start(f32[16,1024]{1,0:T(8,128)S(1)} %get-tuple-element.18), channel_id=1, source_target_pairs={{0,12},{2,14},{4,0},{6,2},{8,4},{10,6},{12,8},{14,10},{1,13},{3,15... | collective-permute-start | bytes 196616 | tf_op jit(solution)/shard_map/ppermute | solution.py:62
  78.6 2.3 %collective-permute-done.10 = f32[16,1024]{1,0:T(8,128)S(1)} collective-permute-done((f32[16,1024]{1,0:T(8,128)S(1)}, f32[16,1024]{1,0:T(8,128)S(1)}, u32[]{:S(2)}, u32[]{:S(2)}) %collective-permute-start.10) | collective-permute-done | bytes 65568 | tf_op jit(solution)/shard_map/ppermute | solution.py:62
  80.9 3.6 %collective-permute-done.9 = f32[16,1024]{1,0:T(8,128)S(1)} collective-permute-done((f32[16,1024]{1,0:T(8,128)S(1)}, f32[16,1024]{1,0:T(8,128)S(1)}, u32[]{:S(2)}, u32[]{:S(2)}) %collective-permute-start.9) | collective-permute-done | bytes 65568 | tf_op jit(solution)/shard_map/ppermute | solution.py:62
  84.6 0.4 collective-permute-start.12
  84.9 3.6 %collective-permute-done.12 = bf16[16,1024]{1,0:T(8,128)(2,1)S(1)} collective-permute-done((bf16[16,1024]{1,0:T(8,128)(2,1)S(1)}, bf16[16,1024]{1,0:T(8,128)(2,1)S(1)}, u32[]{:S(2)}, u32[]{:S(2)}) %collective-permute-start.12) | collective-permute-done | bytes 32800 | tf_op jit(solution)/shard_map/ppermute | solution.py:27
  88.6 0.7 collective-permute-start.14
  89.3 3.2 %collective-permute-start.15 = (bf16[2,16,1024]{2,1,0:T(8,128)(2,1)S(1)}, bf16[2,16,1024]{2,1,0:T(8,128)(2,1)S(1)}, u32[]{:S(2)}, u32[]{:S(2)}) collective-permute-start(bf16[2,16,1024]{2,1,0:T(8,128)(2,1)S(1)} %maximum_select_fusion.3), channel_id=1, source_target_pairs={{0,12},{2,14},{4,0},{6,2},{8,4},{10,6},{12,8},{14,10},{1,13},{3,15... | collective-permute-start | bytes 196616 | tf_op jit(solution)/shard_map/ppermute | solution.py:33
  92.5 2.2 %collective-permute-done.13 = bf16[2,16,1024]{2,1,0:T(8,128)(2,1)S(1)} collective-permute-done((bf16[2,16,1024]{2,1,0:T(8,128)(2,1)S(1)}, bf16[2,16,1024]{2,1,0:T(8,128)(2,1)S(1)}, u32[]{:S(2)}, u32[]{:S(2)}) %collective-permute-start.13) | collective-permute-done | bytes 65568 | tf_op jit(solution)/shard_map/ppermute | solution.py:33
  94.7 0.7 collective-permute-done.15
  95.5 0.7 scatter_fusion.1
  96.2 0.3 copy.119
  96.6 0.8 add_convert_fusion
  (67 shorter events, 2.2 us)
Async XLA Ops:
  0.0 5.8 %collective-permute-start = (bf16[2,4,2048]{2,1,0:T(4,128)(2,1)}, bf16[2,4,2048]{2,1,0:T(4,128)(2,1)S(1)}, u32[]{:S(2)}, u32[]{:S(2)}) collective-permute-start(bf16[2,4,2048]{2,1,0:T(4,128)(2,1)} %param.9), channel_id=1, source_target_pairs={{0,2},{2,0},{4,6},{6,4},{8,10},{10,8},{12,14},{14,12},{1,3},{3,1},... | collective-permute-start | bytes 98312 | tf_op jit(solution)/shard_map/ppermute | solution.py:27
  6.8 6.9 %collective-permute-start.1 = (bf16[2,2,4,2048]{3,2,1,0:T(4,128)(2,1)S(1)}, bf16[2,2,4,2048]{3,2,1,0:T(4,128)(2,1)S(1)}, u32[]{:S(2)}, u32[]{:S(2)}) collective-permute-start(bf16[2,2,4,2048]{3,2,1,0:T(4,128)(2,1)S(1)} %maximum_select_fusion.1), channel_id=1, source_target_pairs={{0,4},{2,6},{4,8},{6,10},{8,12},{10,14},{12,0},{14,2},{1,5},{3,7},... | collective-permute-start | bytes 196616 | tf_op jit(solution)/shard_map/ppermute | solution.py:33
  8.4 7.3 %collective-permute-start.2 = (bf16[2,2,4,2048]{3,2,1,0:T(4,128)(2,1)S(1)}, bf16[2,2,4,2048]{3,2,1,0:T(4,128)(2,1)S(1)}, u32[]{:S(2)}, u32[]{:S(2)}) collective-permute-start(bf16[2,2,4,2048]{3,2,1,0:T(4,128)(2,1)S(1)} %maximum_select_fusion.1), channel_id=1, source_target_pairs={{0,8},{2,10},{4,12},{6,14},{8,0},{10,2},{12,4},{14,6},{1,9},{3,11}... | collective-permute-start | bytes 196616 | tf_op jit(solution)/shard_map/ppermute | solution.py:33
  11.0 4.8 %collective-permute-start.3 = (bf16[2,2,4,2048]{3,2,1,0:T(4,128)(2,1)S(1)}, bf16[2,2,4,2048]{3,2,1,0:T(4,128)(2,1)S(1)}, u32[]{:S(2)}, u32[]{:S(2)}) collective-permute-start(bf16[2,2,4,2048]{3,2,1,0:T(4,128)(2,1)S(1)} %maximum_select_fusion.1), channel_id=1, source_target_pairs={{0,12},{2,14},{4,0},{6,2},{8,4},{10,6},{12,8},{14,10},{1,13},{3,15... | collective-permute-start | bytes 196616 | tf_op jit(solution)/shard_map/ppermute | solution.py:33
  17.7 12.9 %copy-start = (bf16[2,4,2048]{2,1,0:T(4,128)(2,1)S(1)}, bf16[2,4,2048]{2,1,0:T(4,128)(2,1)}, u32[]{:S(2)}) copy-start(bf16[2,4,2048]{2,1,0:T(4,128)(2,1)} %param.9) | copy-start | bytes 98308
  29.5 6.9 %collective-permute-start.4 = (f32[4,130,128]{2,1,0:T(8,128)S(1)}, f32[4,130,128]{2,1,0:T(8,128)S(1)}, u32[]{:S(2)}, u32[]{:S(2)}) collective-permute-start(f32[4,130,128]{2,1,0:T(8,128)S(1)} %get-tuple-element.15), channel_id=1, source_target_pairs={{0,2},{2,0},{4,6},{6,4},{8,10},{10,8},{12,14},{14,12},{1,3},{3,1},... | collective-permute-start | bytes 798728 | tf_op jit(solution)/shard_map/ppermute | solution.py:54
  36.5 8.0 %collective-permute-start.5 = (f32[2,130,128]{2,1,0:T(8,128)S(1)}, f32[2,130,128]{2,1,0:T(8,128)S(1)}, u32[]{:S(2)}, u32[]{:S(2)}) collective-permute-start(f32[2,130,128]{2,1,0:T(8,128)S(1)} %get-tuple-element.12), channel_id=1, source_target_pairs={{0,4},{2,6},{4,8},{6,10},{8,12},{10,14},{12,0},{14,2},{1,5},{3,7},... | collective-permute-start | bytes 399368 | tf_op jit(solution)/shard_map/ppermute | solution.py:62
  38.6 10.0 %collective-permute-start.6 = (f32[2,130,128]{2,1,0:T(8,128)S(1)}, f32[2,130,128]{2,1,0:T(8,128)S(1)}, u32[]{:S(2)}, u32[]{:S(2)}) collective-permute-start(f32[2,130,128]{2,1,0:T(8,128)S(1)} %get-tuple-element.13), channel_id=1, source_target_pairs={{0,8},{2,10},{4,12},{6,14},{8,0},{10,2},{12,4},{14,6},{1,9},{3,11}... | collective-permute-start | bytes 399368 | tf_op jit(solution)/shard_map/ppermute | solution.py:62
  39.5 9.0 %collective-permute-start.7 = (f32[2,130,128]{2,1,0:T(8,128)S(1)}, f32[2,130,128]{2,1,0:T(8,128)S(1)}, u32[]{:S(2)}, u32[]{:S(2)}) collective-permute-start(f32[2,130,128]{2,1,0:T(8,128)S(1)} %get-tuple-element.14), channel_id=1, source_target_pairs={{0,12},{2,14},{4,0},{6,2},{8,4},{10,6},{12,8},{14,10},{1,13},{3,15... | collective-permute-start | bytes 399368 | tf_op jit(solution)/shard_map/ppermute | solution.py:62
  51.7 14.0 %copy-start.2 = (s32[128]{0:T(128)S(1)}, s32[128]{0:T(128)}, u32[]{:S(2)}) copy-start(s32[128]{0:T(128)} %param.16) | copy-start | bytes 1540
  64.6 32.0 %copy-start.1 = (bf16[2,8,8192]{2,1,0:T(8,128)(2,1)S(1)}, bf16[2,8,8192]{2,1,0:T(8,128)(2,1)}, u32[]{:S(2)}) copy-start(bf16[2,8,8192]{2,1,0:T(8,128)(2,1)} %param.17) | copy-start | bytes 786436
  65.3 8.4 %collective-permute-start.8 = (f32[4,16,1024]{2,1,0:T(8,128)S(1)}, f32[4,16,1024]{2,1,0:T(8,128)S(1)}, u32[]{:S(2)}, u32[]{:S(2)}) collective-permute-start(f32[4,16,1024]{2,1,0:T(8,128)S(1)} %dynamic-slice_bitcast_fusion.1), channel_id=1, source_target_pairs={{0,2},{2,0},{4,6},{6,4},{8,10},{10,8},{12,14},{14,12},{1,3},{3,1},... | collective-permute-start | bytes 786440 | tf_op jit(solution)/shard_map/ppermute | solution.py:54
  73.8 7.1 %collective-permute-start.10 = (f32[16,1024]{1,0:T(8,128)S(1)}, f32[16,1024]{1,0:T(8,128)S(1)}, u32[]{:S(2)}, u32[]{:S(2)}) collective-permute-start(f32[16,1024]{1,0:T(8,128)S(1)} %get-tuple-element.19), channel_id=1, source_target_pairs={{0,8},{2,10},{4,12},{6,14},{8,0},{10,2},{12,4},{14,6},{1,9},{3,11}... | collective-permute-start | bytes 196616 | tf_op jit(solution)/shard_map/ppermute | solution.py:62
  75.1 5.8 %collective-permute-start.11 = (f32[16,1024]{1,0:T(8,128)S(1)}, f32[16,1024]{1,0:T(8,128)S(1)}, u32[]{:S(2)}, u32[]{:S(2)}) collective-permute-start(f32[16,1024]{1,0:T(8,128)S(1)} %get-tuple-element.18), channel_id=1, source_target_pairs={{0,12},{2,14},{4,0},{6,2},{8,4},{10,6},{12,8},{14,10},{1,13},{3,15... | collective-permute-start | bytes 196616 | tf_op jit(solution)/shard_map/ppermute | solution.py:62
  78.5 6.1 %collective-permute-start.9 = (f32[16,1024]{1,0:T(8,128)S(1)}, f32[16,1024]{1,0:T(8,128)S(1)}, u32[]{:S(2)}, u32[]{:S(2)}) collective-permute-start(f32[16,1024]{1,0:T(8,128)S(1)} %get-tuple-element.17), channel_id=1, source_target_pairs={{0,4},{2,6},{4,8},{6,10},{8,12},{10,14},{12,0},{14,2},{1,5},{3,7},... | collective-permute-start | bytes 196616 | tf_op jit(solution)/shard_map/ppermute | solution.py:62
  84.6 4.0 %collective-permute-start.12 = (bf16[16,1024]{1,0:T(8,128)(2,1)S(1)}, bf16[16,1024]{1,0:T(8,128)(2,1)S(1)}, u32[]{:S(2)}, u32[]{:S(2)}) collective-permute-start(bf16[16,1024]{1,0:T(8,128)(2,1)S(1)} %fusion.18), channel_id=1, source_target_pairs={{0,2},{2,0},{4,6},{6,4},{8,10},{10,8},{12,14},{14,12},{1,3},{3,1},... | collective-permute-start | bytes 98312 | tf_op jit(solution)/shard_map/ppermute | solution.py:27
  88.6 6.1 %collective-permute-start.13 = (bf16[2,16,1024]{2,1,0:T(8,128)(2,1)S(1)}, bf16[2,16,1024]{2,1,0:T(8,128)(2,1)S(1)}, u32[]{:S(2)}, u32[]{:S(2)}) collective-permute-start(bf16[2,16,1024]{2,1,0:T(8,128)(2,1)S(1)} %maximum_select_fusion.3), channel_id=1, source_target_pairs={{0,4},{2,6},{4,8},{6,10},{8,12},{10,14},{12,0},{14,2},{1,5},{3,7},... | collective-permute-start | bytes 196616 | tf_op jit(solution)/shard_map/ppermute | solution.py:33
  88.6 6.1 %collective-permute-start.14 = (bf16[2,16,1024]{2,1,0:T(8,128)(2,1)S(1)}, bf16[2,16,1024]{2,1,0:T(8,128)(2,1)S(1)}, u32[]{:S(2)}, u32[]{:S(2)}) collective-permute-start(bf16[2,16,1024]{2,1,0:T(8,128)(2,1)S(1)} %maximum_select_fusion.3), channel_id=1, source_target_pairs={{0,8},{2,10},{4,12},{6,14},{8,0},{10,2},{12,4},{14,6},{1,9},{3,11}... | collective-permute-start | bytes 196616 | tf_op jit(solution)/shard_map/ppermute | solution.py:33
  89.3 6.1 %collective-permute-start.15 = (bf16[2,16,1024]{2,1,0:T(8,128)(2,1)S(1)}, bf16[2,16,1024]{2,1,0:T(8,128)(2,1)S(1)}, u32[]{:S(2)}, u32[]{:S(2)}) collective-permute-start(bf16[2,16,1024]{2,1,0:T(8,128)(2,1)S(1)} %maximum_select_fusion.3), channel_id=1, source_target_pairs={{0,12},{2,14},{4,0},{6,2},{8,4},{10,6},{12,8},{14,10},{1,13},{3,15... | collective-permute-start | bytes 196616 | tf_op jit(solution)/shard_map/ppermute | solution.py:33

commit v7 on v5

--- a/solution.py
+++ b/solution.py
@@ -62,39 +62,45 @@
 
 
 def _attend_kernel(q_ref, k_ref, v_ref, tk_ref, tv_ref, valid_ref, numer_ref, peak_ref, mass_ref):
-    rows_n = q_ref.shape[1]
+    heads_n, rows_n = q_ref.shape[0], q_ref.shape[1]
     samples = tk_ref.shape[1]
     per_sample = rows_n // samples
     score_scale = 1.0 / math.sqrt(DH)
     dims_nt = (((1,), (1,)), ((), ()))
-    q = q_ref[0]
-    p_scores = lax.dot_general(q, k_ref[0], dims_nt, preferred_element_type=jnp.float32)
-    p_scores = p_scores * score_scale
-    t_parts = []
-    for r in range(samples):
-        qr = q[r * per_sample:(r + 1) * per_sample]
-        sr = lax.dot_general(qr, tk_ref[0, r], dims_nt, preferred_element_type=jnp.float32)
-        sr = sr * score_scale
-        t_parts.append(jnp.where(valid_ref[r:r + 1, :] > 0.0, sr, NEG_FILL))
-    t_scores = jnp.concatenate(t_parts, axis=0)
-    peak = jnp.maximum(
-        jnp.max(p_scores, axis=1, keepdims=True), jnp.max(t_scores, axis=1, keepdims=True)
-    )
-    p_w = jnp.exp(p_scores - peak)
-    t_w = jnp.exp(t_scores - peak)
-    mass = jnp.sum(p_w, axis=1, keepdims=True) + jnp.sum(t_w, axis=1, keepdims=True)
-    numer = jnp.dot(p_w.astype(jnp.bfloat16), v_ref[0], preferred_element_type=jnp.float32)
-    t_w16 = t_w.astype(jnp.bfloat16)
-    t_numer = [
-        jnp.dot(
-            t_w16[r * per_sample:(r + 1) * per_sample], tv_ref[0, r],
-            preferred_element_type=jnp.float32,
+    for j in range(heads_n):
+        cols = slice(j * DH, (j + 1) * DH)
+        q = q_ref[j]
+        p_scores = lax.dot_general(q, k_ref[0, :, cols], dims_nt, preferred_element_type=jnp.float32)
+        p_scores = p_scores * score_scale
+        t_parts = []
+        for r in range(samples):
+            qr = q[r * per_sample:(r + 1) * per_sample]
+            sr = lax.dot_general(
+                qr, tk_ref[0, r, :, cols], dims_nt, preferred_element_type=jnp.float32
+            )
+            sr = sr * score_scale
+            t_parts.append(jnp.where(valid_ref[r:r + 1, :] > 0.0, sr, NEG_FILL))
+        t_scores = jnp.concatenate(t_parts, axis=0)
+        peak = jnp.maximum(
+            jnp.max(p_scores, axis=1, keepdims=True), jnp.max(t_scores, axis=1, keepdims=True)
         )
-        for r in range(samples)
-    ]
-    numer_ref[0] = numer + jnp.concatenate(t_numer, axis=0)
-    peak_ref[0] = jnp.broadcast_to(peak, peak_ref.shape[1:])
-    mass_ref[0] = jnp.broadcast_to(mass, mass_ref.shape[1:])
+        p_w = jnp.exp(p_scores - peak)
+        t_w = jnp.exp(t_scores - peak)
+        mass = jnp.sum(p_w, axis=1, keepdims=True) + jnp.sum(t_w, axis=1, keepdims=True)
+        numer = jnp.dot(
+            p_w.astype(jnp.bfloat16), v_ref[0, :, cols], preferred_element_type=jnp.float32
+        )
+        t_w16 = t_w.astype(jnp.bfloat16)
+        t_numer = [
+            jnp.dot(
+                t_w16[r * per_sample:(r + 1) * per_sample], tv_ref[0, r, :, cols],
+                preferred_element_type=jnp.float32,
+            )
+            for r in range(samples)
+        ]
+        numer_ref[j] = numer + jnp.concatenate(t_numer, axis=0)
+        peak_ref[j] = jnp.broadcast_to(peak, peak_ref.shape[1:])
+        mass_ref[j] = jnp.broadcast_to(mass, mass_ref.shape[1:])
 
 
 def _attend_local(q_rows, prefix_kv, tail_kv, valid):
@@ -103,21 +109,23 @@
     samples, tail_dev = tail_kv.shape[1], tail_kv.shape[2]
     flops = 4 * kv_heads * rows_n * DH * (prefix_dev + tail_dev)
     bytes_in = 2 * (prefix_kv.size + tail_kv.size + q_rows.size)
+    per_step = 4 if kv_heads % 4 == 0 else 1
+    width = per_step * DH
     return pl.pallas_call(
         _attend_kernel,
-        grid=(kv_heads,),
+        grid=(kv_heads // per_step,),
         in_specs=[
-            pl.BlockSpec((1, rows_n, DH), lambda k: (k, 0, 0)),
-            pl.BlockSpec((1, prefix_dev, DH), lambda k: (0, 0, k)),
-            pl.BlockSpec((1, prefix_dev, DH), lambda k: (1, 0, k)),
-            pl.BlockSpec((1, samples, tail_dev, DH), lambda k: (0, 0, 0, k)),
-            pl.BlockSpec((1, samples, tail_dev, DH), lambda k: (1, 0, 0, k)),
+            pl.BlockSpec((per_step, rows_n, DH), lambda k: (k, 0, 0)),
+            pl.BlockSpec((1, prefix_dev, width), lambda k: (0, 0, k)),
+            pl.BlockSpec((1, prefix_dev, width), lambda k: (1, 0, k)),
+            pl.BlockSpec((1, samples, tail_dev, width), lambda k: (0, 0, 0, k)),
+            pl.BlockSpec((1, samples, tail_dev, width), lambda k: (1, 0, 0, k)),
             pl.BlockSpec((samples, tail_dev), lambda k: (0, 0)),
         ],
         out_specs=[
-            pl.BlockSpec((1, rows_n, DH), lambda k: (k, 0, 0)),
-            pl.BlockSpec((1, rows_n, DH), lambda k: (k, 0, 0)),
-            pl.BlockSpec((1, rows_n, DH), lambda k: (k, 0, 0)),
+            pl.BlockSpec((per_step, rows_n, DH), lambda k: (k, 0, 0)),
+            pl.BlockSpec((per_step, rows_n, DH), lambda k: (k, 0, 0)),
+            pl.BlockSpec((per_step, rows_n, DH), lambda k: (k, 0, 0)),
         ],
         out_shape=[jax.ShapeDtypeStruct((kv_heads, rows_n, DH), jnp.float32)] * 3,
         cost_estimate=pl.CostEstimate(
@@ -125,6 +133,7 @@
             transcendentals=kv_heads * rows_n * (prefix_dev + tail_dev),
             bytes_accessed=bytes_in + 3 * 4 * kv_heads * rows_n * DH,
         ),
+        compiler_params=pltpu.CompilerParams(vmem_limit_bytes=48 * 1024 * 1024),
     )(q_rows, prefix_kv, prefix_kv, tail_kv, tail_kv, valid)
 
 

time: 93.2 us -> 87.9 us (0.943)
  Pallas kernels: 8.58 us -> 5.42 us
  local copies, waits for them, and re-layouts: 9.32 us -> 7.95 us
    pallas_call x1, Pallas kernels: 8.58 us -> 5.42 us  [_attend_local(): pl.pallas_call(_attend_kernel, grid=(kv_heads // per_step,), in_specs=[pl...]
    unnamed x20 -> x22, local copies, waits for them, and re-layouts: 0.47 us -> 2.06 us
    slice x1, local copies, waits for them, and re-layouts: 1.54 us -> 0.34 us  [per_device(): o_mass = by_owner(k_mass[..., 0].reshape(grid4)).reshape(tp_count, -1)]
    reshape x1, local copies, waits for them, and re-layouts: 1.09 us -> 0.04 us  [per_device(): o_numer = by_owner(k_numer.reshape(grid4 + (DH,))).reshape(tp_count, -1, DH)]
  transfers between devices with their start and end apart: 22 -> 22, of which waited for: 14 -> 14; matrix products, arithmetic and copies ran while one was open for 6% -> 5% of each run, Pallas kernels for 0% -> 0%
where the time goes in v7:
time: 87.9 us; the launch traced here: 87.5 us
  starting transfers between devices  38.4 us (44%)
  waiting for transfers between devices  14.9 us (17%)
  matrix products  13.3 us (15%)
  local copies, waits for them, and re-layouts  7.95 us (9%)
  Pallas kernels  5.42 us (6%)
  other arithmetic  4.99 us (6%)
  blocking collectives  1.85 us (2%)
    ppermute x14, starting transfers between devices, _exchange(): lax.ppermute(send, axis_name, [(i, (i + k) % count) for i in range(count)])  23.3 us
    dot_general x1, matrix products, per_device(): jnp.einsum('rhd,hdf->rhf', head_rows_in, head_weights, preferred_element_...  12.9 us
    ppermute x6, starting transfers between devices, _gather_blocks(): lax.ppermute(pair, axis_name, [(i, (i + 2 * d) % count) for i in range(co...  9.99 us
    ppermute x14, waiting for transfers between devices, _exchange(): lax.ppermute(send, axis_name, [(i, (i + k) % count) for i in range(count)])  6.55 us
    ppermute x6, waiting for transfers between devices, _gather_blocks(): lax.ppermute(pair, axis_name, [(i, (i + 2 * d) % count) for i in range(co...  6.46 us
    pallas_call x1, Pallas kernels, _attend_local(): pl.pallas_call(_attend_kernel, grid=(kv_heads // per_step,), in_specs=[pl...  5.42 us
    ppermute x2, starting transfers between devices, _gather_blocks(): other = lax.ppermute(x, axis_name, [(i, i ^ 1) for i in range(count)])  5.16 us
    unnamed x22, local copies, waits for them, and re-layouts  2.06 us
  transfers between devices with their start and end apart: 22, of which 14 were waited for; matrix products, arithmetic and copies ran while one was open for 5% of the time, Pallas kernels for 0%

profile of v7, /device:TPU:0, one launch (start us, length us, event | category | flops | bytes accessed | tf_op | source)
XLA Modules:
  0.0 87.5 jit_solution(4731272718482210087)
XLA Ops:
  0.0 2.9 %collective-permute-start = (bf16[2,4,2048]{2,1,0:T(4,128)(2,1)}, bf16[2,4,2048]{2,1,0:T(4,128)(2,1)S(1)}, u32[]{:S(2)}, u32[]{:S(2)}) collective-permute-start(bf16[2,4,2048]{2,1,0:T(4,128)(2,1)} %param.9), channel_id=1, source_target_pairs={{0,2},{2,0},{4,6},{6,4},{8,10},{10,8},{12,14},{14,12},{1,3},{3,1},... | collective-permute-start | bytes 98312 | tf_op jit(solution)/shard_map/ppermute | solution.py:27
  2.9 0.8 reshape.344
  3.8 0.8 reshape.343
  4.6 0.7 multiply_exponential_fusion.1
  5.4 0.7 compare_convert_fusion.valid_ref
  6.6 0.9 %maximum_select_fusion.1 = bf16[2,2,4,2048]{3,2,1,0:T(4,128)(2,1)S(1)} fusion(bf16[1,2,4,2048]{3,2,1,0:T(4,128)(2,1)S(1)} %bitcast.176, bf16[1,2,4,2048]{3,2,1,0:T(4,128)(2,1)} %bitcast.170, pred[]{:T(512)S(6)} %eq.24), kind=kLoop, calls=%fused_computation.30 | loop fusion | flops 98304 | bytes 131073 | tf_op jit(solution)/shard_map/jit(_where)/select_n | solution.py:29
  7.5 1.6 %collective-permute-start.1 = (bf16[2,2,4,2048]{3,2,1,0:T(4,128)(2,1)S(1)}, bf16[2,2,4,2048]{3,2,1,0:T(4,128)(2,1)S(1)}, u32[]{:S(2)}, u32[]{:S(2)}) collective-permute-start(bf16[2,2,4,2048]{3,2,1,0:T(4,128)(2,1)S(1)} %maximum_select_fusion.1), channel_id=1, source_target_pairs={{0,4},{2,6},{4,8},{6,10},{8,12},{10,14},{12,0},{14,2},{1,5},{3,7},... | collective-permute-start | bytes 196616 | tf_op jit(solution)/shard_map/ppermute | solution.py:33
  9.2 2.6 %collective-permute-start.2 = (bf16[2,2,4,2048]{3,2,1,0:T(4,128)(2,1)S(1)}, bf16[2,2,4,2048]{3,2,1,0:T(4,128)(2,1)S(1)}, u32[]{:S(2)}, u32[]{:S(2)}) collective-permute-start(bf16[2,2,4,2048]{3,2,1,0:T(4,128)(2,1)S(1)} %maximum_select_fusion.1), channel_id=1, source_target_pairs={{0,8},{2,10},{4,12},{6,14},{8,0},{10,2},{12,4},{14,6},{1,9},{3,11}... | collective-permute-start | bytes 196616 | tf_op jit(solution)/shard_map/ppermute | solution.py:33
  11.8 1.3 %collective-permute-start.3 = (bf16[2,2,4,2048]{3,2,1,0:T(4,128)(2,1)S(1)}, bf16[2,2,4,2048]{3,2,1,0:T(4,128)(2,1)S(1)}, u32[]{:S(2)}, u32[]{:S(2)}) collective-permute-start(bf16[2,2,4,2048]{3,2,1,0:T(4,128)(2,1)S(1)} %maximum_select_fusion.1), channel_id=1, source_target_pairs={{0,12},{2,14},{4,0},{6,2},{8,4},{10,6},{12,8},{14,10},{1,13},{3,15... | collective-permute-start | bytes 196616 | tf_op jit(solution)/shard_map/ppermute | solution.py:33
  13.1 0.9 %maximum_select_fusion = bf16[1,2,2,4,2048]{4,3,2,1,0:T(4,128)(2,1)S(1)} fusion(bf16[1,1,2,4,2048]{4,3,2,1,0:T(4,128)(2,1)S(1)} %bitcast.177, bf16[1,1,2,4,2048]{4,3,2,1,0:T(4,128)(2,1)} %bitcast.171, pred[]{:T(512)S(6)} %eq.24), kind=kLoop, calls=%fused_computation.29 | loop fusion | flops 98304 | bytes 131073 | tf_op jit(solution)/shard_map/jit(_where)/select_n | solution.py:29
  14.0 0.4 collective-permute-done.1
  14.5 2.1 %collective-permute-done.2 = bf16[2,2,4,2048]{3,2,1,0:T(4,128)(2,1)S(1)} collective-permute-done((bf16[2,2,4,2048]{3,2,1,0:T(4,128)(2,1)S(1)}, bf16[2,2,4,2048]{3,2,1,0:T(4,128)(2,1)S(1)}, u32[]{:S(2)}, u32[]{:S(2)}) %collective-permute-start.2) | collective-permute-done | bytes 65568 | tf_op jit(solution)/shard_map/ppermute | solution.py:33
  16.9 0.7 scatter_fusion
  17.8 1.6 %copy-done = bf16[2,4,128,1024]{3,2,1,0:T(8,128)(2,1)S(1)} copy-done((bf16[2,4,128,1024]{3,2,1,0:T(8,128)(2,1)S(1)}, bf16[2,4,128,1024]{3,2,1,0:T(8,128)(2,1)}, u32[]{:S(2)}) %copy-start) | copy-done | bytes 2097176
  19.4 5.4 %shard_map.91 = (f32[8,128,128]{2,1,0:T(8,128)S(1)}, f32[8,128,128]{2,1,0:T(8,128)S(1)}, f32[8,128,128]{2,1,0:T(8,128)S(1)}) custom-call(bf16[8,128,128]{2,1,0:T(8,128)(2,1)S(1)} %bitcast.162, bf16[2,1024,1024]{2,1,0:T(8,128)(2,1)} %v_ref.1, bf16[2,1024,1024]{2,1,0:T(8,128)(2,1)} %v_ref.1, bf16[2,4,128,1024]{3,2,1,0:T(8,128)(2,1)S(1)} %copy-done, ...), custom_call_target="tpu_custom_call" | custom-call | flops 603979776 | bytes 8126464 | tf_op jit(solution)/shard_map/pallas_call | solution.py:114
  24.9 0.3 slice_reduce_fusion
  25.8 0.6 collective-permute-start.4
  26.4 1.3 %collective-permute-start.5 = (f32[130,128]{1,0:T(8,128)S(1)}, f32[130,128]{1,0:T(8,128)S(1)}, u32[]{:S(2)}, u32[]{:S(2)}) collective-permute-start(f32[130,128]{1,0:T(8,128)S(1)} %get-tuple-element.16), channel_id=1, source_target_pairs={{0,4},{2,6},{4,8},{6,10},{8,12},{10,14},{12,0},{14,2},{1,5},{3,7},... | collective-permute-start | bytes 199688 | tf_op jit(solution)/shard_map/ppermute | solution.py:60
  27.7 2.9 %collective-permute-start.6 = (f32[130,128]{1,0:T(8,128)S(1)}, f32[130,128]{1,0:T(8,128)S(1)}, u32[]{:S(2)}, u32[]{:S(2)}) collective-permute-start(f32[130,128]{1,0:T(8,128)S(1)} %get-tuple-element.15), channel_id=1, source_target_pairs={{0,6},{2,8},{4,10},{6,12},{8,14},{10,0},{12,2},{14,4},{1,7},{3,9},... | collective-permute-start | bytes 199688 | tf_op jit(solution)/shard_map/ppermute | solution.py:60
  30.6 1.8 %collective-permute-start.7 = (f32[130,128]{1,0:T(8,128)S(1)}, f32[130,128]{1,0:T(8,128)S(1)}, u32[]{:S(2)}, u32[]{:S(2)}) collective-permute-start(f32[130,128]{1,0:T(8,128)S(1)} %get-tuple-element.14), channel_id=1, source_target_pairs={{0,8},{2,10},{4,12},{6,14},{8,0},{10,2},{12,4},{14,6},{1,9},{3,11}... | collective-permute-start | bytes 199688 | tf_op jit(solution)/shard_map/ppermute | solution.py:60
  32.4 1.1 %collective-permute-start.8 = (f32[130,128]{1,0:T(8,128)S(1)}, f32[130,128]{1,0:T(8,128)S(1)}, u32[]{:S(2)}, u32[]{:S(2)}) collective-permute-start(f32[130,128]{1,0:T(8,128)S(1)} %get-tuple-element.13), channel_id=1, source_target_pairs={{0,10},{2,12},{4,14},{6,0},{8,2},{10,4},{12,6},{14,8},{1,11},{3,13... | collective-permute-start | bytes 199688 | tf_op jit(solution)/shard_map/ppermute | solution.py:60
  33.6 1.2 %collective-permute-start.9 = (f32[130,128]{1,0:T(8,128)S(1)}, f32[130,128]{1,0:T(8,128)S(1)}, u32[]{:S(2)}, u32[]{:S(2)}) collective-permute-start(f32[130,128]{1,0:T(8,128)S(1)} %get-tuple-element.12), channel_id=1, source_target_pairs={{0,12},{2,14},{4,0},{6,2},{8,4},{10,6},{12,8},{14,10},{1,13},{3,15... | collective-permute-start | bytes 199688 | tf_op jit(solution)/shard_map/ppermute | solution.py:60
  34.8 1.6 %collective-permute-start.10 = (f32[130,128]{1,0:T(8,128)S(1)}, f32[130,128]{1,0:T(8,128)S(1)}, u32[]{:S(2)}, u32[]{:S(2)}) collective-permute-start(f32[130,128]{1,0:T(8,128)S(1)} %get-tuple-element.11), channel_id=1, source_target_pairs={{0,14},{2,0},{4,2},{6,4},{8,6},{10,8},{12,10},{14,12},{1,15},{3,1}... | collective-permute-start | bytes 199688 | tf_op jit(solution)/shard_map/ppermute | solution.py:60
  36.4 1.7 %collective-permute-done.6 = f32[130,128]{1,0:T(8,128)S(1)} collective-permute-done((f32[130,128]{1,0:T(8,128)S(1)}, f32[130,128]{1,0:T(8,128)S(1)}, u32[]{:S(2)}, u32[]{:S(2)}) %collective-permute-start.6) | collective-permute-done | bytes 66592 | tf_op jit(solution)/shard_map/ppermute | solution.py:60
  38.5 1.2 %collective-permute-done.9 = f32[130,128]{1,0:T(8,128)S(1)} collective-permute-done((f32[130,128]{1,0:T(8,128)S(1)}, f32[130,128]{1,0:T(8,128)S(1)}, u32[]{:S(2)}, u32[]{:S(2)}) %collective-permute-start.9) | collective-permute-done | bytes 66592 | tf_op jit(solution)/shard_map/ppermute | solution.py:60
  40.9 1.9 %all_gather.3 = bf16[2,8,2048]{2,0,1:T(2,128)(2,1)S(1)} all-gather(bf16[2,4,2048]{2,0,1:T(2,128)(2,1)S(1)} %copy.98), channel_id=1, replica_groups=mesh['rep'=2,'tp'=8,'sub'=2] {'sub'}, dimensions={1}, use_global_device_ids=true | all-gather | bytes 98304 | tf_op jit(solution)/shard_map/all_gather | solution.py:207
  42.8 12.9 %fusion.1 = f32[16,8192]{1,0:T(8,128)S(1)} fusion(f32[8192]{0:T(1024)S(1)} %dynamic_slice.61, bf16[16,128,8192]{2,1,0:T(8,128)(2,1)} %bitcast.196, bf16[16,16,128]{2,1,0:T(8,128)(2,1)S(1)} %bitcast.187), kind=kOutput, calls=%fused_computation.4 | convolution fusion | flops 543031296 | bytes 34177024 | tf_op jit(solution)/shard_map/rhd,hdf->rhf/dot_general | solution.py:216
  56.1 0.5 constant_dynamic-slice_fusion.8
  56.6 2.2 %collective-permute-start.11 = (f32[16,1024]{1,0:T(8,128)S(1)}, f32[16,1024]{1,0:T(8,128)S(1)}, u32[]{:S(2)}, u32[]{:S(2)}) collective-permute-start(f32[16,1024]{1,0:T(8,128)S(1)} %bitcast.186), channel_id=1, source_target_pairs={{0,2},{2,4},{4,6},{6,8},{8,10},{10,12},{12,14},{14,0},{1,3},{3,5},... | collective-permute-start | bytes 196616 | tf_op jit(solution)/shard_map/ppermute | solution.py:60
  58.9 2.7 %collective-permute-start.12 = (f32[16,1024]{1,0:T(8,128)S(1)}, f32[16,1024]{1,0:T(8,128)S(1)}, u32[]{:S(2)}, u32[]{:S(2)}) collective-permute-start(f32[16,1024]{1,0:T(8,128)S(1)} %bitcast.185), channel_id=1, source_target_pairs={{0,4},{2,6},{4,8},{6,10},{8,12},{10,14},{12,0},{14,2},{1,5},{3,7},... | collective-permute-start | bytes 196616 | tf_op jit(solution)/shard_map/ppermute | solution.py:60
  61.6 0.6 collective-permute-start.13
  62.2 2.0 %collective-permute-start.14 = (f32[16,1024]{1,0:T(8,128)S(1)}, f32[16,1024]{1,0:T(8,128)S(1)}, u32[]{:S(2)}, u32[]{:S(2)}) collective-permute-start(f32[16,1024]{1,0:T(8,128)S(1)} %bitcast.181), channel_id=1, source_target_pairs={{0,8},{2,10},{4,12},{6,14},{8,0},{10,2},{12,4},{14,6},{1,9},{3,11}... | collective-permute-start | bytes 196616 | tf_op jit(solution)/shard_map/ppermute | solution.py:60
  64.2 2.7 %collective-permute-start.15 = (f32[16,1024]{1,0:T(8,128)S(1)}, f32[16,1024]{1,0:T(8,128)S(1)}, u32[]{:S(2)}, u32[]{:S(2)}) collective-permute-start(f32[16,1024]{1,0:T(8,128)S(1)} %bitcast.182), channel_id=1, source_target_pairs={{0,10},{2,12},{4,14},{6,0},{8,2},{10,4},{12,6},{14,8},{1,11},{3,13... | collective-permute-start | bytes 196616 | tf_op jit(solution)/shard_map/ppermute | solution.py:60
  66.9 1.5 %collective-permute-start.16 = (f32[16,1024]{1,0:T(8,128)S(1)}, f32[16,1024]{1,0:T(8,128)S(1)}, u32[]{:S(2)}, u32[]{:S(2)}) collective-permute-start(f32[16,1024]{1,0:T(8,128)S(1)} %bitcast.184), channel_id=1, source_target_pairs={{0,12},{2,14},{4,0},{6,2},{8,4},{10,6},{12,8},{14,10},{1,13},{3,15... | collective-permute-start | bytes 196616 | tf_op jit(solution)/shard_map/ppermute | solution.py:60
  68.4 1.2 %collective-permute-start.17 = (f32[16,1024]{1,0:T(8,128)S(1)}, f32[16,1024]{1,0:T(8,128)S(1)}, u32[]{:S(2)}, u32[]{:S(2)}) collective-permute-start(f32[16,1024]{1,0:T(8,128)S(1)} %bitcast.183), channel_id=1, source_target_pairs={{0,14},{2,0},{4,2},{6,4},{8,6},{10,8},{12,10},{14,12},{1,15},{3,1}... | collective-permute-start | bytes 196616 | tf_op jit(solution)/shard_map/ppermute | solution.py:60
  69.7 0.5 collective-permute-done.13
  70.1 1.0 %collective-permute-done.14 = f32[16,1024]{1,0:T(8,128)S(1)} collective-permute-done((f32[16,1024]{1,0:T(8,128)S(1)}, f32[16,1024]{1,0:T(8,128)S(1)}, u32[]{:S(2)}, u32[]{:S(2)}) %collective-permute-start.14) | collective-permute-done | bytes 65568 | tf_op jit(solution)/shard_map/ppermute | solution.py:60
  71.2 0.8 collective-permute-done.15
  72.0 0.9 %collective-permute-done.16 = f32[16,1024]{1,0:T(8,128)S(1)} collective-permute-done((f32[16,1024]{1,0:T(8,128)S(1)}, f32[16,1024]{1,0:T(8,128)S(1)}, u32[]{:S(2)}, u32[]{:S(2)}) %collective-permute-start.16) | collective-permute-done | bytes 65568 | tf_op jit(solution)/shard_map/ppermute | solution.py:60
  72.9 2.2 %collective-permute-start.18 = (bf16[16,1024]{1,0:T(8,128)(2,1)S(1)}, bf16[16,1024]{1,0:T(8,128)(2,1)S(1)}, u32[]{:S(2)}, u32[]{:S(2)}) collective-permute-start(bf16[16,1024]{1,0:T(8,128)(2,1)S(1)} %clamp_convert_fusion), channel_id=1, source_target_pairs={{0,2},{2,0},{4,6},{6,4},{8,10},{10,8},{12,14},{14,12},{1,3},{3,1},... | collective-permute-start | bytes 98312 | tf_op jit(solution)/shard_map/ppermute | solution.py:27
  75.2 1.9 %collective-permute-done.18 = bf16[16,1024]{1,0:T(8,128)(2,1)S(1)} collective-permute-done((bf16[16,1024]{1,0:T(8,128)(2,1)S(1)}, bf16[16,1024]{1,0:T(8,128)(2,1)S(1)}, u32[]{:S(2)}, u32[]{:S(2)}) %collective-permute-start.18) | collective-permute-done | bytes 32800 | tf_op jit(solution)/shard_map/ppermute | solution.py:27
  77.1 2.0 %collective-permute-start.19 = (bf16[2,16,1024]{2,1,0:T(8,128)(2,1)S(1)}, bf16[2,16,1024]{2,1,0:T(8,128)(2,1)S(1)}, u32[]{:S(2)}, u32[]{:S(2)}) collective-permute-start(bf16[2,16,1024]{2,1,0:T(8,128)(2,1)S(1)} %maximum_select_fusion.3), channel_id=1, source_target_pairs={{0,4},{2,6},{4,8},{6,10},{8,12},{10,14},{12,0},{14,2},{1,5},{3,7},... | collective-permute-start | bytes 196616 | tf_op jit(solution)/shard_map/ppermute | solution.py:33
  79.0 1.5 %collective-permute-start.20 = (bf16[2,16,1024]{2,1,0:T(8,128)(2,1)S(1)}, bf16[2,16,1024]{2,1,0:T(8,128)(2,1)S(1)}, u32[]{:S(2)}, u32[]{:S(2)}) collective-permute-start(bf16[2,16,1024]{2,1,0:T(8,128)(2,1)S(1)} %maximum_select_fusion.3), channel_id=1, source_target_pairs={{0,8},{2,10},{4,12},{6,14},{8,0},{10,2},{12,4},{14,6},{1,9},{3,11}... | collective-permute-start | bytes 196616 | tf_op jit(solution)/shard_map/ppermute | solution.py:33
  80.5 0.9 %collective-permute-start.21 = (bf16[2,16,1024]{2,1,0:T(8,128)(2,1)S(1)}, bf16[2,16,1024]{2,1,0:T(8,128)(2,1)S(1)}, u32[]{:S(2)}, u32[]{:S(2)}) collective-permute-start(bf16[2,16,1024]{2,1,0:T(8,128)(2,1)S(1)} %maximum_select_fusion.3), channel_id=1, source_target_pairs={{0,12},{2,14},{4,0},{6,2},{8,4},{10,6},{12,8},{14,10},{1,13},{3,15... | collective-permute-start | bytes 196616 | tf_op jit(solution)/shard_map/ppermute | solution.py:33
  81.5 2.1 %collective-permute-done.19 = bf16[2,16,1024]{2,1,0:T(8,128)(2,1)S(1)} collective-permute-done((bf16[2,16,1024]{2,1,0:T(8,128)(2,1)S(1)}, bf16[2,16,1024]{2,1,0:T(8,128)(2,1)S(1)}, u32[]{:S(2)}, u32[]{:S(2)}) %collective-permute-start.19) | collective-permute-done | bytes 65568 | tf_op jit(solution)/shard_map/ppermute | solution.py:33
  83.6 1.5 %collective-permute-done.20 = bf16[2,16,1024]{2,1,0:T(8,128)(2,1)S(1)} collective-permute-done((bf16[2,16,1024]{2,1,0:T(8,128)(2,1)S(1)}, bf16[2,16,1024]{2,1,0:T(8,128)(2,1)S(1)}, u32[]{:S(2)}, u32[]{:S(2)}) %collective-permute-start.20) | collective-permute-done | bytes 65568 | tf_op jit(solution)/shard_map/ppermute | solution.py:33
  85.5 0.7 scatter_fusion.1
  86.7 0.8 add_convert_fusion
  (88 shorter events, 4.7 us)
Async XLA Ops:
  0.0 6.6 %collective-permute-start = (bf16[2,4,2048]{2,1,0:T(4,128)(2,1)}, bf16[2,4,2048]{2,1,0:T(4,128)(2,1)S(1)}, u32[]{:S(2)}, u32[]{:S(2)}) collective-permute-start(bf16[2,4,2048]{2,1,0:T(4,128)(2,1)} %param.9), channel_id=1, source_target_pairs={{0,2},{2,0},{4,6},{6,4},{8,10},{10,8},{12,14},{14,12},{1,3},{3,1},... | collective-permute-start | bytes 98312 | tf_op jit(solution)/shard_map/ppermute | solution.py:27
  7.5 6.9 %collective-permute-start.1 = (bf16[2,2,4,2048]{3,2,1,0:T(4,128)(2,1)S(1)}, bf16[2,2,4,2048]{3,2,1,0:T(4,128)(2,1)S(1)}, u32[]{:S(2)}, u32[]{:S(2)}) collective-permute-start(bf16[2,2,4,2048]{3,2,1,0:T(4,128)(2,1)S(1)} %maximum_select_fusion.1), channel_id=1, source_target_pairs={{0,4},{2,6},{4,8},{6,10},{8,12},{10,14},{12,0},{14,2},{1,5},{3,7},... | collective-permute-start | bytes 196616 | tf_op jit(solution)/shard_map/ppermute | solution.py:33
  9.2 7.3 %collective-permute-start.2 = (bf16[2,2,4,2048]{3,2,1,0:T(4,128)(2,1)S(1)}, bf16[2,2,4,2048]{3,2,1,0:T(4,128)(2,1)S(1)}, u32[]{:S(2)}, u32[]{:S(2)}) collective-permute-start(bf16[2,2,4,2048]{3,2,1,0:T(4,128)(2,1)S(1)} %maximum_select_fusion.1), channel_id=1, source_target_pairs={{0,8},{2,10},{4,12},{6,14},{8,0},{10,2},{12,4},{14,6},{1,9},{3,11}... | collective-permute-start | bytes 196616 | tf_op jit(solution)/shard_map/ppermute | solution.py:33
  11.8 4.8 %collective-permute-start.3 = (bf16[2,2,4,2048]{3,2,1,0:T(4,128)(2,1)S(1)}, bf16[2,2,4,2048]{3,2,1,0:T(4,128)(2,1)S(1)}, u32[]{:S(2)}, u32[]{:S(2)}) collective-permute-start(bf16[2,2,4,2048]{3,2,1,0:T(4,128)(2,1)S(1)} %maximum_select_fusion.1), channel_id=1, source_target_pairs={{0,12},{2,14},{4,0},{6,2},{8,4},{10,6},{12,8},{14,10},{1,13},{3,15... | collective-permute-start | bytes 196616 | tf_op jit(solution)/shard_map/ppermute | solution.py:33
  17.8 1.6 %copy-start = (bf16[2,4,128,1024]{3,2,1,0:T(8,128)(2,1)S(1)}, bf16[2,4,128,1024]{3,2,1,0:T(8,128)(2,1)}, u32[]{:S(2)}) copy-start(bf16[2,4,128,1024]{3,2,1,0:T(8,128)(2,1)} %tv_ref.1) | copy-start | bytes 6291460
  25.8 7.9 %collective-permute-start.4 = (f32[130,128]{1,0:T(8,128)S(1)}, f32[130,128]{1,0:T(8,128)S(1)}, u32[]{:S(2)}, u32[]{:S(2)}) collective-permute-start(f32[130,128]{1,0:T(8,128)S(1)} %get-tuple-element.17), channel_id=1, source_target_pairs={{0,2},{2,4},{4,6},{6,8},{8,10},{10,12},{12,14},{14,0},{1,3},{3,5},... | collective-permute-start | bytes 199688 | tf_op jit(solution)/shard_map/ppermute | solution.py:60
  26.4 8.4 %collective-permute-start.5 = (f32[130,128]{1,0:T(8,128)S(1)}, f32[130,128]{1,0:T(8,128)S(1)}, u32[]{:S(2)}, u32[]{:S(2)}) collective-permute-start(f32[130,128]{1,0:T(8,128)S(1)} %get-tuple-element.16), channel_id=1, source_target_pairs={{0,4},{2,6},{4,8},{6,10},{8,12},{10,14},{12,0},{14,2},{1,5},{3,7},... | collective-permute-start | bytes 199688 | tf_op jit(solution)/shard_map/ppermute | solution.py:60
  27.7 10.4 %collective-permute-start.6 = (f32[130,128]{1,0:T(8,128)S(1)}, f32[130,128]{1,0:T(8,128)S(1)}, u32[]{:S(2)}, u32[]{:S(2)}) collective-permute-start(f32[130,128]{1,0:T(8,128)S(1)} %get-tuple-element.15), channel_id=1, source_target_pairs={{0,6},{2,8},{4,10},{6,12},{8,14},{10,0},{12,2},{14,4},{1,7},{3,9},... | collective-permute-start | bytes 199688 | tf_op jit(solution)/shard_map/ppermute | solution.py:60
  30.6 7.5 %collective-permute-start.7 = (f32[130,128]{1,0:T(8,128)S(1)}, f32[130,128]{1,0:T(8,128)S(1)}, u32[]{:S(2)}, u32[]{:S(2)}) collective-permute-start(f32[130,128]{1,0:T(8,128)S(1)} %get-tuple-element.14), channel_id=1, source_target_pairs={{0,8},{2,10},{4,12},{6,14},{8,0},{10,2},{12,4},{14,6},{1,9},{3,11}... | collective-permute-start | bytes 199688 | tf_op jit(solution)/shard_map/ppermute | solution.py:60
  32.4 6.0 %collective-permute-start.8 = (f32[130,128]{1,0:T(8,128)S(1)}, f32[130,128]{1,0:T(8,128)S(1)}, u32[]{:S(2)}, u32[]{:S(2)}) collective-permute-start(f32[130,128]{1,0:T(8,128)S(1)} %get-tuple-element.13), channel_id=1, source_target_pairs={{0,10},{2,12},{4,14},{6,0},{8,2},{10,4},{12,6},{14,8},{1,11},{3,13... | collective-permute-start | bytes 199688 | tf_op jit(solution)/shard_map/ppermute | solution.py:60
  33.6 6.0 %collective-permute-start.9 = (f32[130,128]{1,0:T(8,128)S(1)}, f32[130,128]{1,0:T(8,128)S(1)}, u32[]{:S(2)}, u32[]{:S(2)}) collective-permute-start(f32[130,128]{1,0:T(8,128)S(1)} %get-tuple-element.12), channel_id=1, source_target_pairs={{0,12},{2,14},{4,0},{6,2},{8,4},{10,6},{12,8},{14,10},{1,13},{3,15... | collective-permute-start | bytes 199688 | tf_op jit(solution)/shard_map/ppermute | solution.py:60
  34.8 4.9 %collective-permute-start.10 = (f32[130,128]{1,0:T(8,128)S(1)}, f32[130,128]{1,0:T(8,128)S(1)}, u32[]{:S(2)}, u32[]{:S(2)}) collective-permute-start(f32[130,128]{1,0:T(8,128)S(1)} %get-tuple-element.11), channel_id=1, source_target_pairs={{0,14},{2,0},{4,2},{6,4},{8,6},{10,8},{12,10},{14,12},{1,15},{3,1}... | collective-permute-start | bytes 199688 | tf_op jit(solution)/shard_map/ppermute | solution.py:60
  42.8 18.8 %copy-start.2 = (s32[128]{0:T(128)S(1)}, s32[128]{0:T(128)}, u32[]{:S(2)}) copy-start(s32[128]{0:T(128)} %param.16) | copy-start | bytes 1540
  55.7 31.0 %copy-start.1 = (bf16[2,8,8192]{2,1,0:T(8,128)(2,1)S(1)}, bf16[2,8,8192]{2,1,0:T(8,128)(2,1)}, u32[]{:S(2)}) copy-start(bf16[2,8,8192]{2,1,0:T(8,128)(2,1)} %param.17) | copy-start | bytes 786436
  56.6 10.3 %collective-permute-start.11 = (f32[16,1024]{1,0:T(8,128)S(1)}, f32[16,1024]{1,0:T(8,128)S(1)}, u32[]{:S(2)}, u32[]{:S(2)}) collective-permute-start(f32[16,1024]{1,0:T(8,128)S(1)} %bitcast.186), channel_id=1, source_target_pairs={{0,2},{2,4},{4,6},{6,8},{8,10},{10,12},{12,14},{14,0},{1,3},{3,5},... | collective-permute-start | bytes 196616 | tf_op jit(solution)/shard_map/ppermute | solution.py:60
  58.9 9.5 %collective-permute-start.12 = (f32[16,1024]{1,0:T(8,128)S(1)}, f32[16,1024]{1,0:T(8,128)S(1)}, u32[]{:S(2)}, u32[]{:S(2)}) collective-permute-start(f32[16,1024]{1,0:T(8,128)S(1)} %bitcast.185), channel_id=1, source_target_pairs={{0,4},{2,6},{4,8},{6,10},{8,12},{10,14},{12,0},{14,2},{1,5},{3,7},... | collective-permute-start | bytes 196616 | tf_op jit(solution)/shard_map/ppermute | solution.py:60
  61.6 8.5 %collective-permute-start.13 = (f32[16,1024]{1,0:T(8,128)S(1)}, f32[16,1024]{1,0:T(8,128)S(1)}, u32[]{:S(2)}, u32[]{:S(2)}) collective-permute-start(f32[16,1024]{1,0:T(8,128)S(1)} %bitcast.180), channel_id=1, source_target_pairs={{0,6},{2,8},{4,10},{6,12},{8,14},{10,0},{12,2},{14,4},{1,7},{3,9},... | collective-permute-start | bytes 196616 | tf_op jit(solution)/shard_map/ppermute | solution.py:60
  62.2 9.0 %collective-permute-start.14 = (f32[16,1024]{1,0:T(8,128)S(1)}, f32[16,1024]{1,0:T(8,128)S(1)}, u32[]{:S(2)}, u32[]{:S(2)}) collective-permute-start(f32[16,1024]{1,0:T(8,128)S(1)} %bitcast.181), channel_id=1, source_target_pairs={{0,8},{2,10},{4,12},{6,14},{8,0},{10,2},{12,4},{14,6},{1,9},{3,11}... | collective-permute-start | bytes 196616 | tf_op jit(solution)/shard_map/ppermute | solution.py:60
  64.2 7.8 %collective-permute-start.15 = (f32[16,1024]{1,0:T(8,128)S(1)}, f32[16,1024]{1,0:T(8,128)S(1)}, u32[]{:S(2)}, u32[]{:S(2)}) collective-permute-start(f32[16,1024]{1,0:T(8,128)S(1)} %bitcast.182), channel_id=1, source_target_pairs={{0,10},{2,12},{4,14},{6,0},{8,2},{10,4},{12,6},{14,8},{1,11},{3,13... | collective-permute-start | bytes 196616 | tf_op jit(solution)/shard_map/ppermute | solution.py:60
  66.9 5.9 %collective-permute-start.16 = (f32[16,1024]{1,0:T(8,128)S(1)}, f32[16,1024]{1,0:T(8,128)S(1)}, u32[]{:S(2)}, u32[]{:S(2)}) collective-permute-start(f32[16,1024]{1,0:T(8,128)S(1)} %bitcast.184), channel_id=1, source_target_pairs={{0,12},{2,14},{4,0},{6,2},{8,4},{10,6},{12,8},{14,10},{1,13},{3,15... | collective-permute-start | bytes 196616 | tf_op jit(solution)/shard_map/ppermute | solution.py:60
  68.4 4.5 %collective-permute-start.17 = (f32[16,1024]{1,0:T(8,128)S(1)}, f32[16,1024]{1,0:T(8,128)S(1)}, u32[]{:S(2)}, u32[]{:S(2)}) collective-permute-start(f32[16,1024]{1,0:T(8,128)S(1)} %bitcast.183), channel_id=1, source_target_pairs={{0,14},{2,0},{4,2},{6,4},{8,6},{10,8},{12,10},{14,12},{1,15},{3,1}... | collective-permute-start | bytes 196616 | tf_op jit(solution)/shard_map/ppermute | solution.py:60
  72.9 4.1 %collective-permute-start.18 = (bf16[16,1024]{1,0:T(8,128)(2,1)S(1)}, bf16[16,1024]{1,0:T(8,128)(2,1)S(1)}, u32[]{:S(2)}, u32[]{:S(2)}) collective-permute-start(bf16[16,1024]{1,0:T(8,128)(2,1)S(1)} %clamp_convert_fusion), channel_id=1, source_target_pairs={{0,2},{2,0},{4,6},{6,4},{8,10},{10,8},{12,14},{14,12},{1,3},{3,1},... | collective-permute-start | bytes 98312 | tf_op jit(solution)/shard_map/ppermute | solution.py:27
  77.1 6.6 %collective-permute-start.19 = (bf16[2,16,1024]{2,1,0:T(8,128)(2,1)S(1)}, bf16[2,16,1024]{2,1,0:T(8,128)(2,1)S(1)}, u32[]{:S(2)}, u32[]{:S(2)}) collective-permute-start(bf16[2,16,1024]{2,1,0:T(8,128)(2,1)S(1)} %maximum_select_fusion.3), channel_id=1, source_target_pairs={{0,4},{2,6},{4,8},{6,10},{8,12},{10,14},{12,0},{14,2},{1,5},{3,7},... | collective-permute-start | bytes 196616 | tf_op jit(solution)/shard_map/ppermute | solution.py:33
  79.0 6.1 %collective-permute-start.20 = (bf16[2,16,1024]{2,1,0:T(8,128)(2,1)S(1)}, bf16[2,16,1024]{2,1,0:T(8,128)(2,1)S(1)}, u32[]{:S(2)}, u32[]{:S(2)}) collective-permute-start(bf16[2,16,1024]{2,1,0:T(8,128)(2,1)S(1)} %maximum_select_fusion.3), channel_id=1, source_target_pairs={{0,8},{2,10},{4,12},{6,14},{8,0},{10,2},{12,4},{14,6},{1,9},{3,11}... | collective-permute-start | bytes 196616 | tf_op jit(solution)/shard_map/ppermute | solution.py:33
  80.5 4.9 %collective-permute-start.21 = (bf16[2,16,1024]{2,1,0:T(8,128)(2,1)S(1)}, bf16[2,16,1024]{2,1,0:T(8,128)(2,1)S(1)}, u32[]{:S(2)}, u32[]{:S(2)}) collective-permute-start(bf16[2,16,1024]{2,1,0:T(8,128)(2,1)S(1)} %maximum_select_fusion.3), channel_id=1, source_target_pairs={{0,12},{2,14},{4,0},{6,2},{8,4},{10,6},{12,8},{14,10},{1,13},{3,15... | collective-permute-start | bytes 196616 | tf_op jit(solution)/shard_map/ppermute | solution.py:33

commit v8 on v7

--- a/solution.py
+++ b/solution.py
@@ -54,7 +54,7 @@
         )
     me = lax.axis_index(axis_name)
     got = [jax.tree.map(lambda b: lax.dynamic_index_in_dim(b, me, 0, keepdims=False), blocks)]
-    for k in range(1, count):
+    for k in range(count - 1, 0, -1):
         dst = (me + k) % count
         send = jax.tree.map(lambda b: lax.dynamic_index_in_dim(b, dst, 0, keepdims=False), blocks)
         got.append(lax.ppermute(send, axis_name, [(i, (i + k) % count) for i in range(count)]))

time: 87.9 us -> 88.2 us (level)
  waiting for transfers between devices: 14.9 us -> 21.8 us
  starting transfers between devices: 38.4 us -> 31.7 us
    ppermute x14, waiting for transfers between devices: 6.55 us -> 12.8 us  [_exchange(): lax.ppermute(send, axis_name, [(i, (i + k) % count) for i in range(count)])]
    ppermute x14, starting transfers between devices: 23.3 us -> 18.8 us  [_exchange(): lax.ppermute(send, axis_name, [(i, (i + k) % count) for i in range(count)])]
    ppermute x2, starting transfers between devices: 5.16 us -> 3.01 us  [_gather_blocks(): other = lax.ppermute(x, axis_name, [(i, i ^ 1) for i in range(count)])]
    ppermute x2, waiting for transfers between devices: 1.89 us -> 3.88 us  [_gather_blocks(): other = lax.ppermute(x, axis_name, [(i, i ^ 1) for i in range(count)])]
    ppermute x6, waiting for transfers between devices: 6.46 us -> 5.19 us  [_gather_blocks(): lax.ppermute(pair, axis_name, [(i, (i + 2 * d) % count) for i in range(co...]
  transfers between devices with their start and end apart: 22 -> 22, of which waited for: 14 -> 9; matrix products, arithmetic and copies ran while one was open for 5% -> 5% of each run, Pallas kernels for 0% -> 0%
where the time goes in v8:
time: 88.2 us; the launch traced here: 87.8 us
  starting transfers between devices  31.7 us (36%)
  waiting for transfers between devices  21.8 us (25%)
  matrix products  13.3 us (15%)
  local copies, waits for them, and re-layouts  7.97 us (9%)
  Pallas kernels  5.43 us (6%)
  other arithmetic  4.99 us (6%)
  blocking collectives  1.85 us (2%)
    ppermute x14, starting transfers between devices, _exchange(): lax.ppermute(send, axis_name, [(i, (i + k) % count) for i in range(count)])  18.8 us
    dot_general x1, matrix products, per_device(): jnp.einsum('rhd,hdf->rhf', head_rows_in, head_weights, preferred_element_...  12.9 us
    ppermute x14, waiting for transfers between devices, _exchange(): lax.ppermute(send, axis_name, [(i, (i + k) % count) for i in range(count)])  12.8 us
    ppermute x6, starting transfers between devices, _gather_blocks(): lax.ppermute(pair, axis_name, [(i, (i + 2 * d) % count) for i in range(co...  9.94 us
    pallas_call x1, Pallas kernels, _attend_local(): pl.pallas_call(_attend_kernel, grid=(kv_heads // per_step,), in_specs=[pl...  5.43 us
    ppermute x6, waiting for transfers between devices, _gather_blocks(): lax.ppermute(pair, axis_name, [(i, (i + 2 * d) % count) for i in range(co...  5.19 us
    ppermute x2, waiting for transfers between devices, _gather_blocks(): other = lax.ppermute(x, axis_name, [(i, i ^ 1) for i in range(count)])  3.88 us
    ppermute x2, starting transfers between devices, _gather_blocks(): other = lax.ppermute(x, axis_name, [(i, i ^ 1) for i in range(count)])  3.01 us
  transfers between devices with their start and end apart: 22, of which 9 were waited for; matrix products, arithmetic and copies ran while one was open for 5% of the time, Pallas kernels for 0%

profile of v8, /device:TPU:0, one launch (start us, length us, event | category | flops | bytes accessed | tf_op | source)
XLA Modules:
  0.0 87.8 jit_solution(13508559001748051615)
XLA Ops:
  0.0 2.9 %collective-permute-start = (bf16[2,4,2048]{2,1,0:T(4,128)(2,1)}, bf16[2,4,2048]{2,1,0:T(4,128)(2,1)S(1)}, u32[]{:S(2)}, u32[]{:S(2)}) collective-permute-start(bf16[2,4,2048]{2,1,0:T(4,128)(2,1)} %param.9), channel_id=1, source_target_pairs={{0,2},{2,0},{4,6},{6,4},{8,10},{10,8},{12,14},{14,12},{1,3},{3,1},... | collective-permute-start | bytes 98312 | tf_op jit(solution)/shard_map/ppermute | solution.py:27
  2.9 0.8 reshape.344
  3.8 0.8 reshape.343
  4.6 0.7 multiply_exponential_fusion.1
  5.4 0.7 compare_convert_fusion.valid_ref
  6.1 0.2 fusion.17
  6.6 0.9 %maximum_select_fusion.1 = bf16[2,2,4,2048]{3,2,1,0:T(4,128)(2,1)S(1)} fusion(bf16[1,2,4,2048]{3,2,1,0:T(4,128)(2,1)S(1)} %bitcast.176, bf16[1,2,4,2048]{3,2,1,0:T(4,128)(2,1)} %bitcast.170, pred[]{:T(512)S(6)} %eq.24), kind=kLoop, calls=%fused_computation.30 | loop fusion | flops 98304 | bytes 131073 | tf_op jit(solution)/shard_map/jit(_where)/select_n | solution.py:29
  7.5 1.6 %collective-permute-start.1 = (bf16[2,2,4,2048]{3,2,1,0:T(4,128)(2,1)S(1)}, bf16[2,2,4,2048]{3,2,1,0:T(4,128)(2,1)S(1)}, u32[]{:S(2)}, u32[]{:S(2)}) collective-permute-start(bf16[2,2,4,2048]{3,2,1,0:T(4,128)(2,1)S(1)} %maximum_select_fusion.1), channel_id=1, source_target_pairs={{0,4},{2,6},{4,8},{6,10},{8,12},{10,14},{12,0},{14,2},{1,5},{3,7},... | collective-permute-start | bytes 196616 | tf_op jit(solution)/shard_map/ppermute | solution.py:33
  9.2 2.6 %collective-permute-start.2 = (bf16[2,2,4,2048]{3,2,1,0:T(4,128)(2,1)S(1)}, bf16[2,2,4,2048]{3,2,1,0:T(4,128)(2,1)S(1)}, u32[]{:S(2)}, u32[]{:S(2)}) collective-permute-start(bf16[2,2,4,2048]{3,2,1,0:T(4,128)(2,1)S(1)} %maximum_select_fusion.1), channel_id=1, source_target_pairs={{0,8},{2,10},{4,12},{6,14},{8,0},{10,2},{12,4},{14,6},{1,9},{3,11}... | collective-permute-start | bytes 196616 | tf_op jit(solution)/shard_map/ppermute | solution.py:33
  11.8 1.3 %collective-permute-start.3 = (bf16[2,2,4,2048]{3,2,1,0:T(4,128)(2,1)S(1)}, bf16[2,2,4,2048]{3,2,1,0:T(4,128)(2,1)S(1)}, u32[]{:S(2)}, u32[]{:S(2)}) collective-permute-start(bf16[2,2,4,2048]{3,2,1,0:T(4,128)(2,1)S(1)} %maximum_select_fusion.1), channel_id=1, source_target_pairs={{0,12},{2,14},{4,0},{6,2},{8,4},{10,6},{12,8},{14,10},{1,13},{3,15... | collective-permute-start | bytes 196616 | tf_op jit(solution)/shard_map/ppermute | solution.py:33
  13.1 0.9 %maximum_select_fusion = bf16[1,2,2,4,2048]{4,3,2,1,0:T(4,128)(2,1)S(1)} fusion(bf16[1,1,2,4,2048]{4,3,2,1,0:T(4,128)(2,1)S(1)} %bitcast.177, bf16[1,1,2,4,2048]{4,3,2,1,0:T(4,128)(2,1)} %bitcast.171, pred[]{:T(512)S(6)} %eq.24), kind=kLoop, calls=%fused_computation.29 | loop fusion | flops 98304 | bytes 131073 | tf_op jit(solution)/shard_map/jit(_where)/select_n | solution.py:29
  14.0 0.4 collective-permute-done.1
  14.5 2.1 %collective-permute-done.2 = bf16[2,2,4,2048]{3,2,1,0:T(4,128)(2,1)S(1)} collective-permute-done((bf16[2,2,4,2048]{3,2,1,0:T(4,128)(2,1)S(1)}, bf16[2,2,4,2048]{3,2,1,0:T(4,128)(2,1)S(1)}, u32[]{:S(2)}, u32[]{:S(2)}) %collective-permute-start.2) | collective-permute-done | bytes 65568 | tf_op jit(solution)/shard_map/ppermute | solution.py:33
  16.5 0.2 pad_maximum_fusion.1
  16.9 0.7 scatter_fusion
  17.6 0.2 reshape.369
  17.8 1.6 %copy-done = bf16[2,4,128,1024]{3,2,1,0:T(8,128)(2,1)S(1)} copy-done((bf16[2,4,128,1024]{3,2,1,0:T(8,128)(2,1)S(1)}, bf16[2,4,128,1024]{3,2,1,0:T(8,128)(2,1)}, u32[]{:S(2)}) %copy-start) | copy-done | bytes 2097176
  19.4 5.4 %shard_map.91 = (f32[8,128,128]{2,1,0:T(8,128)S(1)}, f32[8,128,128]{2,1,0:T(8,128)S(1)}, f32[8,128,128]{2,1,0:T(8,128)S(1)}) custom-call(bf16[8,128,128]{2,1,0:T(8,128)(2,1)S(1)} %bitcast.162, bf16[2,1024,1024]{2,1,0:T(8,128)(2,1)} %v_ref.1, bf16[2,1024,1024]{2,1,0:T(8,128)(2,1)} %v_ref.1, bf16[2,4,128,1024]{3,2,1,0:T(8,128)(2,1)S(1)} %copy-done, ...), custom_call_target="tpu_custom_call" | custom-call | flops 603979776 | bytes 8126464 | tf_op jit(solution)/shard_map/pallas_call | solution.py:114
  24.9 0.3 slice_reduce_fusion
  25.8 2.7 %collective-permute-start.4 = (f32[130,128]{1,0:T(8,128)S(1)}, f32[130,128]{1,0:T(8,128)S(1)}, u32[]{:S(2)}, u32[]{:S(2)}) collective-permute-start(f32[130,128]{1,0:T(8,128)S(1)} %get-tuple-element.17), channel_id=1, source_target_pairs={{0,14},{2,0},{4,2},{6,4},{8,6},{10,8},{12,10},{14,12},{1,15},{3,1}... | collective-permute-start | bytes 199688 | tf_op jit(solution)/shard_map/ppermute | solution.py:60
  28.6 1.5 %collective-permute-start.6 = (f32[130,128]{1,0:T(8,128)S(1)}, f32[130,128]{1,0:T(8,128)S(1)}, u32[]{:S(2)}, u32[]{:S(2)}) collective-permute-start(f32[130,128]{1,0:T(8,128)S(1)} %get-tuple-element.15), channel_id=1, source_target_pairs={{0,10},{2,12},{4,14},{6,0},{8,2},{10,4},{12,6},{14,8},{1,11},{3,13... | collective-permute-start | bytes 199688 | tf_op jit(solution)/shard_map/ppermute | solution.py:60
  30.1 2.9 %collective-permute-start.7 = (f32[130,128]{1,0:T(8,128)S(1)}, f32[130,128]{1,0:T(8,128)S(1)}, u32[]{:S(2)}, u32[]{:S(2)}) collective-permute-start(f32[130,128]{1,0:T(8,128)S(1)} %get-tuple-element.14), channel_id=1, source_target_pairs={{0,8},{2,10},{4,12},{6,14},{8,0},{10,2},{12,4},{14,6},{1,9},{3,11}... | collective-permute-start | bytes 199688 | tf_op jit(solution)/shard_map/ppermute | solution.py:60
  33.0 1.4 %collective-permute-start.9 = (f32[130,128]{1,0:T(8,128)S(1)}, f32[130,128]{1,0:T(8,128)S(1)}, u32[]{:S(2)}, u32[]{:S(2)}) collective-permute-start(f32[130,128]{1,0:T(8,128)S(1)} %get-tuple-element.12), channel_id=1, source_target_pairs={{0,4},{2,6},{4,8},{6,10},{8,12},{10,14},{12,0},{14,2},{1,5},{3,7},... | collective-permute-start | bytes 199688 | tf_op jit(solution)/shard_map/ppermute | solution.py:60
  34.5 0.7 collective-permute-start.10
  35.2 5.3 %collective-permute-done.7 = f32[130,128]{1,0:T(8,128)S(1)} collective-permute-done((f32[130,128]{1,0:T(8,128)S(1)}, f32[130,128]{1,0:T(8,128)S(1)}, u32[]{:S(2)}, u32[]{:S(2)}) %collective-permute-start.7) | collective-permute-done | bytes 66592 | tf_op jit(solution)/shard_map/ppermute | solution.py:60
  40.5 1.6 %collective-permute-done.8 = f32[130,128]{1,0:T(8,128)S(1)} collective-permute-done((f32[130,128]{1,0:T(8,128)S(1)}, f32[130,128]{1,0:T(8,128)S(1)}, u32[]{:S(2)}, u32[]{:S(2)}) %collective-permute-start.8) | collective-permute-done | bytes 66592 | tf_op jit(solution)/shard_map/ppermute | solution.py:60
  42.8 0.2 fusion.2
  43.0 0.2 fusion.19
  43.4 1.9 %all_gather.3 = bf16[2,8,2048]{2,0,1:T(2,128)(2,1)S(1)} all-gather(bf16[2,4,2048]{2,0,1:T(2,128)(2,1)S(1)} %copy.98), channel_id=1, replica_groups=mesh['rep'=2,'tp'=8,'sub'=2] {'sub'}, dimensions={1}, use_global_device_ids=true | all-gather | bytes 98304 | tf_op jit(solution)/shard_map/all_gather | solution.py:207
  45.3 12.9 %fusion.1 = f32[16,8192]{1,0:T(8,128)S(1)} fusion(f32[8192]{0:T(1024)S(1)} %dynamic_slice.61, bf16[16,128,8192]{2,1,0:T(8,128)(2,1)} %bitcast.196, bf16[16,16,128]{2,1,0:T(8,128)(2,1)S(1)} %bitcast.187), kind=kOutput, calls=%fused_computation.4 | convolution fusion | flops 543031296 | bytes 34177024 | tf_op jit(solution)/shard_map/rhd,hdf->rhf/dot_general | solution.py:216
  58.2 0.3 copy.119
  58.5 0.5 constant_dynamic-slice_fusion.8
  59.1 2.1 %collective-permute-start.12 = (f32[16,1024]{1,0:T(8,128)S(1)}, f32[16,1024]{1,0:T(8,128)S(1)}, u32[]{:S(2)}, u32[]{:S(2)}) collective-permute-start(f32[16,1024]{1,0:T(8,128)S(1)} %bitcast.185), channel_id=1, source_target_pairs={{0,12},{2,14},{4,0},{6,2},{8,4},{10,6},{12,8},{14,10},{1,13},{3,15... | collective-permute-start | bytes 196616 | tf_op jit(solution)/shard_map/ppermute | solution.py:60
  61.3 1.5 %collective-permute-start.13 = (f32[16,1024]{1,0:T(8,128)S(1)}, f32[16,1024]{1,0:T(8,128)S(1)}, u32[]{:S(2)}, u32[]{:S(2)}) collective-permute-start(f32[16,1024]{1,0:T(8,128)S(1)} %bitcast.180), channel_id=1, source_target_pairs={{0,10},{2,12},{4,14},{6,0},{8,2},{10,4},{12,6},{14,8},{1,11},{3,13... | collective-permute-start | bytes 196616 | tf_op jit(solution)/shard_map/ppermute | solution.py:60
  62.7 1.4 %collective-permute-start.14 = (f32[16,1024]{1,0:T(8,128)S(1)}, f32[16,1024]{1,0:T(8,128)S(1)}, u32[]{:S(2)}, u32[]{:S(2)}) collective-permute-start(f32[16,1024]{1,0:T(8,128)S(1)} %bitcast.181), channel_id=1, source_target_pairs={{0,8},{2,10},{4,12},{6,14},{8,0},{10,2},{12,4},{14,6},{1,9},{3,11}... | collective-permute-start | bytes 196616 | tf_op jit(solution)/shard_map/ppermute | solution.py:60
  64.1 0.3 collective-permute-start.15
  64.5 2.2 %collective-permute-start.16 = (f32[16,1024]{1,0:T(8,128)S(1)}, f32[16,1024]{1,0:T(8,128)S(1)}, u32[]{:S(2)}, u32[]{:S(2)}) collective-permute-start(f32[16,1024]{1,0:T(8,128)S(1)} %bitcast.184), channel_id=1, source_target_pairs={{0,4},{2,6},{4,8},{6,10},{8,12},{10,14},{12,0},{14,2},{1,5},{3,7},... | collective-permute-start | bytes 196616 | tf_op jit(solution)/shard_map/ppermute | solution.py:60
  66.7 2.0 %collective-permute-start.17 = (f32[16,1024]{1,0:T(8,128)S(1)}, f32[16,1024]{1,0:T(8,128)S(1)}, u32[]{:S(2)}, u32[]{:S(2)}) collective-permute-start(f32[16,1024]{1,0:T(8,128)S(1)} %bitcast.183), channel_id=1, source_target_pairs={{0,2},{2,4},{4,6},{6,8},{8,10},{10,12},{12,14},{14,0},{1,3},{3,5},... | collective-permute-start | bytes 196616 | tf_op jit(solution)/shard_map/ppermute | solution.py:60
  68.8 4.2 %collective-permute-done.14 = f32[16,1024]{1,0:T(8,128)S(1)} collective-permute-done((f32[16,1024]{1,0:T(8,128)S(1)}, f32[16,1024]{1,0:T(8,128)S(1)}, u32[]{:S(2)}, u32[]{:S(2)}) %collective-permute-start.14) | collective-permute-done | bytes 65568 | tf_op jit(solution)/shard_map/ppermute | solution.py:60
  73.0 1.6 %collective-permute-done.15 = f32[16,1024]{1,0:T(8,128)S(1)} collective-permute-done((f32[16,1024]{1,0:T(8,128)S(1)}, f32[16,1024]{1,0:T(8,128)S(1)}, u32[]{:S(2)}, u32[]{:S(2)}) %collective-permute-start.15) | collective-permute-done | bytes 65568 | tf_op jit(solution)/shard_map/ppermute | solution.py:60
  74.8 3.9 %collective-permute-done.18 = bf16[16,1024]{1,0:T(8,128)(2,1)S(1)} collective-permute-done((bf16[16,1024]{1,0:T(8,128)(2,1)S(1)}, bf16[16,1024]{1,0:T(8,128)(2,1)S(1)}, u32[]{:S(2)}, u32[]{:S(2)}) %collective-permute-start.18) | collective-permute-done | bytes 32800 | tf_op jit(solution)/shard_map/ppermute | solution.py:27
  78.8 1.8 %collective-permute-start.20 = (bf16[2,16,1024]{2,1,0:T(8,128)(2,1)S(1)}, bf16[2,16,1024]{2,1,0:T(8,128)(2,1)S(1)}, u32[]{:S(2)}, u32[]{:S(2)}) collective-permute-start(bf16[2,16,1024]{2,1,0:T(8,128)(2,1)S(1)} %maximum_select_fusion.3), channel_id=1, source_target_pairs={{0,8},{2,10},{4,12},{6,14},{8,0},{10,2},{12,4},{14,6},{1,9},{3,11}... | collective-permute-start | bytes 196616 | tf_op jit(solution)/shard_map/ppermute | solution.py:33
  80.6 2.5 %collective-permute-start.21 = (bf16[2,16,1024]{2,1,0:T(8,128)(2,1)S(1)}, bf16[2,16,1024]{2,1,0:T(8,128)(2,1)S(1)}, u32[]{:S(2)}, u32[]{:S(2)}) collective-permute-start(bf16[2,16,1024]{2,1,0:T(8,128)(2,1)S(1)} %maximum_select_fusion.3), channel_id=1, source_target_pairs={{0,12},{2,14},{4,0},{6,2},{8,4},{10,6},{12,8},{14,10},{1,13},{3,15... | collective-permute-start | bytes 196616 | tf_op jit(solution)/shard_map/ppermute | solution.py:33
  83.1 1.8 %collective-permute-done.19 = bf16[2,16,1024]{2,1,0:T(8,128)(2,1)S(1)} collective-permute-done((bf16[2,16,1024]{2,1,0:T(8,128)(2,1)S(1)}, bf16[2,16,1024]{2,1,0:T(8,128)(2,1)S(1)}, u32[]{:S(2)}, u32[]{:S(2)}) %collective-permute-start.19) | collective-permute-done | bytes 65568 | tf_op jit(solution)/shard_map/ppermute | solution.py:33
  84.9 0.8 collective-permute-done.20
  85.8 0.7 scatter_fusion.1
  86.6 0.3 copy.101
  87.0 0.8 add_convert_fusion
  (88 shorter events, 2.6 us)
Async XLA Ops:
  0.0 6.6 %collective-permute-start = (bf16[2,4,2048]{2,1,0:T(4,128)(2,1)}, bf16[2,4,2048]{2,1,0:T(4,128)(2,1)S(1)}, u32[]{:S(2)}, u32[]{:S(2)}) collective-permute-start(bf16[2,4,2048]{2,1,0:T(4,128)(2,1)} %param.9), channel_id=1, source_target_pairs={{0,2},{2,0},{4,6},{6,4},{8,10},{10,8},{12,14},{14,12},{1,3},{3,1},... | collective-permute-start | bytes 98312 | tf_op jit(solution)/shard_map/ppermute | solution.py:27
  7.5 6.9 %collective-permute-start.1 = (bf16[2,2,4,2048]{3,2,1,0:T(4,128)(2,1)S(1)}, bf16[2,2,4,2048]{3,2,1,0:T(4,128)(2,1)S(1)}, u32[]{:S(2)}, u32[]{:S(2)}) collective-permute-start(bf16[2,2,4,2048]{3,2,1,0:T(4,128)(2,1)S(1)} %maximum_select_fusion.1), channel_id=1, source_target_pairs={{0,4},{2,6},{4,8},{6,10},{8,12},{10,14},{12,0},{14,2},{1,5},{3,7},... | collective-permute-start | bytes 196616 | tf_op jit(solution)/shard_map/ppermute | solution.py:33
  9.2 7.3 %collective-permute-start.2 = (bf16[2,2,4,2048]{3,2,1,0:T(4,128)(2,1)S(1)}, bf16[2,2,4,2048]{3,2,1,0:T(4,128)(2,1)S(1)}, u32[]{:S(2)}, u32[]{:S(2)}) collective-permute-start(bf16[2,2,4,2048]{3,2,1,0:T(4,128)(2,1)S(1)} %maximum_select_fusion.1), channel_id=1, source_target_pairs={{0,8},{2,10},{4,12},{6,14},{8,0},{10,2},{12,4},{14,6},{1,9},{3,11}... | collective-permute-start | bytes 196616 | tf_op jit(solution)/shard_map/ppermute | solution.py:33
  11.8 4.8 %collective-permute-start.3 = (bf16[2,2,4,2048]{3,2,1,0:T(4,128)(2,1)S(1)}, bf16[2,2,4,2048]{3,2,1,0:T(4,128)(2,1)S(1)}, u32[]{:S(2)}, u32[]{:S(2)}) collective-permute-start(bf16[2,2,4,2048]{3,2,1,0:T(4,128)(2,1)S(1)} %maximum_select_fusion.1), channel_id=1, source_target_pairs={{0,12},{2,14},{4,0},{6,2},{8,4},{10,6},{12,8},{14,10},{1,13},{3,15... | collective-permute-start | bytes 196616 | tf_op jit(solution)/shard_map/ppermute | solution.py:33
  17.8 1.6 %copy-start = (bf16[2,4,128,1024]{3,2,1,0:T(8,128)(2,1)S(1)}, bf16[2,4,128,1024]{3,2,1,0:T(8,128)(2,1)}, u32[]{:S(2)}) copy-start(bf16[2,4,128,1024]{3,2,1,0:T(8,128)(2,1)} %tv_ref.1) | copy-start | bytes 6291460
  25.8 7.2 %collective-permute-start.4 = (f32[130,128]{1,0:T(8,128)S(1)}, f32[130,128]{1,0:T(8,128)S(1)}, u32[]{:S(2)}, u32[]{:S(2)}) collective-permute-start(f32[130,128]{1,0:T(8,128)S(1)} %get-tuple-element.17), channel_id=1, source_target_pairs={{0,14},{2,0},{4,2},{6,4},{8,6},{10,8},{12,10},{14,12},{1,15},{3,1}... | collective-permute-start | bytes 199688 | tf_op jit(solution)/shard_map/ppermute | solution.py:60
  28.6 5.9 %collective-permute-start.5 = (f32[130,128]{1,0:T(8,128)S(1)}, f32[130,128]{1,0:T(8,128)S(1)}, u32[]{:S(2)}, u32[]{:S(2)}) collective-permute-start(f32[130,128]{1,0:T(8,128)S(1)} %get-tuple-element.16), channel_id=1, source_target_pairs={{0,12},{2,14},{4,0},{6,2},{8,4},{10,6},{12,8},{14,10},{1,13},{3,15... | collective-permute-start | bytes 199688 | tf_op jit(solution)/shard_map/ppermute | solution.py:60
  28.6 6.5 %collective-permute-start.6 = (f32[130,128]{1,0:T(8,128)S(1)}, f32[130,128]{1,0:T(8,128)S(1)}, u32[]{:S(2)}, u32[]{:S(2)}) collective-permute-start(f32[130,128]{1,0:T(8,128)S(1)} %get-tuple-element.15), channel_id=1, source_target_pairs={{0,10},{2,12},{4,14},{6,0},{8,2},{10,4},{12,6},{14,8},{1,11},{3,13... | collective-permute-start | bytes 199688 | tf_op jit(solution)/shard_map/ppermute | solution.py:60
  30.1 10.4 %collective-permute-start.7 = (f32[130,128]{1,0:T(8,128)S(1)}, f32[130,128]{1,0:T(8,128)S(1)}, u32[]{:S(2)}, u32[]{:S(2)}) collective-permute-start(f32[130,128]{1,0:T(8,128)S(1)} %get-tuple-element.14), channel_id=1, source_target_pairs={{0,8},{2,10},{4,12},{6,14},{8,0},{10,2},{12,4},{14,6},{1,9},{3,11}... | collective-permute-start | bytes 199688 | tf_op jit(solution)/shard_map/ppermute | solution.py:60
  33.0 9.1 %collective-permute-start.8 = (f32[130,128]{1,0:T(8,128)S(1)}, f32[130,128]{1,0:T(8,128)S(1)}, u32[]{:S(2)}, u32[]{:S(2)}) collective-permute-start(f32[130,128]{1,0:T(8,128)S(1)} %get-tuple-element.13), channel_id=1, source_target_pairs={{0,6},{2,8},{4,10},{6,12},{8,14},{10,0},{12,2},{14,4},{1,7},{3,9},... | collective-permute-start | bytes 199688 | tf_op jit(solution)/shard_map/ppermute | solution.py:60
  33.0 9.1 %collective-permute-start.9 = (f32[130,128]{1,0:T(8,128)S(1)}, f32[130,128]{1,0:T(8,128)S(1)}, u32[]{:S(2)}, u32[]{:S(2)}) collective-permute-start(f32[130,128]{1,0:T(8,128)S(1)} %get-tuple-element.12), channel_id=1, source_target_pairs={{0,4},{2,6},{4,8},{6,10},{8,12},{10,14},{12,0},{14,2},{1,5},{3,7},... | collective-permute-start | bytes 199688 | tf_op jit(solution)/shard_map/ppermute | solution.py:60
  34.5 7.7 %collective-permute-start.10 = (f32[130,128]{1,0:T(8,128)S(1)}, f32[130,128]{1,0:T(8,128)S(1)}, u32[]{:S(2)}, u32[]{:S(2)}) collective-permute-start(f32[130,128]{1,0:T(8,128)S(1)} %get-tuple-element.11), channel_id=1, source_target_pairs={{0,2},{2,4},{4,6},{6,8},{8,10},{10,12},{12,14},{14,0},{1,3},{3,5},... | collective-permute-start | bytes 199688 | tf_op jit(solution)/shard_map/ppermute | solution.py:60
  45.2 16.0 %copy-start.2 = (s32[128]{0:T(128)S(1)}, s32[128]{0:T(128)}, u32[]{:S(2)}) copy-start(s32[128]{0:T(128)} %param.16) | copy-start | bytes 1540
  58.2 28.8 %copy-start.1 = (bf16[2,8,8192]{2,1,0:T(8,128)(2,1)S(1)}, bf16[2,8,8192]{2,1,0:T(8,128)(2,1)}, u32[]{:S(2)}) copy-start(bf16[2,8,8192]{2,1,0:T(8,128)(2,1)} %param.17) | copy-start | bytes 786436
  59.1 5.4 %collective-permute-start.11 = (f32[16,1024]{1,0:T(8,128)S(1)}, f32[16,1024]{1,0:T(8,128)S(1)}, u32[]{:S(2)}, u32[]{:S(2)}) collective-permute-start(f32[16,1024]{1,0:T(8,128)S(1)} %bitcast.186), channel_id=1, source_target_pairs={{0,14},{2,0},{4,2},{6,4},{8,6},{10,8},{12,10},{14,12},{1,15},{3,1}... | collective-permute-start | bytes 196616 | tf_op jit(solution)/shard_map/ppermute | solution.py:60
  59.1 7.5 %collective-permute-start.12 = (f32[16,1024]{1,0:T(8,128)S(1)}, f32[16,1024]{1,0:T(8,128)S(1)}, u32[]{:S(2)}, u32[]{:S(2)}) collective-permute-start(f32[16,1024]{1,0:T(8,128)S(1)} %bitcast.185), channel_id=1, source_target_pairs={{0,12},{2,14},{4,0},{6,2},{8,4},{10,6},{12,8},{14,10},{1,13},{3,15... | collective-permute-start | bytes 196616 | tf_op jit(solution)/shard_map/ppermute | solution.py:60
  61.3 7.5 %collective-permute-start.13 = (f32[16,1024]{1,0:T(8,128)S(1)}, f32[16,1024]{1,0:T(8,128)S(1)}, u32[]{:S(2)}, u32[]{:S(2)}) collective-permute-start(f32[16,1024]{1,0:T(8,128)S(1)} %bitcast.180), channel_id=1, source_target_pairs={{0,10},{2,12},{4,14},{6,0},{8,2},{10,4},{12,6},{14,8},{1,11},{3,13... | collective-permute-start | bytes 196616 | tf_op jit(solution)/shard_map/ppermute | solution.py:60
  62.7 10.3 %collective-permute-start.14 = (f32[16,1024]{1,0:T(8,128)S(1)}, f32[16,1024]{1,0:T(8,128)S(1)}, u32[]{:S(2)}, u32[]{:S(2)}) collective-permute-start(f32[16,1024]{1,0:T(8,128)S(1)} %bitcast.181), channel_id=1, source_target_pairs={{0,8},{2,10},{4,12},{6,14},{8,0},{10,2},{12,4},{14,6},{1,9},{3,11}... | collective-permute-start | bytes 196616 | tf_op jit(solution)/shard_map/ppermute | solution.py:60
  64.1 10.5 %collective-permute-start.15 = (f32[16,1024]{1,0:T(8,128)S(1)}, f32[16,1024]{1,0:T(8,128)S(1)}, u32[]{:S(2)}, u32[]{:S(2)}) collective-permute-start(f32[16,1024]{1,0:T(8,128)S(1)} %bitcast.182), channel_id=1, source_target_pairs={{0,6},{2,8},{4,10},{6,12},{8,14},{10,0},{12,2},{14,4},{1,7},{3,9},... | collective-permute-start | bytes 196616 | tf_op jit(solution)/shard_map/ppermute | solution.py:60
  64.5 10.2 %collective-permute-start.16 = (f32[16,1024]{1,0:T(8,128)S(1)}, f32[16,1024]{1,0:T(8,128)S(1)}, u32[]{:S(2)}, u32[]{:S(2)}) collective-permute-start(f32[16,1024]{1,0:T(8,128)S(1)} %bitcast.184), channel_id=1, source_target_pairs={{0,4},{2,6},{4,8},{6,10},{8,12},{10,14},{12,0},{14,2},{1,5},{3,7},... | collective-permute-start | bytes 196616 | tf_op jit(solution)/shard_map/ppermute | solution.py:60
  66.7 8.0 %collective-permute-start.17 = (f32[16,1024]{1,0:T(8,128)S(1)}, f32[16,1024]{1,0:T(8,128)S(1)}, u32[]{:S(2)}, u32[]{:S(2)}) collective-permute-start(f32[16,1024]{1,0:T(8,128)S(1)} %bitcast.183), channel_id=1, source_target_pairs={{0,2},{2,4},{4,6},{6,8},{8,10},{10,12},{12,14},{14,0},{1,3},{3,5},... | collective-permute-start | bytes 196616 | tf_op jit(solution)/shard_map/ppermute | solution.py:60
  74.7 4.0 %collective-permute-start.18 = (bf16[16,1024]{1,0:T(8,128)(2,1)S(1)}, bf16[16,1024]{1,0:T(8,128)(2,1)S(1)}, u32[]{:S(2)}, u32[]{:S(2)}) collective-permute-start(bf16[16,1024]{1,0:T(8,128)(2,1)S(1)} %clamp_convert_fusion), channel_id=1, source_target_pairs={{0,2},{2,0},{4,6},{6,4},{8,10},{10,8},{12,14},{14,12},{1,3},{3,1},... | collective-permute-start | bytes 98312 | tf_op jit(solution)/shard_map/ppermute | solution.py:27
  78.7 6.2 %collective-permute-start.19 = (bf16[2,16,1024]{2,1,0:T(8,128)(2,1)S(1)}, bf16[2,16,1024]{2,1,0:T(8,128)(2,1)S(1)}, u32[]{:S(2)}, u32[]{:S(2)}) collective-permute-start(bf16[2,16,1024]{2,1,0:T(8,128)(2,1)S(1)} %maximum_select_fusion.3), channel_id=1, source_target_pairs={{0,4},{2,6},{4,8},{6,10},{8,12},{10,14},{12,0},{14,2},{1,5},{3,7},... | collective-permute-start | bytes 196616 | tf_op jit(solution)/shard_map/ppermute | solution.py:33
  78.8 7.0 %collective-permute-start.20 = (bf16[2,16,1024]{2,1,0:T(8,128)(2,1)S(1)}, bf16[2,16,1024]{2,1,0:T(8,128)(2,1)S(1)}, u32[]{:S(2)}, u32[]{:S(2)}) collective-permute-start(bf16[2,16,1024]{2,1,0:T(8,128)(2,1)S(1)} %maximum_select_fusion.3), channel_id=1, source_target_pairs={{0,8},{2,10},{4,12},{6,14},{8,0},{10,2},{12,4},{14,6},{1,9},{3,11}... | collective-permute-start | bytes 196616 | tf_op jit(solution)/shard_map/ppermute | solution.py:33
  80.6 5.2 %collective-permute-start.21 = (bf16[2,16,1024]{2,1,0:T(8,128)(2,1)S(1)}, bf16[2,16,1024]{2,1,0:T(8,128)(2,1)S(1)}, u32[]{:S(2)}, u32[]{:S(2)}) collective-permute-start(bf16[2,16,1024]{2,1,0:T(8,128)(2,1)S(1)} %maximum_select_fusion.3), channel_id=1, source_target_pairs={{0,12},{2,14},{4,0},{6,2},{8,4},{10,6},{12,8},{14,10},{1,13},{3,15... | collective-permute-start | bytes 196616 | tf_op jit(solution)/shard_map/ppermute | solution.py:33

commit v9 on v7

--- a/solution.py
+++ b/solution.py
@@ -169,12 +169,18 @@
     o_peak = by_owner(k_peak[..., 0].reshape(grid4)).reshape(tp_count, -1)
     o_mass = by_owner(k_mass[..., 0].reshape(grid4)).reshape(tp_count, -1)
     n_rows = steps_n * rows_dev * heads_dev
-    n_stat = -(-2 * n_rows // DH)
+    o_att = (o_numer / o_mass[..., None]).astype(jnp.bfloat16)
     stats = jnp.concatenate([o_peak, o_mass], axis=1)
-    stats = jnp.pad(stats, ((0, 0), (0, n_stat * DH - 2 * n_rows))).reshape(tp_count, n_stat, DH)
-    got = _exchange(jnp.concatenate([o_numer, stats], axis=1), "tp", tp_count)
-    got_numer = got[:, :n_rows].reshape(tp_count, steps_n, rows_dev, heads_dev, DH)
-    got_stats = got[:, n_rows:].reshape(tp_count, -1)[:, : 2 * n_rows]
+    stats_hi = stats.astype(jnp.bfloat16)
+    stats_lo = (stats - stats_hi.astype(jnp.float32)).astype(jnp.bfloat16)
+    stats = jnp.concatenate([stats_hi, stats_lo], axis=1)
+    n_stat = -(-4 * n_rows // (16 * DH)) * 16
+    stats = jnp.pad(stats, ((0, 0), (0, n_stat * DH - 4 * n_rows))).reshape(tp_count, n_stat, DH)
+    got = _exchange(jnp.concatenate([o_att, stats], axis=1), "tp", tp_count)
+    got_numer = got[:, :n_rows].astype(jnp.float32)
+    got_numer = got_numer.reshape(tp_count, steps_n, rows_dev, heads_dev, DH)
+    got_stats = got[:, n_rows:].reshape(tp_count, -1)[:, : 4 * n_rows].astype(jnp.float32)
+    got_stats = got_stats[:, : 2 * n_rows] + got_stats[:, 2 * n_rows:]
     got_stats = got_stats.reshape(tp_count, 2, steps_n, rows_dev, heads_dev)
     got_peak = got_stats[:, 0]
     got_mass = got_stats[:, 1]
@@ -198,7 +204,7 @@
     rescale = jnp.exp(got_peak - peak[None])
     f_w = jnp.exp(f_scores - peak[..., None])
     mass = (got_mass * rescale).sum(0) + f_w.sum(-1)
-    numer = (got_numer * rescale[..., None]).sum(0)
+    numer = (got_numer * (got_mass * rescale)[..., None]).sum(0)
     numer = numer + jnp.einsum(
         "sbhu,ubhd->sbhd", f_w.astype(jnp.bfloat16), f_kv[1], preferred_element_type=jnp.float32
     )

time: 87.9 us -> 89.1 us (1.014)
  waiting for transfers between devices: 14.9 us -> 16.8 us
  starting transfers between devices: 38.4 us -> 37.2 us
    ppermute x14, waiting for transfers between devices: 6.55 us -> 8.52 us  [_exchange(): lax.ppermute(send, axis_name, [(i, (i + k) % count) for i in range(count)])]
    ppermute x14, starting transfers between devices: 23.3 us -> 22 us  [_exchange(): lax.ppermute(send, axis_name, [(i, (i + k) % count) for i in range(count)])]
    unnamed x22 -> x25, local copies, waits for them, and re-layouts: 2.06 us -> 2.11 us
  transfers between devices with their start and end apart: 22 -> 22, of which waited for: 14 -> 12; matrix products, arithmetic and copies ran while one was open for 5% -> 5% of each run, Pallas kernels for 0% -> 0%
where the time goes in v9:
time: 89.1 us; the launch traced here: 88.6 us
  starting transfers between devices  37.2 us (42%)
  waiting for transfers between devices  16.8 us (19%)
  matrix products  13.3 us (15%)
  local copies, waits for them, and re-layouts  8.04 us (9%)
  Pallas kernels  5.43 us (6%)
  other arithmetic  5.25 us (6%)
  blocking collectives  1.85 us (2%)
    ppermute x14, starting transfers between devices, _exchange(): lax.ppermute(send, axis_name, [(i, (i + k) % count) for i in range(count)])  22 us
    dot_general x1, matrix products, per_device(): jnp.einsum('rhd,hdf->rhf', head_rows_in, head_weights, preferred_element_...  12.9 us
    ppermute x6, starting transfers between devices, _gather_blocks(): lax.ppermute(pair, axis_name, [(i, (i + 2 * d) % count) for i in range(co...  10 us
    ppermute x14, waiting for transfers between devices, _exchange(): lax.ppermute(send, axis_name, [(i, (i + k) % count) for i in range(count)])  8.52 us
    ppermute x6, waiting for transfers between devices, _gather_blocks(): lax.ppermute(pair, axis_name, [(i, (i + 2 * d) % count) for i in range(co...  6.4 us
    pallas_call x1, Pallas kernels, _attend_local(): pl.pallas_call(_attend_kernel, grid=(kv_heads // per_step,), in_specs=[pl...  5.43 us
    ppermute x2, starting transfers between devices, _gather_blocks(): other = lax.ppermute(x, axis_name, [(i, i ^ 1) for i in range(count)])  5.16 us
    unnamed x25, local copies, waits for them, and re-layouts  2.11 us
  transfers between devices with their start and end apart: 22, of which 12 were waited for; matrix products, arithmetic and copies ran while one was open for 5% of the time, Pallas kernels for 0%

profile of v9, /device:TPU:0, one launch (start us, length us, event | category | flops | bytes accessed | tf_op | source)
XLA Modules:
  0.0 88.6 jit_solution(14419473135758681588)
XLA Ops:
  0.0 2.9 %collective-permute-start = (bf16[2,4,2048]{2,1,0:T(4,128)(2,1)}, bf16[2,4,2048]{2,1,0:T(4,128)(2,1)S(1)}, u32[]{:S(2)}, u32[]{:S(2)}) collective-permute-start(bf16[2,4,2048]{2,1,0:T(4,128)(2,1)} %param.9), channel_id=1, source_target_pairs={{0,2},{2,0},{4,6},{6,4},{8,10},{10,8},{12,14},{14,12},{1,3},{3,1},... | collective-permute-start | bytes 98312 | tf_op jit(solution)/shard_map/ppermute | solution.py:27
  2.9 0.8 reshape.360
  3.8 0.8 reshape.359
  5.0 0.7 multiply_exponential_fusion.1
  5.7 0.7 compare_convert_fusion.valid_ref
  6.7 0.9 %maximum_select_fusion.1 = bf16[2,2,4,2048]{3,2,1,0:T(4,128)(2,1)S(1)} fusion(bf16[1,2,4,2048]{3,2,1,0:T(4,128)(2,1)S(1)} %bitcast.182, bf16[1,2,4,2048]{3,2,1,0:T(4,128)(2,1)} %bitcast.176, pred[]{:T(512)S(6)} %eq.24), kind=kLoop, calls=%fused_computation.34 | loop fusion | flops 98304 | bytes 131073 | tf_op jit(solution)/shard_map/jit(_where)/select_n | solution.py:29
  7.7 1.6 %collective-permute-start.1 = (bf16[2,2,4,2048]{3,2,1,0:T(4,128)(2,1)S(1)}, bf16[2,2,4,2048]{3,2,1,0:T(4,128)(2,1)S(1)}, u32[]{:S(2)}, u32[]{:S(2)}) collective-permute-start(bf16[2,2,4,2048]{3,2,1,0:T(4,128)(2,1)S(1)} %maximum_select_fusion.1), channel_id=1, source_target_pairs={{0,4},{2,6},{4,8},{6,10},{8,12},{10,14},{12,0},{14,2},{1,5},{3,7},... | collective-permute-start | bytes 196616 | tf_op jit(solution)/shard_map/ppermute | solution.py:33
  9.3 2.6 %collective-permute-start.2 = (bf16[2,2,4,2048]{3,2,1,0:T(4,128)(2,1)S(1)}, bf16[2,2,4,2048]{3,2,1,0:T(4,128)(2,1)S(1)}, u32[]{:S(2)}, u32[]{:S(2)}) collective-permute-start(bf16[2,2,4,2048]{3,2,1,0:T(4,128)(2,1)S(1)} %maximum_select_fusion.1), channel_id=1, source_target_pairs={{0,8},{2,10},{4,12},{6,14},{8,0},{10,2},{12,4},{14,6},{1,9},{3,11}... | collective-permute-start | bytes 196616 | tf_op jit(solution)/shard_map/ppermute | solution.py:33
  11.9 1.3 %collective-permute-start.3 = (bf16[2,2,4,2048]{3,2,1,0:T(4,128)(2,1)S(1)}, bf16[2,2,4,2048]{3,2,1,0:T(4,128)(2,1)S(1)}, u32[]{:S(2)}, u32[]{:S(2)}) collective-permute-start(bf16[2,2,4,2048]{3,2,1,0:T(4,128)(2,1)S(1)} %maximum_select_fusion.1), channel_id=1, source_target_pairs={{0,12},{2,14},{4,0},{6,2},{8,4},{10,6},{12,8},{14,10},{1,13},{3,15... | collective-permute-start | bytes 196616 | tf_op jit(solution)/shard_map/ppermute | solution.py:33
  13.2 0.9 %maximum_select_fusion = bf16[1,2,2,4,2048]{4,3,2,1,0:T(4,128)(2,1)S(1)} fusion(bf16[1,1,2,4,2048]{4,3,2,1,0:T(4,128)(2,1)S(1)} %bitcast.183, bf16[1,1,2,4,2048]{4,3,2,1,0:T(4,128)(2,1)} %bitcast.177, pred[]{:T(512)S(6)} %eq.24), kind=kLoop, calls=%fused_computation.33 | loop fusion | flops 98304 | bytes 131073 | tf_op jit(solution)/shard_map/jit(_where)/select_n | solution.py:29
  14.1 0.4 collective-permute-done.1
  14.6 2.1 %collective-permute-done.2 = bf16[2,2,4,2048]{3,2,1,0:T(4,128)(2,1)S(1)} collective-permute-done((bf16[2,2,4,2048]{3,2,1,0:T(4,128)(2,1)S(1)}, bf16[2,2,4,2048]{3,2,1,0:T(4,128)(2,1)S(1)}, u32[]{:S(2)}, u32[]{:S(2)}) %collective-permute-start.2) | collective-permute-done | bytes 65568 | tf_op jit(solution)/shard_map/ppermute | solution.py:33
  16.6 0.2 pad_maximum_fusion
  17.0 0.7 scatter_fusion
  17.9 1.6 %copy-done = bf16[2,4,128,1024]{3,2,1,0:T(8,128)(2,1)S(1)} copy-done((bf16[2,4,128,1024]{3,2,1,0:T(8,128)(2,1)S(1)}, bf16[2,4,128,1024]{3,2,1,0:T(8,128)(2,1)}, u32[]{:S(2)}) %copy-start) | copy-done | bytes 2097176
  19.5 5.4 %shard_map.91 = (f32[8,128,128]{2,1,0:T(8,128)S(1)}, f32[8,128,128]{2,1,0:T(8,128)S(1)}, f32[8,128,128]{2,1,0:T(8,128)S(1)}) custom-call(bf16[8,128,128]{2,1,0:T(8,128)(2,1)S(1)} %bitcast.167, bf16[2,1024,1024]{2,1,0:T(8,128)(2,1)} %v_ref.1, bf16[2,1024,1024]{2,1,0:T(8,128)(2,1)} %v_ref.1, bf16[2,4,128,1024]{3,2,1,0:T(8,128)(2,1)S(1)} %copy-done, ...), custom_call_target="tpu_custom_call" | custom-call | flops 603979776 | bytes 8126464 | tf_op jit(solution)/shard_map/pallas_call | solution.py:114
  25.0 0.3 slice_reduce_fusion
  26.1 0.4 collective-permute-start.4
  26.5 3.8 %collective-permute-start.8 = (bf16[144,128]{1,0:T(8,128)(2,1)S(1)}, bf16[144,128]{1,0:T(8,128)(2,1)S(1)}, u32[]{:S(2)}, u32[]{:S(2)}) collective-permute-start(bf16[144,128]{1,0:T(8,128)(2,1)S(1)} %get-tuple-element.28), channel_id=1, source_target_pairs={{0,10},{2,12},{4,14},{6,0},{8,2},{10,4},{12,6},{14,8},{1,11},{3,13... | collective-permute-start | bytes 110600 | tf_op jit(solution)/shard_map/ppermute | solution.py:60
  30.3 1.1 %collective-permute-start.5 = (bf16[144,128]{1,0:T(8,128)(2,1)S(1)}, bf16[144,128]{1,0:T(8,128)(2,1)S(1)}, u32[]{:S(2)}, u32[]{:S(2)}) collective-permute-start(bf16[144,128]{1,0:T(8,128)(2,1)S(1)} %get-tuple-element.24), channel_id=1, source_target_pairs={{0,4},{2,6},{4,8},{6,10},{8,12},{10,14},{12,0},{14,2},{1,5},{3,7},... | collective-permute-start | bytes 110600 | tf_op jit(solution)/shard_map/ppermute | solution.py:60
  31.4 3.2 %collective-permute-start.7 = (bf16[144,128]{1,0:T(8,128)(2,1)S(1)}, bf16[144,128]{1,0:T(8,128)(2,1)S(1)}, u32[]{:S(2)}, u32[]{:S(2)}) collective-permute-start(bf16[144,128]{1,0:T(8,128)(2,1)S(1)} %get-tuple-element.26), channel_id=1, source_target_pairs={{0,8},{2,10},{4,12},{6,14},{8,0},{10,2},{12,4},{14,6},{1,9},{3,11}... | collective-permute-start | bytes 110600 | tf_op jit(solution)/shard_map/ppermute | solution.py:60
  34.7 1.4 %collective-permute-done.5 = bf16[144,128]{1,0:T(8,128)(2,1)S(1)} collective-permute-done((bf16[144,128]{1,0:T(8,128)(2,1)S(1)}, bf16[144,128]{1,0:T(8,128)(2,1)S(1)}, u32[]{:S(2)}, u32[]{:S(2)}) %collective-permute-start.5) | collective-permute-done | bytes 36896 | tf_op jit(solution)/shard_map/ppermute | solution.py:60
  36.1 2.0 %collective-permute-start.10 = (bf16[144,128]{1,0:T(8,128)(2,1)S(1)}, bf16[144,128]{1,0:T(8,128)(2,1)S(1)}, u32[]{:S(2)}, u32[]{:S(2)}) collective-permute-start(bf16[144,128]{1,0:T(8,128)(2,1)S(1)} %get-tuple-element.21), channel_id=1, source_target_pairs={{0,14},{2,0},{4,2},{6,4},{8,6},{10,8},{12,10},{14,12},{1,15},{3,1}... | collective-permute-start | bytes 110600 | tf_op jit(solution)/shard_map/ppermute | solution.py:60
  38.1 0.5 collective-permute-done.9
  38.6 1.9 %collective-permute-done.10 = bf16[144,128]{1,0:T(8,128)(2,1)S(1)} collective-permute-done((bf16[144,128]{1,0:T(8,128)(2,1)S(1)}, bf16[144,128]{1,0:T(8,128)(2,1)S(1)}, u32[]{:S(2)}, u32[]{:S(2)}) %collective-permute-start.10) | collective-permute-done | bytes 36896 | tf_op jit(solution)/shard_map/ppermute | solution.py:60
  41.9 1.9 %all_gather.3 = bf16[2,8,2048]{2,0,1:T(2,128)(2,1)S(1)} all-gather(bf16[2,4,2048]{2,0,1:T(2,128)(2,1)S(1)} %copy.105), channel_id=1, replica_groups=mesh['rep'=2,'tp'=8,'sub'=2] {'sub'}, dimensions={1}, use_global_device_ids=true | all-gather | bytes 98304 | tf_op jit(solution)/shard_map/all_gather | solution.py:213
  43.8 12.9 %fusion.1 = f32[16,8192]{1,0:T(8,128)S(1)} fusion(f32[8192]{0:T(1024)S(1)} %dynamic_slice.61, bf16[16,128,8192]{2,1,0:T(8,128)(2,1)} %bitcast.201, bf16[16,16,128]{2,1,0:T(8,128)(2,1)S(1)} %bitcast.193), kind=kOutput, calls=%fused_computation.4 | convolution fusion | flops 543031296 | bytes 34177024 | tf_op jit(solution)/shard_map/rhd,hdf->rhf/dot_general | solution.py:222
  56.7 0.3 copy.127
  57.0 0.5 constant_dynamic-slice_fusion.7
  57.6 3.0 %collective-permute-start.11 = (f32[16,1024]{1,0:T(8,128)S(1)}, f32[16,1024]{1,0:T(8,128)S(1)}, u32[]{:S(2)}, u32[]{:S(2)}) collective-permute-start(f32[16,1024]{1,0:T(8,128)S(1)} %bitcast.192), channel_id=1, source_target_pairs={{0,2},{2,4},{4,6},{6,8},{8,10},{10,12},{12,14},{14,0},{1,3},{3,5},... | collective-permute-start | bytes 196616 | tf_op jit(solution)/shard_map/ppermute | solution.py:60
  60.8 3.9 %collective-permute-start.14 = (f32[16,1024]{1,0:T(8,128)S(1)}, f32[16,1024]{1,0:T(8,128)S(1)}, u32[]{:S(2)}, u32[]{:S(2)}) collective-permute-start(f32[16,1024]{1,0:T(8,128)S(1)} %bitcast.187), channel_id=1, source_target_pairs={{0,8},{2,10},{4,12},{6,14},{8,0},{10,2},{12,4},{14,6},{1,9},{3,11}... | collective-permute-start | bytes 196616 | tf_op jit(solution)/shard_map/ppermute | solution.py:60
  64.6 2.4 %collective-permute-start.15 = (f32[16,1024]{1,0:T(8,128)S(1)}, f32[16,1024]{1,0:T(8,128)S(1)}, u32[]{:S(2)}, u32[]{:S(2)}) collective-permute-start(f32[16,1024]{1,0:T(8,128)S(1)} %bitcast.188), channel_id=1, source_target_pairs={{0,10},{2,12},{4,14},{6,0},{8,2},{10,4},{12,6},{14,8},{1,11},{3,13... | collective-permute-start | bytes 196616 | tf_op jit(solution)/shard_map/ppermute | solution.py:60
  67.1 1.5 %collective-permute-start.16 = (f32[16,1024]{1,0:T(8,128)S(1)}, f32[16,1024]{1,0:T(8,128)S(1)}, u32[]{:S(2)}, u32[]{:S(2)}) collective-permute-start(f32[16,1024]{1,0:T(8,128)S(1)} %bitcast.190), channel_id=1, source_target_pairs={{0,12},{2,14},{4,0},{6,2},{8,4},{10,6},{12,8},{14,10},{1,13},{3,15... | collective-permute-start | bytes 196616 | tf_op jit(solution)/shard_map/ppermute | solution.py:60
  68.6 0.6 collective-permute-start.17
  69.3 0.4 collective-permute-done.13
  69.7 2.3 %collective-permute-done.14 = f32[16,1024]{1,0:T(8,128)S(1)} collective-permute-done((f32[16,1024]{1,0:T(8,128)S(1)}, f32[16,1024]{1,0:T(8,128)S(1)}, u32[]{:S(2)}, u32[]{:S(2)}) %collective-permute-start.14) | collective-permute-done | bytes 65568 | tf_op jit(solution)/shard_map/ppermute | solution.py:60
  72.0 0.4 collective-permute-done.15
  72.4 1.6 %collective-permute-done.16 = f32[16,1024]{1,0:T(8,128)S(1)} collective-permute-done((f32[16,1024]{1,0:T(8,128)S(1)}, f32[16,1024]{1,0:T(8,128)S(1)}, u32[]{:S(2)}, u32[]{:S(2)}) %collective-permute-start.16) | collective-permute-done | bytes 65568 | tf_op jit(solution)/shard_map/ppermute | solution.py:60
  74.1 2.2 %collective-permute-start.18 = (bf16[16,1024]{1,0:T(8,128)(2,1)S(1)}, bf16[16,1024]{1,0:T(8,128)(2,1)S(1)}, u32[]{:S(2)}, u32[]{:S(2)}) collective-permute-start(bf16[16,1024]{1,0:T(8,128)(2,1)S(1)} %clamp_convert_fusion), channel_id=1, source_target_pairs={{0,2},{2,0},{4,6},{6,4},{8,10},{10,8},{12,14},{14,12},{1,3},{3,1},... | collective-permute-start | bytes 98312 | tf_op jit(solution)/shard_map/ppermute | solution.py:27
  76.3 1.9 %collective-permute-done.18 = bf16[16,1024]{1,0:T(8,128)(2,1)S(1)} collective-permute-done((bf16[16,1024]{1,0:T(8,128)(2,1)S(1)}, bf16[16,1024]{1,0:T(8,128)(2,1)S(1)}, u32[]{:S(2)}, u32[]{:S(2)}) %collective-permute-start.18) | collective-permute-done | bytes 32800 | tf_op jit(solution)/shard_map/ppermute | solution.py:27
  78.2 2.0 %collective-permute-start.19 = (bf16[2,16,1024]{2,1,0:T(8,128)(2,1)S(1)}, bf16[2,16,1024]{2,1,0:T(8,128)(2,1)S(1)}, u32[]{:S(2)}, u32[]{:S(2)}) collective-permute-start(bf16[2,16,1024]{2,1,0:T(8,128)(2,1)S(1)} %maximum_select_fusion.3), channel_id=1, source_target_pairs={{0,4},{2,6},{4,8},{6,10},{8,12},{10,14},{12,0},{14,2},{1,5},{3,7},... | collective-permute-start | bytes 196616 | tf_op jit(solution)/shard_map/ppermute | solution.py:33
  80.2 0.5 collective-permute-start.20
  80.8 1.9 %collective-permute-start.21 = (bf16[2,16,1024]{2,1,0:T(8,128)(2,1)S(1)}, bf16[2,16,1024]{2,1,0:T(8,128)(2,1)S(1)}, u32[]{:S(2)}, u32[]{:S(2)}) collective-permute-start(bf16[2,16,1024]{2,1,0:T(8,128)(2,1)S(1)} %maximum_select_fusion.3), channel_id=1, source_target_pairs={{0,12},{2,14},{4,0},{6,2},{8,4},{10,6},{12,8},{14,10},{1,13},{3,15... | collective-permute-start | bytes 196616 | tf_op jit(solution)/shard_map/ppermute | solution.py:33
  82.7 2.3 %collective-permute-done.19 = bf16[2,16,1024]{2,1,0:T(8,128)(2,1)S(1)} collective-permute-done((bf16[2,16,1024]{2,1,0:T(8,128)(2,1)S(1)}, bf16[2,16,1024]{2,1,0:T(8,128)(2,1)S(1)}, u32[]{:S(2)}, u32[]{:S(2)}) %collective-permute-start.19) | collective-permute-done | bytes 65568 | tf_op jit(solution)/shard_map/ppermute | solution.py:33
  85.0 1.6 %collective-permute-done.20 = bf16[2,16,1024]{2,1,0:T(8,128)(2,1)S(1)} collective-permute-done((bf16[2,16,1024]{2,1,0:T(8,128)(2,1)S(1)}, bf16[2,16,1024]{2,1,0:T(8,128)(2,1)S(1)}, u32[]{:S(2)}, u32[]{:S(2)}) %collective-permute-start.20) | collective-permute-done | bytes 65568 | tf_op jit(solution)/shard_map/ppermute | solution.py:33
  86.7 0.7 scatter_fusion.1
  87.4 0.3 copy.108
  87.8 0.8 add_convert_fusion
  (97 shorter events, 3.5 us)
Async XLA Ops:
  0.0 6.7 %collective-permute-start = (bf16[2,4,2048]{2,1,0:T(4,128)(2,1)}, bf16[2,4,2048]{2,1,0:T(4,128)(2,1)S(1)}, u32[]{:S(2)}, u32[]{:S(2)}) collective-permute-start(bf16[2,4,2048]{2,1,0:T(4,128)(2,1)} %param.9), channel_id=1, source_target_pairs={{0,2},{2,0},{4,6},{6,4},{8,10},{10,8},{12,14},{14,12},{1,3},{3,1},... | collective-permute-start | bytes 98312 | tf_op jit(solution)/shard_map/ppermute | solution.py:27
  7.7 6.9 %collective-permute-start.1 = (bf16[2,2,4,2048]{3,2,1,0:T(4,128)(2,1)S(1)}, bf16[2,2,4,2048]{3,2,1,0:T(4,128)(2,1)S(1)}, u32[]{:S(2)}, u32[]{:S(2)}) collective-permute-start(bf16[2,2,4,2048]{3,2,1,0:T(4,128)(2,1)S(1)} %maximum_select_fusion.1), channel_id=1, source_target_pairs={{0,4},{2,6},{4,8},{6,10},{8,12},{10,14},{12,0},{14,2},{1,5},{3,7},... | collective-permute-start | bytes 196616 | tf_op jit(solution)/shard_map/ppermute | solution.py:33
  9.3 7.3 %collective-permute-start.2 = (bf16[2,2,4,2048]{3,2,1,0:T(4,128)(2,1)S(1)}, bf16[2,2,4,2048]{3,2,1,0:T(4,128)(2,1)S(1)}, u32[]{:S(2)}, u32[]{:S(2)}) collective-permute-start(bf16[2,2,4,2048]{3,2,1,0:T(4,128)(2,1)S(1)} %maximum_select_fusion.1), channel_id=1, source_target_pairs={{0,8},{2,10},{4,12},{6,14},{8,0},{10,2},{12,4},{14,6},{1,9},{3,11}... | collective-permute-start | bytes 196616 | tf_op jit(solution)/shard_map/ppermute | solution.py:33
  11.9 4.8 %collective-permute-start.3 = (bf16[2,2,4,2048]{3,2,1,0:T(4,128)(2,1)S(1)}, bf16[2,2,4,2048]{3,2,1,0:T(4,128)(2,1)S(1)}, u32[]{:S(2)}, u32[]{:S(2)}) collective-permute-start(bf16[2,2,4,2048]{3,2,1,0:T(4,128)(2,1)S(1)} %maximum_select_fusion.1), channel_id=1, source_target_pairs={{0,12},{2,14},{4,0},{6,2},{8,4},{10,6},{12,8},{14,10},{1,13},{3,15... | collective-permute-start | bytes 196616 | tf_op jit(solution)/shard_map/ppermute | solution.py:33
  17.9 1.6 %copy-start = (bf16[2,4,128,1024]{3,2,1,0:T(8,128)(2,1)S(1)}, bf16[2,4,128,1024]{3,2,1,0:T(8,128)(2,1)}, u32[]{:S(2)}) copy-start(bf16[2,4,128,1024]{3,2,1,0:T(8,128)(2,1)} %tv_ref.1) | copy-start | bytes 6291460
  26.1 8.6 %collective-permute-start.4 = (bf16[144,128]{1,0:T(8,128)(2,1)S(1)}, bf16[144,128]{1,0:T(8,128)(2,1)S(1)}, u32[]{:S(2)}, u32[]{:S(2)}) collective-permute-start(bf16[144,128]{1,0:T(8,128)(2,1)S(1)} %get-tuple-element.23), channel_id=1, source_target_pairs={{0,2},{2,4},{4,6},{6,8},{8,10},{10,12},{12,14},{14,0},{1,3},{3,5},... | collective-permute-start | bytes 110600 | tf_op jit(solution)/shard_map/ppermute | solution.py:60
  26.5 11.6 %collective-permute-start.8 = (bf16[144,128]{1,0:T(8,128)(2,1)S(1)}, bf16[144,128]{1,0:T(8,128)(2,1)S(1)}, u32[]{:S(2)}, u32[]{:S(2)}) collective-permute-start(bf16[144,128]{1,0:T(8,128)(2,1)S(1)} %get-tuple-element.28), channel_id=1, source_target_pairs={{0,10},{2,12},{4,14},{6,0},{8,2},{10,4},{12,6},{14,8},{1,11},{3,13... | collective-permute-start | bytes 110600 | tf_op jit(solution)/shard_map/ppermute | solution.py:60
  30.3 5.8 %collective-permute-start.5 = (bf16[144,128]{1,0:T(8,128)(2,1)S(1)}, bf16[144,128]{1,0:T(8,128)(2,1)S(1)}, u32[]{:S(2)}, u32[]{:S(2)}) collective-permute-start(bf16[144,128]{1,0:T(8,128)(2,1)S(1)} %get-tuple-element.24), channel_id=1, source_target_pairs={{0,4},{2,6},{4,8},{6,10},{8,12},{10,14},{12,0},{14,2},{1,5},{3,7},... | collective-permute-start | bytes 110600 | tf_op jit(solution)/shard_map/ppermute | solution.py:60
  31.4 6.6 %collective-permute-start.6 = (bf16[144,128]{1,0:T(8,128)(2,1)S(1)}, bf16[144,128]{1,0:T(8,128)(2,1)S(1)}, u32[]{:S(2)}, u32[]{:S(2)}) collective-permute-start(bf16[144,128]{1,0:T(8,128)(2,1)S(1)} %get-tuple-element.25), channel_id=1, source_target_pairs={{0,6},{2,8},{4,10},{6,12},{8,14},{10,0},{12,2},{14,4},{1,7},{3,9},... | collective-permute-start | bytes 110600 | tf_op jit(solution)/shard_map/ppermute | solution.py:60
  31.4 6.6 %collective-permute-start.7 = (bf16[144,128]{1,0:T(8,128)(2,1)S(1)}, bf16[144,128]{1,0:T(8,128)(2,1)S(1)}, u32[]{:S(2)}, u32[]{:S(2)}) collective-permute-start(bf16[144,128]{1,0:T(8,128)(2,1)S(1)} %get-tuple-element.26), channel_id=1, source_target_pairs={{0,8},{2,10},{4,12},{6,14},{8,0},{10,2},{12,4},{14,6},{1,9},{3,11}... | collective-permute-start | bytes 110600 | tf_op jit(solution)/shard_map/ppermute | solution.py:60
  34.7 4.0 %collective-permute-start.9 = (bf16[144,128]{1,0:T(8,128)(2,1)S(1)}, bf16[144,128]{1,0:T(8,128)(2,1)S(1)}, u32[]{:S(2)}, u32[]{:S(2)}) collective-permute-start(bf16[144,128]{1,0:T(8,128)(2,1)S(1)} %get-tuple-element.27), channel_id=1, source_target_pairs={{0,12},{2,14},{4,0},{6,2},{8,4},{10,6},{12,8},{14,10},{1,13},{3,15... | collective-permute-start | bytes 110600 | tf_op jit(solution)/shard_map/ppermute | solution.py:60
  36.1 4.5 %collective-permute-start.10 = (bf16[144,128]{1,0:T(8,128)(2,1)S(1)}, bf16[144,128]{1,0:T(8,128)(2,1)S(1)}, u32[]{:S(2)}, u32[]{:S(2)}) collective-permute-start(bf16[144,128]{1,0:T(8,128)(2,1)S(1)} %get-tuple-element.21), channel_id=1, source_target_pairs={{0,14},{2,0},{4,2},{6,4},{8,6},{10,8},{12,10},{14,12},{1,15},{3,1}... | collective-permute-start | bytes 110600 | tf_op jit(solution)/shard_map/ppermute | solution.py:60
  43.8 16.9 %copy-start.2 = (s32[128]{0:T(128)S(1)}, s32[128]{0:T(128)}, u32[]{:S(2)}) copy-start(s32[128]{0:T(128)} %param.16) | copy-start | bytes 1540
  56.7 31.2 %copy-start.1 = (bf16[2,8,8192]{2,1,0:T(8,128)(2,1)S(1)}, bf16[2,8,8192]{2,1,0:T(8,128)(2,1)}, u32[]{:S(2)}) copy-start(bf16[2,8,8192]{2,1,0:T(8,128)(2,1)} %param.17) | copy-start | bytes 786436
  57.6 9.5 %collective-permute-start.11 = (f32[16,1024]{1,0:T(8,128)S(1)}, f32[16,1024]{1,0:T(8,128)S(1)}, u32[]{:S(2)}, u32[]{:S(2)}) collective-permute-start(f32[16,1024]{1,0:T(8,128)S(1)} %bitcast.192), channel_id=1, source_target_pairs={{0,2},{2,4},{4,6},{6,8},{8,10},{10,12},{12,14},{14,0},{1,3},{3,5},... | collective-permute-start | bytes 196616 | tf_op jit(solution)/shard_map/ppermute | solution.py:60
  60.6 8.1 %collective-permute-start.12 = (f32[16,1024]{1,0:T(8,128)S(1)}, f32[16,1024]{1,0:T(8,128)S(1)}, u32[]{:S(2)}, u32[]{:S(2)}) collective-permute-start(f32[16,1024]{1,0:T(8,128)S(1)} %bitcast.191), channel_id=1, source_target_pairs={{0,4},{2,6},{4,8},{6,10},{8,12},{10,14},{12,0},{14,2},{1,5},{3,7},... | collective-permute-start | bytes 196616 | tf_op jit(solution)/shard_map/ppermute | solution.py:60
  60.7 9.1 %collective-permute-start.13 = (f32[16,1024]{1,0:T(8,128)S(1)}, f32[16,1024]{1,0:T(8,128)S(1)}, u32[]{:S(2)}, u32[]{:S(2)}) collective-permute-start(f32[16,1024]{1,0:T(8,128)S(1)} %bitcast.186), channel_id=1, source_target_pairs={{0,6},{2,8},{4,10},{6,12},{8,14},{10,0},{12,2},{14,4},{1,7},{3,9},... | collective-permute-start | bytes 196616 | tf_op jit(solution)/shard_map/ppermute | solution.py:60
  60.8 11.2 %collective-permute-start.14 = (f32[16,1024]{1,0:T(8,128)S(1)}, f32[16,1024]{1,0:T(8,128)S(1)}, u32[]{:S(2)}, u32[]{:S(2)}) collective-permute-start(f32[16,1024]{1,0:T(8,128)S(1)} %bitcast.187), channel_id=1, source_target_pairs={{0,8},{2,10},{4,12},{6,14},{8,0},{10,2},{12,4},{14,6},{1,9},{3,11}... | collective-permute-start | bytes 196616 | tf_op jit(solution)/shard_map/ppermute | solution.py:60
  64.6 7.8 %collective-permute-start.15 = (f32[16,1024]{1,0:T(8,128)S(1)}, f32[16,1024]{1,0:T(8,128)S(1)}, u32[]{:S(2)}, u32[]{:S(2)}) collective-permute-start(f32[16,1024]{1,0:T(8,128)S(1)} %bitcast.188), channel_id=1, source_target_pairs={{0,10},{2,12},{4,14},{6,0},{8,2},{10,4},{12,6},{14,8},{1,11},{3,13... | collective-permute-start | bytes 196616 | tf_op jit(solution)/shard_map/ppermute | solution.py:60
  67.1 6.9 %collective-permute-start.16 = (f32[16,1024]{1,0:T(8,128)S(1)}, f32[16,1024]{1,0:T(8,128)S(1)}, u32[]{:S(2)}, u32[]{:S(2)}) collective-permute-start(f32[16,1024]{1,0:T(8,128)S(1)} %bitcast.190), channel_id=1, source_target_pairs={{0,12},{2,14},{4,0},{6,2},{8,4},{10,6},{12,8},{14,10},{1,13},{3,15... | collective-permute-start | bytes 196616 | tf_op jit(solution)/shard_map/ppermute | solution.py:60
  68.6 5.4 %collective-permute-start.17 = (f32[16,1024]{1,0:T(8,128)S(1)}, f32[16,1024]{1,0:T(8,128)S(1)}, u32[]{:S(2)}, u32[]{:S(2)}) collective-permute-start(f32[16,1024]{1,0:T(8,128)S(1)} %bitcast.189), channel_id=1, source_target_pairs={{0,14},{2,0},{4,2},{6,4},{8,6},{10,8},{12,10},{14,12},{1,15},{3,1}... | collective-permute-start | bytes 196616 | tf_op jit(solution)/shard_map/ppermute | solution.py:60
  74.1 4.1 %collective-permute-start.18 = (bf16[16,1024]{1,0:T(8,128)(2,1)S(1)}, bf16[16,1024]{1,0:T(8,128)(2,1)S(1)}, u32[]{:S(2)}, u32[]{:S(2)}) collective-permute-start(bf16[16,1024]{1,0:T(8,128)(2,1)S(1)} %clamp_convert_fusion), channel_id=1, source_target_pairs={{0,2},{2,0},{4,6},{6,4},{8,10},{10,8},{12,14},{14,12},{1,3},{3,1},... | collective-permute-start | bytes 98312 | tf_op jit(solution)/shard_map/ppermute | solution.py:27
  78.2 6.8 %collective-permute-start.19 = (bf16[2,16,1024]{2,1,0:T(8,128)(2,1)S(1)}, bf16[2,16,1024]{2,1,0:T(8,128)(2,1)S(1)}, u32[]{:S(2)}, u32[]{:S(2)}) collective-permute-start(bf16[2,16,1024]{2,1,0:T(8,128)(2,1)S(1)} %maximum_select_fusion.3), channel_id=1, source_target_pairs={{0,4},{2,6},{4,8},{6,10},{8,12},{10,14},{12,0},{14,2},{1,5},{3,7},... | collective-permute-start | bytes 196616 | tf_op jit(solution)/shard_map/ppermute | solution.py:33
  80.2 6.4 %collective-permute-start.20 = (bf16[2,16,1024]{2,1,0:T(8,128)(2,1)S(1)}, bf16[2,16,1024]{2,1,0:T(8,128)(2,1)S(1)}, u32[]{:S(2)}, u32[]{:S(2)}) collective-permute-start(bf16[2,16,1024]{2,1,0:T(8,128)(2,1)S(1)} %maximum_select_fusion.3), channel_id=1, source_target_pairs={{0,8},{2,10},{4,12},{6,14},{8,0},{10,2},{12,4},{14,6},{1,9},{3,11}... | collective-permute-start | bytes 196616 | tf_op jit(solution)/shard_map/ppermute | solution.py:33
  80.8 5.8 %collective-permute-start.21 = (bf16[2,16,1024]{2,1,0:T(8,128)(2,1)S(1)}, bf16[2,16,1024]{2,1,0:T(8,128)(2,1)S(1)}, u32[]{:S(2)}, u32[]{:S(2)}) collective-permute-start(bf16[2,16,1024]{2,1,0:T(8,128)(2,1)S(1)} %maximum_select_fusion.3), channel_id=1, source_target_pairs={{0,12},{2,14},{4,0},{6,2},{8,4},{10,6},{12,8},{14,10},{1,13},{3,15... | collective-permute-start | bytes 196616 | tf_op jit(solution)/shard_map/ppermute | solution.py:33

commit v10 on v7

--- a/solution.py
+++ b/solution.py
@@ -1,3 +1,4 @@
+import functools
 import math
 
 import jax
@@ -137,6 +138,76 @@
     )(q_rows, prefix_kv, prefix_kv, tail_kv, tail_kv, valid)
 
 
+def _attend_packed_kernel(
+    group, q_ref, k_ref, v_ref, tk_ref, tv_ref, valid_ref, out_ref
+):
+    heads_n, rows_n = q_ref.shape[0], q_ref.shape[1]
+    samples, tail_dev = tk_ref.shape[1], tk_ref.shape[2]
+    score_scale = 1.0 / math.sqrt(DH)
+    dims_nt = (((1,), (1,)), ((), ()))
+    row_sample = (lax.broadcasted_iota(jnp.int32, (rows_n, tail_dev), 0) // group) % samples
+    for j in range(heads_n):
+        cols = slice(j * DH, (j + 1) * DH)
+        q = q_ref[j]
+        p_scores = lax.dot_general(q, k_ref[0, :, cols], dims_nt, preferred_element_type=jnp.float32)
+        p_scores = p_scores * score_scale
+        t_scores = jnp.full((rows_n, tail_dev), NEG_FILL, jnp.float32)
+        for r in range(samples):
+            sr = lax.dot_general(
+                q, tk_ref[0, r, :, cols], dims_nt, preferred_element_type=jnp.float32
+            )
+            live = (row_sample == r) & (valid_ref[r:r + 1, :] > 0.0)
+            t_scores = jnp.where(live, sr * score_scale, t_scores)
+        peak = jnp.maximum(
+            jnp.max(p_scores, axis=1, keepdims=True), jnp.max(t_scores, axis=1, keepdims=True)
+        )
+        p_w = jnp.exp(p_scores - peak)
+        t_w = jnp.exp(t_scores - peak)
+        mass = jnp.sum(p_w, axis=1, keepdims=True) + jnp.sum(t_w, axis=1, keepdims=True)
+        numer = jnp.dot(
+            p_w.astype(jnp.bfloat16), v_ref[0, :, cols], preferred_element_type=jnp.float32
+        )
+        for r in range(samples):
+            t_w16 = jnp.where(row_sample == r, t_w, 0.0).astype(jnp.bfloat16)
+            numer = numer + jnp.dot(t_w16, tv_ref[0, r, :, cols], preferred_element_type=jnp.float32)
+        out_ref[j, :rows_n, :] = numer
+        peak_row = jnp.transpose(jnp.broadcast_to(peak, (rows_n, DH)))[0:1]
+        mass_row = jnp.transpose(jnp.broadcast_to(mass, (rows_n, DH)))[0:1]
+        out_ref[j, rows_n:, :] = jnp.concatenate(
+            [peak_row, mass_row, jnp.zeros((6, DH), jnp.float32)], axis=0
+        )
+
+
+def _attend_packed(q_rows, prefix_kv, tail_kv, valid, group):
+    kv_heads, rows_n, _ = q_rows.shape
+    prefix_dev = prefix_kv.shape[1]
+    samples, tail_dev = tail_kv.shape[1], tail_kv.shape[2]
+    flops = 4 * kv_heads * rows_n * DH * (prefix_dev + samples * tail_dev)
+    bytes_in = 2 * (prefix_kv.size + tail_kv.size + q_rows.size)
+    per_step = 4 if kv_heads % 4 == 0 else 1
+    width = per_step * DH
+    return pl.pallas_call(
+        functools.partial(_attend_packed_kernel, group),
+        grid=(kv_heads // per_step,),
+        in_specs=[
+            pl.BlockSpec((per_step, rows_n, DH), lambda k: (k, 0, 0)),
+            pl.BlockSpec((1, prefix_dev, width), lambda k: (0, 0, k)),
+            pl.BlockSpec((1, prefix_dev, width), lambda k: (1, 0, k)),
+            pl.BlockSpec((1, samples, tail_dev, width), lambda k: (0, 0, 0, k)),
+            pl.BlockSpec((1, samples, tail_dev, width), lambda k: (1, 0, 0, k)),
+            pl.BlockSpec((samples, tail_dev), lambda k: (0, 0)),
+        ],
+        out_specs=pl.BlockSpec((per_step, rows_n + 8, DH), lambda k: (k, 0, 0)),
+        out_shape=jax.ShapeDtypeStruct((kv_heads, rows_n + 8, DH), jnp.float32),
+        cost_estimate=pl.CostEstimate(
+            flops=flops,
+            transcendentals=kv_heads * rows_n * (prefix_dev + tail_dev),
+            bytes_accessed=bytes_in + 4 * kv_heads * (rows_n + 8) * DH,
+        ),
+        compiler_params=pltpu.CompilerParams(vmem_limit_bytes=48 * 1024 * 1024),
+    )(q_rows, prefix_kv, prefix_kv, tail_kv, tail_kv, valid)
+
+
 def per_device(
     queries, prefix_kv, tail_kv, tail_lengths, fresh_kv, out_weight, scale_in, scale_out, residual
 ):
@@ -154,30 +225,41 @@
 
     q_blocks = _gather_blocks(queries, "tp", tp_count)
     q_all = jnp.moveaxis(q_blocks, 0, 2).reshape(steps_n, rows_dev, kv_heads, group, DH)
-    q_rows = jnp.transpose(q_all, (2, 1, 0, 3, 4)).reshape(kv_heads, -1, DH)
     t_pos = tp_rank * tail_dev + jnp.arange(tail_dev)
     valid = (t_pos[None, :] < tail_lengths[:, None]).astype(jnp.float32)
-    k_numer, k_peak, k_mass = _attend_local(q_rows, prefix_kv, tail_kv, valid)
-
-    def by_owner(x):
-        x = jnp.transpose(x, (2, 1, 0, 3) + tuple(range(4, x.ndim)))
-        x = x.reshape((steps_n, rows_dev, tp_count, heads_dev) + x.shape[4:])
-        return jnp.moveaxis(x, 2, 0)
-
-    grid4 = (kv_heads, rows_dev, steps_n, group)
-    o_numer = by_owner(k_numer.reshape(grid4 + (DH,))).reshape(tp_count, -1, DH)
-    o_peak = by_owner(k_peak[..., 0].reshape(grid4)).reshape(tp_count, -1)
-    o_mass = by_owner(k_mass[..., 0].reshape(grid4)).reshape(tp_count, -1)
     n_rows = steps_n * rows_dev * heads_dev
-    n_stat = -(-2 * n_rows // DH)
-    stats = jnp.concatenate([o_peak, o_mass], axis=1)
-    stats = jnp.pad(stats, ((0, 0), (0, n_stat * DH - 2 * n_rows))).reshape(tp_count, n_stat, DH)
-    got = _exchange(jnp.concatenate([o_numer, stats], axis=1), "tp", tp_count)
-    got_numer = got[:, :n_rows].reshape(tp_count, steps_n, rows_dev, heads_dev, DH)
-    got_stats = got[:, n_rows:].reshape(tp_count, -1)[:, : 2 * n_rows]
-    got_stats = got_stats.reshape(tp_count, 2, steps_n, rows_dev, heads_dev)
-    got_peak = got_stats[:, 0]
-    got_mass = got_stats[:, 1]
+    if tp_count == kv_heads and heads_dev == group and n_rows == DH:
+        q_rows = jnp.transpose(q_all, (2, 0, 1, 3, 4)).reshape(kv_heads, -1, DH)
+        got = _exchange(_attend_packed(q_rows, prefix_kv, tail_kv, valid, group), "tp", tp_count)
+        got_numer = got[:, :n_rows].reshape(tp_count, steps_n, rows_dev, heads_dev, DH)
+        got_peak = got[:, n_rows].reshape(tp_count, steps_n, rows_dev, heads_dev)
+        got_mass = got[:, n_rows + 1].reshape(tp_count, steps_n, rows_dev, heads_dev)
+    else:
+
+        q_rows = jnp.transpose(q_all, (2, 1, 0, 3, 4)).reshape(kv_heads, -1, DH)
+        t_pos = tp_rank * tail_dev + jnp.arange(tail_dev)
+        valid = (t_pos[None, :] < tail_lengths[:, None]).astype(jnp.float32)
+        k_numer, k_peak, k_mass = _attend_local(q_rows, prefix_kv, tail_kv, valid)
+
+        def by_owner(x):
+            x = jnp.transpose(x, (2, 1, 0, 3) + tuple(range(4, x.ndim)))
+            x = x.reshape((steps_n, rows_dev, tp_count, heads_dev) + x.shape[4:])
+            return jnp.moveaxis(x, 2, 0)
+
+        grid4 = (kv_heads, rows_dev, steps_n, group)
+        o_numer = by_owner(k_numer.reshape(grid4 + (DH,))).reshape(tp_count, -1, DH)
+        o_peak = by_owner(k_peak[..., 0].reshape(grid4)).reshape(tp_count, -1)
+        o_mass = by_owner(k_mass[..., 0].reshape(grid4)).reshape(tp_count, -1)
+        n_rows = steps_n * rows_dev * heads_dev
+        n_stat = -(-2 * n_rows // DH)
+        stats = jnp.concatenate([o_peak, o_mass], axis=1)
+        stats = jnp.pad(stats, ((0, 0), (0, n_stat * DH - 2 * n_rows))).reshape(tp_count, n_stat, DH)
+        got = _exchange(jnp.concatenate([o_numer, stats], axis=1), "tp", tp_count)
+        got_numer = got[:, :n_rows].reshape(tp_count, steps_n, rows_dev, heads_dev, DH)
+        got_stats = got[:, n_rows:].reshape(tp_count, -1)[:, : 2 * n_rows]
+        got_stats = got_stats.reshape(tp_count, 2, steps_n, rows_dev, heads_dev)
+        got_peak = got_stats[:, 0]
+        got_mass = got_stats[:, 1]
 
     own_query = queries.reshape(steps_n, rows_dev, heads_dev, DH)
     f_kv = fresh_kv.reshape(2, steps_n, rows_dev, kv_heads, DH)

time: 87.9 us -> 88.1 us (level)
    unnamed x22 -> x23, local copies, waits for them, and re-layouts: 2.06 us -> 2.26 us
  transfers between devices with their start and end apart: 22 -> 22, of which waited for: 14 -> 13; matrix products, arithmetic and copies ran while one was open for 5% -> 6% of each run, Pallas kernels for 0% -> 0%
where the time goes in v10:
time: 88.1 us; the launch traced here: 87.7 us
  starting transfers between devices  38.6 us (44%)
  waiting for transfers between devices  14.7 us (17%)
  matrix products  13.3 us (15%)
  local copies, waits for them, and re-layouts  7.73 us (9%)
  Pallas kernels  5.87 us (7%)
  other arithmetic  5 us (6%)
  blocking collectives  1.85 us (2%)
    ppermute x14, starting transfers between devices, _exchange(): lax.ppermute(send, axis_name, [(i, (i + k) % count) for i in range(count)])  23.5 us
    dot_general x1, matrix products, per_device(): jnp.einsum('rhd,hdf->rhf', head_rows_in, head_weights, preferred_element_...  12.9 us
    ppermute x6, starting transfers between devices, _gather_blocks(): lax.ppermute(pair, axis_name, [(i, (i + 2 * d) % count) for i in range(co...  10 us
    ppermute x6, waiting for transfers between devices, _gather_blocks(): lax.ppermute(pair, axis_name, [(i, (i + 2 * d) % count) for i in range(co...  6.46 us
    ppermute x14, waiting for transfers between devices, _exchange(): lax.ppermute(send, axis_name, [(i, (i + k) % count) for i in range(count)])  6.37 us
    pallas_call x1, Pallas kernels, _attend_packed(): pl.pallas_call(functools.partial(_attend_packed_kernel, group), grid=(kv_...  5.87 us
    ppermute x2, starting transfers between devices, _gather_blocks(): other = lax.ppermute(x, axis_name, [(i, i ^ 1) for i in range(count)])  5.16 us
    unnamed x23, local copies, waits for them, and re-layouts  2.26 us
  transfers between devices with their start and end apart: 22, of which 13 were waited for; matrix products, arithmetic and copies ran while one was open for 6% of the time, Pallas kernels for 0%

profile of v10, /device:TPU:0, one launch (start us, length us, event | category | flops | bytes accessed | tf_op | source)
XLA Modules:
  0.0 87.7 jit_solution(1976559475332539473)
XLA Ops:
  0.0 2.9 %collective-permute-start = (bf16[2,4,2048]{2,1,0:T(4,128)(2,1)}, bf16[2,4,2048]{2,1,0:T(4,128)(2,1)S(1)}, u32[]{:S(2)}, u32[]{:S(2)}) collective-permute-start(bf16[2,4,2048]{2,1,0:T(4,128)(2,1)} %param.9), channel_id=1, source_target_pairs={{0,2},{2,0},{4,6},{6,4},{8,10},{10,8},{12,14},{14,12},{1,3},{3,1},... | collective-permute-start | bytes 98312 | tf_op jit(solution)/shard_map/ppermute | solution.py:28
  2.9 0.8 reshape.341
  3.8 0.8 reshape.340
  4.6 0.7 multiply_exponential_fusion.1
  5.4 0.7 compare_convert_fusion.valid_ref
  6.6 0.9 %maximum_select_fusion.1 = bf16[2,2,4,2048]{3,2,1,0:T(4,128)(2,1)S(1)} fusion(bf16[1,2,4,2048]{3,2,1,0:T(4,128)(2,1)S(1)} %bitcast.144, bf16[1,2,4,2048]{3,2,1,0:T(4,128)(2,1)} %bitcast.140, pred[]{:T(512)S(6)} %eq.24), kind=kLoop, calls=%fused_computation.27 | loop fusion | flops 98304 | bytes 131073 | tf_op jit(solution)/shard_map/jit(_where)/select_n | solution.py:30
  7.5 1.6 %collective-permute-start.1 = (bf16[2,2,4,2048]{3,2,1,0:T(4,128)(2,1)S(1)}, bf16[2,2,4,2048]{3,2,1,0:T(4,128)(2,1)S(1)}, u32[]{:S(2)}, u32[]{:S(2)}) collective-permute-start(bf16[2,2,4,2048]{3,2,1,0:T(4,128)(2,1)S(1)} %maximum_select_fusion.1), channel_id=1, source_target_pairs={{0,4},{2,6},{4,8},{6,10},{8,12},{10,14},{12,0},{14,2},{1,5},{3,7},... | collective-permute-start | bytes 196616 | tf_op jit(solution)/shard_map/ppermute | solution.py:34
  9.1 2.6 %collective-permute-start.2 = (bf16[2,2,4,2048]{3,2,1,0:T(4,128)(2,1)S(1)}, bf16[2,2,4,2048]{3,2,1,0:T(4,128)(2,1)S(1)}, u32[]{:S(2)}, u32[]{:S(2)}) collective-permute-start(bf16[2,2,4,2048]{3,2,1,0:T(4,128)(2,1)S(1)} %maximum_select_fusion.1), channel_id=1, source_target_pairs={{0,8},{2,10},{4,12},{6,14},{8,0},{10,2},{12,4},{14,6},{1,9},{3,11}... | collective-permute-start | bytes 196616 | tf_op jit(solution)/shard_map/ppermute | solution.py:34
  11.7 1.3 %collective-permute-start.3 = (bf16[2,2,4,2048]{3,2,1,0:T(4,128)(2,1)S(1)}, bf16[2,2,4,2048]{3,2,1,0:T(4,128)(2,1)S(1)}, u32[]{:S(2)}, u32[]{:S(2)}) collective-permute-start(bf16[2,2,4,2048]{3,2,1,0:T(4,128)(2,1)S(1)} %maximum_select_fusion.1), channel_id=1, source_target_pairs={{0,12},{2,14},{4,0},{6,2},{8,4},{10,6},{12,8},{14,10},{1,13},{3,15... | collective-permute-start | bytes 196616 | tf_op jit(solution)/shard_map/ppermute | solution.py:34
  13.1 0.9 %maximum_select_fusion = bf16[1,2,2,4,2048]{4,3,2,1,0:T(4,128)(2,1)S(1)} fusion(bf16[1,1,2,4,2048]{4,3,2,1,0:T(4,128)(2,1)S(1)} %bitcast.145, bf16[1,1,2,4,2048]{4,3,2,1,0:T(4,128)(2,1)} %bitcast.141, pred[]{:T(512)S(6)} %eq.24), kind=kLoop, calls=%fused_computation.26 | loop fusion | flops 98304 | bytes 131073 | tf_op jit(solution)/shard_map/jit(_where)/select_n | solution.py:30
  14.0 0.4 collective-permute-done.1
  14.4 2.1 %collective-permute-done.2 = bf16[2,2,4,2048]{3,2,1,0:T(4,128)(2,1)S(1)} collective-permute-done((bf16[2,2,4,2048]{3,2,1,0:T(4,128)(2,1)S(1)}, bf16[2,2,4,2048]{3,2,1,0:T(4,128)(2,1)S(1)}, u32[]{:S(2)}, u32[]{:S(2)}) %collective-permute-start.2) | collective-permute-done | bytes 65568 | tf_op jit(solution)/shard_map/ppermute | solution.py:34
  16.8 0.7 scatter_fusion
  17.8 1.6 %copy-done = bf16[2,4,128,1024]{3,2,1,0:T(8,128)(2,1)S(1)} copy-done((bf16[2,4,128,1024]{3,2,1,0:T(8,128)(2,1)S(1)}, bf16[2,4,128,1024]{3,2,1,0:T(8,128)(2,1)}, u32[]{:S(2)}) %copy-start) | copy-done | bytes 2097176
  19.3 5.9 %shard_map.91 = f32[8,136,128]{2,1,0:T(8,128)S(1)} custom-call(bf16[8,128,128]{2,1,0:T(8,128)(2,1)S(1)} %bitcast.134, bf16[2,1024,1024]{2,1,0:T(8,128)(2,1)} %v_ref.1, bf16[2,1024,1024]{2,1,0:T(8,128)(2,1)} %v_ref.1, bf16[2,4,128,1024]{3,2,1,0:T(8,128)(2,1)S(1)} %copy-done, bf16[2,4,128,1024]{3,2,1,0:T(8,128)(2,1)S(1)} %copy-done, ...), custom_call_target="tpu_custom_call" | custom-call | flops 805306368 | bytes 7110656 | tf_op jit(solution)/shard_map/pallas_call | solution.py:189
  25.3 0.6 collective-permute-start.4
  26.2 1.3 %collective-permute-start.5 = (f32[136,128]{1,0:T(8,128)S(1)}, f32[136,128]{1,0:T(8,128)S(1)}, u32[]{:S(2)}, u32[]{:S(2)}) collective-permute-start(f32[136,128]{1,0:T(8,128)S(1)} %get-tuple-element.12), channel_id=1, source_target_pairs={{0,4},{2,6},{4,8},{6,10},{8,12},{10,14},{12,0},{14,2},{1,5},{3,7},... | collective-permute-start | bytes 208904 | tf_op jit(solution)/shard_map/ppermute | solution.py:61
  27.5 2.9 %collective-permute-start.6 = (f32[136,128]{1,0:T(8,128)S(1)}, f32[136,128]{1,0:T(8,128)S(1)}, u32[]{:S(2)}, u32[]{:S(2)}) collective-permute-start(f32[136,128]{1,0:T(8,128)S(1)} %get-tuple-element.11), channel_id=1, source_target_pairs={{0,6},{2,8},{4,10},{6,12},{8,14},{10,0},{12,2},{14,4},{1,7},{3,9},... | collective-permute-start | bytes 208904 | tf_op jit(solution)/shard_map/ppermute | solution.py:61
  30.4 1.8 %collective-permute-start.7 = (f32[136,128]{1,0:T(8,128)S(1)}, f32[136,128]{1,0:T(8,128)S(1)}, u32[]{:S(2)}, u32[]{:S(2)}) collective-permute-start(f32[136,128]{1,0:T(8,128)S(1)} %get-tuple-element.10), channel_id=1, source_target_pairs={{0,8},{2,10},{4,12},{6,14},{8,0},{10,2},{12,4},{14,6},{1,9},{3,11}... | collective-permute-start | bytes 208904 | tf_op jit(solution)/shard_map/ppermute | solution.py:61
  32.2 1.1 %collective-permute-start.8 = (f32[136,128]{1,0:T(8,128)S(1)}, f32[136,128]{1,0:T(8,128)S(1)}, u32[]{:S(2)}, u32[]{:S(2)}) collective-permute-start(f32[136,128]{1,0:T(8,128)S(1)} %get-tuple-element.9), channel_id=1, source_target_pairs={{0,10},{2,12},{4,14},{6,0},{8,2},{10,4},{12,6},{14,8},{1,11},{3,13... | collective-permute-start | bytes 208904 | tf_op jit(solution)/shard_map/ppermute | solution.py:61
  33.3 1.3 %collective-permute-start.9 = (f32[136,128]{1,0:T(8,128)S(1)}, f32[136,128]{1,0:T(8,128)S(1)}, u32[]{:S(2)}, u32[]{:S(2)}) collective-permute-start(f32[136,128]{1,0:T(8,128)S(1)} %get-tuple-element.8), channel_id=1, source_target_pairs={{0,12},{2,14},{4,0},{6,2},{8,4},{10,6},{12,8},{14,10},{1,13},{3,15... | collective-permute-start | bytes 208904 | tf_op jit(solution)/shard_map/ppermute | solution.py:61
  34.6 1.6 %collective-permute-start.10 = (f32[136,128]{1,0:T(8,128)S(1)}, f32[136,128]{1,0:T(8,128)S(1)}, u32[]{:S(2)}, u32[]{:S(2)}) collective-permute-start(f32[136,128]{1,0:T(8,128)S(1)} %get-tuple-element.7), channel_id=1, source_target_pairs={{0,14},{2,0},{4,2},{6,4},{8,6},{10,8},{12,10},{14,12},{1,15},{3,1}... | collective-permute-start | bytes 208904 | tf_op jit(solution)/shard_map/ppermute | solution.py:61
  36.2 1.7 %collective-permute-done.6 = f32[136,128]{1,0:T(8,128)S(1)} collective-permute-done((f32[136,128]{1,0:T(8,128)S(1)}, f32[136,128]{1,0:T(8,128)S(1)}, u32[]{:S(2)}, u32[]{:S(2)}) %collective-permute-start.6) | collective-permute-done | bytes 69664 | tf_op jit(solution)/shard_map/ppermute | solution.py:61
  38.2 1.2 %collective-permute-done.9 = f32[136,128]{1,0:T(8,128)S(1)} collective-permute-done((f32[136,128]{1,0:T(8,128)S(1)}, f32[136,128]{1,0:T(8,128)S(1)}, u32[]{:S(2)}, u32[]{:S(2)}) %collective-permute-start.9) | collective-permute-done | bytes 69664 | tf_op jit(solution)/shard_map/ppermute | solution.py:61
  41.1 1.9 %all_gather.3 = bf16[2,8,2048]{2,0,1:T(2,128)(2,1)S(1)} all-gather(bf16[2,4,2048]{2,0,1:T(2,128)(2,1)S(1)} %copy.56), channel_id=1, replica_groups=mesh['rep'=2,'tp'=8,'sub'=2] {'sub'}, dimensions={1}, use_global_device_ids=true | all-gather | bytes 98304 | tf_op jit(solution)/shard_map/all_gather | solution.py:289
  43.0 12.9 %fusion.1 = f32[16,8192]{1,0:T(8,128)S(1)} fusion(f32[8192]{0:T(1024)S(1)} %dynamic_slice.61, bf16[16,128,8192]{2,1,0:T(8,128)(2,1)} %bitcast.163, bf16[16,16,128]{2,1,0:T(8,128)(2,1)S(1)} %bitcast.155), kind=kOutput, calls=%fused_computation.4 | convolution fusion | flops 543031296 | bytes 34177024 | tf_op jit(solution)/shard_map/rhd,hdf->rhf/dot_general | solution.py:298
  56.2 0.5 constant_dynamic-slice_fusion.8
  56.8 2.2 %collective-permute-start.11 = (f32[16,1024]{1,0:T(8,128)S(1)}, f32[16,1024]{1,0:T(8,128)S(1)}, u32[]{:S(2)}, u32[]{:S(2)}) collective-permute-start(f32[16,1024]{1,0:T(8,128)S(1)} %bitcast.154), channel_id=1, source_target_pairs={{0,2},{2,4},{4,6},{6,8},{8,10},{10,12},{12,14},{14,0},{1,3},{3,5},... | collective-permute-start | bytes 196616 | tf_op jit(solution)/shard_map/ppermute | solution.py:61
  59.0 2.7 %collective-permute-start.12 = (f32[16,1024]{1,0:T(8,128)S(1)}, f32[16,1024]{1,0:T(8,128)S(1)}, u32[]{:S(2)}, u32[]{:S(2)}) collective-permute-start(f32[16,1024]{1,0:T(8,128)S(1)} %bitcast.153), channel_id=1, source_target_pairs={{0,4},{2,6},{4,8},{6,10},{8,12},{10,14},{12,0},{14,2},{1,5},{3,7},... | collective-permute-start | bytes 196616 | tf_op jit(solution)/shard_map/ppermute | solution.py:61
  61.8 0.6 collective-permute-start.13
  62.4 2.0 %collective-permute-start.14 = (f32[16,1024]{1,0:T(8,128)S(1)}, f32[16,1024]{1,0:T(8,128)S(1)}, u32[]{:S(2)}, u32[]{:S(2)}) collective-permute-start(f32[16,1024]{1,0:T(8,128)S(1)} %bitcast.149), channel_id=1, source_target_pairs={{0,8},{2,10},{4,12},{6,14},{8,0},{10,2},{12,4},{14,6},{1,9},{3,11}... | collective-permute-start | bytes 196616 | tf_op jit(solution)/shard_map/ppermute | solution.py:61
  64.4 2.7 %collective-permute-start.15 = (f32[16,1024]{1,0:T(8,128)S(1)}, f32[16,1024]{1,0:T(8,128)S(1)}, u32[]{:S(2)}, u32[]{:S(2)}) collective-permute-start(f32[16,1024]{1,0:T(8,128)S(1)} %bitcast.150), channel_id=1, source_target_pairs={{0,10},{2,12},{4,14},{6,0},{8,2},{10,4},{12,6},{14,8},{1,11},{3,13... | collective-permute-start | bytes 196616 | tf_op jit(solution)/shard_map/ppermute | solution.py:61
  67.1 1.5 %collective-permute-start.16 = (f32[16,1024]{1,0:T(8,128)S(1)}, f32[16,1024]{1,0:T(8,128)S(1)}, u32[]{:S(2)}, u32[]{:S(2)}) collective-permute-start(f32[16,1024]{1,0:T(8,128)S(1)} %bitcast.152), channel_id=1, source_target_pairs={{0,12},{2,14},{4,0},{6,2},{8,4},{10,6},{12,8},{14,10},{1,13},{3,15... | collective-permute-start | bytes 196616 | tf_op jit(solution)/shard_map/ppermute | solution.py:61
  68.6 1.2 %collective-permute-start.17 = (f32[16,1024]{1,0:T(8,128)S(1)}, f32[16,1024]{1,0:T(8,128)S(1)}, u32[]{:S(2)}, u32[]{:S(2)}) collective-permute-start(f32[16,1024]{1,0:T(8,128)S(1)} %bitcast.151), channel_id=1, source_target_pairs={{0,14},{2,0},{4,2},{6,4},{8,6},{10,8},{12,10},{14,12},{1,15},{3,1}... | collective-permute-start | bytes 196616 | tf_op jit(solution)/shard_map/ppermute | solution.py:61
  69.9 0.4 collective-permute-done.13
  70.3 1.1 %collective-permute-done.14 = f32[16,1024]{1,0:T(8,128)S(1)} collective-permute-done((f32[16,1024]{1,0:T(8,128)S(1)}, f32[16,1024]{1,0:T(8,128)S(1)}, u32[]{:S(2)}, u32[]{:S(2)}) %collective-permute-start.14) | collective-permute-done | bytes 65568 | tf_op jit(solution)/shard_map/ppermute | solution.py:61
  71.4 0.8 collective-permute-done.15
  72.2 0.9 %collective-permute-done.16 = f32[16,1024]{1,0:T(8,128)S(1)} collective-permute-done((f32[16,1024]{1,0:T(8,128)S(1)}, f32[16,1024]{1,0:T(8,128)S(1)}, u32[]{:S(2)}, u32[]{:S(2)}) %collective-permute-start.16) | collective-permute-done | bytes 65568 | tf_op jit(solution)/shard_map/ppermute | solution.py:61
  73.1 2.2 %collective-permute-start.18 = (bf16[16,1024]{1,0:T(8,128)(2,1)S(1)}, bf16[16,1024]{1,0:T(8,128)(2,1)S(1)}, u32[]{:S(2)}, u32[]{:S(2)}) collective-permute-start(bf16[16,1024]{1,0:T(8,128)(2,1)S(1)} %clamp_convert_fusion), channel_id=1, source_target_pairs={{0,2},{2,0},{4,6},{6,4},{8,10},{10,8},{12,14},{14,12},{1,3},{3,1},... | collective-permute-start | bytes 98312 | tf_op jit(solution)/shard_map/ppermute | solution.py:28
  75.3 1.9 %collective-permute-done.18 = bf16[16,1024]{1,0:T(8,128)(2,1)S(1)} collective-permute-done((bf16[16,1024]{1,0:T(8,128)(2,1)S(1)}, bf16[16,1024]{1,0:T(8,128)(2,1)S(1)}, u32[]{:S(2)}, u32[]{:S(2)}) %collective-permute-start.18) | collective-permute-done | bytes 32800 | tf_op jit(solution)/shard_map/ppermute | solution.py:28
  77.2 2.0 %collective-permute-start.19 = (bf16[2,16,1024]{2,1,0:T(8,128)(2,1)S(1)}, bf16[2,16,1024]{2,1,0:T(8,128)(2,1)S(1)}, u32[]{:S(2)}, u32[]{:S(2)}) collective-permute-start(bf16[2,16,1024]{2,1,0:T(8,128)(2,1)S(1)} %maximum_select_fusion.3), channel_id=1, source_target_pairs={{0,4},{2,6},{4,8},{6,10},{8,12},{10,14},{12,0},{14,2},{1,5},{3,7},... | collective-permute-start | bytes 196616 | tf_op jit(solution)/shard_map/ppermute | solution.py:34
  79.2 1.5 %collective-permute-start.20 = (bf16[2,16,1024]{2,1,0:T(8,128)(2,1)S(1)}, bf16[2,16,1024]{2,1,0:T(8,128)(2,1)S(1)}, u32[]{:S(2)}, u32[]{:S(2)}) collective-permute-start(bf16[2,16,1024]{2,1,0:T(8,128)(2,1)S(1)} %maximum_select_fusion.3), channel_id=1, source_target_pairs={{0,8},{2,10},{4,12},{6,14},{8,0},{10,2},{12,4},{14,6},{1,9},{3,11}... | collective-permute-start | bytes 196616 | tf_op jit(solution)/shard_map/ppermute | solution.py:34
  80.7 0.9 %collective-permute-start.21 = (bf16[2,16,1024]{2,1,0:T(8,128)(2,1)S(1)}, bf16[2,16,1024]{2,1,0:T(8,128)(2,1)S(1)}, u32[]{:S(2)}, u32[]{:S(2)}) collective-permute-start(bf16[2,16,1024]{2,1,0:T(8,128)(2,1)S(1)} %maximum_select_fusion.3), channel_id=1, source_target_pairs={{0,12},{2,14},{4,0},{6,2},{8,4},{10,6},{12,8},{14,10},{1,13},{3,15... | collective-permute-start | bytes 196616 | tf_op jit(solution)/shard_map/ppermute | solution.py:34
  81.7 2.1 %collective-permute-done.19 = bf16[2,16,1024]{2,1,0:T(8,128)(2,1)S(1)} collective-permute-done((bf16[2,16,1024]{2,1,0:T(8,128)(2,1)S(1)}, bf16[2,16,1024]{2,1,0:T(8,128)(2,1)S(1)}, u32[]{:S(2)}, u32[]{:S(2)}) %collective-permute-start.19) | collective-permute-done | bytes 65568 | tf_op jit(solution)/shard_map/ppermute | solution.py:34
  83.8 1.5 %collective-permute-done.20 = bf16[2,16,1024]{2,1,0:T(8,128)(2,1)S(1)} collective-permute-done((bf16[2,16,1024]{2,1,0:T(8,128)(2,1)S(1)}, bf16[2,16,1024]{2,1,0:T(8,128)(2,1)S(1)}, u32[]{:S(2)}, u32[]{:S(2)}) %collective-permute-start.20) | collective-permute-done | bytes 65568 | tf_op jit(solution)/shard_map/ppermute | solution.py:34
  85.3 0.3 collective-permute-done.21
  85.7 0.7 scatter_fusion.1
  86.9 0.8 add_convert_fusion
  (83 shorter events, 4.3 us)
Async XLA Ops:
  0.0 6.6 %collective-permute-start = (bf16[2,4,2048]{2,1,0:T(4,128)(2,1)}, bf16[2,4,2048]{2,1,0:T(4,128)(2,1)S(1)}, u32[]{:S(2)}, u32[]{:S(2)}) collective-permute-start(bf16[2,4,2048]{2,1,0:T(4,128)(2,1)} %param.9), channel_id=1, source_target_pairs={{0,2},{2,0},{4,6},{6,4},{8,10},{10,8},{12,14},{14,12},{1,3},{3,1},... | collective-permute-start | bytes 98312 | tf_op jit(solution)/shard_map/ppermute | solution.py:28
  7.5 6.9 %collective-permute-start.1 = (bf16[2,2,4,2048]{3,2,1,0:T(4,128)(2,1)S(1)}, bf16[2,2,4,2048]{3,2,1,0:T(4,128)(2,1)S(1)}, u32[]{:S(2)}, u32[]{:S(2)}) collective-permute-start(bf16[2,2,4,2048]{3,2,1,0:T(4,128)(2,1)S(1)} %maximum_select_fusion.1), channel_id=1, source_target_pairs={{0,4},{2,6},{4,8},{6,10},{8,12},{10,14},{12,0},{14,2},{1,5},{3,7},... | collective-permute-start | bytes 196616 | tf_op jit(solution)/shard_map/ppermute | solution.py:34
  9.1 7.3 %collective-permute-start.2 = (bf16[2,2,4,2048]{3,2,1,0:T(4,128)(2,1)S(1)}, bf16[2,2,4,2048]{3,2,1,0:T(4,128)(2,1)S(1)}, u32[]{:S(2)}, u32[]{:S(2)}) collective-permute-start(bf16[2,2,4,2048]{3,2,1,0:T(4,128)(2,1)S(1)} %maximum_select_fusion.1), channel_id=1, source_target_pairs={{0,8},{2,10},{4,12},{6,14},{8,0},{10,2},{12,4},{14,6},{1,9},{3,11}... | collective-permute-start | bytes 196616 | tf_op jit(solution)/shard_map/ppermute | solution.py:34
  11.7 4.8 %collective-permute-start.3 = (bf16[2,2,4,2048]{3,2,1,0:T(4,128)(2,1)S(1)}, bf16[2,2,4,2048]{3,2,1,0:T(4,128)(2,1)S(1)}, u32[]{:S(2)}, u32[]{:S(2)}) collective-permute-start(bf16[2,2,4,2048]{3,2,1,0:T(4,128)(2,1)S(1)} %maximum_select_fusion.1), channel_id=1, source_target_pairs={{0,12},{2,14},{4,0},{6,2},{8,4},{10,6},{12,8},{14,10},{1,13},{3,15... | collective-permute-start | bytes 196616 | tf_op jit(solution)/shard_map/ppermute | solution.py:34
  17.7 1.6 %copy-start = (bf16[2,4,128,1024]{3,2,1,0:T(8,128)(2,1)S(1)}, bf16[2,4,128,1024]{3,2,1,0:T(8,128)(2,1)}, u32[]{:S(2)}) copy-start(bf16[2,4,128,1024]{3,2,1,0:T(8,128)(2,1)} %tv_ref.1) | copy-start | bytes 6291460
  25.3 8.0 %collective-permute-start.4 = (f32[136,128]{1,0:T(8,128)S(1)}, f32[136,128]{1,0:T(8,128)S(1)}, u32[]{:S(2)}, u32[]{:S(2)}) collective-permute-start(f32[136,128]{1,0:T(8,128)S(1)} %get-tuple-element.13), channel_id=1, source_target_pairs={{0,2},{2,4},{4,6},{6,8},{8,10},{10,12},{12,14},{14,0},{1,3},{3,5},... | collective-permute-start | bytes 208904 | tf_op jit(solution)/shard_map/ppermute | solution.py:61
  26.2 8.4 %collective-permute-start.5 = (f32[136,128]{1,0:T(8,128)S(1)}, f32[136,128]{1,0:T(8,128)S(1)}, u32[]{:S(2)}, u32[]{:S(2)}) collective-permute-start(f32[136,128]{1,0:T(8,128)S(1)} %get-tuple-element.12), channel_id=1, source_target_pairs={{0,4},{2,6},{4,8},{6,10},{8,12},{10,14},{12,0},{14,2},{1,5},{3,7},... | collective-permute-start | bytes 208904 | tf_op jit(solution)/shard_map/ppermute | solution.py:61
  27.5 10.5 %collective-permute-start.6 = (f32[136,128]{1,0:T(8,128)S(1)}, f32[136,128]{1,0:T(8,128)S(1)}, u32[]{:S(2)}, u32[]{:S(2)}) collective-permute-start(f32[136,128]{1,0:T(8,128)S(1)} %get-tuple-element.11), channel_id=1, source_target_pairs={{0,6},{2,8},{4,10},{6,12},{8,14},{10,0},{12,2},{14,4},{1,7},{3,9},... | collective-permute-start | bytes 208904 | tf_op jit(solution)/shard_map/ppermute | solution.py:61
  30.4 7.5 %collective-permute-start.7 = (f32[136,128]{1,0:T(8,128)S(1)}, f32[136,128]{1,0:T(8,128)S(1)}, u32[]{:S(2)}, u32[]{:S(2)}) collective-permute-start(f32[136,128]{1,0:T(8,128)S(1)} %get-tuple-element.10), channel_id=1, source_target_pairs={{0,8},{2,10},{4,12},{6,14},{8,0},{10,2},{12,4},{14,6},{1,9},{3,11}... | collective-permute-start | bytes 208904 | tf_op jit(solution)/shard_map/ppermute | solution.py:61
  32.2 6.0 %collective-permute-start.8 = (f32[136,128]{1,0:T(8,128)S(1)}, f32[136,128]{1,0:T(8,128)S(1)}, u32[]{:S(2)}, u32[]{:S(2)}) collective-permute-start(f32[136,128]{1,0:T(8,128)S(1)} %get-tuple-element.9), channel_id=1, source_target_pairs={{0,10},{2,12},{4,14},{6,0},{8,2},{10,4},{12,6},{14,8},{1,11},{3,13... | collective-permute-start | bytes 208904 | tf_op jit(solution)/shard_map/ppermute | solution.py:61
  33.3 6.1 %collective-permute-start.9 = (f32[136,128]{1,0:T(8,128)S(1)}, f32[136,128]{1,0:T(8,128)S(1)}, u32[]{:S(2)}, u32[]{:S(2)}) collective-permute-start(f32[136,128]{1,0:T(8,128)S(1)} %get-tuple-element.8), channel_id=1, source_target_pairs={{0,12},{2,14},{4,0},{6,2},{8,4},{10,6},{12,8},{14,10},{1,13},{3,15... | collective-permute-start | bytes 208904 | tf_op jit(solution)/shard_map/ppermute | solution.py:61
  34.6 4.8 %collective-permute-start.10 = (f32[136,128]{1,0:T(8,128)S(1)}, f32[136,128]{1,0:T(8,128)S(1)}, u32[]{:S(2)}, u32[]{:S(2)}) collective-permute-start(f32[136,128]{1,0:T(8,128)S(1)} %get-tuple-element.7), channel_id=1, source_target_pairs={{0,14},{2,0},{4,2},{6,4},{8,6},{10,8},{12,10},{14,12},{1,15},{3,1}... | collective-permute-start | bytes 208904 | tf_op jit(solution)/shard_map/ppermute | solution.py:61
  43.0 18.8 %copy-start.2 = (s32[128]{0:T(128)S(1)}, s32[128]{0:T(128)}, u32[]{:S(2)}) copy-start(s32[128]{0:T(128)} %param.16) | copy-start | bytes 1540
  55.9 31.0 %copy-start.1 = (bf16[2,8,8192]{2,1,0:T(8,128)(2,1)S(1)}, bf16[2,8,8192]{2,1,0:T(8,128)(2,1)}, u32[]{:S(2)}) copy-start(bf16[2,8,8192]{2,1,0:T(8,128)(2,1)} %param.17) | copy-start | bytes 786436
  56.8 10.3 %collective-permute-start.11 = (f32[16,1024]{1,0:T(8,128)S(1)}, f32[16,1024]{1,0:T(8,128)S(1)}, u32[]{:S(2)}, u32[]{:S(2)}) collective-permute-start(f32[16,1024]{1,0:T(8,128)S(1)} %bitcast.154), channel_id=1, source_target_pairs={{0,2},{2,4},{4,6},{6,8},{8,10},{10,12},{12,14},{14,0},{1,3},{3,5},... | collective-permute-start | bytes 196616 | tf_op jit(solution)/shard_map/ppermute | solution.py:61
  59.0 9.6 %collective-permute-start.12 = (f32[16,1024]{1,0:T(8,128)S(1)}, f32[16,1024]{1,0:T(8,128)S(1)}, u32[]{:S(2)}, u32[]{:S(2)}) collective-permute-start(f32[16,1024]{1,0:T(8,128)S(1)} %bitcast.153), channel_id=1, source_target_pairs={{0,4},{2,6},{4,8},{6,10},{8,12},{10,14},{12,0},{14,2},{1,5},{3,7},... | collective-permute-start | bytes 196616 | tf_op jit(solution)/shard_map/ppermute | solution.py:61
  61.8 8.5 %collective-permute-start.13 = (f32[16,1024]{1,0:T(8,128)S(1)}, f32[16,1024]{1,0:T(8,128)S(1)}, u32[]{:S(2)}, u32[]{:S(2)}) collective-permute-start(f32[16,1024]{1,0:T(8,128)S(1)} %bitcast.148), channel_id=1, source_target_pairs={{0,6},{2,8},{4,10},{6,12},{8,14},{10,0},{12,2},{14,4},{1,7},{3,9},... | collective-permute-start | bytes 196616 | tf_op jit(solution)/shard_map/ppermute | solution.py:61
  62.4 9.0 %collective-permute-start.14 = (f32[16,1024]{1,0:T(8,128)S(1)}, f32[16,1024]{1,0:T(8,128)S(1)}, u32[]{:S(2)}, u32[]{:S(2)}) collective-permute-start(f32[16,1024]{1,0:T(8,128)S(1)} %bitcast.149), channel_id=1, source_target_pairs={{0,8},{2,10},{4,12},{6,14},{8,0},{10,2},{12,4},{14,6},{1,9},{3,11}... | collective-permute-start | bytes 196616 | tf_op jit(solution)/shard_map/ppermute | solution.py:61
  64.4 7.8 %collective-permute-start.15 = (f32[16,1024]{1,0:T(8,128)S(1)}, f32[16,1024]{1,0:T(8,128)S(1)}, u32[]{:S(2)}, u32[]{:S(2)}) collective-permute-start(f32[16,1024]{1,0:T(8,128)S(1)} %bitcast.150), channel_id=1, source_target_pairs={{0,10},{2,12},{4,14},{6,0},{8,2},{10,4},{12,6},{14,8},{1,11},{3,13... | collective-permute-start | bytes 196616 | tf_op jit(solution)/shard_map/ppermute | solution.py:61
  67.1 5.9 %collective-permute-start.16 = (f32[16,1024]{1,0:T(8,128)S(1)}, f32[16,1024]{1,0:T(8,128)S(1)}, u32[]{:S(2)}, u32[]{:S(2)}) collective-permute-start(f32[16,1024]{1,0:T(8,128)S(1)} %bitcast.152), channel_id=1, source_target_pairs={{0,12},{2,14},{4,0},{6,2},{8,4},{10,6},{12,8},{14,10},{1,13},{3,15... | collective-permute-start | bytes 196616 | tf_op jit(solution)/shard_map/ppermute | solution.py:61
  68.6 4.4 %collective-permute-start.17 = (f32[16,1024]{1,0:T(8,128)S(1)}, f32[16,1024]{1,0:T(8,128)S(1)}, u32[]{:S(2)}, u32[]{:S(2)}) collective-permute-start(f32[16,1024]{1,0:T(8,128)S(1)} %bitcast.151), channel_id=1, source_target_pairs={{0,14},{2,0},{4,2},{6,4},{8,6},{10,8},{12,10},{14,12},{1,15},{3,1}... | collective-permute-start | bytes 196616 | tf_op jit(solution)/shard_map/ppermute | solution.py:61
  73.1 4.1 %collective-permute-start.18 = (bf16[16,1024]{1,0:T(8,128)(2,1)S(1)}, bf16[16,1024]{1,0:T(8,128)(2,1)S(1)}, u32[]{:S(2)}, u32[]{:S(2)}) collective-permute-start(bf16[16,1024]{1,0:T(8,128)(2,1)S(1)} %clamp_convert_fusion), channel_id=1, source_target_pairs={{0,2},{2,0},{4,6},{6,4},{8,10},{10,8},{12,14},{14,12},{1,3},{3,1},... | collective-permute-start | bytes 98312 | tf_op jit(solution)/shard_map/ppermute | solution.py:28
  77.2 6.6 %collective-permute-start.19 = (bf16[2,16,1024]{2,1,0:T(8,128)(2,1)S(1)}, bf16[2,16,1024]{2,1,0:T(8,128)(2,1)S(1)}, u32[]{:S(2)}, u32[]{:S(2)}) collective-permute-start(bf16[2,16,1024]{2,1,0:T(8,128)(2,1)S(1)} %maximum_select_fusion.3), channel_id=1, source_target_pairs={{0,4},{2,6},{4,8},{6,10},{8,12},{10,14},{12,0},{14,2},{1,5},{3,7},... | collective-permute-start | bytes 196616 | tf_op jit(solution)/shard_map/ppermute | solution.py:34
  79.2 6.1 %collective-permute-start.20 = (bf16[2,16,1024]{2,1,0:T(8,128)(2,1)S(1)}, bf16[2,16,1024]{2,1,0:T(8,128)(2,1)S(1)}, u32[]{:S(2)}, u32[]{:S(2)}) collective-permute-start(bf16[2,16,1024]{2,1,0:T(8,128)(2,1)S(1)} %maximum_select_fusion.3), channel_id=1, source_target_pairs={{0,8},{2,10},{4,12},{6,14},{8,0},{10,2},{12,4},{14,6},{1,9},{3,11}... | collective-permute-start | bytes 196616 | tf_op jit(solution)/shard_map/ppermute | solution.py:34
  80.7 4.9 %collective-permute-start.21 = (bf16[2,16,1024]{2,1,0:T(8,128)(2,1)S(1)}, bf16[2,16,1024]{2,1,0:T(8,128)(2,1)S(1)}, u32[]{:S(2)}, u32[]{:S(2)}) collective-permute-start(bf16[2,16,1024]{2,1,0:T(8,128)(2,1)S(1)} %maximum_select_fusion.3), channel_id=1, source_target_pairs={{0,12},{2,14},{4,0},{6,2},{8,4},{10,6},{12,8},{14,10},{1,13},{3,15... | collective-permute-start | bytes 196616 | tf_op jit(solution)/shard_map/ppermute | solution.py:34

commit v11 on v10

--- a/solution.py
+++ b/solution.py
@@ -134,7 +134,6 @@
             transcendentals=kv_heads * rows_n * (prefix_dev + tail_dev),
             bytes_accessed=bytes_in + 3 * 4 * kv_heads * rows_n * DH,
         ),
-        compiler_params=pltpu.CompilerParams(vmem_limit_bytes=48 * 1024 * 1024),
     )(q_rows, prefix_kv, prefix_kv, tail_kv, tail_kv, valid)
 
 
@@ -204,7 +203,6 @@
             transcendentals=kv_heads * rows_n * (prefix_dev + tail_dev),
             bytes_accessed=bytes_in + 4 * kv_heads * (rows_n + 8) * DH,
         ),
-        compiler_params=pltpu.CompilerParams(vmem_limit_bytes=48 * 1024 * 1024),
     )(q_rows, prefix_kv, prefix_kv, tail_kv, tail_kv, valid)
 
 

time: 88.1 us -> 90.3 us (1.025)
  Pallas kernels: 5.87 us -> 7.2 us
    unnamed x23 -> x21, local copies, waits for them, and re-layouts: 2.26 us -> 0.67 us
    pallas_call x1, Pallas kernels: 5.87 us -> 7.2 us  [_attend_packed(): pl.pallas_call(functools.partial(_attend_packed_kernel, group), grid=(kv_...]
    squeeze x1, local copies, waits for them, and re-layouts: 0.06 us -> 1.16 us  [_exchange(): lax.dynamic_index_in_dim(b, dst, 0, keepdims=False)]
  transfers between devices with their start and end apart: 22 -> 22, of which waited for: 13 -> 12; matrix products, arithmetic and copies ran while one was open for 6% -> 6% of each run, Pallas kernels for 0% -> 0%
where the time goes in v11:
time: 90.3 us; the launch traced here: 89.8 us
  starting transfers between devices  38.4 us (43%)
  waiting for transfers between devices  15 us (17%)
  matrix products  13.3 us (15%)
  local copies, waits for them, and re-layouts  7.95 us (9%)
  Pallas kernels  7.2 us (8%)
  other arithmetic  5.57 us (6%)
  blocking collectives  1.85 us (2%)
    ppermute x14, starting transfers between devices, _exchange(): lax.ppermute(send, axis_name, [(i, (i + k) % count) for i in range(count)])  23.5 us
    dot_general x1, matrix products, per_device(): jnp.einsum('rhd,hdf->rhf', head_rows_in, head_weights, preferred_element_...  12.9 us
    ppermute x6, starting transfers between devices, _gather_blocks(): lax.ppermute(pair, axis_name, [(i, (i + 2 * d) % count) for i in range(co...  9.8 us
    pallas_call x1, Pallas kernels, _attend_packed(): pl.pallas_call(functools.partial(_attend_packed_kernel, group), grid=(kv_...  7.2 us
    ppermute x14, waiting for transfers between devices, _exchange(): lax.ppermute(send, axis_name, [(i, (i + k) % count) for i in range(count)])  6.78 us
    ppermute x6, waiting for transfers between devices, _gather_blocks(): lax.ppermute(pair, axis_name, [(i, (i + 2 * d) % count) for i in range(co...  6.29 us
    ppermute x2, starting transfers between devices, _gather_blocks(): other = lax.ppermute(x, axis_name, [(i, i ^ 1) for i in range(count)])  5.16 us
    ppermute x2, waiting for transfers between devices, _gather_blocks(): other = lax.ppermute(x, axis_name, [(i, i ^ 1) for i in range(count)])  1.89 us
  transfers between devices with their start and end apart: 22, of which 12 were waited for; matrix products, arithmetic and copies ran while one was open for 6% of the time, Pallas kernels for 0%

profile of v11, /device:TPU:0, one launch (start us, length us, event | category | flops | bytes accessed | tf_op | source)
XLA Modules:
  0.0 89.8 jit_solution(8794106680133397647)
XLA Ops:
  0.0 2.9 %collective-permute-start = (bf16[2,4,2048]{2,1,0:T(4,128)(2,1)}, bf16[2,4,2048]{2,1,0:T(4,128)(2,1)S(1)}, u32[]{:S(2)}, u32[]{:S(2)}) collective-permute-start(bf16[2,4,2048]{2,1,0:T(4,128)(2,1)} %param.9), channel_id=1, source_target_pairs={{0,2},{2,0},{4,6},{6,4},{8,10},{10,8},{12,14},{14,12},{1,3},{3,1},... | collective-permute-start | bytes 98312 | tf_op jit(solution)/shard_map/ppermute | solution.py:28
  2.9 0.8 reshape.341
  3.8 0.8 reshape.340
  4.6 0.7 multiply_exponential_fusion.1
  5.4 1.3 %compare_convert_fusion.valid_ref = f32[4,128]{1,0:T(4,128)} fusion(s32[128]{0:T(128)S(1)} %iota_add_fusion, s32[4]{0:T(128)} %param.12), kind=kLoop, calls=%fused_computation.82 | loop fusion | flops 1024 | bytes 2576 | tf_op jit(solution)/shard_map/convert_element_type | solution.py:227
  7.2 0.9 %maximum_select_fusion.1 = bf16[2,2,4,2048]{3,2,1,0:T(4,128)(2,1)S(1)} fusion(bf16[1,2,4,2048]{3,2,1,0:T(4,128)(2,1)S(1)} %bitcast.144, bf16[1,2,4,2048]{3,2,1,0:T(4,128)(2,1)} %bitcast.140, pred[]{:T(512)S(6)} %eq.24), kind=kLoop, calls=%fused_computation.27 | loop fusion | flops 98304 | bytes 131073 | tf_op jit(solution)/shard_map/jit(_where)/select_n | solution.py:30
  8.1 1.6 %collective-permute-start.1 = (bf16[2,2,4,2048]{3,2,1,0:T(4,128)(2,1)S(1)}, bf16[2,2,4,2048]{3,2,1,0:T(4,128)(2,1)S(1)}, u32[]{:S(2)}, u32[]{:S(2)}) collective-permute-start(bf16[2,2,4,2048]{3,2,1,0:T(4,128)(2,1)S(1)} %maximum_select_fusion.1), channel_id=1, source_target_pairs={{0,4},{2,6},{4,8},{6,10},{8,12},{10,14},{12,0},{14,2},{1,5},{3,7},... | collective-permute-start | bytes 196616 | tf_op jit(solution)/shard_map/ppermute | solution.py:34
  9.7 2.6 %collective-permute-start.2 = (bf16[2,2,4,2048]{3,2,1,0:T(4,128)(2,1)S(1)}, bf16[2,2,4,2048]{3,2,1,0:T(4,128)(2,1)S(1)}, u32[]{:S(2)}, u32[]{:S(2)}) collective-permute-start(bf16[2,2,4,2048]{3,2,1,0:T(4,128)(2,1)S(1)} %maximum_select_fusion.1), channel_id=1, source_target_pairs={{0,8},{2,10},{4,12},{6,14},{8,0},{10,2},{12,4},{14,6},{1,9},{3,11}... | collective-permute-start | bytes 196616 | tf_op jit(solution)/shard_map/ppermute | solution.py:34
  12.3 1.4 %collective-permute-start.3 = (bf16[2,2,4,2048]{3,2,1,0:T(4,128)(2,1)S(1)}, bf16[2,2,4,2048]{3,2,1,0:T(4,128)(2,1)S(1)}, u32[]{:S(2)}, u32[]{:S(2)}) collective-permute-start(bf16[2,2,4,2048]{3,2,1,0:T(4,128)(2,1)S(1)} %maximum_select_fusion.1), channel_id=1, source_target_pairs={{0,12},{2,14},{4,0},{6,2},{8,4},{10,6},{12,8},{14,10},{1,13},{3,15... | collective-permute-start | bytes 196616 | tf_op jit(solution)/shard_map/ppermute | solution.py:34
  13.7 0.9 %maximum_select_fusion = bf16[1,2,2,4,2048]{4,3,2,1,0:T(4,128)(2,1)S(1)} fusion(bf16[1,1,2,4,2048]{4,3,2,1,0:T(4,128)(2,1)S(1)} %bitcast.145, bf16[1,1,2,4,2048]{4,3,2,1,0:T(4,128)(2,1)} %bitcast.141, pred[]{:T(512)S(6)} %eq.24), kind=kLoop, calls=%fused_computation.26 | loop fusion | flops 98304 | bytes 131073 | tf_op jit(solution)/shard_map/jit(_where)/select_n | solution.py:30
  14.6 0.4 collective-permute-done.1
  15.0 2.1 %collective-permute-done.2 = bf16[2,2,4,2048]{3,2,1,0:T(4,128)(2,1)S(1)} collective-permute-done((bf16[2,2,4,2048]{3,2,1,0:T(4,128)(2,1)S(1)}, bf16[2,2,4,2048]{3,2,1,0:T(4,128)(2,1)S(1)}, u32[]{:S(2)}, u32[]{:S(2)}) %collective-permute-start.2) | collective-permute-done | bytes 65568 | tf_op jit(solution)/shard_map/ppermute | solution.py:34
  17.4 0.7 scatter_fusion
  18.1 0.9 reshape.338
  19.0 7.2 %shard_map.91 = f32[8,136,128]{2,1,0:T(8,128)} custom-call(bf16[8,128,128]{2,1,0:T(8,128)(2,1)} %bitcast.136, bf16[2,1024,1024]{2,1,0:T(8,128)(2,1)} %v_ref.1, bf16[2,1024,1024]{2,1,0:T(8,128)(2,1)} %v_ref.1, bf16[2,4,128,1024]{3,2,1,0:T(8,128)(2,1)} %tv_ref.1, bf16[2,4,128,1024]{3,2,1,0:T(8,128)(2,1)} %tv_ref.1, f32[4,128]{1,0:T(4,128)} %compare_convert_fusion.valid_ref), custom_call_target="tpu_custom_call" | custom-call | flops 805306368 | bytes 7110656 | tf_op jit(solution)/shard_map/pallas_call | solution.py:188
  26.2 1.2 %dynamic-slice_bitcast_fusion = (f32[136,128]{1,0:T(8,128)S(1)}, f32[136,128]{1,0:T(8,128)S(1)}, f32[136,128]{1,0:T(8,128)S(1)}, f32[136,128]{1,0:T(8,128)S(1)},...) fusion(f32[8,136,128]{2,1,0:T(8,128)} %shard_map.91, ...), kind=kLoop, calls=%fused_computation.18 | loop fusion | bytes 1114144 | tf_op jit(solution)/shard_map/jit(dynamic_index_in_dim)/squeeze | solution.py:60
  27.4 0.4 collective-permute-start.4
  28.1 1.5 %collective-permute-start.5 = (f32[136,128]{1,0:T(8,128)S(1)}, f32[136,128]{1,0:T(8,128)S(1)}, u32[]{:S(2)}, u32[]{:S(2)}) collective-permute-start(f32[136,128]{1,0:T(8,128)S(1)} %get-tuple-element.12), channel_id=1, source_target_pairs={{0,4},{2,6},{4,8},{6,10},{8,12},{10,14},{12,0},{14,2},{1,5},{3,7},... | collective-permute-start | bytes 208904 | tf_op jit(solution)/shard_map/ppermute | solution.py:61
  29.6 2.9 %collective-permute-start.6 = (f32[136,128]{1,0:T(8,128)S(1)}, f32[136,128]{1,0:T(8,128)S(1)}, u32[]{:S(2)}, u32[]{:S(2)}) collective-permute-start(f32[136,128]{1,0:T(8,128)S(1)} %get-tuple-element.11), channel_id=1, source_target_pairs={{0,6},{2,8},{4,10},{6,12},{8,14},{10,0},{12,2},{14,4},{1,7},{3,9},... | collective-permute-start | bytes 208904 | tf_op jit(solution)/shard_map/ppermute | solution.py:61
  32.5 1.8 %collective-permute-start.7 = (f32[136,128]{1,0:T(8,128)S(1)}, f32[136,128]{1,0:T(8,128)S(1)}, u32[]{:S(2)}, u32[]{:S(2)}) collective-permute-start(f32[136,128]{1,0:T(8,128)S(1)} %get-tuple-element.10), channel_id=1, source_target_pairs={{0,8},{2,10},{4,12},{6,14},{8,0},{10,2},{12,4},{14,6},{1,9},{3,11}... | collective-permute-start | bytes 208904 | tf_op jit(solution)/shard_map/ppermute | solution.py:61
  34.3 1.1 %collective-permute-start.8 = (f32[136,128]{1,0:T(8,128)S(1)}, f32[136,128]{1,0:T(8,128)S(1)}, u32[]{:S(2)}, u32[]{:S(2)}) collective-permute-start(f32[136,128]{1,0:T(8,128)S(1)} %get-tuple-element.9), channel_id=1, source_target_pairs={{0,10},{2,12},{4,14},{6,0},{8,2},{10,4},{12,6},{14,8},{1,11},{3,13... | collective-permute-start | bytes 208904 | tf_op jit(solution)/shard_map/ppermute | solution.py:61
  35.4 1.3 %collective-permute-start.9 = (f32[136,128]{1,0:T(8,128)S(1)}, f32[136,128]{1,0:T(8,128)S(1)}, u32[]{:S(2)}, u32[]{:S(2)}) collective-permute-start(f32[136,128]{1,0:T(8,128)S(1)} %get-tuple-element.8), channel_id=1, source_target_pairs={{0,12},{2,14},{4,0},{6,2},{8,4},{10,6},{12,8},{14,10},{1,13},{3,15... | collective-permute-start | bytes 208904 | tf_op jit(solution)/shard_map/ppermute | solution.py:61
  36.7 1.6 %collective-permute-start.10 = (f32[136,128]{1,0:T(8,128)S(1)}, f32[136,128]{1,0:T(8,128)S(1)}, u32[]{:S(2)}, u32[]{:S(2)}) collective-permute-start(f32[136,128]{1,0:T(8,128)S(1)} %get-tuple-element.7), channel_id=1, source_target_pairs={{0,14},{2,0},{4,2},{6,4},{8,6},{10,8},{12,10},{14,12},{1,15},{3,1}... | collective-permute-start | bytes 208904 | tf_op jit(solution)/shard_map/ppermute | solution.py:61
  38.3 1.7 %collective-permute-done.6 = f32[136,128]{1,0:T(8,128)S(1)} collective-permute-done((f32[136,128]{1,0:T(8,128)S(1)}, f32[136,128]{1,0:T(8,128)S(1)}, u32[]{:S(2)}, u32[]{:S(2)}) %collective-permute-start.6) | collective-permute-done | bytes 69664 | tf_op jit(solution)/shard_map/ppermute | solution.py:61
  40.1 1.4 %collective-permute-done.8 = f32[136,128]{1,0:T(8,128)S(1)} collective-permute-done((f32[136,128]{1,0:T(8,128)S(1)}, f32[136,128]{1,0:T(8,128)S(1)}, u32[]{:S(2)}, u32[]{:S(2)}) %collective-permute-start.8) | collective-permute-done | bytes 69664 | tf_op jit(solution)/shard_map/ppermute | solution.py:61
  43.1 1.9 %all_gather.3 = bf16[2,8,2048]{2,0,1:T(2,128)(2,1)S(1)} all-gather(bf16[2,4,2048]{2,0,1:T(2,128)(2,1)S(1)} %copy.56), channel_id=1, replica_groups=mesh['rep'=2,'tp'=8,'sub'=2] {'sub'}, dimensions={1}, use_global_device_ids=true | all-gather | bytes 98304 | tf_op jit(solution)/shard_map/all_gather | solution.py:287
  45.0 12.9 %fusion.1 = f32[16,8192]{1,0:T(8,128)S(1)} fusion(f32[8192]{0:T(1024)S(1)} %dynamic_slice.61, bf16[16,128,8192]{2,1,0:T(8,128)(2,1)} %bitcast.163, bf16[16,16,128]{2,1,0:T(8,128)(2,1)S(1)} %bitcast.155), kind=kOutput, calls=%fused_computation.4 | convolution fusion | flops 543031296 | bytes 34177024 | tf_op jit(solution)/shard_map/rhd,hdf->rhf/dot_general | solution.py:296
  58.3 0.5 constant_dynamic-slice_fusion.8
  58.8 2.2 %collective-permute-start.11 = (f32[16,1024]{1,0:T(8,128)S(1)}, f32[16,1024]{1,0:T(8,128)S(1)}, u32[]{:S(2)}, u32[]{:S(2)}) collective-permute-start(f32[16,1024]{1,0:T(8,128)S(1)} %bitcast.154), channel_id=1, source_target_pairs={{0,2},{2,4},{4,6},{6,8},{8,10},{10,12},{12,14},{14,0},{1,3},{3,5},... | collective-permute-start | bytes 196616 | tf_op jit(solution)/shard_map/ppermute | solution.py:61
  61.1 2.7 %collective-permute-start.12 = (f32[16,1024]{1,0:T(8,128)S(1)}, f32[16,1024]{1,0:T(8,128)S(1)}, u32[]{:S(2)}, u32[]{:S(2)}) collective-permute-start(f32[16,1024]{1,0:T(8,128)S(1)} %bitcast.153), channel_id=1, source_target_pairs={{0,4},{2,6},{4,8},{6,10},{8,12},{10,14},{12,0},{14,2},{1,5},{3,7},... | collective-permute-start | bytes 196616 | tf_op jit(solution)/shard_map/ppermute | solution.py:61
  63.9 0.8 collective-permute-start.13
  64.7 1.8 %collective-permute-start.14 = (f32[16,1024]{1,0:T(8,128)S(1)}, f32[16,1024]{1,0:T(8,128)S(1)}, u32[]{:S(2)}, u32[]{:S(2)}) collective-permute-start(f32[16,1024]{1,0:T(8,128)S(1)} %bitcast.149), channel_id=1, source_target_pairs={{0,8},{2,10},{4,12},{6,14},{8,0},{10,2},{12,4},{14,6},{1,9},{3,11}... | collective-permute-start | bytes 196616 | tf_op jit(solution)/shard_map/ppermute | solution.py:61
  66.5 2.9 %collective-permute-start.15 = (f32[16,1024]{1,0:T(8,128)S(1)}, f32[16,1024]{1,0:T(8,128)S(1)}, u32[]{:S(2)}, u32[]{:S(2)}) collective-permute-start(f32[16,1024]{1,0:T(8,128)S(1)} %bitcast.150), channel_id=1, source_target_pairs={{0,10},{2,12},{4,14},{6,0},{8,2},{10,4},{12,6},{14,8},{1,11},{3,13... | collective-permute-start | bytes 196616 | tf_op jit(solution)/shard_map/ppermute | solution.py:61
  69.4 1.3 %collective-permute-start.16 = (f32[16,1024]{1,0:T(8,128)S(1)}, f32[16,1024]{1,0:T(8,128)S(1)}, u32[]{:S(2)}, u32[]{:S(2)}) collective-permute-start(f32[16,1024]{1,0:T(8,128)S(1)} %bitcast.152), channel_id=1, source_target_pairs={{0,12},{2,14},{4,0},{6,2},{8,4},{10,6},{12,8},{14,10},{1,13},{3,15... | collective-permute-start | bytes 196616 | tf_op jit(solution)/shard_map/ppermute | solution.py:61
  70.7 1.2 %collective-permute-start.17 = (f32[16,1024]{1,0:T(8,128)S(1)}, f32[16,1024]{1,0:T(8,128)S(1)}, u32[]{:S(2)}, u32[]{:S(2)}) collective-permute-start(f32[16,1024]{1,0:T(8,128)S(1)} %bitcast.151), channel_id=1, source_target_pairs={{0,14},{2,0},{4,2},{6,4},{8,6},{10,8},{12,10},{14,12},{1,15},{3,1}... | collective-permute-start | bytes 196616 | tf_op jit(solution)/shard_map/ppermute | solution.py:61
  72.0 0.5 collective-permute-done.13
  72.4 0.9 collective-permute-done.14
  73.3 1.0 %collective-permute-done.15 = f32[16,1024]{1,0:T(8,128)S(1)} collective-permute-done((f32[16,1024]{1,0:T(8,128)S(1)}, f32[16,1024]{1,0:T(8,128)S(1)}, u32[]{:S(2)}, u32[]{:S(2)}) %collective-permute-start.15) | collective-permute-done | bytes 65568 | tf_op jit(solution)/shard_map/ppermute | solution.py:61
  74.3 1.2 %collective-permute-done.16 = f32[16,1024]{1,0:T(8,128)S(1)} collective-permute-done((f32[16,1024]{1,0:T(8,128)S(1)}, f32[16,1024]{1,0:T(8,128)S(1)}, u32[]{:S(2)}, u32[]{:S(2)}) %collective-permute-start.16) | collective-permute-done | bytes 65568 | tf_op jit(solution)/shard_map/ppermute | solution.py:61
  75.6 2.2 %collective-permute-start.18 = (bf16[16,1024]{1,0:T(8,128)(2,1)S(1)}, bf16[16,1024]{1,0:T(8,128)(2,1)S(1)}, u32[]{:S(2)}, u32[]{:S(2)}) collective-permute-start(bf16[16,1024]{1,0:T(8,128)(2,1)S(1)} %clamp_convert_fusion), channel_id=1, source_target_pairs={{0,2},{2,0},{4,6},{6,4},{8,10},{10,8},{12,14},{14,12},{1,3},{3,1},... | collective-permute-start | bytes 98312 | tf_op jit(solution)/shard_map/ppermute | solution.py:28
  77.8 1.9 %collective-permute-done.18 = bf16[16,1024]{1,0:T(8,128)(2,1)S(1)} collective-permute-done((bf16[16,1024]{1,0:T(8,128)(2,1)S(1)}, bf16[16,1024]{1,0:T(8,128)(2,1)S(1)}, u32[]{:S(2)}, u32[]{:S(2)}) %collective-permute-start.18) | collective-permute-done | bytes 32800 | tf_op jit(solution)/shard_map/ppermute | solution.py:28
  79.7 1.8 %collective-permute-start.19 = (bf16[2,16,1024]{2,1,0:T(8,128)(2,1)S(1)}, bf16[2,16,1024]{2,1,0:T(8,128)(2,1)S(1)}, u32[]{:S(2)}, u32[]{:S(2)}) collective-permute-start(bf16[2,16,1024]{2,1,0:T(8,128)(2,1)S(1)} %maximum_select_fusion.3), channel_id=1, source_target_pairs={{0,4},{2,6},{4,8},{6,10},{8,12},{10,14},{12,0},{14,2},{1,5},{3,7},... | collective-permute-start | bytes 196616 | tf_op jit(solution)/shard_map/ppermute | solution.py:34
  81.5 1.3 %collective-permute-start.20 = (bf16[2,16,1024]{2,1,0:T(8,128)(2,1)S(1)}, bf16[2,16,1024]{2,1,0:T(8,128)(2,1)S(1)}, u32[]{:S(2)}, u32[]{:S(2)}) collective-permute-start(bf16[2,16,1024]{2,1,0:T(8,128)(2,1)S(1)} %maximum_select_fusion.3), channel_id=1, source_target_pairs={{0,8},{2,10},{4,12},{6,14},{8,0},{10,2},{12,4},{14,6},{1,9},{3,11}... | collective-permute-start | bytes 196616 | tf_op jit(solution)/shard_map/ppermute | solution.py:34
  82.8 1.1 %collective-permute-start.21 = (bf16[2,16,1024]{2,1,0:T(8,128)(2,1)S(1)}, bf16[2,16,1024]{2,1,0:T(8,128)(2,1)S(1)}, u32[]{:S(2)}, u32[]{:S(2)}) collective-permute-start(bf16[2,16,1024]{2,1,0:T(8,128)(2,1)S(1)} %maximum_select_fusion.3), channel_id=1, source_target_pairs={{0,12},{2,14},{4,0},{6,2},{8,4},{10,6},{12,8},{14,10},{1,13},{3,15... | collective-permute-start | bytes 196616 | tf_op jit(solution)/shard_map/ppermute | solution.py:34
  84.0 2.5 %collective-permute-done.19 = bf16[2,16,1024]{2,1,0:T(8,128)(2,1)S(1)} collective-permute-done((bf16[2,16,1024]{2,1,0:T(8,128)(2,1)S(1)}, bf16[2,16,1024]{2,1,0:T(8,128)(2,1)S(1)}, u32[]{:S(2)}, u32[]{:S(2)}) %collective-permute-start.19) | collective-permute-done | bytes 65568 | tf_op jit(solution)/shard_map/ppermute | solution.py:34
  86.4 1.3 %collective-permute-done.20 = bf16[2,16,1024]{2,1,0:T(8,128)(2,1)S(1)} collective-permute-done((bf16[2,16,1024]{2,1,0:T(8,128)(2,1)S(1)}, bf16[2,16,1024]{2,1,0:T(8,128)(2,1)S(1)}, u32[]{:S(2)}, u32[]{:S(2)}) %collective-permute-start.20) | collective-permute-done | bytes 65568 | tf_op jit(solution)/shard_map/ppermute | solution.py:34
  87.8 0.7 scatter_fusion.1
  89.0 0.8 add_convert_fusion
  (81 shorter events, 3.9 us)
Async XLA Ops:
  0.0 7.2 %collective-permute-start = (bf16[2,4,2048]{2,1,0:T(4,128)(2,1)}, bf16[2,4,2048]{2,1,0:T(4,128)(2,1)S(1)}, u32[]{:S(2)}, u32[]{:S(2)}) collective-permute-start(bf16[2,4,2048]{2,1,0:T(4,128)(2,1)} %param.9), channel_id=1, source_target_pairs={{0,2},{2,0},{4,6},{6,4},{8,10},{10,8},{12,14},{14,12},{1,3},{3,1},... | collective-permute-start | bytes 98312 | tf_op jit(solution)/shard_map/ppermute | solution.py:28
  8.1 6.9 %collective-permute-start.1 = (bf16[2,2,4,2048]{3,2,1,0:T(4,128)(2,1)S(1)}, bf16[2,2,4,2048]{3,2,1,0:T(4,128)(2,1)S(1)}, u32[]{:S(2)}, u32[]{:S(2)}) collective-permute-start(bf16[2,2,4,2048]{3,2,1,0:T(4,128)(2,1)S(1)} %maximum_select_fusion.1), channel_id=1, source_target_pairs={{0,4},{2,6},{4,8},{6,10},{8,12},{10,14},{12,0},{14,2},{1,5},{3,7},... | collective-permute-start | bytes 196616 | tf_op jit(solution)/shard_map/ppermute | solution.py:34
  9.7 7.3 %collective-permute-start.2 = (bf16[2,2,4,2048]{3,2,1,0:T(4,128)(2,1)S(1)}, bf16[2,2,4,2048]{3,2,1,0:T(4,128)(2,1)S(1)}, u32[]{:S(2)}, u32[]{:S(2)}) collective-permute-start(bf16[2,2,4,2048]{3,2,1,0:T(4,128)(2,1)S(1)} %maximum_select_fusion.1), channel_id=1, source_target_pairs={{0,8},{2,10},{4,12},{6,14},{8,0},{10,2},{12,4},{14,6},{1,9},{3,11}... | collective-permute-start | bytes 196616 | tf_op jit(solution)/shard_map/ppermute | solution.py:34
  12.3 4.8 %collective-permute-start.3 = (bf16[2,2,4,2048]{3,2,1,0:T(4,128)(2,1)S(1)}, bf16[2,2,4,2048]{3,2,1,0:T(4,128)(2,1)S(1)}, u32[]{:S(2)}, u32[]{:S(2)}) collective-permute-start(bf16[2,2,4,2048]{3,2,1,0:T(4,128)(2,1)S(1)} %maximum_select_fusion.1), channel_id=1, source_target_pairs={{0,12},{2,14},{4,0},{6,2},{8,4},{10,6},{12,8},{14,10},{1,13},{3,15... | collective-permute-start | bytes 196616 | tf_op jit(solution)/shard_map/ppermute | solution.py:34
  27.4 8.0 %collective-permute-start.4 = (f32[136,128]{1,0:T(8,128)S(1)}, f32[136,128]{1,0:T(8,128)S(1)}, u32[]{:S(2)}, u32[]{:S(2)}) collective-permute-start(f32[136,128]{1,0:T(8,128)S(1)} %get-tuple-element.13), channel_id=1, source_target_pairs={{0,2},{2,4},{4,6},{6,8},{8,10},{10,12},{12,14},{14,0},{1,3},{3,5},... | collective-permute-start | bytes 208904 | tf_op jit(solution)/shard_map/ppermute | solution.py:61
  28.1 8.6 %collective-permute-start.5 = (f32[136,128]{1,0:T(8,128)S(1)}, f32[136,128]{1,0:T(8,128)S(1)}, u32[]{:S(2)}, u32[]{:S(2)}) collective-permute-start(f32[136,128]{1,0:T(8,128)S(1)} %get-tuple-element.12), channel_id=1, source_target_pairs={{0,4},{2,6},{4,8},{6,10},{8,12},{10,14},{12,0},{14,2},{1,5},{3,7},... | collective-permute-start | bytes 208904 | tf_op jit(solution)/shard_map/ppermute | solution.py:61
  29.6 10.5 %collective-permute-start.6 = (f32[136,128]{1,0:T(8,128)S(1)}, f32[136,128]{1,0:T(8,128)S(1)}, u32[]{:S(2)}, u32[]{:S(2)}) collective-permute-start(f32[136,128]{1,0:T(8,128)S(1)} %get-tuple-element.11), channel_id=1, source_target_pairs={{0,6},{2,8},{4,10},{6,12},{8,14},{10,0},{12,2},{14,4},{1,7},{3,9},... | collective-permute-start | bytes 208904 | tf_op jit(solution)/shard_map/ppermute | solution.py:61
  32.5 7.5 %collective-permute-start.7 = (f32[136,128]{1,0:T(8,128)S(1)}, f32[136,128]{1,0:T(8,128)S(1)}, u32[]{:S(2)}, u32[]{:S(2)}) collective-permute-start(f32[136,128]{1,0:T(8,128)S(1)} %get-tuple-element.10), channel_id=1, source_target_pairs={{0,8},{2,10},{4,12},{6,14},{8,0},{10,2},{12,4},{14,6},{1,9},{3,11}... | collective-permute-start | bytes 208904 | tf_op jit(solution)/shard_map/ppermute | solution.py:61
  34.3 7.1 %collective-permute-start.8 = (f32[136,128]{1,0:T(8,128)S(1)}, f32[136,128]{1,0:T(8,128)S(1)}, u32[]{:S(2)}, u32[]{:S(2)}) collective-permute-start(f32[136,128]{1,0:T(8,128)S(1)} %get-tuple-element.9), channel_id=1, source_target_pairs={{0,10},{2,12},{4,14},{6,0},{8,2},{10,4},{12,6},{14,8},{1,11},{3,13... | collective-permute-start | bytes 208904 | tf_op jit(solution)/shard_map/ppermute | solution.py:61
  35.4 6.1 %collective-permute-start.9 = (f32[136,128]{1,0:T(8,128)S(1)}, f32[136,128]{1,0:T(8,128)S(1)}, u32[]{:S(2)}, u32[]{:S(2)}) collective-permute-start(f32[136,128]{1,0:T(8,128)S(1)} %get-tuple-element.8), channel_id=1, source_target_pairs={{0,12},{2,14},{4,0},{6,2},{8,4},{10,6},{12,8},{14,10},{1,13},{3,15... | collective-permute-start | bytes 208904 | tf_op jit(solution)/shard_map/ppermute | solution.py:61
  36.7 4.8 %collective-permute-start.10 = (f32[136,128]{1,0:T(8,128)S(1)}, f32[136,128]{1,0:T(8,128)S(1)}, u32[]{:S(2)}, u32[]{:S(2)}) collective-permute-start(f32[136,128]{1,0:T(8,128)S(1)} %get-tuple-element.7), channel_id=1, source_target_pairs={{0,14},{2,0},{4,2},{6,4},{8,6},{10,8},{12,10},{14,12},{1,15},{3,1}... | collective-permute-start | bytes 208904 | tf_op jit(solution)/shard_map/ppermute | solution.py:61
  45.0 18.8 %copy-start.1 = (s32[128]{0:T(128)S(1)}, s32[128]{0:T(128)}, u32[]{:S(2)}) copy-start(s32[128]{0:T(128)} %param.16) | copy-start | bytes 1540
  57.9 31.0 %copy-start = (bf16[2,8,8192]{2,1,0:T(8,128)(2,1)S(1)}, bf16[2,8,8192]{2,1,0:T(8,128)(2,1)}, u32[]{:S(2)}) copy-start(bf16[2,8,8192]{2,1,0:T(8,128)(2,1)} %param.17) | copy-start | bytes 786436
  58.8 10.6 %collective-permute-start.11 = (f32[16,1024]{1,0:T(8,128)S(1)}, f32[16,1024]{1,0:T(8,128)S(1)}, u32[]{:S(2)}, u32[]{:S(2)}) collective-permute-start(f32[16,1024]{1,0:T(8,128)S(1)} %bitcast.154), channel_id=1, source_target_pairs={{0,2},{2,4},{4,6},{6,8},{8,10},{10,12},{12,14},{14,0},{1,3},{3,5},... | collective-permute-start | bytes 196616 | tf_op jit(solution)/shard_map/ppermute | solution.py:61
  61.1 9.6 %collective-permute-start.12 = (f32[16,1024]{1,0:T(8,128)S(1)}, f32[16,1024]{1,0:T(8,128)S(1)}, u32[]{:S(2)}, u32[]{:S(2)}) collective-permute-start(f32[16,1024]{1,0:T(8,128)S(1)} %bitcast.153), channel_id=1, source_target_pairs={{0,4},{2,6},{4,8},{6,10},{8,12},{10,14},{12,0},{14,2},{1,5},{3,7},... | collective-permute-start | bytes 196616 | tf_op jit(solution)/shard_map/ppermute | solution.py:61
  63.9 8.6 %collective-permute-start.13 = (f32[16,1024]{1,0:T(8,128)S(1)}, f32[16,1024]{1,0:T(8,128)S(1)}, u32[]{:S(2)}, u32[]{:S(2)}) collective-permute-start(f32[16,1024]{1,0:T(8,128)S(1)} %bitcast.148), channel_id=1, source_target_pairs={{0,6},{2,8},{4,10},{6,12},{8,14},{10,0},{12,2},{14,4},{1,7},{3,9},... | collective-permute-start | bytes 196616 | tf_op jit(solution)/shard_map/ppermute | solution.py:61
  64.7 8.6 %collective-permute-start.14 = (f32[16,1024]{1,0:T(8,128)S(1)}, f32[16,1024]{1,0:T(8,128)S(1)}, u32[]{:S(2)}, u32[]{:S(2)}) collective-permute-start(f32[16,1024]{1,0:T(8,128)S(1)} %bitcast.149), channel_id=1, source_target_pairs={{0,8},{2,10},{4,12},{6,14},{8,0},{10,2},{12,4},{14,6},{1,9},{3,11}... | collective-permute-start | bytes 196616 | tf_op jit(solution)/shard_map/ppermute | solution.py:61
  66.5 7.8 %collective-permute-start.15 = (f32[16,1024]{1,0:T(8,128)S(1)}, f32[16,1024]{1,0:T(8,128)S(1)}, u32[]{:S(2)}, u32[]{:S(2)}) collective-permute-start(f32[16,1024]{1,0:T(8,128)S(1)} %bitcast.150), channel_id=1, source_target_pairs={{0,10},{2,12},{4,14},{6,0},{8,2},{10,4},{12,6},{14,8},{1,11},{3,13... | collective-permute-start | bytes 196616 | tf_op jit(solution)/shard_map/ppermute | solution.py:61
  69.4 6.1 %collective-permute-start.16 = (f32[16,1024]{1,0:T(8,128)S(1)}, f32[16,1024]{1,0:T(8,128)S(1)}, u32[]{:S(2)}, u32[]{:S(2)}) collective-permute-start(f32[16,1024]{1,0:T(8,128)S(1)} %bitcast.152), channel_id=1, source_target_pairs={{0,12},{2,14},{4,0},{6,2},{8,4},{10,6},{12,8},{14,10},{1,13},{3,15... | collective-permute-start | bytes 196616 | tf_op jit(solution)/shard_map/ppermute | solution.py:61
  70.7 4.9 %collective-permute-start.17 = (f32[16,1024]{1,0:T(8,128)S(1)}, f32[16,1024]{1,0:T(8,128)S(1)}, u32[]{:S(2)}, u32[]{:S(2)}) collective-permute-start(f32[16,1024]{1,0:T(8,128)S(1)} %bitcast.151), channel_id=1, source_target_pairs={{0,14},{2,0},{4,2},{6,4},{8,6},{10,8},{12,10},{14,12},{1,15},{3,1}... | collective-permute-start | bytes 196616 | tf_op jit(solution)/shard_map/ppermute | solution.py:61
  75.6 4.1 %collective-permute-start.18 = (bf16[16,1024]{1,0:T(8,128)(2,1)S(1)}, bf16[16,1024]{1,0:T(8,128)(2,1)S(1)}, u32[]{:S(2)}, u32[]{:S(2)}) collective-permute-start(bf16[16,1024]{1,0:T(8,128)(2,1)S(1)} %clamp_convert_fusion), channel_id=1, source_target_pairs={{0,2},{2,0},{4,6},{6,4},{8,10},{10,8},{12,14},{14,12},{1,3},{3,1},... | collective-permute-start | bytes 98312 | tf_op jit(solution)/shard_map/ppermute | solution.py:28
  79.7 6.7 %collective-permute-start.19 = (bf16[2,16,1024]{2,1,0:T(8,128)(2,1)S(1)}, bf16[2,16,1024]{2,1,0:T(8,128)(2,1)S(1)}, u32[]{:S(2)}, u32[]{:S(2)}) collective-permute-start(bf16[2,16,1024]{2,1,0:T(8,128)(2,1)S(1)} %maximum_select_fusion.3), channel_id=1, source_target_pairs={{0,4},{2,6},{4,8},{6,10},{8,12},{10,14},{12,0},{14,2},{1,5},{3,7},... | collective-permute-start | bytes 196616 | tf_op jit(solution)/shard_map/ppermute | solution.py:34
  81.5 6.3 %collective-permute-start.20 = (bf16[2,16,1024]{2,1,0:T(8,128)(2,1)S(1)}, bf16[2,16,1024]{2,1,0:T(8,128)(2,1)S(1)}, u32[]{:S(2)}, u32[]{:S(2)}) collective-permute-start(bf16[2,16,1024]{2,1,0:T(8,128)(2,1)S(1)} %maximum_select_fusion.3), channel_id=1, source_target_pairs={{0,8},{2,10},{4,12},{6,14},{8,0},{10,2},{12,4},{14,6},{1,9},{3,11}... | collective-permute-start | bytes 196616 | tf_op jit(solution)/shard_map/ppermute | solution.py:34
  82.8 4.9 %collective-permute-start.21 = (bf16[2,16,1024]{2,1,0:T(8,128)(2,1)S(1)}, bf16[2,16,1024]{2,1,0:T(8,128)(2,1)S(1)}, u32[]{:S(2)}, u32[]{:S(2)}) collective-permute-start(bf16[2,16,1024]{2,1,0:T(8,128)(2,1)S(1)} %maximum_select_fusion.3), channel_id=1, source_target_pairs={{0,12},{2,14},{4,0},{6,2},{8,4},{10,6},{12,8},{14,10},{1,13},{3,15... | collective-permute-start | bytes 196616 | tf_op jit(solution)/shard_map/ppermute | solution.py:34

commit v12 on v7

--- a/solution.py
+++ b/solution.py
@@ -1,3 +1,4 @@
+import functools
 import math
 
 import jax
@@ -137,6 +138,206 @@
     )(q_rows, prefix_kv, prefix_kv, tail_kv, tail_kv, valid)
 
 
+def _pairs_kernel(u_ref, q_ref, k_ref, v_ref, tko_ref, tvo_ref, tkp_ref, tvp_ref,
+                  valid_o_ref, valid_p_ref, out_ref, *, group):
+    heads_n, rows_n = q_ref.shape[0], q_ref.shape[1]
+    per_core, tail_dev = tko_ref.shape[1], tko_ref.shape[2]
+    samples = 2 * per_core
+    u = u_ref[0]
+    score_scale = 1.0 / math.sqrt(DH)
+    dims_nt = (((1,), (1,)), ((), ()))
+    row_sample = (lax.broadcasted_iota(jnp.int32, (rows_n, tail_dev), 0) // group) % samples
+    sources = [(tko_ref, tvo_ref, valid_o_ref, u * per_core),
+               (tkp_ref, tvp_ref, valid_p_ref, (1 - u) * per_core)]
+    for j in range(heads_n):
+        cols = slice(j * DH, (j + 1) * DH)
+        q = q_ref[j]
+        p_scores = lax.dot_general(q, k_ref[0, :, cols], dims_nt, preferred_element_type=jnp.float32)
+        p_scores = p_scores * score_scale
+        t_scores = jnp.full((rows_n, tail_dev), NEG_FILL, jnp.float32)
+        for tk_ref, _, valid_ref, first in sources:
+            for r in range(per_core):
+                sr = lax.dot_general(
+                    q, tk_ref[0, r, :, cols], dims_nt, preferred_element_type=jnp.float32
+                )
+                live = (row_sample == first + r) & (valid_ref[r:r + 1, :] > 0.0)
+                t_scores = jnp.where(live, sr * score_scale, t_scores)
+        peak = jnp.maximum(
+            jnp.max(p_scores, axis=1, keepdims=True), jnp.max(t_scores, axis=1, keepdims=True)
+        )
+        p_w = jnp.exp(p_scores - peak)
+        t_w = jnp.exp(t_scores - peak)
+        mass = jnp.sum(p_w, axis=1, keepdims=True) + jnp.sum(t_w, axis=1, keepdims=True)
+        numer = jnp.dot(
+            p_w.astype(jnp.bfloat16), v_ref[0, :, cols], preferred_element_type=jnp.float32
+        )
+        for _, tv_ref, _, first in sources:
+            for r in range(per_core):
+                t_w16 = jnp.where(row_sample == first + r, t_w, 0.0).astype(jnp.bfloat16)
+                numer = numer + jnp.dot(
+                    t_w16, tv_ref[0, r, :, cols], preferred_element_type=jnp.float32
+                )
+        out_ref[j, :rows_n, :] = numer
+        stat_rows = []
+        for col in (peak, mass):
+            for c in range(rows_n // DH):
+                part = jnp.broadcast_to(col[c * DH:(c + 1) * DH], (DH, DH))
+                stat_rows.append(jnp.transpose(part)[0:1])
+        pad = out_ref.shape[1] - rows_n - len(stat_rows)
+        out_ref[j, rows_n:, :] = jnp.concatenate(
+            stat_rows + [jnp.zeros((pad, DH), jnp.float32)], axis=0
+        )
+
+
+def _attend_pairs(u, q_rows, prefix_kv, tail_own, tail_peer, valid_own, valid_peer, group):
+    heads_n, rows_n, _ = q_rows.shape
+    prefix_dev = prefix_kv.shape[1]
+    per_core, tail_dev = tail_own.shape[1], tail_own.shape[2]
+    width = heads_n * DH
+    n_out = rows_n + 8 * (-(-(2 * rows_n // DH) // 8))
+    grid_spec = pltpu.PrefetchScalarGridSpec(
+        num_scalar_prefetch=1,
+        grid=(1,),
+        in_specs=[
+            pl.BlockSpec((heads_n, rows_n, DH), lambda i, u_ref: (0, 0, 0)),
+            pl.BlockSpec((1, prefix_dev, width), lambda i, u_ref: (0, 0, u_ref[0])),
+            pl.BlockSpec((1, prefix_dev, width), lambda i, u_ref: (1, 0, u_ref[0])),
+            pl.BlockSpec((1, per_core, tail_dev, width), lambda i, u_ref: (0, 0, 0, u_ref[0])),
+            pl.BlockSpec((1, per_core, tail_dev, width), lambda i, u_ref: (1, 0, 0, u_ref[0])),
+            pl.BlockSpec((1, per_core, tail_dev, width), lambda i, u_ref: (0, 0, 0, 0)),
+            pl.BlockSpec((1, per_core, tail_dev, width), lambda i, u_ref: (1, 0, 0, 0)),
+            pl.BlockSpec((per_core, tail_dev), lambda i, u_ref: (0, 0)),
+            pl.BlockSpec((per_core, tail_dev), lambda i, u_ref: (0, 0)),
+        ],
+        out_specs=pl.BlockSpec((heads_n, n_out, DH), lambda i, u_ref: (0, 0, 0)),
+    )
+    flops = 4 * heads_n * rows_n * DH * (prefix_dev + 2 * per_core * tail_dev)
+    return pl.pallas_call(
+        functools.partial(_pairs_kernel, group=group),
+        grid_spec=grid_spec,
+        out_shape=jax.ShapeDtypeStruct((heads_n, n_out, DH), jnp.float32),
+        cost_estimate=pl.CostEstimate(
+            flops=flops,
+            transcendentals=heads_n * rows_n * (prefix_dev + 2 * per_core * tail_dev),
+            bytes_accessed=2 * (2 * prefix_dev * width + 4 * per_core * tail_dev * width
+                                + q_rows.size) + 4 * heads_n * n_out * DH,
+        ),
+    )(jnp.reshape(u, (1,)).astype(jnp.int32), q_rows, prefix_kv, prefix_kv, tail_own, tail_own,
+      tail_peer, tail_peer, valid_own, valid_peer)
+
+
+def _linear(t, s):
+    return t * 2 + s
+
+
+def _g_pairs(k, chips):
+    quarter = chips // 2
+    pairs = []
+    for t in range(chips):
+        h, i = t // quarter, t % quarter
+        pairs.append((_linear(t, h), _linear((1 - h) * quarter + (i + k) % quarter, h)))
+        if k < quarter:
+            pairs.append((_linear(t, 1 - h), _linear(h * quarter + (i + k) % quarter, h)))
+    return pairs
+
+
+def _e_pairs(k, chips):
+    quarter = chips // 2
+    pairs = []
+    for t in range(chips):
+        h, i = t // quarter, t % quarter
+        for u in (0, 1):
+            dst = u * quarter + (i + k) % quarter
+            if h != u:
+                pairs.append((_linear(t, u), _linear(dst, 1 - u)))
+            elif k < quarter:
+                pairs.append((_linear(t, u), _linear(dst, u)))
+    return pairs
+
+
+def _combine(src, rows_n):
+    n = src.shape[0]
+    numer = src[:, :rows_n]
+    stat = src[:, rows_n:rows_n + 2 * rows_n // DH].reshape(n, 2, rows_n)
+    peak, mass = stat[:, 0], stat[:, 1]
+    top = peak.max(0)
+    w = jnp.exp(peak - top[None])
+    return (numer * w[..., None]).sum(0), top, (mass * w).sum(0)
+
+
+def _attention_pairs(queries, prefix_kv, tail_kv, tail_lengths, fresh_kv, tp_count, tp_rank,
+                     sub_rank, group):
+    steps_n, rows_dev, width_dev = queries.shape
+    quarter = tp_count // 2
+    tail_dev = tail_kv.shape[2]
+    u = sub_rank
+    i = tp_rank % quarter
+    within = tp_rank // quarter == u
+    swap = [(0, 1), (1, 0)]
+    peer_cols = lax.dynamic_slice_in_dim(tail_kv, (1 - u) * quarter * DH, quarter * DH, 3)
+    tail_peer = lax.ppermute(peer_cols, "sub", swap)
+    lengths_peer = lax.ppermute(tail_lengths, "sub", swap)
+    fresh_peer = lax.ppermute(fresh_kv, "sub", swap)
+    t_pos = tp_rank * tail_dev + jnp.arange(tail_dev)
+    valid_own = (t_pos[None, :] < tail_lengths[:, None]).astype(jnp.float32)
+    valid_peer = (t_pos[None, :] < lengths_peer[:, None]).astype(jnp.float32)
+
+    q_both = lax.all_gather(queries, "sub", axis=1, tiled=True)
+    blocks = []
+    for k in range(1, quarter + 1):
+        got = lax.ppermute(q_both, ("tp", "sub"), _g_pairs(k, tp_count))
+        if k == quarter:
+            got = jnp.where(within, q_both, got)
+        blocks.append(got)
+    order = (i - jnp.arange(1, quarter + 1)) % quarter
+    q_heads = jnp.zeros((quarter,) + q_both.shape, q_both.dtype).at[order].set(jnp.stack(blocks))
+    q_rows = q_heads.reshape(quarter, -1, DH)
+    rows_n = q_rows.shape[1]
+    part = _attend_pairs(u, q_rows, prefix_kv, tail_kv, tail_peer, valid_own, valid_peer, group)
+
+    srcs = []
+    for k in range(1, quarter + 1):
+        send = lax.dynamic_index_in_dim(part, (i + k) % quarter, 0, keepdims=False)
+        got = lax.ppermute(send, ("tp", "sub"), _e_pairs(k, tp_count))
+        if k == quarter:
+            own = lax.dynamic_index_in_dim(part, i, 0, keepdims=False)
+            got = jnp.where(within, own, got)
+        srcs.append(got)
+    numer_c, peak_c, mass_c = _combine(jnp.stack(srcs), rows_n)
+    n_stat = part.shape[1] - rows_n
+    stats = jnp.concatenate([peak_c, mass_c]).reshape(-1, DH)
+    stats = jnp.pad(stats, ((0, n_stat - stats.shape[0]), (0, 0)))
+    both = lax.all_gather(jnp.concatenate([numer_c, stats]), "sub", axis=0, tiled=False)
+    numer_2 = both[:, :rows_n]
+    stat_2 = both[:, rows_n:rows_n + 2 * rows_n // DH].reshape(2, 2, rows_n)
+
+    heads_dev = width_dev // DH
+    score_scale = 1.0 / math.sqrt(DH)
+    fresh_all = jnp.where(
+        u == 0, jnp.concatenate([fresh_kv, fresh_peer], 2), jnp.concatenate([fresh_peer, fresh_kv], 2)
+    )
+    f_kv = lax.dynamic_slice_in_dim(fresh_all, tp_rank * DH, DH, 3)
+    own_query = q_both.reshape(steps_n, 2 * rows_dev, heads_dev, DH)
+    f_scores = (
+        jnp.einsum("sbhd,ubd->sbhu", own_query, f_kv[0], preferred_element_type=jnp.float32)
+        * score_scale
+    )
+    fresh_live = jnp.arange(steps_n)[None, :] <= jnp.arange(steps_n)[:, None]
+    f_scores = jnp.where(fresh_live[:, None, None, :], f_scores, NEG_FILL).reshape(rows_n, steps_n)
+    peak_2 = stat_2[:, 0]
+    top = jnp.maximum(peak_2.max(0), f_scores.max(-1))
+    w2 = jnp.exp(peak_2 - top[None])
+    f_w = jnp.exp(f_scores - top[:, None])
+    mass = (stat_2[:, 1] * w2).sum(0) + f_w.sum(-1)
+    numer = (numer_2 * w2[..., None]).sum(0)
+    f_w16 = f_w.astype(jnp.bfloat16).reshape(steps_n, 2 * rows_dev, heads_dev, steps_n)
+    numer = numer + jnp.einsum(
+        "sbhu,ubd->sbhd", f_w16, f_kv[1], preferred_element_type=jnp.float32
+    ).reshape(rows_n, DH)
+    attended = (numer / mass[:, None]).astype(jnp.bfloat16)
+    return attended.reshape(steps_n, 2 * rows_dev, width_dev)
+
+
 def per_device(
     queries, prefix_kv, tail_kv, tail_lengths, fresh_kv, out_weight, scale_in, scale_out, residual
 ):
@@ -152,6 +353,16 @@
     tail_dev = tail_kv.shape[2]
     score_scale = 1.0 / math.sqrt(DH)
 
+    pairs_ok = (
+        tp_count == kv_heads and heads_dev == group and tp_count % 4 == 0
+        and lax.axis_size("sub") == 2
+    )
+    if pairs_ok:
+        gathered = _attention_pairs(
+            queries, prefix_kv, tail_kv, tail_lengths, fresh_kv, tp_count, tp_rank, sub_rank, group
+        )
+        return _project(gathered, out_weight, scale_in, scale_out, residual, tp_count, tp_rank,
+                        sub_rank)
     q_blocks = _gather_blocks(queries, "tp", tp_count)
     q_all = jnp.moveaxis(q_blocks, 0, 2).reshape(steps_n, rows_dev, kv_heads, group, DH)
     q_rows = jnp.transpose(q_all, (2, 1, 0, 3, 4)).reshape(kv_heads, -1, DH)
@@ -205,7 +416,13 @@
     attended = (numer / mass[..., None]).astype(jnp.bfloat16).reshape(steps_n, rows_dev, width_dev)
 
     gathered = lax.all_gather(attended, "sub", axis=1, tiled=True)
-    samples = gathered.shape[1]
+    return _project(gathered, out_weight, scale_in, scale_out, residual, tp_count, tp_rank,
+                    sub_rank)
+
+
+def _project(gathered, out_weight, scale_in, scale_out, residual, tp_count, tp_rank, sub_rank):
+    steps_n, samples, width_dev = gathered.shape
+    heads_dev = width_dev // DH
     local_width = out_weight.shape[1]
     head_rows_in = gathered.reshape(steps_n * samples, heads_dev, DH)
     head_weights = out_weight.reshape(heads_dev, DH, local_width)

time: 87.9 us -> 98.3 us (1.12)
  blocking collectives: 1.85 us -> 11.2 us
  starting transfers between devices: 38.4 us -> 35.2 us
  Pallas kernels: 5.42 us -> 6.96 us
  waiting for transfers between devices: 14.9 us -> 16.1 us
  local copies, waits for them, and re-layouts: 7.95 us -> 9.14 us
    ppermute x0 -> x11, starting transfers between devices: none -> 15.4 us  [the longest x4 11.7 us: _attention_pairs(): got = lax.ppermute(q_both, ('tp', 'sub'), _g_pairs(k, tp_count))]
    ppermute x14 -> x7, starting transfers between devices: 23.3 us -> 13.1 us  [_exchange(): lax.ppermute(send, axis_name, [(i, (i + k) % count) for i in range(count)])]
    all_gather x1 -> x2, blocking collectives: 1.85 us -> 11.2 us  [the longest x1 9.24 us: _attention_pairs(): lax.all_gather(jnp.concatenate([numer_c, stats]), 'sub', axis=0, tiled=Fa...]
    ppermute x0 -> x11, waiting for transfers between devices: none -> 7.43 us  [the longest x4 5.61 us: _attention_pairs(): got = lax.ppermute(send, ('tp', 'sub'), _e_pairs(k, tp_count))]
    ppermute x6 -> x3, starting transfers between devices: 9.99 us -> 4.47 us  [_gather_blocks(): lax.ppermute(pair, axis_name, [(i, (i + 2 * d) % count) for i in range(co...]
    ppermute x14 -> x7, waiting for transfers between devices: 6.55 us -> 2.68 us  [_exchange(): lax.ppermute(send, axis_name, [(i, (i + k) % count) for i in range(count)])]
    ppermute x2 -> x1, starting transfers between devices: 5.16 us -> 2.23 us  [_gather_blocks(): other = lax.ppermute(x, axis_name, [(i, i ^ 1) for i in range(count)])]
    ppermute x6 -> x3, waiting for transfers between devices: 6.46 us -> 4.17 us  [_gather_blocks(): lax.ppermute(pair, axis_name, [(i, (i + 2 * d) % count) for i in range(co...]
  transfers between devices with their start and end apart: 22 -> 22, of which waited for: 14 -> 11; matrix products, arithmetic and copies ran while one was open for 5% -> 8% of each run, Pallas kernels for 0% -> 0%
where the time goes in v12:
time: 98.3 us; the launch traced here: 97.9 us
  starting transfers between devices  35.2 us (36%)
  waiting for transfers between devices  16.1 us (16%)
  matrix products  13.4 us (14%)
  blocking collectives  11.2 us (11%)
  local copies, waits for them, and re-layouts  9.14 us (9%)
  Pallas kernels  6.96 us (7%)
  other arithmetic  5.11 us (5%)
    ppermute x7, starting transfers between devices, _exchange(): lax.ppermute(send, axis_name, [(i, (i + k) % count) for i in range(count)])  13.1 us
    dot_general x1, matrix products, _project(): jnp.einsum('rhd,hdf->rhf', head_rows_in, head_weights, preferred_element_...  12.9 us
    ppermute x4, starting transfers between devices, _attention_pairs(): got = lax.ppermute(q_both, ('tp', 'sub'), _g_pairs(k, tp_count))  11.7 us
    all_gather x1, blocking collectives, _attention_pairs(): lax.all_gather(jnp.concatenate([numer_c, stats]), 'sub', axis=0, tiled=Fa...  9.24 us
    pallas_call x1, Pallas kernels, _attend_pairs(): pl.pallas_call(functools.partial(_pairs_kernel, group=group), grid_spec=g...  6.96 us
    ppermute x4, waiting for transfers between devices, _attention_pairs(): got = lax.ppermute(send, ('tp', 'sub'), _e_pairs(k, tp_count))  5.61 us
    ppermute x3, starting transfers between devices, _gather_blocks(): lax.ppermute(pair, axis_name, [(i, (i + 2 * d) % count) for i in range(co...  4.47 us
    ppermute x3, waiting for transfers between devices, _gather_blocks(): lax.ppermute(pair, axis_name, [(i, (i + 2 * d) % count) for i in range(co...  4.17 us
  transfers between devices with their start and end apart: 22, of which 11 were waited for; matrix products, arithmetic and copies ran while one was open for 8% of the time, Pallas kernels for 0%

profile of v12, /device:TPU:0, one launch (start us, length us, event | category | flops | bytes accessed | tf_op | source)
XLA Modules:
  0.0 97.9 jit_solution(6047823948652185)
XLA Ops:
  0.0 0.8 copy.64
  0.8 2.0 %all_gather.9 = bf16[2,8,2048]{2,0,1:T(2,128)(2,1)S(1)} all-gather(bf16[2,4,2048]{2,0,1:T(2,128)(2,1)S(1)} %copy.64), channel_id=1, replica_groups=mesh['rep'=2,'tp'=8,'sub'=2] {'sub'}, dimensions={1}, use_global_device_ids=true | all-gather | bytes 98304 | tf_op jit(solution)/shard_map/all_gather | solution.py:285
  2.8 5.8 %collective-permute-start.3 = (bf16[2,8,2048]{2,0,1:T(2,128)(2,1)S(1)}, bf16[2,8,2048]{2,0,1:T(2,128)(2,1)S(1)}, u32[]{:S(2)}, u32[]{:S(2)}) collective-permute-start(bf16[2,8,2048]{2,0,1:T(2,128)(2,1)S(1)} %all_gather.9), channel_id=1, source_target_pairs={{0,8},{2,10},{4,12},{6,14},{9,1},{11,3},{13,5},{15,7},{16,24},{18,... | collective-permute-start | bytes 196616 | tf_op jit(solution)/shard_map/ppermute | solution.py:288
  8.6 0.4 collective-permute-start
  9.0 2.0 %collective-permute-start.1 = (bf16[2,8,2048]{2,0,1:T(2,128)(2,1)S(1)}, bf16[2,8,2048]{2,0,1:T(2,128)(2,1)S(1)}, u32[]{:S(2)}, u32[]{:S(2)}) collective-permute-start(bf16[2,8,2048]{2,0,1:T(2,128)(2,1)S(1)} %all_gather.9), channel_id=1, source_target_pairs={{0,12},{1,4},{2,14},{3,6},{4,8},{5,0},{6,10},{7,2},{9,5},{8,13},{1... | collective-permute-start | bytes 196616 | tf_op jit(solution)/shard_map/ppermute | solution.py:288
  11.0 1.3 %constant_dynamic-slice_fusion.8 = bf16[2,4,128,512]{3,2,1,0:T(8,128)(2,1)S(1)} fusion(bf16[2,4,128,1024]{3,2,1,0:T(8,128)(2,1)} %tvo_ref.1, s32[]{:T(128)S(6)} %select_n.219), kind=kLoop, calls=%fused_computation.74 | loop fusion | bytes 2097156 | tf_op jit(solution)/shard_map/dynamic_slice | solution.py:277
  12.4 0.5 collective-permute-start.5
  12.9 0.7 multiply_exponential_fusion.1
  13.9 0.8 copy.69
  14.8 0.3 collective-permute-start.10
  15.1 1.3 %compare_convert_fusion = (f32[4,128]{1,0:T(4,128)}, f32[4,128]{1,0:T(4,128)}) fusion(s32[128]{0:T(128)S(1)} %iota_add_fusion, s32[4]{0:T(128)S(1)} %collective-permute-done.5, s32[4]{0:T(128)} %param.12), kind=kLoop, calls=%fused_computation.95 | loop fusion | flops 2048 | bytes 4640 | tf_op jit(solution)/shard_map/convert_element_type | solution.py:283
  16.4 3.5 %collective-permute-start.2 = (bf16[2,8,2048]{2,0,1:T(2,128)(2,1)S(1)}, bf16[2,8,2048]{2,0,1:T(2,128)(2,1)S(1)}, u32[]{:S(2)}, u32[]{:S(2)}) collective-permute-start(bf16[2,8,2048]{2,0,1:T(2,128)(2,1)S(1)} %all_gather.9), channel_id=1, source_target_pairs={{0,14},{1,6},{2,8},{3,0},{4,10},{5,2},{6,12},{7,4},{9,7},{8,15},{1... | collective-permute-start | bytes 196616 | tf_op jit(solution)/shard_map/ppermute | solution.py:288
  20.1 1.8 %collective-permute-done.2 = bf16[2,8,2048]{2,0,1:T(2,128)(2,1)S(1)} collective-permute-done((bf16[2,8,2048]{2,0,1:T(2,128)(2,1)S(1)}, bf16[2,8,2048]{2,0,1:T(2,128)(2,1)S(1)}, u32[]{:S(2)}, u32[]{:S(2)}) %collective-permute-start.2) | collective-permute-done | bytes 65568 | tf_op jit(solution)/shard_map/ppermute | solution.py:288
  21.9 0.5 pad_maximum_fusion.1
  22.4 0.7 scatter_fusion
  23.1 0.8 reshape.366.q_ref
  23.9 1.0 copy-done
  24.9 7.0 %shard_map.91 = f32[4,264,128]{2,1,0:T(8,128)} custom-call(s32[1]{0:T(128)} %bitcast.1.u_ref, bf16[4,256,128]{2,1,0:T(8,128)(2,1)} %reshape.366.q_ref, bf16[2,1024,1024]{2,1,0:T(8,128)(2,1)} %v_ref.1, bf16[2,1024,1024]{2,1,0:T(8,128)(2,1)} %v_ref.1, bf16[2,4,128,1024]{3,2,1,0:T(8,128)(2,1)} %tvo_ref.1, bf16[2,4,128,1024]{3,2,1,0:T(8,128)(2,1)} %tvo_ref.1, ...), custom_call_target="tpu_custom_call" | custom-call | flops 1073741824 | bytes 4997120 | tf_op jit(solution)/shard_map/pallas_call | solution.py:215
  31.9 1.1 %dynamic-slice_bitcast_fusion.3 = (f32[264,128]{1,0:T(8,128)S(1)}, f32[264,128]{1,0:T(8,128)S(1)}, f32[264,128]{1,0:T(8,128)S(1)}, f32[264,128]{1,0:T(8,128)S(1)}) fusion(f32[4,264,128]{2,1,0:T(8,128)} %shard_map.91, s32[]{:T(128)S(6)} %select_n.221, s32[]{:T(128)S(6)} %select_n.229, s32[]{:T(128)S(6)} %select_n.225, s32[]{:T(128)S(6)} %select_n.223), kind=kLoop, calls=%fused_computation.24 | loop fusion | bytes 1081360 | tf_op jit(solution)/shard_map/jit(dynamic_index_in_dim)/squeeze | solution.py:300
  33.0 0.7 collective-permute-start.9
  34.1 1.3 %collective-permute-start.8 = (f32[264,128]{1,0:T(8,128)S(1)}, f32[264,128]{1,0:T(8,128)S(1)}, u32[]{:S(2)}, u32[]{:S(2)}) collective-permute-start(f32[264,128]{1,0:T(8,128)S(1)} %get-tuple-element.11), channel_id=1, source_target_pairs={{0,6},{1,14},{2,0},{3,8},{4,2},{5,10},{6,4},{7,12},{8,7},{9,15},{1... | collective-permute-start | bytes 405512 | tf_op jit(solution)/shard_map/ppermute | solution.py:301
  35.4 0.8 collective-permute-start.6
  36.2 0.9 fusion.6
  37.1 2.0 %collective-permute-done.7 = f32[264,128]{1,0:T(8,128)S(1)} collective-permute-done((f32[264,128]{1,0:T(8,128)S(1)}, f32[264,128]{1,0:T(8,128)S(1)}, u32[]{:S(2)}, u32[]{:S(2)}) %collective-permute-start.7) | collective-permute-done | bytes 135200 | tf_op jit(solution)/shard_map/ppermute | solution.py:301
  39.2 3.6 %collective-permute-done.6 = f32[264,128]{1,0:T(8,128)S(1)} collective-permute-done((f32[264,128]{1,0:T(8,128)S(1)}, f32[264,128]{1,0:T(8,128)S(1)}, u32[]{:S(2)}, u32[]{:S(2)}) %collective-permute-start.6) | collective-permute-done | bytes 135200 | tf_op jit(solution)/shard_map/ppermute | solution.py:301
  43.1 9.2 %all-gather = f32[528,128]{1,0:T(8,128)S(1)} all-gather(f32[264,128]{1,0:T(8,128)S(1)} %pad_maximum_fusion.3), channel_id=2, replica_groups=mesh['rep'=2,'tp'=8,'sub'=2] {'sub'}, dimensions={0}, use_global_device_ids=true | all-gather | bytes 405504 | tf_op jit(solution)/shard_map/all_gather | solution.py:310
  53.1 12.9 %fusion.1 = f32[16,8192]{1,0:T(8,128)S(1)} fusion(f32[8192]{0:T(1024)S(1)} %dynamic_slice.52, bf16[16,128,8192]{2,1,0:T(8,128)(2,1)} %bitcast.177, bf16[16,16,128]{2,1,0:T(8,128)(2,1)S(1)} %fusion.8), kind=kOutput, calls=%fused_computation.4 | convolution fusion | flops 543031296 | bytes 34177024 | tf_op jit(solution)/shard_map/rhd,hdf->rhf/dot_general | solution.py:433
  66.1 0.3 copy.93
  66.4 0.5 constant_dynamic-slice_fusion.7
  66.9 2.2 %collective-permute-start.11 = (f32[16,1024]{1,0:T(8,128)S(1)}, f32[16,1024]{1,0:T(8,128)S(1)}, u32[]{:S(2)}, u32[]{:S(2)}) collective-permute-start(f32[16,1024]{1,0:T(8,128)S(1)} %bitcast.168), channel_id=1, source_target_pairs={{0,2},{2,4},{4,6},{6,8},{8,10},{10,12},{12,14},{14,0},{1,3},{3,5},... | collective-permute-start | bytes 196616 | tf_op jit(solution)/shard_map/ppermute | solution.py:61
  69.3 2.5 %collective-permute-start.13 = (f32[16,1024]{1,0:T(8,128)S(1)}, f32[16,1024]{1,0:T(8,128)S(1)}, u32[]{:S(2)}, u32[]{:S(2)}) collective-permute-start(f32[16,1024]{1,0:T(8,128)S(1)} %bitcast.162), channel_id=1, source_target_pairs={{0,6},{2,8},{4,10},{6,12},{8,14},{10,0},{12,2},{14,4},{1,7},{3,9},... | collective-permute-start | bytes 196616 | tf_op jit(solution)/shard_map/ppermute | solution.py:61
  71.8 2.7 %collective-permute-start.14 = (f32[16,1024]{1,0:T(8,128)S(1)}, f32[16,1024]{1,0:T(8,128)S(1)}, u32[]{:S(2)}, u32[]{:S(2)}) collective-permute-start(f32[16,1024]{1,0:T(8,128)S(1)} %bitcast.163), channel_id=1, source_target_pairs={{0,8},{2,10},{4,12},{6,14},{8,0},{10,2},{12,4},{14,6},{1,9},{3,11}... | collective-permute-start | bytes 196616 | tf_op jit(solution)/shard_map/ppermute | solution.py:61
  74.6 2.6 %collective-permute-start.15 = (f32[16,1024]{1,0:T(8,128)S(1)}, f32[16,1024]{1,0:T(8,128)S(1)}, u32[]{:S(2)}, u32[]{:S(2)}) collective-permute-start(f32[16,1024]{1,0:T(8,128)S(1)} %bitcast.164), channel_id=1, source_target_pairs={{0,10},{2,12},{4,14},{6,0},{8,2},{10,4},{12,6},{14,8},{1,11},{3,13... | collective-permute-start | bytes 196616 | tf_op jit(solution)/shard_map/ppermute | solution.py:61
  77.3 2.9 %collective-permute-start.17 = (f32[16,1024]{1,0:T(8,128)S(1)}, f32[16,1024]{1,0:T(8,128)S(1)}, u32[]{:S(2)}, u32[]{:S(2)}) collective-permute-start(f32[16,1024]{1,0:T(8,128)S(1)} %bitcast.165), channel_id=1, source_target_pairs={{0,14},{2,0},{4,2},{6,4},{8,6},{10,8},{12,10},{14,12},{1,15},{3,1}... | collective-permute-start | bytes 196616 | tf_op jit(solution)/shard_map/ppermute | solution.py:61
  80.4 1.2 %collective-permute-done.14 = f32[16,1024]{1,0:T(8,128)S(1)} collective-permute-done((f32[16,1024]{1,0:T(8,128)S(1)}, f32[16,1024]{1,0:T(8,128)S(1)}, u32[]{:S(2)}, u32[]{:S(2)}) %collective-permute-start.14) | collective-permute-done | bytes 65568 | tf_op jit(solution)/shard_map/ppermute | solution.py:61
  81.5 0.6 collective-permute-done.15
  82.1 1.0 collective-permute-done.16
  83.1 2.2 %collective-permute-start.18 = (bf16[16,1024]{1,0:T(8,128)(2,1)S(1)}, bf16[16,1024]{1,0:T(8,128)(2,1)S(1)}, u32[]{:S(2)}, u32[]{:S(2)}) collective-permute-start(bf16[16,1024]{1,0:T(8,128)(2,1)S(1)} %clamp_convert_fusion), channel_id=1, source_target_pairs={{0,2},{2,0},{4,6},{6,4},{8,10},{10,8},{12,14},{14,12},{1,3},{3,1},... | collective-permute-start | bytes 98312 | tf_op jit(solution)/shard_map/ppermute | solution.py:28
  85.3 1.8 %collective-permute-done.18 = bf16[16,1024]{1,0:T(8,128)(2,1)S(1)} collective-permute-done((bf16[16,1024]{1,0:T(8,128)(2,1)S(1)}, bf16[16,1024]{1,0:T(8,128)(2,1)S(1)}, u32[]{:S(2)}, u32[]{:S(2)}) %collective-permute-start.18) | collective-permute-done | bytes 32800 | tf_op jit(solution)/shard_map/ppermute | solution.py:28
  87.2 2.0 %collective-permute-start.19 = (bf16[2,16,1024]{2,1,0:T(8,128)(2,1)S(1)}, bf16[2,16,1024]{2,1,0:T(8,128)(2,1)S(1)}, u32[]{:S(2)}, u32[]{:S(2)}) collective-permute-start(bf16[2,16,1024]{2,1,0:T(8,128)(2,1)S(1)} %maximum_select_fusion.1), channel_id=1, source_target_pairs={{0,4},{2,6},{4,8},{6,10},{8,12},{10,14},{12,0},{14,2},{1,5},{3,7},... | collective-permute-start | bytes 196616 | tf_op jit(solution)/shard_map/ppermute | solution.py:34
  89.2 1.8 %collective-permute-start.20 = (bf16[2,16,1024]{2,1,0:T(8,128)(2,1)S(1)}, bf16[2,16,1024]{2,1,0:T(8,128)(2,1)S(1)}, u32[]{:S(2)}, u32[]{:S(2)}) collective-permute-start(bf16[2,16,1024]{2,1,0:T(8,128)(2,1)S(1)} %maximum_select_fusion.1), channel_id=1, source_target_pairs={{0,8},{2,10},{4,12},{6,14},{8,0},{10,2},{12,4},{14,6},{1,9},{3,11}... | collective-permute-start | bytes 196616 | tf_op jit(solution)/shard_map/ppermute | solution.py:34
  91.0 0.7 collective-permute-start.21
  91.7 2.1 %collective-permute-done.19 = bf16[2,16,1024]{2,1,0:T(8,128)(2,1)S(1)} collective-permute-done((bf16[2,16,1024]{2,1,0:T(8,128)(2,1)S(1)}, bf16[2,16,1024]{2,1,0:T(8,128)(2,1)S(1)}, u32[]{:S(2)}, u32[]{:S(2)}) %collective-permute-start.19) | collective-permute-done | bytes 65568 | tf_op jit(solution)/shard_map/ppermute | solution.py:34
  93.8 1.5 %collective-permute-done.20 = bf16[2,16,1024]{2,1,0:T(8,128)(2,1)S(1)} collective-permute-done((bf16[2,16,1024]{2,1,0:T(8,128)(2,1)S(1)}, bf16[2,16,1024]{2,1,0:T(8,128)(2,1)S(1)}, u32[]{:S(2)}, u32[]{:S(2)}) %collective-permute-start.20) | collective-permute-done | bytes 65568 | tf_op jit(solution)/shard_map/ppermute | solution.py:34
  95.3 0.6 collective-permute-done.21
  95.9 0.7 scatter_fusion.1
  96.7 0.3 copy.76
  97.1 0.8 add_convert_fusion
  (76 shorter events, 2.7 us)
Async XLA Ops:
  2.8 17.2 %collective-permute-start.3 = (bf16[2,8,2048]{2,0,1:T(2,128)(2,1)S(1)}, bf16[2,8,2048]{2,0,1:T(2,128)(2,1)S(1)}, u32[]{:S(2)}, u32[]{:S(2)}) collective-permute-start(bf16[2,8,2048]{2,0,1:T(2,128)(2,1)S(1)} %all_gather.9), channel_id=1, source_target_pairs={{0,8},{2,10},{4,12},{6,14},{9,1},{11,3},{13,5},{15,7},{16,24},{18,... | collective-permute-start | bytes 196616 | tf_op jit(solution)/shard_map/ppermute | solution.py:288
  8.6 11.5 %collective-permute-start = (bf16[2,8,2048]{2,0,1:T(2,128)(2,1)S(1)}, bf16[2,8,2048]{2,0,1:T(2,128)(2,1)S(1)}, u32[]{:S(2)}, u32[]{:S(2)}) collective-permute-start(bf16[2,8,2048]{2,0,1:T(2,128)(2,1)S(1)} %all_gather.9), channel_id=1, source_target_pairs={{0,10},{1,2},{2,12},{3,4},{4,14},{5,6},{6,8},{7,0},{9,3},{8,11},{1... | collective-permute-start | bytes 196616 | tf_op jit(solution)/shard_map/ppermute | solution.py:288
  9.0 11.1 %collective-permute-start.1 = (bf16[2,8,2048]{2,0,1:T(2,128)(2,1)S(1)}, bf16[2,8,2048]{2,0,1:T(2,128)(2,1)S(1)}, u32[]{:S(2)}, u32[]{:S(2)}) collective-permute-start(bf16[2,8,2048]{2,0,1:T(2,128)(2,1)S(1)} %all_gather.9), channel_id=1, source_target_pairs={{0,12},{1,4},{2,14},{3,6},{4,8},{5,0},{6,10},{7,2},{9,5},{8,13},{1... | collective-permute-start | bytes 196616 | tf_op jit(solution)/shard_map/ppermute | solution.py:288
  12.3 11.7 %collective-permute-start.4 = (bf16[2,4,128,512]{3,2,1,0:T(8,128)(2,1)S(1)}, bf16[2,4,128,512]{3,2,1,0:T(8,128)(2,1)S(1)}, u32[]{:S(2)}, u32[]{:S(2)}) collective-permute-start(bf16[2,4,128,512]{3,2,1,0:T(8,128)(2,1)S(1)} %constant_dynamic-slice_fusion.8), channel_id=1, source_target_pairs={{0,1},{1,0},{2,3},{3,2},{4,5},{5,4},{6,7},{7,6},{8,9},{9,8},{10,11... | collective-permute-start | bytes 3145736 | tf_op jit(solution)/shard_map/ppermute | solution.py:278
  12.4 2.4 %collective-permute-start.5 = (s32[4]{0:T(128)}, s32[4]{0:T(128)S(1)}, u32[]{:S(2)}, u32[]{:S(2)}) collective-permute-start(s32[4]{0:T(128)} %param.12), channel_id=1, source_target_pairs={{0,1},{1,0},{2,3},{3,2},{4,5},{5,4},{6,7},{7,6},{8,9},{9,8},{10,11... | collective-permute-start | bytes 56 | tf_op jit(solution)/shard_map/ppermute | solution.py:279
  14.8 1.7 %collective-permute-start.10 = (bf16[2,2,4,1024]{3,1,2,0:T(2,128)(2,1)S(1)}, bf16[2,2,4,1024]{3,1,2,0:T(2,128)(2,1)S(1)}, u32[]{:S(2)}, u32[]{:S(2)}) collective-permute-start(bf16[2,2,4,1024]{3,1,2,0:T(2,128)(2,1)S(1)} %copy.69), channel_id=1, source_target_pairs={{0,1},{1,0},{2,3},{3,2},{4,5},{5,4},{6,7},{7,6},{8,9},{9,8},{10,11... | collective-permute-start | bytes 98312 | tf_op jit(solution)/shard_map/ppermute | solution.py:280
  16.4 5.4 %collective-permute-start.2 = (bf16[2,8,2048]{2,0,1:T(2,128)(2,1)S(1)}, bf16[2,8,2048]{2,0,1:T(2,128)(2,1)S(1)}, u32[]{:S(2)}, u32[]{:S(2)}) collective-permute-start(bf16[2,8,2048]{2,0,1:T(2,128)(2,1)S(1)} %all_gather.9), channel_id=1, source_target_pairs={{0,14},{1,6},{2,8},{3,0},{4,10},{5,2},{6,12},{7,4},{9,7},{8,15},{1... | collective-permute-start | bytes 196616 | tf_op jit(solution)/shard_map/ppermute | solution.py:288
  23.9 1.0 copy-start
  33.0 3.2 %collective-permute-start.9 = (f32[264,128]{1,0:T(8,128)S(1)}, f32[264,128]{1,0:T(8,128)S(1)}, u32[]{:S(2)}, u32[]{:S(2)}) collective-permute-start(f32[264,128]{1,0:T(8,128)S(1)} %get-tuple-element.10), channel_id=1, source_target_pairs={{1,8},{3,10},{5,12},{7,14},{8,1},{10,3},{12,5},{14,7},{17,24},{19,... | collective-permute-start | bytes 405512 | tf_op jit(solution)/shard_map/ppermute | solution.py:301
  34.1 5.0 %collective-permute-start.7 = (f32[264,128]{1,0:T(8,128)S(1)}, f32[264,128]{1,0:T(8,128)S(1)}, u32[]{:S(2)}, u32[]{:S(2)}) collective-permute-start(f32[264,128]{1,0:T(8,128)S(1)} %get-tuple-element.12), channel_id=1, source_target_pairs={{0,4},{1,12},{2,6},{3,14},{4,0},{5,8},{6,2},{7,10},{8,5},{9,13},{1... | collective-permute-start | bytes 405512 | tf_op jit(solution)/shard_map/ppermute | solution.py:301
  34.1 5.1 %collective-permute-start.8 = (f32[264,128]{1,0:T(8,128)S(1)}, f32[264,128]{1,0:T(8,128)S(1)}, u32[]{:S(2)}, u32[]{:S(2)}) collective-permute-start(f32[264,128]{1,0:T(8,128)S(1)} %get-tuple-element.11), channel_id=1, source_target_pairs={{0,6},{1,14},{2,0},{3,8},{4,2},{5,10},{6,4},{7,12},{8,7},{9,15},{1... | collective-permute-start | bytes 405512 | tf_op jit(solution)/shard_map/ppermute | solution.py:301
  35.4 7.4 %collective-permute-start.6 = (f32[264,128]{1,0:T(8,128)S(1)}, f32[264,128]{1,0:T(8,128)S(1)}, u32[]{:S(2)}, u32[]{:S(2)}) collective-permute-start(f32[264,128]{1,0:T(8,128)S(1)} %get-tuple-element.9), channel_id=1, source_target_pairs={{0,2},{1,10},{2,4},{3,12},{4,6},{5,14},{6,0},{7,8},{8,3},{9,11},{1... | collective-permute-start | bytes 405512 | tf_op jit(solution)/shard_map/ppermute | solution.py:301
  53.1 16.1 %copy-start.2 = (s32[128]{0:T(128)S(1)}, s32[128]{0:T(128)}, u32[]{:S(2)}) copy-start(s32[128]{0:T(128)} %param.16) | copy-start | bytes 1540
  66.0 31.1 %copy-start.1 = (bf16[2,8,8192]{2,1,0:T(8,128)(2,1)S(1)}, bf16[2,8,8192]{2,1,0:T(8,128)(2,1)}, u32[]{:S(2)}) copy-start(bf16[2,8,8192]{2,1,0:T(8,128)(2,1)} %param.17) | copy-start | bytes 786436
  66.9 10.2 %collective-permute-start.11 = (f32[16,1024]{1,0:T(8,128)S(1)}, f32[16,1024]{1,0:T(8,128)S(1)}, u32[]{:S(2)}, u32[]{:S(2)}) collective-permute-start(f32[16,1024]{1,0:T(8,128)S(1)} %bitcast.168), channel_id=1, source_target_pairs={{0,2},{2,4},{4,6},{6,8},{8,10},{10,12},{12,14},{14,0},{1,3},{3,5},... | collective-permute-start | bytes 196616 | tf_op jit(solution)/shard_map/ppermute | solution.py:61
  69.2 8.2 %collective-permute-start.12 = (f32[16,1024]{1,0:T(8,128)S(1)}, f32[16,1024]{1,0:T(8,128)S(1)}, u32[]{:S(2)}, u32[]{:S(2)}) collective-permute-start(f32[16,1024]{1,0:T(8,128)S(1)} %bitcast.167), channel_id=1, source_target_pairs={{0,4},{2,6},{4,8},{6,10},{8,12},{10,14},{12,0},{14,2},{1,5},{3,7},... | collective-permute-start | bytes 196616 | tf_op jit(solution)/shard_map/ppermute | solution.py:61
  69.3 11.1 %collective-permute-start.13 = (f32[16,1024]{1,0:T(8,128)S(1)}, f32[16,1024]{1,0:T(8,128)S(1)}, u32[]{:S(2)}, u32[]{:S(2)}) collective-permute-start(f32[16,1024]{1,0:T(8,128)S(1)} %bitcast.162), channel_id=1, source_target_pairs={{0,6},{2,8},{4,10},{6,12},{8,14},{10,0},{12,2},{14,4},{1,7},{3,9},... | collective-permute-start | bytes 196616 | tf_op jit(solution)/shard_map/ppermute | solution.py:61
  71.8 9.7 %collective-permute-start.14 = (f32[16,1024]{1,0:T(8,128)S(1)}, f32[16,1024]{1,0:T(8,128)S(1)}, u32[]{:S(2)}, u32[]{:S(2)}) collective-permute-start(f32[16,1024]{1,0:T(8,128)S(1)} %bitcast.163), channel_id=1, source_target_pairs={{0,8},{2,10},{4,12},{6,14},{8,0},{10,2},{12,4},{14,6},{1,9},{3,11}... | collective-permute-start | bytes 196616 | tf_op jit(solution)/shard_map/ppermute | solution.py:61
  74.6 7.5 %collective-permute-start.15 = (f32[16,1024]{1,0:T(8,128)S(1)}, f32[16,1024]{1,0:T(8,128)S(1)}, u32[]{:S(2)}, u32[]{:S(2)}) collective-permute-start(f32[16,1024]{1,0:T(8,128)S(1)} %bitcast.164), channel_id=1, source_target_pairs={{0,10},{2,12},{4,14},{6,0},{8,2},{10,4},{12,6},{14,8},{1,11},{3,13... | collective-permute-start | bytes 196616 | tf_op jit(solution)/shard_map/ppermute | solution.py:61
  77.2 5.8 %collective-permute-start.16 = (f32[16,1024]{1,0:T(8,128)S(1)}, f32[16,1024]{1,0:T(8,128)S(1)}, u32[]{:S(2)}, u32[]{:S(2)}) collective-permute-start(f32[16,1024]{1,0:T(8,128)S(1)} %bitcast.166), channel_id=1, source_target_pairs={{0,12},{2,14},{4,0},{6,2},{8,4},{10,6},{12,8},{14,10},{1,13},{3,15... | collective-permute-start | bytes 196616 | tf_op jit(solution)/shard_map/ppermute | solution.py:61
  77.3 5.7 %collective-permute-start.17 = (f32[16,1024]{1,0:T(8,128)S(1)}, f32[16,1024]{1,0:T(8,128)S(1)}, u32[]{:S(2)}, u32[]{:S(2)}) collective-permute-start(f32[16,1024]{1,0:T(8,128)S(1)} %bitcast.165), channel_id=1, source_target_pairs={{0,14},{2,0},{4,2},{6,4},{8,6},{10,8},{12,10},{14,12},{1,15},{3,1}... | collective-permute-start | bytes 196616 | tf_op jit(solution)/shard_map/ppermute | solution.py:61
  83.1 4.1 %collective-permute-start.18 = (bf16[16,1024]{1,0:T(8,128)(2,1)S(1)}, bf16[16,1024]{1,0:T(8,128)(2,1)S(1)}, u32[]{:S(2)}, u32[]{:S(2)}) collective-permute-start(bf16[16,1024]{1,0:T(8,128)(2,1)S(1)} %clamp_convert_fusion), channel_id=1, source_target_pairs={{0,2},{2,0},{4,6},{6,4},{8,10},{10,8},{12,14},{14,12},{1,3},{3,1},... | collective-permute-start | bytes 98312 | tf_op jit(solution)/shard_map/ppermute | solution.py:28
  87.2 6.6 %collective-permute-start.19 = (bf16[2,16,1024]{2,1,0:T(8,128)(2,1)S(1)}, bf16[2,16,1024]{2,1,0:T(8,128)(2,1)S(1)}, u32[]{:S(2)}, u32[]{:S(2)}) collective-permute-start(bf16[2,16,1024]{2,1,0:T(8,128)(2,1)S(1)} %maximum_select_fusion.1), channel_id=1, source_target_pairs={{0,4},{2,6},{4,8},{6,10},{8,12},{10,14},{12,0},{14,2},{1,5},{3,7},... | collective-permute-start | bytes 196616 | tf_op jit(solution)/shard_map/ppermute | solution.py:34
  89.2 6.1 %collective-permute-start.20 = (bf16[2,16,1024]{2,1,0:T(8,128)(2,1)S(1)}, bf16[2,16,1024]{2,1,0:T(8,128)(2,1)S(1)}, u32[]{:S(2)}, u32[]{:S(2)}) collective-permute-start(bf16[2,16,1024]{2,1,0:T(8,128)(2,1)S(1)} %maximum_select_fusion.1), channel_id=1, source_target_pairs={{0,8},{2,10},{4,12},{6,14},{8,0},{10,2},{12,4},{14,6},{1,9},{3,11}... | collective-permute-start | bytes 196616 | tf_op jit(solution)/shard_map/ppermute | solution.py:34
  91.0 4.9 %collective-permute-start.21 = (bf16[2,16,1024]{2,1,0:T(8,128)(2,1)S(1)}, bf16[2,16,1024]{2,1,0:T(8,128)(2,1)S(1)}, u32[]{:S(2)}, u32[]{:S(2)}) collective-permute-start(bf16[2,16,1024]{2,1,0:T(8,128)(2,1)S(1)} %maximum_select_fusion.1), channel_id=1, source_target_pairs={{0,12},{2,14},{4,0},{6,2},{8,4},{10,6},{12,8},{14,10},{1,13},{3,15... | collective-permute-start | bytes 196616 | tf_op jit(solution)/shard_map/ppermute | solution.py:34

commit v13 on v12

--- a/solution.py
+++ b/solution.py
@@ -274,13 +274,22 @@
     i = tp_rank % quarter
     within = tp_rank // quarter == u
     swap = [(0, 1), (1, 0)]
-    peer_cols = lax.dynamic_slice_in_dim(tail_kv, (1 - u) * quarter * DH, quarter * DH, 3)
-    tail_peer = lax.ppermute(peer_cols, "sub", swap)
-    lengths_peer = lax.ppermute(tail_lengths, "sub", swap)
-    fresh_peer = lax.ppermute(fresh_kv, "sub", swap)
     t_pos = tp_rank * tail_dev + jnp.arange(tail_dev)
     valid_own = (t_pos[None, :] < tail_lengths[:, None]).astype(jnp.float32)
-    valid_peer = (t_pos[None, :] < lengths_peer[:, None]).astype(jnp.float32)
+    peer_cols = lax.dynamic_slice_in_dim(tail_kv, (1 - u) * quarter * DH, quarter * DH, 3)
+    lane = quarter * DH
+    parcel = jnp.concatenate([
+        peer_cols.reshape(-1, lane),
+        fresh_kv.reshape(-1, lane),
+        jnp.pad(valid_own.astype(jnp.bfloat16).reshape(-1), (0, -valid_own.size % lane)).reshape(-1, lane),
+    ])
+    parcel = lax.ppermute(parcel, "sub", swap)
+    n_tail = peer_cols.size // lane
+    n_fresh = fresh_kv.size // lane
+    tail_peer = parcel[:n_tail].reshape(peer_cols.shape)
+    fresh_peer = parcel[n_tail:n_tail + n_fresh].reshape(fresh_kv.shape)
+    valid_peer = parcel[n_tail + n_fresh:].reshape(-1)[: valid_own.size]
+    valid_peer = valid_peer.reshape(valid_own.shape).astype(jnp.float32)
 
     q_both = lax.all_gather(queries, "sub", axis=1, tiled=True)
     blocks = []
@@ -307,7 +316,9 @@
     n_stat = part.shape[1] - rows_n
     stats = jnp.concatenate([peak_c, mass_c]).reshape(-1, DH)
     stats = jnp.pad(stats, ((0, n_stat - stats.shape[0]), (0, 0)))
-    both = lax.all_gather(jnp.concatenate([numer_c, stats]), "sub", axis=0, tiled=False)
+    mine = jnp.concatenate([numer_c, stats])
+    theirs = lax.ppermute(mine, "sub", swap)
+    both = jnp.where(u == 0, jnp.stack([mine, theirs]), jnp.stack([theirs, mine]))
     numer_2 = both[:, :rows_n]
     stat_2 = both[:, rows_n:rows_n + 2 * rows_n // DH].reshape(2, 2, rows_n)
 

time: 98.3 us -> 93.5 us (0.951)
  blocking collectives: 11.2 us -> 1.96 us
  starting transfers between devices: 35.2 us -> 37.8 us
  waiting for transfers between devices: 16.1 us -> 17.9 us
    all_gather x1 -> x0, blocking collectives: 9.24 us -> none  [_attention_pairs(): lax.all_gather(jnp.concatenate([numer_c, stats]), 'sub', axis=0, tiled=Fa...]
    ppermute x3 -> x2, starting transfers between devices: 0.9 us -> 6.58 us  [the longest x1 5.94 us: _attention_pairs(): theirs = lax.ppermute(mine, 'sub', swap)]
    ppermute x4, starting transfers between devices: 11.7 us -> 8.29 us  [_attention_pairs(): got = lax.ppermute(q_both, ('tp', 'sub'), _g_pairs(k, tp_count))]
    ppermute x4, starting transfers between devices: 2.76 us -> 4.78 us  [_attention_pairs(): got = lax.ppermute(send, ('tp', 'sub'), _e_pairs(k, tp_count))]
    ppermute x3, waiting for transfers between devices: 4.17 us -> 5.95 us  [_gather_blocks(): lax.ppermute(pair, axis_name, [(i, (i + 2 * d) % count) for i in range(co...]
    unnamed x16 -> x23, local copies, waits for them, and re-layouts: 2.97 us -> 1.27 us
    ppermute x4, waiting for transfers between devices: 1.78 us -> 0.66 us  [_attention_pairs(): got = lax.ppermute(q_both, ('tp', 'sub'), _g_pairs(k, tp_count))]
    slice x0 -> x2, local copies, waits for them, and re-layouts: none -> 1.04 us  [the longest x1 1.03 us: _attention_pairs(): tail_peer = parcel[:n_tail].reshape(peer_cols.shape)]
  transfers between devices with their start and end apart: 22 -> 21, of which waited for: 11 -> 13; matrix products, arithmetic and copies ran while one was open for 8% -> 8% of each run, Pallas kernels for 0% -> 0%
where the time goes in v13:
time: 93.5 us; the launch traced here: 93.1 us
  starting transfers between devices  37.8 us (40%)
  waiting for transfers between devices  17.9 us (19%)
  matrix products  13.4 us (14%)
  local copies, waits for them, and re-layouts  9.31 us (10%)
  Pallas kernels  6.98 us (7%)
  other arithmetic  5.1 us (5%)
  blocking collectives  1.96 us (2%)
    dot_general x1, matrix products, _project(): jnp.einsum('rhd,hdf->rhf', head_rows_in, head_weights, preferred_element_...  12.9 us
    ppermute x7, starting transfers between devices, _exchange(): lax.ppermute(send, axis_name, [(i, (i + k) % count) for i in range(count)])  12.4 us
    ppermute x4, starting transfers between devices, _attention_pairs(): got = lax.ppermute(q_both, ('tp', 'sub'), _g_pairs(k, tp_count))  8.29 us
    pallas_call x1, Pallas kernels, _attend_pairs(): pl.pallas_call(functools.partial(_pairs_kernel, group=group), grid_spec=g...  6.98 us
    ppermute x3, waiting for transfers between devices, _gather_blocks(): lax.ppermute(pair, axis_name, [(i, (i + 2 * d) % count) for i in range(co...  5.95 us
    ppermute x1, starting transfers between devices, _attention_pairs(): theirs = lax.ppermute(mine, 'sub', swap)  5.94 us
    ppermute x4, waiting for transfers between devices, _attention_pairs(): got = lax.ppermute(send, ('tp', 'sub'), _e_pairs(k, tp_count))  5.45 us
    ppermute x4, starting transfers between devices, _attention_pairs(): got = lax.ppermute(send, ('tp', 'sub'), _e_pairs(k, tp_count))  4.78 us
  transfers between devices with their start and end apart: 21, of which 13 were waited for; matrix products, arithmetic and copies ran while one was open for 8% of the time, Pallas kernels for 0%

profile of v13, /device:TPU:0, one launch (start us, length us, event | category | flops | bytes accessed | tf_op | source)
XLA Modules:
  0.0 93.1 jit_solution(6763145438872370629)
XLA Ops:
  0.0 0.8 copy.67
  0.8 2.0 %all_gather.3 = bf16[2,8,2048]{2,0,1:T(2,128)(2,1)S(1)} all-gather(bf16[2,4,2048]{2,0,1:T(2,128)(2,1)S(1)} %copy.67), channel_id=1, replica_groups=mesh['rep'=2,'tp'=8,'sub'=2] {'sub'}, dimensions={1}, use_global_device_ids=true | all-gather | bytes 98304 | tf_op jit(solution)/shard_map/all_gather | solution.py:294
  2.8 5.8 %collective-permute-start.3 = (bf16[2,8,2048]{2,0,1:T(2,128)(2,1)S(1)}, bf16[2,8,2048]{2,0,1:T(2,128)(2,1)S(1)}, u32[]{:S(2)}, u32[]{:S(2)}) collective-permute-start(bf16[2,8,2048]{2,0,1:T(2,128)(2,1)S(1)} %all_gather.3), channel_id=1, source_target_pairs={{0,8},{2,10},{4,12},{6,14},{9,1},{11,3},{13,5},{15,7},{16,24},{18,... | collective-permute-start | bytes 196616 | tf_op jit(solution)/shard_map/ppermute | solution.py:297
  8.6 1.4 %collective-permute-start.2 = (bf16[2,8,2048]{2,0,1:T(2,128)(2,1)S(1)}, bf16[2,8,2048]{2,0,1:T(2,128)(2,1)S(1)}, u32[]{:S(2)}, u32[]{:S(2)}) collective-permute-start(bf16[2,8,2048]{2,0,1:T(2,128)(2,1)S(1)} %all_gather.3), channel_id=1, source_target_pairs={{0,14},{1,6},{2,8},{3,0},{4,10},{5,2},{6,12},{7,4},{9,7},{8,15},{1... | collective-permute-start | bytes 196616 | tf_op jit(solution)/shard_map/ppermute | solution.py:297
  10.0 0.9 collective-permute-start.1
  11.1 1.3 %compare_convert_fusion = (f32[4,128]{1,0:T(4,128)}, bf16[1,1,4,128]{3,2,1,0:T(4,128)(2,1)S(1)}) fusion(s32[128]{0:T(128)S(1)} %iota_add_fusion, s32[4]{0:T(128)} %param.12), kind=kLoop, calls=%fused_computation.99 | loop fusion | flops 1536 | bytes 3600 | tf_op jit(solution)/shard_map/convert_element_type | solution.py:278
  12.3 0.8 reshape.414
  13.1 1.3 %constant_dynamic-slice_fusion.8 = bf16[2,4,128,512]{3,2,1,0:T(8,128)(2,1)S(1)} fusion(bf16[2,4,128,1024]{3,2,1,0:T(8,128)(2,1)} %tvo_ref.1, s32[]{:T(128)S(6)} %select_n.228), kind=kLoop, calls=%fused_computation.76 | loop fusion | bytes 2097156 | tf_op jit(solution)/shard_map/dynamic_slice | solution.py:279
  14.5 0.6 collective-permute-start.4
  15.4 0.7 collective-permute-done
  16.0 0.5 pad_maximum_fusion.2
  16.6 0.7 scatter_fusion
  17.3 0.8 reshape.412.q_ref
  18.1 0.6 slice_convert_fusion
  18.7 1.0 %slice.52 = bf16[1024,512]{1,0:T(8,128)(2,1)} slice(bf16[1057,512]{1,0:T(8,128)(2,1)S(1)} %collective-permute-done.4), slice={[0:1024], [0:512]} | slice | bytes 2097152 | tf_op jit(solution)/shard_map/slice | solution.py:289
  19.7 7.0 %shard_map.91 = f32[4,264,128]{2,1,0:T(8,128)} custom-call(s32[1]{0:T(128)} %bitcast.1.u_ref, bf16[4,256,128]{2,1,0:T(8,128)(2,1)} %reshape.412.q_ref, bf16[2,1024,1024]{2,1,0:T(8,128)(2,1)} %v_ref.1, bf16[2,1024,1024]{2,1,0:T(8,128)(2,1)} %v_ref.1, bf16[2,4,128,1024]{3,2,1,0:T(8,128)(2,1)} %tvo_ref.1, bf16[2,4,128,1024]{3,2,1,0:T(8,128)(2,1)} %tvo_ref.1, ...), custom_call_target="tpu_custom_call" | custom-call | flops 1073741824 | bytes 4997120 | tf_op jit(solution)/shard_map/pallas_call | solution.py:215
  26.7 1.1 %dynamic-slice_bitcast_fusion.3 = (f32[264,128]{1,0:T(8,128)S(1)}, f32[264,128]{1,0:T(8,128)S(1)}, f32[264,128]{1,0:T(8,128)S(1)}, f32[264,128]{1,0:T(8,128)S(1)}) fusion(f32[4,264,128]{2,1,0:T(8,128)} %shard_map.91, s32[]{:T(128)S(6)} %select_n.230, s32[]{:T(128)S(6)} %select_n.238, s32[]{:T(128)S(6)} %select_n.234, s32[]{:T(128)S(6)} %select_n.232), kind=kLoop, calls=%fused_computation.26 | loop fusion | bytes 1081360 | tf_op jit(solution)/shard_map/jit(dynamic_index_in_dim)/squeeze | solution.py:309
  27.9 0.7 collective-permute-start.8
  28.9 0.9 collective-permute-start.5
  29.8 2.1 %collective-permute-start.7 = (f32[264,128]{1,0:T(8,128)S(1)}, f32[264,128]{1,0:T(8,128)S(1)}, u32[]{:S(2)}, u32[]{:S(2)}) collective-permute-start(f32[264,128]{1,0:T(8,128)S(1)} %get-tuple-element.11), channel_id=1, source_target_pairs={{0,6},{1,14},{2,0},{3,8},{4,2},{5,10},{6,4},{7,12},{8,7},{9,15},{1... | collective-permute-start | bytes 405512 | tf_op jit(solution)/shard_map/ppermute | solution.py:310
  31.9 1.1 %collective-permute-start.6 = (f32[264,128]{1,0:T(8,128)S(1)}, f32[264,128]{1,0:T(8,128)S(1)}, u32[]{:S(2)}, u32[]{:S(2)}) collective-permute-start(f32[264,128]{1,0:T(8,128)S(1)} %get-tuple-element.12), channel_id=1, source_target_pairs={{0,4},{1,12},{2,6},{3,14},{4,0},{5,8},{6,2},{7,10},{8,5},{9,13},{1... | collective-permute-start | bytes 405512 | tf_op jit(solution)/shard_map/ppermute | solution.py:310
  33.0 0.9 fusion.6
  34.0 1.0 %collective-permute-done.5 = f32[264,128]{1,0:T(8,128)S(1)} collective-permute-done((f32[264,128]{1,0:T(8,128)S(1)}, f32[264,128]{1,0:T(8,128)S(1)}, u32[]{:S(2)}, u32[]{:S(2)}) %collective-permute-start.5) | collective-permute-done | bytes 135200 | tf_op jit(solution)/shard_map/ppermute | solution.py:310
  35.0 1.3 %collective-permute-done.7 = f32[264,128]{1,0:T(8,128)S(1)} collective-permute-done((f32[264,128]{1,0:T(8,128)S(1)}, f32[264,128]{1,0:T(8,128)S(1)}, u32[]{:S(2)}, u32[]{:S(2)}) %collective-permute-start.7) | collective-permute-done | bytes 135200 | tf_op jit(solution)/shard_map/ppermute | solution.py:310
  36.3 3.1 %collective-permute-done.6 = f32[264,128]{1,0:T(8,128)S(1)} collective-permute-done((f32[264,128]{1,0:T(8,128)S(1)}, f32[264,128]{1,0:T(8,128)S(1)}, u32[]{:S(2)}, u32[]{:S(2)}) %collective-permute-start.6) | collective-permute-done | bytes 135200 | tf_op jit(solution)/shard_map/ppermute | solution.py:310
  39.8 5.9 %collective-permute-start.9 = (f32[264,128]{1,0:T(8,128)S(1)}, f32[264,128]{1,0:T(8,128)S(1)}, u32[]{:S(2)}, u32[]{:S(2)}) collective-permute-start(f32[264,128]{1,0:T(8,128)S(1)} %get-tuple-element.22), channel_id=1, source_target_pairs={{0,1},{1,0},{2,3},{3,2},{4,5},{5,4},{6,7},{7,6},{8,9},{9,8},{10,11... | collective-permute-start | bytes 405512 | tf_op jit(solution)/shard_map/ppermute | solution.py:320
  46.1 0.6 collective-permute-done.9
  47.6 12.9 %fusion.1 = f32[16,8192]{1,0:T(8,128)S(1)} fusion(f32[8192]{0:T(1024)S(1)} %dynamic-slice-done, bf16[16,128,8192]{2,1,0:T(8,128)(2,1)} %bitcast.194, bf16[16,16,128]{2,1,0:T(8,128)(2,1)S(1)} %fusion.8), kind=kOutput, calls=%fused_computation.4 | convolution fusion | flops 543031296 | bytes 34177024 | tf_op jit(solution)/shard_map/rhd,hdf->rhf/dot_general | solution.py:444
  60.5 0.3 copy.98
  60.8 0.5 constant_dynamic-slice_fusion.7
  61.5 2.6 %collective-permute-start.11 = (f32[16,1024]{1,0:T(8,128)S(1)}, f32[16,1024]{1,0:T(8,128)S(1)}, u32[]{:S(2)}, u32[]{:S(2)}) collective-permute-start(f32[16,1024]{1,0:T(8,128)S(1)} %bitcast.182), channel_id=1, source_target_pairs={{0,4},{2,6},{4,8},{6,10},{8,12},{10,14},{12,0},{14,2},{1,5},{3,7},... | collective-permute-start | bytes 196616 | tf_op jit(solution)/shard_map/ppermute | solution.py:61
  64.1 2.8 %collective-permute-start.12 = (f32[16,1024]{1,0:T(8,128)S(1)}, f32[16,1024]{1,0:T(8,128)S(1)}, u32[]{:S(2)}, u32[]{:S(2)}) collective-permute-start(f32[16,1024]{1,0:T(8,128)S(1)} %bitcast.181), channel_id=1, source_target_pairs={{0,6},{2,8},{4,10},{6,12},{8,14},{10,0},{12,2},{14,4},{1,7},{3,9},... | collective-permute-start | bytes 196616 | tf_op jit(solution)/shard_map/ppermute | solution.py:61
  66.9 2.1 %collective-permute-start.13 = (f32[16,1024]{1,0:T(8,128)S(1)}, f32[16,1024]{1,0:T(8,128)S(1)}, u32[]{:S(2)}, u32[]{:S(2)}) collective-permute-start(f32[16,1024]{1,0:T(8,128)S(1)} %bitcast.180), channel_id=1, source_target_pairs={{0,8},{2,10},{4,12},{6,14},{8,0},{10,2},{12,4},{14,6},{1,9},{3,11}... | collective-permute-start | bytes 196616 | tf_op jit(solution)/shard_map/ppermute | solution.py:61
  69.1 0.8 collective-permute-start.14
  69.8 2.9 %collective-permute-start.15 = (f32[16,1024]{1,0:T(8,128)S(1)}, f32[16,1024]{1,0:T(8,128)S(1)}, u32[]{:S(2)}, u32[]{:S(2)}) collective-permute-start(f32[16,1024]{1,0:T(8,128)S(1)} %bitcast.178), channel_id=1, source_target_pairs={{0,12},{2,14},{4,0},{6,2},{8,4},{10,6},{12,8},{14,10},{1,13},{3,15... | collective-permute-start | bytes 196616 | tf_op jit(solution)/shard_map/ppermute | solution.py:61
  72.8 1.1 %collective-permute-start.16 = (f32[16,1024]{1,0:T(8,128)S(1)}, f32[16,1024]{1,0:T(8,128)S(1)}, u32[]{:S(2)}, u32[]{:S(2)}) collective-permute-start(f32[16,1024]{1,0:T(8,128)S(1)} %bitcast.177), channel_id=1, source_target_pairs={{0,14},{2,0},{4,2},{6,4},{8,6},{10,8},{12,10},{14,12},{1,15},{3,1}... | collective-permute-start | bytes 196616 | tf_op jit(solution)/shard_map/ppermute | solution.py:61
  74.0 0.8 collective-permute-done.12
  75.0 0.9 collective-permute-done.14
  75.9 1.4 %collective-permute-done.15 = f32[16,1024]{1,0:T(8,128)S(1)} collective-permute-done((f32[16,1024]{1,0:T(8,128)S(1)}, f32[16,1024]{1,0:T(8,128)S(1)}, u32[]{:S(2)}, u32[]{:S(2)}) %collective-permute-start.15) | collective-permute-done | bytes 65568 | tf_op jit(solution)/shard_map/ppermute | solution.py:61
  77.4 2.2 %collective-permute-start.17 = (bf16[16,1024]{1,0:T(8,128)(2,1)S(1)}, bf16[16,1024]{1,0:T(8,128)(2,1)S(1)}, u32[]{:S(2)}, u32[]{:S(2)}) collective-permute-start(bf16[16,1024]{1,0:T(8,128)(2,1)S(1)} %clamp_convert_fusion), channel_id=1, source_target_pairs={{0,2},{2,0},{4,6},{6,4},{8,10},{10,8},{12,14},{14,12},{1,3},{3,1},... | collective-permute-start | bytes 98312 | tf_op jit(solution)/shard_map/ppermute | solution.py:28
  79.7 1.8 %collective-permute-done.17 = bf16[16,1024]{1,0:T(8,128)(2,1)S(1)} collective-permute-done((bf16[16,1024]{1,0:T(8,128)(2,1)S(1)}, bf16[16,1024]{1,0:T(8,128)(2,1)S(1)}, u32[]{:S(2)}, u32[]{:S(2)}) %collective-permute-start.17) | collective-permute-done | bytes 32800 | tf_op jit(solution)/shard_map/ppermute | solution.py:28
  81.6 2.7 %collective-permute-start.20 = (bf16[2,16,1024]{2,1,0:T(8,128)(2,1)S(1)}, bf16[2,16,1024]{2,1,0:T(8,128)(2,1)S(1)}, u32[]{:S(2)}, u32[]{:S(2)}) collective-permute-start(bf16[2,16,1024]{2,1,0:T(8,128)(2,1)S(1)} %maximum_select_fusion.2), channel_id=1, source_target_pairs={{0,12},{2,14},{4,0},{6,2},{8,4},{10,6},{12,8},{14,10},{1,13},{3,15... | collective-permute-start | bytes 196616 | tf_op jit(solution)/shard_map/ppermute | solution.py:34
  84.3 0.8 collective-permute-start.19
  85.2 1.1 %collective-permute-done.20 = bf16[2,16,1024]{2,1,0:T(8,128)(2,1)S(1)} collective-permute-done((bf16[2,16,1024]{2,1,0:T(8,128)(2,1)S(1)}, bf16[2,16,1024]{2,1,0:T(8,128)(2,1)S(1)}, u32[]{:S(2)}, u32[]{:S(2)}) %collective-permute-start.20) | collective-permute-done | bytes 65568 | tf_op jit(solution)/shard_map/ppermute | solution.py:34
  86.3 3.4 %collective-permute-done.19 = bf16[2,16,1024]{2,1,0:T(8,128)(2,1)S(1)} collective-permute-done((bf16[2,16,1024]{2,1,0:T(8,128)(2,1)S(1)}, bf16[2,16,1024]{2,1,0:T(8,128)(2,1)S(1)}, u32[]{:S(2)}, u32[]{:S(2)}) %collective-permute-start.19) | collective-permute-done | bytes 65568 | tf_op jit(solution)/shard_map/ppermute | solution.py:34
  89.7 1.4 %collective-permute-done.18 = bf16[2,16,1024]{2,1,0:T(8,128)(2,1)S(1)} collective-permute-done((bf16[2,16,1024]{2,1,0:T(8,128)(2,1)S(1)}, bf16[2,16,1024]{2,1,0:T(8,128)(2,1)S(1)}, u32[]{:S(2)}, u32[]{:S(2)}) %collective-permute-start.18) | collective-permute-done | bytes 65568 | tf_op jit(solution)/shard_map/ppermute | solution.py:34
  91.2 0.7 scatter_fusion.1
  92.4 0.8 add_convert_fusion
  (89 shorter events, 3.4 us)
Async XLA Ops:
  2.8 12.5 %collective-permute-start.3 = (bf16[2,8,2048]{2,0,1:T(2,128)(2,1)S(1)}, bf16[2,8,2048]{2,0,1:T(2,128)(2,1)S(1)}, u32[]{:S(2)}, u32[]{:S(2)}) collective-permute-start(bf16[2,8,2048]{2,0,1:T(2,128)(2,1)S(1)} %all_gather.3), channel_id=1, source_target_pairs={{0,8},{2,10},{4,12},{6,14},{9,1},{11,3},{13,5},{15,7},{16,24},{18,... | collective-permute-start | bytes 196616 | tf_op jit(solution)/shard_map/ppermute | solution.py:297
  8.6 6.8 %collective-permute-start.2 = (bf16[2,8,2048]{2,0,1:T(2,128)(2,1)S(1)}, bf16[2,8,2048]{2,0,1:T(2,128)(2,1)S(1)}, u32[]{:S(2)}, u32[]{:S(2)}) collective-permute-start(bf16[2,8,2048]{2,0,1:T(2,128)(2,1)S(1)} %all_gather.3), channel_id=1, source_target_pairs={{0,14},{1,6},{2,8},{3,0},{4,10},{5,2},{6,12},{7,4},{9,7},{8,15},{1... | collective-permute-start | bytes 196616 | tf_op jit(solution)/shard_map/ppermute | solution.py:297
  10.0 5.4 %collective-permute-start.1 = (bf16[2,8,2048]{2,0,1:T(2,128)(2,1)S(1)}, bf16[2,8,2048]{2,0,1:T(2,128)(2,1)S(1)}, u32[]{:S(2)}, u32[]{:S(2)}) collective-permute-start(bf16[2,8,2048]{2,0,1:T(2,128)(2,1)S(1)} %all_gather.3), channel_id=1, source_target_pairs={{0,12},{1,4},{2,14},{3,6},{4,8},{5,0},{6,10},{7,2},{9,5},{8,13},{1... | collective-permute-start | bytes 196616 | tf_op jit(solution)/shard_map/ppermute | solution.py:297
  10.9 5.2 %collective-permute-start = (bf16[2,8,2048]{2,0,1:T(2,128)(2,1)S(1)}, bf16[2,8,2048]{2,0,1:T(2,128)(2,1)S(1)}, u32[]{:S(2)}, u32[]{:S(2)}) collective-permute-start(bf16[2,8,2048]{2,0,1:T(2,128)(2,1)S(1)} %all_gather.3), channel_id=1, source_target_pairs={{0,10},{1,2},{2,12},{3,4},{4,14},{5,6},{6,8},{7,0},{9,3},{8,11},{1... | collective-permute-start | bytes 196616 | tf_op jit(solution)/shard_map/ppermute | solution.py:297
  13.1 2.0 %copy-start.4 = (s32[128]{0:T(128)S(1)}, s32[128]{0:T(128)}, u32[]{:S(2)}) copy-start(s32[128]{0:T(128)} %param.15) | copy-start | bytes 1540
  14.5 3.6 %collective-permute-start.4 = (bf16[1057,512]{1,0:T(8,128)(2,1)S(1)}, bf16[1057,512]{1,0:T(8,128)(2,1)S(1)}, u32[]{:S(2)}, u32[]{:S(2)}) collective-permute-start(bf16[1057,512]{1,0:T(8,128)(2,1)S(1)} %pad_maximum_fusion), channel_id=1, source_target_pairs={{0,1},{1,0},{2,3},{3,2},{4,5},{5,4},{6,7},{7,6},{8,9},{9,8},{10,11... | collective-permute-start | bytes 3247112 | tf_op jit(solution)/shard_map/ppermute | solution.py:286
  15.2 13.6 %copy-start.1 = (f32[16384]{0:T(1024)}, f32[16384]{0:T(1024)S(1)}, u32[]{:S(2)}) copy-start(f32[16384]{0:T(1024)S(1)} %broadcast_bitcast_fusion.1) | copy-start | bytes 196612
  19.7 8.9 %copy-start.3 = (bf16[2,2,4,1024]{3,2,1,0:T(4,128)(2,1)S(1)}, bf16[2,2,4,1024]{3,2,1,0:T(4,128)(2,1)}, u32[]{:S(2)}) copy-start(bf16[2,2,4,1024]{3,2,1,0:T(4,128)(2,1)} %param.13) | copy-start | bytes 98308
  27.9 5.2 %collective-permute-start.8 = (f32[264,128]{1,0:T(8,128)S(1)}, f32[264,128]{1,0:T(8,128)S(1)}, u32[]{:S(2)}, u32[]{:S(2)}) collective-permute-start(f32[264,128]{1,0:T(8,128)S(1)} %get-tuple-element.10), channel_id=1, source_target_pairs={{1,8},{3,10},{5,12},{7,14},{8,1},{10,3},{12,5},{14,7},{17,24},{19,... | collective-permute-start | bytes 405512 | tf_op jit(solution)/shard_map/ppermute | solution.py:310
  28.9 6.1 %collective-permute-start.5 = (f32[264,128]{1,0:T(8,128)S(1)}, f32[264,128]{1,0:T(8,128)S(1)}, u32[]{:S(2)}, u32[]{:S(2)}) collective-permute-start(f32[264,128]{1,0:T(8,128)S(1)} %get-tuple-element.9), channel_id=1, source_target_pairs={{0,2},{1,10},{2,4},{3,12},{4,6},{5,14},{6,0},{7,8},{8,3},{9,11},{1... | collective-permute-start | bytes 405512 | tf_op jit(solution)/shard_map/ppermute | solution.py:310
  29.8 6.5 %collective-permute-start.7 = (f32[264,128]{1,0:T(8,128)S(1)}, f32[264,128]{1,0:T(8,128)S(1)}, u32[]{:S(2)}, u32[]{:S(2)}) collective-permute-start(f32[264,128]{1,0:T(8,128)S(1)} %get-tuple-element.11), channel_id=1, source_target_pairs={{0,6},{1,14},{2,0},{3,8},{4,2},{5,10},{6,4},{7,12},{8,7},{9,15},{1... | collective-permute-start | bytes 405512 | tf_op jit(solution)/shard_map/ppermute | solution.py:310
  31.9 7.5 %collective-permute-start.6 = (f32[264,128]{1,0:T(8,128)S(1)}, f32[264,128]{1,0:T(8,128)S(1)}, u32[]{:S(2)}, u32[]{:S(2)}) collective-permute-start(f32[264,128]{1,0:T(8,128)S(1)} %get-tuple-element.12), channel_id=1, source_target_pairs={{0,4},{1,12},{2,6},{3,14},{4,0},{5,8},{6,2},{7,10},{8,5},{9,13},{1... | collective-permute-start | bytes 405512 | tf_op jit(solution)/shard_map/ppermute | solution.py:310
  39.4 8.1 %dynamic-slice-start = ((f32[16384]{0:T(1024)}, s32[]{:T(128)}), f32[8192]{0:T(1024)S(1)}, s32[]{:S(2)}) async-start(f32[16384]{0:T(1024)} %copy-done.1, s32[]{:T(128)} %select_n.245), calls=%async_computation | async-start | bytes 66048 | tf_op jit(solution)/shard_map/dynamic_slice | solution.py:442
  39.8 6.9 %collective-permute-start.9 = (f32[264,128]{1,0:T(8,128)S(1)}, f32[264,128]{1,0:T(8,128)S(1)}, u32[]{:S(2)}, u32[]{:S(2)}) collective-permute-start(f32[264,128]{1,0:T(8,128)S(1)} %get-tuple-element.22), channel_id=1, source_target_pairs={{0,1},{1,0},{2,3},{3,2},{4,5},{5,4},{6,7},{7,6},{8,9},{9,8},{10,11... | collective-permute-start | bytes 405512 | tf_op jit(solution)/shard_map/ppermute | solution.py:320
  60.5 3.6 %copy-start.5 = (s32[128]{0:T(128)S(1)}, s32[128]{0:T(128)}, u32[]{:S(2)}) copy-start(s32[128]{0:T(128)} %param.16) | copy-start | bytes 1540
  60.5 13.5 %copy-start.2 = (f32[16384]{0:T(1024)S(1)}, f32[16384]{0:T(1024)}, u32[]{:S(2)}) copy-start(f32[16384]{0:T(1024)} %copy-done.1) | copy-start | bytes 196612
  61.4 8.5 %collective-permute-start.10 = (f32[16,1024]{1,0:T(8,128)S(1)}, f32[16,1024]{1,0:T(8,128)S(1)}, u32[]{:S(2)}, u32[]{:S(2)}) collective-permute-start(f32[16,1024]{1,0:T(8,128)S(1)} %bitcast.183), channel_id=1, source_target_pairs={{0,2},{2,4},{4,6},{6,8},{8,10},{10,12},{12,14},{14,0},{1,3},{3,5},... | collective-permute-start | bytes 196616 | tf_op jit(solution)/shard_map/ppermute | solution.py:61
  61.5 11.3 %collective-permute-start.11 = (f32[16,1024]{1,0:T(8,128)S(1)}, f32[16,1024]{1,0:T(8,128)S(1)}, u32[]{:S(2)}, u32[]{:S(2)}) collective-permute-start(f32[16,1024]{1,0:T(8,128)S(1)} %bitcast.182), channel_id=1, source_target_pairs={{0,4},{2,6},{4,8},{6,10},{8,12},{10,14},{12,0},{14,2},{1,5},{3,7},... | collective-permute-start | bytes 196616 | tf_op jit(solution)/shard_map/ppermute | solution.py:61
  64.1 10.7 %collective-permute-start.12 = (f32[16,1024]{1,0:T(8,128)S(1)}, f32[16,1024]{1,0:T(8,128)S(1)}, u32[]{:S(2)}, u32[]{:S(2)}) collective-permute-start(f32[16,1024]{1,0:T(8,128)S(1)} %bitcast.181), channel_id=1, source_target_pairs={{0,6},{2,8},{4,10},{6,12},{8,14},{10,0},{12,2},{14,4},{1,7},{3,9},... | collective-permute-start | bytes 196616 | tf_op jit(solution)/shard_map/ppermute | solution.py:61
  66.9 8.1 %collective-permute-start.13 = (f32[16,1024]{1,0:T(8,128)S(1)}, f32[16,1024]{1,0:T(8,128)S(1)}, u32[]{:S(2)}, u32[]{:S(2)}) collective-permute-start(f32[16,1024]{1,0:T(8,128)S(1)} %bitcast.180), channel_id=1, source_target_pairs={{0,8},{2,10},{4,12},{6,14},{8,0},{10,2},{12,4},{14,6},{1,9},{3,11}... | collective-permute-start | bytes 196616 | tf_op jit(solution)/shard_map/ppermute | solution.py:61
  69.1 6.9 %collective-permute-start.14 = (f32[16,1024]{1,0:T(8,128)S(1)}, f32[16,1024]{1,0:T(8,128)S(1)}, u32[]{:S(2)}, u32[]{:S(2)}) collective-permute-start(f32[16,1024]{1,0:T(8,128)S(1)} %bitcast.179), channel_id=1, source_target_pairs={{0,10},{2,12},{4,14},{6,0},{8,2},{10,4},{12,6},{14,8},{1,11},{3,13... | collective-permute-start | bytes 196616 | tf_op jit(solution)/shard_map/ppermute | solution.py:61
  69.8 7.5 %collective-permute-start.15 = (f32[16,1024]{1,0:T(8,128)S(1)}, f32[16,1024]{1,0:T(8,128)S(1)}, u32[]{:S(2)}, u32[]{:S(2)}) collective-permute-start(f32[16,1024]{1,0:T(8,128)S(1)} %bitcast.178), channel_id=1, source_target_pairs={{0,12},{2,14},{4,0},{6,2},{8,4},{10,6},{12,8},{14,10},{1,13},{3,15... | collective-permute-start | bytes 196616 | tf_op jit(solution)/shard_map/ppermute | solution.py:61
  72.8 4.6 %collective-permute-start.16 = (f32[16,1024]{1,0:T(8,128)S(1)}, f32[16,1024]{1,0:T(8,128)S(1)}, u32[]{:S(2)}, u32[]{:S(2)}) collective-permute-start(f32[16,1024]{1,0:T(8,128)S(1)} %bitcast.177), channel_id=1, source_target_pairs={{0,14},{2,0},{4,2},{6,4},{8,6},{10,8},{12,10},{14,12},{1,15},{3,1}... | collective-permute-start | bytes 196616 | tf_op jit(solution)/shard_map/ppermute | solution.py:61
  77.4 4.1 %collective-permute-start.17 = (bf16[16,1024]{1,0:T(8,128)(2,1)S(1)}, bf16[16,1024]{1,0:T(8,128)(2,1)S(1)}, u32[]{:S(2)}, u32[]{:S(2)}) collective-permute-start(bf16[16,1024]{1,0:T(8,128)(2,1)S(1)} %clamp_convert_fusion), channel_id=1, source_target_pairs={{0,2},{2,0},{4,6},{6,4},{8,10},{10,8},{12,14},{14,12},{1,3},{3,1},... | collective-permute-start | bytes 98312 | tf_op jit(solution)/shard_map/ppermute | solution.py:28
  81.6 4.7 %collective-permute-start.20 = (bf16[2,16,1024]{2,1,0:T(8,128)(2,1)S(1)}, bf16[2,16,1024]{2,1,0:T(8,128)(2,1)S(1)}, u32[]{:S(2)}, u32[]{:S(2)}) collective-permute-start(bf16[2,16,1024]{2,1,0:T(8,128)(2,1)S(1)} %maximum_select_fusion.2), channel_id=1, source_target_pairs={{0,12},{2,14},{4,0},{6,2},{8,4},{10,6},{12,8},{14,10},{1,13},{3,15... | collective-permute-start | bytes 196616 | tf_op jit(solution)/shard_map/ppermute | solution.py:34
  84.3 5.4 %collective-permute-start.19 = (bf16[2,16,1024]{2,1,0:T(8,128)(2,1)S(1)}, bf16[2,16,1024]{2,1,0:T(8,128)(2,1)S(1)}, u32[]{:S(2)}, u32[]{:S(2)}) collective-permute-start(bf16[2,16,1024]{2,1,0:T(8,128)(2,1)S(1)} %maximum_select_fusion.2), channel_id=1, source_target_pairs={{0,8},{2,10},{4,12},{6,14},{8,0},{10,2},{12,4},{14,6},{1,9},{3,11}... | collective-permute-start | bytes 196616 | tf_op jit(solution)/shard_map/ppermute | solution.py:34
  85.1 6.1 %collective-permute-start.18 = (bf16[2,16,1024]{2,1,0:T(8,128)(2,1)S(1)}, bf16[2,16,1024]{2,1,0:T(8,128)(2,1)S(1)}, u32[]{:S(2)}, u32[]{:S(2)}) collective-permute-start(bf16[2,16,1024]{2,1,0:T(8,128)(2,1)S(1)} %maximum_select_fusion.2), channel_id=1, source_target_pairs={{0,4},{2,6},{4,8},{6,10},{8,12},{10,14},{12,0},{14,2},{1,5},{3,7},... | collective-permute-start | bytes 196616 | tf_op jit(solution)/shard_map/ppermute | solution.py:34
  91.1 1.2 %copy-start = (bf16[2,8,8192]{2,1,0:T(8,128)(2,1)S(1)}, bf16[2,8,8192]{2,1,0:T(8,128)(2,1)}, u32[]{:S(2)}) copy-start(bf16[2,8,8192]{2,1,0:T(8,128)(2,1)} %param.17) | copy-start | bytes 786436

commit v14 on v7

--- a/solution.py
+++ b/solution.py
@@ -24,17 +24,16 @@
         return lax.all_gather(x, axis_name, axis=0, tiled=False)
     me = lax.axis_index(axis_name)
     if count <= 8:
-        other = lax.ppermute(x, axis_name, [(i, i ^ 1) for i in range(count)])
+        half = count // 2
+        got = [x]
+        for d in range(1, half):
+            got.append(lax.ppermute(x, axis_name, [(i, (i + 2 * d) % count) for i in range(count)]))
+        order = (me // 2 - jnp.arange(half)) % half
+        mine = jnp.zeros((half,) + x.shape, x.dtype).at[order].set(jnp.stack(got))
+        other = lax.ppermute(mine, axis_name, [(i, i ^ 1) for i in range(count)])
         low = me % 2 == 0
-        pair = jnp.where(low, jnp.stack([x, other]), jnp.stack([other, x]))
-        pairs = [pair]
-        for d in range(1, count // 2):
-            pairs.append(
-                lax.ppermute(pair, axis_name, [(i, (i + 2 * d) % count) for i in range(count)])
-            )
-        order = (me // 2 - jnp.arange(count // 2)) % (count // 2)
-        placed = jnp.zeros((count // 2,) + pair.shape, pair.dtype).at[order].set(jnp.stack(pairs))
-        return placed.reshape((count,) + x.shape)
+        pairs = jnp.where(low, jnp.stack([mine, other], 1), jnp.stack([other, mine], 1))
+        return pairs.reshape((count,) + x.shape)
     cur = x[None]
     k = 1
     while k < count:

time: 87.9 us -> 89.8 us (1.022)
  waiting for transfers between devices: 14.9 us -> 25.2 us
  starting transfers between devices: 38.4 us -> 31.2 us
  other arithmetic: 4.99 us -> 3.95 us
    ppermute x8, waiting for transfers between devices: 8.36 us -> 13.5 us  [the longest x2 7.5 us: _gather_blocks(): other = lax.ppermute(mine, axis_name, [(i, i ^ 1) for i in range(count)])]
    ppermute x14, waiting for transfers between devices: 6.55 us -> 11.7 us  [_exchange(): lax.ppermute(send, axis_name, [(i, (i + k) % count) for i in range(count)])]
    ppermute x8, starting transfers between devices: 15.2 us -> 10.6 us  [the longest x6 8.96 us: _gather_blocks(): lax.ppermute(x, axis_name, [(i, (i + 2 * d) % count) for i in range(count)])]
    ppermute x14, starting transfers between devices: 23.3 us -> 20.6 us  [_exchange(): lax.ppermute(send, axis_name, [(i, (i + k) % count) for i in range(count)])]
    select_n x5 -> x2, other arithmetic: 1.83 us -> 0.21 us  [the longest x1 0.19 us: _gather_blocks(): jnp.where(low, jnp.stack([mine, other], 1), jnp.stack([other, mine], 1))]
  transfers between devices with their start and end apart: 22 -> 22, of which waited for: 14 -> 13; matrix products, arithmetic and copies ran while one was open for 5% -> 4% of each run, Pallas kernels for 0% -> 0%
where the time goes in v14:
time: 89.8 us; the launch traced here: 89.4 us
  starting transfers between devices  31.2 us (35%)
  waiting for transfers between devices  25.2 us (28%)
  matrix products  13.3 us (15%)
  local copies, waits for them, and re-layouts  7.97 us (9%)
  Pallas kernels  5.42 us (6%)
  other arithmetic  3.95 us (4%)
  blocking collectives  1.85 us (2%)
    ppermute x14, starting transfers between devices, _exchange(): lax.ppermute(send, axis_name, [(i, (i + k) % count) for i in range(count)])  20.6 us
    dot_general x1, matrix products, per_device(): jnp.einsum('rhd,hdf->rhf', head_rows_in, head_weights, preferred_element_...  12.9 us
    ppermute x14, waiting for transfers between devices, _exchange(): lax.ppermute(send, axis_name, [(i, (i + k) % count) for i in range(count)])  11.7 us
    ppermute x6, starting transfers between devices, _gather_blocks(): lax.ppermute(x, axis_name, [(i, (i + 2 * d) % count) for i in range(count)])  8.96 us
    ppermute x2, waiting for transfers between devices, _gather_blocks(): other = lax.ppermute(mine, axis_name, [(i, i ^ 1) for i in range(count)])  7.5 us
    ppermute x6, waiting for transfers between devices, _gather_blocks(): lax.ppermute(x, axis_name, [(i, (i + 2 * d) % count) for i in range(count)])  6.01 us
    pallas_call x1, Pallas kernels, _attend_local(): pl.pallas_call(_attend_kernel, grid=(kv_heads // per_step,), in_specs=[pl...  5.42 us
    unnamed x22, local copies, waits for them, and re-layouts  2.06 us
  transfers between devices with their start and end apart: 22, of which 13 were waited for; matrix products, arithmetic and copies ran while one was open for 4% of the time, Pallas kernels for 0%

profile of v14, /device:TPU:0, one launch (start us, length us, event | category | flops | bytes accessed | tf_op | source)
XLA Modules:
  0.0 89.4 jit_solution(9736185775115301446)
XLA Ops:
  0.0 5.0 %collective-permute-start.2 = (bf16[2,4,2048]{2,1,0:T(4,128)(2,1)}, bf16[2,4,2048]{2,1,0:T(4,128)(2,1)S(1)}, u32[]{:S(2)}, u32[]{:S(2)}) collective-permute-start(bf16[2,4,2048]{2,1,0:T(4,128)(2,1)} %param.9), channel_id=1, source_target_pairs={{0,12},{2,14},{4,0},{6,2},{8,4},{10,6},{12,8},{14,10},{1,13},{3,15... | collective-permute-start | bytes 98312 | tf_op jit(solution)/shard_map/ppermute | solution.py:30
  5.1 1.0 %collective-permute-start = (bf16[2,4,2048]{2,1,0:T(4,128)(2,1)}, bf16[2,4,2048]{2,1,0:T(4,128)(2,1)S(1)}, u32[]{:S(2)}, u32[]{:S(2)}) collective-permute-start(bf16[2,4,2048]{2,1,0:T(4,128)(2,1)} %param.9), channel_id=1, source_target_pairs={{0,4},{2,6},{4,8},{6,10},{8,12},{10,14},{12,0},{14,2},{1,5},{3,7},... | collective-permute-start | bytes 98312 | tf_op jit(solution)/shard_map/ppermute | solution.py:30
  6.1 0.8 reshape.232
  6.9 0.7 multiply_exponential_fusion.1
  7.7 0.8 reshape.231
  8.7 1.3 %collective-permute-done.1 = bf16[2,4,2048]{2,1,0:T(4,128)(2,1)S(1)} collective-permute-done((bf16[2,4,2048]{2,1,0:T(4,128)(2,1)}, bf16[2,4,2048]{2,1,0:T(4,128)(2,1)S(1)}, u32[]{:S(2)}, u32[]{:S(2)}) %collective-permute-start.1) | collective-permute-done | bytes 32800 | tf_op jit(solution)/shard_map/ppermute | solution.py:30
  10.1 0.9 %collective-permute-done = bf16[2,4,2048]{2,1,0:T(4,128)(2,1)S(1)} collective-permute-done((bf16[2,4,2048]{2,1,0:T(4,128)(2,1)}, bf16[2,4,2048]{2,1,0:T(4,128)(2,1)S(1)}, u32[]{:S(2)}, u32[]{:S(2)}) %collective-permute-start) | collective-permute-done | bytes 32800 | tf_op jit(solution)/shard_map/ppermute | solution.py:30
  11.0 0.9 pad_maximum_fusion.1
  11.9 0.7 scatter_fusion
  12.6 1.6 %collective-permute-start.3 = (bf16[4,2,4,2048]{3,2,1,0:T(4,128)(2,1)S(1)}, bf16[4,2,4,2048]{3,2,1,0:T(4,128)(2,1)S(1)}, u32[]{:S(2)}, u32[]{:S(2)}) collective-permute-start(bf16[4,2,4,2048]{3,2,1,0:T(4,128)(2,1)S(1)} %scatter_fusion), channel_id=1, source_target_pairs={{0,2},{2,0},{4,6},{6,4},{8,10},{10,8},{12,14},{14,12},{1,3},{3,1},... | collective-permute-start | bytes 393224 | tf_op jit(solution)/shard_map/ppermute | solution.py:33
  14.1 0.7 compare_convert_fusion.valid_ref
  15.0 2.6 %collective-permute-done.3 = bf16[4,2,4,2048]{3,2,1,0:T(4,128)(2,1)S(1)} collective-permute-done((bf16[4,2,4,2048]{3,2,1,0:T(4,128)(2,1)S(1)}, bf16[4,2,4,2048]{3,2,1,0:T(4,128)(2,1)S(1)}, u32[]{:S(2)}, u32[]{:S(2)}) %collective-permute-start.3) | collective-permute-done | bytes 131104 | tf_op jit(solution)/shard_map/ppermute | solution.py:33
  18.1 1.6 %copy-done = bf16[2,4,128,1024]{3,2,1,0:T(8,128)(2,1)S(1)} copy-done((bf16[2,4,128,1024]{3,2,1,0:T(8,128)(2,1)S(1)}, bf16[2,4,128,1024]{3,2,1,0:T(8,128)(2,1)}, u32[]{:S(2)}) %copy-start) | copy-done | bytes 2097176
  19.7 5.4 %shard_map.91 = (f32[8,128,128]{2,1,0:T(8,128)S(1)}, f32[8,128,128]{2,1,0:T(8,128)S(1)}, f32[8,128,128]{2,1,0:T(8,128)S(1)}) custom-call(bf16[8,128,128]{2,1,0:T(8,128)(2,1)S(1)} %bitcast.158, bf16[2,1024,1024]{2,1,0:T(8,128)(2,1)} %v_ref.1, bf16[2,1024,1024]{2,1,0:T(8,128)(2,1)} %v_ref.1, bf16[2,4,128,1024]{3,2,1,0:T(8,128)(2,1)S(1)} %copy-done, ...), custom_call_target="tpu_custom_call" | custom-call | flops 603979776 | bytes 8126464 | tf_op jit(solution)/shard_map/pallas_call | solution.py:113
  25.1 0.3 slice_reduce_fusion
  26.1 1.6 %collective-permute-start.4 = (f32[130,128]{1,0:T(8,128)S(1)}, f32[130,128]{1,0:T(8,128)S(1)}, u32[]{:S(2)}, u32[]{:S(2)}) collective-permute-start(f32[130,128]{1,0:T(8,128)S(1)} %get-tuple-element.17), channel_id=1, source_target_pairs={{0,2},{2,4},{4,6},{6,8},{8,10},{10,12},{12,14},{14,0},{1,3},{3,5},... | collective-permute-start | bytes 199688 | tf_op jit(solution)/shard_map/ppermute | solution.py:59
  27.7 0.3 collective-permute-start.5
  28.0 0.9 collective-permute-start.6
  28.9 2.9 %collective-permute-start.7 = (f32[130,128]{1,0:T(8,128)S(1)}, f32[130,128]{1,0:T(8,128)S(1)}, u32[]{:S(2)}, u32[]{:S(2)}) collective-permute-start(f32[130,128]{1,0:T(8,128)S(1)} %get-tuple-element.14), channel_id=1, source_target_pairs={{0,8},{2,10},{4,12},{6,14},{8,0},{10,2},{12,4},{14,6},{1,9},{3,11}... | collective-permute-start | bytes 199688 | tf_op jit(solution)/shard_map/ppermute | solution.py:59
  31.8 0.9 %collective-permute-start.8 = (f32[130,128]{1,0:T(8,128)S(1)}, f32[130,128]{1,0:T(8,128)S(1)}, u32[]{:S(2)}, u32[]{:S(2)}) collective-permute-start(f32[130,128]{1,0:T(8,128)S(1)} %get-tuple-element.13), channel_id=1, source_target_pairs={{0,10},{2,12},{4,14},{6,0},{8,2},{10,4},{12,6},{14,8},{1,11},{3,13... | collective-permute-start | bytes 199688 | tf_op jit(solution)/shard_map/ppermute | solution.py:59
  32.7 1.2 %collective-permute-done.4 = f32[130,128]{1,0:T(8,128)S(1)} collective-permute-done((f32[130,128]{1,0:T(8,128)S(1)}, f32[130,128]{1,0:T(8,128)S(1)}, u32[]{:S(2)}, u32[]{:S(2)}) %collective-permute-start.4) | collective-permute-done | bytes 66592 | tf_op jit(solution)/shard_map/ppermute | solution.py:59
  33.9 1.7 %collective-permute-start.9 = (f32[130,128]{1,0:T(8,128)S(1)}, f32[130,128]{1,0:T(8,128)S(1)}, u32[]{:S(2)}, u32[]{:S(2)}) collective-permute-start(f32[130,128]{1,0:T(8,128)S(1)} %get-tuple-element.12), channel_id=1, source_target_pairs={{0,12},{2,14},{4,0},{6,2},{8,4},{10,6},{12,8},{14,10},{1,13},{3,15... | collective-permute-start | bytes 199688 | tf_op jit(solution)/shard_map/ppermute | solution.py:59
  35.6 1.5 %collective-permute-start.10 = (f32[130,128]{1,0:T(8,128)S(1)}, f32[130,128]{1,0:T(8,128)S(1)}, u32[]{:S(2)}, u32[]{:S(2)}) collective-permute-start(f32[130,128]{1,0:T(8,128)S(1)} %get-tuple-element.11), channel_id=1, source_target_pairs={{0,14},{2,0},{4,2},{6,4},{8,6},{10,8},{12,10},{14,12},{1,15},{3,1}... | collective-permute-start | bytes 199688 | tf_op jit(solution)/shard_map/ppermute | solution.py:59
  37.1 0.6 collective-permute-done.6
  37.8 0.8 collective-permute-done.9
  38.6 1.4 %collective-permute-done.10 = f32[130,128]{1,0:T(8,128)S(1)} collective-permute-done((f32[130,128]{1,0:T(8,128)S(1)}, f32[130,128]{1,0:T(8,128)S(1)}, u32[]{:S(2)}, u32[]{:S(2)}) %collective-permute-start.10) | collective-permute-done | bytes 66592 | tf_op jit(solution)/shard_map/ppermute | solution.py:59
  40.4 0.2 fusion.2
  41.2 1.9 %all_gather.3 = bf16[2,8,2048]{2,0,1:T(2,128)(2,1)S(1)} all-gather(bf16[2,4,2048]{2,0,1:T(2,128)(2,1)S(1)} %copy.140), channel_id=1, replica_groups=mesh['rep'=2,'tp'=8,'sub'=2] {'sub'}, dimensions={1}, use_global_device_ids=true | all-gather | bytes 98304 | tf_op jit(solution)/shard_map/all_gather | solution.py:206
  43.1 12.9 %fusion.1 = f32[16,8192]{1,0:T(8,128)S(1)} fusion(f32[8192]{0:T(1024)S(1)} %dynamic_slice.61, bf16[16,128,8192]{2,1,0:T(8,128)(2,1)} %bitcast.191, bf16[16,16,128]{2,1,0:T(8,128)(2,1)S(1)} %bitcast.182), kind=kOutput, calls=%fused_computation.4 | convolution fusion | flops 543031296 | bytes 34177024 | tf_op jit(solution)/shard_map/rhd,hdf->rhf/dot_general | solution.py:215
  56.0 0.3 copy.161
  56.3 0.5 constant_dynamic-slice_fusion.8
  56.9 4.2 %collective-permute-start.17 = (f32[16,1024]{1,0:T(8,128)S(1)}, f32[16,1024]{1,0:T(8,128)S(1)}, u32[]{:S(2)}, u32[]{:S(2)}) collective-permute-start(f32[16,1024]{1,0:T(8,128)S(1)} %bitcast.181), channel_id=1, source_target_pairs={{0,14},{2,0},{4,2},{6,4},{8,6},{10,8},{12,10},{14,12},{1,15},{3,1}... | collective-permute-start | bytes 196616 | tf_op jit(solution)/shard_map/ppermute | solution.py:59
  61.1 1.1 %collective-permute-start.16 = (f32[16,1024]{1,0:T(8,128)S(1)}, f32[16,1024]{1,0:T(8,128)S(1)}, u32[]{:S(2)}, u32[]{:S(2)}) collective-permute-start(f32[16,1024]{1,0:T(8,128)S(1)} %bitcast.180), channel_id=1, source_target_pairs={{0,12},{2,14},{4,0},{6,2},{8,4},{10,6},{12,8},{14,10},{1,13},{3,15... | collective-permute-start | bytes 196616 | tf_op jit(solution)/shard_map/ppermute | solution.py:59
  62.3 2.0 %collective-permute-start.14 = (f32[16,1024]{1,0:T(8,128)S(1)}, f32[16,1024]{1,0:T(8,128)S(1)}, u32[]{:S(2)}, u32[]{:S(2)}) collective-permute-start(f32[16,1024]{1,0:T(8,128)S(1)} %bitcast.176), channel_id=1, source_target_pairs={{0,8},{2,10},{4,12},{6,14},{8,0},{10,2},{12,4},{14,6},{1,9},{3,11}... | collective-permute-start | bytes 196616 | tf_op jit(solution)/shard_map/ppermute | solution.py:59
  64.3 1.1 %collective-permute-start.13 = (f32[16,1024]{1,0:T(8,128)S(1)}, f32[16,1024]{1,0:T(8,128)S(1)}, u32[]{:S(2)}, u32[]{:S(2)}) collective-permute-start(f32[16,1024]{1,0:T(8,128)S(1)} %bitcast.177), channel_id=1, source_target_pairs={{0,6},{2,8},{4,10},{6,12},{8,14},{10,0},{12,2},{14,4},{1,7},{3,9},... | collective-permute-start | bytes 196616 | tf_op jit(solution)/shard_map/ppermute | solution.py:59
  65.4 1.9 %collective-permute-start.12 = (f32[16,1024]{1,0:T(8,128)S(1)}, f32[16,1024]{1,0:T(8,128)S(1)}, u32[]{:S(2)}, u32[]{:S(2)}) collective-permute-start(f32[16,1024]{1,0:T(8,128)S(1)} %bitcast.179), channel_id=1, source_target_pairs={{0,4},{2,6},{4,8},{6,10},{8,12},{10,14},{12,0},{14,2},{1,5},{3,7},... | collective-permute-start | bytes 196616 | tf_op jit(solution)/shard_map/ppermute | solution.py:59
  67.3 0.6 collective-permute-start.11
  68.0 5.0 %collective-permute-done.14 = f32[16,1024]{1,0:T(8,128)S(1)} collective-permute-done((f32[16,1024]{1,0:T(8,128)S(1)}, f32[16,1024]{1,0:T(8,128)S(1)}, u32[]{:S(2)}, u32[]{:S(2)}) %collective-permute-start.14) | collective-permute-done | bytes 65568 | tf_op jit(solution)/shard_map/ppermute | solution.py:59
  73.0 2.6 %collective-permute-done.13 = f32[16,1024]{1,0:T(8,128)S(1)} collective-permute-done((f32[16,1024]{1,0:T(8,128)S(1)}, f32[16,1024]{1,0:T(8,128)S(1)}, u32[]{:S(2)}, u32[]{:S(2)}) %collective-permute-start.13) | collective-permute-done | bytes 65568 | tf_op jit(solution)/shard_map/ppermute | solution.py:59
  75.8 0.8 collective-permute-start.19
  76.7 1.9 %collective-permute-start.18 = (bf16[16,1024]{1,0:T(8,128)(2,1)S(1)}, bf16[16,1024]{1,0:T(8,128)(2,1)S(1)}, u32[]{:S(2)}, u32[]{:S(2)}) collective-permute-start(bf16[16,1024]{1,0:T(8,128)(2,1)S(1)} %clamp_convert_fusion), channel_id=1, source_target_pairs={{0,4},{2,6},{4,8},{6,10},{8,12},{10,14},{12,0},{14,2},{1,5},{3,7},... | collective-permute-start | bytes 98312 | tf_op jit(solution)/shard_map/ppermute | solution.py:30
  78.6 1.1 %collective-permute-done.20 = bf16[16,1024]{1,0:T(8,128)(2,1)S(1)} collective-permute-done((bf16[16,1024]{1,0:T(8,128)(2,1)S(1)}, bf16[16,1024]{1,0:T(8,128)(2,1)S(1)}, u32[]{:S(2)}, u32[]{:S(2)}) %collective-permute-start.20) | collective-permute-done | bytes 32800 | tf_op jit(solution)/shard_map/ppermute | solution.py:30
  79.7 1.3 %collective-permute-done.19 = bf16[16,1024]{1,0:T(8,128)(2,1)S(1)} collective-permute-done((bf16[16,1024]{1,0:T(8,128)(2,1)S(1)}, bf16[16,1024]{1,0:T(8,128)(2,1)S(1)}, u32[]{:S(2)}, u32[]{:S(2)}) %collective-permute-start.19) | collective-permute-done | bytes 32800 | tf_op jit(solution)/shard_map/ppermute | solution.py:30
  81.0 1.4 %collective-permute-done.18 = bf16[16,1024]{1,0:T(8,128)(2,1)S(1)} collective-permute-done((bf16[16,1024]{1,0:T(8,128)(2,1)S(1)}, bf16[16,1024]{1,0:T(8,128)(2,1)S(1)}, u32[]{:S(2)}, u32[]{:S(2)}) %collective-permute-start.18) | collective-permute-done | bytes 32800 | tf_op jit(solution)/shard_map/ppermute | solution.py:30
  82.4 0.6 scatter_fusion.1
  83.2 4.9 %collective-permute-done.21 = bf16[4,16,1024]{2,1,0:T(8,128)(2,1)S(1)} collective-permute-done((bf16[4,16,1024]{2,1,0:T(8,128)(2,1)S(1)}, bf16[4,16,1024]{2,1,0:T(8,128)(2,1)S(1)}, u32[]{:S(2)}, u32[]{:S(2)}) %collective-permute-start.21) | collective-permute-done | bytes 131104 | tf_op jit(solution)/shard_map/ppermute | solution.py:33
  88.2 0.3 copy.144
  88.7 0.8 add_convert_fusion
  (87 shorter events, 3.4 us)
Async XLA Ops:
  0.0 8.7 %collective-permute-start.2 = (bf16[2,4,2048]{2,1,0:T(4,128)(2,1)}, bf16[2,4,2048]{2,1,0:T(4,128)(2,1)S(1)}, u32[]{:S(2)}, u32[]{:S(2)}) collective-permute-start(bf16[2,4,2048]{2,1,0:T(4,128)(2,1)} %param.9), channel_id=1, source_target_pairs={{0,12},{2,14},{4,0},{6,2},{8,4},{10,6},{12,8},{14,10},{1,13},{3,15... | collective-permute-start | bytes 98312 | tf_op jit(solution)/shard_map/ppermute | solution.py:30
  5.0 5.0 %collective-permute-start.1 = (bf16[2,4,2048]{2,1,0:T(4,128)(2,1)}, bf16[2,4,2048]{2,1,0:T(4,128)(2,1)S(1)}, u32[]{:S(2)}, u32[]{:S(2)}) collective-permute-start(bf16[2,4,2048]{2,1,0:T(4,128)(2,1)} %param.9), channel_id=1, source_target_pairs={{0,8},{2,10},{4,12},{6,14},{8,0},{10,2},{12,4},{14,6},{1,9},{3,11}... | collective-permute-start | bytes 98312 | tf_op jit(solution)/shard_map/ppermute | solution.py:30
  5.1 5.9 %collective-permute-start = (bf16[2,4,2048]{2,1,0:T(4,128)(2,1)}, bf16[2,4,2048]{2,1,0:T(4,128)(2,1)S(1)}, u32[]{:S(2)}, u32[]{:S(2)}) collective-permute-start(bf16[2,4,2048]{2,1,0:T(4,128)(2,1)} %param.9), channel_id=1, source_target_pairs={{0,4},{2,6},{4,8},{6,10},{8,12},{10,14},{12,0},{14,2},{1,5},{3,7},... | collective-permute-start | bytes 98312 | tf_op jit(solution)/shard_map/ppermute | solution.py:30
  12.6 5.0 %collective-permute-start.3 = (bf16[4,2,4,2048]{3,2,1,0:T(4,128)(2,1)S(1)}, bf16[4,2,4,2048]{3,2,1,0:T(4,128)(2,1)S(1)}, u32[]{:S(2)}, u32[]{:S(2)}) collective-permute-start(bf16[4,2,4,2048]{3,2,1,0:T(4,128)(2,1)S(1)} %scatter_fusion), channel_id=1, source_target_pairs={{0,2},{2,0},{4,6},{6,4},{8,10},{10,8},{12,14},{14,12},{1,3},{3,1},... | collective-permute-start | bytes 393224 | tf_op jit(solution)/shard_map/ppermute | solution.py:33
  18.1 1.6 %copy-start = (bf16[2,4,128,1024]{3,2,1,0:T(8,128)(2,1)S(1)}, bf16[2,4,128,1024]{3,2,1,0:T(8,128)(2,1)}, u32[]{:S(2)}) copy-start(bf16[2,4,128,1024]{3,2,1,0:T(8,128)(2,1)} %tv_ref.1) | copy-start | bytes 6291460
  26.1 7.9 %collective-permute-start.4 = (f32[130,128]{1,0:T(8,128)S(1)}, f32[130,128]{1,0:T(8,128)S(1)}, u32[]{:S(2)}, u32[]{:S(2)}) collective-permute-start(f32[130,128]{1,0:T(8,128)S(1)} %get-tuple-element.17), channel_id=1, source_target_pairs={{0,2},{2,4},{4,6},{6,8},{8,10},{10,12},{12,14},{14,0},{1,3},{3,5},... | collective-permute-start | bytes 199688 | tf_op jit(solution)/shard_map/ppermute | solution.py:59
  27.7 7.9 %collective-permute-start.5 = (f32[130,128]{1,0:T(8,128)S(1)}, f32[130,128]{1,0:T(8,128)S(1)}, u32[]{:S(2)}, u32[]{:S(2)}) collective-permute-start(f32[130,128]{1,0:T(8,128)S(1)} %get-tuple-element.16), channel_id=1, source_target_pairs={{0,4},{2,6},{4,8},{6,10},{8,12},{10,14},{12,0},{14,2},{1,5},{3,7},... | collective-permute-start | bytes 199688 | tf_op jit(solution)/shard_map/ppermute | solution.py:59
  28.0 9.7 %collective-permute-start.6 = (f32[130,128]{1,0:T(8,128)S(1)}, f32[130,128]{1,0:T(8,128)S(1)}, u32[]{:S(2)}, u32[]{:S(2)}) collective-permute-start(f32[130,128]{1,0:T(8,128)S(1)} %get-tuple-element.15), channel_id=1, source_target_pairs={{0,6},{2,8},{4,10},{6,12},{8,14},{10,0},{12,2},{14,4},{1,7},{3,9},... | collective-permute-start | bytes 199688 | tf_op jit(solution)/shard_map/ppermute | solution.py:59
  28.9 8.9 %collective-permute-start.7 = (f32[130,128]{1,0:T(8,128)S(1)}, f32[130,128]{1,0:T(8,128)S(1)}, u32[]{:S(2)}, u32[]{:S(2)}) collective-permute-start(f32[130,128]{1,0:T(8,128)S(1)} %get-tuple-element.14), channel_id=1, source_target_pairs={{0,8},{2,10},{4,12},{6,14},{8,0},{10,2},{12,4},{14,6},{1,9},{3,11}... | collective-permute-start | bytes 199688 | tf_op jit(solution)/shard_map/ppermute | solution.py:59
  31.8 6.0 %collective-permute-start.8 = (f32[130,128]{1,0:T(8,128)S(1)}, f32[130,128]{1,0:T(8,128)S(1)}, u32[]{:S(2)}, u32[]{:S(2)}) collective-permute-start(f32[130,128]{1,0:T(8,128)S(1)} %get-tuple-element.13), channel_id=1, source_target_pairs={{0,10},{2,12},{4,14},{6,0},{8,2},{10,4},{12,6},{14,8},{1,11},{3,13... | collective-permute-start | bytes 199688 | tf_op jit(solution)/shard_map/ppermute | solution.py:59
  33.9 4.7 %collective-permute-start.9 = (f32[130,128]{1,0:T(8,128)S(1)}, f32[130,128]{1,0:T(8,128)S(1)}, u32[]{:S(2)}, u32[]{:S(2)}) collective-permute-start(f32[130,128]{1,0:T(8,128)S(1)} %get-tuple-element.12), channel_id=1, source_target_pairs={{0,12},{2,14},{4,0},{6,2},{8,4},{10,6},{12,8},{14,10},{1,13},{3,15... | collective-permute-start | bytes 199688 | tf_op jit(solution)/shard_map/ppermute | solution.py:59
  35.6 4.4 %collective-permute-start.10 = (f32[130,128]{1,0:T(8,128)S(1)}, f32[130,128]{1,0:T(8,128)S(1)}, u32[]{:S(2)}, u32[]{:S(2)}) collective-permute-start(f32[130,128]{1,0:T(8,128)S(1)} %get-tuple-element.11), channel_id=1, source_target_pairs={{0,14},{2,0},{4,2},{6,4},{8,6},{10,8},{12,10},{14,12},{1,15},{3,1}... | collective-permute-start | bytes 199688 | tf_op jit(solution)/shard_map/ppermute | solution.py:59
  43.1 19.1 %copy-start.2 = (s32[128]{0:T(128)S(1)}, s32[128]{0:T(128)}, u32[]{:S(2)}) copy-start(s32[128]{0:T(128)} %param.16) | copy-start | bytes 1540
  56.0 32.7 %copy-start.1 = (bf16[2,8,8192]{2,1,0:T(8,128)(2,1)S(1)}, bf16[2,8,8192]{2,1,0:T(8,128)(2,1)}, u32[]{:S(2)}) copy-start(bf16[2,8,8192]{2,1,0:T(8,128)(2,1)} %param.17) | copy-start | bytes 786436
  56.9 8.5 %collective-permute-start.17 = (f32[16,1024]{1,0:T(8,128)S(1)}, f32[16,1024]{1,0:T(8,128)S(1)}, u32[]{:S(2)}, u32[]{:S(2)}) collective-permute-start(f32[16,1024]{1,0:T(8,128)S(1)} %bitcast.181), channel_id=1, source_target_pairs={{0,14},{2,0},{4,2},{6,4},{8,6},{10,8},{12,10},{14,12},{1,15},{3,1}... | collective-permute-start | bytes 196616 | tf_op jit(solution)/shard_map/ppermute | solution.py:59
  61.1 6.2 %collective-permute-start.16 = (f32[16,1024]{1,0:T(8,128)S(1)}, f32[16,1024]{1,0:T(8,128)S(1)}, u32[]{:S(2)}, u32[]{:S(2)}) collective-permute-start(f32[16,1024]{1,0:T(8,128)S(1)} %bitcast.180), channel_id=1, source_target_pairs={{0,12},{2,14},{4,0},{6,2},{8,4},{10,6},{12,8},{14,10},{1,13},{3,15... | collective-permute-start | bytes 196616 | tf_op jit(solution)/shard_map/ppermute | solution.py:59
  62.2 5.8 %collective-permute-start.15 = (f32[16,1024]{1,0:T(8,128)S(1)}, f32[16,1024]{1,0:T(8,128)S(1)}, u32[]{:S(2)}, u32[]{:S(2)}) collective-permute-start(f32[16,1024]{1,0:T(8,128)S(1)} %bitcast.175), channel_id=1, source_target_pairs={{0,10},{2,12},{4,14},{6,0},{8,2},{10,4},{12,6},{14,8},{1,11},{3,13... | collective-permute-start | bytes 196616 | tf_op jit(solution)/shard_map/ppermute | solution.py:59
  62.3 10.8 %collective-permute-start.14 = (f32[16,1024]{1,0:T(8,128)S(1)}, f32[16,1024]{1,0:T(8,128)S(1)}, u32[]{:S(2)}, u32[]{:S(2)}) collective-permute-start(f32[16,1024]{1,0:T(8,128)S(1)} %bitcast.176), channel_id=1, source_target_pairs={{0,8},{2,10},{4,12},{6,14},{8,0},{10,2},{12,4},{14,6},{1,9},{3,11}... | collective-permute-start | bytes 196616 | tf_op jit(solution)/shard_map/ppermute | solution.py:59
  64.3 11.4 %collective-permute-start.13 = (f32[16,1024]{1,0:T(8,128)S(1)}, f32[16,1024]{1,0:T(8,128)S(1)}, u32[]{:S(2)}, u32[]{:S(2)}) collective-permute-start(f32[16,1024]{1,0:T(8,128)S(1)} %bitcast.177), channel_id=1, source_target_pairs={{0,6},{2,8},{4,10},{6,12},{8,14},{10,0},{12,2},{14,4},{1,7},{3,9},... | collective-permute-start | bytes 196616 | tf_op jit(solution)/shard_map/ppermute | solution.py:59
  65.4 10.3 %collective-permute-start.12 = (f32[16,1024]{1,0:T(8,128)S(1)}, f32[16,1024]{1,0:T(8,128)S(1)}, u32[]{:S(2)}, u32[]{:S(2)}) collective-permute-start(f32[16,1024]{1,0:T(8,128)S(1)} %bitcast.179), channel_id=1, source_target_pairs={{0,4},{2,6},{4,8},{6,10},{8,12},{10,14},{12,0},{14,2},{1,5},{3,7},... | collective-permute-start | bytes 196616 | tf_op jit(solution)/shard_map/ppermute | solution.py:59
  67.3 8.4 %collective-permute-start.11 = (f32[16,1024]{1,0:T(8,128)S(1)}, f32[16,1024]{1,0:T(8,128)S(1)}, u32[]{:S(2)}, u32[]{:S(2)}) collective-permute-start(f32[16,1024]{1,0:T(8,128)S(1)} %bitcast.178), channel_id=1, source_target_pairs={{0,2},{2,4},{4,6},{6,8},{8,10},{10,12},{12,14},{14,0},{1,3},{3,5},... | collective-permute-start | bytes 196616 | tf_op jit(solution)/shard_map/ppermute | solution.py:59
  75.7 4.0 %collective-permute-start.20 = (bf16[16,1024]{1,0:T(8,128)(2,1)S(1)}, bf16[16,1024]{1,0:T(8,128)(2,1)S(1)}, u32[]{:S(2)}, u32[]{:S(2)}) collective-permute-start(bf16[16,1024]{1,0:T(8,128)(2,1)S(1)} %clamp_convert_fusion), channel_id=1, source_target_pairs={{0,12},{2,14},{4,0},{6,2},{8,4},{10,6},{12,8},{14,10},{1,13},{3,15... | collective-permute-start | bytes 98312 | tf_op jit(solution)/shard_map/ppermute | solution.py:30
  75.8 5.2 %collective-permute-start.19 = (bf16[16,1024]{1,0:T(8,128)(2,1)S(1)}, bf16[16,1024]{1,0:T(8,128)(2,1)S(1)}, u32[]{:S(2)}, u32[]{:S(2)}) collective-permute-start(bf16[16,1024]{1,0:T(8,128)(2,1)S(1)} %clamp_convert_fusion), channel_id=1, source_target_pairs={{0,8},{2,10},{4,12},{6,14},{8,0},{10,2},{12,4},{14,6},{1,9},{3,11}... | collective-permute-start | bytes 98312 | tf_op jit(solution)/shard_map/ppermute | solution.py:30
  76.7 5.7 %collective-permute-start.18 = (bf16[16,1024]{1,0:T(8,128)(2,1)S(1)}, bf16[16,1024]{1,0:T(8,128)(2,1)S(1)}, u32[]{:S(2)}, u32[]{:S(2)}) collective-permute-start(bf16[16,1024]{1,0:T(8,128)(2,1)S(1)} %clamp_convert_fusion), channel_id=1, source_target_pairs={{0,4},{2,6},{4,8},{6,10},{8,12},{10,14},{12,0},{14,2},{1,5},{3,7},... | collective-permute-start | bytes 98312 | tf_op jit(solution)/shard_map/ppermute | solution.py:30
  83.1 5.0 %collective-permute-start.21 = (bf16[4,16,1024]{2,1,0:T(8,128)(2,1)S(1)}, bf16[4,16,1024]{2,1,0:T(8,128)(2,1)S(1)}, u32[]{:S(2)}, u32[]{:S(2)}) collective-permute-start(bf16[4,16,1024]{2,1,0:T(8,128)(2,1)S(1)} %scatter_fusion.1), channel_id=1, source_target_pairs={{0,2},{2,0},{4,6},{6,4},{8,10},{10,8},{12,14},{14,12},{1,3},{3,1},... | collective-permute-start | bytes 393224 | tf_op jit(solution)/shard_map/ppermute | solution.py:33

commit v15 on v7

--- a/solution.py
+++ b/solution.py
@@ -55,9 +55,14 @@
     me = lax.axis_index(axis_name)
     got = [jax.tree.map(lambda b: lax.dynamic_index_in_dim(b, me, 0, keepdims=False), blocks)]
     for k in range(1, count):
-        dst = (me + k) % count
+        if _is_pow2(count):
+            dst = me ^ k
+            perm = [(i, i ^ k) for i in range(count)]
+        else:
+            dst = (me + k) % count
+            perm = [(i, (i + k) % count) for i in range(count)]
         send = jax.tree.map(lambda b: lax.dynamic_index_in_dim(b, dst, 0, keepdims=False), blocks)
-        got.append(lax.ppermute(send, axis_name, [(i, (i + k) % count) for i in range(count)]))
+        got.append(lax.ppermute(send, axis_name, perm))
     return jax.tree.map(lambda *xs: jnp.stack(xs), *got)
 
 

time: 87.9 us -> 91.4 us (1.040)
  waiting for transfers between devices: 14.9 us -> 18.5 us
    ppermute x14, waiting for transfers between devices: 6.55 us -> 9.95 us  [_exchange(): got.append(lax.ppermute(send, axis_name, perm))]
    ppermute x6, starting transfers between devices: 9.99 us -> 11.6 us  [_gather_blocks(): lax.ppermute(pair, axis_name, [(i, (i + 2 * d) % count) for i in range(co...]
    ppermute x2, starting transfers between devices: 5.16 us -> 3.87 us  [_gather_blocks(): other = lax.ppermute(x, axis_name, [(i, i ^ 1) for i in range(count)])]
    ppermute x2, waiting for transfers between devices: 1.89 us -> 3.05 us  [_gather_blocks(): other = lax.ppermute(x, axis_name, [(i, i ^ 1) for i in range(count)])]
    ppermute x6, waiting for transfers between devices: 6.46 us -> 5.5 us  [_gather_blocks(): lax.ppermute(pair, axis_name, [(i, (i + 2 * d) % count) for i in range(co...]
  transfers between devices with their start and end apart: 22 -> 22, of which waited for: 14 -> 10; matrix products, arithmetic and copies ran while one was open for 5% -> 5% of each run, Pallas kernels for 0% -> 0%
where the time goes in v15:
time: 91.4 us; the launch traced here: 90.9 us
  starting transfers between devices  38.3 us (42%)
  waiting for transfers between devices  18.5 us (20%)
  matrix products  13.3 us (15%)
  local copies, waits for them, and re-layouts  7.95 us (9%)
  Pallas kernels  5.43 us (6%)
  other arithmetic  5.02 us (5%)
  blocking collectives  1.85 us (2%)
    ppermute x14, starting transfers between devices, _exchange(): got.append(lax.ppermute(send, axis_name, perm))  22.8 us
    dot_general x1, matrix products, per_device(): jnp.einsum('rhd,hdf->rhf', head_rows_in, head_weights, preferred_element_...  12.9 us
    ppermute x6, starting transfers between devices, _gather_blocks(): lax.ppermute(pair, axis_name, [(i, (i + 2 * d) % count) for i in range(co...  11.6 us
    ppermute x14, waiting for transfers between devices, _exchange(): got.append(lax.ppermute(send, axis_name, perm))  9.95 us
    ppermute x6, waiting for transfers between devices, _gather_blocks(): lax.ppermute(pair, axis_name, [(i, (i + 2 * d) % count) for i in range(co...  5.5 us
    pallas_call x1, Pallas kernels, _attend_local(): pl.pallas_call(_attend_kernel, grid=(kv_heads // per_step,), in_specs=[pl...  5.43 us
    ppermute x2, starting transfers between devices, _gather_blocks(): other = lax.ppermute(x, axis_name, [(i, i ^ 1) for i in range(count)])  3.87 us
    ppermute x2, waiting for transfers between devices, _gather_blocks(): other = lax.ppermute(x, axis_name, [(i, i ^ 1) for i in range(count)])  3.05 us
  transfers between devices with their start and end apart: 22, of which 10 were waited for; matrix products, arithmetic and copies ran while one was open for 5% of the time, Pallas kernels for 0%

profile of v15, /device:TPU:0, one launch (start us, length us, event | category | flops | bytes accessed | tf_op | source)
XLA Modules:
  0.0 90.9 jit_solution(13353792059509739771)
XLA Ops:
  0.0 2.9 %collective-permute-start = (bf16[2,4,2048]{2,1,0:T(4,128)(2,1)}, bf16[2,4,2048]{2,1,0:T(4,128)(2,1)S(1)}, u32[]{:S(2)}, u32[]{:S(2)}) collective-permute-start(bf16[2,4,2048]{2,1,0:T(4,128)(2,1)} %param.9), channel_id=1, source_target_pairs={{0,2},{2,0},{4,6},{6,4},{8,10},{10,8},{12,14},{14,12},{1,3},{3,1},... | collective-permute-start | bytes 98312 | tf_op jit(solution)/shard_map/ppermute | solution.py:27
  2.9 0.8 reshape.344
  3.8 0.8 reshape.343
  4.6 0.7 multiply_exponential_fusion.1
  5.4 0.7 compare_convert_fusion.valid_ref
  6.6 0.9 %maximum_select_fusion.1 = bf16[2,2,4,2048]{3,2,1,0:T(4,128)(2,1)S(1)} fusion(bf16[1,2,4,2048]{3,2,1,0:T(4,128)(2,1)S(1)} %bitcast.176, bf16[1,2,4,2048]{3,2,1,0:T(4,128)(2,1)} %bitcast.170, pred[]{:T(512)S(6)} %eq.10), kind=kLoop, calls=%fused_computation.30 | loop fusion | flops 98304 | bytes 131073 | tf_op jit(solution)/shard_map/jit(_where)/select_n | solution.py:29
  7.5 1.6 %collective-permute-start.1 = (bf16[2,2,4,2048]{3,2,1,0:T(4,128)(2,1)S(1)}, bf16[2,2,4,2048]{3,2,1,0:T(4,128)(2,1)S(1)}, u32[]{:S(2)}, u32[]{:S(2)}) collective-permute-start(bf16[2,2,4,2048]{3,2,1,0:T(4,128)(2,1)S(1)} %maximum_select_fusion.1), channel_id=1, source_target_pairs={{0,4},{2,6},{4,8},{6,10},{8,12},{10,14},{12,0},{14,2},{1,5},{3,7},... | collective-permute-start | bytes 196616 | tf_op jit(solution)/shard_map/ppermute | solution.py:33
  9.1 2.6 %collective-permute-start.2 = (bf16[2,2,4,2048]{3,2,1,0:T(4,128)(2,1)S(1)}, bf16[2,2,4,2048]{3,2,1,0:T(4,128)(2,1)S(1)}, u32[]{:S(2)}, u32[]{:S(2)}) collective-permute-start(bf16[2,2,4,2048]{3,2,1,0:T(4,128)(2,1)S(1)} %maximum_select_fusion.1), channel_id=1, source_target_pairs={{0,8},{2,10},{4,12},{6,14},{8,0},{10,2},{12,4},{14,6},{1,9},{3,11}... | collective-permute-start | bytes 196616 | tf_op jit(solution)/shard_map/ppermute | solution.py:33
  11.7 1.3 %collective-permute-start.3 = (bf16[2,2,4,2048]{3,2,1,0:T(4,128)(2,1)S(1)}, bf16[2,2,4,2048]{3,2,1,0:T(4,128)(2,1)S(1)}, u32[]{:S(2)}, u32[]{:S(2)}) collective-permute-start(bf16[2,2,4,2048]{3,2,1,0:T(4,128)(2,1)S(1)} %maximum_select_fusion.1), channel_id=1, source_target_pairs={{0,12},{2,14},{4,0},{6,2},{8,4},{10,6},{12,8},{14,10},{1,13},{3,15... | collective-permute-start | bytes 196616 | tf_op jit(solution)/shard_map/ppermute | solution.py:33
  13.1 0.9 maximum_select_fusion
  14.0 0.4 collective-permute-done.1
  14.4 2.1 %collective-permute-done.2 = bf16[2,2,4,2048]{3,2,1,0:T(4,128)(2,1)S(1)} collective-permute-done((bf16[2,2,4,2048]{3,2,1,0:T(4,128)(2,1)S(1)}, bf16[2,2,4,2048]{3,2,1,0:T(4,128)(2,1)S(1)}, u32[]{:S(2)}, u32[]{:S(2)}) %collective-permute-start.2) | collective-permute-done | bytes 65568 | tf_op jit(solution)/shard_map/ppermute | solution.py:33
  16.8 0.7 scatter_fusion
  17.8 1.6 %copy-done = bf16[2,4,128,1024]{3,2,1,0:T(8,128)(2,1)S(1)} copy-done((bf16[2,4,128,1024]{3,2,1,0:T(8,128)(2,1)S(1)}, bf16[2,4,128,1024]{3,2,1,0:T(8,128)(2,1)}, u32[]{:S(2)}) %copy-start) | copy-done | bytes 2097176
  19.4 5.4 %shard_map.91 = (f32[8,128,128]{2,1,0:T(8,128)S(1)}, f32[8,128,128]{2,1,0:T(8,128)S(1)}, f32[8,128,128]{2,1,0:T(8,128)S(1)}) custom-call(bf16[8,128,128]{2,1,0:T(8,128)(2,1)S(1)} %bitcast.162, bf16[2,1024,1024]{2,1,0:T(8,128)(2,1)} %v_ref.1, bf16[2,1024,1024]{2,1,0:T(8,128)(2,1)} %v_ref.1, bf16[2,4,128,1024]{3,2,1,0:T(8,128)(2,1)S(1)} %copy-done, ...), custom_call_target="tpu_custom_call" | custom-call | flops 603979776 | bytes 8126464 | tf_op jit(solution)/shard_map/pallas_call | solution.py:119
  24.8 0.3 slice_reduce_fusion
  25.7 0.6 collective-permute-start.4
  26.4 1.3 %collective-permute-start.5 = (f32[130,128]{1,0:T(8,128)S(1)}, f32[130,128]{1,0:T(8,128)S(1)}, u32[]{:S(2)}, u32[]{:S(2)}) collective-permute-start(f32[130,128]{1,0:T(8,128)S(1)} %get-tuple-element.16), channel_id=1, source_target_pairs={{0,4},{2,6},{4,0},{6,2},{8,12},{10,14},{12,8},{14,10},{1,5},{3,7},... | collective-permute-start | bytes 199688 | tf_op jit(solution)/shard_map/ppermute | solution.py:65
  27.7 1.7 %collective-permute-start.6 = (f32[130,128]{1,0:T(8,128)S(1)}, f32[130,128]{1,0:T(8,128)S(1)}, u32[]{:S(2)}, u32[]{:S(2)}) collective-permute-start(f32[130,128]{1,0:T(8,128)S(1)} %get-tuple-element.15), channel_id=1, source_target_pairs={{0,6},{2,4},{4,2},{6,0},{8,14},{10,12},{12,10},{14,8},{1,7},{3,5},... | collective-permute-start | bytes 199688 | tf_op jit(solution)/shard_map/ppermute | solution.py:65
  29.4 1.3 %collective-permute-start.7 = (f32[130,128]{1,0:T(8,128)S(1)}, f32[130,128]{1,0:T(8,128)S(1)}, u32[]{:S(2)}, u32[]{:S(2)}) collective-permute-start(f32[130,128]{1,0:T(8,128)S(1)} %get-tuple-element.14), channel_id=1, source_target_pairs={{0,8},{2,10},{4,12},{6,14},{8,0},{10,2},{12,4},{14,6},{1,9},{3,11}... | collective-permute-start | bytes 199688 | tf_op jit(solution)/shard_map/ppermute | solution.py:65
  30.7 1.6 %collective-permute-start.8 = (f32[130,128]{1,0:T(8,128)S(1)}, f32[130,128]{1,0:T(8,128)S(1)}, u32[]{:S(2)}, u32[]{:S(2)}) collective-permute-start(f32[130,128]{1,0:T(8,128)S(1)} %get-tuple-element.13), channel_id=1, source_target_pairs={{0,10},{2,8},{4,14},{6,12},{8,2},{10,0},{12,6},{14,4},{1,11},{3,9}... | collective-permute-start | bytes 199688 | tf_op jit(solution)/shard_map/ppermute | solution.py:65
  32.3 2.7 %collective-permute-start.9 = (f32[130,128]{1,0:T(8,128)S(1)}, f32[130,128]{1,0:T(8,128)S(1)}, u32[]{:S(2)}, u32[]{:S(2)}) collective-permute-start(f32[130,128]{1,0:T(8,128)S(1)} %get-tuple-element.12), channel_id=1, source_target_pairs={{0,12},{2,14},{4,8},{6,10},{8,4},{10,6},{12,0},{14,2},{1,13},{3,15... | collective-permute-start | bytes 199688 | tf_op jit(solution)/shard_map/ppermute | solution.py:65
  35.0 2.1 %collective-permute-start.10 = (f32[130,128]{1,0:T(8,128)S(1)}, f32[130,128]{1,0:T(8,128)S(1)}, u32[]{:S(2)}, u32[]{:S(2)}) collective-permute-start(f32[130,128]{1,0:T(8,128)S(1)} %get-tuple-element.11), channel_id=1, source_target_pairs={{0,14},{2,12},{4,10},{6,8},{8,6},{10,4},{12,2},{14,0},{1,15},{3,13... | collective-permute-start | bytes 199688 | tf_op jit(solution)/shard_map/ppermute | solution.py:65
  37.1 2.0 %collective-permute-done.7 = f32[130,128]{1,0:T(8,128)S(1)} collective-permute-done((f32[130,128]{1,0:T(8,128)S(1)}, f32[130,128]{1,0:T(8,128)S(1)}, u32[]{:S(2)}, u32[]{:S(2)}) %collective-permute-start.7) | collective-permute-done | bytes 66592 | tf_op jit(solution)/shard_map/ppermute | solution.py:65
  39.1 1.7 %collective-permute-done.8 = f32[130,128]{1,0:T(8,128)S(1)} collective-permute-done((f32[130,128]{1,0:T(8,128)S(1)}, f32[130,128]{1,0:T(8,128)S(1)}, u32[]{:S(2)}, u32[]{:S(2)}) %collective-permute-start.8) | collective-permute-done | bytes 66592 | tf_op jit(solution)/shard_map/ppermute | solution.py:65
  40.8 1.3 %collective-permute-done.10 = f32[130,128]{1,0:T(8,128)S(1)} collective-permute-done((f32[130,128]{1,0:T(8,128)S(1)}, f32[130,128]{1,0:T(8,128)S(1)}, u32[]{:S(2)}, u32[]{:S(2)}) %collective-permute-start.10) | collective-permute-done | bytes 66592 | tf_op jit(solution)/shard_map/ppermute | solution.py:65
  43.4 1.9 %all_gather.3 = bf16[2,8,2048]{2,0,1:T(2,128)(2,1)S(1)} all-gather(bf16[2,4,2048]{2,0,1:T(2,128)(2,1)S(1)} %copy.98), channel_id=1, replica_groups=mesh['rep'=2,'tp'=8,'sub'=2] {'sub'}, dimensions={1}, use_global_device_ids=true | all-gather | bytes 98304 | tf_op jit(solution)/shard_map/all_gather | solution.py:212
  45.3 12.9 %fusion.1 = f32[16,8192]{1,0:T(8,128)S(1)} fusion(f32[8192]{0:T(1024)S(1)} %dynamic_slice.61, bf16[16,128,8192]{2,1,0:T(8,128)(2,1)} %bitcast.196, bf16[16,16,128]{2,1,0:T(8,128)(2,1)S(1)} %bitcast.187), kind=kOutput, calls=%fused_computation.4 | convolution fusion | flops 543031296 | bytes 34177024 | tf_op jit(solution)/shard_map/rhd,hdf->rhf/dot_general | solution.py:221
  58.2 0.3 copy.119
  58.5 0.5 constant_dynamic-slice_fusion.8
  59.1 1.6 %collective-permute-start.11 = (f32[16,1024]{1,0:T(8,128)S(1)}, f32[16,1024]{1,0:T(8,128)S(1)}, u32[]{:S(2)}, u32[]{:S(2)}) collective-permute-start(f32[16,1024]{1,0:T(8,128)S(1)} %bitcast.186), channel_id=1, source_target_pairs={{0,2},{2,0},{4,6},{6,4},{8,10},{10,8},{12,14},{14,12},{1,3},{3,1},... | collective-permute-start | bytes 196616 | tf_op jit(solution)/shard_map/ppermute | solution.py:65
  60.7 1.1 %collective-permute-start.12 = (f32[16,1024]{1,0:T(8,128)S(1)}, f32[16,1024]{1,0:T(8,128)S(1)}, u32[]{:S(2)}, u32[]{:S(2)}) collective-permute-start(f32[16,1024]{1,0:T(8,128)S(1)} %bitcast.185), channel_id=1, source_target_pairs={{0,4},{2,6},{4,0},{6,2},{8,12},{10,14},{12,8},{14,10},{1,5},{3,7},... | collective-permute-start | bytes 196616 | tf_op jit(solution)/shard_map/ppermute | solution.py:65
  61.8 1.0 %collective-permute-start.13 = (f32[16,1024]{1,0:T(8,128)S(1)}, f32[16,1024]{1,0:T(8,128)S(1)}, u32[]{:S(2)}, u32[]{:S(2)}) collective-permute-start(f32[16,1024]{1,0:T(8,128)S(1)} %bitcast.180), channel_id=1, source_target_pairs={{0,6},{2,4},{4,2},{6,0},{8,14},{10,12},{12,10},{14,8},{1,7},{3,5},... | collective-permute-start | bytes 196616 | tf_op jit(solution)/shard_map/ppermute | solution.py:65
  62.8 2.7 %collective-permute-start.14 = (f32[16,1024]{1,0:T(8,128)S(1)}, f32[16,1024]{1,0:T(8,128)S(1)}, u32[]{:S(2)}, u32[]{:S(2)}) collective-permute-start(f32[16,1024]{1,0:T(8,128)S(1)} %bitcast.181), channel_id=1, source_target_pairs={{0,8},{2,10},{4,12},{6,14},{8,0},{10,2},{12,4},{14,6},{1,9},{3,11}... | collective-permute-start | bytes 196616 | tf_op jit(solution)/shard_map/ppermute | solution.py:65
  65.5 1.3 %collective-permute-start.15 = (f32[16,1024]{1,0:T(8,128)S(1)}, f32[16,1024]{1,0:T(8,128)S(1)}, u32[]{:S(2)}, u32[]{:S(2)}) collective-permute-start(f32[16,1024]{1,0:T(8,128)S(1)} %bitcast.182), channel_id=1, source_target_pairs={{0,10},{2,8},{4,14},{6,12},{8,2},{10,0},{12,6},{14,4},{1,11},{3,9}... | collective-permute-start | bytes 196616 | tf_op jit(solution)/shard_map/ppermute | solution.py:65
  66.9 1.2 %collective-permute-start.16 = (f32[16,1024]{1,0:T(8,128)S(1)}, f32[16,1024]{1,0:T(8,128)S(1)}, u32[]{:S(2)}, u32[]{:S(2)}) collective-permute-start(f32[16,1024]{1,0:T(8,128)S(1)} %bitcast.184), channel_id=1, source_target_pairs={{0,12},{2,14},{4,8},{6,10},{8,4},{10,6},{12,0},{14,2},{1,13},{3,15... | collective-permute-start | bytes 196616 | tf_op jit(solution)/shard_map/ppermute | solution.py:65
  68.1 2.6 %collective-permute-start.17 = (f32[16,1024]{1,0:T(8,128)S(1)}, f32[16,1024]{1,0:T(8,128)S(1)}, u32[]{:S(2)}, u32[]{:S(2)}) collective-permute-start(f32[16,1024]{1,0:T(8,128)S(1)} %bitcast.183), channel_id=1, source_target_pairs={{0,14},{2,12},{4,10},{6,8},{8,6},{10,4},{12,2},{14,0},{1,15},{3,13... | collective-permute-start | bytes 196616 | tf_op jit(solution)/shard_map/ppermute | solution.py:65
  70.9 0.8 collective-permute-done.14
  71.7 4.1 %collective-permute-done.15 = f32[16,1024]{1,0:T(8,128)S(1)} collective-permute-done((f32[16,1024]{1,0:T(8,128)S(1)}, f32[16,1024]{1,0:T(8,128)S(1)}, u32[]{:S(2)}, u32[]{:S(2)}) %collective-permute-start.15) | collective-permute-done | bytes 65568 | tf_op jit(solution)/shard_map/ppermute | solution.py:65
  75.8 0.9 %collective-permute-start.18 = (bf16[16,1024]{1,0:T(8,128)(2,1)S(1)}, bf16[16,1024]{1,0:T(8,128)(2,1)S(1)}, u32[]{:S(2)}, u32[]{:S(2)}) collective-permute-start(bf16[16,1024]{1,0:T(8,128)(2,1)S(1)} %clamp_convert_fusion), channel_id=1, source_target_pairs={{0,2},{2,0},{4,6},{6,4},{8,10},{10,8},{12,14},{14,12},{1,3},{3,1},... | collective-permute-start | bytes 98312 | tf_op jit(solution)/shard_map/ppermute | solution.py:27
  76.8 3.0 %collective-permute-done.18 = bf16[16,1024]{1,0:T(8,128)(2,1)S(1)} collective-permute-done((bf16[16,1024]{1,0:T(8,128)(2,1)S(1)}, bf16[16,1024]{1,0:T(8,128)(2,1)S(1)}, u32[]{:S(2)}, u32[]{:S(2)}) %collective-permute-start.18) | collective-permute-done | bytes 32800 | tf_op jit(solution)/shard_map/ppermute | solution.py:27
  79.8 3.1 %collective-permute-start.19 = (bf16[2,16,1024]{2,1,0:T(8,128)(2,1)S(1)}, bf16[2,16,1024]{2,1,0:T(8,128)(2,1)S(1)}, u32[]{:S(2)}, u32[]{:S(2)}) collective-permute-start(bf16[2,16,1024]{2,1,0:T(8,128)(2,1)S(1)} %maximum_select_fusion.3), channel_id=1, source_target_pairs={{0,4},{2,6},{4,8},{6,10},{8,12},{10,14},{12,0},{14,2},{1,5},{3,7},... | collective-permute-start | bytes 196616 | tf_op jit(solution)/shard_map/ppermute | solution.py:33
  83.1 2.8 %collective-permute-start.21 = (bf16[2,16,1024]{2,1,0:T(8,128)(2,1)S(1)}, bf16[2,16,1024]{2,1,0:T(8,128)(2,1)S(1)}, u32[]{:S(2)}, u32[]{:S(2)}) collective-permute-start(bf16[2,16,1024]{2,1,0:T(8,128)(2,1)S(1)} %maximum_select_fusion.3), channel_id=1, source_target_pairs={{0,12},{2,14},{4,0},{6,2},{8,4},{10,6},{12,8},{14,10},{1,13},{3,15... | collective-permute-start | bytes 196616 | tf_op jit(solution)/shard_map/ppermute | solution.py:33
  85.9 0.7 collective-permute-done.19
  86.6 2.3 %collective-permute-done.20 = bf16[2,16,1024]{2,1,0:T(8,128)(2,1)S(1)} collective-permute-done((bf16[2,16,1024]{2,1,0:T(8,128)(2,1)S(1)}, bf16[2,16,1024]{2,1,0:T(8,128)(2,1)S(1)}, u32[]{:S(2)}, u32[]{:S(2)}) %collective-permute-start.20) | collective-permute-done | bytes 65568 | tf_op jit(solution)/shard_map/ppermute | solution.py:33
  89.0 0.7 scatter_fusion.1
  89.7 0.3 copy.101
  90.1 0.8 add_convert_fusion
  (88 shorter events, 3.5 us)
Async XLA Ops:
  0.0 6.6 %collective-permute-start = (bf16[2,4,2048]{2,1,0:T(4,128)(2,1)}, bf16[2,4,2048]{2,1,0:T(4,128)(2,1)S(1)}, u32[]{:S(2)}, u32[]{:S(2)}) collective-permute-start(bf16[2,4,2048]{2,1,0:T(4,128)(2,1)} %param.9), channel_id=1, source_target_pairs={{0,2},{2,0},{4,6},{6,4},{8,10},{10,8},{12,14},{14,12},{1,3},{3,1},... | collective-permute-start | bytes 98312 | tf_op jit(solution)/shard_map/ppermute | solution.py:27
  7.5 6.9 %collective-permute-start.1 = (bf16[2,2,4,2048]{3,2,1,0:T(4,128)(2,1)S(1)}, bf16[2,2,4,2048]{3,2,1,0:T(4,128)(2,1)S(1)}, u32[]{:S(2)}, u32[]{:S(2)}) collective-permute-start(bf16[2,2,4,2048]{3,2,1,0:T(4,128)(2,1)S(1)} %maximum_select_fusion.1), channel_id=1, source_target_pairs={{0,4},{2,6},{4,8},{6,10},{8,12},{10,14},{12,0},{14,2},{1,5},{3,7},... | collective-permute-start | bytes 196616 | tf_op jit(solution)/shard_map/ppermute | solution.py:33
  9.1 7.3 %collective-permute-start.2 = (bf16[2,2,4,2048]{3,2,1,0:T(4,128)(2,1)S(1)}, bf16[2,2,4,2048]{3,2,1,0:T(4,128)(2,1)S(1)}, u32[]{:S(2)}, u32[]{:S(2)}) collective-permute-start(bf16[2,2,4,2048]{3,2,1,0:T(4,128)(2,1)S(1)} %maximum_select_fusion.1), channel_id=1, source_target_pairs={{0,8},{2,10},{4,12},{6,14},{8,0},{10,2},{12,4},{14,6},{1,9},{3,11}... | collective-permute-start | bytes 196616 | tf_op jit(solution)/shard_map/ppermute | solution.py:33
  11.7 4.8 %collective-permute-start.3 = (bf16[2,2,4,2048]{3,2,1,0:T(4,128)(2,1)S(1)}, bf16[2,2,4,2048]{3,2,1,0:T(4,128)(2,1)S(1)}, u32[]{:S(2)}, u32[]{:S(2)}) collective-permute-start(bf16[2,2,4,2048]{3,2,1,0:T(4,128)(2,1)S(1)} %maximum_select_fusion.1), channel_id=1, source_target_pairs={{0,12},{2,14},{4,0},{6,2},{8,4},{10,6},{12,8},{14,10},{1,13},{3,15... | collective-permute-start | bytes 196616 | tf_op jit(solution)/shard_map/ppermute | solution.py:33
  17.8 1.6 %copy-start = (bf16[2,4,128,1024]{3,2,1,0:T(8,128)(2,1)S(1)}, bf16[2,4,128,1024]{3,2,1,0:T(8,128)(2,1)}, u32[]{:S(2)}) copy-start(bf16[2,4,128,1024]{3,2,1,0:T(8,128)(2,1)} %tv_ref.1) | copy-start | bytes 6291460
  25.7 6.6 %collective-permute-start.4 = (f32[130,128]{1,0:T(8,128)S(1)}, f32[130,128]{1,0:T(8,128)S(1)}, u32[]{:S(2)}, u32[]{:S(2)}) collective-permute-start(f32[130,128]{1,0:T(8,128)S(1)} %get-tuple-element.17), channel_id=1, source_target_pairs={{0,2},{2,0},{4,6},{6,4},{8,10},{10,8},{12,14},{14,12},{1,3},{3,1},... | collective-permute-start | bytes 199688 | tf_op jit(solution)/shard_map/ppermute | solution.py:65
  26.4 8.6 %collective-permute-start.5 = (f32[130,128]{1,0:T(8,128)S(1)}, f32[130,128]{1,0:T(8,128)S(1)}, u32[]{:S(2)}, u32[]{:S(2)}) collective-permute-start(f32[130,128]{1,0:T(8,128)S(1)} %get-tuple-element.16), channel_id=1, source_target_pairs={{0,4},{2,6},{4,0},{6,2},{8,12},{10,14},{12,8},{14,10},{1,5},{3,7},... | collective-permute-start | bytes 199688 | tf_op jit(solution)/shard_map/ppermute | solution.py:65
  27.7 9.4 %collective-permute-start.6 = (f32[130,128]{1,0:T(8,128)S(1)}, f32[130,128]{1,0:T(8,128)S(1)}, u32[]{:S(2)}, u32[]{:S(2)}) collective-permute-start(f32[130,128]{1,0:T(8,128)S(1)} %get-tuple-element.15), channel_id=1, source_target_pairs={{0,6},{2,4},{4,2},{6,0},{8,14},{10,12},{12,10},{14,8},{1,7},{3,5},... | collective-permute-start | bytes 199688 | tf_op jit(solution)/shard_map/ppermute | solution.py:65
  29.4 9.7 %collective-permute-start.7 = (f32[130,128]{1,0:T(8,128)S(1)}, f32[130,128]{1,0:T(8,128)S(1)}, u32[]{:S(2)}, u32[]{:S(2)}) collective-permute-start(f32[130,128]{1,0:T(8,128)S(1)} %get-tuple-element.14), channel_id=1, source_target_pairs={{0,8},{2,10},{4,12},{6,14},{8,0},{10,2},{12,4},{14,6},{1,9},{3,11}... | collective-permute-start | bytes 199688 | tf_op jit(solution)/shard_map/ppermute | solution.py:65
  30.7 10.1 %collective-permute-start.8 = (f32[130,128]{1,0:T(8,128)S(1)}, f32[130,128]{1,0:T(8,128)S(1)}, u32[]{:S(2)}, u32[]{:S(2)}) collective-permute-start(f32[130,128]{1,0:T(8,128)S(1)} %get-tuple-element.13), channel_id=1, source_target_pairs={{0,10},{2,8},{4,14},{6,12},{8,2},{10,0},{12,6},{14,4},{1,11},{3,9}... | collective-permute-start | bytes 199688 | tf_op jit(solution)/shard_map/ppermute | solution.py:65
  32.3 8.5 %collective-permute-start.9 = (f32[130,128]{1,0:T(8,128)S(1)}, f32[130,128]{1,0:T(8,128)S(1)}, u32[]{:S(2)}, u32[]{:S(2)}) collective-permute-start(f32[130,128]{1,0:T(8,128)S(1)} %get-tuple-element.12), channel_id=1, source_target_pairs={{0,12},{2,14},{4,8},{6,10},{8,4},{10,6},{12,0},{14,2},{1,13},{3,15... | collective-permute-start | bytes 199688 | tf_op jit(solution)/shard_map/ppermute | solution.py:65
  35.0 7.2 %collective-permute-start.10 = (f32[130,128]{1,0:T(8,128)S(1)}, f32[130,128]{1,0:T(8,128)S(1)}, u32[]{:S(2)}, u32[]{:S(2)}) collective-permute-start(f32[130,128]{1,0:T(8,128)S(1)} %get-tuple-element.11), channel_id=1, source_target_pairs={{0,14},{2,12},{4,10},{6,8},{8,6},{10,4},{12,2},{14,0},{1,15},{3,13... | collective-permute-start | bytes 199688 | tf_op jit(solution)/shard_map/ppermute | solution.py:65
  45.3 16.5 %copy-start.2 = (s32[128]{0:T(128)S(1)}, s32[128]{0:T(128)}, u32[]{:S(2)}) copy-start(s32[128]{0:T(128)} %param.16) | copy-start | bytes 1540
  58.2 31.9 %copy-start.1 = (bf16[2,8,8192]{2,1,0:T(8,128)(2,1)S(1)}, bf16[2,8,8192]{2,1,0:T(8,128)(2,1)}, u32[]{:S(2)}) copy-start(bf16[2,8,8192]{2,1,0:T(8,128)(2,1)} %param.17) | copy-start | bytes 786436
  59.1 7.8 %collective-permute-start.11 = (f32[16,1024]{1,0:T(8,128)S(1)}, f32[16,1024]{1,0:T(8,128)S(1)}, u32[]{:S(2)}, u32[]{:S(2)}) collective-permute-start(f32[16,1024]{1,0:T(8,128)S(1)} %bitcast.186), channel_id=1, source_target_pairs={{0,2},{2,0},{4,6},{6,4},{8,10},{10,8},{12,14},{14,12},{1,3},{3,1},... | collective-permute-start | bytes 196616 | tf_op jit(solution)/shard_map/ppermute | solution.py:65
  60.7 7.4 %collective-permute-start.12 = (f32[16,1024]{1,0:T(8,128)S(1)}, f32[16,1024]{1,0:T(8,128)S(1)}, u32[]{:S(2)}, u32[]{:S(2)}) collective-permute-start(f32[16,1024]{1,0:T(8,128)S(1)} %bitcast.185), channel_id=1, source_target_pairs={{0,4},{2,6},{4,0},{6,2},{8,12},{10,14},{12,8},{14,10},{1,5},{3,7},... | collective-permute-start | bytes 196616 | tf_op jit(solution)/shard_map/ppermute | solution.py:65
  61.8 9.1 %collective-permute-start.13 = (f32[16,1024]{1,0:T(8,128)S(1)}, f32[16,1024]{1,0:T(8,128)S(1)}, u32[]{:S(2)}, u32[]{:S(2)}) collective-permute-start(f32[16,1024]{1,0:T(8,128)S(1)} %bitcast.180), channel_id=1, source_target_pairs={{0,6},{2,4},{4,2},{6,0},{8,14},{10,12},{12,10},{14,8},{1,7},{3,5},... | collective-permute-start | bytes 196616 | tf_op jit(solution)/shard_map/ppermute | solution.py:65
  62.8 8.8 %collective-permute-start.14 = (f32[16,1024]{1,0:T(8,128)S(1)}, f32[16,1024]{1,0:T(8,128)S(1)}, u32[]{:S(2)}, u32[]{:S(2)}) collective-permute-start(f32[16,1024]{1,0:T(8,128)S(1)} %bitcast.181), channel_id=1, source_target_pairs={{0,8},{2,10},{4,12},{6,14},{8,0},{10,2},{12,4},{14,6},{1,9},{3,11}... | collective-permute-start | bytes 196616 | tf_op jit(solution)/shard_map/ppermute | solution.py:65
  65.5 10.2 %collective-permute-start.15 = (f32[16,1024]{1,0:T(8,128)S(1)}, f32[16,1024]{1,0:T(8,128)S(1)}, u32[]{:S(2)}, u32[]{:S(2)}) collective-permute-start(f32[16,1024]{1,0:T(8,128)S(1)} %bitcast.182), channel_id=1, source_target_pairs={{0,10},{2,8},{4,14},{6,12},{8,2},{10,0},{12,6},{14,4},{1,11},{3,9}... | collective-permute-start | bytes 196616 | tf_op jit(solution)/shard_map/ppermute | solution.py:65
  66.9 8.9 %collective-permute-start.16 = (f32[16,1024]{1,0:T(8,128)S(1)}, f32[16,1024]{1,0:T(8,128)S(1)}, u32[]{:S(2)}, u32[]{:S(2)}) collective-permute-start(f32[16,1024]{1,0:T(8,128)S(1)} %bitcast.184), channel_id=1, source_target_pairs={{0,12},{2,14},{4,8},{6,10},{8,4},{10,6},{12,0},{14,2},{1,13},{3,15... | collective-permute-start | bytes 196616 | tf_op jit(solution)/shard_map/ppermute | solution.py:65
  68.1 7.7 %collective-permute-start.17 = (f32[16,1024]{1,0:T(8,128)S(1)}, f32[16,1024]{1,0:T(8,128)S(1)}, u32[]{:S(2)}, u32[]{:S(2)}) collective-permute-start(f32[16,1024]{1,0:T(8,128)S(1)} %bitcast.183), channel_id=1, source_target_pairs={{0,14},{2,12},{4,10},{6,8},{8,6},{10,4},{12,2},{14,0},{1,15},{3,13... | collective-permute-start | bytes 196616 | tf_op jit(solution)/shard_map/ppermute | solution.py:65
  75.8 4.0 %collective-permute-start.18 = (bf16[16,1024]{1,0:T(8,128)(2,1)S(1)}, bf16[16,1024]{1,0:T(8,128)(2,1)S(1)}, u32[]{:S(2)}, u32[]{:S(2)}) collective-permute-start(bf16[16,1024]{1,0:T(8,128)(2,1)S(1)} %clamp_convert_fusion), channel_id=1, source_target_pairs={{0,2},{2,0},{4,6},{6,4},{8,10},{10,8},{12,14},{14,12},{1,3},{3,1},... | collective-permute-start | bytes 98312 | tf_op jit(solution)/shard_map/ppermute | solution.py:27
  79.8 6.8 %collective-permute-start.19 = (bf16[2,16,1024]{2,1,0:T(8,128)(2,1)S(1)}, bf16[2,16,1024]{2,1,0:T(8,128)(2,1)S(1)}, u32[]{:S(2)}, u32[]{:S(2)}) collective-permute-start(bf16[2,16,1024]{2,1,0:T(8,128)(2,1)S(1)} %maximum_select_fusion.3), channel_id=1, source_target_pairs={{0,4},{2,6},{4,8},{6,10},{8,12},{10,14},{12,0},{14,2},{1,5},{3,7},... | collective-permute-start | bytes 196616 | tf_op jit(solution)/shard_map/ppermute | solution.py:33
  82.9 6.0 %collective-permute-start.20 = (bf16[2,16,1024]{2,1,0:T(8,128)(2,1)S(1)}, bf16[2,16,1024]{2,1,0:T(8,128)(2,1)S(1)}, u32[]{:S(2)}, u32[]{:S(2)}) collective-permute-start(bf16[2,16,1024]{2,1,0:T(8,128)(2,1)S(1)} %maximum_select_fusion.3), channel_id=1, source_target_pairs={{0,8},{2,10},{4,12},{6,14},{8,0},{10,2},{12,4},{14,6},{1,9},{3,11}... | collective-permute-start | bytes 196616 | tf_op jit(solution)/shard_map/ppermute | solution.py:33
  83.1 5.9 %collective-permute-start.21 = (bf16[2,16,1024]{2,1,0:T(8,128)(2,1)S(1)}, bf16[2,16,1024]{2,1,0:T(8,128)(2,1)S(1)}, u32[]{:S(2)}, u32[]{:S(2)}) collective-permute-start(bf16[2,16,1024]{2,1,0:T(8,128)(2,1)S(1)} %maximum_select_fusion.3), channel_id=1, source_target_pairs={{0,12},{2,14},{4,0},{6,2},{8,4},{10,6},{12,8},{14,10},{1,13},{3,15... | collective-permute-start | bytes 196616 | tf_op jit(solution)/shard_map/ppermute | solution.py:33

commit v16 on v10

--- a/solution.py
+++ b/solution.py
@@ -208,6 +208,39 @@
     )(q_rows, prefix_kv, prefix_kv, tail_kv, tail_kv, valid)
 
 
+def _attend_packed_pairs(blk, q_rows, prefix_kv, tail_kv, valid, group):
+    heads_n, rows_n, _ = q_rows.shape
+    prefix_dev = prefix_kv.shape[1]
+    samples, tail_dev = tail_kv.shape[1], tail_kv.shape[2]
+    flops = 4 * heads_n * rows_n * DH * (prefix_dev + samples * tail_dev)
+    width = 2 * DH
+    grid_spec = pltpu.PrefetchScalarGridSpec(
+        num_scalar_prefetch=1,
+        grid=(heads_n // 2,),
+        in_specs=[
+            pl.BlockSpec((2, rows_n, DH), lambda g, b: (g, 0, 0)),
+            pl.BlockSpec((1, prefix_dev, width), lambda g, b: (0, 0, b[g])),
+            pl.BlockSpec((1, prefix_dev, width), lambda g, b: (1, 0, b[g])),
+            pl.BlockSpec((1, samples, tail_dev, width), lambda g, b: (0, 0, 0, b[g])),
+            pl.BlockSpec((1, samples, tail_dev, width), lambda g, b: (1, 0, 0, b[g])),
+            pl.BlockSpec((samples, tail_dev), lambda g, b: (0, 0)),
+        ],
+        out_specs=pl.BlockSpec((2, rows_n + 8, DH), lambda g, b: (g, 0, 0)),
+    )
+    return pl.pallas_call(
+        lambda b_ref, *refs: _attend_packed_kernel(group, *refs),
+        grid_spec=grid_spec,
+        out_shape=jax.ShapeDtypeStruct((heads_n, rows_n + 8, DH), jnp.float32),
+        cost_estimate=pl.CostEstimate(
+            flops=flops,
+            transcendentals=heads_n * rows_n * (prefix_dev + tail_dev),
+            bytes_accessed=2 * (2 * prefix_dev + 2 * samples * tail_dev) * heads_n * DH
+            + 2 * q_rows.size + 4 * heads_n * (rows_n + 8) * DH,
+        ),
+        compiler_params=pltpu.CompilerParams(vmem_limit_bytes=48 * 1024 * 1024),
+    )(blk.astype(jnp.int32), q_rows, prefix_kv, prefix_kv, tail_kv, tail_kv, valid)
+
+
 def per_device(
     queries, prefix_kv, tail_kv, tail_lengths, fresh_kv, out_weight, scale_in, scale_out, residual
 ):
@@ -223,43 +256,82 @@
     tail_dev = tail_kv.shape[2]
     score_scale = 1.0 / math.sqrt(DH)
 
-    q_blocks = _gather_blocks(queries, "tp", tp_count)
-    q_all = jnp.moveaxis(q_blocks, 0, 2).reshape(steps_n, rows_dev, kv_heads, group, DH)
-    t_pos = tp_rank * tail_dev + jnp.arange(tail_dev)
-    valid = (t_pos[None, :] < tail_lengths[:, None]).astype(jnp.float32)
     n_rows = steps_n * rows_dev * heads_dev
-    if tp_count == kv_heads and heads_dev == group and n_rows == DH:
-        q_rows = jnp.transpose(q_all, (2, 0, 1, 3, 4)).reshape(kv_heads, -1, DH)
-        got = _exchange(_attend_packed(q_rows, prefix_kv, tail_kv, valid, group), "tp", tp_count)
+    pairs_ok = (tp_count == kv_heads and heads_dev == group and n_rows == DH
+                and tp_count in (4, 8))
+    if pairs_ok:
+        t_pos = tp_rank * tail_dev + jnp.arange(tail_dev)
+        valid = (t_pos[None, :] < tail_lengths[:, None]).astype(jnp.float32)
+        half = tp_count // 2
+        mine = tp_rank // 2
+        other = lax.ppermute(queries, "tp", [(i, i ^ 1) for i in range(tp_count)])
+        pair = jnp.where(tp_rank % 2 == 0, jnp.stack([queries, other]), jnp.stack([other, queries]))
+        far = [
+            lax.ppermute(pair, "tp", [(i, (i + 2 * d) % tp_count) for i in range(tp_count)])
+            for d in range(1, half)
+        ]
+        out_near = _attend_packed_pairs(
+            jnp.reshape(mine, (1,)), pair.reshape(2, -1, DH), prefix_kv, tail_kv, valid, group
+        )
+        far_blk = (mine - jnp.arange(1, half)) % half
+        out_far = _attend_packed_pairs(
+            far_blk, jnp.stack(far).reshape(2 * (half - 1), -1, DH), prefix_kv, tail_kv, valid,
+            group,
+        )
+        outs = jnp.concatenate([out_near, out_far])
+
+        def position(head):
+            d = (mine - head // 2) % half
+            return jnp.where(d == 0, head % 2, 2 * d + head % 2)
+
+        got = [lax.dynamic_index_in_dim(outs, position(tp_rank), 0, keepdims=False)]
+        for k in range(1, tp_count):
+            send = lax.dynamic_index_in_dim(outs, position((tp_rank + k) % tp_count), 0, keepdims=False)
+            got.append(lax.ppermute(send, "tp", [(i, (i + k) % tp_count) for i in range(tp_count)]))
+        got = jnp.stack(got)
         got_numer = got[:, :n_rows].reshape(tp_count, steps_n, rows_dev, heads_dev, DH)
         got_peak = got[:, n_rows].reshape(tp_count, steps_n, rows_dev, heads_dev)
         got_mass = got[:, n_rows + 1].reshape(tp_count, steps_n, rows_dev, heads_dev)
+        q_blocks = None
     else:
-
-        q_rows = jnp.transpose(q_all, (2, 1, 0, 3, 4)).reshape(kv_heads, -1, DH)
+        q_blocks = _gather_blocks(queries, "tp", tp_count)
+    if not pairs_ok:
+        q_all = jnp.moveaxis(q_blocks, 0, 2).reshape(steps_n, rows_dev, kv_heads, group, DH)
         t_pos = tp_rank * tail_dev + jnp.arange(tail_dev)
         valid = (t_pos[None, :] < tail_lengths[:, None]).astype(jnp.float32)
-        k_numer, k_peak, k_mass = _attend_local(q_rows, prefix_kv, tail_kv, valid)
-
-        def by_owner(x):
-            x = jnp.transpose(x, (2, 1, 0, 3) + tuple(range(4, x.ndim)))
-            x = x.reshape((steps_n, rows_dev, tp_count, heads_dev) + x.shape[4:])
-            return jnp.moveaxis(x, 2, 0)
-
-        grid4 = (kv_heads, rows_dev, steps_n, group)
-        o_numer = by_owner(k_numer.reshape(grid4 + (DH,))).reshape(tp_count, -1, DH)
-        o_peak = by_owner(k_peak[..., 0].reshape(grid4)).reshape(tp_count, -1)
-        o_mass = by_owner(k_mass[..., 0].reshape(grid4)).reshape(tp_count, -1)
         n_rows = steps_n * rows_dev * heads_dev
-        n_stat = -(-2 * n_rows // DH)
-        stats = jnp.concatenate([o_peak, o_mass], axis=1)
-        stats = jnp.pad(stats, ((0, 0), (0, n_stat * DH - 2 * n_rows))).reshape(tp_count, n_stat, DH)
-        got = _exchange(jnp.concatenate([o_numer, stats], axis=1), "tp", tp_count)
-        got_numer = got[:, :n_rows].reshape(tp_count, steps_n, rows_dev, heads_dev, DH)
-        got_stats = got[:, n_rows:].reshape(tp_count, -1)[:, : 2 * n_rows]
-        got_stats = got_stats.reshape(tp_count, 2, steps_n, rows_dev, heads_dev)
-        got_peak = got_stats[:, 0]
-        got_mass = got_stats[:, 1]
+        if tp_count == kv_heads and heads_dev == group and n_rows == DH:
+            q_rows = jnp.transpose(q_all, (2, 0, 1, 3, 4)).reshape(kv_heads, -1, DH)
+            got = _exchange(_attend_packed(q_rows, prefix_kv, tail_kv, valid, group), "tp", tp_count)
+            got_numer = got[:, :n_rows].reshape(tp_count, steps_n, rows_dev, heads_dev, DH)
+            got_peak = got[:, n_rows].reshape(tp_count, steps_n, rows_dev, heads_dev)
+            got_mass = got[:, n_rows + 1].reshape(tp_count, steps_n, rows_dev, heads_dev)
+        else:
+
+            q_rows = jnp.transpose(q_all, (2, 1, 0, 3, 4)).reshape(kv_heads, -1, DH)
+            t_pos = tp_rank * tail_dev + jnp.arange(tail_dev)
+            valid = (t_pos[None, :] < tail_lengths[:, None]).astype(jnp.float32)
+            k_numer, k_peak, k_mass = _attend_local(q_rows, prefix_kv, tail_kv, valid)
+
+            def by_owner(x):
+                x = jnp.transpose(x, (2, 1, 0, 3) + tuple(range(4, x.ndim)))
+                x = x.reshape((steps_n, rows_dev, tp_count, heads_dev) + x.shape[4:])
+                return jnp.moveaxis(x, 2, 0)
+
+            grid4 = (kv_heads, rows_dev, steps_n, group)
+            o_numer = by_owner(k_numer.reshape(grid4 + (DH,))).reshape(tp_count, -1, DH)
+            o_peak = by_owner(k_peak[..., 0].reshape(grid4)).reshape(tp_count, -1)
+            o_mass = by_owner(k_mass[..., 0].reshape(grid4)).reshape(tp_count, -1)
+            n_rows = steps_n * rows_dev * heads_dev
+            n_stat = -(-2 * n_rows // DH)
+            stats = jnp.concatenate([o_peak, o_mass], axis=1)
+            stats = jnp.pad(stats, ((0, 0), (0, n_stat * DH - 2 * n_rows))).reshape(tp_count, n_stat, DH)
+            got = _exchange(jnp.concatenate([o_numer, stats], axis=1), "tp", tp_count)
+            got_numer = got[:, :n_rows].reshape(tp_count, steps_n, rows_dev, heads_dev, DH)
+            got_stats = got[:, n_rows:].reshape(tp_count, -1)[:, : 2 * n_rows]
+            got_stats = got_stats.reshape(tp_count, 2, steps_n, rows_dev, heads_dev)
+            got_peak = got_stats[:, 0]
+            got_mass = got_stats[:, 1]
 
     own_query = queries.reshape(steps_n, rows_dev, heads_dev, DH)
     f_kv = fresh_kv.reshape(2, steps_n, rows_dev, kv_heads, DH)

time: 88.1 us -> 89.3 us (1.014)
  waiting for transfers between devices: 14.7 us -> 9.93 us
  starting transfers between devices: 38.6 us -> 42.9 us
  Pallas kernels: 5.87 us -> 8.06 us
    ppermute x0 -> x11, starting transfers between devices: none -> 18.2 us  [the longest x7 9.74 us: per_device(): lax.ppermute(send, 'tp', [(i, (i + k) % tp_count) for i in range(tp_count)])]
    ppermute x14 -> x7, starting transfers between devices: 23.5 us -> 15 us  [_exchange(): lax.ppermute(send, axis_name, [(i, (i + k) % count) for i in range(count)])]
    ppermute x6 -> x3, waiting for transfers between devices: 6.46 us -> 1.88 us  [_gather_blocks(): lax.ppermute(pair, axis_name, [(i, (i + 2 * d) % count) for i in range(co...]
    ppermute x14 -> x7, waiting for transfers between devices: 6.37 us -> 1.8 us  [_exchange(): lax.ppermute(send, axis_name, [(i, (i + k) % count) for i in range(count)])]
    ppermute x0 -> x11, waiting for transfers between devices: none -> 4.38 us  [the longest x7 4.35 us: per_device(): lax.ppermute(send, 'tp', [(i, (i + k) % tp_count) for i in range(tp_count)])]
    ppermute x2 -> x1, starting transfers between devices: 5.16 us -> 2.13 us  [_gather_blocks(): other = lax.ppermute(x, axis_name, [(i, i ^ 1) for i in range(count)])]
    ppermute x6 -> x3, starting transfers between devices: 10 us -> 7.51 us  [_gather_blocks(): lax.ppermute(pair, axis_name, [(i, (i + 2 * d) % count) for i in range(co...]
    pallas_call x1 -> x2, Pallas kernels: 5.87 us -> 8.06 us  [_attend_packed_pairs(): pl.pallas_call(lambda b_ref, *refs: _attend_packed_kernel(group, *refs),...]
  transfers between devices with their start and end apart: 22 -> 22, of which waited for: 13 -> 9; matrix products, arithmetic and copies ran while one was open for 6% -> 5% of each run, Pallas kernels for 0% -> 3%
where the time goes in v16:
time: 89.3 us; the launch traced here: 88.9 us
  starting transfers between devices  42.9 us (48%)
  matrix products  13.3 us (15%)
  waiting for transfers between devices  9.93 us (11%)
  Pallas kernels  8.06 us (9%)
  local copies, waits for them, and re-layouts  7.65 us (9%)
  other arithmetic  4.18 us (5%)
  blocking collectives  1.85 us (2%)
  between operations  1.04 us (1%)
    ppermute x7, starting transfers between devices, _exchange(): lax.ppermute(send, axis_name, [(i, (i + k) % count) for i in range(count)])  15 us
    dot_general x1, matrix products, per_device(): jnp.einsum('rhd,hdf->rhf', head_rows_in, head_weights, preferred_element_...  12.9 us
    ppermute x7, starting transfers between devices, per_device(): lax.ppermute(send, 'tp', [(i, (i + k) % tp_count) for i in range(tp_count)])  9.74 us
    pallas_call x2, Pallas kernels, _attend_packed_pairs(): pl.pallas_call(lambda b_ref, *refs: _attend_packed_kernel(group, *refs),...  8.06 us
    ppermute x3, starting transfers between devices, _gather_blocks(): lax.ppermute(pair, axis_name, [(i, (i + 2 * d) % count) for i in range(co...  7.51 us
    ppermute x3, starting transfers between devices, per_device(): lax.ppermute(pair, 'tp', [(i, (i + 2 * d) % tp_count) for i in range(tp_c...  5.57 us
    ppermute x7, waiting for transfers between devices, per_device(): lax.ppermute(send, 'tp', [(i, (i + k) % tp_count) for i in range(tp_count)])  4.35 us
    ppermute x1, starting transfers between devices, per_device(): other = lax.ppermute(queries, 'tp', [(i, i ^ 1) for i in range(tp_count)])  2.94 us
  transfers between devices with their start and end apart: 22, of which 9 were waited for; matrix products, arithmetic and copies ran while one was open for 5% of the time, Pallas kernels for 3%

profile of v16, /device:TPU:0, one launch (start us, length us, event | category | flops | bytes accessed | tf_op | source)
XLA Modules:
  0.0 88.9 jit_solution(13818621868816211108)
XLA Ops:
  0.0 2.9 %collective-permute-start = (bf16[2,4,2048]{2,1,0:T(4,128)(2,1)}, bf16[2,4,2048]{2,1,0:T(4,128)(2,1)S(1)}, u32[]{:S(2)}, u32[]{:S(2)}) collective-permute-start(bf16[2,4,2048]{2,1,0:T(4,128)(2,1)} %param.9), channel_id=1, source_target_pairs={{0,2},{2,0},{4,6},{6,4},{8,10},{10,8},{12,14},{14,12},{1,3},{3,1},... | collective-permute-start | bytes 98312 | tf_op jit(solution)/shard_map/ppermute | solution.py:267
  2.9 0.8 reshape.287
  3.8 0.8 reshape.286
  4.6 0.2 fusion.30
  5.0 0.7 multiply_exponential_fusion.1
  5.7 0.7 compare_convert_fusion.refs_5_
  6.7 0.8 stack.101
  8.1 0.9 %maximum_select_fusion.1 = bf16[2,2,4,2048]{3,2,1,0:T(4,128)(2,1)S(1)} fusion(bf16[1,2,4,2048]{3,2,1,0:T(4,128)(2,1)S(1)} %bitcast.132, bf16[1,2,4,2048]{3,2,1,0:T(4,128)(2,1)} %bitcast.127, pred[]{:T(512)S(6)} %eq.71), kind=kLoop, calls=%fused_computation.50 | loop fusion | flops 98304 | bytes 131073 | tf_op jit(solution)/shard_map/jit(_where)/select_n | solution.py:268
  9.0 1.6 %collective-permute-start.1 = (bf16[2,2,4,2048]{3,2,1,0:T(4,128)(2,1)S(1)}, bf16[2,2,4,2048]{3,2,1,0:T(4,128)(2,1)S(1)}, u32[]{:S(2)}, u32[]{:S(2)}) collective-permute-start(bf16[2,2,4,2048]{3,2,1,0:T(4,128)(2,1)S(1)} %maximum_select_fusion.1), channel_id=1, source_target_pairs={{0,4},{2,6},{4,8},{6,10},{8,12},{10,14},{12,0},{14,2},{1,5},{3,7},... | collective-permute-start | bytes 196616 | tf_op jit(solution)/shard_map/ppermute | solution.py:270
  10.7 2.6 %collective-permute-start.2 = (bf16[2,2,4,2048]{3,2,1,0:T(4,128)(2,1)S(1)}, bf16[2,2,4,2048]{3,2,1,0:T(4,128)(2,1)S(1)}, u32[]{:S(2)}, u32[]{:S(2)}) collective-permute-start(bf16[2,2,4,2048]{3,2,1,0:T(4,128)(2,1)S(1)} %maximum_select_fusion.1), channel_id=1, source_target_pairs={{0,8},{2,10},{4,12},{6,14},{8,0},{10,2},{12,4},{14,6},{1,9},{3,11}... | collective-permute-start | bytes 196616 | tf_op jit(solution)/shard_map/ppermute | solution.py:270
  13.3 1.3 %collective-permute-start.3 = (bf16[2,2,4,2048]{3,2,1,0:T(4,128)(2,1)S(1)}, bf16[2,2,4,2048]{3,2,1,0:T(4,128)(2,1)S(1)}, u32[]{:S(2)}, u32[]{:S(2)}) collective-permute-start(bf16[2,2,4,2048]{3,2,1,0:T(4,128)(2,1)S(1)} %maximum_select_fusion.1), channel_id=1, source_target_pairs={{0,12},{2,14},{4,0},{6,2},{8,4},{10,6},{12,8},{14,10},{1,13},{3,15... | collective-permute-start | bytes 196616 | tf_op jit(solution)/shard_map/ppermute | solution.py:270
  14.7 1.6 %copy-done = bf16[2,4,128,1024]{3,2,1,0:T(8,128)(2,1)S(1)} copy-done((bf16[2,4,128,1024]{3,2,1,0:T(8,128)(2,1)S(1)}, bf16[2,4,128,1024]{3,2,1,0:T(8,128)(2,1)}, u32[]{:S(2)}) %copy-start) | copy-done | bytes 2097176
  16.2 2.6 %shard_map.91 = f32[2,136,128]{2,1,0:T(8,128)S(1)} custom-call(s32[1]{0:T(128)} %bitcast.1.b_ref, bf16[2,128,128]{2,1,0:T(8,128)(2,1)S(1)} %maximum_select_fusion.refs_0_, bf16[2,1024,1024]{2,1,0:T(8,128)(2,1)} %refs_2_.3, bf16[2,1024,1024]{2,1,0:T(8,128)(2,1)} %refs_2_.3, bf16[2,4,128,1024]{3,2,1,0:T(8,128)(2,1)S(1)} %copy-done, ...), custom_call_target="tpu_custom_call" | custom-call | flops 201326592 | bytes 1777664 | tf_op jit(solution)/shard_map/pallas_call | solution.py:230
  19.1 5.5 %shard_map.92 = f32[6,136,128]{2,1,0:T(8,128)S(1)} custom-call(s32[3]{0:T(128)S(1)} %and_select_fusion.b_ref, bf16[6,128,128]{2,1,0:T(8,128)(2,1)S(1)} %reshape.285.refs_0_, bf16[2,1024,1024]{2,1,0:T(8,128)(2,1)} %refs_2_.3, bf16[2,1024,1024]{2,1,0:T(8,128)(2,1)} %refs_2_.3, bf16[2,4,128,1024]{3,2,1,0:T(8,128)(2,1)S(1)} %copy-done.1, ...), custom_call_target="tpu_custom_call" | custom-call | flops 603979776 | bytes 5332992 | tf_op jit(solution)/shard_map/pallas_call | solution.py:230
  24.8 0.6 collective-permute-start.4
  25.4 2.9 %collective-permute-start.8 = (f32[136,128]{1,0:T(8,128)S(1)}, f32[136,128]{1,0:T(8,128)S(1)}, u32[]{:S(2)}, u32[]{:S(2)}) collective-permute-start(f32[136,128]{1,0:T(8,128)S(1)} %get-tuple-element.14), channel_id=1, source_target_pairs={{0,10},{2,12},{4,14},{6,0},{8,2},{10,4},{12,6},{14,8},{1,11},{3,13... | collective-permute-start | bytes 208904 | tf_op jit(solution)/shard_map/ppermute | solution.py:290
  28.3 1.9 %collective-permute-start.5 = (f32[136,128]{1,0:T(8,128)S(1)}, f32[136,128]{1,0:T(8,128)S(1)}, u32[]{:S(2)}, u32[]{:S(2)}) collective-permute-start(f32[136,128]{1,0:T(8,128)S(1)} %get-tuple-element.10), channel_id=1, source_target_pairs={{0,4},{2,6},{4,8},{6,10},{8,12},{10,14},{12,0},{14,2},{1,5},{3,7},... | collective-permute-start | bytes 208904 | tf_op jit(solution)/shard_map/ppermute | solution.py:290
  30.2 2.4 %collective-permute-start.7 = (f32[136,128]{1,0:T(8,128)S(1)}, f32[136,128]{1,0:T(8,128)S(1)}, u32[]{:S(2)}, u32[]{:S(2)}) collective-permute-start(f32[136,128]{1,0:T(8,128)S(1)} %get-tuple-element.12), channel_id=1, source_target_pairs={{0,8},{2,10},{4,12},{6,14},{8,0},{10,2},{12,4},{14,6},{1,9},{3,11}... | collective-permute-start | bytes 208904 | tf_op jit(solution)/shard_map/ppermute | solution.py:290
  32.6 0.6 collective-permute-start.9
  33.2 1.4 %collective-permute-done.5 = f32[136,128]{1,0:T(8,128)S(1)} collective-permute-done((f32[136,128]{1,0:T(8,128)S(1)}, f32[136,128]{1,0:T(8,128)S(1)}, u32[]{:S(2)}, u32[]{:S(2)}) %collective-permute-start.5) | collective-permute-done | bytes 69664 | tf_op jit(solution)/shard_map/ppermute | solution.py:290
  34.6 1.4 %collective-permute-start.10 = (f32[136,128]{1,0:T(8,128)S(1)}, f32[136,128]{1,0:T(8,128)S(1)}, u32[]{:S(2)}, u32[]{:S(2)}) collective-permute-start(f32[136,128]{1,0:T(8,128)S(1)} %get-tuple-element.7), channel_id=1, source_target_pairs={{0,14},{2,0},{4,2},{6,4},{8,6},{10,8},{12,10},{14,12},{1,15},{3,1}... | collective-permute-start | bytes 208904 | tf_op jit(solution)/shard_map/ppermute | solution.py:290
  36.0 2.5 %collective-permute-done.6 = f32[136,128]{1,0:T(8,128)S(1)} collective-permute-done((f32[136,128]{1,0:T(8,128)S(1)}, f32[136,128]{1,0:T(8,128)S(1)}, u32[]{:S(2)}, u32[]{:S(2)}) %collective-permute-start.6) | collective-permute-done | bytes 69664 | tf_op jit(solution)/shard_map/ppermute | solution.py:290
  38.6 0.4 collective-permute-done.10
  40.0 0.2 fusion.2
  40.6 1.9 %all_gather.3 = bf16[2,8,2048]{2,0,1:T(2,128)(2,1)S(1)} all-gather(bf16[2,4,2048]{2,0,1:T(2,128)(2,1)S(1)} %copy.56), channel_id=1, replica_groups=mesh['rep'=2,'tp'=8,'sub'=2] {'sub'}, dimensions={1}, use_global_device_ids=true | all-gather | bytes 98304 | tf_op jit(solution)/shard_map/all_gather | solution.py:361
  42.5 12.9 %fusion.1 = f32[16,8192]{1,0:T(8,128)S(1)} fusion(f32[8192]{0:T(1024)S(1)} %dynamic_slice.61, bf16[16,128,8192]{2,1,0:T(8,128)(2,1)} %bitcast.150, bf16[16,16,128]{2,1,0:T(8,128)(2,1)S(1)} %bitcast.142), kind=kOutput, calls=%fused_computation.3 | convolution fusion | flops 543031296 | bytes 34177024 | tf_op jit(solution)/shard_map/rhd,hdf->rhf/dot_general | solution.py:370
  55.4 0.3 copy.74
  55.8 0.5 constant_dynamic-slice_fusion.8
  56.3 2.8 %collective-permute-start.11 = (f32[16,1024]{1,0:T(8,128)S(1)}, f32[16,1024]{1,0:T(8,128)S(1)}, u32[]{:S(2)}, u32[]{:S(2)}) collective-permute-start(f32[16,1024]{1,0:T(8,128)S(1)} %bitcast.141), channel_id=1, source_target_pairs={{0,2},{2,4},{4,6},{6,8},{8,10},{10,12},{12,14},{14,0},{1,3},{3,5},... | collective-permute-start | bytes 196616 | tf_op jit(solution)/shard_map/ppermute | solution.py:61
  59.2 2.3 %collective-permute-start.12 = (f32[16,1024]{1,0:T(8,128)S(1)}, f32[16,1024]{1,0:T(8,128)S(1)}, u32[]{:S(2)}, u32[]{:S(2)}) collective-permute-start(f32[16,1024]{1,0:T(8,128)S(1)} %bitcast.140), channel_id=1, source_target_pairs={{0,4},{2,6},{4,8},{6,10},{8,12},{10,14},{12,0},{14,2},{1,5},{3,7},... | collective-permute-start | bytes 196616 | tf_op jit(solution)/shard_map/ppermute | solution.py:61
  61.5 1.5 %collective-permute-start.13 = (f32[16,1024]{1,0:T(8,128)S(1)}, f32[16,1024]{1,0:T(8,128)S(1)}, u32[]{:S(2)}, u32[]{:S(2)}) collective-permute-start(f32[16,1024]{1,0:T(8,128)S(1)} %bitcast.135), channel_id=1, source_target_pairs={{0,6},{2,8},{4,10},{6,12},{8,14},{10,0},{12,2},{14,4},{1,7},{3,9},... | collective-permute-start | bytes 196616 | tf_op jit(solution)/shard_map/ppermute | solution.py:61
  63.0 2.0 %collective-permute-start.14 = (f32[16,1024]{1,0:T(8,128)S(1)}, f32[16,1024]{1,0:T(8,128)S(1)}, u32[]{:S(2)}, u32[]{:S(2)}) collective-permute-start(f32[16,1024]{1,0:T(8,128)S(1)} %bitcast.136), channel_id=1, source_target_pairs={{0,8},{2,10},{4,12},{6,14},{8,0},{10,2},{12,4},{14,6},{1,9},{3,11}... | collective-permute-start | bytes 196616 | tf_op jit(solution)/shard_map/ppermute | solution.py:61
  65.0 1.1 %collective-permute-start.15 = (f32[16,1024]{1,0:T(8,128)S(1)}, f32[16,1024]{1,0:T(8,128)S(1)}, u32[]{:S(2)}, u32[]{:S(2)}) collective-permute-start(f32[16,1024]{1,0:T(8,128)S(1)} %bitcast.137), channel_id=1, source_target_pairs={{0,10},{2,12},{4,14},{6,0},{8,2},{10,4},{12,6},{14,8},{1,11},{3,13... | collective-permute-start | bytes 196616 | tf_op jit(solution)/shard_map/ppermute | solution.py:61
  66.1 2.4 %collective-permute-start.16 = (f32[16,1024]{1,0:T(8,128)S(1)}, f32[16,1024]{1,0:T(8,128)S(1)}, u32[]{:S(2)}, u32[]{:S(2)}) collective-permute-start(f32[16,1024]{1,0:T(8,128)S(1)} %bitcast.139), channel_id=1, source_target_pairs={{0,12},{2,14},{4,0},{6,2},{8,4},{10,6},{12,8},{14,10},{1,13},{3,15... | collective-permute-start | bytes 196616 | tf_op jit(solution)/shard_map/ppermute | solution.py:61
  68.5 2.9 %collective-permute-start.17 = (f32[16,1024]{1,0:T(8,128)S(1)}, f32[16,1024]{1,0:T(8,128)S(1)}, u32[]{:S(2)}, u32[]{:S(2)}) collective-permute-start(f32[16,1024]{1,0:T(8,128)S(1)} %bitcast.138), channel_id=1, source_target_pairs={{0,14},{2,0},{4,2},{6,4},{8,6},{10,8},{12,10},{14,12},{1,15},{3,1}... | collective-permute-start | bytes 196616 | tf_op jit(solution)/shard_map/ppermute | solution.py:61
  71.6 0.9 collective-permute-done.14
  72.4 0.5 collective-permute-done.15
  72.9 0.4 collective-permute-done.17
  73.4 2.1 %collective-permute-start.18 = (bf16[16,1024]{1,0:T(8,128)(2,1)S(1)}, bf16[16,1024]{1,0:T(8,128)(2,1)S(1)}, u32[]{:S(2)}, u32[]{:S(2)}) collective-permute-start(bf16[16,1024]{1,0:T(8,128)(2,1)S(1)} %clamp_convert_fusion), channel_id=1, source_target_pairs={{0,2},{2,0},{4,6},{6,4},{8,10},{10,8},{12,14},{14,12},{1,3},{3,1},... | collective-permute-start | bytes 98312 | tf_op jit(solution)/shard_map/ppermute | solution.py:28
  75.6 1.9 %collective-permute-done.18 = bf16[16,1024]{1,0:T(8,128)(2,1)S(1)} collective-permute-done((bf16[16,1024]{1,0:T(8,128)(2,1)S(1)}, bf16[16,1024]{1,0:T(8,128)(2,1)S(1)}, u32[]{:S(2)}, u32[]{:S(2)}) %collective-permute-start.18) | collective-permute-done | bytes 32800 | tf_op jit(solution)/shard_map/ppermute | solution.py:28
  77.5 2.8 %collective-permute-start.19 = (bf16[2,16,1024]{2,1,0:T(8,128)(2,1)S(1)}, bf16[2,16,1024]{2,1,0:T(8,128)(2,1)S(1)}, u32[]{:S(2)}, u32[]{:S(2)}) collective-permute-start(bf16[2,16,1024]{2,1,0:T(8,128)(2,1)S(1)} %maximum_select_fusion.3), channel_id=1, source_target_pairs={{0,4},{2,6},{4,8},{6,10},{8,12},{10,14},{12,0},{14,2},{1,5},{3,7},... | collective-permute-start | bytes 196616 | tf_op jit(solution)/shard_map/ppermute | solution.py:34
  80.2 2.0 %collective-permute-start.20 = (bf16[2,16,1024]{2,1,0:T(8,128)(2,1)S(1)}, bf16[2,16,1024]{2,1,0:T(8,128)(2,1)S(1)}, u32[]{:S(2)}, u32[]{:S(2)}) collective-permute-start(bf16[2,16,1024]{2,1,0:T(8,128)(2,1)S(1)} %maximum_select_fusion.3), channel_id=1, source_target_pairs={{0,8},{2,10},{4,12},{6,14},{8,0},{10,2},{12,4},{14,6},{1,9},{3,11}... | collective-permute-start | bytes 196616 | tf_op jit(solution)/shard_map/ppermute | solution.py:34
  82.3 2.7 %collective-permute-start.21 = (bf16[2,16,1024]{2,1,0:T(8,128)(2,1)S(1)}, bf16[2,16,1024]{2,1,0:T(8,128)(2,1)S(1)}, u32[]{:S(2)}, u32[]{:S(2)}) collective-permute-start(bf16[2,16,1024]{2,1,0:T(8,128)(2,1)S(1)} %maximum_select_fusion.3), channel_id=1, source_target_pairs={{0,12},{2,14},{4,0},{6,2},{8,4},{10,6},{12,8},{14,10},{1,13},{3,15... | collective-permute-start | bytes 196616 | tf_op jit(solution)/shard_map/ppermute | solution.py:34
  85.0 0.4 collective-permute-done.20
  85.4 1.5 %collective-permute-done.21 = bf16[2,16,1024]{2,1,0:T(8,128)(2,1)S(1)} collective-permute-done((bf16[2,16,1024]{2,1,0:T(8,128)(2,1)S(1)}, bf16[2,16,1024]{2,1,0:T(8,128)(2,1)S(1)}, u32[]{:S(2)}, u32[]{:S(2)}) %collective-permute-start.21) | collective-permute-done | bytes 65568 | tf_op jit(solution)/shard_map/ppermute | solution.py:34
  86.9 0.7 scatter_fusion
  87.7 0.3 copy.59
  88.1 0.8 add_convert_fusion
  (88 shorter events, 3.0 us)
Async XLA Ops:
  0.0 8.1 %collective-permute-start = (bf16[2,4,2048]{2,1,0:T(4,128)(2,1)}, bf16[2,4,2048]{2,1,0:T(4,128)(2,1)S(1)}, u32[]{:S(2)}, u32[]{:S(2)}) collective-permute-start(bf16[2,4,2048]{2,1,0:T(4,128)(2,1)} %param.9), channel_id=1, source_target_pairs={{0,2},{2,0},{4,6},{6,4},{8,10},{10,8},{12,14},{14,12},{1,3},{3,1},... | collective-permute-start | bytes 98312 | tf_op jit(solution)/shard_map/ppermute | solution.py:267
  9.0 9.8 %collective-permute-start.1 = (bf16[2,2,4,2048]{3,2,1,0:T(4,128)(2,1)S(1)}, bf16[2,2,4,2048]{3,2,1,0:T(4,128)(2,1)S(1)}, u32[]{:S(2)}, u32[]{:S(2)}) collective-permute-start(bf16[2,2,4,2048]{3,2,1,0:T(4,128)(2,1)S(1)} %maximum_select_fusion.1), channel_id=1, source_target_pairs={{0,4},{2,6},{4,8},{6,10},{8,12},{10,14},{12,0},{14,2},{1,5},{3,7},... | collective-permute-start | bytes 196616 | tf_op jit(solution)/shard_map/ppermute | solution.py:270
  10.7 8.2 %collective-permute-start.2 = (bf16[2,2,4,2048]{3,2,1,0:T(4,128)(2,1)S(1)}, bf16[2,2,4,2048]{3,2,1,0:T(4,128)(2,1)S(1)}, u32[]{:S(2)}, u32[]{:S(2)}) collective-permute-start(bf16[2,2,4,2048]{3,2,1,0:T(4,128)(2,1)S(1)} %maximum_select_fusion.1), channel_id=1, source_target_pairs={{0,8},{2,10},{4,12},{6,14},{8,0},{10,2},{12,4},{14,6},{1,9},{3,11}... | collective-permute-start | bytes 196616 | tf_op jit(solution)/shard_map/ppermute | solution.py:270
  13.3 5.6 %collective-permute-start.3 = (bf16[2,2,4,2048]{3,2,1,0:T(4,128)(2,1)S(1)}, bf16[2,2,4,2048]{3,2,1,0:T(4,128)(2,1)S(1)}, u32[]{:S(2)}, u32[]{:S(2)}) collective-permute-start(bf16[2,2,4,2048]{3,2,1,0:T(4,128)(2,1)S(1)} %maximum_select_fusion.1), channel_id=1, source_target_pairs={{0,12},{2,14},{4,0},{6,2},{8,4},{10,6},{12,8},{14,10},{1,13},{3,15... | collective-permute-start | bytes 196616 | tf_op jit(solution)/shard_map/ppermute | solution.py:270
  14.6 1.6 %copy-start = (bf16[2,4,128,1024]{3,2,1,0:T(8,128)(2,1)S(1)}, bf16[2,4,128,1024]{3,2,1,0:T(8,128)(2,1)}, u32[]{:S(2)}) copy-start(bf16[2,4,128,1024]{3,2,1,0:T(8,128)(2,1)} %refs_4_.3) | copy-start | bytes 6291460
  16.2 2.9 %copy-start.1 = (bf16[2,4,128,1024]{3,2,1,0:T(8,128)(2,1)S(1)}, bf16[2,4,128,1024]{3,2,1,0:T(8,128)(2,1)}, u32[]{:S(2)}) copy-start(bf16[2,4,128,1024]{3,2,1,0:T(8,128)(2,1)} %refs_4_.3) | copy-start | bytes 6291460
  24.8 7.8 %collective-permute-start.4 = (f32[136,128]{1,0:T(8,128)S(1)}, f32[136,128]{1,0:T(8,128)S(1)}, u32[]{:S(2)}, u32[]{:S(2)}) collective-permute-start(f32[136,128]{1,0:T(8,128)S(1)} %get-tuple-element.9), channel_id=1, source_target_pairs={{0,2},{2,4},{4,6},{6,8},{8,10},{10,12},{12,14},{14,0},{1,3},{3,5},... | collective-permute-start | bytes 208904 | tf_op jit(solution)/shard_map/ppermute | solution.py:290
  25.4 13.1 %collective-permute-start.8 = (f32[136,128]{1,0:T(8,128)S(1)}, f32[136,128]{1,0:T(8,128)S(1)}, u32[]{:S(2)}, u32[]{:S(2)}) collective-permute-start(f32[136,128]{1,0:T(8,128)S(1)} %get-tuple-element.14), channel_id=1, source_target_pairs={{0,10},{2,12},{4,14},{6,0},{8,2},{10,4},{12,6},{14,8},{1,11},{3,13... | collective-permute-start | bytes 208904 | tf_op jit(solution)/shard_map/ppermute | solution.py:290
  28.3 6.4 %collective-permute-start.5 = (f32[136,128]{1,0:T(8,128)S(1)}, f32[136,128]{1,0:T(8,128)S(1)}, u32[]{:S(2)}, u32[]{:S(2)}) collective-permute-start(f32[136,128]{1,0:T(8,128)S(1)} %get-tuple-element.10), channel_id=1, source_target_pairs={{0,4},{2,6},{4,8},{6,10},{8,12},{10,14},{12,0},{14,2},{1,5},{3,7},... | collective-permute-start | bytes 208904 | tf_op jit(solution)/shard_map/ppermute | solution.py:290
  30.2 8.3 %collective-permute-start.6 = (f32[136,128]{1,0:T(8,128)S(1)}, f32[136,128]{1,0:T(8,128)S(1)}, u32[]{:S(2)}, u32[]{:S(2)}) collective-permute-start(f32[136,128]{1,0:T(8,128)S(1)} %get-tuple-element.11), channel_id=1, source_target_pairs={{0,6},{2,8},{4,10},{6,12},{8,14},{10,0},{12,2},{14,4},{1,7},{3,9},... | collective-permute-start | bytes 208904 | tf_op jit(solution)/shard_map/ppermute | solution.py:290
  30.2 8.3 %collective-permute-start.7 = (f32[136,128]{1,0:T(8,128)S(1)}, f32[136,128]{1,0:T(8,128)S(1)}, u32[]{:S(2)}, u32[]{:S(2)}) collective-permute-start(f32[136,128]{1,0:T(8,128)S(1)} %get-tuple-element.12), channel_id=1, source_target_pairs={{0,8},{2,10},{4,12},{6,14},{8,0},{10,2},{12,4},{14,6},{1,9},{3,11}... | collective-permute-start | bytes 208904 | tf_op jit(solution)/shard_map/ppermute | solution.py:290
  32.6 5.9 %collective-permute-start.9 = (f32[136,128]{1,0:T(8,128)S(1)}, f32[136,128]{1,0:T(8,128)S(1)}, u32[]{:S(2)}, u32[]{:S(2)}) collective-permute-start(f32[136,128]{1,0:T(8,128)S(1)} %get-tuple-element.13), channel_id=1, source_target_pairs={{0,12},{2,14},{4,0},{6,2},{8,4},{10,6},{12,8},{14,10},{1,13},{3,15... | collective-permute-start | bytes 208904 | tf_op jit(solution)/shard_map/ppermute | solution.py:290
  34.6 4.4 %collective-permute-start.10 = (f32[136,128]{1,0:T(8,128)S(1)}, f32[136,128]{1,0:T(8,128)S(1)}, u32[]{:S(2)}, u32[]{:S(2)}) collective-permute-start(f32[136,128]{1,0:T(8,128)S(1)} %get-tuple-element.7), channel_id=1, source_target_pairs={{0,14},{2,0},{4,2},{6,4},{8,6},{10,8},{12,10},{14,12},{1,15},{3,1}... | collective-permute-start | bytes 208904 | tf_op jit(solution)/shard_map/ppermute | solution.py:290
  42.5 18.9 %copy-start.3 = (s32[128]{0:T(128)S(1)}, s32[128]{0:T(128)}, u32[]{:S(2)}) copy-start(s32[128]{0:T(128)} %param.16) | copy-start | bytes 1540
  55.4 32.7 %copy-start.2 = (bf16[2,8,8192]{2,1,0:T(8,128)(2,1)S(1)}, bf16[2,8,8192]{2,1,0:T(8,128)(2,1)}, u32[]{:S(2)}) copy-start(bf16[2,8,8192]{2,1,0:T(8,128)(2,1)} %param.17) | copy-start | bytes 786436
  56.3 9.8 %collective-permute-start.11 = (f32[16,1024]{1,0:T(8,128)S(1)}, f32[16,1024]{1,0:T(8,128)S(1)}, u32[]{:S(2)}, u32[]{:S(2)}) collective-permute-start(f32[16,1024]{1,0:T(8,128)S(1)} %bitcast.141), channel_id=1, source_target_pairs={{0,2},{2,4},{4,6},{6,8},{8,10},{10,12},{12,14},{14,0},{1,3},{3,5},... | collective-permute-start | bytes 196616 | tf_op jit(solution)/shard_map/ppermute | solution.py:61
  59.2 9.4 %collective-permute-start.12 = (f32[16,1024]{1,0:T(8,128)S(1)}, f32[16,1024]{1,0:T(8,128)S(1)}, u32[]{:S(2)}, u32[]{:S(2)}) collective-permute-start(f32[16,1024]{1,0:T(8,128)S(1)} %bitcast.140), channel_id=1, source_target_pairs={{0,4},{2,6},{4,8},{6,10},{8,12},{10,14},{12,0},{14,2},{1,5},{3,7},... | collective-permute-start | bytes 196616 | tf_op jit(solution)/shard_map/ppermute | solution.py:61
  61.5 10.1 %collective-permute-start.13 = (f32[16,1024]{1,0:T(8,128)S(1)}, f32[16,1024]{1,0:T(8,128)S(1)}, u32[]{:S(2)}, u32[]{:S(2)}) collective-permute-start(f32[16,1024]{1,0:T(8,128)S(1)} %bitcast.135), channel_id=1, source_target_pairs={{0,6},{2,8},{4,10},{6,12},{8,14},{10,0},{12,2},{14,4},{1,7},{3,9},... | collective-permute-start | bytes 196616 | tf_op jit(solution)/shard_map/ppermute | solution.py:61
  63.0 9.4 %collective-permute-start.14 = (f32[16,1024]{1,0:T(8,128)S(1)}, f32[16,1024]{1,0:T(8,128)S(1)}, u32[]{:S(2)}, u32[]{:S(2)}) collective-permute-start(f32[16,1024]{1,0:T(8,128)S(1)} %bitcast.136), channel_id=1, source_target_pairs={{0,8},{2,10},{4,12},{6,14},{8,0},{10,2},{12,4},{14,6},{1,9},{3,11}... | collective-permute-start | bytes 196616 | tf_op jit(solution)/shard_map/ppermute | solution.py:61
  65.0 7.9 %collective-permute-start.15 = (f32[16,1024]{1,0:T(8,128)S(1)}, f32[16,1024]{1,0:T(8,128)S(1)}, u32[]{:S(2)}, u32[]{:S(2)}) collective-permute-start(f32[16,1024]{1,0:T(8,128)S(1)} %bitcast.137), channel_id=1, source_target_pairs={{0,10},{2,12},{4,14},{6,0},{8,2},{10,4},{12,6},{14,8},{1,11},{3,13... | collective-permute-start | bytes 196616 | tf_op jit(solution)/shard_map/ppermute | solution.py:61
  66.1 6.8 %collective-permute-start.16 = (f32[16,1024]{1,0:T(8,128)S(1)}, f32[16,1024]{1,0:T(8,128)S(1)}, u32[]{:S(2)}, u32[]{:S(2)}) collective-permute-start(f32[16,1024]{1,0:T(8,128)S(1)} %bitcast.139), channel_id=1, source_target_pairs={{0,12},{2,14},{4,0},{6,2},{8,4},{10,6},{12,8},{14,10},{1,13},{3,15... | collective-permute-start | bytes 196616 | tf_op jit(solution)/shard_map/ppermute | solution.py:61
  68.5 4.8 %collective-permute-start.17 = (f32[16,1024]{1,0:T(8,128)S(1)}, f32[16,1024]{1,0:T(8,128)S(1)}, u32[]{:S(2)}, u32[]{:S(2)}) collective-permute-start(f32[16,1024]{1,0:T(8,128)S(1)} %bitcast.138), channel_id=1, source_target_pairs={{0,14},{2,0},{4,2},{6,4},{8,6},{10,8},{12,10},{14,12},{1,15},{3,1}... | collective-permute-start | bytes 196616 | tf_op jit(solution)/shard_map/ppermute | solution.py:61
  73.4 4.0 %collective-permute-start.18 = (bf16[16,1024]{1,0:T(8,128)(2,1)S(1)}, bf16[16,1024]{1,0:T(8,128)(2,1)S(1)}, u32[]{:S(2)}, u32[]{:S(2)}) collective-permute-start(bf16[16,1024]{1,0:T(8,128)(2,1)S(1)} %clamp_convert_fusion), channel_id=1, source_target_pairs={{0,2},{2,0},{4,6},{6,4},{8,10},{10,8},{12,14},{14,12},{1,3},{3,1},... | collective-permute-start | bytes 98312 | tf_op jit(solution)/shard_map/ppermute | solution.py:28
  77.5 7.5 %collective-permute-start.19 = (bf16[2,16,1024]{2,1,0:T(8,128)(2,1)S(1)}, bf16[2,16,1024]{2,1,0:T(8,128)(2,1)S(1)}, u32[]{:S(2)}, u32[]{:S(2)}) collective-permute-start(bf16[2,16,1024]{2,1,0:T(8,128)(2,1)S(1)} %maximum_select_fusion.3), channel_id=1, source_target_pairs={{0,4},{2,6},{4,8},{6,10},{8,12},{10,14},{12,0},{14,2},{1,5},{3,7},... | collective-permute-start | bytes 196616 | tf_op jit(solution)/shard_map/ppermute | solution.py:34
  80.2 5.2 %collective-permute-start.20 = (bf16[2,16,1024]{2,1,0:T(8,128)(2,1)S(1)}, bf16[2,16,1024]{2,1,0:T(8,128)(2,1)S(1)}, u32[]{:S(2)}, u32[]{:S(2)}) collective-permute-start(bf16[2,16,1024]{2,1,0:T(8,128)(2,1)S(1)} %maximum_select_fusion.3), channel_id=1, source_target_pairs={{0,8},{2,10},{4,12},{6,14},{8,0},{10,2},{12,4},{14,6},{1,9},{3,11}... | collective-permute-start | bytes 196616 | tf_op jit(solution)/shard_map/ppermute | solution.py:34
  82.3 4.6 %collective-permute-start.21 = (bf16[2,16,1024]{2,1,0:T(8,128)(2,1)S(1)}, bf16[2,16,1024]{2,1,0:T(8,128)(2,1)S(1)}, u32[]{:S(2)}, u32[]{:S(2)}) collective-permute-start(bf16[2,16,1024]{2,1,0:T(8,128)(2,1)S(1)} %maximum_select_fusion.3), channel_id=1, source_target_pairs={{0,12},{2,14},{4,0},{6,2},{8,4},{10,6},{12,8},{14,10},{1,13},{3,15... | collective-permute-start | bytes 196616 | tf_op jit(solution)/shard_map/ppermute | solution.py:34

commit v17 on v16

--- a/solution.py
+++ b/solution.py
@@ -284,10 +284,19 @@
             d = (mine - head // 2) % half
             return jnp.where(d == 0, head % 2, 2 * d + head % 2)
 
-        got = [lax.dynamic_index_in_dim(outs, position(tp_rank), 0, keepdims=False)]
-        for k in range(1, tp_count):
-            send = lax.dynamic_index_in_dim(outs, position((tp_rank + k) % tp_count), 0, keepdims=False)
-            got.append(lax.ppermute(send, "tp", [(i, (i + k) % tp_count) for i in range(tp_count)]))
+        got = [
+            lax.dynamic_index_in_dim(out_near, tp_rank % 2, 0, keepdims=False),
+            lax.ppermute(
+                lax.dynamic_index_in_dim(out_near, 1 - tp_rank % 2, 0, keepdims=False),
+                "tp", [(i, i ^ 1) for i in range(tp_count)],
+            ),
+        ]
+        for d in range(1, half):
+            for flip in (0, 1):
+                dst = ((mine + d) % half) * 2 + (tp_rank % 2 ^ flip)
+                perm = [(i, ((i // 2 + d) % half) * 2 + (i % 2 ^ flip)) for i in range(tp_count)]
+                send = lax.dynamic_index_in_dim(outs, position(dst), 0, keepdims=False)
+                got.append(lax.ppermute(send, "tp", perm))
         got = jnp.stack(got)
         got_numer = got[:, :n_rows].reshape(tp_count, steps_n, rows_dev, heads_dev, DH)
         got_peak = got[:, n_rows].reshape(tp_count, steps_n, rows_dev, heads_dev)

time: 89.3 us -> 87.5 us (0.980)
  starting transfers between devices: 42.9 us -> 38.5 us
  waiting for transfers between devices: 9.93 us -> 12.6 us
    ppermute x7, starting transfers between devices: 15 us -> 11.9 us  [_exchange(): lax.ppermute(send, axis_name, [(i, (i + k) % count) for i in range(count)])]
    ppermute x3, starting transfers between devices: 7.51 us -> 4.53 us  [_gather_blocks(): lax.ppermute(pair, axis_name, [(i, (i + 2 * d) % count) for i in range(co...]
    ppermute x3, waiting for transfers between devices: 1.88 us -> 4.14 us  [_gather_blocks(): lax.ppermute(pair, axis_name, [(i, (i + 2 * d) % count) for i in range(co...]
    ppermute x7, waiting for transfers between devices: 1.8 us -> 3.44 us  [_exchange(): lax.ppermute(send, axis_name, [(i, (i + k) % count) for i in range(count)])]
    ppermute x7, starting transfers between devices: 9.74 us -> 11.3 us  [the longest x6 10.7 us: per_device(): got.append(lax.ppermute(send, 'tp', perm))]
    ppermute x7, waiting for transfers between devices: 4.35 us -> 3.1 us  [the longest x6 3.1 us: per_device(): got.append(lax.ppermute(send, 'tp', perm))]
  transfers between devices with their start and end apart: 22 -> 22, of which waited for: 9 -> 10; matrix products, arithmetic and copies ran while one was open for 5% -> 6% of each run, Pallas kernels for 3% -> 9%
where the time goes in v17:
time: 87.5 us; the launch traced here: 87 us
  starting transfers between devices  38.5 us (44%)
  matrix products  13.3 us (15%)
  waiting for transfers between devices  12.6 us (14%)
  Pallas kernels  8.09 us (9%)
  local copies, waits for them, and re-layouts  7.68 us (9%)
  other arithmetic  4.14 us (5%)
  blocking collectives  1.85 us (2%)
  between operations  0.97 us (1%)
    dot_general x1, matrix products, per_device(): jnp.einsum('rhd,hdf->rhf', head_rows_in, head_weights, preferred_element_...  12.9 us
    ppermute x7, starting transfers between devices, _exchange(): lax.ppermute(send, axis_name, [(i, (i + k) % count) for i in range(count)])  11.9 us
    ppermute x6, starting transfers between devices, per_device(): got.append(lax.ppermute(send, 'tp', perm))  10.7 us
    pallas_call x2, Pallas kernels, _attend_packed_pairs(): pl.pallas_call(lambda b_ref, *refs: _attend_packed_kernel(group, *refs),...  8.09 us
    ppermute x3, starting transfers between devices, per_device(): lax.ppermute(pair, 'tp', [(i, (i + 2 * d) % tp_count) for i in range(tp_c...  5.57 us
    ppermute x3, starting transfers between devices, _gather_blocks(): lax.ppermute(pair, axis_name, [(i, (i + 2 * d) % count) for i in range(co...  4.53 us
    ppermute x3, waiting for transfers between devices, _gather_blocks(): lax.ppermute(pair, axis_name, [(i, (i + 2 * d) % count) for i in range(co...  4.14 us
    ppermute x7, waiting for transfers between devices, _exchange(): lax.ppermute(send, axis_name, [(i, (i + k) % count) for i in range(count)])  3.44 us
  transfers between devices with their start and end apart: 22, of which 10 were waited for; matrix products, arithmetic and copies ran while one was open for 6% of the time, Pallas kernels for 9%

profile of v17, /device:TPU:0, one launch (start us, length us, event | category | flops | bytes accessed | tf_op | source)
XLA Modules:
  0.0 87.0 jit_solution(5288707612527826707)
XLA Ops:
  0.0 2.9 %collective-permute-start = (bf16[2,4,2048]{2,1,0:T(4,128)(2,1)}, bf16[2,4,2048]{2,1,0:T(4,128)(2,1)S(1)}, u32[]{:S(2)}, u32[]{:S(2)}) collective-permute-start(bf16[2,4,2048]{2,1,0:T(4,128)(2,1)} %param.9), channel_id=1, source_target_pairs={{0,2},{2,0},{4,6},{6,4},{8,10},{10,8},{12,14},{14,12},{1,3},{3,1},... | collective-permute-start | bytes 98312 | tf_op jit(solution)/shard_map/ppermute | solution.py:267
  2.9 0.8 reshape.287
  3.8 0.8 reshape.286
  4.6 0.2 fusion.26
  5.0 0.7 multiply_exponential_fusion.1
  5.7 0.7 compare_convert_fusion.refs_5_
  6.9 0.8 stack.101
  8.1 0.9 %maximum_select_fusion.1 = bf16[2,2,4,2048]{3,2,1,0:T(4,128)(2,1)S(1)} fusion(bf16[1,2,4,2048]{3,2,1,0:T(4,128)(2,1)S(1)} %bitcast.132, bf16[1,2,4,2048]{3,2,1,0:T(4,128)(2,1)} %bitcast.127, pred[]{:T(512)S(6)} %eq.68), kind=kLoop, calls=%fused_computation.44 | loop fusion | flops 98304 | bytes 131073 | tf_op jit(solution)/shard_map/jit(_where)/select_n | solution.py:268
  9.0 1.6 %collective-permute-start.2 = (bf16[2,2,4,2048]{3,2,1,0:T(4,128)(2,1)S(1)}, bf16[2,2,4,2048]{3,2,1,0:T(4,128)(2,1)S(1)}, u32[]{:S(2)}, u32[]{:S(2)}) collective-permute-start(bf16[2,2,4,2048]{3,2,1,0:T(4,128)(2,1)S(1)} %maximum_select_fusion.1), channel_id=1, source_target_pairs={{0,4},{2,6},{4,8},{6,10},{8,12},{10,14},{12,0},{14,2},{1,5},{3,7},... | collective-permute-start | bytes 196616 | tf_op jit(solution)/shard_map/ppermute | solution.py:270
  10.6 2.6 %collective-permute-start.3 = (bf16[2,2,4,2048]{3,2,1,0:T(4,128)(2,1)S(1)}, bf16[2,2,4,2048]{3,2,1,0:T(4,128)(2,1)S(1)}, u32[]{:S(2)}, u32[]{:S(2)}) collective-permute-start(bf16[2,2,4,2048]{3,2,1,0:T(4,128)(2,1)S(1)} %maximum_select_fusion.1), channel_id=1, source_target_pairs={{0,8},{2,10},{4,12},{6,14},{8,0},{10,2},{12,4},{14,6},{1,9},{3,11}... | collective-permute-start | bytes 196616 | tf_op jit(solution)/shard_map/ppermute | solution.py:270
  13.2 1.3 %collective-permute-start.4 = (bf16[2,2,4,2048]{3,2,1,0:T(4,128)(2,1)S(1)}, bf16[2,2,4,2048]{3,2,1,0:T(4,128)(2,1)S(1)}, u32[]{:S(2)}, u32[]{:S(2)}) collective-permute-start(bf16[2,2,4,2048]{3,2,1,0:T(4,128)(2,1)S(1)} %maximum_select_fusion.1), channel_id=1, source_target_pairs={{0,12},{2,14},{4,0},{6,2},{8,4},{10,6},{12,8},{14,10},{1,13},{3,15... | collective-permute-start | bytes 196616 | tf_op jit(solution)/shard_map/ppermute | solution.py:270
  14.6 1.6 %copy-done = bf16[2,4,128,1024]{3,2,1,0:T(8,128)(2,1)S(1)} copy-done((bf16[2,4,128,1024]{3,2,1,0:T(8,128)(2,1)S(1)}, bf16[2,4,128,1024]{3,2,1,0:T(8,128)(2,1)}, u32[]{:S(2)}) %copy-start) | copy-done | bytes 2097176
  16.2 2.6 %shard_map.91 = f32[2,136,128]{2,1,0:T(8,128)S(1)} custom-call(s32[1]{0:T(128)} %bitcast.1.b_ref, bf16[2,128,128]{2,1,0:T(8,128)(2,1)S(1)} %maximum_select_fusion.refs_0_, bf16[2,1024,1024]{2,1,0:T(8,128)(2,1)} %refs_2_.3, bf16[2,1024,1024]{2,1,0:T(8,128)(2,1)} %refs_2_.3, bf16[2,4,128,1024]{3,2,1,0:T(8,128)(2,1)S(1)} %copy-done, ...), custom_call_target="tpu_custom_call" | custom-call | flops 201326592 | bytes 1777664 | tf_op jit(solution)/shard_map/pallas_call | solution.py:230
  18.8 0.6 collective-permute-start.1
  19.7 5.5 %shard_map.92 = f32[6,136,128]{2,1,0:T(8,128)S(1)} custom-call(s32[3]{0:T(128)S(1)} %and_select_fusion.b_ref, bf16[6,128,128]{2,1,0:T(8,128)(2,1)S(1)} %reshape.285.refs_0_, bf16[2,1024,1024]{2,1,0:T(8,128)(2,1)} %refs_2_.3, bf16[2,1024,1024]{2,1,0:T(8,128)(2,1)} %refs_2_.3, bf16[2,4,128,1024]{3,2,1,0:T(8,128)(2,1)S(1)} %copy-done.1, ...), custom_call_target="tpu_custom_call" | custom-call | flops 603979776 | bytes 5332992 | tf_op jit(solution)/shard_map/pallas_call | solution.py:230
  25.4 0.7 collective-permute-start.5
  26.1 1.2 %collective-permute-start.6 = (f32[136,128]{1,0:T(8,128)S(1)}, f32[136,128]{1,0:T(8,128)S(1)}, u32[]{:S(2)}, u32[]{:S(2)}) collective-permute-start(f32[136,128]{1,0:T(8,128)S(1)} %get-tuple-element.9), channel_id=1, source_target_pairs={{0,6},{2,4},{4,10},{6,8},{8,14},{10,12},{12,2},{14,0},{1,7},{3,5},... | collective-permute-start | bytes 208904 | tf_op jit(solution)/shard_map/ppermute | solution.py:299
  27.3 3.5 %collective-permute-start.7 = (f32[136,128]{1,0:T(8,128)S(1)}, f32[136,128]{1,0:T(8,128)S(1)}, u32[]{:S(2)}, u32[]{:S(2)}) collective-permute-start(f32[136,128]{1,0:T(8,128)S(1)} %get-tuple-element.10), channel_id=1, source_target_pairs={{0,8},{2,10},{4,12},{6,14},{8,0},{10,2},{12,4},{14,6},{1,9},{3,11}... | collective-permute-start | bytes 208904 | tf_op jit(solution)/shard_map/ppermute | solution.py:299
  30.7 3.0 %collective-permute-start.9 = (f32[136,128]{1,0:T(8,128)S(1)}, f32[136,128]{1,0:T(8,128)S(1)}, u32[]{:S(2)}, u32[]{:S(2)}) collective-permute-start(f32[136,128]{1,0:T(8,128)S(1)} %get-tuple-element.12), channel_id=1, source_target_pairs={{0,12},{2,14},{4,0},{6,2},{8,4},{10,6},{12,8},{14,10},{1,13},{3,15... | collective-permute-start | bytes 208904 | tf_op jit(solution)/shard_map/ppermute | solution.py:299
  33.8 2.3 %collective-permute-start.10 = (f32[136,128]{1,0:T(8,128)S(1)}, f32[136,128]{1,0:T(8,128)S(1)}, u32[]{:S(2)}, u32[]{:S(2)}) collective-permute-start(f32[136,128]{1,0:T(8,128)S(1)} %get-tuple-element.7), channel_id=1, source_target_pairs={{0,14},{2,12},{4,2},{6,0},{8,6},{10,4},{12,10},{14,8},{1,15},{3,13... | collective-permute-start | bytes 208904 | tf_op jit(solution)/shard_map/ppermute | solution.py:299
  36.2 2.3 %collective-permute-done.8 = f32[136,128]{1,0:T(8,128)S(1)} collective-permute-done((f32[136,128]{1,0:T(8,128)S(1)}, f32[136,128]{1,0:T(8,128)S(1)}, u32[]{:S(2)}, u32[]{:S(2)}) %collective-permute-start.8) | collective-permute-done | bytes 69664 | tf_op jit(solution)/shard_map/ppermute | solution.py:299
  38.5 0.8 collective-permute-done.10
  40.3 0.2 fusion.2
  40.5 0.2 fusion.28
  40.9 1.9 %all_gather.3 = bf16[2,8,2048]{2,0,1:T(2,128)(2,1)S(1)} all-gather(bf16[2,4,2048]{2,0,1:T(2,128)(2,1)S(1)} %copy.56), channel_id=1, replica_groups=mesh['rep'=2,'tp'=8,'sub'=2] {'sub'}, dimensions={1}, use_global_device_ids=true | all-gather | bytes 98304 | tf_op jit(solution)/shard_map/all_gather | solution.py:370
  42.8 12.9 %fusion.1 = f32[16,8192]{1,0:T(8,128)S(1)} fusion(f32[8192]{0:T(1024)S(1)} %dynamic_slice.62, bf16[16,128,8192]{2,1,0:T(8,128)(2,1)} %bitcast.150, bf16[16,16,128]{2,1,0:T(8,128)(2,1)S(1)} %bitcast.142), kind=kOutput, calls=%fused_computation.3 | convolution fusion | flops 543031296 | bytes 34177024 | tf_op jit(solution)/shard_map/rhd,hdf->rhf/dot_general | solution.py:379
  55.7 0.3 copy.74
  56.0 0.5 constant_dynamic-slice_fusion.8
  56.6 1.3 %collective-permute-start.11 = (f32[16,1024]{1,0:T(8,128)S(1)}, f32[16,1024]{1,0:T(8,128)S(1)}, u32[]{:S(2)}, u32[]{:S(2)}) collective-permute-start(f32[16,1024]{1,0:T(8,128)S(1)} %bitcast.141), channel_id=1, source_target_pairs={{0,2},{2,4},{4,6},{6,8},{8,10},{10,12},{12,14},{14,0},{1,3},{3,5},... | collective-permute-start | bytes 196616 | tf_op jit(solution)/shard_map/ppermute | solution.py:61
  57.9 2.2 %collective-permute-start.12 = (f32[16,1024]{1,0:T(8,128)S(1)}, f32[16,1024]{1,0:T(8,128)S(1)}, u32[]{:S(2)}, u32[]{:S(2)}) collective-permute-start(f32[16,1024]{1,0:T(8,128)S(1)} %bitcast.140), channel_id=1, source_target_pairs={{0,4},{2,6},{4,8},{6,10},{8,12},{10,14},{12,0},{14,2},{1,5},{3,7},... | collective-permute-start | bytes 196616 | tf_op jit(solution)/shard_map/ppermute | solution.py:61
  60.2 1.6 %collective-permute-start.13 = (f32[16,1024]{1,0:T(8,128)S(1)}, f32[16,1024]{1,0:T(8,128)S(1)}, u32[]{:S(2)}, u32[]{:S(2)}) collective-permute-start(f32[16,1024]{1,0:T(8,128)S(1)} %bitcast.135), channel_id=1, source_target_pairs={{0,6},{2,8},{4,10},{6,12},{8,14},{10,0},{12,2},{14,4},{1,7},{3,9},... | collective-permute-start | bytes 196616 | tf_op jit(solution)/shard_map/ppermute | solution.py:61
  61.8 2.9 %collective-permute-start.14 = (f32[16,1024]{1,0:T(8,128)S(1)}, f32[16,1024]{1,0:T(8,128)S(1)}, u32[]{:S(2)}, u32[]{:S(2)}) collective-permute-start(f32[16,1024]{1,0:T(8,128)S(1)} %bitcast.136), channel_id=1, source_target_pairs={{0,8},{2,10},{4,12},{6,14},{8,0},{10,2},{12,4},{14,6},{1,9},{3,11}... | collective-permute-start | bytes 196616 | tf_op jit(solution)/shard_map/ppermute | solution.py:61
  64.6 1.1 %collective-permute-start.15 = (f32[16,1024]{1,0:T(8,128)S(1)}, f32[16,1024]{1,0:T(8,128)S(1)}, u32[]{:S(2)}, u32[]{:S(2)}) collective-permute-start(f32[16,1024]{1,0:T(8,128)S(1)} %bitcast.137), channel_id=1, source_target_pairs={{0,10},{2,12},{4,14},{6,0},{8,2},{10,4},{12,6},{14,8},{1,11},{3,13... | collective-permute-start | bytes 196616 | tf_op jit(solution)/shard_map/ppermute | solution.py:61
  65.8 1.4 %collective-permute-start.16 = (f32[16,1024]{1,0:T(8,128)S(1)}, f32[16,1024]{1,0:T(8,128)S(1)}, u32[]{:S(2)}, u32[]{:S(2)}) collective-permute-start(f32[16,1024]{1,0:T(8,128)S(1)} %bitcast.139), channel_id=1, source_target_pairs={{0,12},{2,14},{4,0},{6,2},{8,4},{10,6},{12,8},{14,10},{1,13},{3,15... | collective-permute-start | bytes 196616 | tf_op jit(solution)/shard_map/ppermute | solution.py:61
  67.2 1.5 %collective-permute-start.17 = (f32[16,1024]{1,0:T(8,128)S(1)}, f32[16,1024]{1,0:T(8,128)S(1)}, u32[]{:S(2)}, u32[]{:S(2)}) collective-permute-start(f32[16,1024]{1,0:T(8,128)S(1)} %bitcast.138), channel_id=1, source_target_pairs={{0,14},{2,0},{4,2},{6,4},{8,6},{10,8},{12,10},{14,12},{1,15},{3,1}... | collective-permute-start | bytes 196616 | tf_op jit(solution)/shard_map/ppermute | solution.py:61
  68.7 1.4 %collective-permute-done.13 = f32[16,1024]{1,0:T(8,128)S(1)} collective-permute-done((f32[16,1024]{1,0:T(8,128)S(1)}, f32[16,1024]{1,0:T(8,128)S(1)}, u32[]{:S(2)}, u32[]{:S(2)}) %collective-permute-start.13) | collective-permute-done | bytes 65568 | tf_op jit(solution)/shard_map/ppermute | solution.py:61
  70.3 1.7 %collective-permute-done.15 = f32[16,1024]{1,0:T(8,128)S(1)} collective-permute-done((f32[16,1024]{1,0:T(8,128)S(1)}, f32[16,1024]{1,0:T(8,128)S(1)}, u32[]{:S(2)}, u32[]{:S(2)}) %collective-permute-start.15) | collective-permute-done | bytes 65568 | tf_op jit(solution)/shard_map/ppermute | solution.py:61
  72.0 0.2 collective-permute-done.16
  72.2 2.2 %collective-permute-start.18 = (bf16[16,1024]{1,0:T(8,128)(2,1)S(1)}, bf16[16,1024]{1,0:T(8,128)(2,1)S(1)}, u32[]{:S(2)}, u32[]{:S(2)}) collective-permute-start(bf16[16,1024]{1,0:T(8,128)(2,1)S(1)} %clamp_convert_fusion), channel_id=1, source_target_pairs={{0,2},{2,0},{4,6},{6,4},{8,10},{10,8},{12,14},{14,12},{1,3},{3,1},... | collective-permute-start | bytes 98312 | tf_op jit(solution)/shard_map/ppermute | solution.py:28
  74.5 1.9 %collective-permute-done.18 = bf16[16,1024]{1,0:T(8,128)(2,1)S(1)} collective-permute-done((bf16[16,1024]{1,0:T(8,128)(2,1)S(1)}, bf16[16,1024]{1,0:T(8,128)(2,1)S(1)}, u32[]{:S(2)}, u32[]{:S(2)}) %collective-permute-start.18) | collective-permute-done | bytes 32800 | tf_op jit(solution)/shard_map/ppermute | solution.py:28
  76.4 2.1 %collective-permute-start.19 = (bf16[2,16,1024]{2,1,0:T(8,128)(2,1)S(1)}, bf16[2,16,1024]{2,1,0:T(8,128)(2,1)S(1)}, u32[]{:S(2)}, u32[]{:S(2)}) collective-permute-start(bf16[2,16,1024]{2,1,0:T(8,128)(2,1)S(1)} %maximum_select_fusion.3), channel_id=1, source_target_pairs={{0,4},{2,6},{4,8},{6,10},{8,12},{10,14},{12,0},{14,2},{1,5},{3,7},... | collective-permute-start | bytes 196616 | tf_op jit(solution)/shard_map/ppermute | solution.py:34
  78.4 1.7 %collective-permute-start.20 = (bf16[2,16,1024]{2,1,0:T(8,128)(2,1)S(1)}, bf16[2,16,1024]{2,1,0:T(8,128)(2,1)S(1)}, u32[]{:S(2)}, u32[]{:S(2)}) collective-permute-start(bf16[2,16,1024]{2,1,0:T(8,128)(2,1)S(1)} %maximum_select_fusion.3), channel_id=1, source_target_pairs={{0,8},{2,10},{4,12},{6,14},{8,0},{10,2},{12,4},{14,6},{1,9},{3,11}... | collective-permute-start | bytes 196616 | tf_op jit(solution)/shard_map/ppermute | solution.py:34
  80.2 0.7 collective-permute-start.21
  80.9 2.1 %collective-permute-done.19 = bf16[2,16,1024]{2,1,0:T(8,128)(2,1)S(1)} collective-permute-done((bf16[2,16,1024]{2,1,0:T(8,128)(2,1)S(1)}, bf16[2,16,1024]{2,1,0:T(8,128)(2,1)S(1)}, u32[]{:S(2)}, u32[]{:S(2)}) %collective-permute-start.19) | collective-permute-done | bytes 65568 | tf_op jit(solution)/shard_map/ppermute | solution.py:34
  83.0 1.9 %collective-permute-done.20 = bf16[2,16,1024]{2,1,0:T(8,128)(2,1)S(1)} collective-permute-done((bf16[2,16,1024]{2,1,0:T(8,128)(2,1)S(1)}, bf16[2,16,1024]{2,1,0:T(8,128)(2,1)S(1)}, u32[]{:S(2)}, u32[]{:S(2)}) %collective-permute-start.20) | collective-permute-done | bytes 65568 | tf_op jit(solution)/shard_map/ppermute | solution.py:34
  85.1 0.7 scatter_fusion
  85.8 0.3 copy.59
  86.3 0.8 add_convert_fusion
  (88 shorter events, 3.0 us)
Async XLA Ops:
  0.0 8.1 %collective-permute-start = (bf16[2,4,2048]{2,1,0:T(4,128)(2,1)}, bf16[2,4,2048]{2,1,0:T(4,128)(2,1)S(1)}, u32[]{:S(2)}, u32[]{:S(2)}) collective-permute-start(bf16[2,4,2048]{2,1,0:T(4,128)(2,1)} %param.9), channel_id=1, source_target_pairs={{0,2},{2,0},{4,6},{6,4},{8,10},{10,8},{12,14},{14,12},{1,3},{3,1},... | collective-permute-start | bytes 98312 | tf_op jit(solution)/shard_map/ppermute | solution.py:267
  9.0 10.4 %collective-permute-start.2 = (bf16[2,2,4,2048]{3,2,1,0:T(4,128)(2,1)S(1)}, bf16[2,2,4,2048]{3,2,1,0:T(4,128)(2,1)S(1)}, u32[]{:S(2)}, u32[]{:S(2)}) collective-permute-start(bf16[2,2,4,2048]{3,2,1,0:T(4,128)(2,1)S(1)} %maximum_select_fusion.1), channel_id=1, source_target_pairs={{0,4},{2,6},{4,8},{6,10},{8,12},{10,14},{12,0},{14,2},{1,5},{3,7},... | collective-permute-start | bytes 196616 | tf_op jit(solution)/shard_map/ppermute | solution.py:270
  10.6 8.8 %collective-permute-start.3 = (bf16[2,2,4,2048]{3,2,1,0:T(4,128)(2,1)S(1)}, bf16[2,2,4,2048]{3,2,1,0:T(4,128)(2,1)S(1)}, u32[]{:S(2)}, u32[]{:S(2)}) collective-permute-start(bf16[2,2,4,2048]{3,2,1,0:T(4,128)(2,1)S(1)} %maximum_select_fusion.1), channel_id=1, source_target_pairs={{0,8},{2,10},{4,12},{6,14},{8,0},{10,2},{12,4},{14,6},{1,9},{3,11}... | collective-permute-start | bytes 196616 | tf_op jit(solution)/shard_map/ppermute | solution.py:270
  13.2 6.2 %collective-permute-start.4 = (bf16[2,2,4,2048]{3,2,1,0:T(4,128)(2,1)S(1)}, bf16[2,2,4,2048]{3,2,1,0:T(4,128)(2,1)S(1)}, u32[]{:S(2)}, u32[]{:S(2)}) collective-permute-start(bf16[2,2,4,2048]{3,2,1,0:T(4,128)(2,1)S(1)} %maximum_select_fusion.1), channel_id=1, source_target_pairs={{0,12},{2,14},{4,0},{6,2},{8,4},{10,6},{12,8},{14,10},{1,13},{3,15... | collective-permute-start | bytes 196616 | tf_op jit(solution)/shard_map/ppermute | solution.py:270
  14.6 1.6 %copy-start = (bf16[2,4,128,1024]{3,2,1,0:T(8,128)(2,1)S(1)}, bf16[2,4,128,1024]{3,2,1,0:T(8,128)(2,1)}, u32[]{:S(2)}) copy-start(bf16[2,4,128,1024]{3,2,1,0:T(8,128)(2,1)} %refs_4_.3) | copy-start | bytes 6291460
  16.2 3.5 %copy-start.1 = (bf16[2,4,128,1024]{3,2,1,0:T(8,128)(2,1)S(1)}, bf16[2,4,128,1024]{3,2,1,0:T(8,128)(2,1)}, u32[]{:S(2)}) copy-start(bf16[2,4,128,1024]{3,2,1,0:T(8,128)(2,1)} %refs_4_.3) | copy-start | bytes 6291460
  18.8 12.0 %collective-permute-start.1 = (f32[136,128]{1,0:T(8,128)S(1)}, f32[136,128]{1,0:T(8,128)S(1)}, u32[]{:S(2)}, u32[]{:S(2)}) collective-permute-start(f32[136,128]{1,0:T(8,128)S(1)} %get-tuple-element.21), channel_id=1, source_target_pairs={{0,2},{2,0},{4,6},{6,4},{8,10},{10,8},{12,14},{14,12},{1,3},{3,1},... | collective-permute-start | bytes 208904 | tf_op jit(solution)/shard_map/ppermute | solution.py:289
  25.4 8.4 %collective-permute-start.5 = (f32[136,128]{1,0:T(8,128)S(1)}, f32[136,128]{1,0:T(8,128)S(1)}, u32[]{:S(2)}, u32[]{:S(2)}) collective-permute-start(f32[136,128]{1,0:T(8,128)S(1)} %get-tuple-element.8), channel_id=1, source_target_pairs={{0,4},{2,6},{4,8},{6,10},{8,12},{10,14},{12,0},{14,2},{1,5},{3,7},... | collective-permute-start | bytes 208904 | tf_op jit(solution)/shard_map/ppermute | solution.py:299
  26.1 10.0 %collective-permute-start.6 = (f32[136,128]{1,0:T(8,128)S(1)}, f32[136,128]{1,0:T(8,128)S(1)}, u32[]{:S(2)}, u32[]{:S(2)}) collective-permute-start(f32[136,128]{1,0:T(8,128)S(1)} %get-tuple-element.9), channel_id=1, source_target_pairs={{0,6},{2,4},{4,10},{6,8},{8,14},{10,12},{12,2},{14,0},{1,7},{3,5},... | collective-permute-start | bytes 208904 | tf_op jit(solution)/shard_map/ppermute | solution.py:299
  27.3 8.9 %collective-permute-start.7 = (f32[136,128]{1,0:T(8,128)S(1)}, f32[136,128]{1,0:T(8,128)S(1)}, u32[]{:S(2)}, u32[]{:S(2)}) collective-permute-start(f32[136,128]{1,0:T(8,128)S(1)} %get-tuple-element.10), channel_id=1, source_target_pairs={{0,8},{2,10},{4,12},{6,14},{8,0},{10,2},{12,4},{14,6},{1,9},{3,11}... | collective-permute-start | bytes 208904 | tf_op jit(solution)/shard_map/ppermute | solution.py:299
  30.7 7.7 %collective-permute-start.8 = (f32[136,128]{1,0:T(8,128)S(1)}, f32[136,128]{1,0:T(8,128)S(1)}, u32[]{:S(2)}, u32[]{:S(2)}) collective-permute-start(f32[136,128]{1,0:T(8,128)S(1)} %get-tuple-element.11), channel_id=1, source_target_pairs={{0,10},{2,8},{4,14},{6,12},{8,2},{10,0},{12,6},{14,4},{1,11},{3,9}... | collective-permute-start | bytes 208904 | tf_op jit(solution)/shard_map/ppermute | solution.py:299
  30.7 7.7 %collective-permute-start.9 = (f32[136,128]{1,0:T(8,128)S(1)}, f32[136,128]{1,0:T(8,128)S(1)}, u32[]{:S(2)}, u32[]{:S(2)}) collective-permute-start(f32[136,128]{1,0:T(8,128)S(1)} %get-tuple-element.12), channel_id=1, source_target_pairs={{0,12},{2,14},{4,0},{6,2},{8,4},{10,6},{12,8},{14,10},{1,13},{3,15... | collective-permute-start | bytes 208904 | tf_op jit(solution)/shard_map/ppermute | solution.py:299
  33.8 5.5 %collective-permute-start.10 = (f32[136,128]{1,0:T(8,128)S(1)}, f32[136,128]{1,0:T(8,128)S(1)}, u32[]{:S(2)}, u32[]{:S(2)}) collective-permute-start(f32[136,128]{1,0:T(8,128)S(1)} %get-tuple-element.7), channel_id=1, source_target_pairs={{0,14},{2,12},{4,2},{6,0},{8,6},{10,4},{12,10},{14,8},{1,15},{3,13... | collective-permute-start | bytes 208904 | tf_op jit(solution)/shard_map/ppermute | solution.py:299
  42.8 17.3 %copy-start.3 = (s32[128]{0:T(128)S(1)}, s32[128]{0:T(128)}, u32[]{:S(2)}) copy-start(s32[128]{0:T(128)} %param.16) | copy-start | bytes 1540
  55.7 30.6 %copy-start.2 = (bf16[2,8,8192]{2,1,0:T(8,128)(2,1)S(1)}, bf16[2,8,8192]{2,1,0:T(8,128)(2,1)}, u32[]{:S(2)}) copy-start(bf16[2,8,8192]{2,1,0:T(8,128)(2,1)} %param.17) | copy-start | bytes 786436
  56.6 9.2 %collective-permute-start.11 = (f32[16,1024]{1,0:T(8,128)S(1)}, f32[16,1024]{1,0:T(8,128)S(1)}, u32[]{:S(2)}, u32[]{:S(2)}) collective-permute-start(f32[16,1024]{1,0:T(8,128)S(1)} %bitcast.141), channel_id=1, source_target_pairs={{0,2},{2,4},{4,6},{6,8},{8,10},{10,12},{12,14},{14,0},{1,3},{3,5},... | collective-permute-start | bytes 196616 | tf_op jit(solution)/shard_map/ppermute | solution.py:61
  57.9 9.3 %collective-permute-start.12 = (f32[16,1024]{1,0:T(8,128)S(1)}, f32[16,1024]{1,0:T(8,128)S(1)}, u32[]{:S(2)}, u32[]{:S(2)}) collective-permute-start(f32[16,1024]{1,0:T(8,128)S(1)} %bitcast.140), channel_id=1, source_target_pairs={{0,4},{2,6},{4,8},{6,10},{8,12},{10,14},{12,0},{14,2},{1,5},{3,7},... | collective-permute-start | bytes 196616 | tf_op jit(solution)/shard_map/ppermute | solution.py:61
  60.2 10.0 %collective-permute-start.13 = (f32[16,1024]{1,0:T(8,128)S(1)}, f32[16,1024]{1,0:T(8,128)S(1)}, u32[]{:S(2)}, u32[]{:S(2)}) collective-permute-start(f32[16,1024]{1,0:T(8,128)S(1)} %bitcast.135), channel_id=1, source_target_pairs={{0,6},{2,8},{4,10},{6,12},{8,14},{10,0},{12,2},{14,4},{1,7},{3,9},... | collective-permute-start | bytes 196616 | tf_op jit(solution)/shard_map/ppermute | solution.py:61
  61.8 8.5 %collective-permute-start.14 = (f32[16,1024]{1,0:T(8,128)S(1)}, f32[16,1024]{1,0:T(8,128)S(1)}, u32[]{:S(2)}, u32[]{:S(2)}) collective-permute-start(f32[16,1024]{1,0:T(8,128)S(1)} %bitcast.136), channel_id=1, source_target_pairs={{0,8},{2,10},{4,12},{6,14},{8,0},{10,2},{12,4},{14,6},{1,9},{3,11}... | collective-permute-start | bytes 196616 | tf_op jit(solution)/shard_map/ppermute | solution.py:61
  64.6 7.4 %collective-permute-start.15 = (f32[16,1024]{1,0:T(8,128)S(1)}, f32[16,1024]{1,0:T(8,128)S(1)}, u32[]{:S(2)}, u32[]{:S(2)}) collective-permute-start(f32[16,1024]{1,0:T(8,128)S(1)} %bitcast.137), channel_id=1, source_target_pairs={{0,10},{2,12},{4,14},{6,0},{8,2},{10,4},{12,6},{14,8},{1,11},{3,13... | collective-permute-start | bytes 196616 | tf_op jit(solution)/shard_map/ppermute | solution.py:61
  65.8 6.4 %collective-permute-start.16 = (f32[16,1024]{1,0:T(8,128)S(1)}, f32[16,1024]{1,0:T(8,128)S(1)}, u32[]{:S(2)}, u32[]{:S(2)}) collective-permute-start(f32[16,1024]{1,0:T(8,128)S(1)} %bitcast.139), channel_id=1, source_target_pairs={{0,12},{2,14},{4,0},{6,2},{8,4},{10,6},{12,8},{14,10},{1,13},{3,15... | collective-permute-start | bytes 196616 | tf_op jit(solution)/shard_map/ppermute | solution.py:61
  67.2 5.0 %collective-permute-start.17 = (f32[16,1024]{1,0:T(8,128)S(1)}, f32[16,1024]{1,0:T(8,128)S(1)}, u32[]{:S(2)}, u32[]{:S(2)}) collective-permute-start(f32[16,1024]{1,0:T(8,128)S(1)} %bitcast.138), channel_id=1, source_target_pairs={{0,14},{2,0},{4,2},{6,4},{8,6},{10,8},{12,10},{14,12},{1,15},{3,1}... | collective-permute-start | bytes 196616 | tf_op jit(solution)/shard_map/ppermute | solution.py:61
  72.2 4.1 %collective-permute-start.18 = (bf16[16,1024]{1,0:T(8,128)(2,1)S(1)}, bf16[16,1024]{1,0:T(8,128)(2,1)S(1)}, u32[]{:S(2)}, u32[]{:S(2)}) collective-permute-start(bf16[16,1024]{1,0:T(8,128)(2,1)S(1)} %clamp_convert_fusion), channel_id=1, source_target_pairs={{0,2},{2,0},{4,6},{6,4},{8,10},{10,8},{12,14},{14,12},{1,3},{3,1},... | collective-permute-start | bytes 98312 | tf_op jit(solution)/shard_map/ppermute | solution.py:28
  76.4 6.6 %collective-permute-start.19 = (bf16[2,16,1024]{2,1,0:T(8,128)(2,1)S(1)}, bf16[2,16,1024]{2,1,0:T(8,128)(2,1)S(1)}, u32[]{:S(2)}, u32[]{:S(2)}) collective-permute-start(bf16[2,16,1024]{2,1,0:T(8,128)(2,1)S(1)} %maximum_select_fusion.3), channel_id=1, source_target_pairs={{0,4},{2,6},{4,8},{6,10},{8,12},{10,14},{12,0},{14,2},{1,5},{3,7},... | collective-permute-start | bytes 196616 | tf_op jit(solution)/shard_map/ppermute | solution.py:34
  78.4 6.5 %collective-permute-start.20 = (bf16[2,16,1024]{2,1,0:T(8,128)(2,1)S(1)}, bf16[2,16,1024]{2,1,0:T(8,128)(2,1)S(1)}, u32[]{:S(2)}, u32[]{:S(2)}) collective-permute-start(bf16[2,16,1024]{2,1,0:T(8,128)(2,1)S(1)} %maximum_select_fusion.3), channel_id=1, source_target_pairs={{0,8},{2,10},{4,12},{6,14},{8,0},{10,2},{12,4},{14,6},{1,9},{3,11}... | collective-permute-start | bytes 196616 | tf_op jit(solution)/shard_map/ppermute | solution.py:34
  80.2 4.9 %collective-permute-start.21 = (bf16[2,16,1024]{2,1,0:T(8,128)(2,1)S(1)}, bf16[2,16,1024]{2,1,0:T(8,128)(2,1)S(1)}, u32[]{:S(2)}, u32[]{:S(2)}) collective-permute-start(bf16[2,16,1024]{2,1,0:T(8,128)(2,1)S(1)} %maximum_select_fusion.3), channel_id=1, source_target_pairs={{0,12},{2,14},{4,0},{6,2},{8,4},{10,6},{12,8},{14,10},{1,13},{3,15... | collective-permute-start | bytes 196616 | tf_op jit(solution)/shard_map/ppermute | solution.py:34

commit v18 on v17

--- a/solution.py
+++ b/solution.py
@@ -273,17 +273,6 @@
         out_near = _attend_packed_pairs(
             jnp.reshape(mine, (1,)), pair.reshape(2, -1, DH), prefix_kv, tail_kv, valid, group
         )
-        far_blk = (mine - jnp.arange(1, half)) % half
-        out_far = _attend_packed_pairs(
-            far_blk, jnp.stack(far).reshape(2 * (half - 1), -1, DH), prefix_kv, tail_kv, valid,
-            group,
-        )
-        outs = jnp.concatenate([out_near, out_far])
-
-        def position(head):
-            d = (mine - head // 2) % half
-            return jnp.where(d == 0, head % 2, 2 * d + head % 2)
-
         got = [
             lax.dynamic_index_in_dim(out_near, tp_rank % 2, 0, keepdims=False),
             lax.ppermute(
@@ -292,10 +281,13 @@
             ),
         ]
         for d in range(1, half):
+            out_d = _attend_packed_pairs(
+                jnp.reshape((mine - d) % half, (1,)), far[d - 1].reshape(2, -1, DH),
+                prefix_kv, tail_kv, valid, group,
+            )
             for flip in (0, 1):
-                dst = ((mine + d) % half) * 2 + (tp_rank % 2 ^ flip)
-                perm = [(i, ((i // 2 + d) % half) * 2 + (i % 2 ^ flip)) for i in range(tp_count)]
-                send = lax.dynamic_index_in_dim(outs, position(dst), 0, keepdims=False)
+                perm = [(i, ((i // 2 - d) % half) * 2 + (i % 2 ^ flip)) for i in range(tp_count)]
+                send = lax.dynamic_index_in_dim(out_d, tp_rank % 2 ^ flip, 0, keepdims=False)
                 got.append(lax.ppermute(send, "tp", perm))
         got = jnp.stack(got)
         got_numer = got[:, :n_rows].reshape(tp_count, steps_n, rows_dev, heads_dev, DH)

time: 87.5 us -> 88.5 us (1.011)
  starting transfers between devices: 38.5 us -> 35 us
  waiting for transfers between devices: 12.6 us -> 14.9 us
  Pallas kernels: 8.09 us -> 9.79 us
  local copies, waits for them, and re-layouts: 7.68 us -> 8.63 us
    ppermute x7, starting transfers between devices: 11.9 us -> 9.82 us  [_exchange(): lax.ppermute(send, axis_name, [(i, (i + k) % count) for i in range(count)])]
    pallas_call x2 -> x4, Pallas kernels: 8.09 us -> 9.79 us  [_attend_packed_pairs(): pl.pallas_call(lambda b_ref, *refs: _attend_packed_kernel(group, *refs),...]
    ppermute x6, starting transfers between devices: 10.7 us -> 9.03 us  [per_device(): got.append(lax.ppermute(send, 'tp', perm))]
    ppermute x6, waiting for transfers between devices: 3.1 us -> 4.46 us  [per_device(): got.append(lax.ppermute(send, 'tp', perm))]
    ppermute x7, waiting for transfers between devices: 3.44 us -> 4.66 us  [_exchange(): lax.ppermute(send, axis_name, [(i, (i + k) % count) for i in range(count)])]
    unnamed x25 -> x29, local copies, waits for them, and re-layouts: 2.26 us -> 2.28 us
  transfers between devices with their start and end apart: 22 -> 22, of which waited for: 10 -> 9; matrix products, arithmetic and copies ran while one was open for 6% -> 7% of each run, Pallas kernels for 9% -> 11%
where the time goes in v18:
time: 88.5 us; the launch traced here: 87.9 us
  starting transfers between devices  35 us (40%)
  waiting for transfers between devices  14.9 us (17%)
  matrix products  13.3 us (15%)
  Pallas kernels  9.79 us (11%)
  local copies, waits for them, and re-layouts  8.63 us (10%)
  other arithmetic  3.84 us (4%)
  blocking collectives  1.85 us (2%)
    dot_general x1, matrix products, per_device(): jnp.einsum('rhd,hdf->rhf', head_rows_in, head_weights, preferred_element_...  12.9 us
    ppermute x7, starting transfers between devices, _exchange(): lax.ppermute(send, axis_name, [(i, (i + k) % count) for i in range(count)])  9.82 us
    pallas_call x4, Pallas kernels, _attend_packed_pairs(): pl.pallas_call(lambda b_ref, *refs: _attend_packed_kernel(group, *refs),...  9.79 us
    ppermute x6, starting transfers between devices, per_device(): got.append(lax.ppermute(send, 'tp', perm))  9.03 us
    ppermute x3, starting transfers between devices, per_device(): lax.ppermute(pair, 'tp', [(i, (i + 2 * d) % tp_count) for i in range(tp_c...  5.57 us
    ppermute x3, starting transfers between devices, _gather_blocks(): lax.ppermute(pair, axis_name, [(i, (i + 2 * d) % count) for i in range(co...  4.78 us
    ppermute x7, waiting for transfers between devices, _exchange(): lax.ppermute(send, axis_name, [(i, (i + k) % count) for i in range(count)])  4.66 us
    ppermute x6, waiting for transfers between devices, per_device(): got.append(lax.ppermute(send, 'tp', perm))  4.46 us
  transfers between devices with their start and end apart: 22, of which 9 were waited for; matrix products, arithmetic and copies ran while one was open for 7% of the time, Pallas kernels for 11%

profile of v18, /device:TPU:0, one launch (start us, length us, event | category | flops | bytes accessed | tf_op | source)
XLA Modules:
  0.0 87.9 jit_solution(15812518960377945539)
XLA Ops:
  0.0 2.9 %collective-permute-start = (bf16[2,4,2048]{2,1,0:T(4,128)(2,1)}, bf16[2,4,2048]{2,1,0:T(4,128)(2,1)S(1)}, u32[]{:S(2)}, u32[]{:S(2)}) collective-permute-start(bf16[2,4,2048]{2,1,0:T(4,128)(2,1)} %param.9), channel_id=1, source_target_pairs={{0,2},{2,0},{4,6},{6,4},{8,10},{10,8},{12,14},{14,12},{1,3},{3,1},... | collective-permute-start | bytes 98312 | tf_op jit(solution)/shard_map/ppermute | solution.py:267
  2.9 0.8 reshape.307
  3.8 0.8 reshape.306
  5.0 0.7 multiply_exponential_fusion.1
  5.7 0.7 compare_convert_fusion.refs_5_
  6.5 0.8 stack.89
  7.7 0.9 %maximum_select_fusion.1 = bf16[2,2,4,2048]{3,2,1,0:T(4,128)(2,1)S(1)} fusion(bf16[1,2,4,2048]{3,2,1,0:T(4,128)(2,1)S(1)} %bitcast.132, bf16[1,2,4,2048]{3,2,1,0:T(4,128)(2,1)} %bitcast.127, pred[]{:T(512)S(6)} %eq.27), kind=kLoop, calls=%fused_computation.25 | loop fusion | flops 98304 | bytes 131073 | tf_op jit(solution)/shard_map/jit(_where)/select_n | solution.py:268
  8.6 1.6 %collective-permute-start.2 = (bf16[2,2,4,2048]{3,2,1,0:T(4,128)(2,1)S(1)}, bf16[2,2,4,2048]{3,2,1,0:T(4,128)(2,1)S(1)}, u32[]{:S(2)}, u32[]{:S(2)}) collective-permute-start(bf16[2,2,4,2048]{3,2,1,0:T(4,128)(2,1)S(1)} %maximum_select_fusion.1), channel_id=1, source_target_pairs={{0,4},{2,6},{4,8},{6,10},{8,12},{10,14},{12,0},{14,2},{1,5},{3,7},... | collective-permute-start | bytes 196616 | tf_op jit(solution)/shard_map/ppermute | solution.py:270
  10.2 2.6 %collective-permute-start.5 = (bf16[2,2,4,2048]{3,2,1,0:T(4,128)(2,1)S(1)}, bf16[2,2,4,2048]{3,2,1,0:T(4,128)(2,1)S(1)}, u32[]{:S(2)}, u32[]{:S(2)}) collective-permute-start(bf16[2,2,4,2048]{3,2,1,0:T(4,128)(2,1)S(1)} %maximum_select_fusion.1), channel_id=1, source_target_pairs={{0,8},{2,10},{4,12},{6,14},{8,0},{10,2},{12,4},{14,6},{1,9},{3,11}... | collective-permute-start | bytes 196616 | tf_op jit(solution)/shard_map/ppermute | solution.py:270
  12.8 1.3 %collective-permute-start.8 = (bf16[2,2,4,2048]{3,2,1,0:T(4,128)(2,1)S(1)}, bf16[2,2,4,2048]{3,2,1,0:T(4,128)(2,1)}, u32[]{:S(2)}, u32[]{:S(2)}) collective-permute-start(bf16[2,2,4,2048]{3,2,1,0:T(4,128)(2,1)S(1)} %maximum_select_fusion.1), channel_id=1, source_target_pairs={{0,12},{2,14},{4,0},{6,2},{8,4},{10,6},{12,8},{14,10},{1,13},{3,15... | collective-permute-start | bytes 196616 | tf_op jit(solution)/shard_map/ppermute | solution.py:270
  14.2 1.6 %copy-done = bf16[2,4,128,1024]{3,2,1,0:T(8,128)(2,1)S(1)} copy-done((bf16[2,4,128,1024]{3,2,1,0:T(8,128)(2,1)S(1)}, bf16[2,4,128,1024]{3,2,1,0:T(8,128)(2,1)}, u32[]{:S(2)}) %copy-start) | copy-done | bytes 2097176
  15.8 2.6 %shard_map.91 = f32[2,136,128]{2,1,0:T(8,128)S(1)} custom-call(s32[1]{0:T(128)} %bitcast.1.b_ref, bf16[2,128,128]{2,1,0:T(8,128)(2,1)S(1)} %maximum_select_fusion.refs_0_, bf16[2,1024,1024]{2,1,0:T(8,128)(2,1)} %refs_2_.7, bf16[2,1024,1024]{2,1,0:T(8,128)(2,1)} %refs_2_.7, bf16[2,4,128,1024]{3,2,1,0:T(8,128)(2,1)S(1)} %copy-done, ...), custom_call_target="tpu_custom_call" | custom-call | flops 201326592 | bytes 1777664 | tf_op jit(solution)/shard_map/pallas_call | solution.py:230
  18.4 0.6 collective-permute-start.1
  19.1 2.4 %shard_map.92 = f32[2,136,128]{2,1,0:T(8,128)S(1)} custom-call(s32[1]{0:T(128)} %bitcast.4.b_ref, bf16[2,128,128]{2,1,0:T(8,128)(2,1)S(1)} %reshape.301.refs_0_, bf16[2,1024,1024]{2,1,0:T(8,128)(2,1)} %refs_2_.7, bf16[2,1024,1024]{2,1,0:T(8,128)(2,1)} %refs_2_.7, bf16[2,4,128,1024]{3,2,1,0:T(8,128)(2,1)S(1)} %copy-done.1, ...), custom_call_target="tpu_custom_call" | custom-call | flops 201326592 | bytes 1777664 | tf_op jit(solution)/shard_map/pallas_call | solution.py:230
  21.5 0.5 collective-permute-start.3
  22.0 2.3 %collective-permute-start.4 = (f32[136,128]{1,0:T(8,128)S(1)}, f32[136,128]{1,0:T(8,128)S(1)}, u32[]{:S(2)}, u32[]{:S(2)}) collective-permute-start(f32[136,128]{1,0:T(8,128)S(1)} %get-tuple-element.19), channel_id=1, source_target_pairs={{0,14},{2,12},{4,2},{6,0},{8,6},{10,4},{12,10},{14,8},{1,15},{3,13... | collective-permute-start | bytes 208904 | tf_op jit(solution)/shard_map/ppermute | solution.py:291
  24.3 2.4 %shard_map.93 = f32[2,136,128]{2,1,0:T(8,128)S(1)} custom-call(s32[1]{0:T(128)} %bitcast.11.b_ref, bf16[2,128,128]{2,1,0:T(8,128)(2,1)S(1)} %reshape.303.refs_0_, bf16[2,1024,1024]{2,1,0:T(8,128)(2,1)} %refs_2_.7, bf16[2,1024,1024]{2,1,0:T(8,128)(2,1)} %refs_2_.7, bf16[2,4,128,1024]{3,2,1,0:T(8,128)(2,1)S(1)} %copy-done.1, ...), custom_call_target="tpu_custom_call" | custom-call | flops 201326592 | bytes 1777664 | tf_op jit(solution)/shard_map/pallas_call | solution.py:230
  26.8 1.8 %collective-permute-start.6 = (f32[136,128]{1,0:T(8,128)S(1)}, f32[136,128]{1,0:T(8,128)S(1)}, u32[]{:S(2)}, u32[]{:S(2)}) collective-permute-start(f32[136,128]{1,0:T(8,128)S(1)} %get-tuple-element.18), channel_id=1, source_target_pairs={{0,8},{2,10},{4,12},{6,14},{8,0},{10,2},{12,4},{14,6},{1,9},{3,11}... | collective-permute-start | bytes 208904 | tf_op jit(solution)/shard_map/ppermute | solution.py:291
  28.5 1.1 %collective-permute-start.7 = (f32[136,128]{1,0:T(8,128)S(1)}, f32[136,128]{1,0:T(8,128)S(1)}, u32[]{:S(2)}, u32[]{:S(2)}) collective-permute-start(f32[136,128]{1,0:T(8,128)S(1)} %get-tuple-element.17), channel_id=1, source_target_pairs={{0,10},{2,8},{4,14},{6,12},{8,2},{10,0},{12,6},{14,4},{1,11},{3,9}... | collective-permute-start | bytes 208904 | tf_op jit(solution)/shard_map/ppermute | solution.py:291
  29.6 0.9 %reshape.305.refs_0_ = bf16[2,128,128]{2,1,0:T(8,128)(2,1)S(1)} reshape(bf16[2,2,4,2048]{3,2,1,0:T(4,128)(2,1)} %collective-permute-done.8) | data formatting | bytes 131072 | tf_op jit(solution)/shard_map/reshape | solution.py:285
  30.5 2.4 %shard_map.94 = f32[2,136,128]{2,1,0:T(8,128)S(1)} custom-call(s32[1]{0:T(128)} %bitcast.16.b_ref, bf16[2,128,128]{2,1,0:T(8,128)(2,1)S(1)} %reshape.305.refs_0_, bf16[2,1024,1024]{2,1,0:T(8,128)(2,1)} %refs_2_.7, bf16[2,1024,1024]{2,1,0:T(8,128)(2,1)} %refs_2_.7, bf16[2,4,128,1024]{3,2,1,0:T(8,128)(2,1)S(1)} %copy-done.1, ...), custom_call_target="tpu_custom_call" | custom-call | flops 201326592 | bytes 1777664 | tf_op jit(solution)/shard_map/pallas_call | solution.py:230
  33.0 0.9 collective-permute-start.9
  33.8 2.6 %collective-permute-start.10 = (f32[136,128]{1,0:T(8,128)S(1)}, f32[136,128]{1,0:T(8,128)S(1)}, u32[]{:S(2)}, u32[]{:S(2)}) collective-permute-start(f32[136,128]{1,0:T(8,128)S(1)} %get-tuple-element.15), channel_id=1, source_target_pairs={{0,6},{2,4},{4,10},{6,8},{8,14},{10,12},{12,2},{14,0},{1,7},{3,5},... | collective-permute-start | bytes 208904 | tf_op jit(solution)/shard_map/ppermute | solution.py:291
  36.5 2.6 %collective-permute-done.9 = f32[136,128]{1,0:T(8,128)S(1)} collective-permute-done((f32[136,128]{1,0:T(8,128)S(1)}, f32[136,128]{1,0:T(8,128)S(1)}, u32[]{:S(2)}, u32[]{:S(2)}) %collective-permute-start.9) | collective-permute-done | bytes 69664 | tf_op jit(solution)/shard_map/ppermute | solution.py:291
  39.1 1.8 %collective-permute-done.10 = f32[136,128]{1,0:T(8,128)S(1)} collective-permute-done((f32[136,128]{1,0:T(8,128)S(1)}, f32[136,128]{1,0:T(8,128)S(1)}, u32[]{:S(2)}, u32[]{:S(2)}) %collective-permute-start.10) | collective-permute-done | bytes 69664 | tf_op jit(solution)/shard_map/ppermute | solution.py:291
  42.5 1.9 %all_gather.3 = bf16[2,8,2048]{2,0,1:T(2,128)(2,1)S(1)} all-gather(bf16[2,4,2048]{2,0,1:T(2,128)(2,1)S(1)} %copy.56), channel_id=1, replica_groups=mesh['rep'=2,'tp'=8,'sub'=2] {'sub'}, dimensions={1}, use_global_device_ids=true | all-gather | bytes 98304 | tf_op jit(solution)/shard_map/all_gather | solution.py:362
  44.5 12.9 %fusion.1 = f32[16,8192]{1,0:T(8,128)S(1)} fusion(f32[8192]{0:T(1024)S(1)} %dynamic-slice-done, bf16[16,128,8192]{2,1,0:T(8,128)(2,1)} %bitcast.147, bf16[16,16,128]{2,1,0:T(8,128)(2,1)S(1)} %bitcast.142), kind=kOutput, calls=%fused_computation.3 | convolution fusion | flops 543031296 | bytes 34177024 | tf_op jit(solution)/shard_map/rhd,hdf->rhf/dot_general | solution.py:371
  57.4 0.3 copy.74
  57.7 0.5 constant_dynamic-slice_fusion.8
  58.3 1.5 %collective-permute-start.11 = (f32[16,1024]{1,0:T(8,128)S(1)}, f32[16,1024]{1,0:T(8,128)S(1)}, u32[]{:S(2)}, u32[]{:S(2)}) collective-permute-start(f32[16,1024]{1,0:T(8,128)S(1)} %bitcast.141), channel_id=1, source_target_pairs={{0,2},{2,4},{4,6},{6,8},{8,10},{10,12},{12,14},{14,0},{1,3},{3,5},... | collective-permute-start | bytes 196616 | tf_op jit(solution)/shard_map/ppermute | solution.py:61
  59.9 1.8 %collective-permute-start.13 = (f32[16,1024]{1,0:T(8,128)S(1)}, f32[16,1024]{1,0:T(8,128)S(1)}, u32[]{:S(2)}, u32[]{:S(2)}) collective-permute-start(f32[16,1024]{1,0:T(8,128)S(1)} %bitcast.135), channel_id=1, source_target_pairs={{0,6},{2,8},{4,10},{6,12},{8,14},{10,0},{12,2},{14,4},{1,7},{3,9},... | collective-permute-start | bytes 196616 | tf_op jit(solution)/shard_map/ppermute | solution.py:61
  61.7 2.2 %collective-permute-start.14 = (f32[16,1024]{1,0:T(8,128)S(1)}, f32[16,1024]{1,0:T(8,128)S(1)}, u32[]{:S(2)}, u32[]{:S(2)}) collective-permute-start(f32[16,1024]{1,0:T(8,128)S(1)} %bitcast.136), channel_id=1, source_target_pairs={{0,8},{2,10},{4,12},{6,14},{8,0},{10,2},{12,4},{14,6},{1,9},{3,11}... | collective-permute-start | bytes 196616 | tf_op jit(solution)/shard_map/ppermute | solution.py:61
  63.9 1.9 %collective-permute-start.15 = (f32[16,1024]{1,0:T(8,128)S(1)}, f32[16,1024]{1,0:T(8,128)S(1)}, u32[]{:S(2)}, u32[]{:S(2)}) collective-permute-start(f32[16,1024]{1,0:T(8,128)S(1)} %bitcast.137), channel_id=1, source_target_pairs={{0,10},{2,12},{4,14},{6,0},{8,2},{10,4},{12,6},{14,8},{1,11},{3,13... | collective-permute-start | bytes 196616 | tf_op jit(solution)/shard_map/ppermute | solution.py:61
  66.1 1.8 %collective-permute-start.16 = (f32[16,1024]{1,0:T(8,128)S(1)}, f32[16,1024]{1,0:T(8,128)S(1)}, u32[]{:S(2)}, u32[]{:S(2)}) collective-permute-start(f32[16,1024]{1,0:T(8,128)S(1)} %bitcast.139), channel_id=1, source_target_pairs={{0,12},{2,14},{4,0},{6,2},{8,4},{10,6},{12,8},{14,10},{1,13},{3,15... | collective-permute-start | bytes 196616 | tf_op jit(solution)/shard_map/ppermute | solution.py:61
  67.9 0.6 collective-permute-start.17
  68.6 2.4 %collective-permute-done.13 = f32[16,1024]{1,0:T(8,128)S(1)} collective-permute-done((f32[16,1024]{1,0:T(8,128)S(1)}, f32[16,1024]{1,0:T(8,128)S(1)}, u32[]{:S(2)}, u32[]{:S(2)}) %collective-permute-start.13) | collective-permute-done | bytes 65568 | tf_op jit(solution)/shard_map/ppermute | solution.py:61
  70.9 0.4 collective-permute-done.14
  71.4 1.7 %collective-permute-done.16 = f32[16,1024]{1,0:T(8,128)S(1)} collective-permute-done((f32[16,1024]{1,0:T(8,128)S(1)}, f32[16,1024]{1,0:T(8,128)S(1)}, u32[]{:S(2)}, u32[]{:S(2)}) %collective-permute-start.16) | collective-permute-done | bytes 65568 | tf_op jit(solution)/shard_map/ppermute | solution.py:61
  73.1 2.2 %collective-permute-start.18 = (bf16[16,1024]{1,0:T(8,128)(2,1)S(1)}, bf16[16,1024]{1,0:T(8,128)(2,1)S(1)}, u32[]{:S(2)}, u32[]{:S(2)}) collective-permute-start(bf16[16,1024]{1,0:T(8,128)(2,1)S(1)} %clamp_convert_fusion), channel_id=1, source_target_pairs={{0,2},{2,0},{4,6},{6,4},{8,10},{10,8},{12,14},{14,12},{1,3},{3,1},... | collective-permute-start | bytes 98312 | tf_op jit(solution)/shard_map/ppermute | solution.py:28
  75.3 1.9 %collective-permute-done.18 = bf16[16,1024]{1,0:T(8,128)(2,1)S(1)} collective-permute-done((bf16[16,1024]{1,0:T(8,128)(2,1)S(1)}, bf16[16,1024]{1,0:T(8,128)(2,1)S(1)}, u32[]{:S(2)}, u32[]{:S(2)}) %collective-permute-start.18) | collective-permute-done | bytes 32800 | tf_op jit(solution)/shard_map/ppermute | solution.py:28
  77.2 2.3 %collective-permute-start.19 = (bf16[2,16,1024]{2,1,0:T(8,128)(2,1)S(1)}, bf16[2,16,1024]{2,1,0:T(8,128)(2,1)S(1)}, u32[]{:S(2)}, u32[]{:S(2)}) collective-permute-start(bf16[2,16,1024]{2,1,0:T(8,128)(2,1)S(1)} %maximum_select_fusion.3), channel_id=1, source_target_pairs={{0,4},{2,6},{4,8},{6,10},{8,12},{10,14},{12,0},{14,2},{1,5},{3,7},... | collective-permute-start | bytes 196616 | tf_op jit(solution)/shard_map/ppermute | solution.py:34
  79.5 1.3 %collective-permute-start.20 = (bf16[2,16,1024]{2,1,0:T(8,128)(2,1)S(1)}, bf16[2,16,1024]{2,1,0:T(8,128)(2,1)S(1)}, u32[]{:S(2)}, u32[]{:S(2)}) collective-permute-start(bf16[2,16,1024]{2,1,0:T(8,128)(2,1)S(1)} %maximum_select_fusion.3), channel_id=1, source_target_pairs={{0,8},{2,10},{4,12},{6,14},{8,0},{10,2},{12,4},{14,6},{1,9},{3,11}... | collective-permute-start | bytes 196616 | tf_op jit(solution)/shard_map/ppermute | solution.py:34
  80.8 1.2 %collective-permute-start.21 = (bf16[2,16,1024]{2,1,0:T(8,128)(2,1)S(1)}, bf16[2,16,1024]{2,1,0:T(8,128)(2,1)S(1)}, u32[]{:S(2)}, u32[]{:S(2)}) collective-permute-start(bf16[2,16,1024]{2,1,0:T(8,128)(2,1)S(1)} %maximum_select_fusion.3), channel_id=1, source_target_pairs={{0,12},{2,14},{4,0},{6,2},{8,4},{10,6},{12,8},{14,10},{1,13},{3,15... | collective-permute-start | bytes 196616 | tf_op jit(solution)/shard_map/ppermute | solution.py:34
  82.0 1.7 %collective-permute-done.19 = bf16[2,16,1024]{2,1,0:T(8,128)(2,1)S(1)} collective-permute-done((bf16[2,16,1024]{2,1,0:T(8,128)(2,1)S(1)}, bf16[2,16,1024]{2,1,0:T(8,128)(2,1)S(1)}, u32[]{:S(2)}, u32[]{:S(2)}) %collective-permute-start.19) | collective-permute-done | bytes 65568 | tf_op jit(solution)/shard_map/ppermute | solution.py:34
  83.7 2.2 %collective-permute-done.20 = bf16[2,16,1024]{2,1,0:T(8,128)(2,1)S(1)} collective-permute-done((bf16[2,16,1024]{2,1,0:T(8,128)(2,1)S(1)}, bf16[2,16,1024]{2,1,0:T(8,128)(2,1)S(1)}, u32[]{:S(2)}, u32[]{:S(2)}) %collective-permute-start.20) | collective-permute-done | bytes 65568 | tf_op jit(solution)/shard_map/ppermute | solution.py:34
  86.0 0.7 scatter_fusion
  86.7 0.3 copy.59
  87.1 0.8 add_convert_fusion
  (97 shorter events, 3.4 us)
Async XLA Ops:
  0.0 7.7 %collective-permute-start = (bf16[2,4,2048]{2,1,0:T(4,128)(2,1)}, bf16[2,4,2048]{2,1,0:T(4,128)(2,1)S(1)}, u32[]{:S(2)}, u32[]{:S(2)}) collective-permute-start(bf16[2,4,2048]{2,1,0:T(4,128)(2,1)} %param.9), channel_id=1, source_target_pairs={{0,2},{2,0},{4,6},{6,4},{8,10},{10,8},{12,14},{14,12},{1,3},{3,1},... | collective-permute-start | bytes 98312 | tf_op jit(solution)/shard_map/ppermute | solution.py:267
  5.7 15.8 %copy-start.3 = (f32[16384]{0:T(1024)}, f32[16384]{0:T(1024)S(1)}, u32[]{:S(2)}) copy-start(f32[16384]{0:T(1024)S(1)} %broadcast_bitcast_fusion.1) | copy-start | bytes 196612
  8.6 10.4 %collective-permute-start.2 = (bf16[2,2,4,2048]{3,2,1,0:T(4,128)(2,1)S(1)}, bf16[2,2,4,2048]{3,2,1,0:T(4,128)(2,1)S(1)}, u32[]{:S(2)}, u32[]{:S(2)}) collective-permute-start(bf16[2,2,4,2048]{3,2,1,0:T(4,128)(2,1)S(1)} %maximum_select_fusion.1), channel_id=1, source_target_pairs={{0,4},{2,6},{4,8},{6,10},{8,12},{10,14},{12,0},{14,2},{1,5},{3,7},... | collective-permute-start | bytes 196616 | tf_op jit(solution)/shard_map/ppermute | solution.py:270
  10.2 14.1 %collective-permute-start.5 = (bf16[2,2,4,2048]{3,2,1,0:T(4,128)(2,1)S(1)}, bf16[2,2,4,2048]{3,2,1,0:T(4,128)(2,1)S(1)}, u32[]{:S(2)}, u32[]{:S(2)}) collective-permute-start(bf16[2,2,4,2048]{3,2,1,0:T(4,128)(2,1)S(1)} %maximum_select_fusion.1), channel_id=1, source_target_pairs={{0,8},{2,10},{4,12},{6,14},{8,0},{10,2},{12,4},{14,6},{1,9},{3,11}... | collective-permute-start | bytes 196616 | tf_op jit(solution)/shard_map/ppermute | solution.py:270
  12.8 15.7 %collective-permute-start.8 = (bf16[2,2,4,2048]{3,2,1,0:T(4,128)(2,1)S(1)}, bf16[2,2,4,2048]{3,2,1,0:T(4,128)(2,1)}, u32[]{:S(2)}, u32[]{:S(2)}) collective-permute-start(bf16[2,2,4,2048]{3,2,1,0:T(4,128)(2,1)S(1)} %maximum_select_fusion.1), channel_id=1, source_target_pairs={{0,12},{2,14},{4,0},{6,2},{8,4},{10,6},{12,8},{14,10},{1,13},{3,15... | collective-permute-start | bytes 196616 | tf_op jit(solution)/shard_map/ppermute | solution.py:270
  14.2 1.6 %copy-start = (bf16[2,4,128,1024]{3,2,1,0:T(8,128)(2,1)S(1)}, bf16[2,4,128,1024]{3,2,1,0:T(8,128)(2,1)}, u32[]{:S(2)}) copy-start(bf16[2,4,128,1024]{3,2,1,0:T(8,128)(2,1)} %refs_4_.7) | copy-start | bytes 6291460
  15.8 3.2 %copy-start.1 = (bf16[2,4,128,1024]{3,2,1,0:T(8,128)(2,1)S(1)}, bf16[2,4,128,1024]{3,2,1,0:T(8,128)(2,1)}, u32[]{:S(2)}) copy-start(bf16[2,4,128,1024]{3,2,1,0:T(8,128)(2,1)} %refs_4_.7) | copy-start | bytes 6291460
  18.4 14.6 %collective-permute-start.1 = (f32[136,128]{1,0:T(8,128)S(1)}, f32[136,128]{1,0:T(8,128)S(1)}, u32[]{:S(2)}, u32[]{:S(2)}) collective-permute-start(f32[136,128]{1,0:T(8,128)S(1)} %get-tuple-element.21), channel_id=1, source_target_pairs={{0,2},{2,0},{4,6},{6,4},{8,10},{10,8},{12,14},{14,12},{1,3},{3,1},... | collective-permute-start | bytes 208904 | tf_op jit(solution)/shard_map/ppermute | solution.py:278
  21.5 12.3 %collective-permute-start.3 = (f32[136,128]{1,0:T(8,128)S(1)}, f32[136,128]{1,0:T(8,128)S(1)}, u32[]{:S(2)}, u32[]{:S(2)}) collective-permute-start(f32[136,128]{1,0:T(8,128)S(1)} %get-tuple-element.20), channel_id=1, source_target_pairs={{0,12},{2,14},{4,0},{6,2},{8,4},{10,6},{12,8},{14,10},{1,13},{3,15... | collective-permute-start | bytes 208904 | tf_op jit(solution)/shard_map/ppermute | solution.py:291
  22.0 14.4 %collective-permute-start.4 = (f32[136,128]{1,0:T(8,128)S(1)}, f32[136,128]{1,0:T(8,128)S(1)}, u32[]{:S(2)}, u32[]{:S(2)}) collective-permute-start(f32[136,128]{1,0:T(8,128)S(1)} %get-tuple-element.19), channel_id=1, source_target_pairs={{0,14},{2,12},{4,2},{6,0},{8,6},{10,4},{12,10},{14,8},{1,15},{3,13... | collective-permute-start | bytes 208904 | tf_op jit(solution)/shard_map/ppermute | solution.py:291
  26.7 17.7 %dynamic-slice-start = ((f32[16384]{0:T(1024)}, s32[]{:T(128)}), f32[8192]{0:T(1024)S(1)}, s32[]{:S(2)}) async-start(f32[16384]{0:T(1024)} %copy-done.3, s32[]{:T(128)} %select_n.202), calls=%async_computation | async-start | bytes 66048 | tf_op jit(solution)/shard_map/dynamic_slice | solution.py:369
  26.8 9.6 %collective-permute-start.6 = (f32[136,128]{1,0:T(8,128)S(1)}, f32[136,128]{1,0:T(8,128)S(1)}, u32[]{:S(2)}, u32[]{:S(2)}) collective-permute-start(f32[136,128]{1,0:T(8,128)S(1)} %get-tuple-element.18), channel_id=1, source_target_pairs={{0,8},{2,10},{4,12},{6,14},{8,0},{10,2},{12,4},{14,6},{1,9},{3,11}... | collective-permute-start | bytes 208904 | tf_op jit(solution)/shard_map/ppermute | solution.py:291
  28.5 7.9 %collective-permute-start.7 = (f32[136,128]{1,0:T(8,128)S(1)}, f32[136,128]{1,0:T(8,128)S(1)}, u32[]{:S(2)}, u32[]{:S(2)}) collective-permute-start(f32[136,128]{1,0:T(8,128)S(1)} %get-tuple-element.17), channel_id=1, source_target_pairs={{0,10},{2,8},{4,14},{6,12},{8,2},{10,0},{12,6},{14,4},{1,11},{3,9}... | collective-permute-start | bytes 208904 | tf_op jit(solution)/shard_map/ppermute | solution.py:291
  33.0 6.2 %collective-permute-start.9 = (f32[136,128]{1,0:T(8,128)S(1)}, f32[136,128]{1,0:T(8,128)S(1)}, u32[]{:S(2)}, u32[]{:S(2)}) collective-permute-start(f32[136,128]{1,0:T(8,128)S(1)} %get-tuple-element.16), channel_id=1, source_target_pairs={{0,4},{2,6},{4,8},{6,10},{8,12},{10,14},{12,0},{14,2},{1,5},{3,7},... | collective-permute-start | bytes 208904 | tf_op jit(solution)/shard_map/ppermute | solution.py:291
  33.8 7.1 %collective-permute-start.10 = (f32[136,128]{1,0:T(8,128)S(1)}, f32[136,128]{1,0:T(8,128)S(1)}, u32[]{:S(2)}, u32[]{:S(2)}) collective-permute-start(f32[136,128]{1,0:T(8,128)S(1)} %get-tuple-element.15), channel_id=1, source_target_pairs={{0,6},{2,4},{4,10},{6,8},{8,14},{10,12},{12,2},{14,0},{1,7},{3,5},... | collective-permute-start | bytes 208904 | tf_op jit(solution)/shard_map/ppermute | solution.py:291
  44.5 15.4 %copy-start.5 = (s32[128]{0:T(128)S(1)}, s32[128]{0:T(128)}, u32[]{:S(2)}) copy-start(s32[128]{0:T(128)} %param.16) | copy-start | bytes 1540
  44.5 24.1 %copy-start.4 = (f32[16384]{0:T(1024)S(1)}, f32[16384]{0:T(1024)}, u32[]{:S(2)}) copy-start(f32[16384]{0:T(1024)} %copy-done.3) | copy-start | bytes 196612
  57.4 29.7 %copy-start.2 = (bf16[2,8,8192]{2,1,0:T(8,128)(2,1)S(1)}, bf16[2,8,8192]{2,1,0:T(8,128)(2,1)}, u32[]{:S(2)}) copy-start(bf16[2,8,8192]{2,1,0:T(8,128)(2,1)} %param.17) | copy-start | bytes 786436
  58.3 7.8 %collective-permute-start.11 = (f32[16,1024]{1,0:T(8,128)S(1)}, f32[16,1024]{1,0:T(8,128)S(1)}, u32[]{:S(2)}, u32[]{:S(2)}) collective-permute-start(f32[16,1024]{1,0:T(8,128)S(1)} %bitcast.141), channel_id=1, source_target_pairs={{0,2},{2,4},{4,6},{6,8},{8,10},{10,12},{12,14},{14,0},{1,3},{3,5},... | collective-permute-start | bytes 196616 | tf_op jit(solution)/shard_map/ppermute | solution.py:61
  59.8 8.1 %collective-permute-start.12 = (f32[16,1024]{1,0:T(8,128)S(1)}, f32[16,1024]{1,0:T(8,128)S(1)}, u32[]{:S(2)}, u32[]{:S(2)}) collective-permute-start(f32[16,1024]{1,0:T(8,128)S(1)} %bitcast.140), channel_id=1, source_target_pairs={{0,4},{2,6},{4,8},{6,10},{8,12},{10,14},{12,0},{14,2},{1,5},{3,7},... | collective-permute-start | bytes 196616 | tf_op jit(solution)/shard_map/ppermute | solution.py:61
  59.9 11.0 %collective-permute-start.13 = (f32[16,1024]{1,0:T(8,128)S(1)}, f32[16,1024]{1,0:T(8,128)S(1)}, u32[]{:S(2)}, u32[]{:S(2)}) collective-permute-start(f32[16,1024]{1,0:T(8,128)S(1)} %bitcast.135), channel_id=1, source_target_pairs={{0,6},{2,8},{4,10},{6,12},{8,14},{10,0},{12,2},{14,4},{1,7},{3,9},... | collective-permute-start | bytes 196616 | tf_op jit(solution)/shard_map/ppermute | solution.py:61
  61.7 9.7 %collective-permute-start.14 = (f32[16,1024]{1,0:T(8,128)S(1)}, f32[16,1024]{1,0:T(8,128)S(1)}, u32[]{:S(2)}, u32[]{:S(2)}) collective-permute-start(f32[16,1024]{1,0:T(8,128)S(1)} %bitcast.136), channel_id=1, source_target_pairs={{0,8},{2,10},{4,12},{6,14},{8,0},{10,2},{12,4},{14,6},{1,9},{3,11}... | collective-permute-start | bytes 196616 | tf_op jit(solution)/shard_map/ppermute | solution.py:61
  63.9 7.5 %collective-permute-start.15 = (f32[16,1024]{1,0:T(8,128)S(1)}, f32[16,1024]{1,0:T(8,128)S(1)}, u32[]{:S(2)}, u32[]{:S(2)}) collective-permute-start(f32[16,1024]{1,0:T(8,128)S(1)} %bitcast.137), channel_id=1, source_target_pairs={{0,10},{2,12},{4,14},{6,0},{8,2},{10,4},{12,6},{14,8},{1,11},{3,13... | collective-permute-start | bytes 196616 | tf_op jit(solution)/shard_map/ppermute | solution.py:61
  66.1 7.0 %collective-permute-start.16 = (f32[16,1024]{1,0:T(8,128)S(1)}, f32[16,1024]{1,0:T(8,128)S(1)}, u32[]{:S(2)}, u32[]{:S(2)}) collective-permute-start(f32[16,1024]{1,0:T(8,128)S(1)} %bitcast.139), channel_id=1, source_target_pairs={{0,12},{2,14},{4,0},{6,2},{8,4},{10,6},{12,8},{14,10},{1,13},{3,15... | collective-permute-start | bytes 196616 | tf_op jit(solution)/shard_map/ppermute | solution.py:61
  67.9 5.1 %collective-permute-start.17 = (f32[16,1024]{1,0:T(8,128)S(1)}, f32[16,1024]{1,0:T(8,128)S(1)}, u32[]{:S(2)}, u32[]{:S(2)}) collective-permute-start(f32[16,1024]{1,0:T(8,128)S(1)} %bitcast.138), channel_id=1, source_target_pairs={{0,14},{2,0},{4,2},{6,4},{8,6},{10,8},{12,10},{14,12},{1,15},{3,1}... | collective-permute-start | bytes 196616 | tf_op jit(solution)/shard_map/ppermute | solution.py:61
  73.1 4.1 %collective-permute-start.18 = (bf16[16,1024]{1,0:T(8,128)(2,1)S(1)}, bf16[16,1024]{1,0:T(8,128)(2,1)S(1)}, u32[]{:S(2)}, u32[]{:S(2)}) collective-permute-start(bf16[16,1024]{1,0:T(8,128)(2,1)S(1)} %clamp_convert_fusion), channel_id=1, source_target_pairs={{0,2},{2,0},{4,6},{6,4},{8,10},{10,8},{12,14},{14,12},{1,3},{3,1},... | collective-permute-start | bytes 98312 | tf_op jit(solution)/shard_map/ppermute | solution.py:28
  77.2 6.5 %collective-permute-start.19 = (bf16[2,16,1024]{2,1,0:T(8,128)(2,1)S(1)}, bf16[2,16,1024]{2,1,0:T(8,128)(2,1)S(1)}, u32[]{:S(2)}, u32[]{:S(2)}) collective-permute-start(bf16[2,16,1024]{2,1,0:T(8,128)(2,1)S(1)} %maximum_select_fusion.3), channel_id=1, source_target_pairs={{0,4},{2,6},{4,8},{6,10},{8,12},{10,14},{12,0},{14,2},{1,5},{3,7},... | collective-permute-start | bytes 196616 | tf_op jit(solution)/shard_map/ppermute | solution.py:34
  79.5 6.4 %collective-permute-start.20 = (bf16[2,16,1024]{2,1,0:T(8,128)(2,1)S(1)}, bf16[2,16,1024]{2,1,0:T(8,128)(2,1)S(1)}, u32[]{:S(2)}, u32[]{:S(2)}) collective-permute-start(bf16[2,16,1024]{2,1,0:T(8,128)(2,1)S(1)} %maximum_select_fusion.3), channel_id=1, source_target_pairs={{0,8},{2,10},{4,12},{6,14},{8,0},{10,2},{12,4},{14,6},{1,9},{3,11}... | collective-permute-start | bytes 196616 | tf_op jit(solution)/shard_map/ppermute | solution.py:34
  80.8 5.1 %collective-permute-start.21 = (bf16[2,16,1024]{2,1,0:T(8,128)(2,1)S(1)}, bf16[2,16,1024]{2,1,0:T(8,128)(2,1)S(1)}, u32[]{:S(2)}, u32[]{:S(2)}) collective-permute-start(bf16[2,16,1024]{2,1,0:T(8,128)(2,1)S(1)} %maximum_select_fusion.3), channel_id=1, source_target_pairs={{0,12},{2,14},{4,0},{6,2},{8,4},{10,6},{12,8},{14,10},{1,13},{3,15... | collective-permute-start | bytes 196616 | tf_op jit(solution)/shard_map/ppermute | solution.py:34

commit v19 on v17

--- a/solution.py
+++ b/solution.py
@@ -55,10 +55,21 @@
         )
     me = lax.axis_index(axis_name)
     got = [jax.tree.map(lambda b: lax.dynamic_index_in_dim(b, me, 0, keepdims=False), blocks)]
-    for k in range(1, count):
-        dst = (me + k) % count
+    if count in (4, 8):
+        half = count // 2
+        moves = [(me ^ 1, [(i, i ^ 1) for i in range(count)])]
+        for d in range(1, half):
+            for flip in (0, 1):
+                moves.append((
+                    ((me // 2 + d) % half) * 2 + (me % 2 ^ flip),
+                    [(i, ((i // 2 + d) % half) * 2 + (i % 2 ^ flip)) for i in range(count)],
+                ))
+    else:
+        moves = [((me + k) % count, [(i, (i + k) % count) for i in range(count)])
+                 for k in range(1, count)]
+    for dst, perm in moves:
         send = jax.tree.map(lambda b: lax.dynamic_index_in_dim(b, dst, 0, keepdims=False), blocks)
-        got.append(lax.ppermute(send, axis_name, [(i, (i + k) % count) for i in range(count)]))
+        got.append(lax.ppermute(send, axis_name, perm))
     return jax.tree.map(lambda *xs: jnp.stack(xs), *got)
 
 

time: 87.5 us -> 88 us (level)
  waiting for transfers between devices: 12.6 us -> 14.6 us
  starting transfers between devices: 38.5 us -> 37 us
    ppermute x1, starting transfers between devices: 2.23 us -> 1.14 us  [_gather_blocks(): other = lax.ppermute(x, axis_name, [(i, i ^ 1) for i in range(count)])]
    ppermute x7, waiting for transfers between devices: 3.44 us -> 4.48 us  [_exchange(): got.append(lax.ppermute(send, axis_name, perm))]
    ppermute x1, waiting for transfers between devices: 1.86 us -> 2.81 us  [_gather_blocks(): other = lax.ppermute(x, axis_name, [(i, i ^ 1) for i in range(count)])]
where the time goes in v19:
time: 88 us; the launch traced here: 87.6 us
  starting transfers between devices  37 us (42%)
  waiting for transfers between devices  14.6 us (17%)
  matrix products  13.3 us (15%)
  Pallas kernels  8.07 us (9%)
  local copies, waits for them, and re-layouts  7.68 us (9%)
  other arithmetic  4.14 us (5%)
  blocking collectives  1.85 us (2%)
  between operations  0.95 us (1%)
    dot_general x1, matrix products, per_device(): jnp.einsum('rhd,hdf->rhf', head_rows_in, head_weights, preferred_element_...  12.9 us
    ppermute x7, starting transfers between devices, _exchange(): got.append(lax.ppermute(send, axis_name, perm))  12 us
    ppermute x6, starting transfers between devices, per_device(): got.append(lax.ppermute(send, 'tp', perm))  10.7 us
    pallas_call x2, Pallas kernels, _attend_packed_pairs(): pl.pallas_call(lambda b_ref, *refs: _attend_packed_kernel(group, *refs),...  8.07 us
    ppermute x3, starting transfers between devices, per_device(): lax.ppermute(pair, 'tp', [(i, (i + 2 * d) % tp_count) for i in range(tp_c...  5.57 us
    ppermute x7, waiting for transfers between devices, _exchange(): got.append(lax.ppermute(send, axis_name, perm))  4.48 us
    ppermute x3, waiting for transfers between devices, _gather_blocks(): lax.ppermute(pair, axis_name, [(i, (i + 2 * d) % count) for i in range(co...  4.17 us
    ppermute x3, starting transfers between devices, _gather_blocks(): lax.ppermute(pair, axis_name, [(i, (i + 2 * d) % count) for i in range(co...  4.04 us
  transfers between devices with their start and end apart: 22, of which 10 were waited for; matrix products, arithmetic and copies ran while one was open for 6% of the time, Pallas kernels for 9%

profile of v19, /device:TPU:0, one launch (start us, length us, event | category | flops | bytes accessed | tf_op | source)
XLA Modules:
  0.0 87.6 jit_solution(8754495473162081798)
XLA Ops:
  0.0 2.9 %collective-permute-start = (bf16[2,4,2048]{2,1,0:T(4,128)(2,1)}, bf16[2,4,2048]{2,1,0:T(4,128)(2,1)S(1)}, u32[]{:S(2)}, u32[]{:S(2)}) collective-permute-start(bf16[2,4,2048]{2,1,0:T(4,128)(2,1)} %param.9), channel_id=1, source_target_pairs={{0,2},{2,0},{4,6},{6,4},{8,10},{10,8},{12,14},{14,12},{1,3},{3,1},... | collective-permute-start | bytes 98312 | tf_op jit(solution)/shard_map/ppermute | solution.py:278
  2.9 0.8 reshape.287
  3.8 0.8 reshape.286
  5.0 0.7 multiply_exponential_fusion.1
  5.7 0.7 compare_convert_fusion.refs_5_
  7.0 0.8 stack.101
  8.1 0.9 %maximum_select_fusion.1 = bf16[2,2,4,2048]{3,2,1,0:T(4,128)(2,1)S(1)} fusion(bf16[1,2,4,2048]{3,2,1,0:T(4,128)(2,1)S(1)} %bitcast.132, bf16[1,2,4,2048]{3,2,1,0:T(4,128)(2,1)} %bitcast.127, pred[]{:T(512)S(6)} %eq.73), kind=kLoop, calls=%fused_computation.44 | loop fusion | flops 98304 | bytes 131073 | tf_op jit(solution)/shard_map/jit(_where)/select_n | solution.py:279
  9.0 1.6 %collective-permute-start.2 = (bf16[2,2,4,2048]{3,2,1,0:T(4,128)(2,1)S(1)}, bf16[2,2,4,2048]{3,2,1,0:T(4,128)(2,1)S(1)}, u32[]{:S(2)}, u32[]{:S(2)}) collective-permute-start(bf16[2,2,4,2048]{3,2,1,0:T(4,128)(2,1)S(1)} %maximum_select_fusion.1), channel_id=1, source_target_pairs={{0,4},{2,6},{4,8},{6,10},{8,12},{10,14},{12,0},{14,2},{1,5},{3,7},... | collective-permute-start | bytes 196616 | tf_op jit(solution)/shard_map/ppermute | solution.py:281
  10.6 2.6 %collective-permute-start.3 = (bf16[2,2,4,2048]{3,2,1,0:T(4,128)(2,1)S(1)}, bf16[2,2,4,2048]{3,2,1,0:T(4,128)(2,1)S(1)}, u32[]{:S(2)}, u32[]{:S(2)}) collective-permute-start(bf16[2,2,4,2048]{3,2,1,0:T(4,128)(2,1)S(1)} %maximum_select_fusion.1), channel_id=1, source_target_pairs={{0,8},{2,10},{4,12},{6,14},{8,0},{10,2},{12,4},{14,6},{1,9},{3,11}... | collective-permute-start | bytes 196616 | tf_op jit(solution)/shard_map/ppermute | solution.py:281
  13.2 1.3 %collective-permute-start.4 = (bf16[2,2,4,2048]{3,2,1,0:T(4,128)(2,1)S(1)}, bf16[2,2,4,2048]{3,2,1,0:T(4,128)(2,1)S(1)}, u32[]{:S(2)}, u32[]{:S(2)}) collective-permute-start(bf16[2,2,4,2048]{3,2,1,0:T(4,128)(2,1)S(1)} %maximum_select_fusion.1), channel_id=1, source_target_pairs={{0,12},{2,14},{4,0},{6,2},{8,4},{10,6},{12,8},{14,10},{1,13},{3,15... | collective-permute-start | bytes 196616 | tf_op jit(solution)/shard_map/ppermute | solution.py:281
  14.6 1.6 %copy-done = bf16[2,4,128,1024]{3,2,1,0:T(8,128)(2,1)S(1)} copy-done((bf16[2,4,128,1024]{3,2,1,0:T(8,128)(2,1)S(1)}, bf16[2,4,128,1024]{3,2,1,0:T(8,128)(2,1)}, u32[]{:S(2)}) %copy-start) | copy-done | bytes 2097176
  16.2 2.6 %shard_map.91 = f32[2,136,128]{2,1,0:T(8,128)S(1)} custom-call(s32[1]{0:T(128)} %bitcast.1.b_ref, bf16[2,128,128]{2,1,0:T(8,128)(2,1)S(1)} %maximum_select_fusion.refs_0_, bf16[2,1024,1024]{2,1,0:T(8,128)(2,1)} %refs_2_.3, bf16[2,1024,1024]{2,1,0:T(8,128)(2,1)} %refs_2_.3, bf16[2,4,128,1024]{3,2,1,0:T(8,128)(2,1)S(1)} %copy-done, ...), custom_call_target="tpu_custom_call" | custom-call | flops 201326592 | bytes 1777664 | tf_op jit(solution)/shard_map/pallas_call | solution.py:241
  18.8 0.6 collective-permute-start.1
  19.7 5.5 %shard_map.92 = f32[6,136,128]{2,1,0:T(8,128)S(1)} custom-call(s32[3]{0:T(128)S(1)} %and_select_fusion.b_ref, bf16[6,128,128]{2,1,0:T(8,128)(2,1)S(1)} %reshape.285.refs_0_, bf16[2,1024,1024]{2,1,0:T(8,128)(2,1)} %refs_2_.3, bf16[2,1024,1024]{2,1,0:T(8,128)(2,1)} %refs_2_.3, bf16[2,4,128,1024]{3,2,1,0:T(8,128)(2,1)S(1)} %copy-done.1, ...), custom_call_target="tpu_custom_call" | custom-call | flops 603979776 | bytes 5332992 | tf_op jit(solution)/shard_map/pallas_call | solution.py:241
  25.3 0.7 collective-permute-start.5
  26.1 1.2 %collective-permute-start.6 = (f32[136,128]{1,0:T(8,128)S(1)}, f32[136,128]{1,0:T(8,128)S(1)}, u32[]{:S(2)}, u32[]{:S(2)}) collective-permute-start(f32[136,128]{1,0:T(8,128)S(1)} %get-tuple-element.9), channel_id=1, source_target_pairs={{0,6},{2,4},{4,10},{6,8},{8,14},{10,12},{12,2},{14,0},{1,7},{3,5},... | collective-permute-start | bytes 208904 | tf_op jit(solution)/shard_map/ppermute | solution.py:310
  27.2 3.5 %collective-permute-start.7 = (f32[136,128]{1,0:T(8,128)S(1)}, f32[136,128]{1,0:T(8,128)S(1)}, u32[]{:S(2)}, u32[]{:S(2)}) collective-permute-start(f32[136,128]{1,0:T(8,128)S(1)} %get-tuple-element.10), channel_id=1, source_target_pairs={{0,8},{2,10},{4,12},{6,14},{8,0},{10,2},{12,4},{14,6},{1,9},{3,11}... | collective-permute-start | bytes 208904 | tf_op jit(solution)/shard_map/ppermute | solution.py:310
  30.7 3.0 %collective-permute-start.9 = (f32[136,128]{1,0:T(8,128)S(1)}, f32[136,128]{1,0:T(8,128)S(1)}, u32[]{:S(2)}, u32[]{:S(2)}) collective-permute-start(f32[136,128]{1,0:T(8,128)S(1)} %get-tuple-element.12), channel_id=1, source_target_pairs={{0,12},{2,14},{4,0},{6,2},{8,4},{10,6},{12,8},{14,10},{1,13},{3,15... | collective-permute-start | bytes 208904 | tf_op jit(solution)/shard_map/ppermute | solution.py:310
  33.7 2.3 %collective-permute-start.10 = (f32[136,128]{1,0:T(8,128)S(1)}, f32[136,128]{1,0:T(8,128)S(1)}, u32[]{:S(2)}, u32[]{:S(2)}) collective-permute-start(f32[136,128]{1,0:T(8,128)S(1)} %get-tuple-element.7), channel_id=1, source_target_pairs={{0,14},{2,12},{4,2},{6,0},{8,6},{10,4},{12,10},{14,8},{1,15},{3,13... | collective-permute-start | bytes 208904 | tf_op jit(solution)/shard_map/ppermute | solution.py:310
  36.1 0.3 collective-permute-done.7
  36.4 2.1 %collective-permute-done.8 = f32[136,128]{1,0:T(8,128)S(1)} collective-permute-done((f32[136,128]{1,0:T(8,128)S(1)}, f32[136,128]{1,0:T(8,128)S(1)}, u32[]{:S(2)}, u32[]{:S(2)}) %collective-permute-start.8) | collective-permute-done | bytes 69664 | tf_op jit(solution)/shard_map/ppermute | solution.py:310
  38.5 0.8 collective-permute-done.10
  40.3 0.2 fusion.2
  40.9 1.9 %all_gather.3 = bf16[2,8,2048]{2,0,1:T(2,128)(2,1)S(1)} all-gather(bf16[2,4,2048]{2,0,1:T(2,128)(2,1)S(1)} %copy.56), channel_id=1, replica_groups=mesh['rep'=2,'tp'=8,'sub'=2] {'sub'}, dimensions={1}, use_global_device_ids=true | all-gather | bytes 98304 | tf_op jit(solution)/shard_map/all_gather | solution.py:381
  42.8 12.9 %fusion.1 = f32[16,8192]{1,0:T(8,128)S(1)} fusion(f32[8192]{0:T(1024)S(1)} %dynamic_slice.62, bf16[16,128,8192]{2,1,0:T(8,128)(2,1)} %bitcast.150, bf16[16,16,128]{2,1,0:T(8,128)(2,1)S(1)} %bitcast.142), kind=kOutput, calls=%fused_computation.3 | convolution fusion | flops 543031296 | bytes 34177024 | tf_op jit(solution)/shard_map/rhd,hdf->rhf/dot_general | solution.py:390
  55.7 0.3 copy.74
  56.0 0.5 constant_dynamic-slice_fusion.8
  56.6 1.3 %collective-permute-start.11 = (f32[16,1024]{1,0:T(8,128)S(1)}, f32[16,1024]{1,0:T(8,128)S(1)}, u32[]{:S(2)}, u32[]{:S(2)}) collective-permute-start(f32[16,1024]{1,0:T(8,128)S(1)} %bitcast.141), channel_id=1, source_target_pairs={{0,2},{2,0},{4,6},{6,4},{8,10},{10,8},{12,14},{14,12},{1,3},{3,1},... | collective-permute-start | bytes 196616 | tf_op jit(solution)/shard_map/ppermute | solution.py:72
  57.9 2.2 %collective-permute-start.12 = (f32[16,1024]{1,0:T(8,128)S(1)}, f32[16,1024]{1,0:T(8,128)S(1)}, u32[]{:S(2)}, u32[]{:S(2)}) collective-permute-start(f32[16,1024]{1,0:T(8,128)S(1)} %bitcast.140), channel_id=1, source_target_pairs={{0,4},{2,6},{4,8},{6,10},{8,12},{10,14},{12,0},{14,2},{1,5},{3,7},... | collective-permute-start | bytes 196616 | tf_op jit(solution)/shard_map/ppermute | solution.py:72
  60.2 0.6 collective-permute-start.13
  60.8 2.0 %collective-permute-start.14 = (f32[16,1024]{1,0:T(8,128)S(1)}, f32[16,1024]{1,0:T(8,128)S(1)}, u32[]{:S(2)}, u32[]{:S(2)}) collective-permute-start(f32[16,1024]{1,0:T(8,128)S(1)} %bitcast.136), channel_id=1, source_target_pairs={{0,8},{2,10},{4,12},{6,14},{8,0},{10,2},{12,4},{14,6},{1,9},{3,11}... | collective-permute-start | bytes 196616 | tf_op jit(solution)/shard_map/ppermute | solution.py:72
  62.8 1.5 %collective-permute-start.15 = (f32[16,1024]{1,0:T(8,128)S(1)}, f32[16,1024]{1,0:T(8,128)S(1)}, u32[]{:S(2)}, u32[]{:S(2)}) collective-permute-start(f32[16,1024]{1,0:T(8,128)S(1)} %bitcast.137), channel_id=1, source_target_pairs={{0,10},{2,8},{4,14},{6,12},{8,2},{10,0},{12,6},{14,4},{1,11},{3,9}... | collective-permute-start | bytes 196616 | tf_op jit(solution)/shard_map/ppermute | solution.py:72
  64.3 3.8 %collective-permute-start.16 = (f32[16,1024]{1,0:T(8,128)S(1)}, f32[16,1024]{1,0:T(8,128)S(1)}, u32[]{:S(2)}, u32[]{:S(2)}) collective-permute-start(f32[16,1024]{1,0:T(8,128)S(1)} %bitcast.139), channel_id=1, source_target_pairs={{0,12},{2,14},{4,0},{6,2},{8,4},{10,6},{12,8},{14,10},{1,13},{3,15... | collective-permute-start | bytes 196616 | tf_op jit(solution)/shard_map/ppermute | solution.py:72
  68.1 0.6 collective-permute-start.17
  68.8 0.9 collective-permute-done.14
  69.7 2.4 %collective-permute-done.15 = f32[16,1024]{1,0:T(8,128)S(1)} collective-permute-done((f32[16,1024]{1,0:T(8,128)S(1)}, f32[16,1024]{1,0:T(8,128)S(1)}, u32[]{:S(2)}, u32[]{:S(2)}) %collective-permute-start.15) | collective-permute-done | bytes 65568 | tf_op jit(solution)/shard_map/ppermute | solution.py:72
  72.1 1.2 %collective-permute-done.17 = f32[16,1024]{1,0:T(8,128)S(1)} collective-permute-done((f32[16,1024]{1,0:T(8,128)S(1)}, f32[16,1024]{1,0:T(8,128)S(1)}, u32[]{:S(2)}, u32[]{:S(2)}) %collective-permute-start.17) | collective-permute-done | bytes 65568 | tf_op jit(solution)/shard_map/ppermute | solution.py:72
  73.4 1.1 %collective-permute-start.18 = (bf16[16,1024]{1,0:T(8,128)(2,1)S(1)}, bf16[16,1024]{1,0:T(8,128)(2,1)S(1)}, u32[]{:S(2)}, u32[]{:S(2)}) collective-permute-start(bf16[16,1024]{1,0:T(8,128)(2,1)S(1)} %clamp_convert_fusion), channel_id=1, source_target_pairs={{0,2},{2,0},{4,6},{6,4},{8,10},{10,8},{12,14},{14,12},{1,3},{3,1},... | collective-permute-start | bytes 98312 | tf_op jit(solution)/shard_map/ppermute | solution.py:28
  74.5 2.8 %collective-permute-done.18 = bf16[16,1024]{1,0:T(8,128)(2,1)S(1)} collective-permute-done((bf16[16,1024]{1,0:T(8,128)(2,1)S(1)}, bf16[16,1024]{1,0:T(8,128)(2,1)S(1)}, u32[]{:S(2)}, u32[]{:S(2)}) %collective-permute-start.18) | collective-permute-done | bytes 32800 | tf_op jit(solution)/shard_map/ppermute | solution.py:28
  77.3 1.6 %collective-permute-start.19 = (bf16[2,16,1024]{2,1,0:T(8,128)(2,1)S(1)}, bf16[2,16,1024]{2,1,0:T(8,128)(2,1)S(1)}, u32[]{:S(2)}, u32[]{:S(2)}) collective-permute-start(bf16[2,16,1024]{2,1,0:T(8,128)(2,1)S(1)} %maximum_select_fusion.3), channel_id=1, source_target_pairs={{0,4},{2,6},{4,8},{6,10},{8,12},{10,14},{12,0},{14,2},{1,5},{3,7},... | collective-permute-start | bytes 196616 | tf_op jit(solution)/shard_map/ppermute | solution.py:34
  78.9 2.0 %collective-permute-start.20 = (bf16[2,16,1024]{2,1,0:T(8,128)(2,1)S(1)}, bf16[2,16,1024]{2,1,0:T(8,128)(2,1)S(1)}, u32[]{:S(2)}, u32[]{:S(2)}) collective-permute-start(bf16[2,16,1024]{2,1,0:T(8,128)(2,1)S(1)} %maximum_select_fusion.3), channel_id=1, source_target_pairs={{0,8},{2,10},{4,12},{6,14},{8,0},{10,2},{12,4},{14,6},{1,9},{3,11}... | collective-permute-start | bytes 196616 | tf_op jit(solution)/shard_map/ppermute | solution.py:34
  80.9 0.5 collective-permute-start.21
  81.4 2.1 %collective-permute-done.19 = bf16[2,16,1024]{2,1,0:T(8,128)(2,1)S(1)} collective-permute-done((bf16[2,16,1024]{2,1,0:T(8,128)(2,1)S(1)}, bf16[2,16,1024]{2,1,0:T(8,128)(2,1)S(1)}, u32[]{:S(2)}, u32[]{:S(2)}) %collective-permute-start.19) | collective-permute-done | bytes 65568 | tf_op jit(solution)/shard_map/ppermute | solution.py:34
  83.5 1.4 %collective-permute-done.20 = bf16[2,16,1024]{2,1,0:T(8,128)(2,1)S(1)} collective-permute-done((bf16[2,16,1024]{2,1,0:T(8,128)(2,1)S(1)}, bf16[2,16,1024]{2,1,0:T(8,128)(2,1)S(1)}, u32[]{:S(2)}, u32[]{:S(2)}) %collective-permute-start.20) | collective-permute-done | bytes 65568 | tf_op jit(solution)/shard_map/ppermute | solution.py:34
  84.9 0.7 collective-permute-done.21
  85.6 0.7 scatter_fusion
  86.4 0.3 copy.59
  86.8 0.8 add_convert_fusion
  (88 shorter events, 3.2 us)
Async XLA Ops:
  0.0 8.1 %collective-permute-start = (bf16[2,4,2048]{2,1,0:T(4,128)(2,1)}, bf16[2,4,2048]{2,1,0:T(4,128)(2,1)S(1)}, u32[]{:S(2)}, u32[]{:S(2)}) collective-permute-start(bf16[2,4,2048]{2,1,0:T(4,128)(2,1)} %param.9), channel_id=1, source_target_pairs={{0,2},{2,0},{4,6},{6,4},{8,10},{10,8},{12,14},{14,12},{1,3},{3,1},... | collective-permute-start | bytes 98312 | tf_op jit(solution)/shard_map/ppermute | solution.py:278
  9.0 10.4 %collective-permute-start.2 = (bf16[2,2,4,2048]{3,2,1,0:T(4,128)(2,1)S(1)}, bf16[2,2,4,2048]{3,2,1,0:T(4,128)(2,1)S(1)}, u32[]{:S(2)}, u32[]{:S(2)}) collective-permute-start(bf16[2,2,4,2048]{3,2,1,0:T(4,128)(2,1)S(1)} %maximum_select_fusion.1), channel_id=1, source_target_pairs={{0,4},{2,6},{4,8},{6,10},{8,12},{10,14},{12,0},{14,2},{1,5},{3,7},... | collective-permute-start | bytes 196616 | tf_op jit(solution)/shard_map/ppermute | solution.py:281
  10.6 8.8 %collective-permute-start.3 = (bf16[2,2,4,2048]{3,2,1,0:T(4,128)(2,1)S(1)}, bf16[2,2,4,2048]{3,2,1,0:T(4,128)(2,1)S(1)}, u32[]{:S(2)}, u32[]{:S(2)}) collective-permute-start(bf16[2,2,4,2048]{3,2,1,0:T(4,128)(2,1)S(1)} %maximum_select_fusion.1), channel_id=1, source_target_pairs={{0,8},{2,10},{4,12},{6,14},{8,0},{10,2},{12,4},{14,6},{1,9},{3,11}... | collective-permute-start | bytes 196616 | tf_op jit(solution)/shard_map/ppermute | solution.py:281
  13.2 6.2 %collective-permute-start.4 = (bf16[2,2,4,2048]{3,2,1,0:T(4,128)(2,1)S(1)}, bf16[2,2,4,2048]{3,2,1,0:T(4,128)(2,1)S(1)}, u32[]{:S(2)}, u32[]{:S(2)}) collective-permute-start(bf16[2,2,4,2048]{3,2,1,0:T(4,128)(2,1)S(1)} %maximum_select_fusion.1), channel_id=1, source_target_pairs={{0,12},{2,14},{4,0},{6,2},{8,4},{10,6},{12,8},{14,10},{1,13},{3,15... | collective-permute-start | bytes 196616 | tf_op jit(solution)/shard_map/ppermute | solution.py:281
  14.6 1.6 %copy-start = (bf16[2,4,128,1024]{3,2,1,0:T(8,128)(2,1)S(1)}, bf16[2,4,128,1024]{3,2,1,0:T(8,128)(2,1)}, u32[]{:S(2)}) copy-start(bf16[2,4,128,1024]{3,2,1,0:T(8,128)(2,1)} %refs_4_.3) | copy-start | bytes 6291460
  16.2 3.5 %copy-start.1 = (bf16[2,4,128,1024]{3,2,1,0:T(8,128)(2,1)S(1)}, bf16[2,4,128,1024]{3,2,1,0:T(8,128)(2,1)}, u32[]{:S(2)}) copy-start(bf16[2,4,128,1024]{3,2,1,0:T(8,128)(2,1)} %refs_4_.3) | copy-start | bytes 6291460
  18.8 12.0 %collective-permute-start.1 = (f32[136,128]{1,0:T(8,128)S(1)}, f32[136,128]{1,0:T(8,128)S(1)}, u32[]{:S(2)}, u32[]{:S(2)}) collective-permute-start(f32[136,128]{1,0:T(8,128)S(1)} %get-tuple-element.21), channel_id=1, source_target_pairs={{0,2},{2,0},{4,6},{6,4},{8,10},{10,8},{12,14},{14,12},{1,3},{3,1},... | collective-permute-start | bytes 208904 | tf_op jit(solution)/shard_map/ppermute | solution.py:300
  25.3 8.4 %collective-permute-start.5 = (f32[136,128]{1,0:T(8,128)S(1)}, f32[136,128]{1,0:T(8,128)S(1)}, u32[]{:S(2)}, u32[]{:S(2)}) collective-permute-start(f32[136,128]{1,0:T(8,128)S(1)} %get-tuple-element.8), channel_id=1, source_target_pairs={{0,4},{2,6},{4,8},{6,10},{8,12},{10,14},{12,0},{14,2},{1,5},{3,7},... | collective-permute-start | bytes 208904 | tf_op jit(solution)/shard_map/ppermute | solution.py:310
  26.1 10.0 %collective-permute-start.6 = (f32[136,128]{1,0:T(8,128)S(1)}, f32[136,128]{1,0:T(8,128)S(1)}, u32[]{:S(2)}, u32[]{:S(2)}) collective-permute-start(f32[136,128]{1,0:T(8,128)S(1)} %get-tuple-element.9), channel_id=1, source_target_pairs={{0,6},{2,4},{4,10},{6,8},{8,14},{10,12},{12,2},{14,0},{1,7},{3,5},... | collective-permute-start | bytes 208904 | tf_op jit(solution)/shard_map/ppermute | solution.py:310
  27.2 9.1 %collective-permute-start.7 = (f32[136,128]{1,0:T(8,128)S(1)}, f32[136,128]{1,0:T(8,128)S(1)}, u32[]{:S(2)}, u32[]{:S(2)}) collective-permute-start(f32[136,128]{1,0:T(8,128)S(1)} %get-tuple-element.10), channel_id=1, source_target_pairs={{0,8},{2,10},{4,12},{6,14},{8,0},{10,2},{12,4},{14,6},{1,9},{3,11}... | collective-permute-start | bytes 208904 | tf_op jit(solution)/shard_map/ppermute | solution.py:310
  30.7 7.7 %collective-permute-start.8 = (f32[136,128]{1,0:T(8,128)S(1)}, f32[136,128]{1,0:T(8,128)S(1)}, u32[]{:S(2)}, u32[]{:S(2)}) collective-permute-start(f32[136,128]{1,0:T(8,128)S(1)} %get-tuple-element.11), channel_id=1, source_target_pairs={{0,10},{2,8},{4,14},{6,12},{8,2},{10,0},{12,6},{14,4},{1,11},{3,9}... | collective-permute-start | bytes 208904 | tf_op jit(solution)/shard_map/ppermute | solution.py:310
  30.7 7.7 %collective-permute-start.9 = (f32[136,128]{1,0:T(8,128)S(1)}, f32[136,128]{1,0:T(8,128)S(1)}, u32[]{:S(2)}, u32[]{:S(2)}) collective-permute-start(f32[136,128]{1,0:T(8,128)S(1)} %get-tuple-element.12), channel_id=1, source_target_pairs={{0,12},{2,14},{4,0},{6,2},{8,4},{10,6},{12,8},{14,10},{1,13},{3,15... | collective-permute-start | bytes 208904 | tf_op jit(solution)/shard_map/ppermute | solution.py:310
  33.7 5.5 %collective-permute-start.10 = (f32[136,128]{1,0:T(8,128)S(1)}, f32[136,128]{1,0:T(8,128)S(1)}, u32[]{:S(2)}, u32[]{:S(2)}) collective-permute-start(f32[136,128]{1,0:T(8,128)S(1)} %get-tuple-element.7), channel_id=1, source_target_pairs={{0,14},{2,12},{4,2},{6,0},{8,6},{10,4},{12,10},{14,8},{1,15},{3,13... | collective-permute-start | bytes 208904 | tf_op jit(solution)/shard_map/ppermute | solution.py:310
  42.8 17.4 %copy-start.3 = (s32[128]{0:T(128)S(1)}, s32[128]{0:T(128)}, u32[]{:S(2)}) copy-start(s32[128]{0:T(128)} %param.16) | copy-start | bytes 1540
  55.7 31.1 %copy-start.2 = (bf16[2,8,8192]{2,1,0:T(8,128)(2,1)S(1)}, bf16[2,8,8192]{2,1,0:T(8,128)(2,1)}, u32[]{:S(2)}) copy-start(bf16[2,8,8192]{2,1,0:T(8,128)(2,1)} %param.17) | copy-start | bytes 786436
  56.6 7.7 %collective-permute-start.11 = (f32[16,1024]{1,0:T(8,128)S(1)}, f32[16,1024]{1,0:T(8,128)S(1)}, u32[]{:S(2)}, u32[]{:S(2)}) collective-permute-start(f32[16,1024]{1,0:T(8,128)S(1)} %bitcast.141), channel_id=1, source_target_pairs={{0,2},{2,0},{4,6},{6,4},{8,10},{10,8},{12,14},{14,12},{1,3},{3,1},... | collective-permute-start | bytes 196616 | tf_op jit(solution)/shard_map/ppermute | solution.py:72
  57.9 10.2 %collective-permute-start.12 = (f32[16,1024]{1,0:T(8,128)S(1)}, f32[16,1024]{1,0:T(8,128)S(1)}, u32[]{:S(2)}, u32[]{:S(2)}) collective-permute-start(f32[16,1024]{1,0:T(8,128)S(1)} %bitcast.140), channel_id=1, source_target_pairs={{0,4},{2,6},{4,8},{6,10},{8,12},{10,14},{12,0},{14,2},{1,5},{3,7},... | collective-permute-start | bytes 196616 | tf_op jit(solution)/shard_map/ppermute | solution.py:72
  60.2 8.7 %collective-permute-start.13 = (f32[16,1024]{1,0:T(8,128)S(1)}, f32[16,1024]{1,0:T(8,128)S(1)}, u32[]{:S(2)}, u32[]{:S(2)}) collective-permute-start(f32[16,1024]{1,0:T(8,128)S(1)} %bitcast.135), channel_id=1, source_target_pairs={{0,6},{2,4},{4,10},{6,8},{8,14},{10,12},{12,2},{14,0},{1,7},{3,5},... | collective-permute-start | bytes 196616 | tf_op jit(solution)/shard_map/ppermute | solution.py:72
  60.8 8.9 %collective-permute-start.14 = (f32[16,1024]{1,0:T(8,128)S(1)}, f32[16,1024]{1,0:T(8,128)S(1)}, u32[]{:S(2)}, u32[]{:S(2)}) collective-permute-start(f32[16,1024]{1,0:T(8,128)S(1)} %bitcast.136), channel_id=1, source_target_pairs={{0,8},{2,10},{4,12},{6,14},{8,0},{10,2},{12,4},{14,6},{1,9},{3,11}... | collective-permute-start | bytes 196616 | tf_op jit(solution)/shard_map/ppermute | solution.py:72
  62.8 9.4 %collective-permute-start.15 = (f32[16,1024]{1,0:T(8,128)S(1)}, f32[16,1024]{1,0:T(8,128)S(1)}, u32[]{:S(2)}, u32[]{:S(2)}) collective-permute-start(f32[16,1024]{1,0:T(8,128)S(1)} %bitcast.137), channel_id=1, source_target_pairs={{0,10},{2,8},{4,14},{6,12},{8,2},{10,0},{12,6},{14,4},{1,11},{3,9}... | collective-permute-start | bytes 196616 | tf_op jit(solution)/shard_map/ppermute | solution.py:72
  64.3 7.8 %collective-permute-start.16 = (f32[16,1024]{1,0:T(8,128)S(1)}, f32[16,1024]{1,0:T(8,128)S(1)}, u32[]{:S(2)}, u32[]{:S(2)}) collective-permute-start(f32[16,1024]{1,0:T(8,128)S(1)} %bitcast.139), channel_id=1, source_target_pairs={{0,12},{2,14},{4,0},{6,2},{8,4},{10,6},{12,8},{14,10},{1,13},{3,15... | collective-permute-start | bytes 196616 | tf_op jit(solution)/shard_map/ppermute | solution.py:72
  68.1 5.2 %collective-permute-start.17 = (f32[16,1024]{1,0:T(8,128)S(1)}, f32[16,1024]{1,0:T(8,128)S(1)}, u32[]{:S(2)}, u32[]{:S(2)}) collective-permute-start(f32[16,1024]{1,0:T(8,128)S(1)} %bitcast.138), channel_id=1, source_target_pairs={{0,14},{2,12},{4,2},{6,0},{8,6},{10,4},{12,10},{14,8},{1,15},{3,13... | collective-permute-start | bytes 196616 | tf_op jit(solution)/shard_map/ppermute | solution.py:72
  73.4 4.0 %collective-permute-start.18 = (bf16[16,1024]{1,0:T(8,128)(2,1)S(1)}, bf16[16,1024]{1,0:T(8,128)(2,1)S(1)}, u32[]{:S(2)}, u32[]{:S(2)}) collective-permute-start(bf16[16,1024]{1,0:T(8,128)(2,1)S(1)} %clamp_convert_fusion), channel_id=1, source_target_pairs={{0,2},{2,0},{4,6},{6,4},{8,10},{10,8},{12,14},{14,12},{1,3},{3,1},... | collective-permute-start | bytes 98312 | tf_op jit(solution)/shard_map/ppermute | solution.py:28
  77.3 6.1 %collective-permute-start.19 = (bf16[2,16,1024]{2,1,0:T(8,128)(2,1)S(1)}, bf16[2,16,1024]{2,1,0:T(8,128)(2,1)S(1)}, u32[]{:S(2)}, u32[]{:S(2)}) collective-permute-start(bf16[2,16,1024]{2,1,0:T(8,128)(2,1)S(1)} %maximum_select_fusion.3), channel_id=1, source_target_pairs={{0,4},{2,6},{4,8},{6,10},{8,12},{10,14},{12,0},{14,2},{1,5},{3,7},... | collective-permute-start | bytes 196616 | tf_op jit(solution)/shard_map/ppermute | solution.py:34
  78.9 6.0 %collective-permute-start.20 = (bf16[2,16,1024]{2,1,0:T(8,128)(2,1)S(1)}, bf16[2,16,1024]{2,1,0:T(8,128)(2,1)S(1)}, u32[]{:S(2)}, u32[]{:S(2)}) collective-permute-start(bf16[2,16,1024]{2,1,0:T(8,128)(2,1)S(1)} %maximum_select_fusion.3), channel_id=1, source_target_pairs={{0,8},{2,10},{4,12},{6,14},{8,0},{10,2},{12,4},{14,6},{1,9},{3,11}... | collective-permute-start | bytes 196616 | tf_op jit(solution)/shard_map/ppermute | solution.py:34
  80.9 4.7 %collective-permute-start.21 = (bf16[2,16,1024]{2,1,0:T(8,128)(2,1)S(1)}, bf16[2,16,1024]{2,1,0:T(8,128)(2,1)S(1)}, u32[]{:S(2)}, u32[]{:S(2)}) collective-permute-start(bf16[2,16,1024]{2,1,0:T(8,128)(2,1)S(1)} %maximum_select_fusion.3), channel_id=1, source_target_pairs={{0,12},{2,14},{4,0},{6,2},{8,4},{10,6},{12,8},{14,10},{1,13},{3,15... | collective-permute-start | bytes 196616 | tf_op jit(solution)/shard_map/ppermute | solution.py:34
